TPU v7x, 256 devices: a whole 4x4x8 slice. The times are simulated.
256 devices in a mesh: dp: 4 (over x), ctx: 16 (over z, y_hi), tp: 4 (over y_lo, core).
Axes of the slice: x: 4, y: 4 (y_hi: 2, y_lo: 2; y = y_hi * 2 + y_lo), z: 8, core: 2. Of those that a mesh axis runs over, the one named last changes fastest.
Arguments:
- query_rows: bfloat16 [16384, 4096], P(('dp', 'ctx'), 'tp'), parts along dimension 0, may hold values from -6 to 6
- key_matrix: bfloat16 [16384, 512], P(('dp', 'ctx'), 'tp'), parts along dimension 0, may hold values from -6 to 6
- value_matrix: bfloat16 [16384, 512], P(('dp', 'ctx'), 'tp'), parts along dimension 0, may hold values from -6 to 6
- attn_out: bfloat16 [16384, 4096], P(('dp', 'ctx'), 'tp'), parts along dimension 0, may hold values from -6 to 6
- out_grad: bfloat16 [16384, 4096], P(('dp', 'ctx', 'tp')), parts along dimension 0, may hold values from -0.5 to 0.5
- log_sums: float32 [32, 16384], P('tp', ('dp', 'ctx')), parts along dimension 1, may hold values from 3 to 5
- block_mask: int32 [128, 32], P('dp'), parts along dimension 0, may hold values 0 or 1
Outputs:
- query_grad: bfloat16 [16384, 4096], P(('dp', 'ctx'), 'tp'), parts along dimension 0
- key_gradient: bfloat16 [16384, 512], P(('dp', 'ctx'), 'tp'), parts along dimension 0
- value_gradient: bfloat16 [16384, 512], P(('dp', 'ctx'), 'tp'), parts along dimension 0
There are 4 independent parts, one for each index of `dp`. A program takes and returns all parts, laid end to end along the dimension named above; each array names one. Nothing has to cross between parts.
Inputs may be any that keep to these rules, and one draw needn't show every extreme that they name: `block_mask`: entry [a, b] with b < a lets query block a see key block b; entries on and above the diagonal are never read.
All inputs are finite; a program needn't handle non-finite values.
Results may differ from a plain program's by a relative error of at most 0.0049.
Values may be sent and summed in bfloat16 or wider, within the bound.
No kernel may reach another device: no remote copies, remote signals or barrier semaphores. Data moves between devices by JAX's collectives and lax.ppermute only.
A program may use at most 64 MiB of HBM per device.

v0:
```python
import math

import jax
import jax.numpy as jnp
from jax import lax
from jax.sharding import PartitionSpec as P

BLK = 128
HEAD_SIZE = 128


def from_behind(value, axis, steps):
    count = lax.axis_size(axis)
    pairs = [(source, (source + steps) % count) for source in range(count)]
    return lax.ppermute(value, axis, pairs)


def live_region(block_mask, query_start, tok_rows, key_start, key_count):
    block_table = lax.dynamic_slice(
        block_mask, (query_start // BLK, key_start // BLK), (tok_rows // BLK, key_count // BLK)
    )
    block_table = jnp.repeat(jnp.repeat(block_table, BLK, axis=0), BLK, axis=1)
    query_pos = query_start + jnp.arange(tok_rows, dtype=jnp.int32)
    key_pos = key_start + jnp.arange(key_count, dtype=jnp.int32)
    query_block = (query_pos // BLK)[:, None]
    key_block = (key_pos // BLK)[None, :]
    earlier = (key_block < query_block) & (block_table == 1)
    diagonal = (key_block == query_block) & (key_pos[None, :] <= query_pos[:, None])
    return earlier | diagonal


def contract(queries, out_grads, row_delta, log_sums, keys_part, values_part, live_mask):
    logit_scale = 1.0 / math.sqrt(HEAD_SIZE)
    scores = (
        jnp.einsum("igd,jd->gij", queries, keys_part, preferred_element_type=jnp.float32)
        * logit_scale
    )
    probabilities = jnp.where(live_mask[None], jnp.exp(scores - log_sums[:, :, None]), 0.0)
    prob_grad = jnp.einsum(
        "igd,jd->gij", out_grads, values_part, preferred_element_type=jnp.float32
    )
    dscore = (probabilities * (prob_grad - row_delta[:, :, None])).astype(jnp.bfloat16)
    query_term = jnp.einsum("gij,jd->igd", dscore, keys_part, preferred_element_type=jnp.float32)
    key_term = jnp.einsum("gij,igd->jd", dscore, queries, preferred_element_type=jnp.float32)
    value_term = jnp.einsum(
        "gij,igd->jd",
        probabilities.astype(jnp.bfloat16),
        out_grads,
        preferred_element_type=jnp.float32,
    )
    return (query_term, key_term, value_term)


def block_terms(context, keys_part, values_part, key_start):
    queries, out_grads, row_delta, log_sums, block_mask, query_start = context
    tok_rows = queries.shape[0]
    key_count = keys_part.shape[0]
    live_mask = live_region(block_mask, query_start, tok_rows, key_start, key_count)
    return contract(queries, out_grads, row_delta, log_sums, keys_part, values_part, live_mask)


def pass_grads(key_running_total, value_running_total):
    return from_behind((key_running_total, value_running_total), "ctx", -1)


def local(query_rows, key_matrix, value_matrix, attn_out, out_grad, log_sums, block_mask):
    tok_rows = query_rows.shape[0]
    col_width = query_rows.shape[1]
    heads_local = col_width // HEAD_SIZE
    ctx_pos = lax.axis_index("ctx")
    ctx_count = lax.axis_size("ctx")
    tp_pos = lax.axis_index("tp")
    gathered = lax.all_gather(out_grad, "tp", axis=0, tiled=True)
    own_grad = lax.dynamic_slice_in_dim(gathered, tp_pos * col_width, col_width, 1)
    queries = query_rows.reshape(tok_rows, heads_local, HEAD_SIZE)
    out_grads = own_grad.reshape(tok_rows, heads_local, HEAD_SIZE)
    outputs = attn_out.reshape(tok_rows, heads_local, HEAD_SIZE)
    row_delta = jnp.sum(out_grads.astype(jnp.float32) * outputs.astype(jnp.float32), axis=2).T
    query_start = ctx_pos * tok_rows
    context = (queries, out_grads, row_delta, log_sums, block_mask, query_start)
    zero_query = jnp.zeros((tok_rows, heads_local, HEAD_SIZE), jnp.float32)
    zero_key = jnp.zeros((tok_rows, HEAD_SIZE), jnp.float32)

    def visit_turn(turn_index, carried):
        keys_part, values_part, query_acc, key_running_total, value_running_total = carried
        owner_index = jnp.mod(ctx_pos + turn_index, ctx_count)
        query_term, key_term, value_term = block_terms(
            context, keys_part, values_part, owner_index * tok_rows
        )
        key_running_total, value_running_total = pass_grads(
            key_running_total + key_term, value_running_total + value_term
        )
        keys_part, values_part = from_behind((keys_part, values_part), "ctx", -1)
        return (
            keys_part,
            values_part,
            query_acc + query_term,
            key_running_total,
            value_running_total,
        )

    carried = lax.fori_loop(
        0, ctx_count - 1, visit_turn, (key_matrix, value_matrix, zero_query, zero_key, zero_key)
    )
    keys_part, values_part, query_acc, key_running_total, value_running_total = carried
    owner_index = jnp.mod(ctx_pos - 1, ctx_count)
    query_term, key_term, value_term = block_terms(
        context, keys_part, values_part, owner_index * tok_rows
    )
    query_acc = query_acc + query_term
    key_running_total, value_running_total = pass_grads(
        key_running_total + key_term, value_running_total + value_term
    )
    logit_scale = 1.0 / math.sqrt(HEAD_SIZE)
    query_grad = (query_acc * logit_scale).reshape(tok_rows, col_width).astype(jnp.bfloat16)
    key_gradient = (key_running_total * logit_scale).astype(jnp.bfloat16)
    value_gradient = value_running_total.astype(jnp.bfloat16)
    return (query_grad, key_gradient, value_gradient)


def solution(mesh):
    placed = (
        P(("dp", "ctx"), "tp"),
        P(("dp", "ctx"), "tp"),
        P(("dp", "ctx"), "tp"),
        P(("dp", "ctx"), "tp"),
        P(("dp", "ctx", "tp"), None),
        P("tp", ("dp", "ctx")),
        P("dp", None),
    )
    return jax.shard_map(
        local,
        mesh=mesh,
        in_specs=placed,
        out_specs=(P(("dp", "ctx"), "tp"), P(("dp", "ctx"), "tp"), P(("dp", "ctx"), "tp")),
        check_vma=False,
    )
```

profile of v0, /device:TPU:4, one launch (start us, length us, event | category | flops | bytes accessed | tf_op | source)
XLA Modules:
  0.0 370.7 jit_solution(1144416533640938476)
XLA Ops:
  7.2 1.5 copy.90
  8.7 1.5 copy.91
  13.9 31.0 %all-gather.2.cloned.1.call-done = bf16[256,4096]{1,0:T(8,128)(2,1)} async-done(((bf16[64,4096]{1,0:T(8,128)(2,1)}), bf16[256,4096]{1,0:T(8,128)(2,1)}) %all-gather.2.cloned.1.call-update) | async-done | bytes 2097168 | tf_op jit(solution)/shard_map/all_gather | solution.py:73
  46.9 301.9 %while.25 = (s32[]{:T(128)}, bf16[256,128]{1,0:T(8,128)(2,1)}, bf16[256,128]{1,0:T(8,128)(2,1)}, f32[256,8,128]{2,0,1:T(8,128)S(1)}, f32[256,128]{1,0:T(8,128)S(...) while((s32[]{:T(128)}, bf16[256,128]{1,0:T(8,128)(2,1)}, ...), condition=%wide.region_2.3_spmd.clone, body=%wide.region_1.2_spmd.clone.sunk | while | flops 675749888 | bytes 16345880 | solution.py:102
  47.8 5.5 %collective-permute-start.1 = (bf16[256,128]{1,0:T(8,128)(2,1)S(1)}, bf16[256,128]{1,0:T(8,128)(2,1)}, u32[]{:S(2)}, u32[]{:S(2)}) collective-permute-start(bf16[256,128]{1,0:T(8,128)(2,1)S(1)} %copy.77), channel_id=1, source_target_pairs={{0,60},{4,0},{8,4},{12,8},{16,12},{20,16},{24,20},{28,24},{32,28},... | collective-permute-start | bytes 196616 | tf_op jit(solution)/shard_map/while/body/eval_jaxpr/ppermute | solution.py:15
  58.2 3.5 collective-permute-start.2
  65.9 3.6 collective-permute-done.3
  70.4 4.1 %collective-permute-start.1 = (bf16[256,128]{1,0:T(8,128)(2,1)S(1)}, bf16[256,128]{1,0:T(8,128)(2,1)}, u32[]{:S(2)}, u32[]{:S(2)}) collective-permute-start(bf16[256,128]{1,0:T(8,128)(2,1)S(1)} %copy.77), channel_id=1, source_target_pairs={{0,60},{4,0},{8,4},{12,8},{16,12},{20,16},{24,20},{28,24},{32,28},... | collective-permute-start | bytes 196616 | tf_op jit(solution)/shard_map/while/body/eval_jaxpr/ppermute | solution.py:15
  78.9 2.9 collective-permute-start.2
  82.9 1.5 collective-permute-start.3
  85.8 3.8 %collective-permute-done.3 = f32[256,128]{1,0:T(8,128)S(1)} collective-permute-done((f32[256,128]{1,0:T(8,128)}, f32[256,128]{1,0:T(8,128)S(1)}, u32[]{:S(2)}, u32[]{:S(2)}) %collective-permute-start.3) | collective-permute-done | bytes 131104 | tf_op jit(solution)/shard_map/while/body/eval_jaxpr/ppermute | solution.py:15
  90.4 3.6 collective-permute-start.1
  98.9 1.5 collective-permute-start.2
  101.5 2.0 collective-permute-start.3
  105.6 2.6 collective-permute-done.3
  109.0 4.1 %collective-permute-start.1 = (bf16[256,128]{1,0:T(8,128)(2,1)S(1)}, bf16[256,128]{1,0:T(8,128)(2,1)}, u32[]{:S(2)}, u32[]{:S(2)}) collective-permute-start(bf16[256,128]{1,0:T(8,128)(2,1)S(1)} %copy.77), channel_id=1, source_target_pairs={{0,60},{4,0},{8,4},{12,8},{16,12},{20,16},{24,20},{28,24},{32,28},... | collective-permute-start | bytes 196616 | tf_op jit(solution)/shard_map/while/body/eval_jaxpr/ppermute | solution.py:15
  117.2 3.4 collective-permute-start.2
  124.3 4.1 %collective-permute-done.3 = f32[256,128]{1,0:T(8,128)S(1)} collective-permute-done((f32[256,128]{1,0:T(8,128)}, f32[256,128]{1,0:T(8,128)S(1)}, u32[]{:S(2)}, u32[]{:S(2)}) %collective-permute-start.3) | collective-permute-done | bytes 131104 | tf_op jit(solution)/shard_map/while/body/eval_jaxpr/ppermute | solution.py:15
  129.3 2.7 collective-permute-start.1
  136.2 2.2 collective-permute-start.2
  142.9 4.0 %collective-permute-done.3 = f32[256,128]{1,0:T(8,128)S(1)} collective-permute-done((f32[256,128]{1,0:T(8,128)}, f32[256,128]{1,0:T(8,128)S(1)}, u32[]{:S(2)}, u32[]{:S(2)}) %collective-permute-start.3) | collective-permute-done | bytes 131104 | tf_op jit(solution)/shard_map/while/body/eval_jaxpr/ppermute | solution.py:15
  147.7 2.9 collective-permute-start.1
  151.4 1.9 collective-permute-start
  156.5 4.3 %collective-permute-start.2 = (f32[256,128]{1,0:T(8,128)}, f32[256,128]{1,0:T(8,128)S(1)}, u32[]{:S(2)}, u32[]{:S(2)}) collective-permute-start(f32[256,128]{1,0:T(8,128)} %fusion.69), channel_id=1, source_target_pairs={{0,60},{4,0},{8,4},{12,8},{16,12},{20,16},{24,20},{28,24},{32,28},... | collective-permute-start | bytes 393224 | tf_op jit(solution)/shard_map/while/body/eval_jaxpr/ppermute | solution.py:15
  163.9 5.4 %collective-permute-done.3 = f32[256,128]{1,0:T(8,128)S(1)} collective-permute-done((f32[256,128]{1,0:T(8,128)}, f32[256,128]{1,0:T(8,128)S(1)}, u32[]{:S(2)}, u32[]{:S(2)}) %collective-permute-start.3) | collective-permute-done | bytes 131104 | tf_op jit(solution)/shard_map/while/body/eval_jaxpr/ppermute | solution.py:15
  170.2 2.4 collective-permute-start.1
  173.4 1.7 collective-permute-start
  178.5 2.3 collective-permute-start.2
  181.9 1.5 collective-permute-start.3
  185.2 3.6 collective-permute-done.3
  189.6 3.6 collective-permute-start.1
  197.4 3.7 collective-permute-start.2
  202.2 2.4 collective-permute-start.3
  205.5 4.1 %collective-permute-done.3 = f32[256,128]{1,0:T(8,128)S(1)} collective-permute-done((f32[256,128]{1,0:T(8,128)}, f32[256,128]{1,0:T(8,128)S(1)}, u32[]{:S(2)}, u32[]{:S(2)}) %collective-permute-start.3) | collective-permute-done | bytes 131104 | tf_op jit(solution)/shard_map/while/body/eval_jaxpr/ppermute | solution.py:15
  210.4 4.6 %collective-permute-start.1 = (bf16[256,128]{1,0:T(8,128)(2,1)S(1)}, bf16[256,128]{1,0:T(8,128)(2,1)}, u32[]{:S(2)}, u32[]{:S(2)}) collective-permute-start(bf16[256,128]{1,0:T(8,128)(2,1)S(1)} %copy.77), channel_id=1, source_target_pairs={{0,60},{4,0},{8,4},{12,8},{16,12},{20,16},{24,20},{28,24},{32,28},... | collective-permute-start | bytes 196616 | tf_op jit(solution)/shard_map/while/body/eval_jaxpr/ppermute | solution.py:15
  221.5 1.6 collective-permute-start.3
  223.9 3.3 collective-permute-done.2
  227.2 2.3 collective-permute-done.3
  230.4 3.2 collective-permute-start.1
  237.8 1.5 collective-permute-start.2
  242.6 3.3 collective-permute-done.2
  245.8 2.4 collective-permute-done.3
  249.1 3.6 collective-permute-start.1
  256.9 2.9 collective-permute-start.2
  262.9 1.6 collective-permute-done.2
  264.5 3.7 collective-permute-done.3
  269.0 4.1 %collective-permute-start.1 = (bf16[256,128]{1,0:T(8,128)(2,1)S(1)}, bf16[256,128]{1,0:T(8,128)(2,1)}, u32[]{:S(2)}, u32[]{:S(2)}) collective-permute-start(bf16[256,128]{1,0:T(8,128)(2,1)S(1)} %copy.77), channel_id=1, source_target_pairs={{0,60},{4,0},{8,4},{12,8},{16,12},{20,16},{24,20},{28,24},{32,28},... | collective-permute-start | bytes 196616 | tf_op jit(solution)/shard_map/while/body/eval_jaxpr/ppermute | solution.py:15
  277.3 2.9 collective-permute-start.2
  281.3 1.7 collective-permute-start.3
  284.1 3.8 %collective-permute-done.3 = f32[256,128]{1,0:T(8,128)S(1)} collective-permute-done((f32[256,128]{1,0:T(8,128)}, f32[256,128]{1,0:T(8,128)S(1)}, u32[]{:S(2)}, u32[]{:S(2)}) %collective-permute-start.3) | collective-permute-done | bytes 131104 | tf_op jit(solution)/shard_map/while/body/eval_jaxpr/ppermute | solution.py:15
  288.8 3.8 %collective-permute-start.1 = (bf16[256,128]{1,0:T(8,128)(2,1)S(1)}, bf16[256,128]{1,0:T(8,128)(2,1)}, u32[]{:S(2)}, u32[]{:S(2)}) collective-permute-start(bf16[256,128]{1,0:T(8,128)(2,1)S(1)} %copy.77), channel_id=1, source_target_pairs={{0,60},{4,0},{8,4},{12,8},{16,12},{20,16},{24,20},{28,24},{32,28},... | collective-permute-start | bytes 196616 | tf_op jit(solution)/shard_map/while/body/eval_jaxpr/ppermute | solution.py:15
  293.5 1.7 collective-permute-start
  298.5 4.1 %collective-permute-start.2 = (f32[256,128]{1,0:T(8,128)}, f32[256,128]{1,0:T(8,128)S(1)}, u32[]{:S(2)}, u32[]{:S(2)}) collective-permute-start(f32[256,128]{1,0:T(8,128)} %fusion.69), channel_id=1, source_target_pairs={{0,60},{4,0},{8,4},{12,8},{16,12},{20,16},{24,20},{28,24},{32,28},... | collective-permute-start | bytes 393224 | tf_op jit(solution)/shard_map/while/body/eval_jaxpr/ppermute | solution.py:15
  303.7 1.5 collective-permute-start.3
  306.3 4.1 %collective-permute-done.3 = f32[256,128]{1,0:T(8,128)S(1)} collective-permute-done((f32[256,128]{1,0:T(8,128)}, f32[256,128]{1,0:T(8,128)S(1)}, u32[]{:S(2)}, u32[]{:S(2)}) %collective-permute-start.3) | collective-permute-done | bytes 131104 | tf_op jit(solution)/shard_map/while/body/eval_jaxpr/ppermute | solution.py:15
  311.2 3.6 collective-permute-start.1
  319.0 4.8 %collective-permute-start.2 = (f32[256,128]{1,0:T(8,128)}, f32[256,128]{1,0:T(8,128)S(1)}, u32[]{:S(2)}, u32[]{:S(2)}) collective-permute-start(f32[256,128]{1,0:T(8,128)} %fusion.69), channel_id=1, source_target_pairs={{0,60},{4,0},{8,4},{12,8},{16,12},{20,16},{24,20},{28,24},{32,28},... | collective-permute-start | bytes 393224 | tf_op jit(solution)/shard_map/while/body/eval_jaxpr/ppermute | solution.py:15
  326.6 5.2 %collective-permute-done.3 = f32[256,128]{1,0:T(8,128)S(1)} collective-permute-done((f32[256,128]{1,0:T(8,128)}, f32[256,128]{1,0:T(8,128)S(1)}, u32[]{:S(2)}, u32[]{:S(2)}) %collective-permute-start.3) | collective-permute-done | bytes 131104 | tf_op jit(solution)/shard_map/while/body/eval_jaxpr/ppermute | solution.py:15
  332.7 2.1 collective-permute-start.1
  339.0 2.1 collective-permute-start.2
  343.1 2.6 collective-permute-done.2
  345.7 3.2 collective-permute-done.3
  353.1 2.5 collective-permute-start.5
  358.9 3.6 collective-permute-done.4
  (331 shorter events, 135.0 us)
Async XLA Ops:
  7.2 37.6 %all-gather.2.cloned.1.call-start = ((), (), s32[]{:S(2)}) async-start(), calls=%async_computation | async-start | bytes 2621440 | tf_op jit(solution)/shard_map/all_gather | solution.py:73
  13.9 32.7 %copy-start.6 = (f32[8,256]{1,0:T(8,128)S(1)}, f32[8,256]{1,0:T(8,128)}, u32[]{:S(2)}) copy-start(f32[8,256]{1,0:T(8,128)} %param.14) | copy-start | bytes 24580
  47.8 16.8 %collective-permute-start.1 = (bf16[256,128]{1,0:T(8,128)(2,1)S(1)}, bf16[256,128]{1,0:T(8,128)(2,1)}, u32[]{:S(2)}, u32[]{:S(2)}) collective-permute-start(bf16[256,128]{1,0:T(8,128)(2,1)S(1)} %copy.77), channel_id=1, source_target_pairs={{0,60},{4,0},{8,4},{12,8},{16,12},{20,16},{24,20},{28,24},{32,28},... | collective-permute-start | bytes 196616 | tf_op jit(solution)/shard_map/while/body/eval_jaxpr/ppermute | solution.py:15
  54.1 10.5 %collective-permute-start = (bf16[256,128]{1,0:T(8,128)(2,1)S(1)}, bf16[256,128]{1,0:T(8,128)(2,1)}, u32[]{:S(2)}, u32[]{:S(2)}) collective-permute-start(bf16[256,128]{1,0:T(8,128)(2,1)S(1)} %copy.76), channel_id=1, source_target_pairs={{0,60},{4,0},{8,4},{12,8},{16,12},{20,16},{24,20},{28,24},{32,28},... | collective-permute-start | bytes 196616 | tf_op jit(solution)/shard_map/while/body/eval_jaxpr/ppermute | solution.py:15
  58.2 7.7 %collective-permute-start.2 = (f32[256,128]{1,0:T(8,128)}, f32[256,128]{1,0:T(8,128)S(1)}, u32[]{:S(2)}, u32[]{:S(2)}) collective-permute-start(f32[256,128]{1,0:T(8,128)} %fusion.69), channel_id=1, source_target_pairs={{0,60},{4,0},{8,4},{12,8},{16,12},{20,16},{24,20},{28,24},{32,28},... | collective-permute-start | bytes 393224 | tf_op jit(solution)/shard_map/while/body/eval_jaxpr/ppermute | solution.py:15
  62.8 6.7 %collective-permute-start.3 = (f32[256,128]{1,0:T(8,128)}, f32[256,128]{1,0:T(8,128)S(1)}, u32[]{:S(2)}, u32[]{:S(2)}) collective-permute-start(f32[256,128]{1,0:T(8,128)} %fusion.70), channel_id=1, source_target_pairs={{0,60},{4,0},{8,4},{12,8},{16,12},{20,16},{24,20},{28,24},{32,28},... | collective-permute-start | bytes 393224 | tf_op jit(solution)/shard_map/while/body/eval_jaxpr/ppermute | solution.py:15
  70.4 14.8 %collective-permute-start.1 = (bf16[256,128]{1,0:T(8,128)(2,1)S(1)}, bf16[256,128]{1,0:T(8,128)(2,1)}, u32[]{:S(2)}, u32[]{:S(2)}) collective-permute-start(bf16[256,128]{1,0:T(8,128)(2,1)S(1)} %copy.77), channel_id=1, source_target_pairs={{0,60},{4,0},{8,4},{12,8},{16,12},{20,16},{24,20},{28,24},{32,28},... | collective-permute-start | bytes 196616 | tf_op jit(solution)/shard_map/while/body/eval_jaxpr/ppermute | solution.py:15
  75.3 9.9 %collective-permute-start = (bf16[256,128]{1,0:T(8,128)(2,1)S(1)}, bf16[256,128]{1,0:T(8,128)(2,1)}, u32[]{:S(2)}, u32[]{:S(2)}) collective-permute-start(bf16[256,128]{1,0:T(8,128)(2,1)S(1)} %copy.76), channel_id=1, source_target_pairs={{0,60},{4,0},{8,4},{12,8},{16,12},{20,16},{24,20},{28,24},{32,28},... | collective-permute-start | bytes 196616 | tf_op jit(solution)/shard_map/while/body/eval_jaxpr/ppermute | solution.py:15
  78.9 6.9 %collective-permute-start.2 = (f32[256,128]{1,0:T(8,128)}, f32[256,128]{1,0:T(8,128)S(1)}, u32[]{:S(2)}, u32[]{:S(2)}) collective-permute-start(f32[256,128]{1,0:T(8,128)} %fusion.69), channel_id=1, source_target_pairs={{0,60},{4,0},{8,4},{12,8},{16,12},{20,16},{24,20},{28,24},{32,28},... | collective-permute-start | bytes 393224 | tf_op jit(solution)/shard_map/while/body/eval_jaxpr/ppermute | solution.py:15
  82.9 6.7 %collective-permute-start.3 = (f32[256,128]{1,0:T(8,128)}, f32[256,128]{1,0:T(8,128)S(1)}, u32[]{:S(2)}, u32[]{:S(2)}) collective-permute-start(f32[256,128]{1,0:T(8,128)} %fusion.70), channel_id=1, source_target_pairs={{0,60},{4,0},{8,4},{12,8},{16,12},{20,16},{24,20},{28,24},{32,28},... | collective-permute-start | bytes 393224 | tf_op jit(solution)/shard_map/while/body/eval_jaxpr/ppermute | solution.py:15
  90.4 13.9 %collective-permute-start.1 = (bf16[256,128]{1,0:T(8,128)(2,1)S(1)}, bf16[256,128]{1,0:T(8,128)(2,1)}, u32[]{:S(2)}, u32[]{:S(2)}) collective-permute-start(bf16[256,128]{1,0:T(8,128)(2,1)S(1)} %copy.77), channel_id=1, source_target_pairs={{0,60},{4,0},{8,4},{12,8},{16,12},{20,16},{24,20},{28,24},{32,28},... | collective-permute-start | bytes 196616 | tf_op jit(solution)/shard_map/while/body/eval_jaxpr/ppermute | solution.py:15
  94.8 9.5 %collective-permute-start = (bf16[256,128]{1,0:T(8,128)(2,1)S(1)}, bf16[256,128]{1,0:T(8,128)(2,1)}, u32[]{:S(2)}, u32[]{:S(2)}) collective-permute-start(bf16[256,128]{1,0:T(8,128)(2,1)S(1)} %copy.76), channel_id=1, source_target_pairs={{0,60},{4,0},{8,4},{12,8},{16,12},{20,16},{24,20},{28,24},{32,28},... | collective-permute-start | bytes 196616 | tf_op jit(solution)/shard_map/while/body/eval_jaxpr/ppermute | solution.py:15
  98.9 6.7 %collective-permute-start.2 = (f32[256,128]{1,0:T(8,128)}, f32[256,128]{1,0:T(8,128)S(1)}, u32[]{:S(2)}, u32[]{:S(2)}) collective-permute-start(f32[256,128]{1,0:T(8,128)} %fusion.69), channel_id=1, source_target_pairs={{0,60},{4,0},{8,4},{12,8},{16,12},{20,16},{24,20},{28,24},{32,28},... | collective-permute-start | bytes 393224 | tf_op jit(solution)/shard_map/while/body/eval_jaxpr/ppermute | solution.py:15
  101.5 6.7 %collective-permute-start.3 = (f32[256,128]{1,0:T(8,128)}, f32[256,128]{1,0:T(8,128)S(1)}, u32[]{:S(2)}, u32[]{:S(2)}) collective-permute-start(f32[256,128]{1,0:T(8,128)} %fusion.70), channel_id=1, source_target_pairs={{0,60},{4,0},{8,4},{12,8},{16,12},{20,16},{24,20},{28,24},{32,28},... | collective-permute-start | bytes 393224 | tf_op jit(solution)/shard_map/while/body/eval_jaxpr/ppermute | solution.py:15
  109.0 14.2 %collective-permute-start.1 = (bf16[256,128]{1,0:T(8,128)(2,1)S(1)}, bf16[256,128]{1,0:T(8,128)(2,1)}, u32[]{:S(2)}, u32[]{:S(2)}) collective-permute-start(bf16[256,128]{1,0:T(8,128)(2,1)S(1)} %copy.77), channel_id=1, source_target_pairs={{0,60},{4,0},{8,4},{12,8},{16,12},{20,16},{24,20},{28,24},{32,28},... | collective-permute-start | bytes 196616 | tf_op jit(solution)/shard_map/while/body/eval_jaxpr/ppermute | solution.py:15
  113.9 9.4 %collective-permute-start = (bf16[256,128]{1,0:T(8,128)(2,1)S(1)}, bf16[256,128]{1,0:T(8,128)(2,1)}, u32[]{:S(2)}, u32[]{:S(2)}) collective-permute-start(bf16[256,128]{1,0:T(8,128)(2,1)S(1)} %copy.76), channel_id=1, source_target_pairs={{0,60},{4,0},{8,4},{12,8},{16,12},{20,16},{24,20},{28,24},{32,28},... | collective-permute-start | bytes 196616 | tf_op jit(solution)/shard_map/while/body/eval_jaxpr/ppermute | solution.py:15
  117.2 7.1 %collective-permute-start.2 = (f32[256,128]{1,0:T(8,128)}, f32[256,128]{1,0:T(8,128)S(1)}, u32[]{:S(2)}, u32[]{:S(2)}) collective-permute-start(f32[256,128]{1,0:T(8,128)} %fusion.69), channel_id=1, source_target_pairs={{0,60},{4,0},{8,4},{12,8},{16,12},{20,16},{24,20},{28,24},{32,28},... | collective-permute-start | bytes 393224 | tf_op jit(solution)/shard_map/while/body/eval_jaxpr/ppermute | solution.py:15
  121.8 6.7 %collective-permute-start.3 = (f32[256,128]{1,0:T(8,128)}, f32[256,128]{1,0:T(8,128)S(1)}, u32[]{:S(2)}, u32[]{:S(2)}) collective-permute-start(f32[256,128]{1,0:T(8,128)} %fusion.70), channel_id=1, source_target_pairs={{0,60},{4,0},{8,4},{12,8},{16,12},{20,16},{24,20},{28,24},{32,28},... | collective-permute-start | bytes 393224 | tf_op jit(solution)/shard_map/while/body/eval_jaxpr/ppermute | solution.py:15
  129.3 12.5 %collective-permute-start.1 = (bf16[256,128]{1,0:T(8,128)(2,1)S(1)}, bf16[256,128]{1,0:T(8,128)(2,1)}, u32[]{:S(2)}, u32[]{:S(2)}) collective-permute-start(bf16[256,128]{1,0:T(8,128)(2,1)S(1)} %copy.77), channel_id=1, source_target_pairs={{0,60},{4,0},{8,4},{12,8},{16,12},{20,16},{24,20},{28,24},{32,28},... | collective-permute-start | bytes 196616 | tf_op jit(solution)/shard_map/while/body/eval_jaxpr/ppermute | solution.py:15
  132.9 8.9 %collective-permute-start = (bf16[256,128]{1,0:T(8,128)(2,1)S(1)}, bf16[256,128]{1,0:T(8,128)(2,1)}, u32[]{:S(2)}, u32[]{:S(2)}) collective-permute-start(bf16[256,128]{1,0:T(8,128)(2,1)S(1)} %copy.76), channel_id=1, source_target_pairs={{0,60},{4,0},{8,4},{12,8},{16,12},{20,16},{24,20},{28,24},{32,28},... | collective-permute-start | bytes 196616 | tf_op jit(solution)/shard_map/while/body/eval_jaxpr/ppermute | solution.py:15
  136.2 6.7 %collective-permute-start.2 = (f32[256,128]{1,0:T(8,128)}, f32[256,128]{1,0:T(8,128)S(1)}, u32[]{:S(2)}, u32[]{:S(2)}) collective-permute-start(f32[256,128]{1,0:T(8,128)} %fusion.69), channel_id=1, source_target_pairs={{0,60},{4,0},{8,4},{12,8},{16,12},{20,16},{24,20},{28,24},{32,28},... | collective-permute-start | bytes 393224 | tf_op jit(solution)/shard_map/while/body/eval_jaxpr/ppermute | solution.py:15
  139.5 7.3 %collective-permute-start.3 = (f32[256,128]{1,0:T(8,128)}, f32[256,128]{1,0:T(8,128)S(1)}, u32[]{:S(2)}, u32[]{:S(2)}) collective-permute-start(f32[256,128]{1,0:T(8,128)} %fusion.70), channel_id=1, source_target_pairs={{0,60},{4,0},{8,4},{12,8},{16,12},{20,16},{24,20},{28,24},{32,28},... | collective-permute-start | bytes 393224 | tf_op jit(solution)/shard_map/while/body/eval_jaxpr/ppermute | solution.py:15
  147.7 15.3 %collective-permute-start.1 = (bf16[256,128]{1,0:T(8,128)(2,1)S(1)}, bf16[256,128]{1,0:T(8,128)(2,1)}, u32[]{:S(2)}, u32[]{:S(2)}) collective-permute-start(bf16[256,128]{1,0:T(8,128)(2,1)S(1)} %copy.77), channel_id=1, source_target_pairs={{0,60},{4,0},{8,4},{12,8},{16,12},{20,16},{24,20},{28,24},{32,28},... | collective-permute-start | bytes 196616 | tf_op jit(solution)/shard_map/while/body/eval_jaxpr/ppermute | solution.py:15
  151.4 11.6 %collective-permute-start = (bf16[256,128]{1,0:T(8,128)(2,1)S(1)}, bf16[256,128]{1,0:T(8,128)(2,1)}, u32[]{:S(2)}, u32[]{:S(2)}) collective-permute-start(bf16[256,128]{1,0:T(8,128)(2,1)S(1)} %copy.76), channel_id=1, source_target_pairs={{0,60},{4,0},{8,4},{12,8},{16,12},{20,16},{24,20},{28,24},{32,28},... | collective-permute-start | bytes 196616 | tf_op jit(solution)/shard_map/while/body/eval_jaxpr/ppermute | solution.py:15
  156.5 7.4 %collective-permute-start.2 = (f32[256,128]{1,0:T(8,128)}, f32[256,128]{1,0:T(8,128)S(1)}, u32[]{:S(2)}, u32[]{:S(2)}) collective-permute-start(f32[256,128]{1,0:T(8,128)} %fusion.69), channel_id=1, source_target_pairs={{0,60},{4,0},{8,4},{12,8},{16,12},{20,16},{24,20},{28,24},{32,28},... | collective-permute-start | bytes 393224 | tf_op jit(solution)/shard_map/while/body/eval_jaxpr/ppermute | solution.py:15
  162.0 7.4 %collective-permute-start.3 = (f32[256,128]{1,0:T(8,128)}, f32[256,128]{1,0:T(8,128)S(1)}, u32[]{:S(2)}, u32[]{:S(2)}) collective-permute-start(f32[256,128]{1,0:T(8,128)} %fusion.70), channel_id=1, source_target_pairs={{0,60},{4,0},{8,4},{12,8},{16,12},{20,16},{24,20},{28,24},{32,28},... | collective-permute-start | bytes 393224 | tf_op jit(solution)/shard_map/while/body/eval_jaxpr/ppermute | solution.py:15
  170.2 14.1 %collective-permute-start.1 = (bf16[256,128]{1,0:T(8,128)(2,1)S(1)}, bf16[256,128]{1,0:T(8,128)(2,1)}, u32[]{:S(2)}, u32[]{:S(2)}) collective-permute-start(bf16[256,128]{1,0:T(8,128)(2,1)S(1)} %copy.77), channel_id=1, source_target_pairs={{0,60},{4,0},{8,4},{12,8},{16,12},{20,16},{24,20},{28,24},{32,28},... | collective-permute-start | bytes 196616 | tf_op jit(solution)/shard_map/while/body/eval_jaxpr/ppermute | solution.py:15
  173.4 10.8 %collective-permute-start = (bf16[256,128]{1,0:T(8,128)(2,1)S(1)}, bf16[256,128]{1,0:T(8,128)(2,1)}, u32[]{:S(2)}, u32[]{:S(2)}) collective-permute-start(bf16[256,128]{1,0:T(8,128)(2,1)S(1)} %copy.76), channel_id=1, source_target_pairs={{0,60},{4,0},{8,4},{12,8},{16,12},{20,16},{24,20},{28,24},{32,28},... | collective-permute-start | bytes 196616 | tf_op jit(solution)/shard_map/while/body/eval_jaxpr/ppermute | solution.py:15
  178.5 6.7 %collective-permute-start.2 = (f32[256,128]{1,0:T(8,128)}, f32[256,128]{1,0:T(8,128)S(1)}, u32[]{:S(2)}, u32[]{:S(2)}) collective-permute-start(f32[256,128]{1,0:T(8,128)} %fusion.69), channel_id=1, source_target_pairs={{0,60},{4,0},{8,4},{12,8},{16,12},{20,16},{24,20},{28,24},{32,28},... | collective-permute-start | bytes 393224 | tf_op jit(solution)/shard_map/while/body/eval_jaxpr/ppermute | solution.py:15
  181.9 6.9 %collective-permute-start.3 = (f32[256,128]{1,0:T(8,128)}, f32[256,128]{1,0:T(8,128)S(1)}, u32[]{:S(2)}, u32[]{:S(2)}) collective-permute-start(f32[256,128]{1,0:T(8,128)} %fusion.70), channel_id=1, source_target_pairs={{0,60},{4,0},{8,4},{12,8},{16,12},{20,16},{24,20},{28,24},{32,28},... | collective-permute-start | bytes 393224 | tf_op jit(solution)/shard_map/while/body/eval_jaxpr/ppermute | solution.py:15
  189.6 15.8 %collective-permute-start.1 = (bf16[256,128]{1,0:T(8,128)(2,1)S(1)}, bf16[256,128]{1,0:T(8,128)(2,1)}, u32[]{:S(2)}, u32[]{:S(2)}) collective-permute-start(bf16[256,128]{1,0:T(8,128)(2,1)S(1)} %copy.77), channel_id=1, source_target_pairs={{0,60},{4,0},{8,4},{12,8},{16,12},{20,16},{24,20},{28,24},{32,28},... | collective-permute-start | bytes 196616 | tf_op jit(solution)/shard_map/while/body/eval_jaxpr/ppermute | solution.py:15
  194.1 11.4 %collective-permute-start = (bf16[256,128]{1,0:T(8,128)(2,1)S(1)}, bf16[256,128]{1,0:T(8,128)(2,1)}, u32[]{:S(2)}, u32[]{:S(2)}) collective-permute-start(bf16[256,128]{1,0:T(8,128)(2,1)S(1)} %copy.76), channel_id=1, source_target_pairs={{0,60},{4,0},{8,4},{12,8},{16,12},{20,16},{24,20},{28,24},{32,28},... | collective-permute-start | bytes 196616 | tf_op jit(solution)/shard_map/while/body/eval_jaxpr/ppermute | solution.py:15
  197.4 8.1 %collective-permute-start.2 = (f32[256,128]{1,0:T(8,128)}, f32[256,128]{1,0:T(8,128)S(1)}, u32[]{:S(2)}, u32[]{:S(2)}) collective-permute-start(f32[256,128]{1,0:T(8,128)} %fusion.69), channel_id=1, source_target_pairs={{0,60},{4,0},{8,4},{12,8},{16,12},{20,16},{24,20},{28,24},{32,28},... | collective-permute-start | bytes 393224 | tf_op jit(solution)/shard_map/while/body/eval_jaxpr/ppermute | solution.py:15
  202.2 7.4 %collective-permute-start.3 = (f32[256,128]{1,0:T(8,128)}, f32[256,128]{1,0:T(8,128)S(1)}, u32[]{:S(2)}, u32[]{:S(2)}) collective-permute-start(f32[256,128]{1,0:T(8,128)} %fusion.70), channel_id=1, source_target_pairs={{0,60},{4,0},{8,4},{12,8},{16,12},{20,16},{24,20},{28,24},{32,28},... | collective-permute-start | bytes 393224 | tf_op jit(solution)/shard_map/while/body/eval_jaxpr/ppermute | solution.py:15
  210.4 13.5 %collective-permute-start.1 = (bf16[256,128]{1,0:T(8,128)(2,1)S(1)}, bf16[256,128]{1,0:T(8,128)(2,1)}, u32[]{:S(2)}, u32[]{:S(2)}) collective-permute-start(bf16[256,128]{1,0:T(8,128)(2,1)S(1)} %copy.77), channel_id=1, source_target_pairs={{0,60},{4,0},{8,4},{12,8},{16,12},{20,16},{24,20},{28,24},{32,28},... | collective-permute-start | bytes 196616 | tf_op jit(solution)/shard_map/while/body/eval_jaxpr/ppermute | solution.py:15
  215.9 8.1 %collective-permute-start = (bf16[256,128]{1,0:T(8,128)(2,1)S(1)}, bf16[256,128]{1,0:T(8,128)(2,1)}, u32[]{:S(2)}, u32[]{:S(2)}) collective-permute-start(bf16[256,128]{1,0:T(8,128)(2,1)S(1)} %copy.76), channel_id=1, source_target_pairs={{0,60},{4,0},{8,4},{12,8},{16,12},{20,16},{24,20},{28,24},{32,28},... | collective-permute-start | bytes 196616 | tf_op jit(solution)/shard_map/while/body/eval_jaxpr/ppermute | solution.py:15
  219.2 8.1 %collective-permute-start.2 = (f32[256,128]{1,0:T(8,128)}, f32[256,128]{1,0:T(8,128)S(1)}, u32[]{:S(2)}, u32[]{:S(2)}) collective-permute-start(f32[256,128]{1,0:T(8,128)} %fusion.69), channel_id=1, source_target_pairs={{0,60},{4,0},{8,4},{12,8},{16,12},{20,16},{24,20},{28,24},{32,28},... | collective-permute-start | bytes 393224 | tf_op jit(solution)/shard_map/while/body/eval_jaxpr/ppermute | solution.py:15
  221.5 8.1 %collective-permute-start.3 = (f32[256,128]{1,0:T(8,128)}, f32[256,128]{1,0:T(8,128)S(1)}, u32[]{:S(2)}, u32[]{:S(2)}) collective-permute-start(f32[256,128]{1,0:T(8,128)} %fusion.70), channel_id=1, source_target_pairs={{0,60},{4,0},{8,4},{12,8},{16,12},{20,16},{24,20},{28,24},{32,28},... | collective-permute-start | bytes 393224 | tf_op jit(solution)/shard_map/while/body/eval_jaxpr/ppermute | solution.py:15
  230.4 12.1 %collective-permute-start.1 = (bf16[256,128]{1,0:T(8,128)(2,1)S(1)}, bf16[256,128]{1,0:T(8,128)(2,1)}, u32[]{:S(2)}, u32[]{:S(2)}) collective-permute-start(bf16[256,128]{1,0:T(8,128)(2,1)S(1)} %copy.77), channel_id=1, source_target_pairs={{0,60},{4,0},{8,4},{12,8},{16,12},{20,16},{24,20},{28,24},{32,28},... | collective-permute-start | bytes 196616 | tf_op jit(solution)/shard_map/while/body/eval_jaxpr/ppermute | solution.py:15
  234.5 8.0 %collective-permute-start = (bf16[256,128]{1,0:T(8,128)(2,1)S(1)}, bf16[256,128]{1,0:T(8,128)(2,1)}, u32[]{:S(2)}, u32[]{:S(2)}) collective-permute-start(bf16[256,128]{1,0:T(8,128)(2,1)S(1)} %copy.76), channel_id=1, source_target_pairs={{0,60},{4,0},{8,4},{12,8},{16,12},{20,16},{24,20},{28,24},{32,28},... | collective-permute-start | bytes 196616 | tf_op jit(solution)/shard_map/while/body/eval_jaxpr/ppermute | solution.py:15
  237.8 8.0 %collective-permute-start.2 = (f32[256,128]{1,0:T(8,128)}, f32[256,128]{1,0:T(8,128)S(1)}, u32[]{:S(2)}, u32[]{:S(2)}) collective-permute-start(f32[256,128]{1,0:T(8,128)} %fusion.69), channel_id=1, source_target_pairs={{0,60},{4,0},{8,4},{12,8},{16,12},{20,16},{24,20},{28,24},{32,28},... | collective-permute-start | bytes 393224 | tf_op jit(solution)/shard_map/while/body/eval_jaxpr/ppermute | solution.py:15
  240.4 7.8 %collective-permute-start.3 = (f32[256,128]{1,0:T(8,128)}, f32[256,128]{1,0:T(8,128)S(1)}, u32[]{:S(2)}, u32[]{:S(2)}) collective-permute-start(f32[256,128]{1,0:T(8,128)} %fusion.70), channel_id=1, source_target_pairs={{0,60},{4,0},{8,4},{12,8},{16,12},{20,16},{24,20},{28,24},{32,28},... | collective-permute-start | bytes 393224 | tf_op jit(solution)/shard_map/while/body/eval_jaxpr/ppermute | solution.py:15
  249.1 13.7 %collective-permute-start.1 = (bf16[256,128]{1,0:T(8,128)(2,1)S(1)}, bf16[256,128]{1,0:T(8,128)(2,1)}, u32[]{:S(2)}, u32[]{:S(2)}) collective-permute-start(bf16[256,128]{1,0:T(8,128)(2,1)S(1)} %copy.77), channel_id=1, source_target_pairs={{0,60},{4,0},{8,4},{12,8},{16,12},{20,16},{24,20},{28,24},{32,28},... | collective-permute-start | bytes 196616 | tf_op jit(solution)/shard_map/while/body/eval_jaxpr/ppermute | solution.py:15
  253.6 9.3 %collective-permute-start = (bf16[256,128]{1,0:T(8,128)(2,1)S(1)}, bf16[256,128]{1,0:T(8,128)(2,1)}, u32[]{:S(2)}, u32[]{:S(2)}) collective-permute-start(bf16[256,128]{1,0:T(8,128)(2,1)S(1)} %copy.76), channel_id=1, source_target_pairs={{0,60},{4,0},{8,4},{12,8},{16,12},{20,16},{24,20},{28,24},{32,28},... | collective-permute-start | bytes 196616 | tf_op jit(solution)/shard_map/while/body/eval_jaxpr/ppermute | solution.py:15
  256.9 7.6 %collective-permute-start.2 = (f32[256,128]{1,0:T(8,128)}, f32[256,128]{1,0:T(8,128)S(1)}, u32[]{:S(2)}, u32[]{:S(2)}) collective-permute-start(f32[256,128]{1,0:T(8,128)} %fusion.69), channel_id=1, source_target_pairs={{0,60},{4,0},{8,4},{12,8},{16,12},{20,16},{24,20},{28,24},{32,28},... | collective-permute-start | bytes 393224 | tf_op jit(solution)/shard_map/while/body/eval_jaxpr/ppermute | solution.py:15
  260.9 7.3 %collective-permute-start.3 = (f32[256,128]{1,0:T(8,128)}, f32[256,128]{1,0:T(8,128)S(1)}, u32[]{:S(2)}, u32[]{:S(2)}) collective-permute-start(f32[256,128]{1,0:T(8,128)} %fusion.70), channel_id=1, source_target_pairs={{0,60},{4,0},{8,4},{12,8},{16,12},{20,16},{24,20},{28,24},{32,28},... | collective-permute-start | bytes 393224 | tf_op jit(solution)/shard_map/while/body/eval_jaxpr/ppermute | solution.py:15
  269.0 14.9 %collective-permute-start.1 = (bf16[256,128]{1,0:T(8,128)(2,1)S(1)}, bf16[256,128]{1,0:T(8,128)(2,1)}, u32[]{:S(2)}, u32[]{:S(2)}) collective-permute-start(bf16[256,128]{1,0:T(8,128)(2,1)S(1)} %copy.77), channel_id=1, source_target_pairs={{0,60},{4,0},{8,4},{12,8},{16,12},{20,16},{24,20},{28,24},{32,28},... | collective-permute-start | bytes 196616 | tf_op jit(solution)/shard_map/while/body/eval_jaxpr/ppermute | solution.py:15
  273.9 10.0 %collective-permute-start = (bf16[256,128]{1,0:T(8,128)(2,1)S(1)}, bf16[256,128]{1,0:T(8,128)(2,1)}, u32[]{:S(2)}, u32[]{:S(2)}) collective-permute-start(bf16[256,128]{1,0:T(8,128)(2,1)S(1)} %copy.76), channel_id=1, source_target_pairs={{0,60},{4,0},{8,4},{12,8},{16,12},{20,16},{24,20},{28,24},{32,28},... | collective-permute-start | bytes 196616 | tf_op jit(solution)/shard_map/while/body/eval_jaxpr/ppermute | solution.py:15
  277.3 6.9 %collective-permute-start.2 = (f32[256,128]{1,0:T(8,128)}, f32[256,128]{1,0:T(8,128)S(1)}, u32[]{:S(2)}, u32[]{:S(2)}) collective-permute-start(f32[256,128]{1,0:T(8,128)} %fusion.69), channel_id=1, source_target_pairs={{0,60},{4,0},{8,4},{12,8},{16,12},{20,16},{24,20},{28,24},{32,28},... | collective-permute-start | bytes 393224 | tf_op jit(solution)/shard_map/while/body/eval_jaxpr/ppermute | solution.py:15
  281.3 6.7 %collective-permute-start.3 = (f32[256,128]{1,0:T(8,128)}, f32[256,128]{1,0:T(8,128)S(1)}, u32[]{:S(2)}, u32[]{:S(2)}) collective-permute-start(f32[256,128]{1,0:T(8,128)} %fusion.70), channel_id=1, source_target_pairs={{0,60},{4,0},{8,4},{12,8},{16,12},{20,16},{24,20},{28,24},{32,28},... | collective-permute-start | bytes 393224 | tf_op jit(solution)/shard_map/while/body/eval_jaxpr/ppermute | solution.py:15
  288.8 17.2 %collective-permute-start.1 = (bf16[256,128]{1,0:T(8,128)(2,1)S(1)}, bf16[256,128]{1,0:T(8,128)(2,1)}, u32[]{:S(2)}, u32[]{:S(2)}) collective-permute-start(bf16[256,128]{1,0:T(8,128)(2,1)S(1)} %copy.77), channel_id=1, source_target_pairs={{0,60},{4,0},{8,4},{12,8},{16,12},{20,16},{24,20},{28,24},{32,28},... | collective-permute-start | bytes 196616 | tf_op jit(solution)/shard_map/while/body/eval_jaxpr/ppermute | solution.py:15
  293.5 12.6 %collective-permute-start = (bf16[256,128]{1,0:T(8,128)(2,1)S(1)}, bf16[256,128]{1,0:T(8,128)(2,1)}, u32[]{:S(2)}, u32[]{:S(2)}) collective-permute-start(bf16[256,128]{1,0:T(8,128)(2,1)S(1)} %copy.76), channel_id=1, source_target_pairs={{0,60},{4,0},{8,4},{12,8},{16,12},{20,16},{24,20},{28,24},{32,28},... | collective-permute-start | bytes 196616 | tf_op jit(solution)/shard_map/while/body/eval_jaxpr/ppermute | solution.py:15
  298.5 7.8 %collective-permute-start.2 = (f32[256,128]{1,0:T(8,128)}, f32[256,128]{1,0:T(8,128)S(1)}, u32[]{:S(2)}, u32[]{:S(2)}) collective-permute-start(f32[256,128]{1,0:T(8,128)} %fusion.69), channel_id=1, source_target_pairs={{0,60},{4,0},{8,4},{12,8},{16,12},{20,16},{24,20},{28,24},{32,28},... | collective-permute-start | bytes 393224 | tf_op jit(solution)/shard_map/while/body/eval_jaxpr/ppermute | solution.py:15
  303.7 6.7 %collective-permute-start.3 = (f32[256,128]{1,0:T(8,128)}, f32[256,128]{1,0:T(8,128)S(1)}, u32[]{:S(2)}, u32[]{:S(2)}) collective-permute-start(f32[256,128]{1,0:T(8,128)} %fusion.70), channel_id=1, source_target_pairs={{0,60},{4,0},{8,4},{12,8},{16,12},{20,16},{24,20},{28,24},{32,28},... | collective-permute-start | bytes 393224 | tf_op jit(solution)/shard_map/while/body/eval_jaxpr/ppermute | solution.py:15
  311.2 14.7 %collective-permute-start.1 = (bf16[256,128]{1,0:T(8,128)(2,1)S(1)}, bf16[256,128]{1,0:T(8,128)(2,1)}, u32[]{:S(2)}, u32[]{:S(2)}) collective-permute-start(bf16[256,128]{1,0:T(8,128)(2,1)S(1)} %copy.77), channel_id=1, source_target_pairs={{0,60},{4,0},{8,4},{12,8},{16,12},{20,16},{24,20},{28,24},{32,28},... | collective-permute-start | bytes 196616 | tf_op jit(solution)/shard_map/while/body/eval_jaxpr/ppermute | solution.py:15
  315.6 10.2 %collective-permute-start = (bf16[256,128]{1,0:T(8,128)(2,1)S(1)}, bf16[256,128]{1,0:T(8,128)(2,1)}, u32[]{:S(2)}, u32[]{:S(2)}) collective-permute-start(bf16[256,128]{1,0:T(8,128)(2,1)S(1)} %copy.76), channel_id=1, source_target_pairs={{0,60},{4,0},{8,4},{12,8},{16,12},{20,16},{24,20},{28,24},{32,28},... | collective-permute-start | bytes 196616 | tf_op jit(solution)/shard_map/while/body/eval_jaxpr/ppermute | solution.py:15
  319.0 7.6 %collective-permute-start.2 = (f32[256,128]{1,0:T(8,128)}, f32[256,128]{1,0:T(8,128)S(1)}, u32[]{:S(2)}, u32[]{:S(2)}) collective-permute-start(f32[256,128]{1,0:T(8,128)} %fusion.69), channel_id=1, source_target_pairs={{0,60},{4,0},{8,4},{12,8},{16,12},{20,16},{24,20},{28,24},{32,28},... | collective-permute-start | bytes 393224 | tf_op jit(solution)/shard_map/while/body/eval_jaxpr/ppermute | solution.py:15
  324.9 6.9 %collective-permute-start.3 = (f32[256,128]{1,0:T(8,128)}, f32[256,128]{1,0:T(8,128)S(1)}, u32[]{:S(2)}, u32[]{:S(2)}) collective-permute-start(f32[256,128]{1,0:T(8,128)} %fusion.70), channel_id=1, source_target_pairs={{0,60},{4,0},{8,4},{12,8},{16,12},{20,16},{24,20},{28,24},{32,28},... | collective-permute-start | bytes 393224 | tf_op jit(solution)/shard_map/while/body/eval_jaxpr/ppermute | solution.py:15
  332.7 10.4 %collective-permute-start.1 = (bf16[256,128]{1,0:T(8,128)(2,1)S(1)}, bf16[256,128]{1,0:T(8,128)(2,1)}, u32[]{:S(2)}, u32[]{:S(2)}) collective-permute-start(bf16[256,128]{1,0:T(8,128)(2,1)S(1)} %copy.77), channel_id=1, source_target_pairs={{0,60},{4,0},{8,4},{12,8},{16,12},{20,16},{24,20},{28,24},{32,28},... | collective-permute-start | bytes 196616 | tf_op jit(solution)/shard_map/while/body/eval_jaxpr/ppermute | solution.py:15
  335.7 7.4 %collective-permute-start = (bf16[256,128]{1,0:T(8,128)(2,1)S(1)}, bf16[256,128]{1,0:T(8,128)(2,1)}, u32[]{:S(2)}, u32[]{:S(2)}) collective-permute-start(bf16[256,128]{1,0:T(8,128)(2,1)S(1)} %copy.76), channel_id=1, source_target_pairs={{0,60},{4,0},{8,4},{12,8},{16,12},{20,16},{24,20},{28,24},{32,28},... | collective-permute-start | bytes 196616 | tf_op jit(solution)/shard_map/while/body/eval_jaxpr/ppermute | solution.py:15
  339.0 6.7 %collective-permute-start.2 = (f32[256,128]{1,0:T(8,128)}, f32[256,128]{1,0:T(8,128)S(1)}, u32[]{:S(2)}, u32[]{:S(2)}) collective-permute-start(f32[256,128]{1,0:T(8,128)} %fusion.69), channel_id=1, source_target_pairs={{0,60},{4,0},{8,4},{12,8},{16,12},{20,16},{24,20},{28,24},{32,28},... | collective-permute-start | bytes 393224 | tf_op jit(solution)/shard_map/while/body/eval_jaxpr/ppermute | solution.py:15
  342.2 6.7 %collective-permute-start.3 = (f32[256,128]{1,0:T(8,128)}, f32[256,128]{1,0:T(8,128)S(1)}, u32[]{:S(2)}, u32[]{:S(2)}) collective-permute-start(f32[256,128]{1,0:T(8,128)} %fusion.70), channel_id=1, source_target_pairs={{0,60},{4,0},{8,4},{12,8},{16,12},{20,16},{24,20},{28,24},{32,28},... | collective-permute-start | bytes 393224 | tf_op jit(solution)/shard_map/while/body/eval_jaxpr/ppermute | solution.py:15
  353.1 5.8 %collective-permute-start.5 = (bf16[256,128]{1,0:T(8,128)(2,1)S(1)}, bf16[256,128]{1,0:T(8,128)(2,1)S(1)}, u32[]{:S(2)}, u32[]{:S(2)}) collective-permute-start(bf16[256,128]{1,0:T(8,128)(2,1)S(1)} %fusion.20), channel_id=1, source_target_pairs={{0,60},{4,0},{8,4},{12,8},{16,12},{20,16},{24,20},{28,24},{32,28},... | collective-permute-start | bytes 196616 | tf_op jit(solution)/shard_map/ppermute | solution.py:15
  356.0 6.5 %collective-permute-start.4 = (f32[256,128]{1,0:T(8,128)S(1)}, f32[256,128]{1,0:T(8,128)S(1)}, u32[]{:S(2)}, u32[]{:S(2)}) collective-permute-start(f32[256,128]{1,0:T(8,128)S(1)} %fusion.19), channel_id=1, source_target_pairs={{0,60},{4,0},{8,4},{12,8},{16,12},{20,16},{24,20},{28,24},{32,28},... | collective-permute-start | bytes 393224 | tf_op jit(solution)/shard_map/ppermute | solution.py:15
  (6 other events, 43.3 us)
Sparse Core Ops, SparseCore 0:
  10.3 34.4 all-gather.1
where the time goes:
time: 374 us; the launch traced here: 371 us
  starting transfers between devices  124 us (33%)
  waiting for transfers between devices  110 us (29%)
  matrix products  66.1 us (18%)
  local copies, waits for them, and re-layouts  49.1 us (13%)
  between operations  14.3 us (4%)
  other arithmetic  5.13 us (1%)
    ppermute x62, starting transfers between devices, from_behind(): return lax.ppermute(value, axis, pairs)  124 us
    ppermute x62, waiting for transfers between devices, from_behind(): return lax.ppermute(value, axis, pairs)  79.5 us
    all_gather x1, waiting for transfers between devices, local(): gathered = lax.all_gather(out_grad, 'tp', axis=0, tiled=True)  31 us
    while x60, local copies, waits for them, and re-layouts  26.5 us
    dot_general x16, matrix products, contract(): jnp.einsum('gij,igd->jd', probabilities.astype(jnp.bfloat16), out_grads,...  17 us
    dot_general x16, matrix products, contract(): jnp.einsum('gij,igd->jd', dscore, queries, preferred_element_type=jnp.flo...  16.8 us
    dot_general x16, matrix products, contract(): jnp.einsum('gij,jd->igd', dscore, keys_part, preferred_element_type=jnp.f...  14.2 us
    dynamic_slice x30, local copies, waits for them, and re-layouts, live_region(): lax.dynamic_slice(block_mask, (query_start // BLK, key_start // BLK), (to...  13.2 us
  transfers between devices with their start and end apart: 63, of which 32 were waited for; matrix products, arithmetic and copies ran while one was open for 26% of the time, Pallas kernels for 0%

commit v1 on v0

v1 whole, which is shorter than its diff:
```python
import math

import jax
import jax.numpy as jnp
from jax import lax
from jax.sharding import PartitionSpec as P

BLK = 128
HEAD_SIZE = 128


def live_region(block_mask, query_start, tok_rows, key_start, key_count):
    block_table = lax.dynamic_slice(
        block_mask, (query_start // BLK, key_start // BLK), (tok_rows // BLK, key_count // BLK)
    )
    block_table = jnp.repeat(jnp.repeat(block_table, BLK, axis=0), BLK, axis=1)
    query_pos = query_start + jnp.arange(tok_rows, dtype=jnp.int32)
    key_pos = key_start + jnp.arange(key_count, dtype=jnp.int32)
    query_block = (query_pos // BLK)[:, None]
    key_block = (key_pos // BLK)[None, :]
    earlier = (key_block < query_block) & (block_table == 1)
    diagonal = (key_block == query_block) & (key_pos[None, :] <= query_pos[:, None])
    return earlier | diagonal


def contract(queries, out_grads, row_delta, log_sums, keys_part, values_part, live_mask):
    logit_scale = 1.0 / math.sqrt(HEAD_SIZE)
    scores = (
        jnp.einsum("igd,jd->gij", queries, keys_part, preferred_element_type=jnp.float32)
        * logit_scale
    )
    probabilities = jnp.where(live_mask[None], jnp.exp(scores - log_sums[:, :, None]), 0.0)
    prob_grad = jnp.einsum(
        "igd,jd->gij", out_grads, values_part, preferred_element_type=jnp.float32
    )
    dscore = (probabilities * (prob_grad - row_delta[:, :, None])).astype(jnp.bfloat16)
    query_term = jnp.einsum("gij,jd->igd", dscore, keys_part, preferred_element_type=jnp.float32)
    key_term = jnp.einsum("gij,igd->jd", dscore, queries, preferred_element_type=jnp.float32)
    value_term = jnp.einsum(
        "gij,igd->jd",
        probabilities.astype(jnp.bfloat16),
        out_grads,
        preferred_element_type=jnp.float32,
    )
    return (query_term, key_term, value_term)


def local(query_rows, key_matrix, value_matrix, attn_out, out_grad, log_sums, block_mask):
    tok_rows = query_rows.shape[0]
    col_width = query_rows.shape[1]
    heads_local = col_width // HEAD_SIZE
    ctx_pos = lax.axis_index("ctx")
    ctx_count = lax.axis_size("ctx")
    tp_count = lax.axis_size("tp")
    grad_rows = out_grad.shape[0]
    pieces = out_grad.reshape(grad_rows, tp_count, col_width)
    own_grad = lax.all_to_all(pieces, "tp", split_axis=1, concat_axis=0, tiled=True)
    own_grad = own_grad.reshape(tok_rows, col_width)
    queries = query_rows.reshape(tok_rows, heads_local, HEAD_SIZE)
    out_grads = own_grad.reshape(tok_rows, heads_local, HEAD_SIZE)
    outputs = attn_out.reshape(tok_rows, heads_local, HEAD_SIZE)
    row_delta = jnp.sum(out_grads.astype(jnp.float32) * outputs.astype(jnp.float32), axis=2).T
    query_start = ctx_pos * tok_rows
    key_values = jnp.concatenate([key_matrix, value_matrix], axis=1)
    all_key_values = lax.all_gather(key_values, "ctx", axis=0, tiled=True)
    zero_query = jnp.zeros((tok_rows, heads_local, HEAD_SIZE), jnp.float32)
    zero_partial = jnp.zeros((ctx_count * tok_rows, 2 * HEAD_SIZE), jnp.float32)

    def visit_span(span, carried):
        query_acc, partial = carried
        key_start = span * tok_rows
        span_kv = lax.dynamic_slice_in_dim(all_key_values, key_start, tok_rows, 0)
        keys_part = span_kv[:, :HEAD_SIZE]
        values_part = span_kv[:, HEAD_SIZE:]
        live_mask = live_region(block_mask, query_start, tok_rows, key_start, tok_rows)
        query_term, key_term, value_term = contract(
            queries, out_grads, row_delta, log_sums, keys_part, values_part, live_mask
        )
        span_partial = jnp.concatenate([key_term, value_term], axis=1)
        partial = lax.dynamic_update_slice_in_dim(partial, span_partial, key_start, 0)
        return (query_acc + query_term, partial)

    query_acc, partial = lax.fori_loop(0, ctx_pos + 1, visit_span, (zero_query, zero_partial))
    summed = lax.psum_scatter(partial, "ctx", scatter_dimension=0, tiled=True)
    logit_scale = 1.0 / math.sqrt(HEAD_SIZE)
    query_grad = (query_acc * logit_scale).reshape(tok_rows, col_width).astype(jnp.bfloat16)
    key_gradient = (summed[:, :HEAD_SIZE] * logit_scale).astype(jnp.bfloat16)
    value_gradient = summed[:, HEAD_SIZE:].astype(jnp.bfloat16)
    return (query_grad, key_gradient, value_gradient)


def solution(mesh):
    placed = (
        P(("dp", "ctx"), "tp"),
        P(("dp", "ctx"), "tp"),
        P(("dp", "ctx"), "tp"),
        P(("dp", "ctx"), "tp"),
        P(("dp", "ctx", "tp"), None),
        P("tp", ("dp", "ctx")),
        P("dp", None),
    )
    return jax.shard_map(
        local,
        mesh=mesh,
        in_specs=placed,
        out_specs=(P(("dp", "ctx"), "tp"), P(("dp", "ctx"), "tp"), P(("dp", "ctx"), "tp")),
        check_vma=False,
    )
```

time: 374 us -> 432 us (1.16)
  waiting for transfers between devices: 110 us -> 393 us
  starting transfers between devices: 124 us -> 3.55 us
  matrix products: 66.1 us -> 4.83 us
  local copies, waits for them, and re-layouts: 49.1 us -> 9.4 us
    reduce_scatter x0 -> x1, waiting for transfers between devices: none -> 310 us  [local(): summed = lax.psum_scatter(partial, 'ctx', scatter_dimension=0, tiled=True)]
    ppermute x62 -> x0, starting transfers between devices: 124 us -> none  [from_behind(): return lax.ppermute(value, axis, pairs)]
    ppermute x62 -> x0, waiting for transfers between devices: 79.5 us -> none  [from_behind(): return lax.ppermute(value, axis, pairs)]
    all_gather x1, waiting for transfers between devices: 31 us -> 75.2 us  [local(): all_key_values = lax.all_gather(key_values, 'ctx', axis=0, tiled=True)]
    while x61 -> x4, local copies, waits for them, and re-layouts: 26.8 us -> 0.47 us  [the longest x2 0.38 us: local(): lax.fori_loop(0, ctx_pos + 1, visit_span, (zero_query, zero_partial))]
    dot_general x16 -> x1, matrix products: 17 us -> 0.48 us  [contract(): jnp.einsum('gij,igd->jd', probabilities.astype(jnp.bfloat16), out_grads,...]
    dot_general x16 -> x1, matrix products: 16.8 us -> 0.48 us  [contract(): jnp.einsum('gij,igd->jd', dscore, queries, preferred_element_type=jnp.flo...]
    dot_general x16 -> x1, matrix products: 14.2 us -> 1.19 us  [contract(): jnp.einsum('gij,jd->igd', dscore, keys_part, preferred_element_type=jnp.f...]
  transfers between devices with their start and end apart: 63 -> 3, of which waited for: 32 -> 3; matrix products, arithmetic and copies ran while one was open for 26% -> 1% of each run, Pallas kernels for 0% -> 0%
where the time goes in v1:
time: 432 us; the launch traced here: 429 us
  waiting for transfers between devices  393 us (91%)
  between operations  14.2 us (3%)
  local copies, waits for them, and re-layouts  9.4 us (2%)
  matrix products  4.83 us (1%)
    reduce_scatter x1, waiting for transfers between devices, local(): summed = lax.psum_scatter(partial, 'ctx', scatter_dimension=0, tiled=True)  310 us
    all_gather x1, waiting for transfers between devices, local(): all_key_values = lax.all_gather(key_values, 'ctx', axis=0, tiled=True)  75.2 us
  transfers between devices with their start and end apart: 3, of which 3 were waited for; matrix products, arithmetic and copies ran while one was open for 1% of the time, Pallas kernels for 0%

profile of v1, /device:TPU:4, one launch (start us, length us, event | category | flops | bytes accessed | tf_op | source)
XLA Modules:
  0.0 429.3 jit_solution(2428679739724852573)
XLA Ops:
  7.2 0.0 copy-start.1
  7.2 0.0 copy-start
  7.2 0.0 all-gather.2.cloned.1.call-start
  7.2 1.6 pad_maximum_fusion.1
  8.8 0.0 all-gather.2.cloned.1.call-update
  8.9 1.9 copy.66
  10.7 3.5 all-to-all-start
  14.2 0.0 reduce-scatter.2.cloned.1.call-start
  14.3 0.0 copy-done.1
  14.3 0.2 copy.40
  14.5 0.0 copy-done
  14.5 0.1 convert_bitcast_fusion
  14.6 0.2 copy.62
  14.8 8.2 %all-to-all-done = bf16[64,4,1024]{2,0,1:T(8,128)(2,1)S(1)} async-done(((bf16[64,4,1024]{2,0,1:T(8,128)(2,1)}), bf16[64,4,1024]{2,0,1:T(8,128)(2,1)S(1)}, u32[]{:S(2)}, u32[]{:S(2)}) %all-to-all-start) | async-done | bytes 524320 | tf_op jit(solution)/shard_map/all_to_all | solution.py:57
  23.0 0.1 copy.61
  23.1 0.3 copy.43
  23.5 0.3 multiply_reduce_fusion
  23.8 0.1 copy.44
  23.9 75.2 %all-gather.2.cloned.1.call-done = bf16[4096,256]{1,0:T(8,128)(2,1)} async-done(((bf16[256,256]{1,0:T(8,128)(2,1)}), bf16[4096,256]{1,0:T(8,128)(2,1)}) %all-gather.2.cloned.1.call-update) | async-done | bytes 2097168 | tf_op jit(solution)/shard_map/all_gather | solution.py:65
  99.1 0.1 broadcast_in_dim.48
  99.2 0.0 copy-start.2
  99.2 2.2 broadcast_in_dim.49.clone
  101.4 0.0 copy-done.2
  101.4 6.9 %while.15 = (s32[]{:T(128)}, f32[256,8,128]{0,2,1:T(8,128)S(1)}, f32[4096,256]{1,0:T(8,128)}, s32[]{:T(128)}, bf16[4096,256]{1,0:T(8,128)(2,1)}, /*index=5*/s32[...) while((s32[]{:T(128)}, f32[256,8,128]{0,2,1:T(8,128)S(1)}, ...), condition=%wide.region_2.3_spmd, body=%wide.region_1.2_spmd.sunk | while | flops 675487744 | bytes 15821342 | solution.py:83
  101.4 0.8 dynamic_slice.15
  102.2 0.1 copy.70
  102.3 0.1 broadcast_bitcast_fusion.2
  102.4 0.2 fusion.34
  102.6 1.4 fusion.35
  104.0 0.5 convolution_bitcast_fusion.5
  104.5 1.3 fusion.36
  105.7 0.5 convolution_bitcast_fusion.6
  106.2 1.2 fusion.37
  107.5 0.1 copy.72
  107.6 0.7 constant_dynamic-update-slice_fusion.2
  108.3 0.0 reduce-scatter.2.cloned.1.call-update
  108.3 0.1 multiply_convert_fusion
  108.4 1.0 copy.54
  109.4 309.9 %reduce-scatter.2.cloned.1.call-done = f32[256,256]{1,0:T(8,128)} async-done(((f32[4096,256]{1,0:T(8,128)}), f32[256,256]{1,0:T(8,128)}) %reduce-scatter.2.cloned.1.call-update) | async-done | bytes 262160 | tf_op jit(solution)/shard_map/reduce_scatter | solution.py:84
  419.3 1.5 slice.29
  420.9 1.5 fusion.9
  (5 shorter events, 0.1 us)
Async XLA Ops:
  7.2 7.1 %copy-start.1 = (bf16[256,1024]{1,0:T(8,128)(2,1)S(1)}, bf16[256,1024]{1,0:T(8,128)(2,1)}, u32[]{:S(2)}) copy-start(bf16[256,1024]{1,0:T(8,128)(2,1)} %param.9) | copy-start | bytes 1572868
  7.2 7.3 %copy-start = (bf16[256,1024]{1,0:T(8,128)(2,1)S(1)}, bf16[256,1024]{1,0:T(8,128)(2,1)}, u32[]{:S(2)}) copy-start(bf16[256,1024]{1,0:T(8,128)(2,1)} %param.12) | copy-start | bytes 1572868
  7.2 91.9 %all-gather.2.cloned.1.call-start = ((), (), s32[]{:S(2)}) async-start(), calls=%async_computation.2 | async-start | bytes 2228224 | tf_op jit(solution)/shard_map/all_gather | solution.py:65
  10.7 12.3 %all-to-all-start = ((bf16[64,4,1024]{2,0,1:T(8,128)(2,1)}), bf16[64,4,1024]{2,0,1:T(8,128)(2,1)S(1)}, u32[]{:S(2)}, u32[]{:S(2)}) async-start(bf16[64,4,1024]{2,0,1:T(8,128)(2,1)} %bitcast.62), calls=%async_computation | async-start | bytes 1048576 | tf_op jit(solution)/shard_map/all_to_all | solution.py:57
  14.2 405.1 %reduce-scatter.2.cloned.1.call-start = ((), (), s32[]{:S(2)}) async-start(), calls=%async_computation.3 | async-start | bytes 4456448 | tf_op jit(solution)/shard_map/reduce_scatter | solution.py:84
  99.2 2.2 copy-start.2
Sparse Core Ops, SparseCore 0:
  10.6 88.4 all-gather.1
  108.5 310.8 reduce-scatter.1

commit v2 on v1

--- a/solution.py
+++ b/solution.py
@@ -7,6 +7,29 @@
 
 BLK = 128
 HEAD_SIZE = 128
+Y_HI = 2
+
+
+def ring_of(ctx_count):
+    half = ctx_count // Y_HI
+    return [Y_HI * p if p < half else Y_HI * (ctx_count - 1 - p) + 1 for p in range(ctx_count)]
+
+
+def ring_index(ctx_pos, ctx_count):
+    half = ctx_count // Y_HI
+    z = ctx_pos // Y_HI
+    return jnp.where(ctx_pos % Y_HI == 0, z, ctx_count - 1 - z)
+
+
+def owner_of(ring_pos, ctx_count):
+    half = ctx_count // Y_HI
+    return jnp.where(ring_pos < half, Y_HI * ring_pos, Y_HI * (ctx_count - 1 - ring_pos) + 1)
+
+
+def from_ahead(value, ctx_count):
+    order = ring_of(ctx_count)
+    pairs = [(order[p], order[(p - 1) % ctx_count]) for p in range(ctx_count)]
+    return lax.ppermute(value, "ctx", pairs)
 
 
 def live_region(block_mask, query_start, tok_rows, key_start, key_count):
@@ -55,33 +78,46 @@
     grad_rows = out_grad.shape[0]
     pieces = out_grad.reshape(grad_rows, tp_count, col_width)
     own_grad = lax.all_to_all(pieces, "tp", split_axis=1, concat_axis=0, tiled=True)
-    own_grad = own_grad.reshape(tok_rows, col_width)
     queries = query_rows.reshape(tok_rows, heads_local, HEAD_SIZE)
     out_grads = own_grad.reshape(tok_rows, heads_local, HEAD_SIZE)
     outputs = attn_out.reshape(tok_rows, heads_local, HEAD_SIZE)
     row_delta = jnp.sum(out_grads.astype(jnp.float32) * outputs.astype(jnp.float32), axis=2).T
     query_start = ctx_pos * tok_rows
-    key_values = jnp.concatenate([key_matrix, value_matrix], axis=1)
-    all_key_values = lax.all_gather(key_values, "ctx", axis=0, tiled=True)
-    zero_query = jnp.zeros((tok_rows, heads_local, HEAD_SIZE), jnp.float32)
-    zero_partial = jnp.zeros((ctx_count * tok_rows, 2 * HEAD_SIZE), jnp.float32)
+    ring_pos = ring_index(ctx_pos, ctx_count)
 
-    def visit_span(span, carried):
-        query_acc, partial = carried
-        key_start = span * tok_rows
-        span_kv = lax.dynamic_slice_in_dim(all_key_values, key_start, tok_rows, 0)
-        keys_part = span_kv[:, :HEAD_SIZE]
-        values_part = span_kv[:, HEAD_SIZE:]
+    def terms(key_values, turn):
+        owner = owner_of((ring_pos + turn) % ctx_count, ctx_count)
+        key_start = owner * tok_rows
         live_mask = live_region(block_mask, query_start, tok_rows, key_start, tok_rows)
         query_term, key_term, value_term = contract(
-            queries, out_grads, row_delta, log_sums, keys_part, values_part, live_mask
+            queries,
+            out_grads,
+            row_delta,
+            log_sums,
+            key_values[:, :HEAD_SIZE],
+            key_values[:, HEAD_SIZE:],
+            live_mask,
         )
-        span_partial = jnp.concatenate([key_term, value_term], axis=1)
-        partial = lax.dynamic_update_slice_in_dim(partial, span_partial, key_start, 0)
-        return (query_acc + query_term, partial)
+        return query_term, jnp.concatenate([key_term, value_term], axis=1)
 
-    query_acc, partial = lax.fori_loop(0, ctx_pos + 1, visit_span, (zero_query, zero_partial))
-    summed = lax.psum_scatter(partial, "ctx", scatter_dimension=0, tiled=True)
+    key_values = jnp.concatenate([key_matrix, value_matrix], axis=1)
+    next_kv = from_ahead(key_values, ctx_count)
+    query_acc, pending = terms(key_values, 0)
+
+    def visit_turn(turn, carried):
+        key_values, query_acc, pending = carried
+        received = from_ahead(pending, ctx_count)
+        next_kv = from_ahead(key_values, ctx_count)
+        query_term, kv_term = terms(key_values, turn)
+        return (next_kv, query_acc + query_term, received + kv_term)
+
+    key_values, query_acc, pending = lax.fori_loop(
+        1, ctx_count - 1, visit_turn, (next_kv, query_acc, pending)
+    )
+    received = from_ahead(pending, ctx_count)
+    query_term, kv_term = terms(key_values, ctx_count - 1)
+    query_acc = query_acc + query_term
+    summed = from_ahead(received + kv_term, ctx_count)
     logit_scale = 1.0 / math.sqrt(HEAD_SIZE)
     query_grad = (query_acc * logit_scale).reshape(tok_rows, col_width).astype(jnp.bfloat16)
     key_gradient = (summed[:, :HEAD_SIZE] * logit_scale).astype(jnp.bfloat16)

time: 432 us -> 201 us (0.47)
  waiting for transfers between devices: 393 us -> 59.6 us
  starting transfers between devices: 3.55 us -> 63.8 us
  matrix products: 4.83 us -> 44.9 us
  between operations: 14.2 us -> 1.04 us
  local copies, waits for them, and re-layouts: 9.4 us -> 20.9 us
    reduce_scatter x1 -> x0, waiting for transfers between devices: 310 us -> none  [local(): summed = lax.psum_scatter(partial, 'ctx', scatter_dimension=0, tiled=True)]
    all_gather x1 -> x0, waiting for transfers between devices: 75.2 us -> none  [local(): all_key_values = lax.all_gather(key_values, 'ctx', axis=0, tiled=True)]
    ppermute x0 -> x31, starting transfers between devices: none -> 60.3 us  [from_ahead(): return lax.ppermute(value, 'ctx', pairs)]
    ppermute x0 -> x31, waiting for transfers between devices: none -> 55.7 us  [from_ahead(): return lax.ppermute(value, 'ctx', pairs)]
    dynamic_slice x2 -> x28, local copies, waits for them, and re-layouts: 0.87 us -> 12.3 us  [live_region(): lax.dynamic_slice(block_mask, (query_start // BLK, key_start // BLK), (to...]
    dot_general x1 -> x16, matrix products: 1.42 us -> 10.5 us  [contract(): jnp.einsum('igd,jd->gij', queries, keys_part, preferred_element_type=jnp....]
    dot_general x1 -> x16, matrix products: 0.48 us -> 9.36 us  [contract(): jnp.einsum('gij,igd->jd', probabilities.astype(jnp.bfloat16), out_grads,...]
    dot_general x1 -> x16, matrix products: 1.19 us -> 9.75 us  [contract(): jnp.einsum('gij,jd->igd', dscore, keys_part, preferred_element_type=jnp.f...]
  transfers between devices with their start and end apart: 3 -> 32, of which waited for: 3 -> 17; matrix products, arithmetic and copies ran while one was open for 1% -> 34% of each run, Pallas kernels for 0% -> 0%
where the time goes in v2:
time: 201 us; the launch traced here: 198 us
  starting transfers between devices  63.8 us (32%)
  waiting for transfers between devices  59.6 us (30%)
  matrix products  44.9 us (22%)
  local copies, waits for them, and re-layouts  20.9 us (10%)
  other arithmetic  6.32 us (3%)
    ppermute x31, starting transfers between devices, from_ahead(): return lax.ppermute(value, 'ctx', pairs)  60.3 us
    ppermute x31, waiting for transfers between devices, from_ahead(): return lax.ppermute(value, 'ctx', pairs)  55.7 us
    dynamic_slice x28, local copies, waits for them, and re-layouts, live_region(): lax.dynamic_slice(block_mask, (query_start // BLK, key_start // BLK), (to...  12.3 us
    dot_general x16, matrix products, contract(): jnp.einsum('igd,jd->gij', queries, keys_part, preferred_element_type=jnp....  10.5 us
    dot_general x16, matrix products, contract(): jnp.einsum('gij,jd->igd', dscore, keys_part, preferred_element_type=jnp.f...  9.75 us
    dot_general x16, matrix products, contract(): jnp.einsum('gij,igd->jd', probabilities.astype(jnp.bfloat16), out_grads,...  9.36 us
    dot_general x16, matrix products, contract(): jnp.einsum('igd,jd->gij', out_grads, values_part, preferred_element_type=...  7.76 us
    dot_general x16, matrix products, contract(): jnp.einsum('gij,igd->jd', dscore, queries, preferred_element_type=jnp.flo...  7.57 us
  transfers between devices with their start and end apart: 32, of which 17 were waited for; matrix products, arithmetic and copies ran while one was open for 34% of the time, Pallas kernels for 0%

profile of v2, /device:TPU:4, one launch (start us, length us, event | category | flops | bytes accessed | tf_op | source)
XLA Modules:
  0.0 198.1 jit_solution(15610170460860256305)
XLA Ops:
  0.6 1.0 pad_maximum_fusion.1
  1.6 3.3 %collective-permute-start.2 = (bf16[256,256]{1,0:T(8,128)(2,1)S(1)}, bf16[256,256]{1,0:T(8,128)(2,1)S(1)}, u32[]{:S(2)}, u32[]{:S(2)}) collective-permute-start(bf16[256,256]{1,0:T(8,128)(2,1)S(1)} %pad_maximum_fusion.1), channel_id=1, source_target_pairs={{0,4},{8,0},{16,8},{24,16},{32,24},{40,32},{48,40},{56,48},{60,56}... | collective-permute-start | bytes 393224 | tf_op jit(solution)/shard_map/ppermute | solution.py:32
  4.9 1.9 copy.127
  6.8 3.5 %all-to-all-start = ((bf16[64,4,1024]{2,0,1:T(8,128)(2,1)}), bf16[64,4,1024]{2,0,1:T(8,128)(2,1)S(1)}, u32[]{:S(2)}, u32[]{:S(2)}) async-start(bf16[64,4,1024]{2,0,1:T(8,128)(2,1)} %bitcast.144), calls=%async_computation | async-start | bytes 1048576 | tf_op jit(solution)/shard_map/all_to_all | solution.py:80
  10.5 0.9 dynamic-slice_compare_fusion
  12.5 0.8 fusion.25
  13.3 1.9 fusion.20
  15.2 3.9 %all-to-all-done = bf16[64,4,1024]{2,0,1:T(8,128)(2,1)S(1)} async-done(((bf16[64,4,1024]{2,0,1:T(8,128)(2,1)}), bf16[64,4,1024]{2,0,1:T(8,128)(2,1)S(1)}, u32[]{:S(2)}, u32[]{:S(2)}) %all-to-all-start) | async-done | bytes 524320 | tf_op jit(solution)/shard_map/all_to_all | solution.py:80
  19.9 2.2 %convolution_bitcast_fusion.7 = f32[256,128]{0,1:T(8,128)S(1)} fusion(bf16[256,8,128]{0,2,1:T(8,128)(2,1)S(1)} %copy.81, f32[8,256,256]{1,2,0:T(8,128)} %fusion.20), kind=kOutput, calls=%fused_computation.49 | convolution fusion | flops 134742016 | bytes 2752512 | tf_op jit(solution)/shard_map/gij,igd->jd/dot_general | solution.py:62
  23.7 155.6 %while.20 = (s32[]{:T(128)}, bf16[256,256]{1,0:T(8,128)(2,1)S(1)}, f32[256,8,128]{2,0,1:T(8,128)S(1)}, f32[256,256]{0,1:T(8,128)S(1)}, s32[]{:T(128)}, /*index=5...) while((s32[]{:T(128)}, bf16[256,256]{1,0:T(8,128)(2,1)S(1)}, ...), condition=%wide.region_2.3_spmd, body=%wide.region_1.2_spmd.sunk | while | flops 675553344 | bytes 16870148 | solution.py:114
  23.7 2.0 %collective-permute-start = (bf16[256,256]{1,0:T(8,128)(2,1)S(1)}, bf16[256,256]{1,0:T(8,128)(2,1)S(1)}, u32[]{:S(2)}, u32[]{:S(2)}) collective-permute-start(bf16[256,256]{1,0:T(8,128)(2,1)S(1)} %copy.137), channel_id=1, source_target_pairs={{0,4},{8,0},{16,8},{24,16},{32,24},{40,32},{48,40},{56,48},{60,56}... | collective-permute-start | bytes 393224 | tf_op jit(solution)/shard_map/while/body/eval_jaxpr/ppermute | solution.py:32
  25.7 1.9 collective-permute-start.1
  27.6 0.8 dynamic_slice.22
  30.8 0.6 fusion.80
  31.4 3.0 %collective-permute-done.1 = f32[256,256]{0,1:T(8,128)S(1)} collective-permute-done((f32[256,256]{0,1:T(8,128)S(1)}, f32[256,256]{0,1:T(8,128)S(1)}, u32[]{:S(2)}, u32[]{:S(2)}) %collective-permute-start.1) | collective-permute-done | bytes 262176 | tf_op jit(solution)/shard_map/while/body/eval_jaxpr/ppermute | solution.py:32
  34.5 3.5 %collective-permute-start = (bf16[256,256]{1,0:T(8,128)(2,1)S(1)}, bf16[256,256]{1,0:T(8,128)(2,1)S(1)}, u32[]{:S(2)}, u32[]{:S(2)}) collective-permute-start(bf16[256,256]{1,0:T(8,128)(2,1)S(1)} %copy.137), channel_id=1, source_target_pairs={{0,4},{8,0},{16,8},{24,16},{32,24},{40,32},{48,40},{56,48},{60,56}... | collective-permute-start | bytes 393224 | tf_op jit(solution)/shard_map/while/body/eval_jaxpr/ppermute | solution.py:32
  38.4 0.8 dynamic_slice.22
  41.6 0.6 fusion.80
  42.2 3.3 %collective-permute-done.1 = f32[256,256]{0,1:T(8,128)S(1)} collective-permute-done((f32[256,256]{0,1:T(8,128)S(1)}, f32[256,256]{0,1:T(8,128)S(1)}, u32[]{:S(2)}, u32[]{:S(2)}) %collective-permute-start.1) | collective-permute-done | bytes 262176 | tf_op jit(solution)/shard_map/while/body/eval_jaxpr/ppermute | solution.py:32
  45.6 4.1 %collective-permute-start = (bf16[256,256]{1,0:T(8,128)(2,1)S(1)}, bf16[256,256]{1,0:T(8,128)(2,1)S(1)}, u32[]{:S(2)}, u32[]{:S(2)}) collective-permute-start(bf16[256,256]{1,0:T(8,128)(2,1)S(1)} %copy.137), channel_id=1, source_target_pairs={{0,4},{8,0},{16,8},{24,16},{32,24},{40,32},{48,40},{56,48},{60,56}... | collective-permute-start | bytes 393224 | tf_op jit(solution)/shard_map/while/body/eval_jaxpr/ppermute | solution.py:32
  49.7 0.8 dynamic_slice.22
  53.5 2.7 %collective-permute-done.1 = f32[256,256]{0,1:T(8,128)S(1)} collective-permute-done((f32[256,256]{0,1:T(8,128)S(1)}, f32[256,256]{0,1:T(8,128)S(1)}, u32[]{:S(2)}, u32[]{:S(2)}) %collective-permute-start.1) | collective-permute-done | bytes 262176 | tf_op jit(solution)/shard_map/while/body/eval_jaxpr/ppermute | solution.py:32
  56.3 4.0 %collective-permute-start = (bf16[256,256]{1,0:T(8,128)(2,1)S(1)}, bf16[256,256]{1,0:T(8,128)(2,1)S(1)}, u32[]{:S(2)}, u32[]{:S(2)}) collective-permute-start(bf16[256,256]{1,0:T(8,128)(2,1)S(1)} %copy.137), channel_id=1, source_target_pairs={{0,4},{8,0},{16,8},{24,16},{32,24},{40,32},{48,40},{56,48},{60,56}... | collective-permute-start | bytes 393224 | tf_op jit(solution)/shard_map/while/body/eval_jaxpr/ppermute | solution.py:32
  60.4 0.8 dynamic_slice.22
  64.2 2.7 %collective-permute-done.1 = f32[256,256]{0,1:T(8,128)S(1)} collective-permute-done((f32[256,256]{0,1:T(8,128)S(1)}, f32[256,256]{0,1:T(8,128)S(1)}, u32[]{:S(2)}, u32[]{:S(2)}) %collective-permute-start.1) | collective-permute-done | bytes 262176 | tf_op jit(solution)/shard_map/while/body/eval_jaxpr/ppermute | solution.py:32
  67.0 3.1 %collective-permute-start = (bf16[256,256]{1,0:T(8,128)(2,1)S(1)}, bf16[256,256]{1,0:T(8,128)(2,1)S(1)}, u32[]{:S(2)}, u32[]{:S(2)}) collective-permute-start(bf16[256,256]{1,0:T(8,128)(2,1)S(1)} %copy.137), channel_id=1, source_target_pairs={{0,4},{8,0},{16,8},{24,16},{32,24},{40,32},{48,40},{56,48},{60,56}... | collective-permute-start | bytes 393224 | tf_op jit(solution)/shard_map/while/body/eval_jaxpr/ppermute | solution.py:32
  70.2 0.8 dynamic_slice.22
  74.0 4.0 %collective-permute-done.1 = f32[256,256]{0,1:T(8,128)S(1)} collective-permute-done((f32[256,256]{0,1:T(8,128)S(1)}, f32[256,256]{0,1:T(8,128)S(1)}, u32[]{:S(2)}, u32[]{:S(2)}) %collective-permute-start.1) | collective-permute-done | bytes 262176 | tf_op jit(solution)/shard_map/while/body/eval_jaxpr/ppermute | solution.py:32
  78.0 2.1 %collective-permute-start = (bf16[256,256]{1,0:T(8,128)(2,1)S(1)}, bf16[256,256]{1,0:T(8,128)(2,1)S(1)}, u32[]{:S(2)}, u32[]{:S(2)}) collective-permute-start(bf16[256,256]{1,0:T(8,128)(2,1)S(1)} %copy.137), channel_id=1, source_target_pairs={{0,4},{8,0},{16,8},{24,16},{32,24},{40,32},{48,40},{56,48},{60,56}... | collective-permute-start | bytes 393224 | tf_op jit(solution)/shard_map/while/body/eval_jaxpr/ppermute | solution.py:32
  80.3 0.8 dynamic_slice.22
  84.1 4.9 %collective-permute-done.1 = f32[256,256]{0,1:T(8,128)S(1)} collective-permute-done((f32[256,256]{0,1:T(8,128)S(1)}, f32[256,256]{0,1:T(8,128)S(1)}, u32[]{:S(2)}, u32[]{:S(2)}) %collective-permute-start.1) | collective-permute-done | bytes 262176 | tf_op jit(solution)/shard_map/while/body/eval_jaxpr/ppermute | solution.py:32
  89.1 2.3 %collective-permute-start = (bf16[256,256]{1,0:T(8,128)(2,1)S(1)}, bf16[256,256]{1,0:T(8,128)(2,1)S(1)}, u32[]{:S(2)}, u32[]{:S(2)}) collective-permute-start(bf16[256,256]{1,0:T(8,128)(2,1)S(1)} %copy.137), channel_id=1, source_target_pairs={{0,4},{8,0},{16,8},{24,16},{32,24},{40,32},{48,40},{56,48},{60,56}... | collective-permute-start | bytes 393224 | tf_op jit(solution)/shard_map/while/body/eval_jaxpr/ppermute | solution.py:32
  91.6 0.8 dynamic_slice.22
  95.4 5.2 %collective-permute-done.1 = f32[256,256]{0,1:T(8,128)S(1)} collective-permute-done((f32[256,256]{0,1:T(8,128)S(1)}, f32[256,256]{0,1:T(8,128)S(1)}, u32[]{:S(2)}, u32[]{:S(2)}) %collective-permute-start.1) | collective-permute-done | bytes 262176 | tf_op jit(solution)/shard_map/while/body/eval_jaxpr/ppermute | solution.py:32
  100.7 3.0 %collective-permute-start = (bf16[256,256]{1,0:T(8,128)(2,1)S(1)}, bf16[256,256]{1,0:T(8,128)(2,1)S(1)}, u32[]{:S(2)}, u32[]{:S(2)}) collective-permute-start(bf16[256,256]{1,0:T(8,128)(2,1)S(1)} %copy.137), channel_id=1, source_target_pairs={{0,4},{8,0},{16,8},{24,16},{32,24},{40,32},{48,40},{56,48},{60,56}... | collective-permute-start | bytes 393224 | tf_op jit(solution)/shard_map/while/body/eval_jaxpr/ppermute | solution.py:32
  103.8 0.8 dynamic_slice.22
  107.5 5.4 %collective-permute-done.1 = f32[256,256]{0,1:T(8,128)S(1)} collective-permute-done((f32[256,256]{0,1:T(8,128)S(1)}, f32[256,256]{0,1:T(8,128)S(1)}, u32[]{:S(2)}, u32[]{:S(2)}) %collective-permute-start.1) | collective-permute-done | bytes 262176 | tf_op jit(solution)/shard_map/while/body/eval_jaxpr/ppermute | solution.py:32
  113.0 4.1 %collective-permute-start = (bf16[256,256]{1,0:T(8,128)(2,1)S(1)}, bf16[256,256]{1,0:T(8,128)(2,1)S(1)}, u32[]{:S(2)}, u32[]{:S(2)}) collective-permute-start(bf16[256,256]{1,0:T(8,128)(2,1)S(1)} %copy.137), channel_id=1, source_target_pairs={{0,4},{8,0},{16,8},{24,16},{32,24},{40,32},{48,40},{56,48},{60,56}... | collective-permute-start | bytes 393224 | tf_op jit(solution)/shard_map/while/body/eval_jaxpr/ppermute | solution.py:32
  117.2 0.8 dynamic_slice.22
  120.9 4.8 %collective-permute-done.1 = f32[256,256]{0,1:T(8,128)S(1)} collective-permute-done((f32[256,256]{0,1:T(8,128)S(1)}, f32[256,256]{0,1:T(8,128)S(1)}, u32[]{:S(2)}, u32[]{:S(2)}) %collective-permute-start.1) | collective-permute-done | bytes 262176 | tf_op jit(solution)/shard_map/while/body/eval_jaxpr/ppermute | solution.py:32
  125.8 4.1 %collective-permute-start = (bf16[256,256]{1,0:T(8,128)(2,1)S(1)}, bf16[256,256]{1,0:T(8,128)(2,1)S(1)}, u32[]{:S(2)}, u32[]{:S(2)}) collective-permute-start(bf16[256,256]{1,0:T(8,128)(2,1)S(1)} %copy.137), channel_id=1, source_target_pairs={{0,4},{8,0},{16,8},{24,16},{32,24},{40,32},{48,40},{56,48},{60,56}... | collective-permute-start | bytes 393224 | tf_op jit(solution)/shard_map/while/body/eval_jaxpr/ppermute | solution.py:32
  130.0 0.8 dynamic_slice.22
  133.7 3.9 %collective-permute-done.1 = f32[256,256]{0,1:T(8,128)S(1)} collective-permute-done((f32[256,256]{0,1:T(8,128)S(1)}, f32[256,256]{0,1:T(8,128)S(1)}, u32[]{:S(2)}, u32[]{:S(2)}) %collective-permute-start.1) | collective-permute-done | bytes 262176 | tf_op jit(solution)/shard_map/while/body/eval_jaxpr/ppermute | solution.py:32
  137.8 4.1 %collective-permute-start = (bf16[256,256]{1,0:T(8,128)(2,1)S(1)}, bf16[256,256]{1,0:T(8,128)(2,1)S(1)}, u32[]{:S(2)}, u32[]{:S(2)}) collective-permute-start(bf16[256,256]{1,0:T(8,128)(2,1)S(1)} %copy.137), channel_id=1, source_target_pairs={{0,4},{8,0},{16,8},{24,16},{32,24},{40,32},{48,40},{56,48},{60,56}... | collective-permute-start | bytes 393224 | tf_op jit(solution)/shard_map/while/body/eval_jaxpr/ppermute | solution.py:32
  141.9 0.8 dynamic_slice.22
  145.7 3.0 %collective-permute-done.1 = f32[256,256]{0,1:T(8,128)S(1)} collective-permute-done((f32[256,256]{0,1:T(8,128)S(1)}, f32[256,256]{0,1:T(8,128)S(1)}, u32[]{:S(2)}, u32[]{:S(2)}) %collective-permute-start.1) | collective-permute-done | bytes 262176 | tf_op jit(solution)/shard_map/while/body/eval_jaxpr/ppermute | solution.py:32
  148.8 4.1 %collective-permute-start = (bf16[256,256]{1,0:T(8,128)(2,1)S(1)}, bf16[256,256]{1,0:T(8,128)(2,1)S(1)}, u32[]{:S(2)}, u32[]{:S(2)}) collective-permute-start(bf16[256,256]{1,0:T(8,128)(2,1)S(1)} %copy.137), channel_id=1, source_target_pairs={{0,4},{8,0},{16,8},{24,16},{32,24},{40,32},{48,40},{56,48},{60,56}... | collective-permute-start | bytes 393224 | tf_op jit(solution)/shard_map/while/body/eval_jaxpr/ppermute | solution.py:32
  153.0 0.8 dynamic_slice.22
  156.7 2.7 %collective-permute-done.1 = f32[256,256]{0,1:T(8,128)S(1)} collective-permute-done((f32[256,256]{0,1:T(8,128)S(1)}, f32[256,256]{0,1:T(8,128)S(1)}, u32[]{:S(2)}, u32[]{:S(2)}) %collective-permute-start.1) | collective-permute-done | bytes 262176 | tf_op jit(solution)/shard_map/while/body/eval_jaxpr/ppermute | solution.py:32
  159.5 3.4 %collective-permute-start = (bf16[256,256]{1,0:T(8,128)(2,1)S(1)}, bf16[256,256]{1,0:T(8,128)(2,1)S(1)}, u32[]{:S(2)}, u32[]{:S(2)}) collective-permute-start(bf16[256,256]{1,0:T(8,128)(2,1)S(1)} %copy.137), channel_id=1, source_target_pairs={{0,4},{8,0},{16,8},{24,16},{32,24},{40,32},{48,40},{56,48},{60,56}... | collective-permute-start | bytes 393224 | tf_op jit(solution)/shard_map/while/body/eval_jaxpr/ppermute | solution.py:32
  163.1 0.8 dynamic_slice.22
  166.9 2.5 %collective-permute-done.1 = f32[256,256]{0,1:T(8,128)S(1)} collective-permute-done((f32[256,256]{0,1:T(8,128)S(1)}, f32[256,256]{0,1:T(8,128)S(1)}, u32[]{:S(2)}, u32[]{:S(2)}) %collective-permute-start.1) | collective-permute-done | bytes 262176 | tf_op jit(solution)/shard_map/while/body/eval_jaxpr/ppermute | solution.py:32
  169.4 3.0 %collective-permute-start = (bf16[256,256]{1,0:T(8,128)(2,1)S(1)}, bf16[256,256]{1,0:T(8,128)(2,1)S(1)}, u32[]{:S(2)}, u32[]{:S(2)}) collective-permute-start(bf16[256,256]{1,0:T(8,128)(2,1)S(1)} %copy.137), channel_id=1, source_target_pairs={{0,4},{8,0},{16,8},{24,16},{32,24},{40,32},{48,40},{56,48},{60,56}... | collective-permute-start | bytes 393224 | tf_op jit(solution)/shard_map/while/body/eval_jaxpr/ppermute | solution.py:32
  172.5 0.8 dynamic_slice.22
  176.3 2.9 %collective-permute-done.1 = f32[256,256]{0,1:T(8,128)S(1)} collective-permute-done((f32[256,256]{0,1:T(8,128)S(1)}, f32[256,256]{0,1:T(8,128)S(1)}, u32[]{:S(2)}, u32[]{:S(2)}) %collective-permute-start.1) | collective-permute-done | bytes 262176 | tf_op jit(solution)/shard_map/while/body/eval_jaxpr/ppermute | solution.py:32
  180.4 1.4 fusion.14
  181.8 2.8 %collective-permute-start.3 = (f32[256,256]{0,1:T(8,128)}, f32[256,256]{0,1:T(8,128)S(1)}, u32[]{:S(2)}, u32[]{:S(2)}) collective-permute-start(f32[256,256]{0,1:T(8,128)} %copy-done.6), channel_id=1, source_target_pairs={{0,4},{8,0},{16,8},{24,16},{32,24},{40,32},{48,40},{56,48},{60,56}... | collective-permute-start | bytes 786440 | tf_op jit(solution)/shard_map/ppermute | solution.py:32
  184.5 1.3 copy.90
  186.7 2.1 %collective-permute-done.3 = f32[256,256]{0,1:T(8,128)S(1)} collective-permute-done((f32[256,256]{0,1:T(8,128)}, f32[256,256]{0,1:T(8,128)S(1)}, u32[]{:S(2)}, u32[]{:S(2)}) %collective-permute-start.3) | collective-permute-done | bytes 262176 | tf_op jit(solution)/shard_map/ppermute | solution.py:32
  188.8 4.0 %collective-permute-start.4 = (f32[256,256]{0,1:T(8,128)S(1)}, f32[256,256]{0,1:T(8,128)S(1)}, u32[]{:S(2)}, u32[]{:S(2)}) collective-permute-start(f32[256,256]{0,1:T(8,128)S(1)} %maximum_add_fusion.1), channel_id=1, source_target_pairs={{0,4},{8,0},{16,8},{24,16},{32,24},{40,32},{48,40},{56,48},{60,56}... | collective-permute-start | bytes 786440 | tf_op jit(solution)/shard_map/ppermute | solution.py:32
  192.9 1.0 copy.94
  193.9 2.7 %collective-permute-done.4 = f32[256,256]{0,1:T(8,128)S(1)} collective-permute-done((f32[256,256]{0,1:T(8,128)S(1)}, f32[256,256]{0,1:T(8,128)S(1)}, u32[]{:S(2)}, u32[]{:S(2)}) %collective-permute-start.4) | collective-permute-done | bytes 262176 | tf_op jit(solution)/shard_map/ppermute | solution.py:32
  196.7 0.7 copy.95
  197.4 0.7 copy.96
  (269 shorter events, 47.8 us)
Async XLA Ops:
  0.6 11.1 %copy-start.3 = (bf16[256,1024]{1,0:T(8,128)(2,1)S(1)}, bf16[256,1024]{1,0:T(8,128)(2,1)}, u32[]{:S(2)}) copy-start(bf16[256,1024]{1,0:T(8,128)(2,1)} %param.9) | copy-start | bytes 1572868
  0.6 11.3 %copy-start.4 = (bf16[256,1024]{1,0:T(8,128)(2,1)S(1)}, bf16[256,1024]{1,0:T(8,128)(2,1)}, u32[]{:S(2)}) copy-start(bf16[256,1024]{1,0:T(8,128)(2,1)} %param.12) | copy-start | bytes 1572868
  1.6 22.0 %collective-permute-start.2 = (bf16[256,256]{1,0:T(8,128)(2,1)S(1)}, bf16[256,256]{1,0:T(8,128)(2,1)S(1)}, u32[]{:S(2)}, u32[]{:S(2)}) collective-permute-start(bf16[256,256]{1,0:T(8,128)(2,1)S(1)} %pad_maximum_fusion.1), channel_id=1, source_target_pairs={{0,4},{8,0},{16,8},{24,16},{32,24},{40,32},{48,40},{56,48},{60,56}... | collective-permute-start | bytes 393224 | tf_op jit(solution)/shard_map/ppermute | solution.py:32
  6.8 12.3 %all-to-all-start = ((bf16[64,4,1024]{2,0,1:T(8,128)(2,1)}), bf16[64,4,1024]{2,0,1:T(8,128)(2,1)S(1)}, u32[]{:S(2)}, u32[]{:S(2)}) async-start(bf16[64,4,1024]{2,0,1:T(8,128)(2,1)} %bitcast.144), calls=%async_computation | async-start | bytes 1048576 | tf_op jit(solution)/shard_map/all_to_all | solution.py:80
  10.3 3.1 %copy-start.7 = (bf16[256,128]{1,0:T(8,128)(2,1)S(1)}, bf16[256,128]{1,0:T(8,128)(2,1)}, u32[]{:S(2)}) copy-start(bf16[256,128]{1,0:T(8,128)(2,1)} %param.10) | copy-start | bytes 196612
  10.3 3.1 %copy-start.9 = (f32[8,256]{1,0:T(8,128)S(1)}, f32[8,256]{1,0:T(8,128)}, u32[]{:S(2)}) copy-start(f32[8,256]{1,0:T(8,128)} %param.14) | copy-start | bytes 24580
  19.5 2.7 %copy-start.5 = (bf16[256,128]{1,0:T(8,128)(2,1)S(1)}, bf16[256,128]{1,0:T(8,128)(2,1)}, u32[]{:S(2)}) copy-start(bf16[256,128]{1,0:T(8,128)(2,1)} %param.11) | copy-start | bytes 196612
  19.9 2.2 %copy-start.1 = (f32[8,256,256]{1,2,0:T(8,128)S(1)}, f32[8,256,256]{1,2,0:T(8,128)}, u32[]{:S(2)}) copy-start(f32[8,256,256]{1,2,0:T(8,128)} %fusion.20) | copy-start | bytes 6291460
  23.6 155.7 %copy-start.8 = (pred[256,256]{0,1:T(8,128)(4,1)S(1)}, pred[256,256]{0,1:T(8,128)(4,1)}, u32[]{:S(2)}) copy-start(pred[256,256]{0,1:T(8,128)(4,1)} %get-tuple-element.454) | copy-start | bytes 196612
  23.7 10.8 %collective-permute-start = (bf16[256,256]{1,0:T(8,128)(2,1)S(1)}, bf16[256,256]{1,0:T(8,128)(2,1)S(1)}, u32[]{:S(2)}, u32[]{:S(2)}) collective-permute-start(bf16[256,256]{1,0:T(8,128)(2,1)S(1)} %copy.137), channel_id=1, source_target_pairs={{0,4},{8,0},{16,8},{24,16},{32,24},{40,32},{48,40},{56,48},{60,56}... | collective-permute-start | bytes 393224 | tf_op jit(solution)/shard_map/while/body/eval_jaxpr/ppermute | solution.py:32
  25.7 8.7 %collective-permute-start.1 = (f32[256,256]{0,1:T(8,128)S(1)}, f32[256,256]{0,1:T(8,128)S(1)}, u32[]{:S(2)}, u32[]{:S(2)}) collective-permute-start(f32[256,256]{0,1:T(8,128)S(1)} %get-tuple-element.571), channel_id=1, source_target_pairs={{0,4},{8,0},{16,8},{24,16},{32,24},{40,32},{48,40},{56,48},{60,56}... | collective-permute-start | bytes 786440 | tf_op jit(solution)/shard_map/while/body/eval_jaxpr/ppermute | solution.py:32
  34.5 11.0 %collective-permute-start = (bf16[256,256]{1,0:T(8,128)(2,1)S(1)}, bf16[256,256]{1,0:T(8,128)(2,1)S(1)}, u32[]{:S(2)}, u32[]{:S(2)}) collective-permute-start(bf16[256,256]{1,0:T(8,128)(2,1)S(1)} %copy.137), channel_id=1, source_target_pairs={{0,4},{8,0},{16,8},{24,16},{32,24},{40,32},{48,40},{56,48},{60,56}... | collective-permute-start | bytes 393224 | tf_op jit(solution)/shard_map/while/body/eval_jaxpr/ppermute | solution.py:32
  38.0 7.5 %collective-permute-start.1 = (f32[256,256]{0,1:T(8,128)S(1)}, f32[256,256]{0,1:T(8,128)S(1)}, u32[]{:S(2)}, u32[]{:S(2)}) collective-permute-start(f32[256,256]{0,1:T(8,128)S(1)} %get-tuple-element.571), channel_id=1, source_target_pairs={{0,4},{8,0},{16,8},{24,16},{32,24},{40,32},{48,40},{56,48},{60,56}... | collective-permute-start | bytes 786440 | tf_op jit(solution)/shard_map/while/body/eval_jaxpr/ppermute | solution.py:32
  45.6 10.7 %collective-permute-start = (bf16[256,256]{1,0:T(8,128)(2,1)S(1)}, bf16[256,256]{1,0:T(8,128)(2,1)S(1)}, u32[]{:S(2)}, u32[]{:S(2)}) collective-permute-start(bf16[256,256]{1,0:T(8,128)(2,1)S(1)} %copy.137), channel_id=1, source_target_pairs={{0,4},{8,0},{16,8},{24,16},{32,24},{40,32},{48,40},{56,48},{60,56}... | collective-permute-start | bytes 393224 | tf_op jit(solution)/shard_map/while/body/eval_jaxpr/ppermute | solution.py:32
  49.6 6.6 %collective-permute-start.1 = (f32[256,256]{0,1:T(8,128)S(1)}, f32[256,256]{0,1:T(8,128)S(1)}, u32[]{:S(2)}, u32[]{:S(2)}) collective-permute-start(f32[256,256]{0,1:T(8,128)S(1)} %get-tuple-element.571), channel_id=1, source_target_pairs={{0,4},{8,0},{16,8},{24,16},{32,24},{40,32},{48,40},{56,48},{60,56}... | collective-permute-start | bytes 786440 | tf_op jit(solution)/shard_map/while/body/eval_jaxpr/ppermute | solution.py:32
  56.3 10.7 %collective-permute-start = (bf16[256,256]{1,0:T(8,128)(2,1)S(1)}, bf16[256,256]{1,0:T(8,128)(2,1)S(1)}, u32[]{:S(2)}, u32[]{:S(2)}) collective-permute-start(bf16[256,256]{1,0:T(8,128)(2,1)S(1)} %copy.137), channel_id=1, source_target_pairs={{0,4},{8,0},{16,8},{24,16},{32,24},{40,32},{48,40},{56,48},{60,56}... | collective-permute-start | bytes 393224 | tf_op jit(solution)/shard_map/while/body/eval_jaxpr/ppermute | solution.py:32
  60.3 6.6 %collective-permute-start.1 = (f32[256,256]{0,1:T(8,128)S(1)}, f32[256,256]{0,1:T(8,128)S(1)}, u32[]{:S(2)}, u32[]{:S(2)}) collective-permute-start(f32[256,256]{0,1:T(8,128)S(1)} %get-tuple-element.571), channel_id=1, source_target_pairs={{0,4},{8,0},{16,8},{24,16},{32,24},{40,32},{48,40},{56,48},{60,56}... | collective-permute-start | bytes 786440 | tf_op jit(solution)/shard_map/while/body/eval_jaxpr/ppermute | solution.py:32
  67.0 11.0 %collective-permute-start = (bf16[256,256]{1,0:T(8,128)(2,1)S(1)}, bf16[256,256]{1,0:T(8,128)(2,1)S(1)}, u32[]{:S(2)}, u32[]{:S(2)}) collective-permute-start(bf16[256,256]{1,0:T(8,128)(2,1)S(1)} %copy.137), channel_id=1, source_target_pairs={{0,4},{8,0},{16,8},{24,16},{32,24},{40,32},{48,40},{56,48},{60,56}... | collective-permute-start | bytes 393224 | tf_op jit(solution)/shard_map/while/body/eval_jaxpr/ppermute | solution.py:32
  70.1 7.9 %collective-permute-start.1 = (f32[256,256]{0,1:T(8,128)S(1)}, f32[256,256]{0,1:T(8,128)S(1)}, u32[]{:S(2)}, u32[]{:S(2)}) collective-permute-start(f32[256,256]{0,1:T(8,128)S(1)} %get-tuple-element.571), channel_id=1, source_target_pairs={{0,4},{8,0},{16,8},{24,16},{32,24},{40,32},{48,40},{56,48},{60,56}... | collective-permute-start | bytes 786440 | tf_op jit(solution)/shard_map/while/body/eval_jaxpr/ppermute | solution.py:32
  78.0 11.0 %collective-permute-start = (bf16[256,256]{1,0:T(8,128)(2,1)S(1)}, bf16[256,256]{1,0:T(8,128)(2,1)S(1)}, u32[]{:S(2)}, u32[]{:S(2)}) collective-permute-start(bf16[256,256]{1,0:T(8,128)(2,1)S(1)} %copy.137), channel_id=1, source_target_pairs={{0,4},{8,0},{16,8},{24,16},{32,24},{40,32},{48,40},{56,48},{60,56}... | collective-permute-start | bytes 393224 | tf_op jit(solution)/shard_map/while/body/eval_jaxpr/ppermute | solution.py:32
  80.2 8.8 %collective-permute-start.1 = (f32[256,256]{0,1:T(8,128)S(1)}, f32[256,256]{0,1:T(8,128)S(1)}, u32[]{:S(2)}, u32[]{:S(2)}) collective-permute-start(f32[256,256]{0,1:T(8,128)S(1)} %get-tuple-element.571), channel_id=1, source_target_pairs={{0,4},{8,0},{16,8},{24,16},{32,24},{40,32},{48,40},{56,48},{60,56}... | collective-permute-start | bytes 786440 | tf_op jit(solution)/shard_map/while/body/eval_jaxpr/ppermute | solution.py:32
  89.1 11.6 %collective-permute-start = (bf16[256,256]{1,0:T(8,128)(2,1)S(1)}, bf16[256,256]{1,0:T(8,128)(2,1)S(1)}, u32[]{:S(2)}, u32[]{:S(2)}) collective-permute-start(bf16[256,256]{1,0:T(8,128)(2,1)S(1)} %copy.137), channel_id=1, source_target_pairs={{0,4},{8,0},{16,8},{24,16},{32,24},{40,32},{48,40},{56,48},{60,56}... | collective-permute-start | bytes 393224 | tf_op jit(solution)/shard_map/while/body/eval_jaxpr/ppermute | solution.py:32
  91.4 9.2 %collective-permute-start.1 = (f32[256,256]{0,1:T(8,128)S(1)}, f32[256,256]{0,1:T(8,128)S(1)}, u32[]{:S(2)}, u32[]{:S(2)}) collective-permute-start(f32[256,256]{0,1:T(8,128)S(1)} %get-tuple-element.571), channel_id=1, source_target_pairs={{0,4},{8,0},{16,8},{24,16},{32,24},{40,32},{48,40},{56,48},{60,56}... | collective-permute-start | bytes 786440 | tf_op jit(solution)/shard_map/while/body/eval_jaxpr/ppermute | solution.py:32
  100.7 12.3 %collective-permute-start = (bf16[256,256]{1,0:T(8,128)(2,1)S(1)}, bf16[256,256]{1,0:T(8,128)(2,1)S(1)}, u32[]{:S(2)}, u32[]{:S(2)}) collective-permute-start(bf16[256,256]{1,0:T(8,128)(2,1)S(1)} %copy.137), channel_id=1, source_target_pairs={{0,4},{8,0},{16,8},{24,16},{32,24},{40,32},{48,40},{56,48},{60,56}... | collective-permute-start | bytes 393224 | tf_op jit(solution)/shard_map/while/body/eval_jaxpr/ppermute | solution.py:32
  103.6 9.3 %collective-permute-start.1 = (f32[256,256]{0,1:T(8,128)S(1)}, f32[256,256]{0,1:T(8,128)S(1)}, u32[]{:S(2)}, u32[]{:S(2)}) collective-permute-start(f32[256,256]{0,1:T(8,128)S(1)} %get-tuple-element.571), channel_id=1, source_target_pairs={{0,4},{8,0},{16,8},{24,16},{32,24},{40,32},{48,40},{56,48},{60,56}... | collective-permute-start | bytes 786440 | tf_op jit(solution)/shard_map/while/body/eval_jaxpr/ppermute | solution.py:32
  113.0 12.8 %collective-permute-start = (bf16[256,256]{1,0:T(8,128)(2,1)S(1)}, bf16[256,256]{1,0:T(8,128)(2,1)S(1)}, u32[]{:S(2)}, u32[]{:S(2)}) collective-permute-start(bf16[256,256]{1,0:T(8,128)(2,1)S(1)} %copy.137), channel_id=1, source_target_pairs={{0,4},{8,0},{16,8},{24,16},{32,24},{40,32},{48,40},{56,48},{60,56}... | collective-permute-start | bytes 393224 | tf_op jit(solution)/shard_map/while/body/eval_jaxpr/ppermute | solution.py:32
  117.1 8.7 %collective-permute-start.1 = (f32[256,256]{0,1:T(8,128)S(1)}, f32[256,256]{0,1:T(8,128)S(1)}, u32[]{:S(2)}, u32[]{:S(2)}) collective-permute-start(f32[256,256]{0,1:T(8,128)S(1)} %get-tuple-element.571), channel_id=1, source_target_pairs={{0,4},{8,0},{16,8},{24,16},{32,24},{40,32},{48,40},{56,48},{60,56}... | collective-permute-start | bytes 786440 | tf_op jit(solution)/shard_map/while/body/eval_jaxpr/ppermute | solution.py:32
  125.8 11.9 %collective-permute-start = (bf16[256,256]{1,0:T(8,128)(2,1)S(1)}, bf16[256,256]{1,0:T(8,128)(2,1)S(1)}, u32[]{:S(2)}, u32[]{:S(2)}) collective-permute-start(bf16[256,256]{1,0:T(8,128)(2,1)S(1)} %copy.137), channel_id=1, source_target_pairs={{0,4},{8,0},{16,8},{24,16},{32,24},{40,32},{48,40},{56,48},{60,56}... | collective-permute-start | bytes 393224 | tf_op jit(solution)/shard_map/while/body/eval_jaxpr/ppermute | solution.py:32
  129.8 7.8 %collective-permute-start.1 = (f32[256,256]{0,1:T(8,128)S(1)}, f32[256,256]{0,1:T(8,128)S(1)}, u32[]{:S(2)}, u32[]{:S(2)}) collective-permute-start(f32[256,256]{0,1:T(8,128)S(1)} %get-tuple-element.571), channel_id=1, source_target_pairs={{0,4},{8,0},{16,8},{24,16},{32,24},{40,32},{48,40},{56,48},{60,56}... | collective-permute-start | bytes 786440 | tf_op jit(solution)/shard_map/while/body/eval_jaxpr/ppermute | solution.py:32
  137.8 11.0 %collective-permute-start = (bf16[256,256]{1,0:T(8,128)(2,1)S(1)}, bf16[256,256]{1,0:T(8,128)(2,1)S(1)}, u32[]{:S(2)}, u32[]{:S(2)}) collective-permute-start(bf16[256,256]{1,0:T(8,128)(2,1)S(1)} %copy.137), channel_id=1, source_target_pairs={{0,4},{8,0},{16,8},{24,16},{32,24},{40,32},{48,40},{56,48},{60,56}... | collective-permute-start | bytes 393224 | tf_op jit(solution)/shard_map/while/body/eval_jaxpr/ppermute | solution.py:32
  141.8 6.9 %collective-permute-start.1 = (f32[256,256]{0,1:T(8,128)S(1)}, f32[256,256]{0,1:T(8,128)S(1)}, u32[]{:S(2)}, u32[]{:S(2)}) collective-permute-start(f32[256,256]{0,1:T(8,128)S(1)} %get-tuple-element.571), channel_id=1, source_target_pairs={{0,4},{8,0},{16,8},{24,16},{32,24},{40,32},{48,40},{56,48},{60,56}... | collective-permute-start | bytes 786440 | tf_op jit(solution)/shard_map/while/body/eval_jaxpr/ppermute | solution.py:32
  148.8 10.7 %collective-permute-start = (bf16[256,256]{1,0:T(8,128)(2,1)S(1)}, bf16[256,256]{1,0:T(8,128)(2,1)S(1)}, u32[]{:S(2)}, u32[]{:S(2)}) collective-permute-start(bf16[256,256]{1,0:T(8,128)(2,1)S(1)} %copy.137), channel_id=1, source_target_pairs={{0,4},{8,0},{16,8},{24,16},{32,24},{40,32},{48,40},{56,48},{60,56}... | collective-permute-start | bytes 393224 | tf_op jit(solution)/shard_map/while/body/eval_jaxpr/ppermute | solution.py:32
  152.9 6.6 %collective-permute-start.1 = (f32[256,256]{0,1:T(8,128)S(1)}, f32[256,256]{0,1:T(8,128)S(1)}, u32[]{:S(2)}, u32[]{:S(2)}) collective-permute-start(f32[256,256]{0,1:T(8,128)S(1)} %get-tuple-element.571), channel_id=1, source_target_pairs={{0,4},{8,0},{16,8},{24,16},{32,24},{40,32},{48,40},{56,48},{60,56}... | collective-permute-start | bytes 786440 | tf_op jit(solution)/shard_map/while/body/eval_jaxpr/ppermute | solution.py:32
  159.5 9.9 %collective-permute-start = (bf16[256,256]{1,0:T(8,128)(2,1)S(1)}, bf16[256,256]{1,0:T(8,128)(2,1)S(1)}, u32[]{:S(2)}, u32[]{:S(2)}) collective-permute-start(bf16[256,256]{1,0:T(8,128)(2,1)S(1)} %copy.137), channel_id=1, source_target_pairs={{0,4},{8,0},{16,8},{24,16},{32,24},{40,32},{48,40},{56,48},{60,56}... | collective-permute-start | bytes 393224 | tf_op jit(solution)/shard_map/while/body/eval_jaxpr/ppermute | solution.py:32
  163.0 6.4 %collective-permute-start.1 = (f32[256,256]{0,1:T(8,128)S(1)}, f32[256,256]{0,1:T(8,128)S(1)}, u32[]{:S(2)}, u32[]{:S(2)}) collective-permute-start(f32[256,256]{0,1:T(8,128)S(1)} %get-tuple-element.571), channel_id=1, source_target_pairs={{0,4},{8,0},{16,8},{24,16},{32,24},{40,32},{48,40},{56,48},{60,56}... | collective-permute-start | bytes 786440 | tf_op jit(solution)/shard_map/while/body/eval_jaxpr/ppermute | solution.py:32
  169.4 9.8 %collective-permute-start = (bf16[256,256]{1,0:T(8,128)(2,1)S(1)}, bf16[256,256]{1,0:T(8,128)(2,1)S(1)}, u32[]{:S(2)}, u32[]{:S(2)}) collective-permute-start(bf16[256,256]{1,0:T(8,128)(2,1)S(1)} %copy.137), channel_id=1, source_target_pairs={{0,4},{8,0},{16,8},{24,16},{32,24},{40,32},{48,40},{56,48},{60,56}... | collective-permute-start | bytes 393224 | tf_op jit(solution)/shard_map/while/body/eval_jaxpr/ppermute | solution.py:32
  172.4 6.8 %collective-permute-start.1 = (f32[256,256]{0,1:T(8,128)S(1)}, f32[256,256]{0,1:T(8,128)S(1)}, u32[]{:S(2)}, u32[]{:S(2)}) collective-permute-start(f32[256,256]{0,1:T(8,128)S(1)} %get-tuple-element.571), channel_id=1, source_target_pairs={{0,4},{8,0},{16,8},{24,16},{32,24},{40,32},{48,40},{56,48},{60,56}... | collective-permute-start | bytes 786440 | tf_op jit(solution)/shard_map/while/body/eval_jaxpr/ppermute | solution.py:32
  179.3 2.5 %copy-start.6 = (f32[256,256]{0,1:T(8,128)}, f32[256,256]{0,1:T(8,128)S(1)}, u32[]{:S(2)}) copy-start(f32[256,256]{0,1:T(8,128)S(1)} %get-tuple-element.378) | copy-start | bytes 786436
  181.8 4.1 %copy-start = (bf16[8,256,256]{1,2,0:T(8,128)(2,1)S(1)}, bf16[8,256,256]{1,2,0:T(8,128)(2,1)}, u32[]{:S(2)}) copy-start(bf16[8,256,256]{1,2,0:T(8,128)(2,1)} %fusion.14) | copy-start | bytes 3145732
  181.8 7.0 %collective-permute-start.3 = (f32[256,256]{0,1:T(8,128)}, f32[256,256]{0,1:T(8,128)S(1)}, u32[]{:S(2)}, u32[]{:S(2)}) collective-permute-start(f32[256,256]{0,1:T(8,128)} %copy-done.6), channel_id=1, source_target_pairs={{0,4},{8,0},{16,8},{24,16},{32,24},{40,32},{48,40},{56,48},{60,56}... | collective-permute-start | bytes 786440 | tf_op jit(solution)/shard_map/ppermute | solution.py:32
  185.9 6.9 %copy-start.2 = (f32[256,8,128]{0,2,1:T(8,128)S(1)}, f32[256,8,128]{0,2,1:T(8,128)}, u32[]{:S(2)}) copy-start(f32[256,8,128]{0,2,1:T(8,128)} %copy.90) | copy-start | bytes 3145732
  188.8 7.8 %collective-permute-start.4 = (f32[256,256]{0,1:T(8,128)S(1)}, f32[256,256]{0,1:T(8,128)S(1)}, u32[]{:S(2)}, u32[]{:S(2)}) collective-permute-start(f32[256,256]{0,1:T(8,128)S(1)} %maximum_add_fusion.1), channel_id=1, source_target_pairs={{0,4},{8,0},{16,8},{24,16},{32,24},{40,32},{48,40},{56,48},{60,56}... | collective-permute-start | bytes 786440 | tf_op jit(solution)/shard_map/ppermute | solution.py:32

commit v3 on v2

--- a/solution.py
+++ b/solution.py
@@ -32,13 +32,17 @@
     return lax.ppermute(value, "ctx", pairs)
 
 
-def live_region(block_mask, query_start, tok_rows, key_start, key_count):
-    block_table = lax.dynamic_slice(
-        block_mask, (query_start // BLK, key_start // BLK), (tok_rows // BLK, key_count // BLK)
-    )
+def from_behind(value, ctx_count):
+    order = ring_of(ctx_count)
+    pairs = [(order[p], order[(p + 1) % ctx_count]) for p in range(ctx_count)]
+    return lax.ppermute(value, "ctx", pairs)
+
+
+def live_region(block_mask, query_start, tok_rows, key_pos):
+    query_rows = lax.dynamic_slice_in_dim(block_mask, query_start // BLK, tok_rows // BLK, 0)
+    block_table = jnp.take(query_rows, key_pos[::BLK] // BLK, axis=1)
     block_table = jnp.repeat(jnp.repeat(block_table, BLK, axis=0), BLK, axis=1)
     query_pos = query_start + jnp.arange(tok_rows, dtype=jnp.int32)
-    key_pos = key_start + jnp.arange(key_count, dtype=jnp.int32)
     query_block = (query_pos // BLK)[:, None]
     key_block = (key_pos // BLK)[None, :]
     earlier = (key_block < query_block) & (block_table == 1)
@@ -85,10 +89,17 @@
     query_start = ctx_pos * tok_rows
     ring_pos = ring_index(ctx_pos, ctx_count)
 
-    def terms(key_values, turn):
-        owner = owner_of((ring_pos + turn) % ctx_count, ctx_count)
-        key_start = owner * tok_rows
-        live_mask = live_region(block_mask, query_start, tok_rows, key_start, tok_rows)
+    half = tok_rows // 2
+    offsets = jnp.arange(half, dtype=jnp.int32)
+
+    def terms(ahead_kv, behind_kv, turn):
+        ahead_owner = owner_of((ring_pos + turn) % ctx_count, ctx_count)
+        behind_owner = owner_of((ring_pos - turn) % ctx_count, ctx_count)
+        key_pos = jnp.concatenate(
+            [ahead_owner * tok_rows + offsets, behind_owner * tok_rows + half + offsets]
+        )
+        live_mask = live_region(block_mask, query_start, tok_rows, key_pos)
+        key_values = jnp.concatenate([ahead_kv, behind_kv], axis=0)
         query_term, key_term, value_term = contract(
             queries,
             out_grads,
@@ -98,26 +109,48 @@
             key_values[:, HEAD_SIZE:],
             live_mask,
         )
-        return query_term, jnp.concatenate([key_term, value_term], axis=1)
+        kv_term = jnp.concatenate([key_term, value_term], axis=1)
+        return query_term, kv_term[:half], kv_term[half:]
 
     key_values = jnp.concatenate([key_matrix, value_matrix], axis=1)
-    next_kv = from_ahead(key_values, ctx_count)
-    query_acc, pending = terms(key_values, 0)
+    ahead_kv = key_values[:half]
+    behind_kv = key_values[half:]
+    next_ahead = from_ahead(ahead_kv, ctx_count)
+    next_behind = from_behind(behind_kv, ctx_count)
+    query_acc, ahead_pending, behind_pending = terms(ahead_kv, behind_kv, 0)
 
     def visit_turn(turn, carried):
-        key_values, query_acc, pending = carried
-        received = from_ahead(pending, ctx_count)
-        next_kv = from_ahead(key_values, ctx_count)
-        query_term, kv_term = terms(key_values, turn)
-        return (next_kv, query_acc + query_term, received + kv_term)
+        ahead_kv, behind_kv, query_acc, ahead_pending, behind_pending = carried
+        ahead_received = from_ahead(ahead_pending, ctx_count)
+        behind_received = from_behind(behind_pending, ctx_count)
+        next_ahead = from_ahead(ahead_kv, ctx_count)
+        next_behind = from_behind(behind_kv, ctx_count)
+        query_term, ahead_term, behind_term = terms(ahead_kv, behind_kv, turn)
+        return (
+            next_ahead,
+            next_behind,
+            query_acc + query_term,
+            ahead_received + ahead_term,
+            behind_received + behind_term,
+        )
 
-    key_values, query_acc, pending = lax.fori_loop(
-        1, ctx_count - 1, visit_turn, (next_kv, query_acc, pending)
+    ahead_kv, behind_kv, query_acc, ahead_pending, behind_pending = lax.fori_loop(
+        1,
+        ctx_count - 1,
+        visit_turn,
+        (next_ahead, next_behind, query_acc, ahead_pending, behind_pending),
     )
-    received = from_ahead(pending, ctx_count)
-    query_term, kv_term = terms(key_values, ctx_count - 1)
+    ahead_received = from_ahead(ahead_pending, ctx_count)
+    behind_received = from_behind(behind_pending, ctx_count)
+    query_term, ahead_term, behind_term = terms(ahead_kv, behind_kv, ctx_count - 1)
     query_acc = query_acc + query_term
-    summed = from_ahead(received + kv_term, ctx_count)
+    summed = jnp.concatenate(
+        [
+            from_ahead(ahead_received + ahead_term, ctx_count),
+            from_behind(behind_received + behind_term, ctx_count),
+        ],
+        axis=0,
+    )
     logit_scale = 1.0 / math.sqrt(HEAD_SIZE)
     query_grad = (query_acc * logit_scale).reshape(tok_rows, col_width).astype(jnp.bfloat16)
     key_gradient = (summed[:, :HEAD_SIZE] * logit_scale).astype(jnp.bfloat16)

time: 201 us -> 206 us (1.025)
  starting transfers between devices: 63.8 us -> 105 us
  waiting for transfers between devices: 59.6 us -> 19.2 us
  other arithmetic: 6.32 us -> 15.2 us
  matrix products: 44.9 us -> 40.7 us
    ppermute x31, waiting for transfers between devices: 55.7 us -> 5.1 us  [from_ahead(): return lax.ppermute(value, 'ctx', pairs)]
    ppermute x0 -> x31, starting transfers between devices: none -> 26.4 us  [from_behind(): return lax.ppermute(value, 'ctx', pairs)]
    ppermute x31, starting transfers between devices: 60.3 us -> 75.6 us  [from_ahead(): return lax.ppermute(value, 'ctx', pairs)]
    dynamic_slice x28 -> x1, local copies, waits for them, and re-layouts: 12.3 us -> 0.01 us  [live_region(): lax.dynamic_slice_in_dim(block_mask, query_start // BLK, tok_rows // BLK, 0)]
    ppermute x0 -> x31, waiting for transfers between devices: none -> 10.3 us  [from_behind(): return lax.ppermute(value, 'ctx', pairs)]
    add x15 -> x31, other arithmetic: 0.51 us -> 9.65 us  [the longest x14 9.57 us: visit_turn(): behind_received + behind_term]
    gather x0 -> x16, local copies, waits for them, and re-layouts: none -> 8.93 us  [live_region(): block_table = jnp.take(query_rows, key_pos[::BLK] // BLK, axis=1)]
    dot_general x16, matrix products: 9.75 us -> 6.61 us  [contract(): jnp.einsum('gij,jd->igd', dscore, keys_part, preferred_element_type=jnp.f...]
  transfers between devices with their start and end apart: 32 -> 63, of which waited for: 17 -> 19; matrix products, arithmetic and copies ran while one was open for 34% -> 35% of each run, Pallas kernels for 0% -> 0%
where the time goes in v3:
time: 206 us; the launch traced here: 205 us
  starting transfers between devices  105 us (51%)
  matrix products  40.7 us (20%)
  local copies, waits for them, and re-layouts  21.8 us (11%)
  waiting for transfers between devices  19.2 us (9%)
  other arithmetic  15.2 us (7%)
    ppermute x31, starting transfers between devices, from_ahead(): return lax.ppermute(value, 'ctx', pairs)  75.6 us
    ppermute x31, starting transfers between devices, from_behind(): return lax.ppermute(value, 'ctx', pairs)  26.4 us
    dot_general x16, matrix products, contract(): jnp.einsum('igd,jd->gij', queries, keys_part, preferred_element_type=jnp....  10.5 us
    ppermute x31, waiting for transfers between devices, from_behind(): return lax.ppermute(value, 'ctx', pairs)  10.3 us
    add x14, other arithmetic, visit_turn(): behind_received + behind_term  9.57 us
    gather x16, local copies, waits for them, and re-layouts, live_region(): block_table = jnp.take(query_rows, key_pos[::BLK] // BLK, axis=1)  8.93 us
    dot_general x16, matrix products, contract(): jnp.einsum('igd,jd->gij', out_grads, values_part, preferred_element_type=...  8.39 us
    dot_general x16, matrix products, contract(): jnp.einsum('gij,igd->jd', probabilities.astype(jnp.bfloat16), out_grads,...  7.62 us
  transfers between devices with their start and end apart: 63, of which 19 were waited for; matrix products, arithmetic and copies ran while one was open for 35% of the time, Pallas kernels for 0%

profile of v3, /device:TPU:4, one launch (start us, length us, event | category | flops | bytes accessed | tf_op | source)
XLA Modules:
  0.0 204.6 jit_solution(9192930713635592331)
XLA Ops:
  0.7 0.9 constant_dynamic-update-slice_fusion.3
  3.1 1.9 collective-permute-start.5
  5.0 1.6 collective-permute-start.4
  6.7 1.9 copy.126
  8.5 3.5 %all-to-all-start = ((bf16[64,4,1024]{2,0,1:T(8,128)(2,1)}), bf16[64,4,1024]{2,0,1:T(8,128)(2,1)S(1)}, u32[]{:S(2)}, u32[]{:S(2)}) async-start(bf16[64,4,1024]{2,0,1:T(8,128)(2,1)} %bitcast.149), calls=%async_computation | async-start | bytes 1048576 | tf_op jit(solution)/shard_map/all_to_all | solution.py:84
  15.1 1.9 fusion.19
  17.0 3.8 %all-to-all-done = bf16[64,4,1024]{2,0,1:T(8,128)(2,1)S(1)} async-done(((bf16[64,4,1024]{2,0,1:T(8,128)(2,1)}), bf16[64,4,1024]{2,0,1:T(8,128)(2,1)S(1)}, u32[]{:S(2)}, u32[]{:S(2)}) %all-to-all-start) | async-done | bytes 524320 | tf_op jit(solution)/shard_map/all_to_all | solution.py:84
  21.7 2.0 fusion.17
  24.2 1.5 convolution_bitcast_fusion.4
  26.2 1.6 copy.81
  28.4 158.5 %while.26 = (s32[]{:T(128)}, bf16[128,256]{1,0:T(8,128)(2,1)S(1)}, bf16[128,256]{1,0:T(8,128)(2,1)S(1)}, f32[256,8,128]{0,2,1:T(8,128)S(1)}, f32[128,256]{0,1:T(...) while((s32[]{:T(128)}, bf16[128,256]{1,0:T(8,128)(2,1)S(1)}, ...), condition=%wide.region_2.4_spmd.clone.clone, body=%wide.region_1.3_spmd.clone.clone.sunk | while | flops 675554688 | bytes 17138552 | solution.py:137
  28.5 1.8 collective-permute-start
  31.0 3.1 %collective-permute-start.3 = (f32[128,256]{0,1:T(8,128)}, f32[128,256]{0,1:T(8,128)S(1)}, u32[]{:S(2)}, u32[]{:S(2)}) collective-permute-start(f32[128,256]{0,1:T(8,128)} %get-tuple-element.749), channel_id=1, source_target_pairs={{0,4},{8,0},{16,8},{24,16},{32,24},{40,32},{48,40},{56,48},{60,56}... | collective-permute-start | bytes 393224 | tf_op jit(solution)/shard_map/while/body/eval_jaxpr/ppermute | solution.py:32
  38.6 3.0 %collective-permute-start = (bf16[128,256]{1,0:T(8,128)(2,1)S(1)}, bf16[128,256]{1,0:T(8,128)(2,1)S(1)}, u32[]{:S(2)}, u32[]{:S(2)}) collective-permute-start(bf16[128,256]{1,0:T(8,128)(2,1)S(1)} %copy.140), channel_id=1, source_target_pairs={{0,4},{8,0},{16,8},{24,16},{32,24},{40,32},{48,40},{56,48},{60,56}... | collective-permute-start | bytes 196616 | tf_op jit(solution)/shard_map/while/body/eval_jaxpr/ppermute | solution.py:32
  41.6 1.7 collective-permute-start.2
  43.3 1.9 collective-permute-start.3
  50.3 2.4 %collective-permute-start = (bf16[128,256]{1,0:T(8,128)(2,1)S(1)}, bf16[128,256]{1,0:T(8,128)(2,1)S(1)}, u32[]{:S(2)}, u32[]{:S(2)}) collective-permute-start(bf16[128,256]{1,0:T(8,128)(2,1)S(1)} %copy.140), channel_id=1, source_target_pairs={{0,4},{8,0},{16,8},{24,16},{32,24},{40,32},{48,40},{56,48},{60,56}... | collective-permute-start | bytes 196616 | tf_op jit(solution)/shard_map/while/body/eval_jaxpr/ppermute | solution.py:32
  52.6 1.3 collective-permute-start.1
  54.0 2.1 %collective-permute-start.2 = (f32[128,256]{0,1:T(8,128)S(1)}, f32[128,256]{0,1:T(8,128)S(1)}, u32[]{:S(2)}, u32[]{:S(2)}) collective-permute-start(f32[128,256]{0,1:T(8,128)S(1)} %get-tuple-element.750), channel_id=1, source_target_pairs={{0,8},{8,16},{16,24},{24,32},{32,40},{40,48},{48,56},{56,60},{60,5... | collective-permute-start | bytes 393224 | tf_op jit(solution)/shard_map/while/body/eval_jaxpr/ppermute | solution.py:38
  56.0 1.5 collective-permute-start.3
  60.9 1.0 collective-permute-done.3
  62.6 2.8 %collective-permute-start = (bf16[128,256]{1,0:T(8,128)(2,1)S(1)}, bf16[128,256]{1,0:T(8,128)(2,1)S(1)}, u32[]{:S(2)}, u32[]{:S(2)}) collective-permute-start(bf16[128,256]{1,0:T(8,128)(2,1)S(1)} %copy.140), channel_id=1, source_target_pairs={{0,4},{8,0},{16,8},{24,16},{32,24},{40,32},{48,40},{56,48},{60,56}... | collective-permute-start | bytes 196616 | tf_op jit(solution)/shard_map/while/body/eval_jaxpr/ppermute | solution.py:32
  65.5 1.3 collective-permute-start.2
  66.8 2.3 %collective-permute-start.3 = (f32[128,256]{0,1:T(8,128)}, f32[128,256]{0,1:T(8,128)S(1)}, u32[]{:S(2)}, u32[]{:S(2)}) collective-permute-start(f32[128,256]{0,1:T(8,128)} %get-tuple-element.749), channel_id=1, source_target_pairs={{0,4},{8,0},{16,8},{24,16},{32,24},{40,32},{48,40},{56,48},{60,56}... | collective-permute-start | bytes 393224 | tf_op jit(solution)/shard_map/while/body/eval_jaxpr/ppermute | solution.py:32
  73.3 3.2 %collective-permute-start = (bf16[128,256]{1,0:T(8,128)(2,1)S(1)}, bf16[128,256]{1,0:T(8,128)(2,1)S(1)}, u32[]{:S(2)}, u32[]{:S(2)}) collective-permute-start(bf16[128,256]{1,0:T(8,128)(2,1)S(1)} %copy.140), channel_id=1, source_target_pairs={{0,4},{8,0},{16,8},{24,16},{32,24},{40,32},{48,40},{56,48},{60,56}... | collective-permute-start | bytes 196616 | tf_op jit(solution)/shard_map/while/body/eval_jaxpr/ppermute | solution.py:32
  76.6 1.7 collective-permute-start.2
  78.3 1.9 collective-permute-start.3
  83.5 1.7 collective-permute-done.2
  85.9 2.6 %collective-permute-start = (bf16[128,256]{1,0:T(8,128)(2,1)S(1)}, bf16[128,256]{1,0:T(8,128)(2,1)S(1)}, u32[]{:S(2)}, u32[]{:S(2)}) collective-permute-start(bf16[128,256]{1,0:T(8,128)(2,1)S(1)} %copy.140), channel_id=1, source_target_pairs={{0,4},{8,0},{16,8},{24,16},{32,24},{40,32},{48,40},{56,48},{60,56}... | collective-permute-start | bytes 196616 | tf_op jit(solution)/shard_map/while/body/eval_jaxpr/ppermute | solution.py:32
  88.5 1.2 collective-permute-start.2
  89.7 2.4 %collective-permute-start.3 = (f32[128,256]{0,1:T(8,128)}, f32[128,256]{0,1:T(8,128)S(1)}, u32[]{:S(2)}, u32[]{:S(2)}) collective-permute-start(f32[128,256]{0,1:T(8,128)} %get-tuple-element.749), channel_id=1, source_target_pairs={{0,4},{8,0},{16,8},{24,16},{32,24},{40,32},{48,40},{56,48},{60,56}... | collective-permute-start | bytes 393224 | tf_op jit(solution)/shard_map/while/body/eval_jaxpr/ppermute | solution.py:32
  95.5 1.4 collective-permute-done.2
  97.6 2.2 %collective-permute-start = (bf16[128,256]{1,0:T(8,128)(2,1)S(1)}, bf16[128,256]{1,0:T(8,128)(2,1)S(1)}, u32[]{:S(2)}, u32[]{:S(2)}) collective-permute-start(bf16[128,256]{1,0:T(8,128)(2,1)S(1)} %copy.140), channel_id=1, source_target_pairs={{0,4},{8,0},{16,8},{24,16},{32,24},{40,32},{48,40},{56,48},{60,56}... | collective-permute-start | bytes 196616 | tf_op jit(solution)/shard_map/while/body/eval_jaxpr/ppermute | solution.py:32
  100.6 2.8 %collective-permute-start.3 = (f32[128,256]{0,1:T(8,128)}, f32[128,256]{0,1:T(8,128)S(1)}, u32[]{:S(2)}, u32[]{:S(2)}) collective-permute-start(f32[128,256]{0,1:T(8,128)} %get-tuple-element.749), channel_id=1, source_target_pairs={{0,4},{8,0},{16,8},{24,16},{32,24},{40,32},{48,40},{56,48},{60,56}... | collective-permute-start | bytes 393224 | tf_op jit(solution)/shard_map/while/body/eval_jaxpr/ppermute | solution.py:32
  107.7 3.2 %collective-permute-start = (bf16[128,256]{1,0:T(8,128)(2,1)S(1)}, bf16[128,256]{1,0:T(8,128)(2,1)S(1)}, u32[]{:S(2)}, u32[]{:S(2)}) collective-permute-start(bf16[128,256]{1,0:T(8,128)(2,1)S(1)} %copy.140), channel_id=1, source_target_pairs={{0,4},{8,0},{16,8},{24,16},{32,24},{40,32},{48,40},{56,48},{60,56}... | collective-permute-start | bytes 196616 | tf_op jit(solution)/shard_map/while/body/eval_jaxpr/ppermute | solution.py:32
  110.9 1.3 collective-permute-start.2
  112.2 2.3 %collective-permute-start.3 = (f32[128,256]{0,1:T(8,128)}, f32[128,256]{0,1:T(8,128)S(1)}, u32[]{:S(2)}, u32[]{:S(2)}) collective-permute-start(f32[128,256]{0,1:T(8,128)} %get-tuple-element.749), channel_id=1, source_target_pairs={{0,4},{8,0},{16,8},{24,16},{32,24},{40,32},{48,40},{56,48},{60,56}... | collective-permute-start | bytes 393224 | tf_op jit(solution)/shard_map/while/body/eval_jaxpr/ppermute | solution.py:32
  118.8 3.2 %collective-permute-start = (bf16[128,256]{1,0:T(8,128)(2,1)S(1)}, bf16[128,256]{1,0:T(8,128)(2,1)S(1)}, u32[]{:S(2)}, u32[]{:S(2)}) collective-permute-start(bf16[128,256]{1,0:T(8,128)(2,1)S(1)} %copy.140), channel_id=1, source_target_pairs={{0,4},{8,0},{16,8},{24,16},{32,24},{40,32},{48,40},{56,48},{60,56}... | collective-permute-start | bytes 196616 | tf_op jit(solution)/shard_map/while/body/eval_jaxpr/ppermute | solution.py:32
  122.0 1.6 collective-permute-start.2
  123.5 2.1 %collective-permute-start.3 = (f32[128,256]{0,1:T(8,128)}, f32[128,256]{0,1:T(8,128)S(1)}, u32[]{:S(2)}, u32[]{:S(2)}) collective-permute-start(f32[128,256]{0,1:T(8,128)} %get-tuple-element.749), channel_id=1, source_target_pairs={{0,4},{8,0},{16,8},{24,16},{32,24},{40,32},{48,40},{56,48},{60,56}... | collective-permute-start | bytes 393224 | tf_op jit(solution)/shard_map/while/body/eval_jaxpr/ppermute | solution.py:32
  129.8 3.8 %collective-permute-start = (bf16[128,256]{1,0:T(8,128)(2,1)S(1)}, bf16[128,256]{1,0:T(8,128)(2,1)S(1)}, u32[]{:S(2)}, u32[]{:S(2)}) collective-permute-start(bf16[128,256]{1,0:T(8,128)(2,1)S(1)} %copy.140), channel_id=1, source_target_pairs={{0,4},{8,0},{16,8},{24,16},{32,24},{40,32},{48,40},{56,48},{60,56}... | collective-permute-start | bytes 196616 | tf_op jit(solution)/shard_map/while/body/eval_jaxpr/ppermute | solution.py:32
  133.7 1.4 collective-permute-start.2
  135.1 2.2 %collective-permute-start.3 = (f32[128,256]{0,1:T(8,128)}, f32[128,256]{0,1:T(8,128)S(1)}, u32[]{:S(2)}, u32[]{:S(2)}) collective-permute-start(f32[128,256]{0,1:T(8,128)} %get-tuple-element.749), channel_id=1, source_target_pairs={{0,4},{8,0},{16,8},{24,16},{32,24},{40,32},{48,40},{56,48},{60,56}... | collective-permute-start | bytes 393224 | tf_op jit(solution)/shard_map/while/body/eval_jaxpr/ppermute | solution.py:32
  141.6 3.2 %collective-permute-start = (bf16[128,256]{1,0:T(8,128)(2,1)S(1)}, bf16[128,256]{1,0:T(8,128)(2,1)S(1)}, u32[]{:S(2)}, u32[]{:S(2)}) collective-permute-start(bf16[128,256]{1,0:T(8,128)(2,1)S(1)} %copy.140), channel_id=1, source_target_pairs={{0,4},{8,0},{16,8},{24,16},{32,24},{40,32},{48,40},{56,48},{60,56}... | collective-permute-start | bytes 196616 | tf_op jit(solution)/shard_map/while/body/eval_jaxpr/ppermute | solution.py:32
  144.8 1.6 collective-permute-start.2
  146.4 2.0 collective-permute-start.3
  151.8 2.0 collective-permute-done.2
  154.5 2.4 %collective-permute-start = (bf16[128,256]{1,0:T(8,128)(2,1)S(1)}, bf16[128,256]{1,0:T(8,128)(2,1)S(1)}, u32[]{:S(2)}, u32[]{:S(2)}) collective-permute-start(bf16[128,256]{1,0:T(8,128)(2,1)S(1)} %copy.140), channel_id=1, source_target_pairs={{0,4},{8,0},{16,8},{24,16},{32,24},{40,32},{48,40},{56,48},{60,56}... | collective-permute-start | bytes 196616 | tf_op jit(solution)/shard_map/while/body/eval_jaxpr/ppermute | solution.py:32
  157.5 2.9 %collective-permute-start.3 = (f32[128,256]{0,1:T(8,128)}, f32[128,256]{0,1:T(8,128)S(1)}, u32[]{:S(2)}, u32[]{:S(2)}) collective-permute-start(f32[128,256]{0,1:T(8,128)} %get-tuple-element.749), channel_id=1, source_target_pairs={{0,4},{8,0},{16,8},{24,16},{32,24},{40,32},{48,40},{56,48},{60,56}... | collective-permute-start | bytes 393224 | tf_op jit(solution)/shard_map/while/body/eval_jaxpr/ppermute | solution.py:32
  163.8 1.3 collective-permute-done.2
  165.8 2.2 %collective-permute-start = (bf16[128,256]{1,0:T(8,128)(2,1)S(1)}, bf16[128,256]{1,0:T(8,128)(2,1)S(1)}, u32[]{:S(2)}, u32[]{:S(2)}) collective-permute-start(bf16[128,256]{1,0:T(8,128)(2,1)S(1)} %copy.140), channel_id=1, source_target_pairs={{0,4},{8,0},{16,8},{24,16},{32,24},{40,32},{48,40},{56,48},{60,56}... | collective-permute-start | bytes 196616 | tf_op jit(solution)/shard_map/while/body/eval_jaxpr/ppermute | solution.py:32
  168.0 1.0 collective-permute-start.2
  169.0 2.6 %collective-permute-start.3 = (f32[128,256]{0,1:T(8,128)}, f32[128,256]{0,1:T(8,128)S(1)}, u32[]{:S(2)}, u32[]{:S(2)}) collective-permute-start(f32[128,256]{0,1:T(8,128)} %get-tuple-element.749), channel_id=1, source_target_pairs={{0,4},{8,0},{16,8},{24,16},{32,24},{40,32},{48,40},{56,48},{60,56}... | collective-permute-start | bytes 393224 | tf_op jit(solution)/shard_map/while/body/eval_jaxpr/ppermute | solution.py:32
  175.9 3.2 %collective-permute-start = (bf16[128,256]{1,0:T(8,128)(2,1)S(1)}, bf16[128,256]{1,0:T(8,128)(2,1)S(1)}, u32[]{:S(2)}, u32[]{:S(2)}) collective-permute-start(bf16[128,256]{1,0:T(8,128)(2,1)S(1)} %copy.140), channel_id=1, source_target_pairs={{0,4},{8,0},{16,8},{24,16},{32,24},{40,32},{48,40},{56,48},{60,56}... | collective-permute-start | bytes 196616 | tf_op jit(solution)/shard_map/while/body/eval_jaxpr/ppermute | solution.py:32
  179.1 1.4 collective-permute-start.2
  180.5 2.2 %collective-permute-start.3 = (f32[128,256]{0,1:T(8,128)}, f32[128,256]{0,1:T(8,128)S(1)}, u32[]{:S(2)}, u32[]{:S(2)}) collective-permute-start(f32[128,256]{0,1:T(8,128)} %get-tuple-element.749), channel_id=1, source_target_pairs={{0,4},{8,0},{16,8},{24,16},{32,24},{40,32},{48,40},{56,48},{60,56}... | collective-permute-start | bytes 393224 | tf_op jit(solution)/shard_map/while/body/eval_jaxpr/ppermute | solution.py:32
  188.5 2.5 %collective-permute-start.8 = (f32[128,256]{0,1:T(8,128)S(1)}, f32[128,256]{0,1:T(8,128)S(1)}, u32[]{:S(2)}, u32[]{:S(2)}) collective-permute-start(f32[128,256]{0,1:T(8,128)S(1)} %get-tuple-element.458), channel_id=1, source_target_pairs={{0,8},{8,16},{16,24},{24,32},{32,40},{40,48},{48,56},{56,60},{60,5... | collective-permute-start | bytes 393224 | tf_op jit(solution)/shard_map/ppermute | solution.py:38
  191.0 1.1 collective-permute-start.6
  193.0 2.1 %collective-permute-done.8 = f32[128,256]{0,1:T(8,128)S(1)} collective-permute-done((f32[128,256]{0,1:T(8,128)S(1)}, f32[128,256]{0,1:T(8,128)S(1)}, u32[]{:S(2)}, u32[]{:S(2)}) %collective-permute-start.8) | collective-permute-done | bytes 131104 | tf_op jit(solution)/shard_map/ppermute | solution.py:38
  195.1 0.9 collective-permute-done.6
  196.0 2.1 %collective-permute-start.9 = (f32[128,256]{0,1:T(8,128)S(1)}, f32[128,256]{0,1:T(8,128)S(1)}, u32[]{:S(2)}, u32[]{:S(2)}) collective-permute-start(f32[128,256]{0,1:T(8,128)S(1)} %get-tuple-element.607), channel_id=1, source_target_pairs={{0,8},{8,16},{16,24},{24,32},{32,40},{40,48},{48,56},{56,60},{60,5... | collective-permute-start | bytes 393224 | tf_op jit(solution)/shard_map/ppermute | solution.py:38
  198.1 1.5 collective-permute-start.7
  199.8 1.0 copy.91
  200.8 2.3 %collective-permute-done.7 = f32[128,256]{0,1:T(8,128)S(1)} collective-permute-done((f32[128,256]{0,1:T(8,128)S(1)}, f32[128,256]{0,1:T(8,128)S(1)}, u32[]{:S(2)}, u32[]{:S(2)}) %collective-permute-start.7) | collective-permute-done | bytes 131104 | tf_op jit(solution)/shard_map/ppermute | solution.py:32
  (429 shorter events, 72.0 us)
Async XLA Ops:
  0.7 13.6 %copy-start.3 = (bf16[256,1024]{1,0:T(8,128)(2,1)S(1)}, bf16[256,1024]{1,0:T(8,128)(2,1)}, u32[]{:S(2)}) copy-start(bf16[256,1024]{1,0:T(8,128)(2,1)} %param.14) | copy-start | bytes 1572868
  3.1 25.3 %collective-permute-start.5 = (bf16[128,256]{1,0:T(8,128)(2,1)}, bf16[128,256]{1,0:T(8,128)(2,1)S(1)}, u32[]{:S(2)}, u32[]{:S(2)}) collective-permute-start(bf16[128,256]{1,0:T(8,128)(2,1)} %get-tuple-element.611), channel_id=1, source_target_pairs={{0,8},{8,16},{16,24},{24,32},{32,40},{40,48},{48,56},{56,60},{60,5... | collective-permute-start | bytes 196616 | tf_op jit(solution)/shard_map/ppermute | solution.py:38
  5.0 23.4 %collective-permute-start.4 = (bf16[128,256]{1,0:T(8,128)(2,1)}, bf16[128,256]{1,0:T(8,128)(2,1)S(1)}, u32[]{:S(2)}, u32[]{:S(2)}) collective-permute-start(bf16[128,256]{1,0:T(8,128)(2,1)} %get-tuple-element.612), channel_id=1, source_target_pairs={{0,4},{8,0},{16,8},{24,16},{32,24},{40,32},{48,40},{56,48},{60,56}... | collective-permute-start | bytes 196616 | tf_op jit(solution)/shard_map/ppermute | solution.py:32
  8.5 12.3 %all-to-all-start = ((bf16[64,4,1024]{2,0,1:T(8,128)(2,1)}), bf16[64,4,1024]{2,0,1:T(8,128)(2,1)S(1)}, u32[]{:S(2)}, u32[]{:S(2)}) async-start(bf16[64,4,1024]{2,0,1:T(8,128)(2,1)} %bitcast.149), calls=%async_computation | async-start | bytes 1048576 | tf_op jit(solution)/shard_map/all_to_all | solution.py:84
  28.5 10.1 %collective-permute-start = (bf16[128,256]{1,0:T(8,128)(2,1)S(1)}, bf16[128,256]{1,0:T(8,128)(2,1)S(1)}, u32[]{:S(2)}, u32[]{:S(2)}) collective-permute-start(bf16[128,256]{1,0:T(8,128)(2,1)S(1)} %copy.140), channel_id=1, source_target_pairs={{0,4},{8,0},{16,8},{24,16},{32,24},{40,32},{48,40},{56,48},{60,56}... | collective-permute-start | bytes 196616 | tf_op jit(solution)/shard_map/while/body/eval_jaxpr/ppermute | solution.py:32
  30.2 8.4 %collective-permute-start.1 = (bf16[128,256]{1,0:T(8,128)(2,1)S(1)}, bf16[128,256]{1,0:T(8,128)(2,1)S(1)}, u32[]{:S(2)}, u32[]{:S(2)}) collective-permute-start(bf16[128,256]{1,0:T(8,128)(2,1)S(1)} %copy.141), channel_id=1, source_target_pairs={{0,8},{8,16},{16,24},{24,32},{32,40},{40,48},{48,56},{56,60},{60,5... | collective-permute-start | bytes 196616 | tf_op jit(solution)/shard_map/while/body/eval_jaxpr/ppermute | solution.py:38
  30.6 7.3 %collective-permute-start.2 = (f32[128,256]{0,1:T(8,128)S(1)}, f32[128,256]{0,1:T(8,128)S(1)}, u32[]{:S(2)}, u32[]{:S(2)}) collective-permute-start(f32[128,256]{0,1:T(8,128)S(1)} %get-tuple-element.750), channel_id=1, source_target_pairs={{0,8},{8,16},{16,24},{24,32},{32,40},{40,48},{48,56},{56,60},{60,5... | collective-permute-start | bytes 393224 | tf_op jit(solution)/shard_map/while/body/eval_jaxpr/ppermute | solution.py:38
  31.0 6.9 %collective-permute-start.3 = (f32[128,256]{0,1:T(8,128)}, f32[128,256]{0,1:T(8,128)S(1)}, u32[]{:S(2)}, u32[]{:S(2)}) collective-permute-start(f32[128,256]{0,1:T(8,128)} %get-tuple-element.749), channel_id=1, source_target_pairs={{0,4},{8,0},{16,8},{24,16},{32,24},{40,32},{48,40},{56,48},{60,56}... | collective-permute-start | bytes 393224 | tf_op jit(solution)/shard_map/while/body/eval_jaxpr/ppermute | solution.py:32
  38.6 11.7 %collective-permute-start = (bf16[128,256]{1,0:T(8,128)(2,1)S(1)}, bf16[128,256]{1,0:T(8,128)(2,1)S(1)}, u32[]{:S(2)}, u32[]{:S(2)}) collective-permute-start(bf16[128,256]{1,0:T(8,128)(2,1)S(1)} %copy.140), channel_id=1, source_target_pairs={{0,4},{8,0},{16,8},{24,16},{32,24},{40,32},{48,40},{56,48},{60,56}... | collective-permute-start | bytes 196616 | tf_op jit(solution)/shard_map/while/body/eval_jaxpr/ppermute | solution.py:32
  41.6 8.7 %collective-permute-start.1 = (bf16[128,256]{1,0:T(8,128)(2,1)S(1)}, bf16[128,256]{1,0:T(8,128)(2,1)S(1)}, u32[]{:S(2)}, u32[]{:S(2)}) collective-permute-start(bf16[128,256]{1,0:T(8,128)(2,1)S(1)} %copy.141), channel_id=1, source_target_pairs={{0,8},{8,16},{16,24},{24,32},{32,40},{40,48},{48,56},{56,60},{60,5... | collective-permute-start | bytes 196616 | tf_op jit(solution)/shard_map/while/body/eval_jaxpr/ppermute | solution.py:38
  41.6 7.2 %collective-permute-start.2 = (f32[128,256]{0,1:T(8,128)S(1)}, f32[128,256]{0,1:T(8,128)S(1)}, u32[]{:S(2)}, u32[]{:S(2)}) collective-permute-start(f32[128,256]{0,1:T(8,128)S(1)} %get-tuple-element.750), channel_id=1, source_target_pairs={{0,8},{8,16},{16,24},{24,32},{32,40},{40,48},{48,56},{56,60},{60,5... | collective-permute-start | bytes 393224 | tf_op jit(solution)/shard_map/while/body/eval_jaxpr/ppermute | solution.py:38
  43.3 6.3 %collective-permute-start.3 = (f32[128,256]{0,1:T(8,128)}, f32[128,256]{0,1:T(8,128)S(1)}, u32[]{:S(2)}, u32[]{:S(2)}) collective-permute-start(f32[128,256]{0,1:T(8,128)} %get-tuple-element.749), channel_id=1, source_target_pairs={{0,4},{8,0},{16,8},{24,16},{32,24},{40,32},{48,40},{56,48},{60,56}... | collective-permute-start | bytes 393224 | tf_op jit(solution)/shard_map/while/body/eval_jaxpr/ppermute | solution.py:32
  50.3 12.3 %collective-permute-start = (bf16[128,256]{1,0:T(8,128)(2,1)S(1)}, bf16[128,256]{1,0:T(8,128)(2,1)S(1)}, u32[]{:S(2)}, u32[]{:S(2)}) collective-permute-start(bf16[128,256]{1,0:T(8,128)(2,1)S(1)} %copy.140), channel_id=1, source_target_pairs={{0,4},{8,0},{16,8},{24,16},{32,24},{40,32},{48,40},{56,48},{60,56}... | collective-permute-start | bytes 196616 | tf_op jit(solution)/shard_map/while/body/eval_jaxpr/ppermute | solution.py:32
  52.6 10.0 %collective-permute-start.1 = (bf16[128,256]{1,0:T(8,128)(2,1)S(1)}, bf16[128,256]{1,0:T(8,128)(2,1)S(1)}, u32[]{:S(2)}, u32[]{:S(2)}) collective-permute-start(bf16[128,256]{1,0:T(8,128)(2,1)S(1)} %copy.141), channel_id=1, source_target_pairs={{0,8},{8,16},{16,24},{24,32},{32,40},{40,48},{48,56},{56,60},{60,5... | collective-permute-start | bytes 196616 | tf_op jit(solution)/shard_map/while/body/eval_jaxpr/ppermute | solution.py:38
  54.0 6.9 %collective-permute-start.2 = (f32[128,256]{0,1:T(8,128)S(1)}, f32[128,256]{0,1:T(8,128)S(1)}, u32[]{:S(2)}, u32[]{:S(2)}) collective-permute-start(f32[128,256]{0,1:T(8,128)S(1)} %get-tuple-element.750), channel_id=1, source_target_pairs={{0,8},{8,16},{16,24},{24,32},{32,40},{40,48},{48,56},{56,60},{60,5... | collective-permute-start | bytes 393224 | tf_op jit(solution)/shard_map/while/body/eval_jaxpr/ppermute | solution.py:38
  56.0 5.9 %collective-permute-start.3 = (f32[128,256]{0,1:T(8,128)}, f32[128,256]{0,1:T(8,128)S(1)}, u32[]{:S(2)}, u32[]{:S(2)}) collective-permute-start(f32[128,256]{0,1:T(8,128)} %get-tuple-element.749), channel_id=1, source_target_pairs={{0,4},{8,0},{16,8},{24,16},{32,24},{40,32},{48,40},{56,48},{60,56}... | collective-permute-start | bytes 393224 | tf_op jit(solution)/shard_map/while/body/eval_jaxpr/ppermute | solution.py:32
  62.6 10.7 %collective-permute-start = (bf16[128,256]{1,0:T(8,128)(2,1)S(1)}, bf16[128,256]{1,0:T(8,128)(2,1)S(1)}, u32[]{:S(2)}, u32[]{:S(2)}) collective-permute-start(bf16[128,256]{1,0:T(8,128)(2,1)S(1)} %copy.140), channel_id=1, source_target_pairs={{0,4},{8,0},{16,8},{24,16},{32,24},{40,32},{48,40},{56,48},{60,56}... | collective-permute-start | bytes 196616 | tf_op jit(solution)/shard_map/while/body/eval_jaxpr/ppermute | solution.py:32
  65.5 7.9 %collective-permute-start.1 = (bf16[128,256]{1,0:T(8,128)(2,1)S(1)}, bf16[128,256]{1,0:T(8,128)(2,1)S(1)}, u32[]{:S(2)}, u32[]{:S(2)}) collective-permute-start(bf16[128,256]{1,0:T(8,128)(2,1)S(1)} %copy.141), channel_id=1, source_target_pairs={{0,8},{8,16},{16,24},{24,32},{32,40},{40,48},{48,56},{56,60},{60,5... | collective-permute-start | bytes 196616 | tf_op jit(solution)/shard_map/while/body/eval_jaxpr/ppermute | solution.py:38
  65.5 7.2 %collective-permute-start.2 = (f32[128,256]{0,1:T(8,128)S(1)}, f32[128,256]{0,1:T(8,128)S(1)}, u32[]{:S(2)}, u32[]{:S(2)}) collective-permute-start(f32[128,256]{0,1:T(8,128)S(1)} %get-tuple-element.750), channel_id=1, source_target_pairs={{0,8},{8,16},{16,24},{24,32},{32,40},{40,48},{48,56},{56,60},{60,5... | collective-permute-start | bytes 393224 | tf_op jit(solution)/shard_map/while/body/eval_jaxpr/ppermute | solution.py:38
  66.8 5.8 %collective-permute-start.3 = (f32[128,256]{0,1:T(8,128)}, f32[128,256]{0,1:T(8,128)S(1)}, u32[]{:S(2)}, u32[]{:S(2)}) collective-permute-start(f32[128,256]{0,1:T(8,128)} %get-tuple-element.749), channel_id=1, source_target_pairs={{0,4},{8,0},{16,8},{24,16},{32,24},{40,32},{48,40},{56,48},{60,56}... | collective-permute-start | bytes 393224 | tf_op jit(solution)/shard_map/while/body/eval_jaxpr/ppermute | solution.py:32
  73.3 12.6 %collective-permute-start = (bf16[128,256]{1,0:T(8,128)(2,1)S(1)}, bf16[128,256]{1,0:T(8,128)(2,1)S(1)}, u32[]{:S(2)}, u32[]{:S(2)}) collective-permute-start(bf16[128,256]{1,0:T(8,128)(2,1)S(1)} %copy.140), channel_id=1, source_target_pairs={{0,4},{8,0},{16,8},{24,16},{32,24},{40,32},{48,40},{56,48},{60,56}... | collective-permute-start | bytes 196616 | tf_op jit(solution)/shard_map/while/body/eval_jaxpr/ppermute | solution.py:32
  76.5 9.4 %collective-permute-start.1 = (bf16[128,256]{1,0:T(8,128)(2,1)S(1)}, bf16[128,256]{1,0:T(8,128)(2,1)S(1)}, u32[]{:S(2)}, u32[]{:S(2)}) collective-permute-start(bf16[128,256]{1,0:T(8,128)(2,1)S(1)} %copy.141), channel_id=1, source_target_pairs={{0,8},{8,16},{16,24},{24,32},{32,40},{40,48},{48,56},{56,60},{60,5... | collective-permute-start | bytes 196616 | tf_op jit(solution)/shard_map/while/body/eval_jaxpr/ppermute | solution.py:38
  76.6 8.7 %collective-permute-start.2 = (f32[128,256]{0,1:T(8,128)S(1)}, f32[128,256]{0,1:T(8,128)S(1)}, u32[]{:S(2)}, u32[]{:S(2)}) collective-permute-start(f32[128,256]{0,1:T(8,128)S(1)} %get-tuple-element.750), channel_id=1, source_target_pairs={{0,8},{8,16},{16,24},{24,32},{32,40},{40,48},{48,56},{56,60},{60,5... | collective-permute-start | bytes 393224 | tf_op jit(solution)/shard_map/while/body/eval_jaxpr/ppermute | solution.py:38
  78.3 6.9 %collective-permute-start.3 = (f32[128,256]{0,1:T(8,128)}, f32[128,256]{0,1:T(8,128)S(1)}, u32[]{:S(2)}, u32[]{:S(2)}) collective-permute-start(f32[128,256]{0,1:T(8,128)} %get-tuple-element.749), channel_id=1, source_target_pairs={{0,4},{8,0},{16,8},{24,16},{32,24},{40,32},{48,40},{56,48},{60,56}... | collective-permute-start | bytes 393224 | tf_op jit(solution)/shard_map/while/body/eval_jaxpr/ppermute | solution.py:32
  85.9 11.7 %collective-permute-start = (bf16[128,256]{1,0:T(8,128)(2,1)S(1)}, bf16[128,256]{1,0:T(8,128)(2,1)S(1)}, u32[]{:S(2)}, u32[]{:S(2)}) collective-permute-start(bf16[128,256]{1,0:T(8,128)(2,1)S(1)} %copy.140), channel_id=1, source_target_pairs={{0,4},{8,0},{16,8},{24,16},{32,24},{40,32},{48,40},{56,48},{60,56}... | collective-permute-start | bytes 196616 | tf_op jit(solution)/shard_map/while/body/eval_jaxpr/ppermute | solution.py:32
  88.5 9.0 %collective-permute-start.1 = (bf16[128,256]{1,0:T(8,128)(2,1)S(1)}, bf16[128,256]{1,0:T(8,128)(2,1)S(1)}, u32[]{:S(2)}, u32[]{:S(2)}) collective-permute-start(bf16[128,256]{1,0:T(8,128)(2,1)S(1)} %copy.141), channel_id=1, source_target_pairs={{0,8},{8,16},{16,24},{24,32},{32,40},{40,48},{48,56},{56,60},{60,5... | collective-permute-start | bytes 196616 | tf_op jit(solution)/shard_map/while/body/eval_jaxpr/ppermute | solution.py:38
  88.5 8.3 %collective-permute-start.2 = (f32[128,256]{0,1:T(8,128)S(1)}, f32[128,256]{0,1:T(8,128)S(1)}, u32[]{:S(2)}, u32[]{:S(2)}) collective-permute-start(f32[128,256]{0,1:T(8,128)S(1)} %get-tuple-element.750), channel_id=1, source_target_pairs={{0,8},{8,16},{16,24},{24,32},{32,40},{40,48},{48,56},{56,60},{60,5... | collective-permute-start | bytes 393224 | tf_op jit(solution)/shard_map/while/body/eval_jaxpr/ppermute | solution.py:38
  89.7 7.2 %collective-permute-start.3 = (f32[128,256]{0,1:T(8,128)}, f32[128,256]{0,1:T(8,128)S(1)}, u32[]{:S(2)}, u32[]{:S(2)}) collective-permute-start(f32[128,256]{0,1:T(8,128)} %get-tuple-element.749), channel_id=1, source_target_pairs={{0,4},{8,0},{16,8},{24,16},{32,24},{40,32},{48,40},{56,48},{60,56}... | collective-permute-start | bytes 393224 | tf_op jit(solution)/shard_map/while/body/eval_jaxpr/ppermute | solution.py:32
  97.6 10.1 %collective-permute-start = (bf16[128,256]{1,0:T(8,128)(2,1)S(1)}, bf16[128,256]{1,0:T(8,128)(2,1)S(1)}, u32[]{:S(2)}, u32[]{:S(2)}) collective-permute-start(bf16[128,256]{1,0:T(8,128)(2,1)S(1)} %copy.140), channel_id=1, source_target_pairs={{0,4},{8,0},{16,8},{24,16},{32,24},{40,32},{48,40},{56,48},{60,56}... | collective-permute-start | bytes 196616 | tf_op jit(solution)/shard_map/while/body/eval_jaxpr/ppermute | solution.py:32
  99.8 7.9 %collective-permute-start.1 = (bf16[128,256]{1,0:T(8,128)(2,1)S(1)}, bf16[128,256]{1,0:T(8,128)(2,1)S(1)}, u32[]{:S(2)}, u32[]{:S(2)}) collective-permute-start(bf16[128,256]{1,0:T(8,128)(2,1)S(1)} %copy.141), channel_id=1, source_target_pairs={{0,8},{8,16},{16,24},{24,32},{32,40},{40,48},{48,56},{56,60},{60,5... | collective-permute-start | bytes 196616 | tf_op jit(solution)/shard_map/while/body/eval_jaxpr/ppermute | solution.py:38
  99.8 7.2 %collective-permute-start.2 = (f32[128,256]{0,1:T(8,128)S(1)}, f32[128,256]{0,1:T(8,128)S(1)}, u32[]{:S(2)}, u32[]{:S(2)}) collective-permute-start(f32[128,256]{0,1:T(8,128)S(1)} %get-tuple-element.750), channel_id=1, source_target_pairs={{0,8},{8,16},{16,24},{24,32},{32,40},{40,48},{48,56},{56,60},{60,5... | collective-permute-start | bytes 393224 | tf_op jit(solution)/shard_map/while/body/eval_jaxpr/ppermute | solution.py:38
  100.6 6.3 %collective-permute-start.3 = (f32[128,256]{0,1:T(8,128)}, f32[128,256]{0,1:T(8,128)S(1)}, u32[]{:S(2)}, u32[]{:S(2)}) collective-permute-start(f32[128,256]{0,1:T(8,128)} %get-tuple-element.749), channel_id=1, source_target_pairs={{0,4},{8,0},{16,8},{24,16},{32,24},{40,32},{48,40},{56,48},{60,56}... | collective-permute-start | bytes 393224 | tf_op jit(solution)/shard_map/while/body/eval_jaxpr/ppermute | solution.py:32
  107.7 11.1 %collective-permute-start = (bf16[128,256]{1,0:T(8,128)(2,1)S(1)}, bf16[128,256]{1,0:T(8,128)(2,1)S(1)}, u32[]{:S(2)}, u32[]{:S(2)}) collective-permute-start(bf16[128,256]{1,0:T(8,128)(2,1)S(1)} %copy.140), channel_id=1, source_target_pairs={{0,4},{8,0},{16,8},{24,16},{32,24},{40,32},{48,40},{56,48},{60,56}... | collective-permute-start | bytes 196616 | tf_op jit(solution)/shard_map/while/body/eval_jaxpr/ppermute | solution.py:32
  110.9 7.9 %collective-permute-start.1 = (bf16[128,256]{1,0:T(8,128)(2,1)S(1)}, bf16[128,256]{1,0:T(8,128)(2,1)S(1)}, u32[]{:S(2)}, u32[]{:S(2)}) collective-permute-start(bf16[128,256]{1,0:T(8,128)(2,1)S(1)} %copy.141), channel_id=1, source_target_pairs={{0,8},{8,16},{16,24},{24,32},{32,40},{40,48},{48,56},{56,60},{60,5... | collective-permute-start | bytes 196616 | tf_op jit(solution)/shard_map/while/body/eval_jaxpr/ppermute | solution.py:38
  110.9 7.2 %collective-permute-start.2 = (f32[128,256]{0,1:T(8,128)S(1)}, f32[128,256]{0,1:T(8,128)S(1)}, u32[]{:S(2)}, u32[]{:S(2)}) collective-permute-start(f32[128,256]{0,1:T(8,128)S(1)} %get-tuple-element.750), channel_id=1, source_target_pairs={{0,8},{8,16},{16,24},{24,32},{32,40},{40,48},{48,56},{56,60},{60,5... | collective-permute-start | bytes 393224 | tf_op jit(solution)/shard_map/while/body/eval_jaxpr/ppermute | solution.py:38
  112.2 5.8 %collective-permute-start.3 = (f32[128,256]{0,1:T(8,128)}, f32[128,256]{0,1:T(8,128)S(1)}, u32[]{:S(2)}, u32[]{:S(2)}) collective-permute-start(f32[128,256]{0,1:T(8,128)} %get-tuple-element.749), channel_id=1, source_target_pairs={{0,4},{8,0},{16,8},{24,16},{32,24},{40,32},{48,40},{56,48},{60,56}... | collective-permute-start | bytes 393224 | tf_op jit(solution)/shard_map/while/body/eval_jaxpr/ppermute | solution.py:32
  118.8 11.1 %collective-permute-start = (bf16[128,256]{1,0:T(8,128)(2,1)S(1)}, bf16[128,256]{1,0:T(8,128)(2,1)S(1)}, u32[]{:S(2)}, u32[]{:S(2)}) collective-permute-start(bf16[128,256]{1,0:T(8,128)(2,1)S(1)} %copy.140), channel_id=1, source_target_pairs={{0,4},{8,0},{16,8},{24,16},{32,24},{40,32},{48,40},{56,48},{60,56}... | collective-permute-start | bytes 196616 | tf_op jit(solution)/shard_map/while/body/eval_jaxpr/ppermute | solution.py:32
  122.0 7.9 %collective-permute-start.1 = (bf16[128,256]{1,0:T(8,128)(2,1)S(1)}, bf16[128,256]{1,0:T(8,128)(2,1)S(1)}, u32[]{:S(2)}, u32[]{:S(2)}) collective-permute-start(bf16[128,256]{1,0:T(8,128)(2,1)S(1)} %copy.141), channel_id=1, source_target_pairs={{0,8},{8,16},{16,24},{24,32},{32,40},{40,48},{48,56},{56,60},{60,5... | collective-permute-start | bytes 196616 | tf_op jit(solution)/shard_map/while/body/eval_jaxpr/ppermute | solution.py:38
  122.0 7.2 %collective-permute-start.2 = (f32[128,256]{0,1:T(8,128)S(1)}, f32[128,256]{0,1:T(8,128)S(1)}, u32[]{:S(2)}, u32[]{:S(2)}) collective-permute-start(f32[128,256]{0,1:T(8,128)S(1)} %get-tuple-element.750), channel_id=1, source_target_pairs={{0,8},{8,16},{16,24},{24,32},{32,40},{40,48},{48,56},{56,60},{60,5... | collective-permute-start | bytes 393224 | tf_op jit(solution)/shard_map/while/body/eval_jaxpr/ppermute | solution.py:38
  123.5 5.6 %collective-permute-start.3 = (f32[128,256]{0,1:T(8,128)}, f32[128,256]{0,1:T(8,128)S(1)}, u32[]{:S(2)}, u32[]{:S(2)}) collective-permute-start(f32[128,256]{0,1:T(8,128)} %get-tuple-element.749), channel_id=1, source_target_pairs={{0,4},{8,0},{16,8},{24,16},{32,24},{40,32},{48,40},{56,48},{60,56}... | collective-permute-start | bytes 393224 | tf_op jit(solution)/shard_map/while/body/eval_jaxpr/ppermute | solution.py:32
  129.8 11.7 %collective-permute-start = (bf16[128,256]{1,0:T(8,128)(2,1)S(1)}, bf16[128,256]{1,0:T(8,128)(2,1)S(1)}, u32[]{:S(2)}, u32[]{:S(2)}) collective-permute-start(bf16[128,256]{1,0:T(8,128)(2,1)S(1)} %copy.140), channel_id=1, source_target_pairs={{0,4},{8,0},{16,8},{24,16},{32,24},{40,32},{48,40},{56,48},{60,56}... | collective-permute-start | bytes 196616 | tf_op jit(solution)/shard_map/while/body/eval_jaxpr/ppermute | solution.py:32
  133.7 7.9 %collective-permute-start.1 = (bf16[128,256]{1,0:T(8,128)(2,1)S(1)}, bf16[128,256]{1,0:T(8,128)(2,1)S(1)}, u32[]{:S(2)}, u32[]{:S(2)}) collective-permute-start(bf16[128,256]{1,0:T(8,128)(2,1)S(1)} %copy.141), channel_id=1, source_target_pairs={{0,8},{8,16},{16,24},{24,32},{32,40},{40,48},{48,56},{56,60},{60,5... | collective-permute-start | bytes 196616 | tf_op jit(solution)/shard_map/while/body/eval_jaxpr/ppermute | solution.py:38
  133.7 7.2 %collective-permute-start.2 = (f32[128,256]{0,1:T(8,128)S(1)}, f32[128,256]{0,1:T(8,128)S(1)}, u32[]{:S(2)}, u32[]{:S(2)}) collective-permute-start(f32[128,256]{0,1:T(8,128)S(1)} %get-tuple-element.750), channel_id=1, source_target_pairs={{0,8},{8,16},{16,24},{24,32},{32,40},{40,48},{48,56},{56,60},{60,5... | collective-permute-start | bytes 393224 | tf_op jit(solution)/shard_map/while/body/eval_jaxpr/ppermute | solution.py:38
  135.1 5.8 %collective-permute-start.3 = (f32[128,256]{0,1:T(8,128)}, f32[128,256]{0,1:T(8,128)S(1)}, u32[]{:S(2)}, u32[]{:S(2)}) collective-permute-start(f32[128,256]{0,1:T(8,128)} %get-tuple-element.749), channel_id=1, source_target_pairs={{0,4},{8,0},{16,8},{24,16},{32,24},{40,32},{48,40},{56,48},{60,56}... | collective-permute-start | bytes 393224 | tf_op jit(solution)/shard_map/while/body/eval_jaxpr/ppermute | solution.py:32
  141.6 12.9 %collective-permute-start = (bf16[128,256]{1,0:T(8,128)(2,1)S(1)}, bf16[128,256]{1,0:T(8,128)(2,1)S(1)}, u32[]{:S(2)}, u32[]{:S(2)}) collective-permute-start(bf16[128,256]{1,0:T(8,128)(2,1)S(1)} %copy.140), channel_id=1, source_target_pairs={{0,4},{8,0},{16,8},{24,16},{32,24},{40,32},{48,40},{56,48},{60,56}... | collective-permute-start | bytes 196616 | tf_op jit(solution)/shard_map/while/body/eval_jaxpr/ppermute | solution.py:32
  144.8 9.7 %collective-permute-start.1 = (bf16[128,256]{1,0:T(8,128)(2,1)S(1)}, bf16[128,256]{1,0:T(8,128)(2,1)S(1)}, u32[]{:S(2)}, u32[]{:S(2)}) collective-permute-start(bf16[128,256]{1,0:T(8,128)(2,1)S(1)} %copy.141), channel_id=1, source_target_pairs={{0,8},{8,16},{16,24},{24,32},{32,40},{40,48},{48,56},{56,60},{60,5... | collective-permute-start | bytes 196616 | tf_op jit(solution)/shard_map/while/body/eval_jaxpr/ppermute | solution.py:38
  144.8 9.0 %collective-permute-start.2 = (f32[128,256]{0,1:T(8,128)S(1)}, f32[128,256]{0,1:T(8,128)S(1)}, u32[]{:S(2)}, u32[]{:S(2)}) collective-permute-start(f32[128,256]{0,1:T(8,128)S(1)} %get-tuple-element.750), channel_id=1, source_target_pairs={{0,8},{8,16},{16,24},{24,32},{32,40},{40,48},{48,56},{56,60},{60,5... | collective-permute-start | bytes 393224 | tf_op jit(solution)/shard_map/while/body/eval_jaxpr/ppermute | solution.py:38
  146.4 7.4 %collective-permute-start.3 = (f32[128,256]{0,1:T(8,128)}, f32[128,256]{0,1:T(8,128)S(1)}, u32[]{:S(2)}, u32[]{:S(2)}) collective-permute-start(f32[128,256]{0,1:T(8,128)} %get-tuple-element.749), channel_id=1, source_target_pairs={{0,4},{8,0},{16,8},{24,16},{32,24},{40,32},{48,40},{56,48},{60,56}... | collective-permute-start | bytes 393224 | tf_op jit(solution)/shard_map/while/body/eval_jaxpr/ppermute | solution.py:32
  154.5 11.3 %collective-permute-start = (bf16[128,256]{1,0:T(8,128)(2,1)S(1)}, bf16[128,256]{1,0:T(8,128)(2,1)S(1)}, u32[]{:S(2)}, u32[]{:S(2)}) collective-permute-start(bf16[128,256]{1,0:T(8,128)(2,1)S(1)} %copy.140), channel_id=1, source_target_pairs={{0,4},{8,0},{16,8},{24,16},{32,24},{40,32},{48,40},{56,48},{60,56}... | collective-permute-start | bytes 196616 | tf_op jit(solution)/shard_map/while/body/eval_jaxpr/ppermute | solution.py:32
  156.8 9.0 %collective-permute-start.1 = (bf16[128,256]{1,0:T(8,128)(2,1)S(1)}, bf16[128,256]{1,0:T(8,128)(2,1)S(1)}, u32[]{:S(2)}, u32[]{:S(2)}) collective-permute-start(bf16[128,256]{1,0:T(8,128)(2,1)S(1)} %copy.141), channel_id=1, source_target_pairs={{0,8},{8,16},{16,24},{24,32},{32,40},{40,48},{48,56},{56,60},{60,5... | collective-permute-start | bytes 196616 | tf_op jit(solution)/shard_map/while/body/eval_jaxpr/ppermute | solution.py:38
  156.8 8.3 %collective-permute-start.2 = (f32[128,256]{0,1:T(8,128)S(1)}, f32[128,256]{0,1:T(8,128)S(1)}, u32[]{:S(2)}, u32[]{:S(2)}) collective-permute-start(f32[128,256]{0,1:T(8,128)S(1)} %get-tuple-element.750), channel_id=1, source_target_pairs={{0,8},{8,16},{16,24},{24,32},{32,40},{40,48},{48,56},{56,60},{60,5... | collective-permute-start | bytes 393224 | tf_op jit(solution)/shard_map/while/body/eval_jaxpr/ppermute | solution.py:38
  157.5 7.6 %collective-permute-start.3 = (f32[128,256]{0,1:T(8,128)}, f32[128,256]{0,1:T(8,128)S(1)}, u32[]{:S(2)}, u32[]{:S(2)}) collective-permute-start(f32[128,256]{0,1:T(8,128)} %get-tuple-element.749), channel_id=1, source_target_pairs={{0,4},{8,0},{16,8},{24,16},{32,24},{40,32},{48,40},{56,48},{60,56}... | collective-permute-start | bytes 393224 | tf_op jit(solution)/shard_map/while/body/eval_jaxpr/ppermute | solution.py:32
  165.8 10.1 %collective-permute-start = (bf16[128,256]{1,0:T(8,128)(2,1)S(1)}, bf16[128,256]{1,0:T(8,128)(2,1)S(1)}, u32[]{:S(2)}, u32[]{:S(2)}) collective-permute-start(bf16[128,256]{1,0:T(8,128)(2,1)S(1)} %copy.140), channel_id=1, source_target_pairs={{0,4},{8,0},{16,8},{24,16},{32,24},{40,32},{48,40},{56,48},{60,56}... | collective-permute-start | bytes 196616 | tf_op jit(solution)/shard_map/while/body/eval_jaxpr/ppermute | solution.py:32
  168.0 7.9 %collective-permute-start.1 = (bf16[128,256]{1,0:T(8,128)(2,1)S(1)}, bf16[128,256]{1,0:T(8,128)(2,1)S(1)}, u32[]{:S(2)}, u32[]{:S(2)}) collective-permute-start(bf16[128,256]{1,0:T(8,128)(2,1)S(1)} %copy.141), channel_id=1, source_target_pairs={{0,8},{8,16},{16,24},{24,32},{32,40},{40,48},{48,56},{56,60},{60,5... | collective-permute-start | bytes 196616 | tf_op jit(solution)/shard_map/while/body/eval_jaxpr/ppermute | solution.py:38
  168.0 7.2 %collective-permute-start.2 = (f32[128,256]{0,1:T(8,128)S(1)}, f32[128,256]{0,1:T(8,128)S(1)}, u32[]{:S(2)}, u32[]{:S(2)}) collective-permute-start(f32[128,256]{0,1:T(8,128)S(1)} %get-tuple-element.750), channel_id=1, source_target_pairs={{0,8},{8,16},{16,24},{24,32},{32,40},{40,48},{48,56},{56,60},{60,5... | collective-permute-start | bytes 393224 | tf_op jit(solution)/shard_map/while/body/eval_jaxpr/ppermute | solution.py:38
  169.0 6.2 %collective-permute-start.3 = (f32[128,256]{0,1:T(8,128)}, f32[128,256]{0,1:T(8,128)S(1)}, u32[]{:S(2)}, u32[]{:S(2)}) collective-permute-start(f32[128,256]{0,1:T(8,128)} %get-tuple-element.749), channel_id=1, source_target_pairs={{0,4},{8,0},{16,8},{24,16},{32,24},{40,32},{48,40},{56,48},{60,56}... | collective-permute-start | bytes 393224 | tf_op jit(solution)/shard_map/while/body/eval_jaxpr/ppermute | solution.py:32
  175.9 11.1 %collective-permute-start = (bf16[128,256]{1,0:T(8,128)(2,1)S(1)}, bf16[128,256]{1,0:T(8,128)(2,1)S(1)}, u32[]{:S(2)}, u32[]{:S(2)}) collective-permute-start(bf16[128,256]{1,0:T(8,128)(2,1)S(1)} %copy.140), channel_id=1, source_target_pairs={{0,4},{8,0},{16,8},{24,16},{32,24},{40,32},{48,40},{56,48},{60,56}... | collective-permute-start | bytes 196616 | tf_op jit(solution)/shard_map/while/body/eval_jaxpr/ppermute | solution.py:32
  179.1 7.9 %collective-permute-start.1 = (bf16[128,256]{1,0:T(8,128)(2,1)S(1)}, bf16[128,256]{1,0:T(8,128)(2,1)S(1)}, u32[]{:S(2)}, u32[]{:S(2)}) collective-permute-start(bf16[128,256]{1,0:T(8,128)(2,1)S(1)} %copy.141), channel_id=1, source_target_pairs={{0,8},{8,16},{16,24},{24,32},{32,40},{40,48},{48,56},{56,60},{60,5... | collective-permute-start | bytes 196616 | tf_op jit(solution)/shard_map/while/body/eval_jaxpr/ppermute | solution.py:38
  179.1 7.2 %collective-permute-start.2 = (f32[128,256]{0,1:T(8,128)S(1)}, f32[128,256]{0,1:T(8,128)S(1)}, u32[]{:S(2)}, u32[]{:S(2)}) collective-permute-start(f32[128,256]{0,1:T(8,128)S(1)} %get-tuple-element.750), channel_id=1, source_target_pairs={{0,8},{8,16},{16,24},{24,32},{32,40},{40,48},{48,56},{56,60},{60,5... | collective-permute-start | bytes 393224 | tf_op jit(solution)/shard_map/while/body/eval_jaxpr/ppermute | solution.py:38
  180.5 5.8 %collective-permute-start.3 = (f32[128,256]{0,1:T(8,128)}, f32[128,256]{0,1:T(8,128)S(1)}, u32[]{:S(2)}, u32[]{:S(2)}) collective-permute-start(f32[128,256]{0,1:T(8,128)} %get-tuple-element.749), channel_id=1, source_target_pairs={{0,4},{8,0},{16,8},{24,16},{32,24},{40,32},{48,40},{56,48},{60,56}... | collective-permute-start | bytes 393224 | tf_op jit(solution)/shard_map/while/body/eval_jaxpr/ppermute | solution.py:32
  188.5 6.5 %collective-permute-start.8 = (f32[128,256]{0,1:T(8,128)S(1)}, f32[128,256]{0,1:T(8,128)S(1)}, u32[]{:S(2)}, u32[]{:S(2)}) collective-permute-start(f32[128,256]{0,1:T(8,128)S(1)} %get-tuple-element.458), channel_id=1, source_target_pairs={{0,8},{8,16},{16,24},{24,32},{32,40},{40,48},{48,56},{56,60},{60,5... | collective-permute-start | bytes 393224 | tf_op jit(solution)/shard_map/ppermute | solution.py:38
  191.0 5.0 %collective-permute-start.6 = (f32[128,256]{0,1:T(8,128)S(1)}, f32[128,256]{0,1:T(8,128)S(1)}, u32[]{:S(2)}, u32[]{:S(2)}) collective-permute-start(f32[128,256]{0,1:T(8,128)S(1)} %copy-done.6), channel_id=1, source_target_pairs={{0,4},{8,0},{16,8},{24,16},{32,24},{40,32},{48,40},{56,48},{60,56}... | collective-permute-start | bytes 393224 | tf_op jit(solution)/shard_map/ppermute | solution.py:32
  196.0 7.1 %collective-permute-start.9 = (f32[128,256]{0,1:T(8,128)S(1)}, f32[128,256]{0,1:T(8,128)S(1)}, u32[]{:S(2)}, u32[]{:S(2)}) collective-permute-start(f32[128,256]{0,1:T(8,128)S(1)} %get-tuple-element.607), channel_id=1, source_target_pairs={{0,8},{8,16},{16,24},{24,32},{32,40},{40,48},{48,56},{56,60},{60,5... | collective-permute-start | bytes 393224 | tf_op jit(solution)/shard_map/ppermute | solution.py:38
  198.1 5.0 %collective-permute-start.7 = (f32[128,256]{0,1:T(8,128)S(1)}, f32[128,256]{0,1:T(8,128)S(1)}, u32[]{:S(2)}, u32[]{:S(2)}) collective-permute-start(f32[128,256]{0,1:T(8,128)S(1)} %get-tuple-element.608), channel_id=1, source_target_pairs={{0,4},{8,0},{16,8},{24,16},{32,24},{40,32},{48,40},{56,48},{60,56}... | collective-permute-start | bytes 393224 | tf_op jit(solution)/shard_map/ppermute | solution.py:32
  (7 other events, 40.9 us)

commit v4 on v3

--- a/solution.py
+++ b/solution.py
@@ -10,31 +10,18 @@
 Y_HI = 2
 
 
-def ring_of(ctx_count):
-    half = ctx_count // Y_HI
-    return [Y_HI * p if p < half else Y_HI * (ctx_count - 1 - p) + 1 for p in range(ctx_count)]
-
-
-def ring_index(ctx_pos, ctx_count):
-    half = ctx_count // Y_HI
-    z = ctx_pos // Y_HI
-    return jnp.where(ctx_pos % Y_HI == 0, z, ctx_count - 1 - z)
-
-
-def owner_of(ring_pos, ctx_count):
-    half = ctx_count // Y_HI
-    return jnp.where(ring_pos < half, Y_HI * ring_pos, Y_HI * (ctx_count - 1 - ring_pos) + 1)
-
-
-def from_ahead(value, ctx_count):
-    order = ring_of(ctx_count)
-    pairs = [(order[p], order[(p - 1) % ctx_count]) for p in range(ctx_count)]
+def along_z(value, ctx_count, shift):
+    z_count = ctx_count // Y_HI
+    pairs = [
+        (Y_HI * ((z + shift) % z_count) + h, Y_HI * z + h)
+        for z in range(z_count)
+        for h in range(Y_HI)
+    ]
     return lax.ppermute(value, "ctx", pairs)
 
 
-def from_behind(value, ctx_count):
-    order = ring_of(ctx_count)
-    pairs = [(order[p], order[(p + 1) % ctx_count]) for p in range(ctx_count)]
+def from_partner(value, ctx_count):
+    pairs = [(c, c ^ 1) for c in range(ctx_count)]
     return lax.ppermute(value, "ctx", pairs)
 
 
@@ -87,16 +74,17 @@
     outputs = attn_out.reshape(tok_rows, heads_local, HEAD_SIZE)
     row_delta = jnp.sum(out_grads.astype(jnp.float32) * outputs.astype(jnp.float32), axis=2).T
     query_start = ctx_pos * tok_rows
-    ring_pos = ring_index(ctx_pos, ctx_count)
-
-    half = tok_rows // 2
-    offsets = jnp.arange(half, dtype=jnp.int32)
+    z_pos = ctx_pos // Y_HI
+    z_count = ctx_count // Y_HI
+    y_hi = ctx_pos % Y_HI
+    super_rows = Y_HI * tok_rows
+    offsets = jnp.arange(tok_rows, dtype=jnp.int32)
 
     def terms(ahead_kv, behind_kv, turn):
-        ahead_owner = owner_of((ring_pos + turn) % ctx_count, ctx_count)
-        behind_owner = owner_of((ring_pos - turn) % ctx_count, ctx_count)
+        ahead_owner = (z_pos + turn) % z_count
+        behind_owner = (z_pos - turn) % z_count
         key_pos = jnp.concatenate(
-            [ahead_owner * tok_rows + offsets, behind_owner * tok_rows + half + offsets]
+            [ahead_owner * super_rows + offsets, behind_owner * super_rows + tok_rows + offsets]
         )
         live_mask = live_region(block_mask, query_start, tok_rows, key_pos)
         key_values = jnp.concatenate([ahead_kv, behind_kv], axis=0)
@@ -110,21 +98,22 @@
             live_mask,
         )
         kv_term = jnp.concatenate([key_term, value_term], axis=1)
-        return query_term, kv_term[:half], kv_term[half:]
+        return query_term, kv_term[:tok_rows], kv_term[tok_rows:]
 
     key_values = jnp.concatenate([key_matrix, value_matrix], axis=1)
-    ahead_kv = key_values[:half]
-    behind_kv = key_values[half:]
-    next_ahead = from_ahead(ahead_kv, ctx_count)
-    next_behind = from_behind(behind_kv, ctx_count)
+    partner_kv = from_partner(key_values, ctx_count)
+    ahead_kv = jnp.where(y_hi == 0, key_values, partner_kv)
+    behind_kv = jnp.where(y_hi == 0, partner_kv, key_values)
+    next_ahead = along_z(ahead_kv, ctx_count, 1)
+    next_behind = along_z(behind_kv, ctx_count, -1)
     query_acc, ahead_pending, behind_pending = terms(ahead_kv, behind_kv, 0)
 
     def visit_turn(turn, carried):
         ahead_kv, behind_kv, query_acc, ahead_pending, behind_pending = carried
-        ahead_received = from_ahead(ahead_pending, ctx_count)
-        behind_received = from_behind(behind_pending, ctx_count)
-        next_ahead = from_ahead(ahead_kv, ctx_count)
-        next_behind = from_behind(behind_kv, ctx_count)
+        ahead_received = along_z(ahead_pending, ctx_count, 1)
+        behind_received = along_z(behind_pending, ctx_count, -1)
+        next_ahead = along_z(ahead_kv, ctx_count, 1)
+        next_behind = along_z(behind_kv, ctx_count, -1)
         query_term, ahead_term, behind_term = terms(ahead_kv, behind_kv, turn)
         return (
             next_ahead,
@@ -136,21 +125,19 @@
 
     ahead_kv, behind_kv, query_acc, ahead_pending, behind_pending = lax.fori_loop(
         1,
-        ctx_count - 1,
+        z_count - 1,
         visit_turn,
         (next_ahead, next_behind, query_acc, ahead_pending, behind_pending),
     )
-    ahead_received = from_ahead(ahead_pending, ctx_count)
-    behind_received = from_behind(behind_pending, ctx_count)
-    query_term, ahead_term, behind_term = terms(ahead_kv, behind_kv, ctx_count - 1)
+    ahead_received = along_z(ahead_pending, ctx_count, 1)
+    behind_received = along_z(behind_pending, ctx_count, -1)
+    query_term, ahead_term, behind_term = terms(ahead_kv, behind_kv, z_count - 1)
     query_acc = query_acc + query_term
-    summed = jnp.concatenate(
-        [
-            from_ahead(ahead_received + ahead_term, ctx_count),
-            from_behind(behind_received + behind_term, ctx_count),
-        ],
-        axis=0,
-    )
+    ahead_total = along_z(ahead_received + ahead_term, ctx_count, 1)
+    behind_total = along_z(behind_received + behind_term, ctx_count, -1)
+    own_total = jnp.where(y_hi == 0, ahead_total, behind_total)
+    other_total = jnp.where(y_hi == 0, behind_total, ahead_total)
+    summed = own_total + from_partner(other_total, ctx_count)
     logit_scale = 1.0 / math.sqrt(HEAD_SIZE)
     query_grad = (query_acc * logit_scale).reshape(tok_rows, col_width).astype(jnp.bfloat16)
     key_gradient = (summed[:, :HEAD_SIZE] * logit_scale).astype(jnp.bfloat16)

time: 206 us -> 141 us (0.68)
  starting transfers between devices: 105 us -> 50.6 us
  other arithmetic: 15.2 us -> 11.2 us
  local copies, waits for them, and re-layouts: 21.8 us -> 18 us
    ppermute x62 -> x32, starting transfers between devices: 102 us -> 47.1 us  [the longest x30 43.4 us: along_z(): return lax.ppermute(value, 'ctx', pairs)]
    gather x16 -> x8, local copies, waits for them, and re-layouts: 8.93 us -> 4.47 us  [live_region(): block_table = jnp.take(query_rows, key_pos[::BLK] // BLK, axis=1)]
    add x14 -> x6, other arithmetic: 9.57 us -> 5.28 us  [visit_turn(): behind_received + behind_term]
    all_to_all x1, waiting for transfers between devices: 3.85 us -> 0.01 us  [local(): lax.all_to_all(pieces, 'tp', split_axis=1, concat_axis=0, tiled=True)]
    ppermute x62 -> x32, waiting for transfers between devices: 15.4 us -> 19.1 us  [the longest x30 12.7 us: along_z(): return lax.ppermute(value, 'ctx', pairs)]
    dot_general x16 -> x8, matrix products: 10.5 us -> 7.5 us  [contract(): jnp.einsum('igd,jd->gij', queries, keys_part, preferred_element_type=jnp....]
    dot_general x16 -> x8, matrix products: 8.39 us -> 11.2 us  [contract(): jnp.einsum('igd,jd->gij', out_grads, values_part, preferred_element_type=...]
    dot_general x16 -> x8, matrix products: 6.61 us -> 3.84 us  [contract(): jnp.einsum('gij,jd->igd', dscore, keys_part, preferred_element_type=jnp.f...]
  transfers between devices with their start and end apart: 63 -> 33, of which waited for: 19 -> 7; matrix products, arithmetic and copies ran while one was open for 35% -> 45% of each run, Pallas kernels for 0% -> 0%
where the time goes in v4:
time: 141 us; the launch traced here: 140 us
  starting transfers between devices  50.6 us (36%)
  matrix products  39.2 us (28%)
  waiting for transfers between devices  19.1 us (14%)
  local copies, waits for them, and re-layouts  18 us (13%)
  other arithmetic  11.2 us (8%)
    ppermute x30, starting transfers between devices, along_z(): return lax.ppermute(value, 'ctx', pairs)  43.4 us
    ppermute x30, waiting for transfers between devices, along_z(): return lax.ppermute(value, 'ctx', pairs)  12.7 us
    dot_general x8, matrix products, contract(): jnp.einsum('igd,jd->gij', out_grads, values_part, preferred_element_type=...  11.2 us
    dot_general x8, matrix products, contract(): jnp.einsum('gij,igd->jd', probabilities.astype(jnp.bfloat16), out_grads,...  10.3 us
    dot_general x8, matrix products, contract(): jnp.einsum('igd,jd->gij', queries, keys_part, preferred_element_type=jnp....  7.5 us
    ppermute x2, waiting for transfers between devices, from_partner(): return lax.ppermute(value, 'ctx', pairs)  6.4 us
    dot_general x8, matrix products, contract(): jnp.einsum('gij,igd->jd', dscore, queries, preferred_element_type=jnp.flo...  6.3 us
    add x6, other arithmetic, visit_turn(): behind_received + behind_term  5.28 us
  transfers between devices with their start and end apart: 33, of which 7 were waited for; matrix products, arithmetic and copies ran while one was open for 45% of the time, Pallas kernels for 0%

profile of v4, /device:TPU:4, one launch (start us, length us, event | category | flops | bytes accessed | tf_op | source)
XLA Modules:
  0.0 139.9 jit_solution(2138529075353427642)
XLA Ops:
  0.6 0.9 constant_dynamic-update-slice_fusion.3
  1.5 0.9 constant_dynamic-update-slice_fusion.2
  2.4 3.3 %collective-permute-start.4 = (bf16[256,256]{1,0:T(8,128)(2,1)S(1)}, bf16[256,256]{1,0:T(8,128)(2,1)S(1)}, u32[]{:S(2)}, u32[]{:S(2)}) collective-permute-start(bf16[256,256]{1,0:T(8,128)(2,1)S(1)} %constant_dynamic-update-slice_fusion.2), channel_id=1, source_target_pairs={{0,4},{4,0},{8,12},{12,8},{16,20},{20,16},{24,28},{28,24},{32,36},... | collective-permute-start | bytes 393224 | tf_op jit(solution)/shard_map/ppermute | solution.py:25
  5.7 1.9 %copy.137 = bf16[8,4,8,1024]{3,2,0,1:T(8,128)(2,1)} copy(bf16[8,4,8,1024]{3,2,1,0:T(8,128)(2,1)} %bitcast.204) | data formatting | bytes 1048576 | tf_op jit(solution)/shard_map/reshape | solution.py:70
  7.5 3.5 %all-to-all-start = ((bf16[64,4,1024]{2,0,1:T(8,128)(2,1)}), bf16[64,4,1024]{2,0,1:T(8,128)(2,1)S(1)}, u32[]{:S(2)}, u32[]{:S(2)}) async-start(bf16[64,4,1024]{2,0,1:T(8,128)(2,1)} %bitcast.157), calls=%async_computation | async-start | bytes 1048576 | tf_op jit(solution)/shard_map/all_to_all | solution.py:71
  13.2 1.2 copy.79
  14.4 1.2 copy.83
  16.0 1.2 fusion.45
  17.3 2.0 %collective-permute-start.6 = (bf16[256,256]{1,0:T(8,128)(2,1)S(1)}, bf16[256,256]{1,0:T(8,128)(2,1)S(1)}, u32[]{:S(2)}, u32[]{:S(2)}) collective-permute-start(bf16[256,256]{1,0:T(8,128)(2,1)S(1)} %get-tuple-element.611), channel_id=1, source_target_pairs={{56,0},{60,4},{0,8},{4,12},{8,16},{12,20},{16,24},{20,28},{24,32},... | collective-permute-start | bytes 393224 | tf_op jit(solution)/shard_map/ppermute | solution.py:20
  19.3 4.2 %collective-permute-start.5 = (bf16[256,256]{1,0:T(8,128)(2,1)S(1)}, bf16[256,256]{1,0:T(8,128)(2,1)S(1)}, u32[]{:S(2)}, u32[]{:S(2)}) collective-permute-start(bf16[256,256]{1,0:T(8,128)(2,1)S(1)} %get-tuple-element.612), channel_id=1, source_target_pairs={{8,0},{12,4},{16,8},{20,12},{24,16},{28,20},{32,24},{36,28},{40,32... | collective-permute-start | bytes 393224 | tf_op jit(solution)/shard_map/ppermute | solution.py:20
  23.5 2.7 %fusion.60 = f32[512,256,8]{1,0,2:T(8,128)} fusion(bf16[256,8,128]{0,2,1:T(8,128)(2,1)S(1)} %bitcast.194, bf16[256,256]{1,0:T(8,128)(2,1)S(1)} %get-tuple-element.612, bf16[256,256]{1,0:T(8,128)(2,1)S(1)} %get-tuple-element.611), kind=kOutput, calls=%fused_computation.116 | convolution fusion | flops 268697600 | bytes 4980736 | tf_op jit(solution)/shard_map/igd,jd->gij/dot_general | solution.py:43
  27.0 3.4 %fusion.39 = f32[512,128]{0,1:T(8,128)S(1)} fusion(bf16[256,8,128]{0,2,1:T(8,128)(2,1)S(1)} %copy.90, f32[512,256,8]{1,0,2:T(8,128)} %fusion.60, f32[8,256]{1,0:T(8,128)S(1)} %copy-done.7, pred[256,512]{0,1:T(8,128)(4,1)} %get-tuple-element.614), kind=kOutput, calls=%fused_computation.76 | convolution fusion | flops 272629760 | bytes 5120000 | tf_op jit(solution)/shard_map/gij,igd->jd/dot_general | solution.py:53
  30.5 1.4 %fusion.28 = bf16[8,256,512]{1,2,0:T(8,128)(2,1)S(1)} fusion(f32[512,256,8]{1,0,2:T(8,128)S(1)} %copy-done.1, f32[8,256]{1,0:T(8,128)S(1)} %copy.85, f32[8,256]{1,0:T(8,128)S(1)} %copy-done.7, pred[256,512]{0,1:T(8,128)(4,1)S(1)} %copy-done.6, bf16[256,8,128]{2,1,0:T(8,128)(2,1)S(1)} %bitcast.199, bf16[256,256]{1,0:T(8,128)(2,1)S(1)} %get-tuple-element.611, ...), kind=kOutput, calls=%fused_computation.64 | convolution fusion | flops 274989056 | bytes 7225344 | tf_op jit(solution)/shard_map/igd,jd->gij/dot_general | solution.py:47
  32.4 0.8 convolution_bitcast_fusion.5
  33.3 0.8 pad_maximum_fusion.2
  34.1 75.4 %while.26 = (s32[]{:T(128)}, bf16[256,256]{1,0:T(8,128)(2,1)S(1)}, bf16[256,256]{1,0:T(8,128)(2,1)S(1)}, f32[256,8,128]{0,2,1:T(8,128)S(1)}, f32[256,256]{0,1:T(...) while((s32[]{:T(128)}, bf16[256,256]{1,0:T(8,128)(2,1)S(1)}, ...), condition=%wide.region_2.4_spmd.clone.clone, body=%wide.region_1.3_spmd.clone.clone.sunk | while | flops 1353987712 | bytes 32291700 | solution.py:126
  34.1 1.8 %collective-permute-start = (bf16[256,256]{1,0:T(8,128)(2,1)S(1)}, bf16[256,256]{1,0:T(8,128)(2,1)S(1)}, u32[]{:S(2)}, u32[]{:S(2)}) collective-permute-start(bf16[256,256]{1,0:T(8,128)(2,1)S(1)} %copy.149), channel_id=1, source_target_pairs={{8,0},{12,4},{16,8},{20,12},{24,16},{28,20},{32,24},{36,28},{40,32... | collective-permute-start | bytes 393224 | tf_op jit(solution)/shard_map/while/body/eval_jaxpr/ppermute | solution.py:20
  36.4 3.1 %collective-permute-start.3 = (f32[256,256]{0,1:T(8,128)}, f32[256,256]{0,1:T(8,128)S(1)}, u32[]{:S(2)}, u32[]{:S(2)}) collective-permute-start(f32[256,256]{0,1:T(8,128)} %get-tuple-element.747), channel_id=1, source_target_pairs={{8,0},{12,4},{16,8},{20,12},{24,16},{28,20},{32,24},{36,28},{40,32... | collective-permute-start | bytes 786440 | tf_op jit(solution)/shard_map/while/body/eval_jaxpr/ppermute | solution.py:20
  41.5 1.0 fusion.114
  42.6 1.4 %fusion.112 = bf16[8,256,512]{1,2,0:T(8,128)(2,1)S(1)} fusion(f32[512,256,8]{1,0,2:T(8,128)S(1)} %fusion.110, bf16[256,8,128]{0,2,1:T(8,128)(2,1)S(1)} %copy-done.3, f32[8,256]{1,0:T(8,128)S(1)} %get-tuple-element.774, f32[8,256]{1,0:T(8,128)S(1)} %get-tuple-element.772, pred[256,512]{0,1:T(8,128)(4,1)S(1)} %fusion.111, ...), kind=kOutput, calls=%fused_computation.6.clone.1 | convolution fusion | flops 274726912 | bytes 7094272 | tf_op jit(solution)/shard_map/while/body/eval_jaxpr/igd,jd->gij/dot_general | solution.py:47
  44.5 0.8 convolution_bitcast_fusion.7
  45.3 2.5 %collective-permute-done.2 = f32[256,256]{0,1:T(8,128)S(1)} collective-permute-done((f32[256,256]{0,1:T(8,128)}, f32[256,256]{0,1:T(8,128)S(1)}, u32[]{:S(2)}, u32[]{:S(2)}) %collective-permute-start.2) | collective-permute-done | bytes 262176 | tf_op jit(solution)/shard_map/while/body/eval_jaxpr/ppermute | solution.py:20
  47.8 0.9 fusion.115
  49.4 1.5 %collective-permute-start.1 = (bf16[256,256]{1,0:T(8,128)(2,1)S(1)}, bf16[256,256]{1,0:T(8,128)(2,1)S(1)}, u32[]{:S(2)}, u32[]{:S(2)}) collective-permute-start(bf16[256,256]{1,0:T(8,128)(2,1)S(1)} %copy.150), channel_id=1, source_target_pairs={{56,0},{60,4},{0,8},{4,12},{8,16},{12,20},{16,24},{20,28},{24,32},... | collective-permute-start | bytes 393224 | tf_op jit(solution)/shard_map/while/body/eval_jaxpr/ppermute | solution.py:20
  51.0 3.1 %collective-permute-start.3 = (f32[256,256]{0,1:T(8,128)}, f32[256,256]{0,1:T(8,128)S(1)}, u32[]{:S(2)}, u32[]{:S(2)}) collective-permute-start(f32[256,256]{0,1:T(8,128)} %get-tuple-element.747), channel_id=1, source_target_pairs={{8,0},{12,4},{16,8},{20,12},{24,16},{28,20},{32,24},{36,28},{40,32... | collective-permute-start | bytes 786440 | tf_op jit(solution)/shard_map/while/body/eval_jaxpr/ppermute | solution.py:20
  56.1 1.0 fusion.114
  57.1 1.4 %fusion.112 = bf16[8,256,512]{1,2,0:T(8,128)(2,1)S(1)} fusion(f32[512,256,8]{1,0,2:T(8,128)S(1)} %fusion.110, bf16[256,8,128]{0,2,1:T(8,128)(2,1)S(1)} %copy-done.3, f32[8,256]{1,0:T(8,128)S(1)} %get-tuple-element.774, f32[8,256]{1,0:T(8,128)S(1)} %get-tuple-element.772, pred[256,512]{0,1:T(8,128)(4,1)S(1)} %fusion.111, ...), kind=kOutput, calls=%fused_computation.6.clone.1 | convolution fusion | flops 274726912 | bytes 7094272 | tf_op jit(solution)/shard_map/while/body/eval_jaxpr/igd,jd->gij/dot_general | solution.py:47
  59.0 0.8 convolution_bitcast_fusion.7
  59.9 0.9 fusion.115
  60.8 2.0 %collective-permute-start = (bf16[256,256]{1,0:T(8,128)(2,1)S(1)}, bf16[256,256]{1,0:T(8,128)(2,1)S(1)}, u32[]{:S(2)}, u32[]{:S(2)}) collective-permute-start(bf16[256,256]{1,0:T(8,128)(2,1)S(1)} %copy.149), channel_id=1, source_target_pairs={{8,0},{12,4},{16,8},{20,12},{24,16},{28,20},{32,24},{36,28},{40,32... | collective-permute-start | bytes 393224 | tf_op jit(solution)/shard_map/while/body/eval_jaxpr/ppermute | solution.py:20
  63.3 3.0 %collective-permute-start.3 = (f32[256,256]{0,1:T(8,128)}, f32[256,256]{0,1:T(8,128)S(1)}, u32[]{:S(2)}, u32[]{:S(2)}) collective-permute-start(f32[256,256]{0,1:T(8,128)} %get-tuple-element.747), channel_id=1, source_target_pairs={{8,0},{12,4},{16,8},{20,12},{24,16},{28,20},{32,24},{36,28},{40,32... | collective-permute-start | bytes 786440 | tf_op jit(solution)/shard_map/while/body/eval_jaxpr/ppermute | solution.py:20
  68.3 1.0 fusion.114
  69.3 1.4 %fusion.112 = bf16[8,256,512]{1,2,0:T(8,128)(2,1)S(1)} fusion(f32[512,256,8]{1,0,2:T(8,128)S(1)} %fusion.110, bf16[256,8,128]{0,2,1:T(8,128)(2,1)S(1)} %copy-done.3, f32[8,256]{1,0:T(8,128)S(1)} %get-tuple-element.774, f32[8,256]{1,0:T(8,128)S(1)} %get-tuple-element.772, pred[256,512]{0,1:T(8,128)(4,1)S(1)} %fusion.111, ...), kind=kOutput, calls=%fused_computation.6.clone.1 | convolution fusion | flops 274726912 | bytes 7094272 | tf_op jit(solution)/shard_map/while/body/eval_jaxpr/igd,jd->gij/dot_general | solution.py:47
  71.2 0.8 convolution_bitcast_fusion.7
  72.1 0.9 fusion.115
  73.0 2.1 %collective-permute-start = (bf16[256,256]{1,0:T(8,128)(2,1)S(1)}, bf16[256,256]{1,0:T(8,128)(2,1)S(1)}, u32[]{:S(2)}, u32[]{:S(2)}) collective-permute-start(bf16[256,256]{1,0:T(8,128)(2,1)S(1)} %copy.149), channel_id=1, source_target_pairs={{8,0},{12,4},{16,8},{20,12},{24,16},{28,20},{32,24},{36,28},{40,32... | collective-permute-start | bytes 393224 | tf_op jit(solution)/shard_map/while/body/eval_jaxpr/ppermute | solution.py:20
  75.6 2.9 %collective-permute-start.3 = (f32[256,256]{0,1:T(8,128)}, f32[256,256]{0,1:T(8,128)S(1)}, u32[]{:S(2)}, u32[]{:S(2)}) collective-permute-start(f32[256,256]{0,1:T(8,128)} %get-tuple-element.747), channel_id=1, source_target_pairs={{8,0},{12,4},{16,8},{20,12},{24,16},{28,20},{32,24},{36,28},{40,32... | collective-permute-start | bytes 786440 | tf_op jit(solution)/shard_map/while/body/eval_jaxpr/ppermute | solution.py:20
  80.5 1.0 fusion.114
  81.5 1.4 %fusion.112 = bf16[8,256,512]{1,2,0:T(8,128)(2,1)S(1)} fusion(f32[512,256,8]{1,0,2:T(8,128)S(1)} %fusion.110, bf16[256,8,128]{0,2,1:T(8,128)(2,1)S(1)} %copy-done.3, f32[8,256]{1,0:T(8,128)S(1)} %get-tuple-element.774, f32[8,256]{1,0:T(8,128)S(1)} %get-tuple-element.772, pred[256,512]{0,1:T(8,128)(4,1)S(1)} %fusion.111, ...), kind=kOutput, calls=%fused_computation.6.clone.1 | convolution fusion | flops 274726912 | bytes 7094272 | tf_op jit(solution)/shard_map/while/body/eval_jaxpr/igd,jd->gij/dot_general | solution.py:47
  84.2 0.9 fusion.115
  85.2 2.1 %collective-permute-start = (bf16[256,256]{1,0:T(8,128)(2,1)S(1)}, bf16[256,256]{1,0:T(8,128)(2,1)S(1)}, u32[]{:S(2)}, u32[]{:S(2)}) collective-permute-start(bf16[256,256]{1,0:T(8,128)(2,1)S(1)} %copy.149), channel_id=1, source_target_pairs={{8,0},{12,4},{16,8},{20,12},{24,16},{28,20},{32,24},{36,28},{40,32... | collective-permute-start | bytes 393224 | tf_op jit(solution)/shard_map/while/body/eval_jaxpr/ppermute | solution.py:20
  87.4 0.8 collective-permute-start.2
  88.2 2.5 %collective-permute-start.3 = (f32[256,256]{0,1:T(8,128)}, f32[256,256]{0,1:T(8,128)S(1)}, u32[]{:S(2)}, u32[]{:S(2)}) collective-permute-start(f32[256,256]{0,1:T(8,128)} %get-tuple-element.747), channel_id=1, source_target_pairs={{8,0},{12,4},{16,8},{20,12},{24,16},{28,20},{32,24},{36,28},{40,32... | collective-permute-start | bytes 786440 | tf_op jit(solution)/shard_map/while/body/eval_jaxpr/ppermute | solution.py:20
  92.7 1.0 fusion.114
  93.7 1.4 %fusion.112 = bf16[8,256,512]{1,2,0:T(8,128)(2,1)S(1)} fusion(f32[512,256,8]{1,0,2:T(8,128)S(1)} %fusion.110, bf16[256,8,128]{0,2,1:T(8,128)(2,1)S(1)} %copy-done.3, f32[8,256]{1,0:T(8,128)S(1)} %get-tuple-element.774, f32[8,256]{1,0:T(8,128)S(1)} %get-tuple-element.772, pred[256,512]{0,1:T(8,128)(4,1)S(1)} %fusion.111, ...), kind=kOutput, calls=%fused_computation.6.clone.1 | convolution fusion | flops 274726912 | bytes 7094272 | tf_op jit(solution)/shard_map/while/body/eval_jaxpr/igd,jd->gij/dot_general | solution.py:47
  96.4 0.9 fusion.115
  97.3 2.1 %collective-permute-start = (bf16[256,256]{1,0:T(8,128)(2,1)S(1)}, bf16[256,256]{1,0:T(8,128)(2,1)S(1)}, u32[]{:S(2)}, u32[]{:S(2)}) collective-permute-start(bf16[256,256]{1,0:T(8,128)(2,1)S(1)} %copy.149), channel_id=1, source_target_pairs={{8,0},{12,4},{16,8},{20,12},{24,16},{28,20},{32,24},{36,28},{40,32... | collective-permute-start | bytes 393224 | tf_op jit(solution)/shard_map/while/body/eval_jaxpr/ppermute | solution.py:20
  99.6 0.9 collective-permute-start.2
  100.5 2.4 %collective-permute-start.3 = (f32[256,256]{0,1:T(8,128)}, f32[256,256]{0,1:T(8,128)S(1)}, u32[]{:S(2)}, u32[]{:S(2)}) collective-permute-start(f32[256,256]{0,1:T(8,128)} %get-tuple-element.747), channel_id=1, source_target_pairs={{8,0},{12,4},{16,8},{20,12},{24,16},{28,20},{32,24},{36,28},{40,32... | collective-permute-start | bytes 786440 | tf_op jit(solution)/shard_map/while/body/eval_jaxpr/ppermute | solution.py:20
  104.9 1.0 fusion.114
  105.9 1.4 %fusion.112 = bf16[8,256,512]{1,2,0:T(8,128)(2,1)S(1)} fusion(f32[512,256,8]{1,0,2:T(8,128)S(1)} %fusion.110, bf16[256,8,128]{0,2,1:T(8,128)(2,1)S(1)} %copy-done.3, f32[8,256]{1,0:T(8,128)S(1)} %get-tuple-element.774, f32[8,256]{1,0:T(8,128)S(1)} %get-tuple-element.772, pred[256,512]{0,1:T(8,128)(4,1)S(1)} %fusion.111, ...), kind=kOutput, calls=%fused_computation.6.clone.1 | convolution fusion | flops 274726912 | bytes 7094272 | tf_op jit(solution)/shard_map/while/body/eval_jaxpr/igd,jd->gij/dot_general | solution.py:47
  108.6 0.9 fusion.115
  109.5 1.1 copy.104
  110.7 1.1 copy.98
  111.7 2.3 %collective-permute-start.7 = (f32[256,256]{1,0:T(8,128)S(1)}, f32[256,256]{1,0:T(8,128)S(1)}, u32[]{:S(2)}, u32[]{:S(2)}) collective-permute-start(f32[256,256]{1,0:T(8,128)S(1)} %copy.98), channel_id=1, source_target_pairs={{8,0},{12,4},{16,8},{20,12},{24,16},{28,20},{32,24},{36,28},{40,32... | collective-permute-start | bytes 786440 | tf_op jit(solution)/shard_map/ppermute | solution.py:20
  114.8 1.4 %fusion.24 = bf16[8,256,512]{1,2,0:T(8,128)(2,1)S(1)} fusion(f32[512,256,8]{1,0,2:T(8,128)S(1)} %fusion.59, f32[8,256]{1,0:T(8,128)S(1)} %get-tuple-element.806, f32[8,256]{1,0:T(8,128)S(1)} %get-tuple-element.807, pred[256,512]{0,1:T(8,128)(4,1)S(1)} %copy-done.5, bf16[256,8,128]{2,1,0:T(8,128)(2,1)S(1)} %bitcast.200, ...), kind=kOutput, calls=%fused_computation.58 | convolution fusion | flops 274726912 | bytes 7094272 | tf_op jit(solution)/shard_map/igd,jd->gij/dot_general | solution.py:47
  116.2 0.8 fusion.42
  117.8 1.0 collective-permute-done.7
  118.8 3.9 %collective-permute-done.9 = f32[256,256]{1,0:T(8,128)S(1)} collective-permute-done((f32[256,256]{1,0:T(8,128)S(1)}, f32[256,256]{1,0:T(8,128)S(1)}, u32[]{:S(2)}, u32[]{:S(2)}) %collective-permute-start.9) | collective-permute-done | bytes 262176 | tf_op jit(solution)/shard_map/ppermute | solution.py:20
  122.9 2.0 %collective-permute-start.10 = (f32[256,256]{1,0:T(8,128)S(1)}, f32[256,256]{1,0:T(8,128)S(1)}, u32[]{:S(2)}, u32[]{:S(2)}) collective-permute-start(f32[256,256]{1,0:T(8,128)S(1)} %get-tuple-element.608), channel_id=1, source_target_pairs={{56,0},{60,4},{0,8},{4,12},{8,16},{12,20},{16,24},{20,28},{24,32},... | collective-permute-start | bytes 786440 | tf_op jit(solution)/shard_map/ppermute | solution.py:20
  125.4 3.9 %collective-permute-done.8 = f32[256,256]{1,0:T(8,128)S(1)} collective-permute-done((f32[256,256]{1,0:T(8,128)S(1)}, f32[256,256]{1,0:T(8,128)S(1)}, u32[]{:S(2)}, u32[]{:S(2)}) %collective-permute-start.8) | collective-permute-done | bytes 262176 | tf_op jit(solution)/shard_map/ppermute | solution.py:20
  129.2 1.3 collective-permute-done.10
  131.1 1.0 copy.105
  132.1 6.4 %collective-permute-done.11 = f32[256,256]{1,0:T(8,128)S(1)} collective-permute-done((f32[256,256]{1,0:T(8,128)S(1)}, f32[256,256]{1,0:T(8,128)S(1)}, u32[]{:S(2)}, u32[]{:S(2)}) %collective-permute-start.11) | collective-permute-done | bytes 262176 | tf_op jit(solution)/shard_map/ppermute | solution.py:25
  (210 shorter events, 27.3 us)
Async XLA Ops:
  0.6 10.8 %copy-start = (s32[32,32]{1,0:T(8,128)S(1)}, s32[32,32]{1,0:T(8,128)}, u32[]{:S(2)}) copy-start(s32[32,32]{1,0:T(8,128)} %param.17) | copy-start | bytes 12292
  2.4 14.9 %collective-permute-start.4 = (bf16[256,256]{1,0:T(8,128)(2,1)S(1)}, bf16[256,256]{1,0:T(8,128)(2,1)S(1)}, u32[]{:S(2)}, u32[]{:S(2)}) collective-permute-start(bf16[256,256]{1,0:T(8,128)(2,1)S(1)} %constant_dynamic-update-slice_fusion.2), channel_id=1, source_target_pairs={{0,4},{4,0},{8,12},{12,8},{16,20},{20,16},{24,28},{28,24},{32,36},... | collective-permute-start | bytes 393224 | tf_op jit(solution)/shard_map/ppermute | solution.py:25
  7.5 18.6 %all-to-all-start = ((bf16[64,4,1024]{2,0,1:T(8,128)(2,1)}), bf16[64,4,1024]{2,0,1:T(8,128)(2,1)S(1)}, u32[]{:S(2)}, u32[]{:S(2)}) async-start(bf16[64,4,1024]{2,0,1:T(8,128)(2,1)} %bitcast.157), calls=%async_computation | async-start | bytes 1048576 | tf_op jit(solution)/shard_map/all_to_all | solution.py:71
  17.3 16.8 %collective-permute-start.6 = (bf16[256,256]{1,0:T(8,128)(2,1)S(1)}, bf16[256,256]{1,0:T(8,128)(2,1)S(1)}, u32[]{:S(2)}, u32[]{:S(2)}) collective-permute-start(bf16[256,256]{1,0:T(8,128)(2,1)S(1)} %get-tuple-element.611), channel_id=1, source_target_pairs={{56,0},{60,4},{0,8},{4,12},{8,16},{12,20},{16,24},{20,28},{24,32},... | collective-permute-start | bytes 393224 | tf_op jit(solution)/shard_map/ppermute | solution.py:20
  19.3 14.8 %collective-permute-start.5 = (bf16[256,256]{1,0:T(8,128)(2,1)S(1)}, bf16[256,256]{1,0:T(8,128)(2,1)S(1)}, u32[]{:S(2)}, u32[]{:S(2)}) collective-permute-start(bf16[256,256]{1,0:T(8,128)(2,1)S(1)} %get-tuple-element.612), channel_id=1, source_target_pairs={{8,0},{12,4},{16,8},{20,12},{24,16},{28,20},{32,24},{36,28},{40,32... | collective-permute-start | bytes 393224 | tf_op jit(solution)/shard_map/ppermute | solution.py:20
  23.5 3.5 %copy-start.7 = (f32[8,256]{1,0:T(8,128)S(1)}, f32[8,256]{1,0:T(8,128)}, u32[]{:S(2)}) copy-start(f32[8,256]{1,0:T(8,128)} %param.16) | copy-start | bytes 24580
  26.6 5.4 %copy-start.2 = (bf16[256,8,128]{0,2,1:T(8,128)(2,1)}, bf16[256,8,128]{0,2,1:T(8,128)(2,1)S(1)}, u32[]{:S(2)}) copy-start(bf16[256,8,128]{0,2,1:T(8,128)(2,1)S(1)} %copy.90) | copy-start | bytes 1572868
  27.0 3.4 %copy-start.6 = (pred[256,512]{0,1:T(8,128)(4,1)S(1)}, pred[256,512]{0,1:T(8,128)(4,1)}, u32[]{:S(2)}) copy-start(pred[256,512]{0,1:T(8,128)(4,1)} %get-tuple-element.614) | copy-start | bytes 393220
  27.0 3.5 %copy-start.1 = (f32[512,256,8]{1,0,2:T(8,128)S(1)}, f32[512,256,8]{1,0,2:T(8,128)}, u32[]{:S(2)}) copy-start(f32[512,256,8]{1,0,2:T(8,128)} %fusion.60) | copy-start | bytes 12582916
  34.1 14.5 %collective-permute-start = (bf16[256,256]{1,0:T(8,128)(2,1)S(1)}, bf16[256,256]{1,0:T(8,128)(2,1)S(1)}, u32[]{:S(2)}, u32[]{:S(2)}) collective-permute-start(bf16[256,256]{1,0:T(8,128)(2,1)S(1)} %copy.149), channel_id=1, source_target_pairs={{8,0},{12,4},{16,8},{20,12},{24,16},{28,20},{32,24},{36,28},{40,32... | collective-permute-start | bytes 393224 | tf_op jit(solution)/shard_map/while/body/eval_jaxpr/ppermute | solution.py:20
  35.9 12.7 %collective-permute-start.1 = (bf16[256,256]{1,0:T(8,128)(2,1)S(1)}, bf16[256,256]{1,0:T(8,128)(2,1)S(1)}, u32[]{:S(2)}, u32[]{:S(2)}) collective-permute-start(bf16[256,256]{1,0:T(8,128)(2,1)S(1)} %copy.150), channel_id=1, source_target_pairs={{56,0},{60,4},{0,8},{4,12},{8,16},{12,20},{16,24},{20,28},{24,32},... | collective-permute-start | bytes 393224 | tf_op jit(solution)/shard_map/while/body/eval_jaxpr/ppermute | solution.py:20
  36.3 11.5 %collective-permute-start.2 = (f32[256,256]{0,1:T(8,128)}, f32[256,256]{0,1:T(8,128)S(1)}, u32[]{:S(2)}, u32[]{:S(2)}) collective-permute-start(f32[256,256]{0,1:T(8,128)} %get-tuple-element.748), channel_id=1, source_target_pairs={{56,0},{60,4},{0,8},{4,12},{8,16},{12,20},{16,24},{20,28},{24,32},... | collective-permute-start | bytes 786440 | tf_op jit(solution)/shard_map/while/body/eval_jaxpr/ppermute | solution.py:20
  36.4 11.4 %collective-permute-start.3 = (f32[256,256]{0,1:T(8,128)}, f32[256,256]{0,1:T(8,128)S(1)}, u32[]{:S(2)}, u32[]{:S(2)}) collective-permute-start(f32[256,256]{0,1:T(8,128)} %get-tuple-element.747), channel_id=1, source_target_pairs={{8,0},{12,4},{16,8},{20,12},{24,16},{28,20},{32,24},{36,28},{40,32... | collective-permute-start | bytes 786440 | tf_op jit(solution)/shard_map/while/body/eval_jaxpr/ppermute | solution.py:20
  40.5 1.0 copy-start.3
  48.7 12.2 %collective-permute-start = (bf16[256,256]{1,0:T(8,128)(2,1)S(1)}, bf16[256,256]{1,0:T(8,128)(2,1)S(1)}, u32[]{:S(2)}, u32[]{:S(2)}) collective-permute-start(bf16[256,256]{1,0:T(8,128)(2,1)S(1)} %copy.149), channel_id=1, source_target_pairs={{8,0},{12,4},{16,8},{20,12},{24,16},{28,20},{32,24},{36,28},{40,32... | collective-permute-start | bytes 393224 | tf_op jit(solution)/shard_map/while/body/eval_jaxpr/ppermute | solution.py:20
  49.4 11.4 %collective-permute-start.1 = (bf16[256,256]{1,0:T(8,128)(2,1)S(1)}, bf16[256,256]{1,0:T(8,128)(2,1)S(1)}, u32[]{:S(2)}, u32[]{:S(2)}) collective-permute-start(bf16[256,256]{1,0:T(8,128)(2,1)S(1)} %copy.150), channel_id=1, source_target_pairs={{56,0},{60,4},{0,8},{4,12},{8,16},{12,20},{16,24},{20,28},{24,32},... | collective-permute-start | bytes 393224 | tf_op jit(solution)/shard_map/while/body/eval_jaxpr/ppermute | solution.py:20
  50.9 9.1 %collective-permute-start.2 = (f32[256,256]{0,1:T(8,128)}, f32[256,256]{0,1:T(8,128)S(1)}, u32[]{:S(2)}, u32[]{:S(2)}) collective-permute-start(f32[256,256]{0,1:T(8,128)} %get-tuple-element.748), channel_id=1, source_target_pairs={{56,0},{60,4},{0,8},{4,12},{8,16},{12,20},{16,24},{20,28},{24,32},... | collective-permute-start | bytes 786440 | tf_op jit(solution)/shard_map/while/body/eval_jaxpr/ppermute | solution.py:20
  51.0 9.0 %collective-permute-start.3 = (f32[256,256]{0,1:T(8,128)}, f32[256,256]{0,1:T(8,128)S(1)}, u32[]{:S(2)}, u32[]{:S(2)}) collective-permute-start(f32[256,256]{0,1:T(8,128)} %get-tuple-element.747), channel_id=1, source_target_pairs={{8,0},{12,4},{16,8},{20,12},{24,16},{28,20},{32,24},{36,28},{40,32... | collective-permute-start | bytes 786440 | tf_op jit(solution)/shard_map/while/body/eval_jaxpr/ppermute | solution.py:20
  55.1 1.0 copy-start.3
  60.8 12.1 %collective-permute-start = (bf16[256,256]{1,0:T(8,128)(2,1)S(1)}, bf16[256,256]{1,0:T(8,128)(2,1)S(1)}, u32[]{:S(2)}, u32[]{:S(2)}) collective-permute-start(bf16[256,256]{1,0:T(8,128)(2,1)S(1)} %copy.149), channel_id=1, source_target_pairs={{8,0},{12,4},{16,8},{20,12},{24,16},{28,20},{32,24},{36,28},{40,32... | collective-permute-start | bytes 393224 | tf_op jit(solution)/shard_map/while/body/eval_jaxpr/ppermute | solution.py:20
  62.9 10.1 %collective-permute-start.1 = (bf16[256,256]{1,0:T(8,128)(2,1)S(1)}, bf16[256,256]{1,0:T(8,128)(2,1)S(1)}, u32[]{:S(2)}, u32[]{:S(2)}) collective-permute-start(bf16[256,256]{1,0:T(8,128)(2,1)S(1)} %copy.150), channel_id=1, source_target_pairs={{56,0},{60,4},{0,8},{4,12},{8,16},{12,20},{16,24},{20,28},{24,32},... | collective-permute-start | bytes 393224 | tf_op jit(solution)/shard_map/while/body/eval_jaxpr/ppermute | solution.py:20
  63.0 9.0 %collective-permute-start.2 = (f32[256,256]{0,1:T(8,128)}, f32[256,256]{0,1:T(8,128)S(1)}, u32[]{:S(2)}, u32[]{:S(2)}) collective-permute-start(f32[256,256]{0,1:T(8,128)} %get-tuple-element.748), channel_id=1, source_target_pairs={{56,0},{60,4},{0,8},{4,12},{8,16},{12,20},{16,24},{20,28},{24,32},... | collective-permute-start | bytes 786440 | tf_op jit(solution)/shard_map/while/body/eval_jaxpr/ppermute | solution.py:20
  63.3 8.7 %collective-permute-start.3 = (f32[256,256]{0,1:T(8,128)}, f32[256,256]{0,1:T(8,128)S(1)}, u32[]{:S(2)}, u32[]{:S(2)}) collective-permute-start(f32[256,256]{0,1:T(8,128)} %get-tuple-element.747), channel_id=1, source_target_pairs={{8,0},{12,4},{16,8},{20,12},{24,16},{28,20},{32,24},{36,28},{40,32... | collective-permute-start | bytes 786440 | tf_op jit(solution)/shard_map/while/body/eval_jaxpr/ppermute | solution.py:20
  67.3 1.0 copy-start.3
  73.0 12.2 %collective-permute-start = (bf16[256,256]{1,0:T(8,128)(2,1)S(1)}, bf16[256,256]{1,0:T(8,128)(2,1)S(1)}, u32[]{:S(2)}, u32[]{:S(2)}) collective-permute-start(bf16[256,256]{1,0:T(8,128)(2,1)S(1)} %copy.149), channel_id=1, source_target_pairs={{8,0},{12,4},{16,8},{20,12},{24,16},{28,20},{32,24},{36,28},{40,32... | collective-permute-start | bytes 393224 | tf_op jit(solution)/shard_map/while/body/eval_jaxpr/ppermute | solution.py:20
  75.1 10.1 %collective-permute-start.1 = (bf16[256,256]{1,0:T(8,128)(2,1)S(1)}, bf16[256,256]{1,0:T(8,128)(2,1)S(1)}, u32[]{:S(2)}, u32[]{:S(2)}) collective-permute-start(bf16[256,256]{1,0:T(8,128)(2,1)S(1)} %copy.150), channel_id=1, source_target_pairs={{56,0},{60,4},{0,8},{4,12},{8,16},{12,20},{16,24},{20,28},{24,32},... | collective-permute-start | bytes 393224 | tf_op jit(solution)/shard_map/while/body/eval_jaxpr/ppermute | solution.py:20
  75.2 9.1 %collective-permute-start.2 = (f32[256,256]{0,1:T(8,128)}, f32[256,256]{0,1:T(8,128)S(1)}, u32[]{:S(2)}, u32[]{:S(2)}) collective-permute-start(f32[256,256]{0,1:T(8,128)} %get-tuple-element.748), channel_id=1, source_target_pairs={{56,0},{60,4},{0,8},{4,12},{8,16},{12,20},{16,24},{20,28},{24,32},... | collective-permute-start | bytes 786440 | tf_op jit(solution)/shard_map/while/body/eval_jaxpr/ppermute | solution.py:20
  75.6 8.6 %collective-permute-start.3 = (f32[256,256]{0,1:T(8,128)}, f32[256,256]{0,1:T(8,128)S(1)}, u32[]{:S(2)}, u32[]{:S(2)}) collective-permute-start(f32[256,256]{0,1:T(8,128)} %get-tuple-element.747), channel_id=1, source_target_pairs={{8,0},{12,4},{16,8},{20,12},{24,16},{28,20},{32,24},{36,28},{40,32... | collective-permute-start | bytes 786440 | tf_op jit(solution)/shard_map/while/body/eval_jaxpr/ppermute | solution.py:20
  79.4 1.0 copy-start.3
  85.2 12.2 %collective-permute-start = (bf16[256,256]{1,0:T(8,128)(2,1)S(1)}, bf16[256,256]{1,0:T(8,128)(2,1)S(1)}, u32[]{:S(2)}, u32[]{:S(2)}) collective-permute-start(bf16[256,256]{1,0:T(8,128)(2,1)S(1)} %copy.149), channel_id=1, source_target_pairs={{8,0},{12,4},{16,8},{20,12},{24,16},{28,20},{32,24},{36,28},{40,32... | collective-permute-start | bytes 393224 | tf_op jit(solution)/shard_map/while/body/eval_jaxpr/ppermute | solution.py:20
  87.3 10.1 %collective-permute-start.1 = (bf16[256,256]{1,0:T(8,128)(2,1)S(1)}, bf16[256,256]{1,0:T(8,128)(2,1)S(1)}, u32[]{:S(2)}, u32[]{:S(2)}) collective-permute-start(bf16[256,256]{1,0:T(8,128)(2,1)S(1)} %copy.150), channel_id=1, source_target_pairs={{56,0},{60,4},{0,8},{4,12},{8,16},{12,20},{16,24},{20,28},{24,32},... | collective-permute-start | bytes 393224 | tf_op jit(solution)/shard_map/while/body/eval_jaxpr/ppermute | solution.py:20
  87.4 9.1 %collective-permute-start.2 = (f32[256,256]{0,1:T(8,128)}, f32[256,256]{0,1:T(8,128)S(1)}, u32[]{:S(2)}, u32[]{:S(2)}) collective-permute-start(f32[256,256]{0,1:T(8,128)} %get-tuple-element.748), channel_id=1, source_target_pairs={{56,0},{60,4},{0,8},{4,12},{8,16},{12,20},{16,24},{20,28},{24,32},... | collective-permute-start | bytes 786440 | tf_op jit(solution)/shard_map/while/body/eval_jaxpr/ppermute | solution.py:20
  88.2 8.2 %collective-permute-start.3 = (f32[256,256]{0,1:T(8,128)}, f32[256,256]{0,1:T(8,128)S(1)}, u32[]{:S(2)}, u32[]{:S(2)}) collective-permute-start(f32[256,256]{0,1:T(8,128)} %get-tuple-element.747), channel_id=1, source_target_pairs={{8,0},{12,4},{16,8},{20,12},{24,16},{28,20},{32,24},{36,28},{40,32... | collective-permute-start | bytes 786440 | tf_op jit(solution)/shard_map/while/body/eval_jaxpr/ppermute | solution.py:20
  91.6 1.0 copy-start.3
  97.3 12.2 %collective-permute-start = (bf16[256,256]{1,0:T(8,128)(2,1)S(1)}, bf16[256,256]{1,0:T(8,128)(2,1)S(1)}, u32[]{:S(2)}, u32[]{:S(2)}) collective-permute-start(bf16[256,256]{1,0:T(8,128)(2,1)S(1)} %copy.149), channel_id=1, source_target_pairs={{8,0},{12,4},{16,8},{20,12},{24,16},{28,20},{32,24},{36,28},{40,32... | collective-permute-start | bytes 393224 | tf_op jit(solution)/shard_map/while/body/eval_jaxpr/ppermute | solution.py:20
  99.5 10.1 %collective-permute-start.1 = (bf16[256,256]{1,0:T(8,128)(2,1)S(1)}, bf16[256,256]{1,0:T(8,128)(2,1)S(1)}, u32[]{:S(2)}, u32[]{:S(2)}) collective-permute-start(bf16[256,256]{1,0:T(8,128)(2,1)S(1)} %copy.150), channel_id=1, source_target_pairs={{56,0},{60,4},{0,8},{4,12},{8,16},{12,20},{16,24},{20,28},{24,32},... | collective-permute-start | bytes 393224 | tf_op jit(solution)/shard_map/while/body/eval_jaxpr/ppermute | solution.py:20
  99.6 9.1 %collective-permute-start.2 = (f32[256,256]{0,1:T(8,128)}, f32[256,256]{0,1:T(8,128)S(1)}, u32[]{:S(2)}, u32[]{:S(2)}) collective-permute-start(f32[256,256]{0,1:T(8,128)} %get-tuple-element.748), channel_id=1, source_target_pairs={{56,0},{60,4},{0,8},{4,12},{8,16},{12,20},{16,24},{20,28},{24,32},... | collective-permute-start | bytes 786440 | tf_op jit(solution)/shard_map/while/body/eval_jaxpr/ppermute | solution.py:20
  100.5 8.2 %collective-permute-start.3 = (f32[256,256]{0,1:T(8,128)}, f32[256,256]{0,1:T(8,128)S(1)}, u32[]{:S(2)}, u32[]{:S(2)}) collective-permute-start(f32[256,256]{0,1:T(8,128)} %get-tuple-element.747), channel_id=1, source_target_pairs={{8,0},{12,4},{16,8},{20,12},{24,16},{28,20},{32,24},{36,28},{40,32... | collective-permute-start | bytes 786440 | tf_op jit(solution)/shard_map/while/body/eval_jaxpr/ppermute | solution.py:20
  103.8 1.0 copy-start.3
  109.5 5.3 %copy-start.5 = (pred[256,512]{0,1:T(8,128)(4,1)S(1)}, pred[256,512]{0,1:T(8,128)(4,1)}, u32[]{:S(2)}) copy-start(pred[256,512]{0,1:T(8,128)(4,1)} %get-tuple-element.613) | copy-start | bytes 393220
  111.7 7.1 %collective-permute-start.7 = (f32[256,256]{1,0:T(8,128)S(1)}, f32[256,256]{1,0:T(8,128)S(1)}, u32[]{:S(2)}, u32[]{:S(2)}) collective-permute-start(f32[256,256]{1,0:T(8,128)S(1)} %copy.98), channel_id=1, source_target_pairs={{8,0},{12,4},{16,8},{20,12},{24,16},{28,20},{32,24},{36,28},{40,32... | collective-permute-start | bytes 786440 | tf_op jit(solution)/shard_map/ppermute | solution.py:20
  114.1 8.6 %collective-permute-start.9 = (f32[256,256]{1,0:T(8,128)S(1)}, f32[256,256]{1,0:T(8,128)S(1)}, u32[]{:S(2)}, u32[]{:S(2)}) collective-permute-start(f32[256,256]{1,0:T(8,128)S(1)} %copy.104), channel_id=1, source_target_pairs={{56,0},{60,4},{0,8},{4,12},{8,16},{12,20},{16,24},{20,28},{24,32},... | collective-permute-start | bytes 786440 | tf_op jit(solution)/shard_map/ppermute | solution.py:20
  114.8 1.4 %copy-start.4 = (bf16[256,8,128]{0,2,1:T(8,128)(2,1)S(1)}, bf16[256,8,128]{0,2,1:T(8,128)(2,1)}, u32[]{:S(2)}) copy-start(bf16[256,8,128]{0,2,1:T(8,128)(2,1)} %get-tuple-element.795) | copy-start | bytes 1572868
  122.8 6.5 %collective-permute-start.8 = (f32[256,256]{1,0:T(8,128)S(1)}, f32[256,256]{1,0:T(8,128)S(1)}, u32[]{:S(2)}, u32[]{:S(2)}) collective-permute-start(f32[256,256]{1,0:T(8,128)S(1)} %get-tuple-element.607), channel_id=1, source_target_pairs={{8,0},{12,4},{16,8},{20,12},{24,16},{28,20},{32,24},{36,28},{40,32... | collective-permute-start | bytes 786440 | tf_op jit(solution)/shard_map/ppermute | solution.py:20
  122.9 7.7 %collective-permute-start.10 = (f32[256,256]{1,0:T(8,128)S(1)}, f32[256,256]{1,0:T(8,128)S(1)}, u32[]{:S(2)}, u32[]{:S(2)}) collective-permute-start(f32[256,256]{1,0:T(8,128)S(1)} %get-tuple-element.608), channel_id=1, source_target_pairs={{56,0},{60,4},{0,8},{4,12},{8,16},{12,20},{16,24},{20,28},{24,32},... | collective-permute-start | bytes 786440 | tf_op jit(solution)/shard_map/ppermute | solution.py:20
  130.6 8.0 %collective-permute-start.11 = (f32[256,256]{1,0:T(8,128)S(1)}, f32[256,256]{1,0:T(8,128)S(1)}, u32[]{:S(2)}, u32[]{:S(2)}) collective-permute-start(f32[256,256]{1,0:T(8,128)S(1)} %broadcast_select_fusion), channel_id=1, source_target_pairs={{0,4},{4,0},{8,12},{12,8},{16,20},{20,16},{24,28},{28,24},{32,36},... | collective-permute-start | bytes 786440 | tf_op jit(solution)/shard_map/ppermute | solution.py:25

commit v5 on v4

v5 whole, which is shorter than its diff:
```python
import math

import jax
import jax.numpy as jnp
from jax import lax
from jax.experimental import pallas as pl
from jax.experimental.pallas import tpu as pltpu
from jax.sharding import PartitionSpec as P

BLK = 128
HEAD_SIZE = 128
Y_HI = 2


def along_z(value, ctx_count, shift):
    z_count = ctx_count // Y_HI
    pairs = [
        (Y_HI * ((z + shift) % z_count) + h, Y_HI * z + h)
        for z in range(z_count)
        for h in range(Y_HI)
    ]
    return lax.ppermute(value, "ctx", pairs)


def from_partner(value, ctx_count):
    pairs = [(c, c ^ 1) for c in range(ctx_count)]
    return lax.ppermute(value, "ctx", pairs)


def turn_kernel(info_ref, q_ref, do_ref, kv_ref, lse_ref, delta_ref, dq_in_ref, dq_ref, dkdv_ref):
    tok_rows = q_ref.shape[0]
    key_count = kv_ref.shape[0]
    heads = q_ref.shape[1] // HEAD_SIZE
    scale = 1.0 / math.sqrt(HEAD_SIZE)
    row = lax.broadcasted_iota(jnp.int32, (tok_rows, key_count), 0)
    row_block = row // BLK
    flags = info_ref[0:1, :]
    for r in range(1, tok_rows // BLK):
        flags = jnp.where(row_block == r, info_ref[r : r + 1, :], flags)
    nb = tok_rows // BLK
    diag = (info_ref[nb : nb + 1, :] == row_block) & (info_ref[nb + 1 : nb + 2, :] <= row)
    live = (flags == 1) | diag
    keys = kv_ref[:, :HEAD_SIZE]
    values = kv_ref[:, HEAD_SIZE:]
    dk = jnp.zeros((key_count, HEAD_SIZE), jnp.float32)
    dv = jnp.zeros((key_count, HEAD_SIZE), jnp.float32)
    for h in range(heads):
        cols = slice(h * HEAD_SIZE, (h + 1) * HEAD_SIZE)
        q = q_ref[:, cols]
        do = do_ref[:, cols]
        s = lax.dot_general(q, keys, (((1,), (1,)), ((), ())), preferred_element_type=jnp.float32)
        p = jnp.where(live, jnp.exp(s * scale - lse_ref[:, h : h + 1]), 0.0)
        dp = lax.dot_general(do, values, (((1,), (1,)), ((), ())), preferred_element_type=jnp.float32)
        ds = (p * (dp - delta_ref[:, h : h + 1])).astype(jnp.bfloat16).astype(keys.dtype)
        dq_ref[:, cols] = dq_in_ref[:, cols] + jnp.dot(ds, keys, preferred_element_type=jnp.float32)
        dk = dk + lax.dot_general(ds, q, (((0,), (0,)), ((), ())), preferred_element_type=jnp.float32)
        dv = dv + lax.dot_general(
            p.astype(jnp.bfloat16).astype(do.dtype), do, (((0,), (0,)), ((), ())), preferred_element_type=jnp.float32
        )
    dkdv_ref[:, :HEAD_SIZE] = dk
    dkdv_ref[:, HEAD_SIZE:] = dv


def turn_call(info, q, do, kv, lse_t, delta_t, dq_acc):
    tok_rows, width = q.shape
    key_count = kv.shape[0]
    spec = pl.BlockSpec(memory_space=pltpu.MemorySpace.VMEM)
    return pl.pallas_call(
        turn_kernel,
        out_shape=(
            jax.ShapeDtypeStruct((tok_rows, width), jnp.float32),
            jax.ShapeDtypeStruct((key_count, 2 * HEAD_SIZE), jnp.float32),
        ),
        in_specs=[spec] * 7,
        out_specs=(spec, spec),
        input_output_aliases={6: 0},
    )(info, q, do, kv, lse_t, delta_t, dq_acc)


def local(query_rows, key_matrix, value_matrix, attn_out, out_grad, log_sums, block_mask):
    tok_rows = query_rows.shape[0]
    col_width = query_rows.shape[1]
    heads_local = col_width // HEAD_SIZE
    ctx_pos = lax.axis_index("ctx")
    ctx_count = lax.axis_size("ctx")
    tp_count = lax.axis_size("tp")
    grad_rows = out_grad.shape[0]
    pieces = out_grad.reshape(grad_rows, tp_count, col_width)
    own_grad = lax.all_to_all(pieces, "tp", split_axis=1, concat_axis=0, tiled=True)
    own_grad = own_grad.reshape(tok_rows, col_width)
    out_grads = own_grad.reshape(tok_rows, heads_local, HEAD_SIZE)
    outputs = attn_out.reshape(tok_rows, heads_local, HEAD_SIZE)
    delta_t = jnp.sum(out_grads.astype(jnp.float32) * outputs.astype(jnp.float32), axis=2)
    lse_t = log_sums.T
    query_start = ctx_pos * tok_rows
    z_pos = ctx_pos // Y_HI
    z_count = ctx_count // Y_HI
    y_hi = ctx_pos % Y_HI
    super_rows = Y_HI * tok_rows
    offsets = jnp.arange(tok_rows, dtype=jnp.int32)

    def terms(ahead_kv, behind_kv, turn, query_acc):
        ahead_owner = (z_pos + turn) % z_count
        behind_owner = (z_pos - turn) % z_count
        key_pos = jnp.concatenate(
            [ahead_owner * super_rows + offsets, behind_owner * super_rows + tok_rows + offsets]
        )
        key_block = key_pos // BLK
        query_block = query_start // BLK + jnp.arange(tok_rows // BLK, dtype=jnp.int32)
        mask_rows = lax.dynamic_slice_in_dim(block_mask, query_start // BLK, tok_rows // BLK, 0)
        allowed = jnp.take(mask_rows, key_block, axis=1)
        flags = (key_block[None, :] < query_block[:, None]) & (allowed == 1)
        info = jnp.concatenate(
            [
                flags.astype(jnp.int32),
                (key_block - query_start // BLK)[None, :],
                (key_pos - query_start)[None, :],
            ],
            axis=0,
        )
        key_values = jnp.concatenate([ahead_kv, behind_kv], axis=0)
        query_acc, kv_term = turn_call(
            info, query_rows, own_grad, key_values, lse_t, delta_t, query_acc
        )
        return query_acc, kv_term[:tok_rows], kv_term[tok_rows:]

    key_values = jnp.concatenate([key_matrix, value_matrix], axis=1)
    partner_kv = from_partner(key_values, ctx_count)
    ahead_kv = jnp.where(y_hi == 0, key_values, partner_kv)
    behind_kv = jnp.where(y_hi == 0, partner_kv, key_values)
    next_ahead = along_z(ahead_kv, ctx_count, 1)
    next_behind = along_z(behind_kv, ctx_count, -1)
    zero_query = jnp.zeros((tok_rows, col_width), jnp.float32)
    query_acc, ahead_pending, behind_pending = terms(ahead_kv, behind_kv, 0, zero_query)

    def visit_turn(turn, carried):
        ahead_kv, behind_kv, query_acc, ahead_pending, behind_pending = carried
        ahead_received = along_z(ahead_pending, ctx_count, 1)
        behind_received = along_z(behind_pending, ctx_count, -1)
        next_ahead = along_z(ahead_kv, ctx_count, 1)
        next_behind = along_z(behind_kv, ctx_count, -1)
        query_acc, ahead_term, behind_term = terms(ahead_kv, behind_kv, turn, query_acc)
        return (
            next_ahead,
            next_behind,
            query_acc,
            ahead_received + ahead_term,
            behind_received + behind_term,
        )

    ahead_kv, behind_kv, query_acc, ahead_pending, behind_pending = lax.fori_loop(
        1,
        z_count - 1,
        visit_turn,
        (next_ahead, next_behind, query_acc, ahead_pending, behind_pending),
    )
    ahead_received = along_z(ahead_pending, ctx_count, 1)
    behind_received = along_z(behind_pending, ctx_count, -1)
    query_acc, ahead_term, behind_term = terms(ahead_kv, behind_kv, z_count - 1, query_acc)
    ahead_total = along_z(ahead_received + ahead_term, ctx_count, 1)
    behind_total = along_z(behind_received + behind_term, ctx_count, -1)
    own_total = jnp.where(y_hi == 0, ahead_total, behind_total)
    other_total = jnp.where(y_hi == 0, behind_total, ahead_total)
    summed = own_total + from_partner(other_total, ctx_count)
    logit_scale = 1.0 / math.sqrt(HEAD_SIZE)
    query_grad = (query_acc * logit_scale).astype(jnp.bfloat16)
    key_gradient = (summed[:, :HEAD_SIZE] * logit_scale).astype(jnp.bfloat16)
    value_gradient = summed[:, HEAD_SIZE:].astype(jnp.bfloat16)
    return (query_grad, key_gradient, value_gradient)


def solution(mesh):
    placed = (
        P(("dp", "ctx"), "tp"),
        P(("dp", "ctx"), "tp"),
        P(("dp", "ctx"), "tp"),
        P(("dp", "ctx"), "tp"),
        P(("dp", "ctx", "tp"), None),
        P("tp", ("dp", "ctx")),
        P("dp", None),
    )
    return jax.shard_map(
        local,
        mesh=mesh,
        in_specs=placed,
        out_specs=(P(("dp", "ctx"), "tp"), P(("dp", "ctx"), "tp"), P(("dp", "ctx"), "tp")),
        check_vma=False,
    )
```

time: 141 us -> 205 us (1.45)
  Pallas kernels: 0 us -> 45.9 us
  matrix products: 39.2 us -> 0 us
  other arithmetic: 11.2 us -> 42.9 us
  local copies, waits for them, and re-layouts: 18 us -> 48.8 us
  waiting for transfers between devices: 19.1 us -> 12.9 us
    pallas_call x0 -> x8, Pallas kernels: none -> 45.9 us  [turn_call(): pl.pallas_call(turn_kernel, out_shape=(jax.ShapeDtypeStruct((tok_rows, wi...]
    dot_general x40 -> x0, matrix products: 39.2 us -> none  [the longest x8 11.2 us: contract(): jnp.einsum('igd,jd->gij', out_grads, values_part, preferred_element_type=...]
    while x32 -> x96, local copies, waits for them, and re-layouts: 2.39 us -> 20.6 us  [the longest x2 2.19 us: local(): lax.fori_loop(1, z_count - 1, visit_turn, (next_ahead, next_behind, query...]
    gather x8 -> x16, local copies, waits for them, and re-layouts: 4.47 us -> 17.8 us  [terms(): allowed = jnp.take(mask_rows, key_block, axis=1)]
    concatenate x1 -> x16, other arithmetic: 0.84 us -> 11.7 us  [the longest x8 6.78 us: terms(): key_values = jnp.concatenate([ahead_kv, behind_kv], axis=0)]
    ppermute x30, waiting for transfers between devices: 12.7 us -> 6.2 us  [along_z(): return lax.ppermute(value, 'ctx', pairs)]
    convert_element_type x1 -> x9, other arithmetic: 0.17 us -> 6.26 us  [the longest x7 5.27 us: terms(): flags.astype(jnp.int32)]
    add x6, other arithmetic: 5.28 us -> 11.4 us  [visit_turn(): behind_received + behind_term]
  transfers between devices with their start and end apart: 33 -> 33, of which waited for: 7 -> 3; matrix products, arithmetic and copies ran while one was open for 45% -> 32% of each run, Pallas kernels for 0% -> 23%
where the time goes in v5:
time: 205 us; the launch traced here: 203 us
  starting transfers between devices  51 us (25%)
  local copies, waits for them, and re-layouts  48.8 us (24%)
  Pallas kernels  45.9 us (22%)
  other arithmetic  42.9 us (21%)
  waiting for transfers between devices  12.9 us (6%)
    pallas_call x8, Pallas kernels, turn_call(): pl.pallas_call(turn_kernel, out_shape=(jax.ShapeDtypeStruct((tok_rows, wi...  45.9 us
    ppermute x30, starting transfers between devices, along_z(): return lax.ppermute(value, 'ctx', pairs)  43.9 us
    while x96, local copies, waits for them, and re-layouts  20.6 us
    gather x16, local copies, waits for them, and re-layouts, terms(): allowed = jnp.take(mask_rows, key_block, axis=1)  17.8 us
    add x6, other arithmetic, visit_turn(): behind_received + behind_term  11.4 us
    concatenate x8, other arithmetic, terms(): key_values = jnp.concatenate([ahead_kv, behind_kv], axis=0)  6.78 us
    ppermute x2, waiting for transfers between devices, from_partner(): return lax.ppermute(value, 'ctx', pairs)  6.67 us
    ppermute x30, waiting for transfers between devices, along_z(): return lax.ppermute(value, 'ctx', pairs)  6.2 us
  transfers between devices with their start and end apart: 33, of which 3 were waited for; matrix products, arithmetic and copies ran while one was open for 32% of the time, Pallas kernels for 23%

profile of v5, /device:TPU:4, one launch (start us, length us, event | category | flops | bytes accessed | tf_op | source)
XLA Modules:
  0.0 202.7 jit_solution(12521240467543297723)
XLA Ops:
  0.7 0.9 constant_dynamic-update-slice_fusion.1
  1.6 3.3 %collective-permute-start.4 = (bf16[256,256]{1,0:T(8,128)(2,1)S(1)}, bf16[256,256]{1,0:T(8,128)(2,1)S(1)}, u32[]{:S(2)}, u32[]{:S(2)}) collective-permute-start(bf16[256,256]{1,0:T(8,128)(2,1)S(1)} %constant_dynamic-update-slice_fusion), channel_id=1, source_target_pairs={{0,4},{4,0},{8,12},{12,8},{16,20},{20,16},{24,28},{28,24},{32,36},... | collective-permute-start | bytes 393224 | tf_op jit(solution)/shard_map/ppermute | solution.py:27
  4.9 1.9 copy.24
  6.7 3.5 %all-to-all-start = ((bf16[64,4,1024]{2,0,1:T(8,128)(2,1)}), bf16[64,4,1024]{2,0,1:T(8,128)(2,1)S(1)}, u32[]{:S(2)}, u32[]{:S(2)}) async-start(bf16[64,4,1024]{2,0,1:T(8,128)(2,1)} %bitcast.30), calls=%async_computation | async-start | bytes 1048576 | tf_op jit(solution)/shard_map/all_to_all | solution.py:89
  10.6 1.0 gather_fusion.2
  11.7 1.0 gather_fusion.1
  15.7 1.2 copy.22
  17.0 2.0 collective-permute-start.6
  19.0 4.2 %collective-permute-start.5 = (bf16[256,256]{1,0:T(8,128)(2,1)S(1)}, bf16[256,256]{1,0:T(8,128)(2,1)}, u32[]{:S(2)}, u32[]{:S(2)}) collective-permute-start(bf16[256,256]{1,0:T(8,128)(2,1)S(1)} %get-tuple-element.579), channel_id=1, source_target_pairs={{8,0},{12,4},{16,8},{20,12},{24,16},{28,20},{32,24},{36,28},{40,32... | collective-permute-start | bytes 393224 | tf_op jit(solution)/shard_map/ppermute | solution.py:22
  24.2 1.0 copy-done.2
  25.7 0.9 copy-done.1
  26.6 5.7 %shard_map.94 = (f32[256,1024]{1,0:T(8,128)S(1)}, f32[512,256]{1,0:T(8,128)}) custom-call(s32[4,512]{1,0:T(4,128)} %pad_add_fusion.4.info_ref, bf16[256,1024]{1,0:T(8,128)(2,1)S(1)} %copy-done.1, bf16[256,1024]{1,0:T(8,128)(2,1)S(1)} %bitcast.37, bf16[512,256]{1,0:T(8,128)(2,1)} %pad_maximum_fusion.1.kv_ref, ...), custom_call_target="tpu_custom_call", output_to_operand_aliasing={{0}: (6, {})} | custom-call | tf_op jit(solution)/shard_map/pallas_call | solution.py:68
  32.4 1.9 fusion.12
  34.2 137.6 %while.26 = (s32[]{:T(128)}, bf16[256,256]{1,0:T(8,128)(2,1)}, bf16[256,256]{1,0:T(8,128)(2,1)S(1)}, f32[256,1024]{1,0:T(8,128)S(1)}, f32[256,256]{1,0:T(8,128)}...) while((s32[]{:T(128)}, bf16[256,256]{1,0:T(8,128)(2,1)}, ...), condition=%wide.region_2.4_spmd.clone.clone, body=%wide.region_1.3_spmd.clone.clone.sunk | while | flops 688159 | bytes 5863283 | solution.py:151
  34.3 0.9 copy.37
  35.2 1.8 collective-permute-start
  37.4 3.1 %collective-permute-start.3 = (f32[256,256]{1,0:T(8,128)}, f32[256,256]{1,0:T(8,128)S(1)}, u32[]{:S(2)}, u32[]{:S(2)}) collective-permute-start(f32[256,256]{1,0:T(8,128)} %get-tuple-element.719), channel_id=1, source_target_pairs={{8,0},{12,4},{16,8},{20,12},{24,16},{28,20},{32,24},{36,28},{40,32... | collective-permute-start | bytes 786440 | tf_op jit(solution)/shard_map/while/body/eval_jaxpr/ppermute | solution.py:22
  43.4 1.9 gather_fusion
  46.7 0.8 and_convert_fusion.4
  49.5 5.7 %eval_jaxpr.9 = (f32[256,1024]{1,0:T(8,128)S(1)}, f32[512,256]{1,0:T(8,128)}) custom-call(s32[4,512]{1,0:T(4,128)} %pad_add_fusion.10.info_ref, bf16[256,1024]{1,0:T(8,128)(2,1)S(1)} %get-tuple-element.745.q_ref, bf16[256,1024]{1,0:T(8,128)(2,1)S(1)} %get-tuple-element.746.do_ref, ...), custom_call_target="tpu_custom_call", output_to_operand_aliasing={{0}: (6, {})} | custom-call | tf_op jit(solution)/shard_map/while/body/eval_jaxpr/pallas_call | solution.py:68
  55.3 1.9 slice_add_fusion.5
  57.2 0.9 copy.37
  58.1 1.8 collective-permute-start
  60.3 3.1 %collective-permute-start.3 = (f32[256,256]{1,0:T(8,128)}, f32[256,256]{1,0:T(8,128)S(1)}, u32[]{:S(2)}, u32[]{:S(2)}) collective-permute-start(f32[256,256]{1,0:T(8,128)} %get-tuple-element.719), channel_id=1, source_target_pairs={{8,0},{12,4},{16,8},{20,12},{24,16},{28,20},{32,24},{36,28},{40,32... | collective-permute-start | bytes 786440 | tf_op jit(solution)/shard_map/while/body/eval_jaxpr/ppermute | solution.py:22
  66.4 1.9 gather_fusion
  69.6 0.8 and_convert_fusion.4
  72.5 5.7 %eval_jaxpr.9 = (f32[256,1024]{1,0:T(8,128)S(1)}, f32[512,256]{1,0:T(8,128)}) custom-call(s32[4,512]{1,0:T(4,128)} %pad_add_fusion.10.info_ref, bf16[256,1024]{1,0:T(8,128)(2,1)S(1)} %get-tuple-element.745.q_ref, bf16[256,1024]{1,0:T(8,128)(2,1)S(1)} %get-tuple-element.746.do_ref, ...), custom_call_target="tpu_custom_call", output_to_operand_aliasing={{0}: (6, {})} | custom-call | tf_op jit(solution)/shard_map/while/body/eval_jaxpr/pallas_call | solution.py:68
  78.2 1.9 slice_add_fusion.5
  80.1 0.9 copy.37
  81.0 1.8 collective-permute-start
  83.2 3.1 %collective-permute-start.3 = (f32[256,256]{1,0:T(8,128)}, f32[256,256]{1,0:T(8,128)S(1)}, u32[]{:S(2)}, u32[]{:S(2)}) collective-permute-start(f32[256,256]{1,0:T(8,128)} %get-tuple-element.719), channel_id=1, source_target_pairs={{8,0},{12,4},{16,8},{20,12},{24,16},{28,20},{32,24},{36,28},{40,32... | collective-permute-start | bytes 786440 | tf_op jit(solution)/shard_map/while/body/eval_jaxpr/ppermute | solution.py:22
  89.3 1.9 gather_fusion
  92.6 0.8 and_convert_fusion.4
  95.4 5.7 %eval_jaxpr.9 = (f32[256,1024]{1,0:T(8,128)S(1)}, f32[512,256]{1,0:T(8,128)}) custom-call(s32[4,512]{1,0:T(4,128)} %pad_add_fusion.10.info_ref, bf16[256,1024]{1,0:T(8,128)(2,1)S(1)} %get-tuple-element.745.q_ref, bf16[256,1024]{1,0:T(8,128)(2,1)S(1)} %get-tuple-element.746.do_ref, ...), custom_call_target="tpu_custom_call", output_to_operand_aliasing={{0}: (6, {})} | custom-call | tf_op jit(solution)/shard_map/while/body/eval_jaxpr/pallas_call | solution.py:68
  101.1 1.9 slice_add_fusion.5
  103.0 0.9 copy.37
  103.9 1.8 collective-permute-start
  106.1 3.1 %collective-permute-start.3 = (f32[256,256]{1,0:T(8,128)}, f32[256,256]{1,0:T(8,128)S(1)}, u32[]{:S(2)}, u32[]{:S(2)}) collective-permute-start(f32[256,256]{1,0:T(8,128)} %get-tuple-element.719), channel_id=1, source_target_pairs={{8,0},{12,4},{16,8},{20,12},{24,16},{28,20},{32,24},{36,28},{40,32... | collective-permute-start | bytes 786440 | tf_op jit(solution)/shard_map/while/body/eval_jaxpr/ppermute | solution.py:22
  112.2 1.9 gather_fusion
  118.3 5.7 %eval_jaxpr.9 = (f32[256,1024]{1,0:T(8,128)S(1)}, f32[512,256]{1,0:T(8,128)}) custom-call(s32[4,512]{1,0:T(4,128)} %pad_add_fusion.10.info_ref, bf16[256,1024]{1,0:T(8,128)(2,1)S(1)} %get-tuple-element.745.q_ref, bf16[256,1024]{1,0:T(8,128)(2,1)S(1)} %get-tuple-element.746.do_ref, ...), custom_call_target="tpu_custom_call", output_to_operand_aliasing={{0}: (6, {})} | custom-call | tf_op jit(solution)/shard_map/while/body/eval_jaxpr/pallas_call | solution.py:68
  124.1 1.9 slice_add_fusion.5
  126.0 0.9 copy.37
  126.9 1.8 collective-permute-start
  129.1 3.1 %collective-permute-start.3 = (f32[256,256]{1,0:T(8,128)}, f32[256,256]{1,0:T(8,128)S(1)}, u32[]{:S(2)}, u32[]{:S(2)}) collective-permute-start(f32[256,256]{1,0:T(8,128)} %get-tuple-element.719), channel_id=1, source_target_pairs={{8,0},{12,4},{16,8},{20,12},{24,16},{28,20},{32,24},{36,28},{40,32... | collective-permute-start | bytes 786440 | tf_op jit(solution)/shard_map/while/body/eval_jaxpr/ppermute | solution.py:22
  135.1 1.9 gather_fusion
  138.4 0.8 and_convert_fusion.4
  141.2 5.7 %eval_jaxpr.9 = (f32[256,1024]{1,0:T(8,128)S(1)}, f32[512,256]{1,0:T(8,128)}) custom-call(s32[4,512]{1,0:T(4,128)} %pad_add_fusion.10.info_ref, bf16[256,1024]{1,0:T(8,128)(2,1)S(1)} %get-tuple-element.745.q_ref, bf16[256,1024]{1,0:T(8,128)(2,1)S(1)} %get-tuple-element.746.do_ref, ...), custom_call_target="tpu_custom_call", output_to_operand_aliasing={{0}: (6, {})} | custom-call | tf_op jit(solution)/shard_map/while/body/eval_jaxpr/pallas_call | solution.py:68
  147.0 1.9 slice_add_fusion.5
  148.9 0.9 copy.37
  149.8 1.8 collective-permute-start
  152.0 3.1 %collective-permute-start.3 = (f32[256,256]{1,0:T(8,128)}, f32[256,256]{1,0:T(8,128)S(1)}, u32[]{:S(2)}, u32[]{:S(2)}) collective-permute-start(f32[256,256]{1,0:T(8,128)} %get-tuple-element.719), channel_id=1, source_target_pairs={{8,0},{12,4},{16,8},{20,12},{24,16},{28,20},{32,24},{36,28},{40,32... | collective-permute-start | bytes 786440 | tf_op jit(solution)/shard_map/while/body/eval_jaxpr/ppermute | solution.py:22
  158.1 1.9 gather_fusion
  161.4 0.8 and_convert_fusion.4
  164.2 5.7 %eval_jaxpr.9 = (f32[256,1024]{1,0:T(8,128)S(1)}, f32[512,256]{1,0:T(8,128)}) custom-call(s32[4,512]{1,0:T(4,128)} %pad_add_fusion.10.info_ref, bf16[256,1024]{1,0:T(8,128)(2,1)S(1)} %get-tuple-element.745.q_ref, bf16[256,1024]{1,0:T(8,128)(2,1)S(1)} %get-tuple-element.746.do_ref, ...), custom_call_target="tpu_custom_call", output_to_operand_aliasing={{0}: (6, {})} | custom-call | tf_op jit(solution)/shard_map/while/body/eval_jaxpr/pallas_call | solution.py:68
  169.9 1.9 slice_add_fusion.5
  172.1 3.2 %collective-permute-start.7 = (f32[256,256]{1,0:T(8,128)}, f32[256,256]{1,0:T(8,128)S(1)}, u32[]{:S(2)}, u32[]{:S(2)}) collective-permute-start(f32[256,256]{1,0:T(8,128)} %get-tuple-element.463), channel_id=1, source_target_pairs={{8,0},{12,4},{16,8},{20,12},{24,16},{28,20},{32,24},{36,28},{40,32... | collective-permute-start | bytes 786440 | tf_op jit(solution)/shard_map/ppermute | solution.py:22
  176.7 1.6 pad_maximum_fusion.2.kv_ref
  178.3 5.7 %shard_map.95 = (f32[256,1024]{1,0:T(8,128)S(1)}, f32[512,256]{1,0:T(8,128)}) custom-call(s32[4,512]{1,0:T(4,128)} %pad_add_fusion.3.info_ref, bf16[256,1024]{1,0:T(8,128)(2,1)S(1)} %get-tuple-element.757, bf16[256,1024]{1,0:T(8,128)(2,1)S(1)} %get-tuple-element.756, bf16[512,256]{1,0:T(8,128)(2,1)} %pad_maximum_fusion.2.kv_ref, ...), custom_call_target="tpu_custom_call", output_to_operand_aliasing={{0}: (6, {})} | custom-call | tf_op jit(solution)/shard_map/pallas_call | solution.py:68
  184.0 1.1 slice_add_fusion.3
  185.8 1.5 collective-permute-start.10
  187.2 4.3 %collective-permute-done.8 = f32[256,256]{1,0:T(8,128)S(1)} collective-permute-done((f32[256,256]{1,0:T(8,128)S(1)}, f32[256,256]{1,0:T(8,128)S(1)}, u32[]{:S(2)}, u32[]{:S(2)}) %collective-permute-start.8) | collective-permute-done | bytes 262176 | tf_op jit(solution)/shard_map/ppermute | solution.py:22
  191.6 1.8 collective-permute-done.10
  193.8 0.9 multiply_convert_fusion
  194.7 6.7 %collective-permute-done.11 = f32[256,256]{1,0:T(8,128)S(1)} collective-permute-done((f32[256,256]{1,0:T(8,128)S(1)}, f32[256,256]{1,0:T(8,128)S(1)}, u32[]{:S(2)}, u32[]{:S(2)}) %collective-permute-start.11) | collective-permute-done | bytes 262176 | tf_op jit(solution)/shard_map/ppermute | solution.py:27
  (239 shorter events, 50.4 us)
Async XLA Ops:
  0.6 9.8 %copy-start = (s32[32,32]{1,0:T(8,128)S(1)}, s32[32,32]{1,0:T(8,128)}, u32[]{:S(2)}) copy-start(s32[32,32]{1,0:T(8,128)} %param.17) | copy-start | bytes 12292
  0.6 0.9 copy-start.10
  1.6 15.3 %collective-permute-start.4 = (bf16[256,256]{1,0:T(8,128)(2,1)S(1)}, bf16[256,256]{1,0:T(8,128)(2,1)S(1)}, u32[]{:S(2)}, u32[]{:S(2)}) collective-permute-start(bf16[256,256]{1,0:T(8,128)(2,1)S(1)} %constant_dynamic-update-slice_fusion), channel_id=1, source_target_pairs={{0,4},{4,0},{8,12},{12,8},{16,20},{20,16},{24,28},{28,24},{32,36},... | collective-permute-start | bytes 393224 | tf_op jit(solution)/shard_map/ppermute | solution.py:27
  6.7 17.2 %all-to-all-start = ((bf16[64,4,1024]{2,0,1:T(8,128)(2,1)}), bf16[64,4,1024]{2,0,1:T(8,128)(2,1)S(1)}, u32[]{:S(2)}, u32[]{:S(2)}) async-start(bf16[64,4,1024]{2,0,1:T(8,128)(2,1)} %bitcast.30), calls=%async_computation | async-start | bytes 1048576 | tf_op jit(solution)/shard_map/all_to_all | solution.py:89
  10.2 2.7 %copy-start.4 = (bf16[256,1024]{1,0:T(8,128)(2,1)S(1)}, bf16[256,1024]{1,0:T(8,128)(2,1)}, u32[]{:S(2)}) copy-start(bf16[256,1024]{1,0:T(8,128)(2,1)} %param.14) | copy-start | bytes 1572868
  10.6 1.2 copy-start.3
  14.9 0.7 copy-start.14
  17.0 17.3 %collective-permute-start.6 = (bf16[256,256]{1,0:T(8,128)(2,1)S(1)}, bf16[256,256]{1,0:T(8,128)(2,1)S(1)}, u32[]{:S(2)}, u32[]{:S(2)}) collective-permute-start(bf16[256,256]{1,0:T(8,128)(2,1)S(1)} %get-tuple-element.578), channel_id=1, source_target_pairs={{56,0},{60,4},{0,8},{4,12},{8,16},{12,20},{16,24},{20,28},{24,32},... | collective-permute-start | bytes 393224 | tf_op jit(solution)/shard_map/ppermute | solution.py:22
  19.0 15.3 %collective-permute-start.5 = (bf16[256,256]{1,0:T(8,128)(2,1)S(1)}, bf16[256,256]{1,0:T(8,128)(2,1)}, u32[]{:S(2)}, u32[]{:S(2)}) collective-permute-start(bf16[256,256]{1,0:T(8,128)(2,1)S(1)} %get-tuple-element.579), channel_id=1, source_target_pairs={{8,0},{12,4},{16,8},{20,12},{24,16},{28,20},{32,24},{36,28},{40,32... | collective-permute-start | bytes 393224 | tf_op jit(solution)/shard_map/ppermute | solution.py:22
  24.0 1.2 copy-start.2
  25.6 1.0 copy-start.1
  35.2 22.0 %collective-permute-start = (bf16[256,256]{1,0:T(8,128)(2,1)S(1)}, bf16[256,256]{1,0:T(8,128)(2,1)}, u32[]{:S(2)}, u32[]{:S(2)}) collective-permute-start(bf16[256,256]{1,0:T(8,128)(2,1)S(1)} %copy.37), channel_id=1, source_target_pairs={{8,0},{12,4},{16,8},{20,12},{24,16},{28,20},{32,24},{36,28},{40,32... | collective-permute-start | bytes 393224 | tf_op jit(solution)/shard_map/while/body/eval_jaxpr/ppermute | solution.py:22
  36.9 20.2 %collective-permute-start.1 = (bf16[256,256]{1,0:T(8,128)(2,1)S(1)}, bf16[256,256]{1,0:T(8,128)(2,1)S(1)}, u32[]{:S(2)}, u32[]{:S(2)}) collective-permute-start(bf16[256,256]{1,0:T(8,128)(2,1)S(1)} %copy.38), channel_id=1, source_target_pairs={{56,0},{60,4},{0,8},{4,12},{8,16},{12,20},{16,24},{20,28},{24,32},... | collective-permute-start | bytes 393224 | tf_op jit(solution)/shard_map/while/body/eval_jaxpr/ppermute | solution.py:22
  37.3 18.0 %collective-permute-start.2 = (f32[256,256]{1,0:T(8,128)}, f32[256,256]{1,0:T(8,128)S(1)}, u32[]{:S(2)}, u32[]{:S(2)}) collective-permute-start(f32[256,256]{1,0:T(8,128)} %get-tuple-element.720), channel_id=1, source_target_pairs={{56,0},{60,4},{0,8},{4,12},{8,16},{12,20},{16,24},{20,28},{24,32},... | collective-permute-start | bytes 786440 | tf_op jit(solution)/shard_map/while/body/eval_jaxpr/ppermute | solution.py:22
  37.4 17.9 %collective-permute-start.3 = (f32[256,256]{1,0:T(8,128)}, f32[256,256]{1,0:T(8,128)S(1)}, u32[]{:S(2)}, u32[]{:S(2)}) collective-permute-start(f32[256,256]{1,0:T(8,128)} %get-tuple-element.719), channel_id=1, source_target_pairs={{8,0},{12,4},{16,8},{20,12},{24,16},{28,20},{32,24},{36,28},{40,32... | collective-permute-start | bytes 786440 | tf_op jit(solution)/shard_map/while/body/eval_jaxpr/ppermute | solution.py:22
  46.0 0.6 copy-start.11
  46.0 0.7 copy-start.13
  47.5 0.7 copy-start.9
  47.5 0.7 copy-start.7
  58.1 22.0 %collective-permute-start = (bf16[256,256]{1,0:T(8,128)(2,1)S(1)}, bf16[256,256]{1,0:T(8,128)(2,1)}, u32[]{:S(2)}, u32[]{:S(2)}) collective-permute-start(bf16[256,256]{1,0:T(8,128)(2,1)S(1)} %copy.37), channel_id=1, source_target_pairs={{8,0},{12,4},{16,8},{20,12},{24,16},{28,20},{32,24},{36,28},{40,32... | collective-permute-start | bytes 393224 | tf_op jit(solution)/shard_map/while/body/eval_jaxpr/ppermute | solution.py:22
  59.9 20.2 %collective-permute-start.1 = (bf16[256,256]{1,0:T(8,128)(2,1)S(1)}, bf16[256,256]{1,0:T(8,128)(2,1)S(1)}, u32[]{:S(2)}, u32[]{:S(2)}) collective-permute-start(bf16[256,256]{1,0:T(8,128)(2,1)S(1)} %copy.38), channel_id=1, source_target_pairs={{56,0},{60,4},{0,8},{4,12},{8,16},{12,20},{16,24},{20,28},{24,32},... | collective-permute-start | bytes 393224 | tf_op jit(solution)/shard_map/while/body/eval_jaxpr/ppermute | solution.py:22
  60.2 18.0 %collective-permute-start.2 = (f32[256,256]{1,0:T(8,128)}, f32[256,256]{1,0:T(8,128)S(1)}, u32[]{:S(2)}, u32[]{:S(2)}) collective-permute-start(f32[256,256]{1,0:T(8,128)} %get-tuple-element.720), channel_id=1, source_target_pairs={{56,0},{60,4},{0,8},{4,12},{8,16},{12,20},{16,24},{20,28},{24,32},... | collective-permute-start | bytes 786440 | tf_op jit(solution)/shard_map/while/body/eval_jaxpr/ppermute | solution.py:22
  60.3 17.9 %collective-permute-start.3 = (f32[256,256]{1,0:T(8,128)}, f32[256,256]{1,0:T(8,128)S(1)}, u32[]{:S(2)}, u32[]{:S(2)}) collective-permute-start(f32[256,256]{1,0:T(8,128)} %get-tuple-element.719), channel_id=1, source_target_pairs={{8,0},{12,4},{16,8},{20,12},{24,16},{28,20},{32,24},{36,28},{40,32... | collective-permute-start | bytes 786440 | tf_op jit(solution)/shard_map/while/body/eval_jaxpr/ppermute | solution.py:22
  69.0 0.6 copy-start.11
  69.0 0.7 copy-start.13
  70.4 0.7 copy-start.9
  70.4 0.7 copy-start.7
  81.0 22.0 %collective-permute-start = (bf16[256,256]{1,0:T(8,128)(2,1)S(1)}, bf16[256,256]{1,0:T(8,128)(2,1)}, u32[]{:S(2)}, u32[]{:S(2)}) collective-permute-start(bf16[256,256]{1,0:T(8,128)(2,1)S(1)} %copy.37), channel_id=1, source_target_pairs={{8,0},{12,4},{16,8},{20,12},{24,16},{28,20},{32,24},{36,28},{40,32... | collective-permute-start | bytes 393224 | tf_op jit(solution)/shard_map/while/body/eval_jaxpr/ppermute | solution.py:22
  82.8 20.2 %collective-permute-start.1 = (bf16[256,256]{1,0:T(8,128)(2,1)S(1)}, bf16[256,256]{1,0:T(8,128)(2,1)S(1)}, u32[]{:S(2)}, u32[]{:S(2)}) collective-permute-start(bf16[256,256]{1,0:T(8,128)(2,1)S(1)} %copy.38), channel_id=1, source_target_pairs={{56,0},{60,4},{0,8},{4,12},{8,16},{12,20},{16,24},{20,28},{24,32},... | collective-permute-start | bytes 393224 | tf_op jit(solution)/shard_map/while/body/eval_jaxpr/ppermute | solution.py:22
  83.1 18.0 %collective-permute-start.2 = (f32[256,256]{1,0:T(8,128)}, f32[256,256]{1,0:T(8,128)S(1)}, u32[]{:S(2)}, u32[]{:S(2)}) collective-permute-start(f32[256,256]{1,0:T(8,128)} %get-tuple-element.720), channel_id=1, source_target_pairs={{56,0},{60,4},{0,8},{4,12},{8,16},{12,20},{16,24},{20,28},{24,32},... | collective-permute-start | bytes 786440 | tf_op jit(solution)/shard_map/while/body/eval_jaxpr/ppermute | solution.py:22
  83.2 17.9 %collective-permute-start.3 = (f32[256,256]{1,0:T(8,128)}, f32[256,256]{1,0:T(8,128)S(1)}, u32[]{:S(2)}, u32[]{:S(2)}) collective-permute-start(f32[256,256]{1,0:T(8,128)} %get-tuple-element.719), channel_id=1, source_target_pairs={{8,0},{12,4},{16,8},{20,12},{24,16},{28,20},{32,24},{36,28},{40,32... | collective-permute-start | bytes 786440 | tf_op jit(solution)/shard_map/while/body/eval_jaxpr/ppermute | solution.py:22
  91.9 0.6 copy-start.11
  91.9 0.7 copy-start.13
  93.3 0.7 copy-start.9
  93.3 0.7 copy-start.7
  103.9 22.0 %collective-permute-start = (bf16[256,256]{1,0:T(8,128)(2,1)S(1)}, bf16[256,256]{1,0:T(8,128)(2,1)}, u32[]{:S(2)}, u32[]{:S(2)}) collective-permute-start(bf16[256,256]{1,0:T(8,128)(2,1)S(1)} %copy.37), channel_id=1, source_target_pairs={{8,0},{12,4},{16,8},{20,12},{24,16},{28,20},{32,24},{36,28},{40,32... | collective-permute-start | bytes 393224 | tf_op jit(solution)/shard_map/while/body/eval_jaxpr/ppermute | solution.py:22
  105.7 20.2 %collective-permute-start.1 = (bf16[256,256]{1,0:T(8,128)(2,1)S(1)}, bf16[256,256]{1,0:T(8,128)(2,1)S(1)}, u32[]{:S(2)}, u32[]{:S(2)}) collective-permute-start(bf16[256,256]{1,0:T(8,128)(2,1)S(1)} %copy.38), channel_id=1, source_target_pairs={{56,0},{60,4},{0,8},{4,12},{8,16},{12,20},{16,24},{20,28},{24,32},... | collective-permute-start | bytes 393224 | tf_op jit(solution)/shard_map/while/body/eval_jaxpr/ppermute | solution.py:22
  106.0 18.0 %collective-permute-start.2 = (f32[256,256]{1,0:T(8,128)}, f32[256,256]{1,0:T(8,128)S(1)}, u32[]{:S(2)}, u32[]{:S(2)}) collective-permute-start(f32[256,256]{1,0:T(8,128)} %get-tuple-element.720), channel_id=1, source_target_pairs={{56,0},{60,4},{0,8},{4,12},{8,16},{12,20},{16,24},{20,28},{24,32},... | collective-permute-start | bytes 786440 | tf_op jit(solution)/shard_map/while/body/eval_jaxpr/ppermute | solution.py:22
  106.1 17.9 %collective-permute-start.3 = (f32[256,256]{1,0:T(8,128)}, f32[256,256]{1,0:T(8,128)S(1)}, u32[]{:S(2)}, u32[]{:S(2)}) collective-permute-start(f32[256,256]{1,0:T(8,128)} %get-tuple-element.719), channel_id=1, source_target_pairs={{8,0},{12,4},{16,8},{20,12},{24,16},{28,20},{32,24},{36,28},{40,32... | collective-permute-start | bytes 786440 | tf_op jit(solution)/shard_map/while/body/eval_jaxpr/ppermute | solution.py:22
  114.8 0.7 copy-start.13
  116.3 0.7 copy-start.9
  116.3 0.7 copy-start.7
  126.9 22.0 %collective-permute-start = (bf16[256,256]{1,0:T(8,128)(2,1)S(1)}, bf16[256,256]{1,0:T(8,128)(2,1)}, u32[]{:S(2)}, u32[]{:S(2)}) collective-permute-start(bf16[256,256]{1,0:T(8,128)(2,1)S(1)} %copy.37), channel_id=1, source_target_pairs={{8,0},{12,4},{16,8},{20,12},{24,16},{28,20},{32,24},{36,28},{40,32... | collective-permute-start | bytes 393224 | tf_op jit(solution)/shard_map/while/body/eval_jaxpr/ppermute | solution.py:22
  128.6 20.2 %collective-permute-start.1 = (bf16[256,256]{1,0:T(8,128)(2,1)S(1)}, bf16[256,256]{1,0:T(8,128)(2,1)S(1)}, u32[]{:S(2)}, u32[]{:S(2)}) collective-permute-start(bf16[256,256]{1,0:T(8,128)(2,1)S(1)} %copy.38), channel_id=1, source_target_pairs={{56,0},{60,4},{0,8},{4,12},{8,16},{12,20},{16,24},{20,28},{24,32},... | collective-permute-start | bytes 393224 | tf_op jit(solution)/shard_map/while/body/eval_jaxpr/ppermute | solution.py:22
  129.0 18.0 %collective-permute-start.2 = (f32[256,256]{1,0:T(8,128)}, f32[256,256]{1,0:T(8,128)S(1)}, u32[]{:S(2)}, u32[]{:S(2)}) collective-permute-start(f32[256,256]{1,0:T(8,128)} %get-tuple-element.720), channel_id=1, source_target_pairs={{56,0},{60,4},{0,8},{4,12},{8,16},{12,20},{16,24},{20,28},{24,32},... | collective-permute-start | bytes 786440 | tf_op jit(solution)/shard_map/while/body/eval_jaxpr/ppermute | solution.py:22
  129.1 17.9 %collective-permute-start.3 = (f32[256,256]{1,0:T(8,128)}, f32[256,256]{1,0:T(8,128)S(1)}, u32[]{:S(2)}, u32[]{:S(2)}) collective-permute-start(f32[256,256]{1,0:T(8,128)} %get-tuple-element.719), channel_id=1, source_target_pairs={{8,0},{12,4},{16,8},{20,12},{24,16},{28,20},{32,24},{36,28},{40,32... | collective-permute-start | bytes 786440 | tf_op jit(solution)/shard_map/while/body/eval_jaxpr/ppermute | solution.py:22
  137.7 0.7 copy-start.13
  139.2 0.7 copy-start.9
  139.2 0.7 copy-start.7
  149.8 22.0 %collective-permute-start = (bf16[256,256]{1,0:T(8,128)(2,1)S(1)}, bf16[256,256]{1,0:T(8,128)(2,1)}, u32[]{:S(2)}, u32[]{:S(2)}) collective-permute-start(bf16[256,256]{1,0:T(8,128)(2,1)S(1)} %copy.37), channel_id=1, source_target_pairs={{8,0},{12,4},{16,8},{20,12},{24,16},{28,20},{32,24},{36,28},{40,32... | collective-permute-start | bytes 393224 | tf_op jit(solution)/shard_map/while/body/eval_jaxpr/ppermute | solution.py:22
  151.6 20.2 %collective-permute-start.1 = (bf16[256,256]{1,0:T(8,128)(2,1)S(1)}, bf16[256,256]{1,0:T(8,128)(2,1)S(1)}, u32[]{:S(2)}, u32[]{:S(2)}) collective-permute-start(bf16[256,256]{1,0:T(8,128)(2,1)S(1)} %copy.38), channel_id=1, source_target_pairs={{56,0},{60,4},{0,8},{4,12},{8,16},{12,20},{16,24},{20,28},{24,32},... | collective-permute-start | bytes 393224 | tf_op jit(solution)/shard_map/while/body/eval_jaxpr/ppermute | solution.py:22
  151.9 18.0 %collective-permute-start.2 = (f32[256,256]{1,0:T(8,128)}, f32[256,256]{1,0:T(8,128)S(1)}, u32[]{:S(2)}, u32[]{:S(2)}) collective-permute-start(f32[256,256]{1,0:T(8,128)} %get-tuple-element.720), channel_id=1, source_target_pairs={{56,0},{60,4},{0,8},{4,12},{8,16},{12,20},{16,24},{20,28},{24,32},... | collective-permute-start | bytes 786440 | tf_op jit(solution)/shard_map/while/body/eval_jaxpr/ppermute | solution.py:22
  152.0 17.9 %collective-permute-start.3 = (f32[256,256]{1,0:T(8,128)}, f32[256,256]{1,0:T(8,128)S(1)}, u32[]{:S(2)}, u32[]{:S(2)}) collective-permute-start(f32[256,256]{1,0:T(8,128)} %get-tuple-element.719), channel_id=1, source_target_pairs={{8,0},{12,4},{16,8},{20,12},{24,16},{28,20},{32,24},{36,28},{40,32... | collective-permute-start | bytes 786440 | tf_op jit(solution)/shard_map/while/body/eval_jaxpr/ppermute | solution.py:22
  160.7 0.7 copy-start.13
  162.1 0.7 copy-start.9
  162.1 0.7 copy-start.7
  171.8 3.6 %copy-start.16 = (s32[1,512]{1,0:T(1,128)S(1)}, s32[1,512]{1,0:T(1,128)}, u32[]{:S(2)}) copy-start(s32[1,512]{1,0:T(1,128)} %get-tuple-element.587) | copy-start | bytes 6148
  171.8 3.6 %copy-start.12 = (s32[2,512]{1,0:T(2,128)S(1)}, s32[2,512]{1,0:T(2,128)}, u32[]{:S(2)}) copy-start(s32[2,512]{1,0:T(2,128)} %get-tuple-element.585) | copy-start | bytes 12292
  171.8 12.2 %collective-permute-start.9 = (f32[256,256]{1,0:T(8,128)}, f32[256,256]{1,0:T(8,128)S(1)}, u32[]{:S(2)}, u32[]{:S(2)}) collective-permute-start(f32[256,256]{1,0:T(8,128)} %get-tuple-element.465), channel_id=1, source_target_pairs={{56,0},{60,4},{0,8},{4,12},{8,16},{12,20},{16,24},{20,28},{24,32},... | collective-permute-start | bytes 786440 | tf_op jit(solution)/shard_map/ppermute | solution.py:22
  172.1 11.9 %collective-permute-start.7 = (f32[256,256]{1,0:T(8,128)}, f32[256,256]{1,0:T(8,128)S(1)}, u32[]{:S(2)}, u32[]{:S(2)}) collective-permute-start(f32[256,256]{1,0:T(8,128)} %get-tuple-element.463), channel_id=1, source_target_pairs={{8,0},{12,4},{16,8},{20,12},{24,16},{28,20},{32,24},{36,28},{40,32... | collective-permute-start | bytes 786440 | tf_op jit(solution)/shard_map/ppermute | solution.py:22
  175.4 0.7 copy-start.15
  185.1 6.5 %collective-permute-start.8 = (f32[256,256]{1,0:T(8,128)S(1)}, f32[256,256]{1,0:T(8,128)S(1)}, u32[]{:S(2)}, u32[]{:S(2)}) collective-permute-start(f32[256,256]{1,0:T(8,128)S(1)} %get-tuple-element.574), channel_id=1, source_target_pairs={{8,0},{12,4},{16,8},{20,12},{24,16},{28,20},{32,24},{36,28},{40,32... | collective-permute-start | bytes 786440 | tf_op jit(solution)/shard_map/ppermute | solution.py:22
  185.8 7.6 %collective-permute-start.10 = (f32[256,256]{1,0:T(8,128)S(1)}, f32[256,256]{1,0:T(8,128)S(1)}, u32[]{:S(2)}, u32[]{:S(2)}) collective-permute-start(f32[256,256]{1,0:T(8,128)S(1)} %get-tuple-element.575), channel_id=1, source_target_pairs={{56,0},{60,4},{0,8},{4,12},{8,16},{12,20},{16,24},{20,28},{24,32},... | collective-permute-start | bytes 786440 | tf_op jit(solution)/shard_map/ppermute | solution.py:22
  193.4 8.0 %collective-permute-start.11 = (f32[256,256]{1,0:T(8,128)S(1)}, f32[256,256]{1,0:T(8,128)S(1)}, u32[]{:S(2)}, u32[]{:S(2)}) collective-permute-start(f32[256,256]{1,0:T(8,128)S(1)} %broadcast_select_fusion), channel_id=1, source_target_pairs={{0,4},{4,0},{8,12},{12,8},{16,20},{20,16},{24,28},{28,24},{32,36},... | collective-permute-start | bytes 786440 | tf_op jit(solution)/shard_map/ppermute | solution.py:27
  (21 other events, 12.4 us)

commit v6 on v5

v6 whole, which is shorter than its diff:
```python
import math

import jax
import jax.numpy as jnp
from jax import lax
from jax.experimental import pallas as pl
from jax.experimental.pallas import tpu as pltpu
from jax.sharding import PartitionSpec as P

BLK = 128
HEAD_SIZE = 128
Y_HI = 2


def along_z(value, ctx_count, shift):
    z_count = ctx_count // Y_HI
    pairs = [
        (Y_HI * ((z + shift) % z_count) + h, Y_HI * z + h)
        for z in range(z_count)
        for h in range(Y_HI)
    ]
    return lax.ppermute(value, "ctx", pairs)


def from_partner(value, ctx_count):
    pairs = [(c, c ^ 1) for c in range(ctx_count)]
    return lax.ppermute(value, "ctx", pairs)


def turn_kernel(turn_ref, code_ref, q_ref, do_ref, ahead_kv_ref, behind_kv_ref, lse_ref, delta_ref, dq_in_ref,
                dq_ref, ahead_ref, behind_ref):
    heads, tok_rows, _ = q_ref.shape
    key_count = 2 * ahead_kv_ref.shape[0]
    row_blocks = tok_rows // BLK
    key_blocks = key_count // BLK
    half_blocks = key_blocks // 2
    scale = 1.0 / math.sqrt(HEAD_SIZE)
    turn = turn_ref[0]
    codes = [[code_ref[turn, r * key_blocks + c] for c in range(key_blocks)] for r in range(row_blocks)]
    ahead_ref[...] = jnp.zeros(ahead_ref.shape, jnp.float32)
    behind_ref[...] = jnp.zeros(behind_ref.shape, jnp.float32)
    row = lax.broadcasted_iota(jnp.int32, (tok_rows, BLK), 0)
    col = lax.broadcasted_iota(jnp.int32, (tok_rows, BLK), 1)
    row_block = row // BLK
    below = col <= row - row_block * BLK

    def head_body(h, carry):
        q = q_ref[h]
        do = do_ref[h]
        lse = lse_ref[h]
        delta = delta_ref[h]
        dq_ref[h] = dq_in_ref[h]
        for c in range(key_blocks):
            any_live = codes[0][c] > 0
            for r in range(1, row_blocks):
                any_live = any_live | (codes[r][c] > 0)

            @pl.when(any_live)
            def _():
                code = jnp.full((tok_rows, BLK), codes[0][c], jnp.int32)
                for r in range(1, row_blocks):
                    code = jnp.where(row_block == r, codes[r][c], code)
                live = (code == 1) | ((code == 2) & below)
                kv_ref = ahead_kv_ref if c < half_blocks else behind_kv_ref
                rows = slice((c % half_blocks) * BLK, (c % half_blocks + 1) * BLK)
                keys = kv_ref[rows, :HEAD_SIZE]
                values = kv_ref[rows, HEAD_SIZE:]
                s = lax.dot_general(q, keys, (((1,), (1,)), ((), ())), preferred_element_type=jnp.float32)
                p = jnp.where(live, jnp.exp(s * scale - lse), 0.0)
                dp = lax.dot_general(do, values, (((1,), (1,)), ((), ())), preferred_element_type=jnp.float32)
                ds = (p * (dp - delta)).astype(jnp.bfloat16).astype(keys.dtype)
                dq_ref[h] = dq_ref[h] + jnp.dot(ds, keys, preferred_element_type=jnp.float32)
                dk = lax.dot_general(ds, q, (((0,), (0,)), ((), ())), preferred_element_type=jnp.float32)
                dv = lax.dot_general(
                    p.astype(jnp.bfloat16).astype(do.dtype), do, (((0,), (0,)), ((), ())),
                    preferred_element_type=jnp.float32,
                )
                out = ahead_ref if c < half_blocks else behind_ref
                out[rows, :HEAD_SIZE] = out[rows, :HEAD_SIZE] + dk
                out[rows, HEAD_SIZE:] = out[rows, HEAD_SIZE:] + dv

        return carry

    lax.fori_loop(0, heads, head_body, 0)


def turn_call(turn, codes, q, do, ahead_kv, behind_kv, lse, delta, dq_acc):
    heads, tok_rows, _ = q.shape
    half = ahead_kv.shape[0]
    vmem = pl.BlockSpec(memory_space=pltpu.MemorySpace.VMEM)
    smem = pl.BlockSpec(memory_space=pltpu.MemorySpace.SMEM)
    return pl.pallas_call(
        turn_kernel,
        out_shape=(
            jax.ShapeDtypeStruct(dq_acc.shape, jnp.float32),
            jax.ShapeDtypeStruct((half, 2 * HEAD_SIZE), jnp.float32),
            jax.ShapeDtypeStruct((half, 2 * HEAD_SIZE), jnp.float32),
        ),
        in_specs=[smem, smem] + [vmem] * 7,
        out_specs=(vmem, vmem, vmem),
        input_output_aliases={8: 0},
    )(turn, codes, q, do, ahead_kv, behind_kv, lse, delta, dq_acc)


def local(query_rows, key_matrix, value_matrix, attn_out, out_grad, log_sums, block_mask):
    tok_rows = query_rows.shape[0]
    col_width = query_rows.shape[1]
    heads_local = col_width // HEAD_SIZE
    ctx_pos = lax.axis_index("ctx")
    ctx_count = lax.axis_size("ctx")
    tp_count = lax.axis_size("tp")
    grad_rows = out_grad.shape[0]
    pieces = out_grad.reshape(grad_rows, tp_count, col_width)
    own_grad = lax.all_to_all(pieces, "tp", split_axis=1, concat_axis=0, tiled=True)
    out_grads = own_grad.reshape(tok_rows, heads_local, HEAD_SIZE)
    outputs = attn_out.reshape(tok_rows, heads_local, HEAD_SIZE)
    row_delta = jnp.sum(out_grads.astype(jnp.float32) * outputs.astype(jnp.float32), axis=2)
    delta_heads = row_delta.T[:, :, None]
    lse_heads = log_sums[:, :, None]
    query_heads = query_rows.reshape(tok_rows, heads_local, HEAD_SIZE).transpose(1, 0, 2)
    grad_heads = out_grads.transpose(1, 0, 2)
    query_start = ctx_pos * tok_rows
    z_pos = ctx_pos // Y_HI
    z_count = ctx_count // Y_HI
    y_hi = ctx_pos % Y_HI
    super_rows = Y_HI * tok_rows
    turns = jnp.arange(z_count, dtype=jnp.int32)
    ahead_owner = (z_pos + turns) % z_count
    behind_owner = (z_pos - turns) % z_count
    half_blocks = tok_rows // BLK
    key_block = jnp.concatenate(
        [
            ahead_owner[:, None] * (2 * half_blocks) + jnp.arange(half_blocks)[None, :],
            behind_owner[:, None] * (2 * half_blocks) + half_blocks + jnp.arange(half_blocks)[None, :],
        ],
        axis=1,
    )
    query_block = query_start // BLK + jnp.arange(half_blocks, dtype=jnp.int32)
    qb = query_block[None, :, None]
    kb = key_block[:, None, :]
    allowed = block_mask[qb, kb]
    codes = jnp.where(kb == qb, 2, jnp.where((kb < qb) & (allowed == 1), 1, 0))
    codes = codes.reshape(z_count, -1).astype(jnp.int32)

    def terms(ahead_kv, behind_kv, turn, query_acc):
        turn_index = jnp.reshape(turn, (1,)).astype(jnp.int32)
        return turn_call(
            turn_index,
            codes,
            query_heads,
            grad_heads,
            ahead_kv,
            behind_kv,
            lse_heads,
            delta_heads,
            query_acc,
        )

    key_values = jnp.concatenate([key_matrix, value_matrix], axis=1)
    partner_kv = from_partner(key_values, ctx_count)
    ahead_kv = jnp.where(y_hi == 0, key_values, partner_kv)
    behind_kv = jnp.where(y_hi == 0, partner_kv, key_values)
    next_ahead = along_z(ahead_kv, ctx_count, 1)
    next_behind = along_z(behind_kv, ctx_count, -1)
    zero_query = jnp.zeros((heads_local, tok_rows, HEAD_SIZE), jnp.float32)
    query_acc, ahead_pending, behind_pending = terms(ahead_kv, behind_kv, 0, zero_query)

    def visit_turn(turn, carried):
        ahead_kv, behind_kv, query_acc, ahead_pending, behind_pending = carried
        ahead_received = along_z(ahead_pending, ctx_count, 1)
        behind_received = along_z(behind_pending, ctx_count, -1)
        next_ahead = along_z(ahead_kv, ctx_count, 1)
        next_behind = along_z(behind_kv, ctx_count, -1)
        query_acc, ahead_term, behind_term = terms(ahead_kv, behind_kv, turn, query_acc)
        return (
            next_ahead,
            next_behind,
            query_acc,
            ahead_received + ahead_term,
            behind_received + behind_term,
        )

    ahead_kv, behind_kv, query_acc, ahead_pending, behind_pending = lax.fori_loop(
        1,
        z_count - 1,
        visit_turn,
        (next_ahead, next_behind, query_acc, ahead_pending, behind_pending),
    )
    ahead_received = along_z(ahead_pending, ctx_count, 1)
    behind_received = along_z(behind_pending, ctx_count, -1)
    query_acc, ahead_term, behind_term = terms(ahead_kv, behind_kv, z_count - 1, query_acc)
    ahead_total = along_z(ahead_received + ahead_term, ctx_count, 1)
    behind_total = along_z(behind_received + behind_term, ctx_count, -1)
    own_total = jnp.where(y_hi == 0, ahead_total, behind_total)
    other_total = jnp.where(y_hi == 0, behind_total, ahead_total)
    summed = own_total + from_partner(other_total, ctx_count)
    logit_scale = 1.0 / math.sqrt(HEAD_SIZE)
    query_grad = (query_acc * logit_scale).transpose(1, 0, 2).reshape(tok_rows, col_width)
    query_grad = query_grad.astype(jnp.bfloat16)
    key_gradient = (summed[:, :HEAD_SIZE] * logit_scale).astype(jnp.bfloat16)
    value_gradient = summed[:, HEAD_SIZE:].astype(jnp.bfloat16)
    return (query_grad, key_gradient, value_gradient)


def solution(mesh):
    placed = (
        P(("dp", "ctx"), "tp"),
        P(("dp", "ctx"), "tp"),
        P(("dp", "ctx"), "tp"),
        P(("dp", "ctx"), "tp"),
        P(("dp", "ctx", "tp"), None),
        P("tp", ("dp", "ctx")),
        P("dp", None),
    )
    return jax.shard_map(
        local,
        mesh=mesh,
        in_specs=placed,
        out_specs=(P(("dp", "ctx"), "tp"), P(("dp", "ctx"), "tp"), P(("dp", "ctx"), "tp")),
        check_vma=False,
    )
```

time: 205 us -> 236 us (1.15)
  starting transfers between devices: 51 us -> 147 us
  local copies, waits for them, and re-layouts: 48.8 us -> 20.6 us
  Pallas kernels: 45.9 us -> 28 us
  other arithmetic: 42.9 us -> 25.1 us
    ppermute x30, starting transfers between devices: 43.9 us -> 127 us  [along_z(): return lax.ppermute(value, 'ctx', pairs)]
    pallas_call x8, Pallas kernels: 45.9 us -> 28 us  [turn_call(): pl.pallas_call(turn_kernel, out_shape=(jax.ShapeDtypeStruct(dq_acc.shape,...]
    while x96 -> x36, local copies, waits for them, and re-layouts: 20.6 us -> 2.97 us
    gather x16 -> x1, local copies, waits for them, and re-layouts: 17.8 us -> 0.81 us  [local(): allowed = block_mask[qb, kb]]
    ppermute x2, starting transfers between devices: 3.69 us -> 16.3 us  [from_partner(): return lax.ppermute(value, 'ctx', pairs)]
    concatenate x16 -> x3, other arithmetic: 11.7 us -> 0.16 us  [local(): allowed = block_mask[qb, kb]]
    add x17 -> x9, other arithmetic: 3.61 us -> 10.4 us  [the longest x6 10.2 us: visit_turn(): ahead_received + ahead_term]
    convert_element_type x9 -> x1, other arithmetic: 6.26 us -> 0.11 us  [local(): query_grad = query_grad.astype(jnp.bfloat16)]
  transfers between devices with their start and end apart: 33 -> 33, of which waited for: 3 -> 5; matrix products, arithmetic and copies ran while one was open for 32% -> 17% of each run, Pallas kernels for 23% -> 12%
where the time goes in v6:
time: 236 us; the launch traced here: 235 us
  starting transfers between devices  147 us (62%)
  Pallas kernels  28 us (12%)
  other arithmetic  25.1 us (11%)
  local copies, waits for them, and re-layouts  20.6 us (9%)
  waiting for transfers between devices  13 us (6%)
    ppermute x30, starting transfers between devices, along_z(): return lax.ppermute(value, 'ctx', pairs)  127 us
    pallas_call x8, Pallas kernels, turn_call(): pl.pallas_call(turn_kernel, out_shape=(jax.ShapeDtypeStruct(dq_acc.shape,...  28 us
    ppermute x2, starting transfers between devices, from_partner(): return lax.ppermute(value, 'ctx', pairs)  16.3 us
    add x6, other arithmetic, visit_turn(): behind_received + behind_term  11 us
    add x6, other arithmetic, visit_turn(): ahead_received + ahead_term  10.2 us
    ppermute x30, waiting for transfers between devices, along_z(): return lax.ppermute(value, 'ctx', pairs)  9.95 us
    another operation x12, local copies, waits for them, and re-layouts  5.48 us
  transfers between devices with their start and end apart: 33, of which 5 were waited for; matrix products, arithmetic and copies ran while one was open for 17% of the time, Pallas kernels for 12%

profile of v6, /device:TPU:4, one launch (start us, length us, event | category | flops | bytes accessed | tf_op | source)
XLA Modules:
  0.0 234.8 jit_solution(13757368101658957881)
XLA Ops:
  0.7 0.9 constant_dynamic-update-slice_fusion.1
  1.6 3.3 %collective-permute-start.4 = (bf16[256,256]{1,0:T(8,128)(2,1)S(1)}, bf16[256,256]{1,0:T(8,128)(2,1)S(1)}, u32[]{:S(2)}, u32[]{:S(2)}) collective-permute-start(bf16[256,256]{1,0:T(8,128)(2,1)S(1)} %constant_dynamic-update-slice_fusion), channel_id=1, source_target_pairs={{0,4},{4,0},{8,12},{12,8},{16,20},{20,16},{24,28},{28,24},{32,36},... | collective-permute-start | bytes 393224 | tf_op jit(solution)/shard_map/ppermute | solution.py:27
  4.9 1.9 copy.57
  6.8 3.5 %all-to-all-start = ((bf16[64,4,1024]{2,0,1:T(8,128)(2,1)}), bf16[64,4,1024]{2,0,1:T(8,128)(2,1)S(1)}, u32[]{:S(2)}, u32[]{:S(2)}) async-start(bf16[64,4,1024]{2,0,1:T(8,128)(2,1)} %bitcast.28), calls=%async_computation | async-start | bytes 1048576 | tf_op jit(solution)/shard_map/all_to_all | solution.py:114
  11.0 0.8 gather_fusion
  12.3 1.0 copy.37
  14.6 0.6 select_select_fusion.code_ref
  15.3 2.0 collective-permute-start.6
  17.3 4.0 %collective-permute-start.5 = (bf16[256,256]{1,0:T(8,128)(2,1)S(1)}, bf16[256,256]{1,0:T(8,128)(2,1)}, u32[]{:S(2)}, u32[]{:S(2)}) collective-permute-start(bf16[256,256]{1,0:T(8,128)(2,1)S(1)} %get-tuple-element.247.ahead_kv_ref), channel_id=1, source_target_pairs={{8,0},{12,4},{16,8},{20,12},{24,16},{28,20},{32,24},{36,28},{40,32... | collective-permute-start | bytes 393224 | tf_op jit(solution)/shard_map/ppermute | solution.py:22
  21.4 0.9 copy.58
  22.3 1.0 multiply_reduce_fusion
  23.3 2.5 %copy.44.delta_ref = f32[8,256,1]{2,1,0:T(8,128)S(1)} copy(f32[8,256,1]{0,1,2:T(8,128)} %bitcast.43) | data formatting | bytes 16384 | tf_op jit(solution)/shard_map/broadcast_in_dim | solution.py:118
  25.9 9.3 %shard_map.94 = (f32[8,256,128]{2,1,0:T(8,128)S(1)}, f32[256,256]{1,0:T(8,128)}, f32[256,256]{1,0:T(8,128)}) custom-call(s32[1]{0:T(128)} %constant.89.clone.1.turn_ref, s32[8,8]{1,0:T(8,128)} %select_select_fusion.code_ref, bf16[8,256,128]{2,1,0:T(8,128)(2,1)} %bitcast.32, bf16[8,256,128]{2,1,0:T(8,128)(2,1)} %bitcast.34, ...), custom_call_target="tpu_custom_call", output_to_operand_aliasing={{0}: (8, {})} | custom-call | tf_op jit(solution)/shard_map/pallas_call | solution.py:92
  35.2 136.8 %while.21 = (s32[]{:T(128)}, bf16[256,256]{1,0:T(8,128)(2,1)}, bf16[256,256]{1,0:T(8,128)(2,1)S(1)}, f32[8,256,128]{2,1,0:T(8,128)S(1)}, f32[256,256]{1,0:T(8,12...) while((s32[]{:T(128)}, bf16[256,256]{1,0:T(8,128)(2,1)}, ...), condition=%wide.region_2.3_spmd, body=%wide.region_1.2_spmd.sunk | while | flops 131074 | bytes 7340393 | solution.py:183
  35.3 3.7 %collective-permute-start.2 = (f32[256,256]{1,0:T(8,128)}, f32[256,256]{1,0:T(8,128)}, u32[]{:S(2)}, u32[]{:S(2)}) collective-permute-start(f32[256,256]{1,0:T(8,128)} %get-tuple-element.341), channel_id=1, source_target_pairs={{8,0},{12,4},{16,8},{20,12},{24,16},{28,20},{32,24},{36,28},{40,32... | collective-permute-start | bytes 786440 | tf_op jit(solution)/shard_map/while/body/eval_jaxpr/ppermute | solution.py:22
  39.0 0.9 copy.69.ahead_kv_ref
  39.9 1.9 collective-permute-start
  42.5 2.7 %eval_jaxpr.5 = (f32[8,256,128]{2,1,0:T(8,128)S(1)}, f32[256,256]{1,0:T(8,128)}, f32[256,256]{1,0:T(8,128)}) custom-call(s32[1]{0:T(128)} %bitcast.31.turn_ref, s32[8,8]{1,0:T(8,128)} %get-tuple-element.355.code_ref, bf16[8,256,128]{2,1,0:T(8,128)(2,1)} %get-tuple-element.356.q_ref, ...), custom_call_target="tpu_custom_call", output_to_operand_aliasing={{0}: (8, {})} | custom-call | tf_op jit(solution)/shard_map/while/body/eval_jaxpr/pallas_call | solution.py:92
  45.2 0.7 collective-permute-done.3
  46.0 1.8 add.201
  47.8 1.7 add.200
  49.5 6.0 %collective-permute-start.3 = (f32[256,256]{1,0:T(8,128)}, f32[256,256]{1,0:T(8,128)}, u32[]{:S(2)}, u32[]{:S(2)}) collective-permute-start(f32[256,256]{1,0:T(8,128)} %get-tuple-element.342), channel_id=1, source_target_pairs={{56,0},{60,4},{0,8},{4,12},{8,16},{12,20},{16,24},{20,28},{24,32},... | collective-permute-start | bytes 786440 | tf_op jit(solution)/shard_map/while/body/eval_jaxpr/ppermute | solution.py:22
  55.5 9.3 %collective-permute-start.2 = (f32[256,256]{1,0:T(8,128)}, f32[256,256]{1,0:T(8,128)}, u32[]{:S(2)}, u32[]{:S(2)}) collective-permute-start(f32[256,256]{1,0:T(8,128)} %get-tuple-element.341), channel_id=1, source_target_pairs={{8,0},{12,4},{16,8},{20,12},{24,16},{28,20},{32,24},{36,28},{40,32... | collective-permute-start | bytes 786440 | tf_op jit(solution)/shard_map/while/body/eval_jaxpr/ppermute | solution.py:22
  64.9 0.9 copy.69.ahead_kv_ref
  65.8 1.9 collective-permute-start
  68.4 2.7 %eval_jaxpr.5 = (f32[8,256,128]{2,1,0:T(8,128)S(1)}, f32[256,256]{1,0:T(8,128)}, f32[256,256]{1,0:T(8,128)}) custom-call(s32[1]{0:T(128)} %bitcast.31.turn_ref, s32[8,8]{1,0:T(8,128)} %get-tuple-element.355.code_ref, bf16[8,256,128]{2,1,0:T(8,128)(2,1)} %get-tuple-element.356.q_ref, ...), custom_call_target="tpu_custom_call", output_to_operand_aliasing={{0}: (8, {})} | custom-call | tf_op jit(solution)/shard_map/while/body/eval_jaxpr/pallas_call | solution.py:92
  71.1 1.8 add.201
  72.9 1.7 add.200
  74.7 16.0 %collective-permute-start.2 = (f32[256,256]{1,0:T(8,128)}, f32[256,256]{1,0:T(8,128)}, u32[]{:S(2)}, u32[]{:S(2)}) collective-permute-start(f32[256,256]{1,0:T(8,128)} %get-tuple-element.341), channel_id=1, source_target_pairs={{8,0},{12,4},{16,8},{20,12},{24,16},{28,20},{32,24},{36,28},{40,32... | collective-permute-start | bytes 786440 | tf_op jit(solution)/shard_map/while/body/eval_jaxpr/ppermute | solution.py:22
  90.7 0.9 copy.69.ahead_kv_ref
  91.6 1.9 collective-permute-start
  94.2 2.7 %eval_jaxpr.5 = (f32[8,256,128]{2,1,0:T(8,128)S(1)}, f32[256,256]{1,0:T(8,128)}, f32[256,256]{1,0:T(8,128)}) custom-call(s32[1]{0:T(128)} %bitcast.31.turn_ref, s32[8,8]{1,0:T(8,128)} %get-tuple-element.355.code_ref, bf16[8,256,128]{2,1,0:T(8,128)(2,1)} %get-tuple-element.356.q_ref, ...), custom_call_target="tpu_custom_call", output_to_operand_aliasing={{0}: (8, {})} | custom-call | tf_op jit(solution)/shard_map/while/body/eval_jaxpr/pallas_call | solution.py:92
  96.9 1.8 add.201
  98.7 1.7 add.200
  100.5 16.0 %collective-permute-start.2 = (f32[256,256]{1,0:T(8,128)}, f32[256,256]{1,0:T(8,128)}, u32[]{:S(2)}, u32[]{:S(2)}) collective-permute-start(f32[256,256]{1,0:T(8,128)} %get-tuple-element.341), channel_id=1, source_target_pairs={{8,0},{12,4},{16,8},{20,12},{24,16},{28,20},{32,24},{36,28},{40,32... | collective-permute-start | bytes 786440 | tf_op jit(solution)/shard_map/while/body/eval_jaxpr/ppermute | solution.py:22
  116.5 0.9 copy.69.ahead_kv_ref
  117.4 1.9 collective-permute-start
  120.0 2.7 %eval_jaxpr.5 = (f32[8,256,128]{2,1,0:T(8,128)S(1)}, f32[256,256]{1,0:T(8,128)}, f32[256,256]{1,0:T(8,128)}) custom-call(s32[1]{0:T(128)} %bitcast.31.turn_ref, s32[8,8]{1,0:T(8,128)} %get-tuple-element.355.code_ref, bf16[8,256,128]{2,1,0:T(8,128)(2,1)} %get-tuple-element.356.q_ref, ...), custom_call_target="tpu_custom_call", output_to_operand_aliasing={{0}: (8, {})} | custom-call | tf_op jit(solution)/shard_map/while/body/eval_jaxpr/pallas_call | solution.py:92
  122.7 1.8 add.201
  124.5 1.7 add.200
  126.3 16.0 %collective-permute-start.2 = (f32[256,256]{1,0:T(8,128)}, f32[256,256]{1,0:T(8,128)}, u32[]{:S(2)}, u32[]{:S(2)}) collective-permute-start(f32[256,256]{1,0:T(8,128)} %get-tuple-element.341), channel_id=1, source_target_pairs={{8,0},{12,4},{16,8},{20,12},{24,16},{28,20},{32,24},{36,28},{40,32... | collective-permute-start | bytes 786440 | tf_op jit(solution)/shard_map/while/body/eval_jaxpr/ppermute | solution.py:22
  142.3 0.9 copy.69.ahead_kv_ref
  143.2 1.9 collective-permute-start
  145.9 2.7 %eval_jaxpr.5 = (f32[8,256,128]{2,1,0:T(8,128)S(1)}, f32[256,256]{1,0:T(8,128)}, f32[256,256]{1,0:T(8,128)}) custom-call(s32[1]{0:T(128)} %bitcast.31.turn_ref, s32[8,8]{1,0:T(8,128)} %get-tuple-element.355.code_ref, bf16[8,256,128]{2,1,0:T(8,128)(2,1)} %get-tuple-element.356.q_ref, ...), custom_call_target="tpu_custom_call", output_to_operand_aliasing={{0}: (8, {})} | custom-call | tf_op jit(solution)/shard_map/while/body/eval_jaxpr/pallas_call | solution.py:92
  148.5 1.8 add.201
  150.4 1.7 add.200
  152.2 9.3 %collective-permute-start.2 = (f32[256,256]{1,0:T(8,128)}, f32[256,256]{1,0:T(8,128)}, u32[]{:S(2)}, u32[]{:S(2)}) collective-permute-start(f32[256,256]{1,0:T(8,128)} %get-tuple-element.341), channel_id=1, source_target_pairs={{8,0},{12,4},{16,8},{20,12},{24,16},{28,20},{32,24},{36,28},{40,32... | collective-permute-start | bytes 786440 | tf_op jit(solution)/shard_map/while/body/eval_jaxpr/ppermute | solution.py:22
  161.5 0.9 copy.69.ahead_kv_ref
  162.4 2.7 %collective-permute-start = (bf16[256,256]{1,0:T(8,128)(2,1)S(1)}, bf16[256,256]{1,0:T(8,128)(2,1)}, u32[]{:S(2)}, u32[]{:S(2)}) collective-permute-start(bf16[256,256]{1,0:T(8,128)(2,1)S(1)} %copy.69.ahead_kv_ref), channel_id=1, source_target_pairs={{8,0},{12,4},{16,8},{20,12},{24,16},{28,20},{32,24},{36,28},{40,32... | collective-permute-start | bytes 393224 | tf_op jit(solution)/shard_map/while/body/eval_jaxpr/ppermute | solution.py:22
  165.8 2.7 %eval_jaxpr.5 = (f32[8,256,128]{2,1,0:T(8,128)S(1)}, f32[256,256]{1,0:T(8,128)}, f32[256,256]{1,0:T(8,128)}) custom-call(s32[1]{0:T(128)} %bitcast.31.turn_ref, s32[8,8]{1,0:T(8,128)} %get-tuple-element.355.code_ref, bf16[8,256,128]{2,1,0:T(8,128)(2,1)} %get-tuple-element.356.q_ref, ...), custom_call_target="tpu_custom_call", output_to_operand_aliasing={{0}: (8, {})} | custom-call | tf_op jit(solution)/shard_map/while/body/eval_jaxpr/pallas_call | solution.py:92
  168.5 1.8 add.201
  170.3 1.7 add.200
  172.0 16.0 %collective-permute-start.7 = (f32[256,256]{1,0:T(8,128)}, f32[256,256]{1,0:T(8,128)}, u32[]{:S(2)}, u32[]{:S(2)}) collective-permute-start(f32[256,256]{1,0:T(8,128)} %get-tuple-element.190), channel_id=1, source_target_pairs={{8,0},{12,4},{16,8},{20,12},{24,16},{28,20},{32,24},{36,28},{40,32... | collective-permute-start | bytes 786440 | tf_op jit(solution)/shard_map/ppermute | solution.py:22
  188.0 2.6 %shard_map.95 = (f32[8,256,128]{2,1,0:T(8,128)S(1)}, f32[256,256]{1,0:T(8,128)}, f32[256,256]{1,0:T(8,128)}) custom-call(s32[1]{0:T(128)} %constant.76.clone.1.turn_ref, s32[8,8]{1,0:T(8,128)} %get-tuple-element.380, bf16[8,256,128]{2,1,0:T(8,128)(2,1)} %get-tuple-element.363, ...), custom_call_target="tpu_custom_call", output_to_operand_aliasing={{0}: (8, {})} | custom-call | tf_op jit(solution)/shard_map/pallas_call | solution.py:92
  190.6 1.6 collective-permute-done.7
  192.2 1.1 add.154
  193.3 15.1 %collective-permute-start.8 = (f32[256,256]{1,0:T(8,128)S(1)}, f32[256,256]{1,0:T(8,128)S(1)}, u32[]{:S(2)}, u32[]{:S(2)}) collective-permute-start(f32[256,256]{1,0:T(8,128)S(1)} %add.154), channel_id=1, source_target_pairs={{8,0},{12,4},{16,8},{20,12},{24,16},{28,20},{32,24},{36,28},{40,32... | collective-permute-start | bytes 786440 | tf_op jit(solution)/shard_map/ppermute | solution.py:22
  208.5 3.8 %collective-permute-done.8 = f32[256,256]{1,0:T(8,128)S(1)} collective-permute-done((f32[256,256]{1,0:T(8,128)S(1)}, f32[256,256]{1,0:T(8,128)S(1)}, u32[]{:S(2)}, u32[]{:S(2)}) %collective-permute-start.8) | collective-permute-done | bytes 262176 | tf_op jit(solution)/shard_map/ppermute | solution.py:22
  212.3 3.8 %collective-permute-done.10 = f32[256,256]{1,0:T(8,128)S(1)} collective-permute-done((f32[256,256]{1,0:T(8,128)S(1)}, f32[256,256]{1,0:T(8,128)S(1)}, u32[]{:S(2)}, u32[]{:S(2)}) %collective-permute-start.10) | collective-permute-done | bytes 262176 | tf_op jit(solution)/shard_map/ppermute | solution.py:22
  216.1 13.0 %collective-permute-start.11 = (f32[256,256]{1,0:T(8,128)S(1)}, f32[256,256]{1,0:T(8,128)S(1)}, u32[]{:S(2)}, u32[]{:S(2)}) collective-permute-start(f32[256,256]{1,0:T(8,128)S(1)} %broadcast_select_fusion), channel_id=1, source_target_pairs={{0,4},{4,0},{8,12},{12,8},{16,20},{20,16},{24,28},{28,24},{32,36},... | collective-permute-start | bytes 786440 | tf_op jit(solution)/shard_map/ppermute | solution.py:27
  229.5 1.0 copy.50
  230.5 3.0 %collective-permute-done.11 = f32[256,256]{1,0:T(8,128)S(1)} collective-permute-done((f32[256,256]{1,0:T(8,128)S(1)}, f32[256,256]{1,0:T(8,128)S(1)}, u32[]{:S(2)}, u32[]{:S(2)}) %collective-permute-start.11) | collective-permute-done | bytes 262176 | tf_op jit(solution)/shard_map/ppermute | solution.py:27
  233.5 0.6 slice.17
  234.2 0.6 fusion.1
  (126 shorter events, 7.6 us)
Async XLA Ops:
  0.6 10.4 %copy-start = (s32[32,32]{1,0:T(8,128)S(1)}, s32[32,32]{1,0:T(8,128)}, u32[]{:S(2)}) copy-start(s32[32,32]{1,0:T(8,128)} %param.15) | copy-start | bytes 12292
  0.6 0.9 copy-start.9
  1.6 13.6 %collective-permute-start.4 = (bf16[256,256]{1,0:T(8,128)(2,1)S(1)}, bf16[256,256]{1,0:T(8,128)(2,1)S(1)}, u32[]{:S(2)}, u32[]{:S(2)}) collective-permute-start(bf16[256,256]{1,0:T(8,128)(2,1)S(1)} %constant_dynamic-update-slice_fusion), channel_id=1, source_target_pairs={{0,4},{4,0},{8,12},{12,8},{16,20},{20,16},{24,28},{28,24},{32,36},... | collective-permute-start | bytes 393224 | tf_op jit(solution)/shard_map/ppermute | solution.py:27
  6.8 14.5 %all-to-all-start = ((bf16[64,4,1024]{2,0,1:T(8,128)(2,1)}), bf16[64,4,1024]{2,0,1:T(8,128)(2,1)S(1)}, u32[]{:S(2)}, u32[]{:S(2)}) async-start(bf16[64,4,1024]{2,0,1:T(8,128)(2,1)} %bitcast.28), calls=%async_computation | async-start | bytes 1048576 | tf_op jit(solution)/shard_map/all_to_all | solution.py:114
  11.0 1.0 copy-start.6
  12.3 1.0 copy-start.7
  13.5 0.7 copy-start.10
  15.2 6.2 %copy-start.4 = (bf16[256,256]{1,0:T(8,128)(2,1)}, bf16[256,256]{1,0:T(8,128)(2,1)S(1)}, u32[]{:S(2)}) copy-start(bf16[256,256]{1,0:T(8,128)(2,1)S(1)} %get-tuple-element.247.ahead_kv_ref) | copy-start | bytes 393220
  15.3 6.2 %copy-start.5 = (bf16[256,256]{1,0:T(8,128)(2,1)}, bf16[256,256]{1,0:T(8,128)(2,1)S(1)}, u32[]{:S(2)}) copy-start(bf16[256,256]{1,0:T(8,128)(2,1)S(1)} %get-tuple-element.246.behind_kv_ref) | copy-start | bytes 393220
  15.3 20.0 %collective-permute-start.6 = (bf16[256,256]{1,0:T(8,128)(2,1)S(1)}, bf16[256,256]{1,0:T(8,128)(2,1)S(1)}, u32[]{:S(2)}, u32[]{:S(2)}) collective-permute-start(bf16[256,256]{1,0:T(8,128)(2,1)S(1)} %get-tuple-element.246.behind_kv_ref), channel_id=1, source_target_pairs={{56,0},{60,4},{0,8},{4,12},{8,16},{12,20},{16,24},{20,28},{24,32},... | collective-permute-start | bytes 393224 | tf_op jit(solution)/shard_map/ppermute | solution.py:22
  17.3 18.0 %collective-permute-start.5 = (bf16[256,256]{1,0:T(8,128)(2,1)S(1)}, bf16[256,256]{1,0:T(8,128)(2,1)}, u32[]{:S(2)}, u32[]{:S(2)}) collective-permute-start(bf16[256,256]{1,0:T(8,128)(2,1)S(1)} %get-tuple-element.247.ahead_kv_ref), channel_id=1, source_target_pairs={{8,0},{12,4},{16,8},{20,12},{24,16},{28,20},{32,24},{36,28},{40,32... | collective-permute-start | bytes 393224 | tf_op jit(solution)/shard_map/ppermute | solution.py:22
  35.2 10.7 %collective-permute-start.3 = (f32[256,256]{1,0:T(8,128)}, f32[256,256]{1,0:T(8,128)}, u32[]{:S(2)}, u32[]{:S(2)}) collective-permute-start(f32[256,256]{1,0:T(8,128)} %get-tuple-element.342), channel_id=1, source_target_pairs={{56,0},{60,4},{0,8},{4,12},{8,16},{12,20},{16,24},{20,28},{24,32},... | collective-permute-start | bytes 786440 | tf_op jit(solution)/shard_map/while/body/eval_jaxpr/ppermute | solution.py:22
  35.3 12.5 %collective-permute-start.2 = (f32[256,256]{1,0:T(8,128)}, f32[256,256]{1,0:T(8,128)}, u32[]{:S(2)}, u32[]{:S(2)}) collective-permute-start(f32[256,256]{1,0:T(8,128)} %get-tuple-element.341), channel_id=1, source_target_pairs={{8,0},{12,4},{16,8},{20,12},{24,16},{28,20},{32,24},{36,28},{40,32... | collective-permute-start | bytes 786440 | tf_op jit(solution)/shard_map/while/body/eval_jaxpr/ppermute | solution.py:22
  39.9 2.0 copy-start.1
  39.9 9.6 %collective-permute-start = (bf16[256,256]{1,0:T(8,128)(2,1)S(1)}, bf16[256,256]{1,0:T(8,128)(2,1)}, u32[]{:S(2)}, u32[]{:S(2)}) collective-permute-start(bf16[256,256]{1,0:T(8,128)(2,1)S(1)} %copy.69.ahead_kv_ref), channel_id=1, source_target_pairs={{8,0},{12,4},{16,8},{20,12},{24,16},{28,20},{32,24},{36,28},{40,32... | collective-permute-start | bytes 393224 | tf_op jit(solution)/shard_map/while/body/eval_jaxpr/ppermute | solution.py:22
  41.9 0.6 copy-start.2
  41.9 7.6 %collective-permute-start.1 = (bf16[256,256]{1,0:T(8,128)(2,1)S(1)}, bf16[256,256]{1,0:T(8,128)(2,1)S(1)}, u32[]{:S(2)}, u32[]{:S(2)}) collective-permute-start(bf16[256,256]{1,0:T(8,128)(2,1)S(1)} %copy.70.behind_kv_ref), channel_id=1, source_target_pairs={{56,0},{60,4},{0,8},{4,12},{8,16},{12,20},{16,24},{20,28},{24,32},... | collective-permute-start | bytes 393224 | tf_op jit(solution)/shard_map/while/body/eval_jaxpr/ppermute | solution.py:22
  46.0 1.8 copy-start.3
  49.5 21.5 %collective-permute-start.3 = (f32[256,256]{1,0:T(8,128)}, f32[256,256]{1,0:T(8,128)}, u32[]{:S(2)}, u32[]{:S(2)}) collective-permute-start(f32[256,256]{1,0:T(8,128)} %get-tuple-element.342), channel_id=1, source_target_pairs={{56,0},{60,4},{0,8},{4,12},{8,16},{12,20},{16,24},{20,28},{24,32},... | collective-permute-start | bytes 786440 | tf_op jit(solution)/shard_map/while/body/eval_jaxpr/ppermute | solution.py:22
  55.5 17.4 %collective-permute-start.2 = (f32[256,256]{1,0:T(8,128)}, f32[256,256]{1,0:T(8,128)}, u32[]{:S(2)}, u32[]{:S(2)}) collective-permute-start(f32[256,256]{1,0:T(8,128)} %get-tuple-element.341), channel_id=1, source_target_pairs={{8,0},{12,4},{16,8},{20,12},{24,16},{28,20},{32,24},{36,28},{40,32... | collective-permute-start | bytes 786440 | tf_op jit(solution)/shard_map/while/body/eval_jaxpr/ppermute | solution.py:22
  65.8 2.0 copy-start.1
  65.8 8.8 %collective-permute-start = (bf16[256,256]{1,0:T(8,128)(2,1)S(1)}, bf16[256,256]{1,0:T(8,128)(2,1)}, u32[]{:S(2)}, u32[]{:S(2)}) collective-permute-start(bf16[256,256]{1,0:T(8,128)(2,1)S(1)} %copy.69.ahead_kv_ref), channel_id=1, source_target_pairs={{8,0},{12,4},{16,8},{20,12},{24,16},{28,20},{32,24},{36,28},{40,32... | collective-permute-start | bytes 393224 | tf_op jit(solution)/shard_map/while/body/eval_jaxpr/ppermute | solution.py:22
  67.7 0.6 copy-start.2
  67.7 6.9 %collective-permute-start.1 = (bf16[256,256]{1,0:T(8,128)(2,1)S(1)}, bf16[256,256]{1,0:T(8,128)(2,1)S(1)}, u32[]{:S(2)}, u32[]{:S(2)}) collective-permute-start(bf16[256,256]{1,0:T(8,128)(2,1)S(1)} %copy.70.behind_kv_ref), channel_id=1, source_target_pairs={{56,0},{60,4},{0,8},{4,12},{8,16},{12,20},{16,24},{20,28},{24,32},... | collective-permute-start | bytes 393224 | tf_op jit(solution)/shard_map/while/body/eval_jaxpr/ppermute | solution.py:22
  71.1 1.8 copy-start.3
  74.6 22.3 %collective-permute-start.3 = (f32[256,256]{1,0:T(8,128)}, f32[256,256]{1,0:T(8,128)}, u32[]{:S(2)}, u32[]{:S(2)}) collective-permute-start(f32[256,256]{1,0:T(8,128)} %get-tuple-element.342), channel_id=1, source_target_pairs={{56,0},{60,4},{0,8},{4,12},{8,16},{12,20},{16,24},{20,28},{24,32},... | collective-permute-start | bytes 786440 | tf_op jit(solution)/shard_map/while/body/eval_jaxpr/ppermute | solution.py:22
  74.7 24.0 %collective-permute-start.2 = (f32[256,256]{1,0:T(8,128)}, f32[256,256]{1,0:T(8,128)}, u32[]{:S(2)}, u32[]{:S(2)}) collective-permute-start(f32[256,256]{1,0:T(8,128)} %get-tuple-element.341), channel_id=1, source_target_pairs={{8,0},{12,4},{16,8},{20,12},{24,16},{28,20},{32,24},{36,28},{40,32... | collective-permute-start | bytes 786440 | tf_op jit(solution)/shard_map/while/body/eval_jaxpr/ppermute | solution.py:22
  91.6 2.0 copy-start.1
  91.6 8.8 %collective-permute-start = (bf16[256,256]{1,0:T(8,128)(2,1)S(1)}, bf16[256,256]{1,0:T(8,128)(2,1)}, u32[]{:S(2)}, u32[]{:S(2)}) collective-permute-start(bf16[256,256]{1,0:T(8,128)(2,1)S(1)} %copy.69.ahead_kv_ref), channel_id=1, source_target_pairs={{8,0},{12,4},{16,8},{20,12},{24,16},{28,20},{32,24},{36,28},{40,32... | collective-permute-start | bytes 393224 | tf_op jit(solution)/shard_map/while/body/eval_jaxpr/ppermute | solution.py:22
  93.6 0.6 copy-start.2
  93.6 6.9 %collective-permute-start.1 = (bf16[256,256]{1,0:T(8,128)(2,1)S(1)}, bf16[256,256]{1,0:T(8,128)(2,1)S(1)}, u32[]{:S(2)}, u32[]{:S(2)}) collective-permute-start(bf16[256,256]{1,0:T(8,128)(2,1)S(1)} %copy.70.behind_kv_ref), channel_id=1, source_target_pairs={{56,0},{60,4},{0,8},{4,12},{8,16},{12,20},{16,24},{20,28},{24,32},... | collective-permute-start | bytes 393224 | tf_op jit(solution)/shard_map/while/body/eval_jaxpr/ppermute | solution.py:22
  96.9 1.8 copy-start.3
  100.4 22.3 %collective-permute-start.3 = (f32[256,256]{1,0:T(8,128)}, f32[256,256]{1,0:T(8,128)}, u32[]{:S(2)}, u32[]{:S(2)}) collective-permute-start(f32[256,256]{1,0:T(8,128)} %get-tuple-element.342), channel_id=1, source_target_pairs={{56,0},{60,4},{0,8},{4,12},{8,16},{12,20},{16,24},{20,28},{24,32},... | collective-permute-start | bytes 786440 | tf_op jit(solution)/shard_map/while/body/eval_jaxpr/ppermute | solution.py:22
  100.5 24.0 %collective-permute-start.2 = (f32[256,256]{1,0:T(8,128)}, f32[256,256]{1,0:T(8,128)}, u32[]{:S(2)}, u32[]{:S(2)}) collective-permute-start(f32[256,256]{1,0:T(8,128)} %get-tuple-element.341), channel_id=1, source_target_pairs={{8,0},{12,4},{16,8},{20,12},{24,16},{28,20},{32,24},{36,28},{40,32... | collective-permute-start | bytes 786440 | tf_op jit(solution)/shard_map/while/body/eval_jaxpr/ppermute | solution.py:22
  117.4 2.0 copy-start.1
  117.4 8.8 %collective-permute-start = (bf16[256,256]{1,0:T(8,128)(2,1)S(1)}, bf16[256,256]{1,0:T(8,128)(2,1)}, u32[]{:S(2)}, u32[]{:S(2)}) collective-permute-start(bf16[256,256]{1,0:T(8,128)(2,1)S(1)} %copy.69.ahead_kv_ref), channel_id=1, source_target_pairs={{8,0},{12,4},{16,8},{20,12},{24,16},{28,20},{32,24},{36,28},{40,32... | collective-permute-start | bytes 393224 | tf_op jit(solution)/shard_map/while/body/eval_jaxpr/ppermute | solution.py:22
  119.4 0.6 copy-start.2
  119.4 6.9 %collective-permute-start.1 = (bf16[256,256]{1,0:T(8,128)(2,1)S(1)}, bf16[256,256]{1,0:T(8,128)(2,1)S(1)}, u32[]{:S(2)}, u32[]{:S(2)}) collective-permute-start(bf16[256,256]{1,0:T(8,128)(2,1)S(1)} %copy.70.behind_kv_ref), channel_id=1, source_target_pairs={{56,0},{60,4},{0,8},{4,12},{8,16},{12,20},{16,24},{20,28},{24,32},... | collective-permute-start | bytes 393224 | tf_op jit(solution)/shard_map/while/body/eval_jaxpr/ppermute | solution.py:22
  122.7 1.8 copy-start.3
  126.3 22.3 %collective-permute-start.3 = (f32[256,256]{1,0:T(8,128)}, f32[256,256]{1,0:T(8,128)}, u32[]{:S(2)}, u32[]{:S(2)}) collective-permute-start(f32[256,256]{1,0:T(8,128)} %get-tuple-element.342), channel_id=1, source_target_pairs={{56,0},{60,4},{0,8},{4,12},{8,16},{12,20},{16,24},{20,28},{24,32},... | collective-permute-start | bytes 786440 | tf_op jit(solution)/shard_map/while/body/eval_jaxpr/ppermute | solution.py:22
  126.3 24.0 %collective-permute-start.2 = (f32[256,256]{1,0:T(8,128)}, f32[256,256]{1,0:T(8,128)}, u32[]{:S(2)}, u32[]{:S(2)}) collective-permute-start(f32[256,256]{1,0:T(8,128)} %get-tuple-element.341), channel_id=1, source_target_pairs={{8,0},{12,4},{16,8},{20,12},{24,16},{28,20},{32,24},{36,28},{40,32... | collective-permute-start | bytes 786440 | tf_op jit(solution)/shard_map/while/body/eval_jaxpr/ppermute | solution.py:22
  143.2 2.0 copy-start.1
  143.2 8.8 %collective-permute-start = (bf16[256,256]{1,0:T(8,128)(2,1)S(1)}, bf16[256,256]{1,0:T(8,128)(2,1)}, u32[]{:S(2)}, u32[]{:S(2)}) collective-permute-start(bf16[256,256]{1,0:T(8,128)(2,1)S(1)} %copy.69.ahead_kv_ref), channel_id=1, source_target_pairs={{8,0},{12,4},{16,8},{20,12},{24,16},{28,20},{32,24},{36,28},{40,32... | collective-permute-start | bytes 393224 | tf_op jit(solution)/shard_map/while/body/eval_jaxpr/ppermute | solution.py:22
  145.2 0.6 copy-start.2
  145.2 6.9 %collective-permute-start.1 = (bf16[256,256]{1,0:T(8,128)(2,1)S(1)}, bf16[256,256]{1,0:T(8,128)(2,1)S(1)}, u32[]{:S(2)}, u32[]{:S(2)}) collective-permute-start(bf16[256,256]{1,0:T(8,128)(2,1)S(1)} %copy.70.behind_kv_ref), channel_id=1, source_target_pairs={{56,0},{60,4},{0,8},{4,12},{8,16},{12,20},{16,24},{20,28},{24,32},... | collective-permute-start | bytes 393224 | tf_op jit(solution)/shard_map/while/body/eval_jaxpr/ppermute | solution.py:22
  148.5 1.8 copy-start.3
  152.1 16.4 %collective-permute-start.3 = (f32[256,256]{1,0:T(8,128)}, f32[256,256]{1,0:T(8,128)}, u32[]{:S(2)}, u32[]{:S(2)}) collective-permute-start(f32[256,256]{1,0:T(8,128)} %get-tuple-element.342), channel_id=1, source_target_pairs={{56,0},{60,4},{0,8},{4,12},{8,16},{12,20},{16,24},{20,28},{24,32},... | collective-permute-start | bytes 786440 | tf_op jit(solution)/shard_map/while/body/eval_jaxpr/ppermute | solution.py:22
  152.2 18.1 %collective-permute-start.2 = (f32[256,256]{1,0:T(8,128)}, f32[256,256]{1,0:T(8,128)}, u32[]{:S(2)}, u32[]{:S(2)}) collective-permute-start(f32[256,256]{1,0:T(8,128)} %get-tuple-element.341), channel_id=1, source_target_pairs={{8,0},{12,4},{16,8},{20,12},{24,16},{28,20},{32,24},{36,28},{40,32... | collective-permute-start | bytes 786440 | tf_op jit(solution)/shard_map/while/body/eval_jaxpr/ppermute | solution.py:22
  162.4 2.7 %copy-start.1 = (bf16[256,256]{1,0:T(8,128)(2,1)}, bf16[256,256]{1,0:T(8,128)(2,1)S(1)}, u32[]{:S(2)}) copy-start(bf16[256,256]{1,0:T(8,128)(2,1)S(1)} %copy.69.ahead_kv_ref) | copy-start | bytes 393220 | tf_op jit(solution)/shard_map/while
  162.4 9.6 %collective-permute-start = (bf16[256,256]{1,0:T(8,128)(2,1)S(1)}, bf16[256,256]{1,0:T(8,128)(2,1)}, u32[]{:S(2)}, u32[]{:S(2)}) collective-permute-start(bf16[256,256]{1,0:T(8,128)(2,1)S(1)} %copy.69.ahead_kv_ref), channel_id=1, source_target_pairs={{8,0},{12,4},{16,8},{20,12},{24,16},{28,20},{32,24},{36,28},{40,32... | collective-permute-start | bytes 393224 | tf_op jit(solution)/shard_map/while/body/eval_jaxpr/ppermute | solution.py:22
  165.1 0.6 copy-start.2
  165.1 6.9 %collective-permute-start.1 = (bf16[256,256]{1,0:T(8,128)(2,1)S(1)}, bf16[256,256]{1,0:T(8,128)(2,1)S(1)}, u32[]{:S(2)}, u32[]{:S(2)}) collective-permute-start(bf16[256,256]{1,0:T(8,128)(2,1)S(1)} %copy.70.behind_kv_ref), channel_id=1, source_target_pairs={{56,0},{60,4},{0,8},{4,12},{8,16},{12,20},{16,24},{20,28},{24,32},... | collective-permute-start | bytes 393224 | tf_op jit(solution)/shard_map/while/body/eval_jaxpr/ppermute | solution.py:22
  168.5 1.8 copy-start.3
  172.0 20.2 %collective-permute-start.7 = (f32[256,256]{1,0:T(8,128)}, f32[256,256]{1,0:T(8,128)}, u32[]{:S(2)}, u32[]{:S(2)}) collective-permute-start(f32[256,256]{1,0:T(8,128)} %get-tuple-element.190), channel_id=1, source_target_pairs={{8,0},{12,4},{16,8},{20,12},{24,16},{28,20},{32,24},{36,28},{40,32... | collective-permute-start | bytes 786440 | tf_op jit(solution)/shard_map/ppermute | solution.py:22
  188.0 20.4 %collective-permute-start.9 = (f32[256,256]{1,0:T(8,128)}, f32[256,256]{1,0:T(8,128)S(1)}, u32[]{:S(2)}, u32[]{:S(2)}) collective-permute-start(f32[256,256]{1,0:T(8,128)} %get-tuple-element.192), channel_id=1, source_target_pairs={{56,0},{60,4},{0,8},{4,12},{8,16},{12,20},{16,24},{20,28},{24,32},... | collective-permute-start | bytes 786440 | tf_op jit(solution)/shard_map/ppermute | solution.py:22
  192.2 16.2 %copy-start.8 = (f32[256,256]{1,0:T(8,128)S(1)}, f32[256,256]{1,0:T(8,128)}, u32[]{:S(2)}) copy-start(f32[256,256]{1,0:T(8,128)} %get-tuple-element.193) | copy-start | bytes 786436
  193.3 19.0 %collective-permute-start.8 = (f32[256,256]{1,0:T(8,128)S(1)}, f32[256,256]{1,0:T(8,128)S(1)}, u32[]{:S(2)}, u32[]{:S(2)}) collective-permute-start(f32[256,256]{1,0:T(8,128)S(1)} %add.154), channel_id=1, source_target_pairs={{8,0},{12,4},{16,8},{20,12},{24,16},{28,20},{32,24},{36,28},{40,32... | collective-permute-start | bytes 786440 | tf_op jit(solution)/shard_map/ppermute | solution.py:22
  208.4 7.7 %collective-permute-start.10 = (f32[256,256]{1,0:T(8,128)S(1)}, f32[256,256]{1,0:T(8,128)S(1)}, u32[]{:S(2)}, u32[]{:S(2)}) collective-permute-start(f32[256,256]{1,0:T(8,128)S(1)} %add.155), channel_id=1, source_target_pairs={{56,0},{60,4},{0,8},{4,12},{8,16},{12,20},{16,24},{20,28},{24,32},... | collective-permute-start | bytes 786440 | tf_op jit(solution)/shard_map/ppermute | solution.py:22
  216.1 17.3 %collective-permute-start.11 = (f32[256,256]{1,0:T(8,128)S(1)}, f32[256,256]{1,0:T(8,128)S(1)}, u32[]{:S(2)}, u32[]{:S(2)}) collective-permute-start(f32[256,256]{1,0:T(8,128)S(1)} %broadcast_select_fusion), channel_id=1, source_target_pairs={{0,4},{4,0},{8,12},{12,8},{16,20},{20,16},{24,28},{28,24},{32,36},... | collective-permute-start | bytes 786440 | tf_op jit(solution)/shard_map/ppermute | solution.py:27

commit v7 on v6

v7 whole, which is shorter than its diff:
```python
import math

import jax
import jax.numpy as jnp
from jax import lax
from jax.experimental import pallas as pl
from jax.experimental.pallas import tpu as pltpu
from jax.sharding import PartitionSpec as P

BLK = 128
HEAD_SIZE = 128
Y_HI = 2


def along_z(value, ctx_count, shift):
    z_count = ctx_count // Y_HI
    pairs = [
        (Y_HI * ((z + shift) % z_count) + h, Y_HI * z + h)
        for z in range(z_count)
        for h in range(Y_HI)
    ]
    return lax.ppermute(value, "ctx", pairs)


def from_partner(value, ctx_count):
    pairs = [(c, c ^ 1) for c in range(ctx_count)]
    return lax.ppermute(value, "ctx", pairs)


def turn_kernel(turn_ref, code_ref, q_ref, do_ref, ahead_kv_ref, behind_kv_ref, lse_ref, delta_ref,
                dq_in_ref, ahead_in_ref, behind_in_ref, dq_ref, ahead_ref, behind_ref):
    heads, tok_rows, _ = q_ref.shape
    half = ahead_kv_ref.shape[0]
    key_count = 2 * half
    row_blocks = tok_rows // BLK
    key_blocks = key_count // BLK
    scale = 1.0 / math.sqrt(HEAD_SIZE)
    turn = turn_ref[0]
    key_row = lax.broadcasted_iota(jnp.int32, (key_count, tok_rows), 0)
    query_col = lax.broadcasted_iota(jnp.int32, (key_count, tok_rows), 1)
    key_block = key_row // BLK
    query_block = query_col // BLK
    code = jnp.zeros((key_count, tok_rows), jnp.int32)
    for r in range(row_blocks):
        for c in range(key_blocks):
            code = jnp.where((query_block == r) & (key_block == c), code_ref[turn, r * key_blocks + c], code)
    below = (key_row - key_block * BLK) <= (query_col - query_block * BLK)
    live = (code == 1) | ((code == 2) & below)
    keys = jnp.concatenate([ahead_kv_ref[:, :HEAD_SIZE], behind_kv_ref[:, :HEAD_SIZE]], axis=0)
    values = jnp.concatenate([ahead_kv_ref[:, HEAD_SIZE:], behind_kv_ref[:, HEAD_SIZE:]], axis=0)
    dk = jnp.zeros((key_count, HEAD_SIZE), jnp.float32)
    dv = jnp.zeros((key_count, HEAD_SIZE), jnp.float32)
    for h in range(heads):
        q = q_ref[h]
        do = do_ref[h]
        st = lax.dot_general(keys, q, (((1,), (1,)), ((), ())), preferred_element_type=jnp.float32)
        pt = jnp.where(live, jnp.exp(st * scale - lse_ref[h]), 0.0)
        dpt = lax.dot_general(values, do, (((1,), (1,)), ((), ())), preferred_element_type=jnp.float32)
        dst = (pt * (dpt - delta_ref[h])).astype(jnp.bfloat16).astype(keys.dtype)
        dq_ref[h] = dq_in_ref[h] + lax.dot_general(
            dst, keys, (((0,), (0,)), ((), ())), preferred_element_type=jnp.float32
        )
        dk = dk + jnp.dot(dst, q, preferred_element_type=jnp.float32)
        dv = dv + jnp.dot(pt.astype(jnp.bfloat16).astype(do.dtype), do, preferred_element_type=jnp.float32)
    ahead_ref[:, :HEAD_SIZE] = ahead_in_ref[:, :HEAD_SIZE] + dk[:half]
    ahead_ref[:, HEAD_SIZE:] = ahead_in_ref[:, HEAD_SIZE:] + dv[:half]
    behind_ref[:, :HEAD_SIZE] = behind_in_ref[:, :HEAD_SIZE] + dk[half:]
    behind_ref[:, HEAD_SIZE:] = behind_in_ref[:, HEAD_SIZE:] + dv[half:]


def turn_call(turn, codes, q, do, ahead_kv, behind_kv, lse, delta, dq_acc, ahead_in, behind_in):
    vmem = pl.BlockSpec(memory_space=pltpu.MemorySpace.VMEM)
    smem = pl.BlockSpec(memory_space=pltpu.MemorySpace.SMEM)
    return pl.pallas_call(
        turn_kernel,
        out_shape=(
            jax.ShapeDtypeStruct(dq_acc.shape, jnp.float32),
            jax.ShapeDtypeStruct(ahead_in.shape, jnp.float32),
            jax.ShapeDtypeStruct(behind_in.shape, jnp.float32),
        ),
        in_specs=[smem, smem] + [vmem] * 9,
        out_specs=(vmem, vmem, vmem),
        input_output_aliases={8: 0, 9: 1, 10: 2},
    )(turn, codes, q, do, ahead_kv, behind_kv, lse, delta, dq_acc, ahead_in, behind_in)


def local(query_rows, key_matrix, value_matrix, attn_out, out_grad, log_sums, block_mask):
    tok_rows = query_rows.shape[0]
    col_width = query_rows.shape[1]
    heads_local = col_width // HEAD_SIZE
    ctx_pos = lax.axis_index("ctx")
    ctx_count = lax.axis_size("ctx")
    tp_count = lax.axis_size("tp")
    grad_rows = out_grad.shape[0]
    pieces = out_grad.reshape(grad_rows, tp_count, col_width)
    own_grad = lax.all_to_all(pieces, "tp", split_axis=1, concat_axis=0, tiled=True)
    out_grads = own_grad.reshape(tok_rows, heads_local, HEAD_SIZE)
    outputs = attn_out.reshape(tok_rows, heads_local, HEAD_SIZE)
    row_delta = jnp.sum(out_grads.astype(jnp.float32) * outputs.astype(jnp.float32), axis=2)
    delta_heads = row_delta.T[:, None, :]
    lse_heads = log_sums[:, None, :]
    query_heads = query_rows.reshape(tok_rows, heads_local, HEAD_SIZE).transpose(1, 0, 2)
    grad_heads = out_grads.transpose(1, 0, 2)
    query_start = ctx_pos * tok_rows
    z_pos = ctx_pos // Y_HI
    z_count = ctx_count // Y_HI
    y_hi = ctx_pos % Y_HI
    super_rows = Y_HI * tok_rows
    turns = jnp.arange(z_count, dtype=jnp.int32)
    ahead_owner = (z_pos + turns) % z_count
    behind_owner = (z_pos - turns) % z_count
    half_blocks = tok_rows // BLK
    key_block = jnp.concatenate(
        [
            ahead_owner[:, None] * (2 * half_blocks) + jnp.arange(half_blocks)[None, :],
            behind_owner[:, None] * (2 * half_blocks) + half_blocks + jnp.arange(half_blocks)[None, :],
        ],
        axis=1,
    )
    query_block = query_start // BLK + jnp.arange(half_blocks, dtype=jnp.int32)
    qb = query_block[None, :, None]
    kb = key_block[:, None, :]
    allowed = block_mask[qb, kb]
    codes = jnp.where(kb == qb, 2, jnp.where((kb < qb) & (allowed == 1), 1, 0))
    codes = codes.reshape(z_count, -1).astype(jnp.int32)

    def terms(ahead_kv, behind_kv, turn, query_acc, ahead_in, behind_in):
        turn_index = jnp.reshape(turn, (1,)).astype(jnp.int32)
        return turn_call(
            turn_index,
            codes,
            query_heads,
            grad_heads,
            ahead_kv,
            behind_kv,
            lse_heads,
            delta_heads,
            query_acc,
            ahead_in,
            behind_in,
        )

    key_values = jnp.concatenate([key_matrix, value_matrix], axis=1)
    partner_kv = from_partner(key_values, ctx_count)
    ahead_kv = jnp.where(y_hi == 0, key_values, partner_kv)
    behind_kv = jnp.where(y_hi == 0, partner_kv, key_values)
    next_ahead = along_z(ahead_kv, ctx_count, 1)
    next_behind = along_z(behind_kv, ctx_count, -1)
    zero_query = jnp.zeros((heads_local, tok_rows, HEAD_SIZE), jnp.float32)
    zero_total = jnp.zeros((tok_rows, 2 * HEAD_SIZE), jnp.float32)
    query_acc, ahead_pending, behind_pending = terms(
        ahead_kv, behind_kv, 0, zero_query, zero_total, zero_total
    )

    def visit_turn(turn, carried):
        ahead_kv, behind_kv, query_acc, ahead_pending, behind_pending = carried
        ahead_received = along_z(ahead_pending, ctx_count, 1)
        behind_received = along_z(behind_pending, ctx_count, -1)
        next_ahead = along_z(ahead_kv, ctx_count, 1)
        next_behind = along_z(behind_kv, ctx_count, -1)
        query_acc, ahead_pending, behind_pending = terms(
            ahead_kv, behind_kv, turn, query_acc, ahead_received, behind_received
        )
        return (next_ahead, next_behind, query_acc, ahead_pending, behind_pending)

    ahead_kv, behind_kv, query_acc, ahead_pending, behind_pending = lax.fori_loop(
        1,
        z_count - 1,
        visit_turn,
        (next_ahead, next_behind, query_acc, ahead_pending, behind_pending),
    )
    ahead_received = along_z(ahead_pending, ctx_count, 1)
    behind_received = along_z(behind_pending, ctx_count, -1)
    query_acc, ahead_pending, behind_pending = terms(
        ahead_kv, behind_kv, z_count - 1, query_acc, ahead_received, behind_received
    )
    ahead_total = along_z(ahead_pending, ctx_count, 1)
    behind_total = along_z(behind_pending, ctx_count, -1)
    own_total = jnp.where(y_hi == 0, ahead_total, behind_total)
    other_total = jnp.where(y_hi == 0, behind_total, ahead_total)
    summed = own_total + from_partner(other_total, ctx_count)
    logit_scale = 1.0 / math.sqrt(HEAD_SIZE)
    query_grad = (query_acc * logit_scale).transpose(1, 0, 2).reshape(tok_rows, col_width)
    query_grad = query_grad.astype(jnp.bfloat16)
    key_gradient = (summed[:, :HEAD_SIZE] * logit_scale).astype(jnp.bfloat16)
    value_gradient = summed[:, HEAD_SIZE:].astype(jnp.bfloat16)
    return (query_grad, key_gradient, value_gradient)


def solution(mesh):
    placed = (
        P(("dp", "ctx"), "tp"),
        P(("dp", "ctx"), "tp"),
        P(("dp", "ctx"), "tp"),
        P(("dp", "ctx"), "tp"),
        P(("dp", "ctx", "tp"), None),
        P("tp", ("dp", "ctx")),
        P("dp", None),
    )
    return jax.shard_map(
        local,
        mesh=mesh,
        in_specs=placed,
        out_specs=(P(("dp", "ctx"), "tp"), P(("dp", "ctx"), "tp"), P(("dp", "ctx"), "tp")),
        check_vma=False,
    )
```

time: 236 us -> 174 us (0.74)
  starting transfers between devices: 147 us -> 52.9 us
  waiting for transfers between devices: 13 us -> 40.6 us
  other arithmetic: 25.1 us -> 2.51 us
  Pallas kernels: 28 us -> 50.4 us
  local copies, waits for them, and re-layouts: 20.6 us -> 25.7 us
    ppermute x30, starting transfers between devices: 127 us -> 45.7 us  [along_z(): return lax.ppermute(value, 'ctx', pairs)]
    ppermute x30, waiting for transfers between devices: 9.95 us -> 34.5 us  [along_z(): return lax.ppermute(value, 'ctx', pairs)]
    pallas_call x8, Pallas kernels: 28 us -> 50.4 us  [turn_call(): pl.pallas_call(turn_kernel, out_shape=(jax.ShapeDtypeStruct(dq_acc.shape,...]
    add x14 -> x0, other arithmetic: 22.3 us -> none  [the longest x6 11 us: visit_turn(): behind_received + behind_term]
    ppermute x2, starting transfers between devices: 16.3 us -> 3.7 us  [from_partner(): return lax.ppermute(value, 'ctx', pairs)]
    while x36 -> x72, local copies, waits for them, and re-layouts: 2.97 us -> 14.8 us
    another operation x12, local copies, waits for them, and re-layouts: 5.48 us -> 0.11 us
    ppermute x2, waiting for transfers between devices: 3.01 us -> 6.12 us  [from_partner(): return lax.ppermute(value, 'ctx', pairs)]
  transfers between devices with their start and end apart: 33 -> 33, of which waited for: 5 -> 15; matrix products, arithmetic and copies ran while one was open for 17% -> 11% of each run, Pallas kernels for 12% -> 25%
where the time goes in v7:
time: 174 us; the launch traced here: 173 us
  starting transfers between devices  52.9 us (30%)
  Pallas kernels  50.4 us (29%)
  waiting for transfers between devices  40.6 us (23%)
  local copies, waits for them, and re-layouts  25.7 us (15%)
  other arithmetic  2.51 us (1%)
    pallas_call x8, Pallas kernels, turn_call(): pl.pallas_call(turn_kernel, out_shape=(jax.ShapeDtypeStruct(dq_acc.shape,...  50.4 us
    ppermute x30, starting transfers between devices, along_z(): return lax.ppermute(value, 'ctx', pairs)  45.7 us
    ppermute x30, waiting for transfers between devices, along_z(): return lax.ppermute(value, 'ctx', pairs)  34.5 us
    while x72, local copies, waits for them, and re-layouts  14.8 us
    ppermute x2, waiting for transfers between devices, from_partner(): return lax.ppermute(value, 'ctx', pairs)  6.12 us
    unnamed x23, local copies, waits for them, and re-layouts  4.62 us
    ppermute x2, starting transfers between devices, from_partner(): return lax.ppermute(value, 'ctx', pairs)  3.7 us
  transfers between devices with their start and end apart: 33, of which 15 were waited for; matrix products, arithmetic and copies ran while one was open for 11% of the time, Pallas kernels for 25%

profile of v7, /device:TPU:4, one launch (start us, length us, event | category | flops | bytes accessed | tf_op | source)
XLA Modules:
  0.0 173.5 jit_solution(12522707207761850545)
XLA Ops:
  0.7 1.5 constant_dynamic-update-slice_fusion.1
  2.8 3.2 %collective-permute-start.4 = (bf16[256,256]{1,0:T(8,128)(2,1)}, bf16[256,256]{1,0:T(8,128)(2,1)}, u32[]{:S(2)}, u32[]{:S(2)}) collective-permute-start(bf16[256,256]{1,0:T(8,128)(2,1)} %constant_dynamic-update-slice_fusion), channel_id=1, source_target_pairs={{0,4},{4,0},{8,12},{12,8},{16,20},{20,16},{24,28},{28,24},{32,36},... | collective-permute-start | bytes 393224 | tf_op jit(solution)/shard_map/ppermute | solution.py:27
  6.0 1.9 %copy.49 = bf16[8,4,8,1024]{3,2,0,1:T(8,128)(2,1)} copy(bf16[8,4,8,1024]{3,2,1,0:T(8,128)(2,1)} %bitcast.39) | data formatting | bytes 1048576 | tf_op jit(solution)/shard_map/reshape | solution.py:95
  7.9 3.5 %all-to-all-start = ((bf16[64,4,1024]{2,0,1:T(8,128)(2,1)}), bf16[64,4,1024]{2,0,1:T(8,128)(2,1)S(1)}, u32[]{:S(2)}, u32[]{:S(2)}) async-start(bf16[64,4,1024]{2,0,1:T(8,128)(2,1)} %bitcast.25), calls=%async_computation | async-start | bytes 1048576 | tf_op jit(solution)/shard_map/all_to_all | solution.py:96
  12.2 0.8 gather_fusion
  13.7 0.8 copy-done.9
  15.0 1.0 broadcast_select_fusion.1
  16.0 2.0 %collective-permute-start.6 = (bf16[256,256]{1,0:T(8,128)(2,1)S(1)}, bf16[256,256]{1,0:T(8,128)(2,1)S(1)}, u32[]{:S(2)}, u32[]{:S(2)}) collective-permute-start(bf16[256,256]{1,0:T(8,128)(2,1)S(1)} %get-tuple-element.228.behind_kv_ref), channel_id=1, source_target_pairs={{56,0},{60,4},{0,8},{4,12},{8,16},{12,20},{16,24},{20,28},{24,32},... | collective-permute-start | bytes 393224 | tf_op jit(solution)/shard_map/ppermute | solution.py:22
  18.0 4.2 %collective-permute-start.5 = (bf16[256,256]{1,0:T(8,128)(2,1)S(1)}, bf16[256,256]{1,0:T(8,128)(2,1)S(1)}, u32[]{:S(2)}, u32[]{:S(2)}) collective-permute-start(bf16[256,256]{1,0:T(8,128)(2,1)S(1)} %get-tuple-element.229.ahead_kv_ref), channel_id=1, source_target_pairs={{8,0},{12,4},{16,8},{20,12},{24,16},{28,20},{32,24},{36,28},{40,32... | collective-permute-start | bytes 393224 | tf_op jit(solution)/shard_map/ppermute | solution.py:22
  22.9 0.7 broadcast_in_dim.45.ahead_in_ref
  23.7 6.2 %shard_map.94 = (f32[8,256,128]{2,1,0:T(8,128)S(1)}, f32[256,256]{1,0:T(8,128)}, f32[256,256]{1,0:T(8,128)S(1)}) custom-call(s32[1]{0:T(128)} %constant.90.clone.1.turn_ref, s32[8,8]{1,0:T(8,128)S(1)} %select_select_fusion.code_ref, bf16[8,256,128]{2,1,0:T(8,128)(2,1)S(1)} %bitcast.29, ...), custom_call_target="tpu_custom_call", output_to_operand_aliasing={{0}: (8, {}), {1}: (9, {}), {2}: (10, {})} | custom-call | tf_op jit(solution)/shard_map/pallas_call | solution.py:74
  29.9 107.3 %while.21 = (s32[]{:T(128)}, bf16[256,256]{1,0:T(8,128)(2,1)S(1)}, bf16[256,256]{1,0:T(8,128)(2,1)S(1)}, f32[8,256,128]{2,1,0:T(8,128)S(1)}, f32[256,256]{1,0:T(...) while((s32[]{:T(128)}, bf16[256,256]{1,0:T(8,128)(2,1)S(1)}, ...), condition=%wide.region_2.3_spmd, body=%wide.region_1.2_spmd.sunk | while | flops 2 | bytes 8913313 | solution.py:166
  30.0 3.9 %collective-permute-start.2 = (f32[256,256]{1,0:T(8,128)}, f32[256,256]{1,0:T(8,128)S(1)}, u32[]{:S(2)}, u32[]{:S(2)}) collective-permute-start(f32[256,256]{1,0:T(8,128)} %get-tuple-element.323), channel_id=1, source_target_pairs={{8,0},{12,4},{16,8},{20,12},{24,16},{28,20},{32,24},{36,28},{40,32... | collective-permute-start | bytes 786440 | tf_op jit(solution)/shard_map/while/body/eval_jaxpr/ppermute | solution.py:22
  33.9 2.0 %collective-permute-start = (bf16[256,256]{1,0:T(8,128)(2,1)S(1)}, bf16[256,256]{1,0:T(8,128)(2,1)S(1)}, u32[]{:S(2)}, u32[]{:S(2)}) collective-permute-start(bf16[256,256]{1,0:T(8,128)(2,1)S(1)} %copy.65.ahead_kv_ref), channel_id=1, source_target_pairs={{8,0},{12,4},{16,8},{20,12},{24,16},{28,20},{32,24},{36,28},{40,32... | collective-permute-start | bytes 393224 | tf_op jit(solution)/shard_map/while/body/eval_jaxpr/ppermute | solution.py:22
  36.1 4.8 %collective-permute-done.3.behind_in_ref = f32[256,256]{1,0:T(8,128)S(1)} collective-permute-done((f32[256,256]{1,0:T(8,128)S(1)}, f32[256,256]{1,0:T(8,128)S(1)}, u32[]{:S(2)}, u32[]{:S(2)}) %collective-permute-start.3) | collective-permute-done | bytes 262176 | tf_op jit(solution)/shard_map/while/body/eval_jaxpr/ppermute | solution.py:22
  40.9 0.7 copy-done.1
  41.7 6.3 %eval_jaxpr.5 = (f32[8,256,128]{2,1,0:T(8,128)S(1)}, f32[256,256]{1,0:T(8,128)}, f32[256,256]{1,0:T(8,128)}) custom-call(s32[1]{0:T(128)} %bitcast.28.turn_ref, s32[8,8]{1,0:T(8,128)S(1)} %get-tuple-element.337.code_ref, bf16[8,256,128]{2,1,0:T(8,128)(2,1)S(1)} %get-tuple-element.338.q_ref, ...), custom_call_target="tpu_custom_call", output_to_operand_aliasing={{0}: (8, {}), {1}: (9, {}), {2}: (10, {})} | custom-call | tf_op jit(solution)/shard_map/while/body/eval_jaxpr/pallas_call | solution.py:74
  48.1 1.7 copy.74
  50.0 3.5 %collective-permute-start.2 = (f32[256,256]{1,0:T(8,128)}, f32[256,256]{1,0:T(8,128)S(1)}, u32[]{:S(2)}, u32[]{:S(2)}) collective-permute-start(f32[256,256]{1,0:T(8,128)} %get-tuple-element.323), channel_id=1, source_target_pairs={{8,0},{12,4},{16,8},{20,12},{24,16},{28,20},{32,24},{36,28},{40,32... | collective-permute-start | bytes 786440 | tf_op jit(solution)/shard_map/while/body/eval_jaxpr/ppermute | solution.py:22
  53.5 2.0 %collective-permute-start = (bf16[256,256]{1,0:T(8,128)(2,1)S(1)}, bf16[256,256]{1,0:T(8,128)(2,1)S(1)}, u32[]{:S(2)}, u32[]{:S(2)}) collective-permute-start(bf16[256,256]{1,0:T(8,128)(2,1)S(1)} %copy.65.ahead_kv_ref), channel_id=1, source_target_pairs={{8,0},{12,4},{16,8},{20,12},{24,16},{28,20},{32,24},{36,28},{40,32... | collective-permute-start | bytes 393224 | tf_op jit(solution)/shard_map/while/body/eval_jaxpr/ppermute | solution.py:22
  55.7 3.4 %collective-permute-done.3.behind_in_ref = f32[256,256]{1,0:T(8,128)S(1)} collective-permute-done((f32[256,256]{1,0:T(8,128)S(1)}, f32[256,256]{1,0:T(8,128)S(1)}, u32[]{:S(2)}, u32[]{:S(2)}) %collective-permute-start.3) | collective-permute-done | bytes 262176 | tf_op jit(solution)/shard_map/while/body/eval_jaxpr/ppermute | solution.py:22
  59.2 0.7 copy-done.1
  59.9 6.3 %eval_jaxpr.5 = (f32[8,256,128]{2,1,0:T(8,128)S(1)}, f32[256,256]{1,0:T(8,128)}, f32[256,256]{1,0:T(8,128)}) custom-call(s32[1]{0:T(128)} %bitcast.28.turn_ref, s32[8,8]{1,0:T(8,128)S(1)} %get-tuple-element.337.code_ref, bf16[8,256,128]{2,1,0:T(8,128)(2,1)S(1)} %get-tuple-element.338.q_ref, ...), custom_call_target="tpu_custom_call", output_to_operand_aliasing={{0}: (8, {}), {1}: (9, {}), {2}: (10, {})} | custom-call | tf_op jit(solution)/shard_map/while/body/eval_jaxpr/pallas_call | solution.py:74
  66.3 1.7 copy.74
  68.0 1.7 %collective-permute-start.3 = (f32[256,256]{1,0:T(8,128)S(1)}, f32[256,256]{1,0:T(8,128)S(1)}, u32[]{:S(2)}, u32[]{:S(2)}) collective-permute-start(f32[256,256]{1,0:T(8,128)S(1)} %get-tuple-element.324), channel_id=1, source_target_pairs={{56,0},{60,4},{0,8},{4,12},{8,16},{12,20},{16,24},{20,28},{24,32},... | collective-permute-start | bytes 786440 | tf_op jit(solution)/shard_map/while/body/eval_jaxpr/ppermute | solution.py:22
  69.8 1.6 collective-permute-start.2
  71.4 1.6 collective-permute-start
  73.6 2.2 %collective-permute-done.3.behind_in_ref = f32[256,256]{1,0:T(8,128)S(1)} collective-permute-done((f32[256,256]{1,0:T(8,128)S(1)}, f32[256,256]{1,0:T(8,128)S(1)}, u32[]{:S(2)}, u32[]{:S(2)}) %collective-permute-start.3) | collective-permute-done | bytes 262176 | tf_op jit(solution)/shard_map/while/body/eval_jaxpr/ppermute | solution.py:22
  77.1 6.3 %eval_jaxpr.5 = (f32[8,256,128]{2,1,0:T(8,128)S(1)}, f32[256,256]{1,0:T(8,128)}, f32[256,256]{1,0:T(8,128)}) custom-call(s32[1]{0:T(128)} %bitcast.28.turn_ref, s32[8,8]{1,0:T(8,128)S(1)} %get-tuple-element.337.code_ref, bf16[8,256,128]{2,1,0:T(8,128)(2,1)S(1)} %get-tuple-element.338.q_ref, ...), custom_call_target="tpu_custom_call", output_to_operand_aliasing={{0}: (8, {}), {1}: (9, {}), {2}: (10, {})} | custom-call | tf_op jit(solution)/shard_map/while/body/eval_jaxpr/pallas_call | solution.py:74
  83.4 1.7 copy.74
  85.2 1.8 %collective-permute-start.3 = (f32[256,256]{1,0:T(8,128)S(1)}, f32[256,256]{1,0:T(8,128)S(1)}, u32[]{:S(2)}, u32[]{:S(2)}) collective-permute-start(f32[256,256]{1,0:T(8,128)S(1)} %get-tuple-element.324), channel_id=1, source_target_pairs={{56,0},{60,4},{0,8},{4,12},{8,16},{12,20},{16,24},{20,28},{24,32},... | collective-permute-start | bytes 786440 | tf_op jit(solution)/shard_map/while/body/eval_jaxpr/ppermute | solution.py:22
  87.0 1.5 collective-permute-start.2
  88.5 1.6 collective-permute-start
  90.7 2.1 %collective-permute-done.3.behind_in_ref = f32[256,256]{1,0:T(8,128)S(1)} collective-permute-done((f32[256,256]{1,0:T(8,128)S(1)}, f32[256,256]{1,0:T(8,128)S(1)}, u32[]{:S(2)}, u32[]{:S(2)}) %collective-permute-start.3) | collective-permute-done | bytes 262176 | tf_op jit(solution)/shard_map/while/body/eval_jaxpr/ppermute | solution.py:22
  92.8 0.7 collective-permute-done.2.ahead_in_ref
  93.6 0.7 copy-done.3
  94.3 6.3 %eval_jaxpr.5 = (f32[8,256,128]{2,1,0:T(8,128)S(1)}, f32[256,256]{1,0:T(8,128)}, f32[256,256]{1,0:T(8,128)}) custom-call(s32[1]{0:T(128)} %bitcast.28.turn_ref, s32[8,8]{1,0:T(8,128)S(1)} %get-tuple-element.337.code_ref, bf16[8,256,128]{2,1,0:T(8,128)(2,1)S(1)} %get-tuple-element.338.q_ref, ...), custom_call_target="tpu_custom_call", output_to_operand_aliasing={{0}: (8, {}), {1}: (9, {}), {2}: (10, {})} | custom-call | tf_op jit(solution)/shard_map/while/body/eval_jaxpr/pallas_call | solution.py:74
  100.6 1.7 copy.74
  102.4 1.9 %collective-permute-start.3 = (f32[256,256]{1,0:T(8,128)S(1)}, f32[256,256]{1,0:T(8,128)S(1)}, u32[]{:S(2)}, u32[]{:S(2)}) collective-permute-start(f32[256,256]{1,0:T(8,128)S(1)} %get-tuple-element.324), channel_id=1, source_target_pairs={{56,0},{60,4},{0,8},{4,12},{8,16},{12,20},{16,24},{20,28},{24,32},... | collective-permute-start | bytes 786440 | tf_op jit(solution)/shard_map/while/body/eval_jaxpr/ppermute | solution.py:22
  104.3 1.4 collective-permute-start.2
  105.7 1.6 collective-permute-start
  107.9 2.1 %collective-permute-done.3.behind_in_ref = f32[256,256]{1,0:T(8,128)S(1)} collective-permute-done((f32[256,256]{1,0:T(8,128)S(1)}, f32[256,256]{1,0:T(8,128)S(1)}, u32[]{:S(2)}, u32[]{:S(2)}) %collective-permute-start.3) | collective-permute-done | bytes 262176 | tf_op jit(solution)/shard_map/while/body/eval_jaxpr/ppermute | solution.py:22
  110.0 0.8 collective-permute-done.2.ahead_in_ref
  111.6 6.3 %eval_jaxpr.5 = (f32[8,256,128]{2,1,0:T(8,128)S(1)}, f32[256,256]{1,0:T(8,128)}, f32[256,256]{1,0:T(8,128)}) custom-call(s32[1]{0:T(128)} %bitcast.28.turn_ref, s32[8,8]{1,0:T(8,128)S(1)} %get-tuple-element.337.code_ref, bf16[8,256,128]{2,1,0:T(8,128)(2,1)S(1)} %get-tuple-element.338.q_ref, ...), custom_call_target="tpu_custom_call", output_to_operand_aliasing={{0}: (8, {}), {1}: (9, {}), {2}: (10, {})} | custom-call | tf_op jit(solution)/shard_map/while/body/eval_jaxpr/pallas_call | solution.py:74
  117.9 1.7 copy.74
  119.7 2.1 %collective-permute-start.3 = (f32[256,256]{1,0:T(8,128)S(1)}, f32[256,256]{1,0:T(8,128)S(1)}, u32[]{:S(2)}, u32[]{:S(2)}) collective-permute-start(f32[256,256]{1,0:T(8,128)S(1)} %get-tuple-element.324), channel_id=1, source_target_pairs={{56,0},{60,4},{0,8},{4,12},{8,16},{12,20},{16,24},{20,28},{24,32},... | collective-permute-start | bytes 786440 | tf_op jit(solution)/shard_map/while/body/eval_jaxpr/ppermute | solution.py:22
  121.8 1.2 collective-permute-start.2
  123.0 1.5 collective-permute-start
  124.5 0.7 collective-permute-start.1
  125.2 2.1 %collective-permute-done.3.behind_in_ref = f32[256,256]{1,0:T(8,128)S(1)} collective-permute-done((f32[256,256]{1,0:T(8,128)S(1)}, f32[256,256]{1,0:T(8,128)S(1)}, u32[]{:S(2)}, u32[]{:S(2)}) %collective-permute-start.3) | collective-permute-done | bytes 262176 | tf_op jit(solution)/shard_map/while/body/eval_jaxpr/ppermute | solution.py:22
  127.3 1.0 collective-permute-done.2.ahead_in_ref
  129.1 6.3 %eval_jaxpr.5 = (f32[8,256,128]{2,1,0:T(8,128)S(1)}, f32[256,256]{1,0:T(8,128)}, f32[256,256]{1,0:T(8,128)}) custom-call(s32[1]{0:T(128)} %bitcast.28.turn_ref, s32[8,8]{1,0:T(8,128)S(1)} %get-tuple-element.337.code_ref, bf16[8,256,128]{2,1,0:T(8,128)(2,1)S(1)} %get-tuple-element.338.q_ref, ...), custom_call_target="tpu_custom_call", output_to_operand_aliasing={{0}: (8, {}), {1}: (9, {}), {2}: (10, {})} | custom-call | tf_op jit(solution)/shard_map/while/body/eval_jaxpr/pallas_call | solution.py:74
  135.4 1.7 copy.74
  137.2 1.6 collective-permute-start.8
  138.8 1.9 %collective-permute-start.7 = (f32[256,256]{1,0:T(8,128)}, f32[256,256]{1,0:T(8,128)S(1)}, u32[]{:S(2)}, u32[]{:S(2)}) collective-permute-start(f32[256,256]{1,0:T(8,128)} %get-tuple-element.193), channel_id=1, source_target_pairs={{8,0},{12,4},{16,8},{20,12},{24,16},{28,20},{32,24},{36,28},{40,32... | collective-permute-start | bytes 786440 | tf_op jit(solution)/shard_map/ppermute | solution.py:22
  140.7 4.3 %collective-permute-done.8.behind_in_ref = f32[256,256]{1,0:T(8,128)S(1)} collective-permute-done((f32[256,256]{1,0:T(8,128)S(1)}, f32[256,256]{1,0:T(8,128)S(1)}, u32[]{:S(2)}, u32[]{:S(2)}) %collective-permute-start.8) | collective-permute-done | bytes 262176 | tf_op jit(solution)/shard_map/ppermute | solution.py:22
  145.1 2.5 %collective-permute-done.7.ahead_in_ref = f32[256,256]{1,0:T(8,128)S(1)} collective-permute-done((f32[256,256]{1,0:T(8,128)}, f32[256,256]{1,0:T(8,128)S(1)}, u32[]{:S(2)}, u32[]{:S(2)}) %collective-permute-start.7) | collective-permute-done | bytes 262176 | tf_op jit(solution)/shard_map/ppermute | solution.py:22
  147.5 0.7 copy-done.11
  148.2 6.2 %shard_map.95 = (f32[8,256,128]{2,1,0:T(8,128)S(1)}, f32[256,256]{1,0:T(8,128)}, f32[256,256]{1,0:T(8,128)}) custom-call(s32[1]{0:T(128)} %constant.77.clone.1.turn_ref, s32[8,8]{1,0:T(8,128)S(1)} %get-tuple-element.362, bf16[8,256,128]{2,1,0:T(8,128)(2,1)S(1)} %get-tuple-element.343, ...), custom_call_target="tpu_custom_call", output_to_operand_aliasing={{0}: (8, {}), {1}: (9, {}), {2}: (10, {})} | custom-call | tf_op jit(solution)/shard_map/pallas_call | solution.py:74
  154.4 1.9 %collective-permute-start.9 = (f32[256,256]{1,0:T(8,128)}, f32[256,256]{1,0:T(8,128)S(1)}, u32[]{:S(2)}, u32[]{:S(2)}) collective-permute-start(f32[256,256]{1,0:T(8,128)} %get-tuple-element.196), channel_id=1, source_target_pairs={{8,0},{12,4},{16,8},{20,12},{24,16},{28,20},{32,24},{36,28},{40,32... | collective-permute-start | bytes 786440 | tf_op jit(solution)/shard_map/ppermute | solution.py:22
  156.5 4.6 %collective-permute-done.9 = f32[256,256]{1,0:T(8,128)S(1)} collective-permute-done((f32[256,256]{1,0:T(8,128)}, f32[256,256]{1,0:T(8,128)S(1)}, u32[]{:S(2)}, u32[]{:S(2)}) %collective-permute-start.9) | collective-permute-done | bytes 262176 | tf_op jit(solution)/shard_map/ppermute | solution.py:22
  161.0 3.1 %collective-permute-done.10 = f32[256,256]{1,0:T(8,128)S(1)} collective-permute-done((f32[256,256]{1,0:T(8,128)}, f32[256,256]{1,0:T(8,128)S(1)}, u32[]{:S(2)}, u32[]{:S(2)}) %collective-permute-start.10) | collective-permute-done | bytes 262176 | tf_op jit(solution)/shard_map/ppermute | solution.py:22
  165.0 1.0 copy.44
  166.0 6.1 %collective-permute-done.11 = f32[256,256]{1,0:T(8,128)S(1)} collective-permute-done((f32[256,256]{1,0:T(8,128)S(1)}, f32[256,256]{1,0:T(8,128)S(1)}, u32[]{:S(2)}, u32[]{:S(2)}) %collective-permute-start.11) | collective-permute-done | bytes 262176 | tf_op jit(solution)/shard_map/ppermute | solution.py:27
  (153 shorter events, 11.0 us)
Async XLA Ops:
  0.6 11.5 %copy-start = (s32[32,32]{1,0:T(8,128)S(1)}, s32[32,32]{1,0:T(8,128)}, u32[]{:S(2)}) copy-start(s32[32,32]{1,0:T(8,128)} %param.15) | copy-start | bytes 12292
  0.6 1.5 copy-start.12
  2.8 12.2 %collective-permute-start.4 = (bf16[256,256]{1,0:T(8,128)(2,1)}, bf16[256,256]{1,0:T(8,128)(2,1)}, u32[]{:S(2)}, u32[]{:S(2)}) collective-permute-start(bf16[256,256]{1,0:T(8,128)(2,1)} %constant_dynamic-update-slice_fusion), channel_id=1, source_target_pairs={{0,4},{4,0},{8,12},{12,8},{16,20},{20,16},{24,28},{28,24},{32,36},... | collective-permute-start | bytes 393224 | tf_op jit(solution)/shard_map/ppermute | solution.py:27
  7.9 14.3 %all-to-all-start = ((bf16[64,4,1024]{2,0,1:T(8,128)(2,1)}), bf16[64,4,1024]{2,0,1:T(8,128)(2,1)S(1)}, u32[]{:S(2)}, u32[]{:S(2)}) async-start(bf16[64,4,1024]{2,0,1:T(8,128)(2,1)} %bitcast.25), calls=%async_computation | async-start | bytes 1048576 | tf_op jit(solution)/shard_map/all_to_all | solution.py:96
  12.2 0.9 copy-start.13
  12.2 1.0 copy-start.8
  13.4 1.0 copy-start.9
  16.0 6.3 %copy-start.6 = (bf16[256,256]{1,0:T(8,128)(2,1)}, bf16[256,256]{1,0:T(8,128)(2,1)S(1)}, u32[]{:S(2)}) copy-start(bf16[256,256]{1,0:T(8,128)(2,1)S(1)} %get-tuple-element.229.ahead_kv_ref) | copy-start | bytes 393220
  16.0 6.3 %copy-start.7 = (bf16[256,256]{1,0:T(8,128)(2,1)}, bf16[256,256]{1,0:T(8,128)(2,1)S(1)}, u32[]{:S(2)}) copy-start(bf16[256,256]{1,0:T(8,128)(2,1)S(1)} %get-tuple-element.228.behind_kv_ref) | copy-start | bytes 393220
  16.0 13.9 %collective-permute-start.6 = (bf16[256,256]{1,0:T(8,128)(2,1)S(1)}, bf16[256,256]{1,0:T(8,128)(2,1)S(1)}, u32[]{:S(2)}, u32[]{:S(2)}) collective-permute-start(bf16[256,256]{1,0:T(8,128)(2,1)S(1)} %get-tuple-element.228.behind_kv_ref), channel_id=1, source_target_pairs={{56,0},{60,4},{0,8},{4,12},{8,16},{12,20},{16,24},{20,28},{24,32},... | collective-permute-start | bytes 393224 | tf_op jit(solution)/shard_map/ppermute | solution.py:22
  18.0 11.9 %collective-permute-start.5 = (bf16[256,256]{1,0:T(8,128)(2,1)S(1)}, bf16[256,256]{1,0:T(8,128)(2,1)S(1)}, u32[]{:S(2)}, u32[]{:S(2)}) collective-permute-start(bf16[256,256]{1,0:T(8,128)(2,1)S(1)} %get-tuple-element.229.ahead_kv_ref), channel_id=1, source_target_pairs={{8,0},{12,4},{16,8},{20,12},{24,16},{28,20},{32,24},{36,28},{40,32... | collective-permute-start | bytes 393224 | tf_op jit(solution)/shard_map/ppermute | solution.py:22
  29.9 11.0 %collective-permute-start.3 = (f32[256,256]{1,0:T(8,128)S(1)}, f32[256,256]{1,0:T(8,128)S(1)}, u32[]{:S(2)}, u32[]{:S(2)}) collective-permute-start(f32[256,256]{1,0:T(8,128)S(1)} %get-tuple-element.324), channel_id=1, source_target_pairs={{56,0},{60,4},{0,8},{4,12},{8,16},{12,20},{16,24},{20,28},{24,32},... | collective-permute-start | bytes 786440 | tf_op jit(solution)/shard_map/while/body/eval_jaxpr/ppermute | solution.py:22
  30.0 11.0 %collective-permute-start.2 = (f32[256,256]{1,0:T(8,128)}, f32[256,256]{1,0:T(8,128)S(1)}, u32[]{:S(2)}, u32[]{:S(2)}) collective-permute-start(f32[256,256]{1,0:T(8,128)} %get-tuple-element.323), channel_id=1, source_target_pairs={{8,0},{12,4},{16,8},{20,12},{24,16},{28,20},{32,24},{36,28},{40,32... | collective-permute-start | bytes 786440 | tf_op jit(solution)/shard_map/while/body/eval_jaxpr/ppermute | solution.py:22
  33.9 2.0 %copy-start.4 = (bf16[256,256]{1,0:T(8,128)(2,1)}, bf16[256,256]{1,0:T(8,128)(2,1)S(1)}, u32[]{:S(2)}) copy-start(bf16[256,256]{1,0:T(8,128)(2,1)S(1)} %copy.65.ahead_kv_ref) | copy-start | bytes 393220 | tf_op jit(solution)/shard_map/while
  33.9 15.9 %collective-permute-start = (bf16[256,256]{1,0:T(8,128)(2,1)S(1)}, bf16[256,256]{1,0:T(8,128)(2,1)S(1)}, u32[]{:S(2)}, u32[]{:S(2)}) collective-permute-start(bf16[256,256]{1,0:T(8,128)(2,1)S(1)} %copy.65.ahead_kv_ref), channel_id=1, source_target_pairs={{8,0},{12,4},{16,8},{20,12},{24,16},{28,20},{32,24},{36,28},{40,32... | collective-permute-start | bytes 393224 | tf_op jit(solution)/shard_map/while/body/eval_jaxpr/ppermute | solution.py:22
  35.9 5.0 %copy-start.5 = (bf16[256,256]{1,0:T(8,128)(2,1)}, bf16[256,256]{1,0:T(8,128)(2,1)S(1)}, u32[]{:S(2)}) copy-start(bf16[256,256]{1,0:T(8,128)(2,1)S(1)} %copy.66.behind_kv_ref) | copy-start | bytes 393220 | tf_op jit(solution)/shard_map/while
  35.9 13.9 %collective-permute-start.1 = (bf16[256,256]{1,0:T(8,128)(2,1)S(1)}, bf16[256,256]{1,0:T(8,128)(2,1)S(1)}, u32[]{:S(2)}, u32[]{:S(2)}) collective-permute-start(bf16[256,256]{1,0:T(8,128)(2,1)S(1)} %copy.66.behind_kv_ref), channel_id=1, source_target_pairs={{56,0},{60,4},{0,8},{4,12},{8,16},{12,20},{16,24},{20,28},{24,32},... | collective-permute-start | bytes 393224 | tf_op jit(solution)/shard_map/while/body/eval_jaxpr/ppermute | solution.py:22
  40.9 0.8 copy-start.3
  48.1 1.7 copy-start.2
  49.8 9.3 %collective-permute-start.3 = (f32[256,256]{1,0:T(8,128)S(1)}, f32[256,256]{1,0:T(8,128)S(1)}, u32[]{:S(2)}, u32[]{:S(2)}) collective-permute-start(f32[256,256]{1,0:T(8,128)S(1)} %get-tuple-element.324), channel_id=1, source_target_pairs={{56,0},{60,4},{0,8},{4,12},{8,16},{12,20},{16,24},{20,28},{24,32},... | collective-permute-start | bytes 786440 | tf_op jit(solution)/shard_map/while/body/eval_jaxpr/ppermute | solution.py:22
  50.0 9.2 %collective-permute-start.2 = (f32[256,256]{1,0:T(8,128)}, f32[256,256]{1,0:T(8,128)S(1)}, u32[]{:S(2)}, u32[]{:S(2)}) collective-permute-start(f32[256,256]{1,0:T(8,128)} %get-tuple-element.323), channel_id=1, source_target_pairs={{8,0},{12,4},{16,8},{20,12},{24,16},{28,20},{32,24},{36,28},{40,32... | collective-permute-start | bytes 786440 | tf_op jit(solution)/shard_map/while/body/eval_jaxpr/ppermute | solution.py:22
  53.5 2.0 %copy-start.4 = (bf16[256,256]{1,0:T(8,128)(2,1)}, bf16[256,256]{1,0:T(8,128)(2,1)S(1)}, u32[]{:S(2)}) copy-start(bf16[256,256]{1,0:T(8,128)(2,1)S(1)} %copy.65.ahead_kv_ref) | copy-start | bytes 393220 | tf_op jit(solution)/shard_map/while
  53.5 14.5 %collective-permute-start = (bf16[256,256]{1,0:T(8,128)(2,1)S(1)}, bf16[256,256]{1,0:T(8,128)(2,1)S(1)}, u32[]{:S(2)}, u32[]{:S(2)}) collective-permute-start(bf16[256,256]{1,0:T(8,128)(2,1)S(1)} %copy.65.ahead_kv_ref), channel_id=1, source_target_pairs={{8,0},{12,4},{16,8},{20,12},{24,16},{28,20},{32,24},{36,28},{40,32... | collective-permute-start | bytes 393224 | tf_op jit(solution)/shard_map/while/body/eval_jaxpr/ppermute | solution.py:22
  55.5 3.6 %copy-start.5 = (bf16[256,256]{1,0:T(8,128)(2,1)}, bf16[256,256]{1,0:T(8,128)(2,1)S(1)}, u32[]{:S(2)}) copy-start(bf16[256,256]{1,0:T(8,128)(2,1)S(1)} %copy.66.behind_kv_ref) | copy-start | bytes 393220 | tf_op jit(solution)/shard_map/while
  55.5 12.5 %collective-permute-start.1 = (bf16[256,256]{1,0:T(8,128)(2,1)S(1)}, bf16[256,256]{1,0:T(8,128)(2,1)S(1)}, u32[]{:S(2)}, u32[]{:S(2)}) collective-permute-start(bf16[256,256]{1,0:T(8,128)(2,1)S(1)} %copy.66.behind_kv_ref), channel_id=1, source_target_pairs={{56,0},{60,4},{0,8},{4,12},{8,16},{12,20},{16,24},{20,28},{24,32},... | collective-permute-start | bytes 393224 | tf_op jit(solution)/shard_map/while/body/eval_jaxpr/ppermute | solution.py:22
  59.1 0.8 copy-start.3
  66.3 1.7 copy-start.2
  68.0 7.8 %collective-permute-start.3 = (f32[256,256]{1,0:T(8,128)S(1)}, f32[256,256]{1,0:T(8,128)S(1)}, u32[]{:S(2)}, u32[]{:S(2)}) collective-permute-start(f32[256,256]{1,0:T(8,128)S(1)} %get-tuple-element.324), channel_id=1, source_target_pairs={{56,0},{60,4},{0,8},{4,12},{8,16},{12,20},{16,24},{20,28},{24,32},... | collective-permute-start | bytes 786440 | tf_op jit(solution)/shard_map/while/body/eval_jaxpr/ppermute | solution.py:22
  69.8 6.6 %collective-permute-start.2 = (f32[256,256]{1,0:T(8,128)}, f32[256,256]{1,0:T(8,128)S(1)}, u32[]{:S(2)}, u32[]{:S(2)}) collective-permute-start(f32[256,256]{1,0:T(8,128)} %get-tuple-element.323), channel_id=1, source_target_pairs={{8,0},{12,4},{16,8},{20,12},{24,16},{28,20},{32,24},{36,28},{40,32... | collective-permute-start | bytes 786440 | tf_op jit(solution)/shard_map/while/body/eval_jaxpr/ppermute | solution.py:22
  71.4 1.6 copy-start.4
  71.4 13.8 %collective-permute-start = (bf16[256,256]{1,0:T(8,128)(2,1)S(1)}, bf16[256,256]{1,0:T(8,128)(2,1)S(1)}, u32[]{:S(2)}, u32[]{:S(2)}) collective-permute-start(bf16[256,256]{1,0:T(8,128)(2,1)S(1)} %copy.65.ahead_kv_ref), channel_id=1, source_target_pairs={{8,0},{12,4},{16,8},{20,12},{24,16},{28,20},{32,24},{36,28},{40,32... | collective-permute-start | bytes 393224 | tf_op jit(solution)/shard_map/while/body/eval_jaxpr/ppermute | solution.py:22
  73.0 3.4 %copy-start.5 = (bf16[256,256]{1,0:T(8,128)(2,1)}, bf16[256,256]{1,0:T(8,128)(2,1)S(1)}, u32[]{:S(2)}) copy-start(bf16[256,256]{1,0:T(8,128)(2,1)S(1)} %copy.66.behind_kv_ref) | copy-start | bytes 393220 | tf_op jit(solution)/shard_map/while
  73.0 12.2 %collective-permute-start.1 = (bf16[256,256]{1,0:T(8,128)(2,1)S(1)}, bf16[256,256]{1,0:T(8,128)(2,1)S(1)}, u32[]{:S(2)}, u32[]{:S(2)}) collective-permute-start(bf16[256,256]{1,0:T(8,128)(2,1)S(1)} %copy.66.behind_kv_ref), channel_id=1, source_target_pairs={{56,0},{60,4},{0,8},{4,12},{8,16},{12,20},{16,24},{20,28},{24,32},... | collective-permute-start | bytes 393224 | tf_op jit(solution)/shard_map/while/body/eval_jaxpr/ppermute | solution.py:22
  83.4 1.7 copy-start.2
  85.2 7.7 %collective-permute-start.3 = (f32[256,256]{1,0:T(8,128)S(1)}, f32[256,256]{1,0:T(8,128)S(1)}, u32[]{:S(2)}, u32[]{:S(2)}) collective-permute-start(f32[256,256]{1,0:T(8,128)S(1)} %get-tuple-element.324), channel_id=1, source_target_pairs={{56,0},{60,4},{0,8},{4,12},{8,16},{12,20},{16,24},{20,28},{24,32},... | collective-permute-start | bytes 786440 | tf_op jit(solution)/shard_map/while/body/eval_jaxpr/ppermute | solution.py:22
  87.0 6.6 %collective-permute-start.2 = (f32[256,256]{1,0:T(8,128)}, f32[256,256]{1,0:T(8,128)S(1)}, u32[]{:S(2)}, u32[]{:S(2)}) collective-permute-start(f32[256,256]{1,0:T(8,128)} %get-tuple-element.323), channel_id=1, source_target_pairs={{8,0},{12,4},{16,8},{20,12},{24,16},{28,20},{32,24},{36,28},{40,32... | collective-permute-start | bytes 786440 | tf_op jit(solution)/shard_map/while/body/eval_jaxpr/ppermute | solution.py:22
  88.5 1.7 copy-start.4
  88.5 13.8 %collective-permute-start = (bf16[256,256]{1,0:T(8,128)(2,1)S(1)}, bf16[256,256]{1,0:T(8,128)(2,1)S(1)}, u32[]{:S(2)}, u32[]{:S(2)}) collective-permute-start(bf16[256,256]{1,0:T(8,128)(2,1)S(1)} %copy.65.ahead_kv_ref), channel_id=1, source_target_pairs={{8,0},{12,4},{16,8},{20,12},{24,16},{28,20},{32,24},{36,28},{40,32... | collective-permute-start | bytes 393224 | tf_op jit(solution)/shard_map/while/body/eval_jaxpr/ppermute | solution.py:22
  90.2 3.4 %copy-start.5 = (bf16[256,256]{1,0:T(8,128)(2,1)}, bf16[256,256]{1,0:T(8,128)(2,1)S(1)}, u32[]{:S(2)}) copy-start(bf16[256,256]{1,0:T(8,128)(2,1)S(1)} %copy.66.behind_kv_ref) | copy-start | bytes 393220 | tf_op jit(solution)/shard_map/while
  90.2 12.2 %collective-permute-start.1 = (bf16[256,256]{1,0:T(8,128)(2,1)S(1)}, bf16[256,256]{1,0:T(8,128)(2,1)S(1)}, u32[]{:S(2)}, u32[]{:S(2)}) collective-permute-start(bf16[256,256]{1,0:T(8,128)(2,1)S(1)} %copy.66.behind_kv_ref), channel_id=1, source_target_pairs={{56,0},{60,4},{0,8},{4,12},{8,16},{12,20},{16,24},{20,28},{24,32},... | collective-permute-start | bytes 393224 | tf_op jit(solution)/shard_map/while/body/eval_jaxpr/ppermute | solution.py:22
  92.8 0.7 copy-start.1
  100.6 1.7 copy-start.2
  102.4 7.7 %collective-permute-start.3 = (f32[256,256]{1,0:T(8,128)S(1)}, f32[256,256]{1,0:T(8,128)S(1)}, u32[]{:S(2)}, u32[]{:S(2)}) collective-permute-start(f32[256,256]{1,0:T(8,128)S(1)} %get-tuple-element.324), channel_id=1, source_target_pairs={{56,0},{60,4},{0,8},{4,12},{8,16},{12,20},{16,24},{20,28},{24,32},... | collective-permute-start | bytes 786440 | tf_op jit(solution)/shard_map/while/body/eval_jaxpr/ppermute | solution.py:22
  104.3 6.6 %collective-permute-start.2 = (f32[256,256]{1,0:T(8,128)}, f32[256,256]{1,0:T(8,128)S(1)}, u32[]{:S(2)}, u32[]{:S(2)}) collective-permute-start(f32[256,256]{1,0:T(8,128)} %get-tuple-element.323), channel_id=1, source_target_pairs={{8,0},{12,4},{16,8},{20,12},{24,16},{28,20},{32,24},{36,28},{40,32... | collective-permute-start | bytes 786440 | tf_op jit(solution)/shard_map/while/body/eval_jaxpr/ppermute | solution.py:22
  105.7 1.6 copy-start.4
  105.7 13.9 %collective-permute-start = (bf16[256,256]{1,0:T(8,128)(2,1)S(1)}, bf16[256,256]{1,0:T(8,128)(2,1)S(1)}, u32[]{:S(2)}, u32[]{:S(2)}) collective-permute-start(bf16[256,256]{1,0:T(8,128)(2,1)S(1)} %copy.65.ahead_kv_ref), channel_id=1, source_target_pairs={{8,0},{12,4},{16,8},{20,12},{24,16},{28,20},{32,24},{36,28},{40,32... | collective-permute-start | bytes 393224 | tf_op jit(solution)/shard_map/while/body/eval_jaxpr/ppermute | solution.py:22
  107.3 3.6 %copy-start.5 = (bf16[256,256]{1,0:T(8,128)(2,1)}, bf16[256,256]{1,0:T(8,128)(2,1)S(1)}, u32[]{:S(2)}) copy-start(bf16[256,256]{1,0:T(8,128)(2,1)S(1)} %copy.66.behind_kv_ref) | copy-start | bytes 393220 | tf_op jit(solution)/shard_map/while
  107.3 12.3 %collective-permute-start.1 = (bf16[256,256]{1,0:T(8,128)(2,1)S(1)}, bf16[256,256]{1,0:T(8,128)(2,1)S(1)}, u32[]{:S(2)}, u32[]{:S(2)}) collective-permute-start(bf16[256,256]{1,0:T(8,128)(2,1)S(1)} %copy.66.behind_kv_ref), channel_id=1, source_target_pairs={{56,0},{60,4},{0,8},{4,12},{8,16},{12,20},{16,24},{20,28},{24,32},... | collective-permute-start | bytes 393224 | tf_op jit(solution)/shard_map/while/body/eval_jaxpr/ppermute | solution.py:22
  110.0 0.8 copy-start.1
  117.9 1.7 copy-start.2
  119.7 7.7 %collective-permute-start.3 = (f32[256,256]{1,0:T(8,128)S(1)}, f32[256,256]{1,0:T(8,128)S(1)}, u32[]{:S(2)}, u32[]{:S(2)}) collective-permute-start(f32[256,256]{1,0:T(8,128)S(1)} %get-tuple-element.324), channel_id=1, source_target_pairs={{56,0},{60,4},{0,8},{4,12},{8,16},{12,20},{16,24},{20,28},{24,32},... | collective-permute-start | bytes 786440 | tf_op jit(solution)/shard_map/while/body/eval_jaxpr/ppermute | solution.py:22
  121.8 6.6 %collective-permute-start.2 = (f32[256,256]{1,0:T(8,128)}, f32[256,256]{1,0:T(8,128)S(1)}, u32[]{:S(2)}, u32[]{:S(2)}) collective-permute-start(f32[256,256]{1,0:T(8,128)} %get-tuple-element.323), channel_id=1, source_target_pairs={{8,0},{12,4},{16,8},{20,12},{24,16},{28,20},{32,24},{36,28},{40,32... | collective-permute-start | bytes 786440 | tf_op jit(solution)/shard_map/while/body/eval_jaxpr/ppermute | solution.py:22
  123.0 1.5 copy-start.4
  123.0 14.1 %collective-permute-start = (bf16[256,256]{1,0:T(8,128)(2,1)S(1)}, bf16[256,256]{1,0:T(8,128)(2,1)S(1)}, u32[]{:S(2)}, u32[]{:S(2)}) collective-permute-start(bf16[256,256]{1,0:T(8,128)(2,1)S(1)} %copy.65.ahead_kv_ref), channel_id=1, source_target_pairs={{8,0},{12,4},{16,8},{20,12},{24,16},{28,20},{32,24},{36,28},{40,32... | collective-permute-start | bytes 393224 | tf_op jit(solution)/shard_map/while/body/eval_jaxpr/ppermute | solution.py:22
  124.5 3.9 %copy-start.5 = (bf16[256,256]{1,0:T(8,128)(2,1)}, bf16[256,256]{1,0:T(8,128)(2,1)S(1)}, u32[]{:S(2)}) copy-start(bf16[256,256]{1,0:T(8,128)(2,1)S(1)} %copy.66.behind_kv_ref) | copy-start | bytes 393220 | tf_op jit(solution)/shard_map/while
  124.5 12.6 %collective-permute-start.1 = (bf16[256,256]{1,0:T(8,128)(2,1)S(1)}, bf16[256,256]{1,0:T(8,128)(2,1)S(1)}, u32[]{:S(2)}, u32[]{:S(2)}) collective-permute-start(bf16[256,256]{1,0:T(8,128)(2,1)S(1)} %copy.66.behind_kv_ref), channel_id=1, source_target_pairs={{56,0},{60,4},{0,8},{4,12},{8,16},{12,20},{16,24},{20,28},{24,32},... | collective-permute-start | bytes 393224 | tf_op jit(solution)/shard_map/while/body/eval_jaxpr/ppermute | solution.py:22
  127.3 1.0 copy-start.1
  135.4 1.7 copy-start.2
  137.2 7.9 %collective-permute-start.8 = (f32[256,256]{1,0:T(8,128)S(1)}, f32[256,256]{1,0:T(8,128)S(1)}, u32[]{:S(2)}, u32[]{:S(2)}) collective-permute-start(f32[256,256]{1,0:T(8,128)S(1)} %get-tuple-element.194), channel_id=1, source_target_pairs={{56,0},{60,4},{0,8},{4,12},{8,16},{12,20},{16,24},{20,28},{24,32},... | collective-permute-start | bytes 786440 | tf_op jit(solution)/shard_map/ppermute | solution.py:22
  138.8 8.8 %collective-permute-start.7 = (f32[256,256]{1,0:T(8,128)}, f32[256,256]{1,0:T(8,128)S(1)}, u32[]{:S(2)}, u32[]{:S(2)}) collective-permute-start(f32[256,256]{1,0:T(8,128)} %get-tuple-element.193), channel_id=1, source_target_pairs={{8,0},{12,4},{16,8},{20,12},{24,16},{28,20},{32,24},{36,28},{40,32... | collective-permute-start | bytes 786440 | tf_op jit(solution)/shard_map/ppermute | solution.py:22
  145.1 2.5 %copy-start.10 = (f32[256,256]{1,0:T(8,128)}, f32[256,256]{1,0:T(8,128)S(1)}, u32[]{:S(2)}) copy-start(f32[256,256]{1,0:T(8,128)S(1)} %collective-permute-done.8.behind_in_ref) | copy-start | bytes 786436
  154.4 6.6 %collective-permute-start.9 = (f32[256,256]{1,0:T(8,128)}, f32[256,256]{1,0:T(8,128)S(1)}, u32[]{:S(2)}, u32[]{:S(2)}) collective-permute-start(f32[256,256]{1,0:T(8,128)} %get-tuple-element.196), channel_id=1, source_target_pairs={{8,0},{12,4},{16,8},{20,12},{24,16},{28,20},{32,24},{36,28},{40,32... | collective-permute-start | bytes 786440 | tf_op jit(solution)/shard_map/ppermute | solution.py:22
  156.4 7.8 %collective-permute-start.10 = (f32[256,256]{1,0:T(8,128)}, f32[256,256]{1,0:T(8,128)S(1)}, u32[]{:S(2)}, u32[]{:S(2)}) collective-permute-start(f32[256,256]{1,0:T(8,128)} %get-tuple-element.197), channel_id=1, source_target_pairs={{56,0},{60,4},{0,8},{4,12},{8,16},{12,20},{16,24},{20,28},{24,32},... | collective-permute-start | bytes 786440 | tf_op jit(solution)/shard_map/ppermute | solution.py:22
  164.2 8.0 %collective-permute-start.11 = (f32[256,256]{1,0:T(8,128)S(1)}, f32[256,256]{1,0:T(8,128)S(1)}, u32[]{:S(2)}, u32[]{:S(2)}) collective-permute-start(f32[256,256]{1,0:T(8,128)S(1)} %broadcast_select_fusion), channel_id=1, source_target_pairs={{0,4},{4,0},{8,12},{12,8},{16,20},{20,16},{24,28},{28,24},{32,36},... | collective-permute-start | bytes 786440 | tf_op jit(solution)/shard_map/ppermute | solution.py:27
  (8 other events, 5.6 us)

commit v8 on v4

--- a/solution.py
+++ b/solution.py
@@ -17,6 +17,17 @@
         for z in range(z_count)
         for h in range(Y_HI)
     ]
+    return lax.ppermute(value, "ctx", pairs)
+
+
+def to_owner(value, ctx_count, ring_half):
+    z_count = ctx_count // Y_HI
+    pairs = []
+    for z in range(z_count):
+        for h in range(Y_HI):
+            first = (h == 0) == (ring_half == 0)
+            target = Y_HI * ((z - 1) % z_count) if first else Y_HI * ((z + 1) % z_count) + 1
+            pairs.append((Y_HI * z + h, target))
     return lax.ppermute(value, "ctx", pairs)
 
 
@@ -133,11 +144,11 @@
     behind_received = along_z(behind_pending, ctx_count, -1)
     query_term, ahead_term, behind_term = terms(ahead_kv, behind_kv, z_count - 1)
     query_acc = query_acc + query_term
-    ahead_total = along_z(ahead_received + ahead_term, ctx_count, 1)
-    behind_total = along_z(behind_received + behind_term, ctx_count, -1)
-    own_total = jnp.where(y_hi == 0, ahead_total, behind_total)
-    other_total = jnp.where(y_hi == 0, behind_total, ahead_total)
-    summed = own_total + from_partner(other_total, ctx_count)
+    ahead_final = ahead_received + ahead_term
+    behind_final = behind_received + behind_term
+    same_ring = jnp.where(y_hi == 0, ahead_final, behind_final)
+    other_ring = jnp.where(y_hi == 0, behind_final, ahead_final)
+    summed = to_owner(same_ring, ctx_count, 0) + to_owner(other_ring, ctx_count, 1)
     logit_scale = 1.0 / math.sqrt(HEAD_SIZE)
     query_grad = (query_acc * logit_scale).reshape(tok_rows, col_width).astype(jnp.bfloat16)
     key_gradient = (summed[:, :HEAD_SIZE] * logit_scale).astype(jnp.bfloat16)

time: 141 us -> 139 us (0.986)
  waiting for transfers between devices: 19.1 us -> 13 us
  matrix products: 39.2 us -> 43.7 us
    ppermute x2 -> x1, waiting for transfers between devices: 6.4 us -> 0.01 us  [from_partner(): return lax.ppermute(value, 'ctx', pairs)]
    ppermute x0 -> x2, waiting for transfers between devices: none -> 5.76 us  [to_owner(): return lax.ppermute(value, 'ctx', pairs)]
    ppermute x30 -> x28, waiting for transfers between devices: 12.7 us -> 7.23 us  [along_z(): return lax.ppermute(value, 'ctx', pairs)]
    ppermute x30 -> x28, starting transfers between devices: 43.4 us -> 40.9 us  [along_z(): return lax.ppermute(value, 'ctx', pairs)]
    ppermute x0 -> x2, starting transfers between devices: none -> 1.92 us  [to_owner(): return lax.ppermute(value, 'ctx', pairs)]
    dot_general x8, matrix products: 3.84 us -> 5.43 us  [contract(): jnp.einsum('gij,jd->igd', dscore, keys_part, preferred_element_type=jnp.f...]
    dot_general x8, matrix products: 6.3 us -> 7.88 us  [contract(): jnp.einsum('gij,igd->jd', dscore, queries, preferred_element_type=jnp.flo...]
    ppermute x2 -> x1, starting transfers between devices: 3.67 us -> 3.28 us  [from_partner(): return lax.ppermute(value, 'ctx', pairs)]
  transfers between devices with their start and end apart: 33 -> 32, of which waited for: 7 -> 4; matrix products, arithmetic and copies ran while one was open for 45% -> 46% of each run, Pallas kernels for 0% -> 0%
where the time goes in v8:
time: 139 us; the launch traced here: 138 us
  starting transfers between devices  49.6 us (36%)
  matrix products  43.7 us (31%)
  local copies, waits for them, and re-layouts  18.2 us (13%)
  waiting for transfers between devices  13 us (9%)
  other arithmetic  11.2 us (8%)
    ppermute x28, starting transfers between devices, along_z(): return lax.ppermute(value, 'ctx', pairs)  40.9 us
    dot_general x8, matrix products, contract(): jnp.einsum('igd,jd->gij', out_grads, values_part, preferred_element_type=...  12.6 us
    dot_general x8, matrix products, contract(): jnp.einsum('gij,igd->jd', probabilities.astype(jnp.bfloat16), out_grads,...  10.3 us
    dot_general x8, matrix products, contract(): jnp.einsum('gij,igd->jd', dscore, queries, preferred_element_type=jnp.flo...  7.88 us
    dot_general x8, matrix products, contract(): jnp.einsum('igd,jd->gij', queries, keys_part, preferred_element_type=jnp....  7.49 us
    ppermute x28, waiting for transfers between devices, along_z(): return lax.ppermute(value, 'ctx', pairs)  7.23 us
    ppermute x2, waiting for transfers between devices, to_owner(): return lax.ppermute(value, 'ctx', pairs)  5.76 us
    dot_general x8, matrix products, contract(): jnp.einsum('gij,jd->igd', dscore, keys_part, preferred_element_type=jnp.f...  5.43 us
  transfers between devices with their start and end apart: 32, of which 4 were waited for; matrix products, arithmetic and copies ran while one was open for 46% of the time, Pallas kernels for 0%

profile of v8, /device:TPU:4, one launch (start us, length us, event | category | flops | bytes accessed | tf_op | source)
XLA Modules:
  0.0 137.7 jit_solution(1901505560115003875)
XLA Ops:
  0.6 0.9 constant_dynamic-update-slice_fusion.3
  1.5 0.9 constant_dynamic-update-slice_fusion.2
  2.4 3.3 %collective-permute-start.4 = (bf16[256,256]{1,0:T(8,128)(2,1)S(1)}, bf16[256,256]{1,0:T(8,128)(2,1)S(1)}, u32[]{:S(2)}, u32[]{:S(2)}) collective-permute-start(bf16[256,256]{1,0:T(8,128)(2,1)S(1)} %constant_dynamic-update-slice_fusion.2), channel_id=1, source_target_pairs={{0,4},{4,0},{8,12},{12,8},{16,20},{20,16},{24,28},{28,24},{32,36},... | collective-permute-start | bytes 393224 | tf_op jit(solution)/shard_map/ppermute | solution.py:36
  5.7 1.9 %copy.137 = bf16[8,4,8,1024]{3,2,0,1:T(8,128)(2,1)} copy(bf16[8,4,8,1024]{3,2,1,0:T(8,128)(2,1)} %bitcast.204) | data formatting | bytes 1048576 | tf_op jit(solution)/shard_map/reshape | solution.py:81
  7.5 3.5 %all-to-all-start = ((bf16[64,4,1024]{2,0,1:T(8,128)(2,1)}), bf16[64,4,1024]{2,0,1:T(8,128)(2,1)S(1)}, u32[]{:S(2)}, u32[]{:S(2)}) async-start(bf16[64,4,1024]{2,0,1:T(8,128)(2,1)} %bitcast.157), calls=%async_computation | async-start | bytes 1048576 | tf_op jit(solution)/shard_map/all_to_all | solution.py:82
  13.2 1.2 copy.79
  14.4 1.2 copy.83
  16.0 1.2 fusion.45
  17.3 2.0 %collective-permute-start.6 = (bf16[256,256]{1,0:T(8,128)(2,1)S(1)}, bf16[256,256]{1,0:T(8,128)(2,1)S(1)}, u32[]{:S(2)}, u32[]{:S(2)}) collective-permute-start(bf16[256,256]{1,0:T(8,128)(2,1)S(1)} %get-tuple-element.611), channel_id=1, source_target_pairs={{56,0},{60,4},{0,8},{4,12},{8,16},{12,20},{16,24},{20,28},{24,32},... | collective-permute-start | bytes 393224 | tf_op jit(solution)/shard_map/ppermute | solution.py:20
  19.3 4.0 %collective-permute-start.5 = (bf16[256,256]{1,0:T(8,128)(2,1)S(1)}, bf16[256,256]{1,0:T(8,128)(2,1)S(1)}, u32[]{:S(2)}, u32[]{:S(2)}) collective-permute-start(bf16[256,256]{1,0:T(8,128)(2,1)S(1)} %get-tuple-element.612), channel_id=1, source_target_pairs={{8,0},{12,4},{16,8},{20,12},{24,16},{28,20},{32,24},{36,28},{40,32... | collective-permute-start | bytes 393224 | tf_op jit(solution)/shard_map/ppermute | solution.py:20
  23.3 2.7 %fusion.60 = f32[512,256,8]{1,0,2:T(8,128)} fusion(bf16[256,8,128]{0,2,1:T(8,128)(2,1)S(1)} %bitcast.194, bf16[256,256]{1,0:T(8,128)(2,1)S(1)} %get-tuple-element.612, bf16[256,256]{1,0:T(8,128)(2,1)S(1)} %get-tuple-element.611), kind=kOutput, calls=%fused_computation.116 | convolution fusion | flops 268697600 | bytes 4980736 | tf_op jit(solution)/shard_map/igd,jd->gij/dot_general | solution.py:54
  26.8 3.4 %fusion.39 = f32[512,128]{0,1:T(8,128)S(1)} fusion(bf16[256,8,128]{0,2,1:T(8,128)(2,1)S(1)} %copy.90, f32[512,256,8]{1,0,2:T(8,128)} %fusion.60, f32[8,256]{1,0:T(8,128)S(1)} %copy-done.7, pred[256,512]{0,1:T(8,128)(4,1)} %get-tuple-element.614), kind=kOutput, calls=%fused_computation.76 | convolution fusion | flops 272629760 | bytes 5120000 | tf_op jit(solution)/shard_map/gij,igd->jd/dot_general | solution.py:64
  30.3 1.4 %fusion.28 = bf16[8,256,512]{1,2,0:T(8,128)(2,1)S(1)} fusion(f32[512,256,8]{1,0,2:T(8,128)S(1)} %copy-done.1, f32[8,256]{1,0:T(8,128)S(1)} %copy.85, f32[8,256]{1,0:T(8,128)S(1)} %copy-done.7, pred[256,512]{0,1:T(8,128)(4,1)S(1)} %copy-done.6, bf16[256,8,128]{2,1,0:T(8,128)(2,1)S(1)} %bitcast.199, bf16[256,256]{1,0:T(8,128)(2,1)S(1)} %get-tuple-element.611, ...), kind=kOutput, calls=%fused_computation.64 | convolution fusion | flops 274989056 | bytes 7225344 | tf_op jit(solution)/shard_map/igd,jd->gij/dot_general | solution.py:58
  32.2 0.8 convolution_bitcast_fusion.5
  33.1 0.9 pad_maximum_fusion.2
  33.9 75.8 %while.26 = (s32[]{:T(128)}, bf16[256,256]{1,0:T(8,128)(2,1)S(1)}, bf16[256,256]{1,0:T(8,128)(2,1)S(1)}, f32[256,8,128]{0,2,1:T(8,128)S(1)}, f32[256,256]{0,1:T(...) while((s32[]{:T(128)}, bf16[256,256]{1,0:T(8,128)(2,1)S(1)}, ...), condition=%wide.region_2.4_spmd.clone.clone, body=%wide.region_1.3_spmd.clone.clone.sunk | while | flops 1353987712 | bytes 32291700 | solution.py:137
  34.1 2.0 %collective-permute-start = (bf16[256,256]{1,0:T(8,128)(2,1)S(1)}, bf16[256,256]{1,0:T(8,128)(2,1)S(1)}, u32[]{:S(2)}, u32[]{:S(2)}) collective-permute-start(bf16[256,256]{1,0:T(8,128)(2,1)S(1)} %copy.149), channel_id=1, source_target_pairs={{8,0},{12,4},{16,8},{20,12},{24,16},{28,20},{32,24},{36,28},{40,32... | collective-permute-start | bytes 393224 | tf_op jit(solution)/shard_map/while/body/eval_jaxpr/ppermute | solution.py:20
  36.3 3.1 %collective-permute-start.3 = (f32[256,256]{0,1:T(8,128)}, f32[256,256]{0,1:T(8,128)S(1)}, u32[]{:S(2)}, u32[]{:S(2)}) collective-permute-start(f32[256,256]{0,1:T(8,128)} %get-tuple-element.747), channel_id=1, source_target_pairs={{8,0},{12,4},{16,8},{20,12},{24,16},{28,20},{32,24},{36,28},{40,32... | collective-permute-start | bytes 786440 | tf_op jit(solution)/shard_map/while/body/eval_jaxpr/ppermute | solution.py:20
  41.5 1.0 fusion.114
  42.5 1.4 %fusion.112 = bf16[8,256,512]{1,2,0:T(8,128)(2,1)S(1)} fusion(f32[512,256,8]{1,0,2:T(8,128)S(1)} %fusion.110, bf16[256,8,128]{0,2,1:T(8,128)(2,1)S(1)} %copy-done.3, f32[8,256]{1,0:T(8,128)S(1)} %get-tuple-element.774, f32[8,256]{1,0:T(8,128)S(1)} %get-tuple-element.772, pred[256,512]{0,1:T(8,128)(4,1)S(1)} %fusion.111, ...), kind=kOutput, calls=%fused_computation.6.clone.1 | convolution fusion | flops 274726912 | bytes 7094272 | tf_op jit(solution)/shard_map/while/body/eval_jaxpr/igd,jd->gij/dot_general | solution.py:58
  44.4 0.8 convolution_bitcast_fusion.7
  45.2 2.7 %collective-permute-done.2 = f32[256,256]{0,1:T(8,128)S(1)} collective-permute-done((f32[256,256]{0,1:T(8,128)}, f32[256,256]{0,1:T(8,128)S(1)}, u32[]{:S(2)}, u32[]{:S(2)}) %collective-permute-start.2) | collective-permute-done | bytes 262176 | tf_op jit(solution)/shard_map/while/body/eval_jaxpr/ppermute | solution.py:20
  47.9 0.9 fusion.115
  49.4 1.7 %collective-permute-start.1 = (bf16[256,256]{1,0:T(8,128)(2,1)S(1)}, bf16[256,256]{1,0:T(8,128)(2,1)S(1)}, u32[]{:S(2)}, u32[]{:S(2)}) collective-permute-start(bf16[256,256]{1,0:T(8,128)(2,1)S(1)} %copy.150), channel_id=1, source_target_pairs={{56,0},{60,4},{0,8},{4,12},{8,16},{12,20},{16,24},{20,28},{24,32},... | collective-permute-start | bytes 393224 | tf_op jit(solution)/shard_map/while/body/eval_jaxpr/ppermute | solution.py:20
  51.1 3.1 %collective-permute-start.3 = (f32[256,256]{0,1:T(8,128)}, f32[256,256]{0,1:T(8,128)S(1)}, u32[]{:S(2)}, u32[]{:S(2)}) collective-permute-start(f32[256,256]{0,1:T(8,128)} %get-tuple-element.747), channel_id=1, source_target_pairs={{8,0},{12,4},{16,8},{20,12},{24,16},{28,20},{32,24},{36,28},{40,32... | collective-permute-start | bytes 786440 | tf_op jit(solution)/shard_map/while/body/eval_jaxpr/ppermute | solution.py:20
  56.3 1.0 fusion.114
  57.3 1.4 %fusion.112 = bf16[8,256,512]{1,2,0:T(8,128)(2,1)S(1)} fusion(f32[512,256,8]{1,0,2:T(8,128)S(1)} %fusion.110, bf16[256,8,128]{0,2,1:T(8,128)(2,1)S(1)} %copy-done.3, f32[8,256]{1,0:T(8,128)S(1)} %get-tuple-element.774, f32[8,256]{1,0:T(8,128)S(1)} %get-tuple-element.772, pred[256,512]{0,1:T(8,128)(4,1)S(1)} %fusion.111, ...), kind=kOutput, calls=%fused_computation.6.clone.1 | convolution fusion | flops 274726912 | bytes 7094272 | tf_op jit(solution)/shard_map/while/body/eval_jaxpr/igd,jd->gij/dot_general | solution.py:58
  59.2 0.8 convolution_bitcast_fusion.7
  60.1 0.9 fusion.115
  61.0 2.0 %collective-permute-start = (bf16[256,256]{1,0:T(8,128)(2,1)S(1)}, bf16[256,256]{1,0:T(8,128)(2,1)S(1)}, u32[]{:S(2)}, u32[]{:S(2)}) collective-permute-start(bf16[256,256]{1,0:T(8,128)(2,1)S(1)} %copy.149), channel_id=1, source_target_pairs={{8,0},{12,4},{16,8},{20,12},{24,16},{28,20},{32,24},{36,28},{40,32... | collective-permute-start | bytes 393224 | tf_op jit(solution)/shard_map/while/body/eval_jaxpr/ppermute | solution.py:20
  63.5 3.0 %collective-permute-start.3 = (f32[256,256]{0,1:T(8,128)}, f32[256,256]{0,1:T(8,128)S(1)}, u32[]{:S(2)}, u32[]{:S(2)}) collective-permute-start(f32[256,256]{0,1:T(8,128)} %get-tuple-element.747), channel_id=1, source_target_pairs={{8,0},{12,4},{16,8},{20,12},{24,16},{28,20},{32,24},{36,28},{40,32... | collective-permute-start | bytes 786440 | tf_op jit(solution)/shard_map/while/body/eval_jaxpr/ppermute | solution.py:20
  68.5 1.0 fusion.114
  69.5 1.4 %fusion.112 = bf16[8,256,512]{1,2,0:T(8,128)(2,1)S(1)} fusion(f32[512,256,8]{1,0,2:T(8,128)S(1)} %fusion.110, bf16[256,8,128]{0,2,1:T(8,128)(2,1)S(1)} %copy-done.3, f32[8,256]{1,0:T(8,128)S(1)} %get-tuple-element.774, f32[8,256]{1,0:T(8,128)S(1)} %get-tuple-element.772, pred[256,512]{0,1:T(8,128)(4,1)S(1)} %fusion.111, ...), kind=kOutput, calls=%fused_computation.6.clone.1 | convolution fusion | flops 274726912 | bytes 7094272 | tf_op jit(solution)/shard_map/while/body/eval_jaxpr/igd,jd->gij/dot_general | solution.py:58
  72.2 0.9 fusion.115
  73.1 2.1 %collective-permute-start = (bf16[256,256]{1,0:T(8,128)(2,1)S(1)}, bf16[256,256]{1,0:T(8,128)(2,1)S(1)}, u32[]{:S(2)}, u32[]{:S(2)}) collective-permute-start(bf16[256,256]{1,0:T(8,128)(2,1)S(1)} %copy.149), channel_id=1, source_target_pairs={{8,0},{12,4},{16,8},{20,12},{24,16},{28,20},{32,24},{36,28},{40,32... | collective-permute-start | bytes 393224 | tf_op jit(solution)/shard_map/while/body/eval_jaxpr/ppermute | solution.py:20
  75.8 2.9 %collective-permute-start.3 = (f32[256,256]{0,1:T(8,128)}, f32[256,256]{0,1:T(8,128)S(1)}, u32[]{:S(2)}, u32[]{:S(2)}) collective-permute-start(f32[256,256]{0,1:T(8,128)} %get-tuple-element.747), channel_id=1, source_target_pairs={{8,0},{12,4},{16,8},{20,12},{24,16},{28,20},{32,24},{36,28},{40,32... | collective-permute-start | bytes 786440 | tf_op jit(solution)/shard_map/while/body/eval_jaxpr/ppermute | solution.py:20
  80.7 1.0 fusion.114
  81.7 1.4 %fusion.112 = bf16[8,256,512]{1,2,0:T(8,128)(2,1)S(1)} fusion(f32[512,256,8]{1,0,2:T(8,128)S(1)} %fusion.110, bf16[256,8,128]{0,2,1:T(8,128)(2,1)S(1)} %copy-done.3, f32[8,256]{1,0:T(8,128)S(1)} %get-tuple-element.774, f32[8,256]{1,0:T(8,128)S(1)} %get-tuple-element.772, pred[256,512]{0,1:T(8,128)(4,1)S(1)} %fusion.111, ...), kind=kOutput, calls=%fused_computation.6.clone.1 | convolution fusion | flops 274726912 | bytes 7094272 | tf_op jit(solution)/shard_map/while/body/eval_jaxpr/igd,jd->gij/dot_general | solution.py:58
  83.6 0.8 convolution_bitcast_fusion.7
  84.4 0.9 fusion.115
  85.3 2.1 %collective-permute-start = (bf16[256,256]{1,0:T(8,128)(2,1)S(1)}, bf16[256,256]{1,0:T(8,128)(2,1)S(1)}, u32[]{:S(2)}, u32[]{:S(2)}) collective-permute-start(bf16[256,256]{1,0:T(8,128)(2,1)S(1)} %copy.149), channel_id=1, source_target_pairs={{8,0},{12,4},{16,8},{20,12},{24,16},{28,20},{32,24},{36,28},{40,32... | collective-permute-start | bytes 393224 | tf_op jit(solution)/shard_map/while/body/eval_jaxpr/ppermute | solution.py:20
  87.6 0.8 collective-permute-start.2
  88.4 2.5 %collective-permute-start.3 = (f32[256,256]{0,1:T(8,128)}, f32[256,256]{0,1:T(8,128)S(1)}, u32[]{:S(2)}, u32[]{:S(2)}) collective-permute-start(f32[256,256]{0,1:T(8,128)} %get-tuple-element.747), channel_id=1, source_target_pairs={{8,0},{12,4},{16,8},{20,12},{24,16},{28,20},{32,24},{36,28},{40,32... | collective-permute-start | bytes 786440 | tf_op jit(solution)/shard_map/while/body/eval_jaxpr/ppermute | solution.py:20
  92.9 1.0 fusion.114
  93.9 1.4 %fusion.112 = bf16[8,256,512]{1,2,0:T(8,128)(2,1)S(1)} fusion(f32[512,256,8]{1,0,2:T(8,128)S(1)} %fusion.110, bf16[256,8,128]{0,2,1:T(8,128)(2,1)S(1)} %copy-done.3, f32[8,256]{1,0:T(8,128)S(1)} %get-tuple-element.774, f32[8,256]{1,0:T(8,128)S(1)} %get-tuple-element.772, pred[256,512]{0,1:T(8,128)(4,1)S(1)} %fusion.111, ...), kind=kOutput, calls=%fused_computation.6.clone.1 | convolution fusion | flops 274726912 | bytes 7094272 | tf_op jit(solution)/shard_map/while/body/eval_jaxpr/igd,jd->gij/dot_general | solution.py:58
  95.8 0.8 convolution_bitcast_fusion.7
  96.6 0.9 fusion.115
  97.5 2.1 %collective-permute-start = (bf16[256,256]{1,0:T(8,128)(2,1)S(1)}, bf16[256,256]{1,0:T(8,128)(2,1)S(1)}, u32[]{:S(2)}, u32[]{:S(2)}) collective-permute-start(bf16[256,256]{1,0:T(8,128)(2,1)S(1)} %copy.149), channel_id=1, source_target_pairs={{8,0},{12,4},{16,8},{20,12},{24,16},{28,20},{32,24},{36,28},{40,32... | collective-permute-start | bytes 393224 | tf_op jit(solution)/shard_map/while/body/eval_jaxpr/ppermute | solution.py:20
  99.8 0.9 collective-permute-start.2
  100.7 2.4 %collective-permute-start.3 = (f32[256,256]{0,1:T(8,128)}, f32[256,256]{0,1:T(8,128)S(1)}, u32[]{:S(2)}, u32[]{:S(2)}) collective-permute-start(f32[256,256]{0,1:T(8,128)} %get-tuple-element.747), channel_id=1, source_target_pairs={{8,0},{12,4},{16,8},{20,12},{24,16},{28,20},{32,24},{36,28},{40,32... | collective-permute-start | bytes 786440 | tf_op jit(solution)/shard_map/while/body/eval_jaxpr/ppermute | solution.py:20
  105.1 1.0 fusion.114
  106.1 1.4 %fusion.112 = bf16[8,256,512]{1,2,0:T(8,128)(2,1)S(1)} fusion(f32[512,256,8]{1,0,2:T(8,128)S(1)} %fusion.110, bf16[256,8,128]{0,2,1:T(8,128)(2,1)S(1)} %copy-done.3, f32[8,256]{1,0:T(8,128)S(1)} %get-tuple-element.774, f32[8,256]{1,0:T(8,128)S(1)} %get-tuple-element.772, pred[256,512]{0,1:T(8,128)(4,1)S(1)} %fusion.111, ...), kind=kOutput, calls=%fused_computation.6.clone.1 | convolution fusion | flops 274726912 | bytes 7094272 | tf_op jit(solution)/shard_map/while/body/eval_jaxpr/igd,jd->gij/dot_general | solution.py:58
  108.8 0.9 fusion.115
  110.8 0.9 fusion.42
  111.7 2.8 %fusion.24 = bf16[8,256,512]{1,2,0:T(8,128)(2,1)} fusion(f32[512,256,8]{1,0,2:T(8,128)S(1)} %fusion.59, f32[8,256]{1,0:T(8,128)S(1)} %get-tuple-element.804, f32[8,256]{1,0:T(8,128)S(1)} %get-tuple-element.805, pred[256,512]{0,1:T(8,128)(4,1)S(1)} %copy-done.5, bf16[256,8,128]{2,1,0:T(8,128)(2,1)S(1)} %bitcast.200, ...), kind=kOutput, calls=%fused_computation.58 | convolution fusion | flops 274726912 | bytes 7094272 | tf_op jit(solution)/shard_map/igd,jd->gij/dot_general | solution.py:58
  114.4 1.1 copy.104
  115.5 1.1 copy.98
  116.6 2.1 %collective-permute-start.7 = (f32[256,256]{1,0:T(8,128)S(1)}, f32[256,256]{1,0:T(8,128)S(1)}, u32[]{:S(2)}, u32[]{:S(2)}) collective-permute-start(f32[256,256]{1,0:T(8,128)S(1)} %copy.98), channel_id=1, source_target_pairs={{8,0},{12,4},{16,8},{20,12},{24,16},{28,20},{32,24},{36,28},{40,32... | collective-permute-start | bytes 786440 | tf_op jit(solution)/shard_map/ppermute | solution.py:20
  118.7 2.1 %convolution_bitcast_fusion.2 = f32[256,8,128]{0,2,1:T(8,128)S(1)} fusion(bf16[8,256,512]{1,2,0:T(8,128)(2,1)} %fusion.24, bf16[512,256]{1,0:T(8,128)(2,1)S(1)} %constant_dynamic-update-slice_fusion.4), kind=kOutput, calls=%fused_computation.74 | convolution fusion | flops 268435456 | bytes 3276800 | tf_op jit(solution)/shard_map/gij,jd->igd/dot_general | solution.py:62
  120.8 2.3 %convolution_bitcast_fusion.4 = f32[512,128]{1,0:T(8,128)S(1)} fusion(bf16[8,256,512]{1,2,0:T(8,128)(2,1)} %fusion.24, bf16[256,8,128]{0,2,1:T(8,128)(2,1)S(1)} %get-tuple-element.781), kind=kOutput, calls=%fused_computation.78 | convolution fusion | flops 268435456 | bytes 2883584 | tf_op jit(solution)/shard_map/gij,igd->jd/dot_general | solution.py:63
  123.1 4.4 %collective-permute-done.8 = f32[256,256]{1,0:T(8,128)S(1)} collective-permute-done((f32[256,256]{1,0:T(8,128)S(1)}, f32[256,256]{1,0:T(8,128)S(1)}, u32[]{:S(2)}, u32[]{:S(2)}) %collective-permute-start.8) | collective-permute-done | bytes 262176 | tf_op jit(solution)/shard_map/ppermute | solution.py:20
  127.6 1.8 %collective-permute-start.9 = (f32[256,256]{1,0:T(8,128)S(1)}, f32[256,256]{1,0:T(8,128)S(1)}, u32[]{:S(2)}, u32[]{:S(2)}) collective-permute-start(f32[256,256]{1,0:T(8,128)S(1)} %get-tuple-element.608), channel_id=1, source_target_pairs={{0,56},{4,12},{8,0},{12,20},{16,8},{20,28},{24,16},{28,36},{32,24}... | collective-permute-start | bytes 786440 | tf_op jit(solution)/shard_map/ppermute | solution.py:31
  129.6 1.0 copy.105
  130.6 5.8 %collective-permute-done.10 = f32[256,256]{1,0:T(8,128)S(1)} collective-permute-done((f32[256,256]{1,0:T(8,128)S(1)}, f32[256,256]{1,0:T(8,128)S(1)}, u32[]{:S(2)}, u32[]{:S(2)}) %collective-permute-start.10) | collective-permute-done | bytes 262176 | tf_op jit(solution)/shard_map/ppermute | solution.py:31
  (207 shorter events, 24.8 us)
Async XLA Ops:
  0.6 10.8 %copy-start = (s32[32,32]{1,0:T(8,128)S(1)}, s32[32,32]{1,0:T(8,128)}, u32[]{:S(2)}) copy-start(s32[32,32]{1,0:T(8,128)} %param.17) | copy-start | bytes 12292
  2.4 14.9 %collective-permute-start.4 = (bf16[256,256]{1,0:T(8,128)(2,1)S(1)}, bf16[256,256]{1,0:T(8,128)(2,1)S(1)}, u32[]{:S(2)}, u32[]{:S(2)}) collective-permute-start(bf16[256,256]{1,0:T(8,128)(2,1)S(1)} %constant_dynamic-update-slice_fusion.2), channel_id=1, source_target_pairs={{0,4},{4,0},{8,12},{12,8},{16,20},{20,16},{24,28},{28,24},{32,36},... | collective-permute-start | bytes 393224 | tf_op jit(solution)/shard_map/ppermute | solution.py:36
  7.5 18.4 %all-to-all-start = ((bf16[64,4,1024]{2,0,1:T(8,128)(2,1)}), bf16[64,4,1024]{2,0,1:T(8,128)(2,1)S(1)}, u32[]{:S(2)}, u32[]{:S(2)}) async-start(bf16[64,4,1024]{2,0,1:T(8,128)(2,1)} %bitcast.157), calls=%async_computation | async-start | bytes 1048576 | tf_op jit(solution)/shard_map/all_to_all | solution.py:82
  17.3 16.7 %collective-permute-start.6 = (bf16[256,256]{1,0:T(8,128)(2,1)S(1)}, bf16[256,256]{1,0:T(8,128)(2,1)S(1)}, u32[]{:S(2)}, u32[]{:S(2)}) collective-permute-start(bf16[256,256]{1,0:T(8,128)(2,1)S(1)} %get-tuple-element.611), channel_id=1, source_target_pairs={{56,0},{60,4},{0,8},{4,12},{8,16},{12,20},{16,24},{20,28},{24,32},... | collective-permute-start | bytes 393224 | tf_op jit(solution)/shard_map/ppermute | solution.py:20
  19.3 14.7 %collective-permute-start.5 = (bf16[256,256]{1,0:T(8,128)(2,1)S(1)}, bf16[256,256]{1,0:T(8,128)(2,1)S(1)}, u32[]{:S(2)}, u32[]{:S(2)}) collective-permute-start(bf16[256,256]{1,0:T(8,128)(2,1)S(1)} %get-tuple-element.612), channel_id=1, source_target_pairs={{8,0},{12,4},{16,8},{20,12},{24,16},{28,20},{32,24},{36,28},{40,32... | collective-permute-start | bytes 393224 | tf_op jit(solution)/shard_map/ppermute | solution.py:20
  23.3 3.5 %copy-start.7 = (f32[8,256]{1,0:T(8,128)S(1)}, f32[8,256]{1,0:T(8,128)}, u32[]{:S(2)}) copy-start(f32[8,256]{1,0:T(8,128)} %param.16) | copy-start | bytes 24580
  26.4 5.4 %copy-start.2 = (bf16[256,8,128]{0,2,1:T(8,128)(2,1)}, bf16[256,8,128]{0,2,1:T(8,128)(2,1)S(1)}, u32[]{:S(2)}) copy-start(bf16[256,8,128]{0,2,1:T(8,128)(2,1)S(1)} %copy.90) | copy-start | bytes 1572868
  26.8 3.4 %copy-start.6 = (pred[256,512]{0,1:T(8,128)(4,1)S(1)}, pred[256,512]{0,1:T(8,128)(4,1)}, u32[]{:S(2)}) copy-start(pred[256,512]{0,1:T(8,128)(4,1)} %get-tuple-element.614) | copy-start | bytes 393220
  26.8 3.5 %copy-start.1 = (f32[512,256,8]{1,0,2:T(8,128)S(1)}, f32[512,256,8]{1,0,2:T(8,128)}, u32[]{:S(2)}) copy-start(f32[512,256,8]{1,0,2:T(8,128)} %fusion.60) | copy-start | bytes 12582916
  34.1 14.8 %collective-permute-start = (bf16[256,256]{1,0:T(8,128)(2,1)S(1)}, bf16[256,256]{1,0:T(8,128)(2,1)S(1)}, u32[]{:S(2)}, u32[]{:S(2)}) collective-permute-start(bf16[256,256]{1,0:T(8,128)(2,1)S(1)} %copy.149), channel_id=1, source_target_pairs={{8,0},{12,4},{16,8},{20,12},{24,16},{28,20},{32,24},{36,28},{40,32... | collective-permute-start | bytes 393224 | tf_op jit(solution)/shard_map/while/body/eval_jaxpr/ppermute | solution.py:20
  36.1 12.7 %collective-permute-start.1 = (bf16[256,256]{1,0:T(8,128)(2,1)S(1)}, bf16[256,256]{1,0:T(8,128)(2,1)S(1)}, u32[]{:S(2)}, u32[]{:S(2)}) collective-permute-start(bf16[256,256]{1,0:T(8,128)(2,1)S(1)} %copy.150), channel_id=1, source_target_pairs={{56,0},{60,4},{0,8},{4,12},{8,16},{12,20},{16,24},{20,28},{24,32},... | collective-permute-start | bytes 393224 | tf_op jit(solution)/shard_map/while/body/eval_jaxpr/ppermute | solution.py:20
  36.2 11.7 %collective-permute-start.2 = (f32[256,256]{0,1:T(8,128)}, f32[256,256]{0,1:T(8,128)S(1)}, u32[]{:S(2)}, u32[]{:S(2)}) collective-permute-start(f32[256,256]{0,1:T(8,128)} %get-tuple-element.748), channel_id=1, source_target_pairs={{56,0},{60,4},{0,8},{4,12},{8,16},{12,20},{16,24},{20,28},{24,32},... | collective-permute-start | bytes 786440 | tf_op jit(solution)/shard_map/while/body/eval_jaxpr/ppermute | solution.py:20
  36.3 11.6 %collective-permute-start.3 = (f32[256,256]{0,1:T(8,128)}, f32[256,256]{0,1:T(8,128)S(1)}, u32[]{:S(2)}, u32[]{:S(2)}) collective-permute-start(f32[256,256]{0,1:T(8,128)} %get-tuple-element.747), channel_id=1, source_target_pairs={{8,0},{12,4},{16,8},{20,12},{24,16},{28,20},{32,24},{36,28},{40,32... | collective-permute-start | bytes 786440 | tf_op jit(solution)/shard_map/while/body/eval_jaxpr/ppermute | solution.py:20
  40.4 1.0 copy-start.3
  48.8 12.2 %collective-permute-start = (bf16[256,256]{1,0:T(8,128)(2,1)S(1)}, bf16[256,256]{1,0:T(8,128)(2,1)S(1)}, u32[]{:S(2)}, u32[]{:S(2)}) collective-permute-start(bf16[256,256]{1,0:T(8,128)(2,1)S(1)} %copy.149), channel_id=1, source_target_pairs={{8,0},{12,4},{16,8},{20,12},{24,16},{28,20},{32,24},{36,28},{40,32... | collective-permute-start | bytes 393224 | tf_op jit(solution)/shard_map/while/body/eval_jaxpr/ppermute | solution.py:20
  49.4 11.6 %collective-permute-start.1 = (bf16[256,256]{1,0:T(8,128)(2,1)S(1)}, bf16[256,256]{1,0:T(8,128)(2,1)S(1)}, u32[]{:S(2)}, u32[]{:S(2)}) collective-permute-start(bf16[256,256]{1,0:T(8,128)(2,1)S(1)} %copy.150), channel_id=1, source_target_pairs={{56,0},{60,4},{0,8},{4,12},{8,16},{12,20},{16,24},{20,28},{24,32},... | collective-permute-start | bytes 393224 | tf_op jit(solution)/shard_map/while/body/eval_jaxpr/ppermute | solution.py:20
  51.0 9.1 %collective-permute-start.2 = (f32[256,256]{0,1:T(8,128)}, f32[256,256]{0,1:T(8,128)S(1)}, u32[]{:S(2)}, u32[]{:S(2)}) collective-permute-start(f32[256,256]{0,1:T(8,128)} %get-tuple-element.748), channel_id=1, source_target_pairs={{56,0},{60,4},{0,8},{4,12},{8,16},{12,20},{16,24},{20,28},{24,32},... | collective-permute-start | bytes 786440 | tf_op jit(solution)/shard_map/while/body/eval_jaxpr/ppermute | solution.py:20
  51.1 9.0 %collective-permute-start.3 = (f32[256,256]{0,1:T(8,128)}, f32[256,256]{0,1:T(8,128)S(1)}, u32[]{:S(2)}, u32[]{:S(2)}) collective-permute-start(f32[256,256]{0,1:T(8,128)} %get-tuple-element.747), channel_id=1, source_target_pairs={{8,0},{12,4},{16,8},{20,12},{24,16},{28,20},{32,24},{36,28},{40,32... | collective-permute-start | bytes 786440 | tf_op jit(solution)/shard_map/while/body/eval_jaxpr/ppermute | solution.py:20
  55.2 1.0 copy-start.3
  61.0 12.1 %collective-permute-start = (bf16[256,256]{1,0:T(8,128)(2,1)S(1)}, bf16[256,256]{1,0:T(8,128)(2,1)S(1)}, u32[]{:S(2)}, u32[]{:S(2)}) collective-permute-start(bf16[256,256]{1,0:T(8,128)(2,1)S(1)} %copy.149), channel_id=1, source_target_pairs={{8,0},{12,4},{16,8},{20,12},{24,16},{28,20},{32,24},{36,28},{40,32... | collective-permute-start | bytes 393224 | tf_op jit(solution)/shard_map/while/body/eval_jaxpr/ppermute | solution.py:20
  63.1 10.1 %collective-permute-start.1 = (bf16[256,256]{1,0:T(8,128)(2,1)S(1)}, bf16[256,256]{1,0:T(8,128)(2,1)S(1)}, u32[]{:S(2)}, u32[]{:S(2)}) collective-permute-start(bf16[256,256]{1,0:T(8,128)(2,1)S(1)} %copy.150), channel_id=1, source_target_pairs={{56,0},{60,4},{0,8},{4,12},{8,16},{12,20},{16,24},{20,28},{24,32},... | collective-permute-start | bytes 393224 | tf_op jit(solution)/shard_map/while/body/eval_jaxpr/ppermute | solution.py:20
  63.2 9.0 %collective-permute-start.2 = (f32[256,256]{0,1:T(8,128)}, f32[256,256]{0,1:T(8,128)S(1)}, u32[]{:S(2)}, u32[]{:S(2)}) collective-permute-start(f32[256,256]{0,1:T(8,128)} %get-tuple-element.748), channel_id=1, source_target_pairs={{56,0},{60,4},{0,8},{4,12},{8,16},{12,20},{16,24},{20,28},{24,32},... | collective-permute-start | bytes 786440 | tf_op jit(solution)/shard_map/while/body/eval_jaxpr/ppermute | solution.py:20
  63.5 8.7 %collective-permute-start.3 = (f32[256,256]{0,1:T(8,128)}, f32[256,256]{0,1:T(8,128)S(1)}, u32[]{:S(2)}, u32[]{:S(2)}) collective-permute-start(f32[256,256]{0,1:T(8,128)} %get-tuple-element.747), channel_id=1, source_target_pairs={{8,0},{12,4},{16,8},{20,12},{24,16},{28,20},{32,24},{36,28},{40,32... | collective-permute-start | bytes 786440 | tf_op jit(solution)/shard_map/while/body/eval_jaxpr/ppermute | solution.py:20
  67.4 1.0 copy-start.3
  73.1 12.2 %collective-permute-start = (bf16[256,256]{1,0:T(8,128)(2,1)S(1)}, bf16[256,256]{1,0:T(8,128)(2,1)S(1)}, u32[]{:S(2)}, u32[]{:S(2)}) collective-permute-start(bf16[256,256]{1,0:T(8,128)(2,1)S(1)} %copy.149), channel_id=1, source_target_pairs={{8,0},{12,4},{16,8},{20,12},{24,16},{28,20},{32,24},{36,28},{40,32... | collective-permute-start | bytes 393224 | tf_op jit(solution)/shard_map/while/body/eval_jaxpr/ppermute | solution.py:20
  75.3 10.1 %collective-permute-start.1 = (bf16[256,256]{1,0:T(8,128)(2,1)S(1)}, bf16[256,256]{1,0:T(8,128)(2,1)S(1)}, u32[]{:S(2)}, u32[]{:S(2)}) collective-permute-start(bf16[256,256]{1,0:T(8,128)(2,1)S(1)} %copy.150), channel_id=1, source_target_pairs={{56,0},{60,4},{0,8},{4,12},{8,16},{12,20},{16,24},{20,28},{24,32},... | collective-permute-start | bytes 393224 | tf_op jit(solution)/shard_map/while/body/eval_jaxpr/ppermute | solution.py:20
  75.3 9.1 %collective-permute-start.2 = (f32[256,256]{0,1:T(8,128)}, f32[256,256]{0,1:T(8,128)S(1)}, u32[]{:S(2)}, u32[]{:S(2)}) collective-permute-start(f32[256,256]{0,1:T(8,128)} %get-tuple-element.748), channel_id=1, source_target_pairs={{56,0},{60,4},{0,8},{4,12},{8,16},{12,20},{16,24},{20,28},{24,32},... | collective-permute-start | bytes 786440 | tf_op jit(solution)/shard_map/while/body/eval_jaxpr/ppermute | solution.py:20
  75.8 8.6 %collective-permute-start.3 = (f32[256,256]{0,1:T(8,128)}, f32[256,256]{0,1:T(8,128)S(1)}, u32[]{:S(2)}, u32[]{:S(2)}) collective-permute-start(f32[256,256]{0,1:T(8,128)} %get-tuple-element.747), channel_id=1, source_target_pairs={{8,0},{12,4},{16,8},{20,12},{24,16},{28,20},{32,24},{36,28},{40,32... | collective-permute-start | bytes 786440 | tf_op jit(solution)/shard_map/while/body/eval_jaxpr/ppermute | solution.py:20
  79.6 1.0 copy-start.3
  85.3 12.2 %collective-permute-start = (bf16[256,256]{1,0:T(8,128)(2,1)S(1)}, bf16[256,256]{1,0:T(8,128)(2,1)S(1)}, u32[]{:S(2)}, u32[]{:S(2)}) collective-permute-start(bf16[256,256]{1,0:T(8,128)(2,1)S(1)} %copy.149), channel_id=1, source_target_pairs={{8,0},{12,4},{16,8},{20,12},{24,16},{28,20},{32,24},{36,28},{40,32... | collective-permute-start | bytes 393224 | tf_op jit(solution)/shard_map/while/body/eval_jaxpr/ppermute | solution.py:20
  87.5 10.1 %collective-permute-start.1 = (bf16[256,256]{1,0:T(8,128)(2,1)S(1)}, bf16[256,256]{1,0:T(8,128)(2,1)S(1)}, u32[]{:S(2)}, u32[]{:S(2)}) collective-permute-start(bf16[256,256]{1,0:T(8,128)(2,1)S(1)} %copy.150), channel_id=1, source_target_pairs={{56,0},{60,4},{0,8},{4,12},{8,16},{12,20},{16,24},{20,28},{24,32},... | collective-permute-start | bytes 393224 | tf_op jit(solution)/shard_map/while/body/eval_jaxpr/ppermute | solution.py:20
  87.6 9.1 %collective-permute-start.2 = (f32[256,256]{0,1:T(8,128)}, f32[256,256]{0,1:T(8,128)S(1)}, u32[]{:S(2)}, u32[]{:S(2)}) collective-permute-start(f32[256,256]{0,1:T(8,128)} %get-tuple-element.748), channel_id=1, source_target_pairs={{56,0},{60,4},{0,8},{4,12},{8,16},{12,20},{16,24},{20,28},{24,32},... | collective-permute-start | bytes 786440 | tf_op jit(solution)/shard_map/while/body/eval_jaxpr/ppermute | solution.py:20
  88.4 8.2 %collective-permute-start.3 = (f32[256,256]{0,1:T(8,128)}, f32[256,256]{0,1:T(8,128)S(1)}, u32[]{:S(2)}, u32[]{:S(2)}) collective-permute-start(f32[256,256]{0,1:T(8,128)} %get-tuple-element.747), channel_id=1, source_target_pairs={{8,0},{12,4},{16,8},{20,12},{24,16},{28,20},{32,24},{36,28},{40,32... | collective-permute-start | bytes 786440 | tf_op jit(solution)/shard_map/while/body/eval_jaxpr/ppermute | solution.py:20
  91.8 1.0 copy-start.3
  97.5 12.2 %collective-permute-start = (bf16[256,256]{1,0:T(8,128)(2,1)S(1)}, bf16[256,256]{1,0:T(8,128)(2,1)S(1)}, u32[]{:S(2)}, u32[]{:S(2)}) collective-permute-start(bf16[256,256]{1,0:T(8,128)(2,1)S(1)} %copy.149), channel_id=1, source_target_pairs={{8,0},{12,4},{16,8},{20,12},{24,16},{28,20},{32,24},{36,28},{40,32... | collective-permute-start | bytes 393224 | tf_op jit(solution)/shard_map/while/body/eval_jaxpr/ppermute | solution.py:20
  99.7 10.1 %collective-permute-start.1 = (bf16[256,256]{1,0:T(8,128)(2,1)S(1)}, bf16[256,256]{1,0:T(8,128)(2,1)S(1)}, u32[]{:S(2)}, u32[]{:S(2)}) collective-permute-start(bf16[256,256]{1,0:T(8,128)(2,1)S(1)} %copy.150), channel_id=1, source_target_pairs={{56,0},{60,4},{0,8},{4,12},{8,16},{12,20},{16,24},{20,28},{24,32},... | collective-permute-start | bytes 393224 | tf_op jit(solution)/shard_map/while/body/eval_jaxpr/ppermute | solution.py:20
  99.8 9.1 %collective-permute-start.2 = (f32[256,256]{0,1:T(8,128)}, f32[256,256]{0,1:T(8,128)S(1)}, u32[]{:S(2)}, u32[]{:S(2)}) collective-permute-start(f32[256,256]{0,1:T(8,128)} %get-tuple-element.748), channel_id=1, source_target_pairs={{56,0},{60,4},{0,8},{4,12},{8,16},{12,20},{16,24},{20,28},{24,32},... | collective-permute-start | bytes 786440 | tf_op jit(solution)/shard_map/while/body/eval_jaxpr/ppermute | solution.py:20
  100.7 8.2 %collective-permute-start.3 = (f32[256,256]{0,1:T(8,128)}, f32[256,256]{0,1:T(8,128)S(1)}, u32[]{:S(2)}, u32[]{:S(2)}) collective-permute-start(f32[256,256]{0,1:T(8,128)} %get-tuple-element.747), channel_id=1, source_target_pairs={{8,0},{12,4},{16,8},{20,12},{24,16},{28,20},{32,24},{36,28},{40,32... | collective-permute-start | bytes 786440 | tf_op jit(solution)/shard_map/while/body/eval_jaxpr/ppermute | solution.py:20
  104.0 1.0 copy-start.3
  109.7 1.0 copy-start.4
  109.7 1.1 copy-start.5
  116.6 6.5 %collective-permute-start.7 = (f32[256,256]{1,0:T(8,128)S(1)}, f32[256,256]{1,0:T(8,128)S(1)}, u32[]{:S(2)}, u32[]{:S(2)}) collective-permute-start(f32[256,256]{1,0:T(8,128)S(1)} %copy.98), channel_id=1, source_target_pairs={{8,0},{12,4},{16,8},{20,12},{24,16},{28,20},{32,24},{36,28},{40,32... | collective-permute-start | bytes 786440 | tf_op jit(solution)/shard_map/ppermute | solution.py:20
  118.7 8.8 %collective-permute-start.8 = (f32[256,256]{1,0:T(8,128)S(1)}, f32[256,256]{1,0:T(8,128)S(1)}, u32[]{:S(2)}, u32[]{:S(2)}) collective-permute-start(f32[256,256]{1,0:T(8,128)S(1)} %copy.104), channel_id=1, source_target_pairs={{56,0},{60,4},{0,8},{4,12},{8,16},{12,20},{16,24},{20,28},{24,32},... | collective-permute-start | bytes 786440 | tf_op jit(solution)/shard_map/ppermute | solution.py:20
  127.5 8.9 %collective-permute-start.10 = (f32[256,256]{1,0:T(8,128)S(1)}, f32[256,256]{1,0:T(8,128)S(1)}, u32[]{:S(2)}, u32[]{:S(2)}) collective-permute-start(f32[256,256]{1,0:T(8,128)S(1)} %get-tuple-element.607), channel_id=1, source_target_pairs={{0,12},{4,56},{8,20},{12,0},{16,28},{20,8},{24,36},{28,16},{32,44}... | collective-permute-start | bytes 786440 | tf_op jit(solution)/shard_map/ppermute | solution.py:31
  127.6 8.8 %collective-permute-start.9 = (f32[256,256]{1,0:T(8,128)S(1)}, f32[256,256]{1,0:T(8,128)S(1)}, u32[]{:S(2)}, u32[]{:S(2)}) collective-permute-start(f32[256,256]{1,0:T(8,128)S(1)} %get-tuple-element.608), channel_id=1, source_target_pairs={{0,56},{4,12},{8,0},{12,20},{16,8},{20,28},{24,16},{28,36},{32,24}... | collective-permute-start | bytes 786440 | tf_op jit(solution)/shard_map/ppermute | solution.py:31

commit v9 on v8

--- a/solution.py
+++ b/solution.py
@@ -119,12 +119,17 @@
     next_behind = along_z(behind_kv, ctx_count, -1)
     query_acc, ahead_pending, behind_pending = terms(ahead_kv, behind_kv, 0)
 
+    kv_width = key_values.shape[1]
+
+    def bundled(kv, pending, shift):
+        both = jnp.concatenate([kv.astype(jnp.float32), pending], axis=1)
+        moved = along_z(both, ctx_count, shift)
+        return moved[:, :kv_width].astype(kv.dtype), moved[:, kv_width:]
+
     def visit_turn(turn, carried):
         ahead_kv, behind_kv, query_acc, ahead_pending, behind_pending = carried
-        ahead_received = along_z(ahead_pending, ctx_count, 1)
-        behind_received = along_z(behind_pending, ctx_count, -1)
-        next_ahead = along_z(ahead_kv, ctx_count, 1)
-        next_behind = along_z(behind_kv, ctx_count, -1)
+        next_ahead, ahead_received = bundled(ahead_kv, ahead_pending, 1)
+        next_behind, behind_received = bundled(behind_kv, behind_pending, -1)
         query_term, ahead_term, behind_term = terms(ahead_kv, behind_kv, turn)
         return (
             next_ahead,

time: 139 us -> 163 us (1.17)
  waiting for transfers between devices: 13 us -> 44.8 us
  starting transfers between devices: 49.6 us -> 29.5 us
  local copies, waits for them, and re-layouts: 18.2 us -> 33.2 us
  matrix products: 43.7 us -> 39.1 us
    ppermute x28 -> x16, waiting for transfers between devices: 7.23 us -> 37.2 us  [along_z(): return lax.ppermute(value, 'ctx', pairs)]
    ppermute x28 -> x16, starting transfers between devices: 40.9 us -> 22.3 us  [along_z(): return lax.ppermute(value, 'ctx', pairs)]
    slice x0 -> x12, local copies, waits for them, and re-layouts: none -> 11.6 us  [bundled(): return (moved[:, :kv_width].astype(kv.dtype), moved[:, kv_width:])]
    while x32 -> x66, local copies, waits for them, and re-layouts: 2.36 us -> 5.54 us  [the longest x2 2.15 us: local(): lax.fori_loop(1, z_count - 1, visit_turn, (next_ahead, next_behind, query...]
    ppermute x2, waiting for transfers between devices: 5.76 us -> 7.6 us  [to_owner(): return lax.ppermute(value, 'ctx', pairs)]
    unnamed x21 -> x25, local copies, waits for them, and re-layouts: 5.02 us -> 5.2 us
  transfers between devices with their start and end apart: 32 -> 20, of which waited for: 4 -> 16; matrix products, arithmetic and copies ran while one was open for 46% -> 34% of each run, Pallas kernels for 0% -> 0%
where the time goes in v9:
time: 163 us; the launch traced here: 162 us
  waiting for transfers between devices  44.8 us (27%)
  matrix products  39.1 us (24%)
  local copies, waits for them, and re-layouts  33.2 us (20%)
  starting transfers between devices  29.5 us (18%)
  other arithmetic  12.2 us (7%)
    ppermute x16, waiting for transfers between devices, along_z(): return lax.ppermute(value, 'ctx', pairs)  37.2 us
    ppermute x16, starting transfers between devices, along_z(): return lax.ppermute(value, 'ctx', pairs)  22.3 us
    slice x12, local copies, waits for them, and re-layouts, bundled(): return (moved[:, :kv_width].astype(kv.dtype), moved[:, kv_width:])  11.6 us
    dot_general x8, matrix products, contract(): jnp.einsum('igd,jd->gij', out_grads, values_part, preferred_element_type=...  11.2 us
    dot_general x8, matrix products, contract(): jnp.einsum('gij,igd->jd', probabilities.astype(jnp.bfloat16), out_grads,...  10.3 us
    ppermute x2, waiting for transfers between devices, to_owner(): return lax.ppermute(value, 'ctx', pairs)  7.6 us
    dot_general x8, matrix products, contract(): jnp.einsum('igd,jd->gij', queries, keys_part, preferred_element_type=jnp....  7.5 us
    add x6, other arithmetic, visit_turn(): behind_received + behind_term  6.59 us
  transfers between devices with their start and end apart: 20, of which 16 were waited for; matrix products, arithmetic and copies ran while one was open for 34% of the time, Pallas kernels for 0%

profile of v9, /device:TPU:4, one launch (start us, length us, event | category | flops | bytes accessed | tf_op | source)
XLA Modules:
  0.0 161.6 jit_solution(1883353190979519365)
XLA Ops:
  2.4 3.3 %collective-permute-start.2 = (bf16[256,256]{1,0:T(8,128)(2,1)S(1)}, bf16[256,256]{1,0:T(8,128)(2,1)S(1)}, u32[]{:S(2)}, u32[]{:S(2)}) collective-permute-start(bf16[256,256]{1,0:T(8,128)(2,1)S(1)} %constant_dynamic-update-slice_fusion.2), channel_id=1, source_target_pairs={{0,4},{4,0},{8,12},{12,8},{16,20},{20,16},{24,28},{28,24},{32,36},... | collective-permute-start | bytes 393224 | tf_op jit(solution)/shard_map/ppermute | solution.py:36
  5.7 1.9 %copy.161 = bf16[8,4,8,1024]{3,2,0,1:T(8,128)(2,1)} copy(bf16[8,4,8,1024]{3,2,1,0:T(8,128)(2,1)} %bitcast.204) | data formatting | bytes 1048576 | tf_op jit(solution)/shard_map/reshape | solution.py:81
  7.5 3.5 %all-to-all-start = ((bf16[64,4,1024]{2,0,1:T(8,128)(2,1)}), bf16[64,4,1024]{2,0,1:T(8,128)(2,1)S(1)}, u32[]{:S(2)}, u32[]{:S(2)}) async-start(bf16[64,4,1024]{2,0,1:T(8,128)(2,1)} %bitcast.157), calls=%async_computation | async-start | bytes 1048576 | tf_op jit(solution)/shard_map/all_to_all | solution.py:82
  13.2 1.2 copy.103
  14.4 1.2 copy.107
  16.0 1.2 fusion.45
  17.2 5.9 %collective-permute-start.3 = (bf16[256,256]{1,0:T(8,128)(2,1)S(1)}, bf16[256,256]{1,0:T(8,128)(2,1)S(1)}, u32[]{:S(2)}, u32[]{:S(2)}) collective-permute-start(bf16[256,256]{1,0:T(8,128)(2,1)S(1)} %get-tuple-element.651), channel_id=1, source_target_pairs={{8,0},{12,4},{16,8},{20,12},{24,16},{28,20},{32,24},{36,28},{40,32... | collective-permute-start | bytes 393224 | tf_op jit(solution)/shard_map/ppermute | solution.py:20
  23.1 2.7 %fusion.60 = f32[512,256,8]{1,0,2:T(8,128)} fusion(bf16[256,8,128]{0,2,1:T(8,128)(2,1)S(1)} %bitcast.194, bf16[256,256]{1,0:T(8,128)(2,1)S(1)} %get-tuple-element.651, bf16[256,256]{1,0:T(8,128)(2,1)S(1)} %get-tuple-element.650), kind=kOutput, calls=%fused_computation.120 | convolution fusion | flops 268697600 | bytes 4980736 | tf_op jit(solution)/shard_map/igd,jd->gij/dot_general | solution.py:54
  26.7 3.4 %fusion.39 = f32[512,128]{0,1:T(8,128)S(1)} fusion(bf16[256,8,128]{0,2,1:T(8,128)(2,1)S(1)} %copy.114, f32[512,256,8]{1,0,2:T(8,128)} %fusion.60, f32[8,256]{1,0:T(8,128)S(1)} %copy-done.8, pred[256,512]{0,1:T(8,128)(4,1)S(1)} %get-tuple-element.653), kind=kOutput, calls=%fused_computation.80 | convolution fusion | flops 272629760 | bytes 5120000 | tf_op jit(solution)/shard_map/gij,igd->jd/dot_general | solution.py:64
  30.1 1.4 fusion.28
  33.2 104.5 %while.26 = (s32[]{:T(128)}, bf16[256,256]{1,0:T(8,128)(2,1)S(1)}, bf16[256,256]{1,0:T(8,128)(2,1)S(1)}, f32[256,8,128]{0,2,1:T(8,128)S(1)}, f32[256,256]{1,0:T(...) while((s32[]{:T(128)}, bf16[256,256]{1,0:T(8,128)(2,1)S(1)}, ...), condition=%wide.region_2.4_spmd.clone.clone, body=%wide.region_1.3_spmd.clone.clone.sunk | while | flops 1354380928 | bytes 39369496 | solution.py:142
  33.7 3.3 %collective-permute-start = (f32[256,512]{0,1:T(8,128)S(1)}, f32[256,512]{0,1:T(8,128)}, u32[]{:S(2)}, u32[]{:S(2)}) collective-permute-start(f32[256,512]{0,1:T(8,128)S(1)} %pad_maximum_fusion.8), channel_id=1, source_target_pairs={{8,0},{12,4},{16,8},{20,12},{24,16},{28,20},{32,24},{36,28},{40,32... | collective-permute-start | bytes 1572872 | tf_op jit(solution)/shard_map/while/body/eval_jaxpr/ppermute | solution.py:20
  39.4 1.4 fusion.112
  42.1 1.0 fusion.114
  43.1 5.1 %collective-permute-done = f32[256,512]{0,1:T(8,128)} collective-permute-done((f32[256,512]{0,1:T(8,128)S(1)}, f32[256,512]{0,1:T(8,128)}, u32[]{:S(2)}, u32[]{:S(2)}) %collective-permute-start) | collective-permute-done | bytes 524320 | tf_op jit(solution)/shard_map/while/body/eval_jaxpr/ppermute | solution.py:20
  48.2 3.9 %collective-permute-done.1 = f32[256,512]{0,1:T(8,128)} collective-permute-done((f32[256,512]{0,1:T(8,128)S(1)}, f32[256,512]{0,1:T(8,128)}, u32[]{:S(2)}, u32[]{:S(2)}) %collective-permute-start.1) | collective-permute-done | bytes 524320 | tf_op jit(solution)/shard_map/while/body/eval_jaxpr/ppermute | solution.py:20
  52.1 1.1 fusion.115
  53.5 1.0 slice.268
  54.6 1.0 slice.269
  56.4 2.1 %collective-permute-start.1 = (f32[256,512]{0,1:T(8,128)S(1)}, f32[256,512]{0,1:T(8,128)}, u32[]{:S(2)}, u32[]{:S(2)}) collective-permute-start(f32[256,512]{0,1:T(8,128)S(1)} %pad_maximum_fusion.9), channel_id=1, source_target_pairs={{56,0},{60,4},{0,8},{4,12},{8,16},{12,20},{16,24},{20,28},{24,32},... | collective-permute-start | bytes 1572872 | tf_op jit(solution)/shard_map/while/body/eval_jaxpr/ppermute | solution.py:20
  60.5 1.4 fusion.112
  63.2 1.0 fusion.114
  64.2 4.5 %collective-permute-done = f32[256,512]{0,1:T(8,128)} collective-permute-done((f32[256,512]{0,1:T(8,128)S(1)}, f32[256,512]{0,1:T(8,128)}, u32[]{:S(2)}, u32[]{:S(2)}) %collective-permute-start) | collective-permute-done | bytes 524320 | tf_op jit(solution)/shard_map/while/body/eval_jaxpr/ppermute | solution.py:20
  68.7 1.6 %collective-permute-done.1 = f32[256,512]{0,1:T(8,128)} collective-permute-done((f32[256,512]{0,1:T(8,128)S(1)}, f32[256,512]{0,1:T(8,128)}, u32[]{:S(2)}, u32[]{:S(2)}) %collective-permute-start.1) | collective-permute-done | bytes 524320 | tf_op jit(solution)/shard_map/while/body/eval_jaxpr/ppermute | solution.py:20
  70.3 1.1 fusion.115
  71.7 1.0 slice.268
  72.7 1.0 slice.269
  74.5 2.1 %collective-permute-start.1 = (f32[256,512]{0,1:T(8,128)S(1)}, f32[256,512]{0,1:T(8,128)}, u32[]{:S(2)}, u32[]{:S(2)}) collective-permute-start(f32[256,512]{0,1:T(8,128)S(1)} %pad_maximum_fusion.9), channel_id=1, source_target_pairs={{56,0},{60,4},{0,8},{4,12},{8,16},{12,20},{16,24},{20,28},{24,32},... | collective-permute-start | bytes 1572872 | tf_op jit(solution)/shard_map/while/body/eval_jaxpr/ppermute | solution.py:20
  78.6 1.4 fusion.112
  81.3 1.0 fusion.114
  82.4 3.6 %collective-permute-done = f32[256,512]{0,1:T(8,128)} collective-permute-done((f32[256,512]{0,1:T(8,128)S(1)}, f32[256,512]{0,1:T(8,128)}, u32[]{:S(2)}, u32[]{:S(2)}) %collective-permute-start) | collective-permute-done | bytes 524320 | tf_op jit(solution)/shard_map/while/body/eval_jaxpr/ppermute | solution.py:20
  85.9 1.6 %collective-permute-done.1 = f32[256,512]{0,1:T(8,128)} collective-permute-done((f32[256,512]{0,1:T(8,128)S(1)}, f32[256,512]{0,1:T(8,128)}, u32[]{:S(2)}, u32[]{:S(2)}) %collective-permute-start.1) | collective-permute-done | bytes 524320 | tf_op jit(solution)/shard_map/while/body/eval_jaxpr/ppermute | solution.py:20
  87.5 1.1 fusion.115
  88.9 1.0 slice.268
  90.0 1.0 slice.269
  91.8 2.1 %collective-permute-start.1 = (f32[256,512]{0,1:T(8,128)S(1)}, f32[256,512]{0,1:T(8,128)}, u32[]{:S(2)}, u32[]{:S(2)}) collective-permute-start(f32[256,512]{0,1:T(8,128)S(1)} %pad_maximum_fusion.9), channel_id=1, source_target_pairs={{56,0},{60,4},{0,8},{4,12},{8,16},{12,20},{16,24},{20,28},{24,32},... | collective-permute-start | bytes 1572872 | tf_op jit(solution)/shard_map/while/body/eval_jaxpr/ppermute | solution.py:20
  95.9 1.4 fusion.112
  98.6 1.0 fusion.114
  99.6 2.6 %collective-permute-done = f32[256,512]{0,1:T(8,128)} collective-permute-done((f32[256,512]{0,1:T(8,128)S(1)}, f32[256,512]{0,1:T(8,128)}, u32[]{:S(2)}, u32[]{:S(2)}) %collective-permute-start) | collective-permute-done | bytes 524320 | tf_op jit(solution)/shard_map/while/body/eval_jaxpr/ppermute | solution.py:20
  102.2 1.6 %collective-permute-done.1 = f32[256,512]{0,1:T(8,128)} collective-permute-done((f32[256,512]{0,1:T(8,128)S(1)}, f32[256,512]{0,1:T(8,128)}, u32[]{:S(2)}, u32[]{:S(2)}) %collective-permute-start.1) | collective-permute-done | bytes 524320 | tf_op jit(solution)/shard_map/while/body/eval_jaxpr/ppermute | solution.py:20
  103.9 1.1 fusion.115
  105.2 1.0 slice.268
  106.3 1.0 slice.269
  108.1 2.1 %collective-permute-start.1 = (f32[256,512]{0,1:T(8,128)S(1)}, f32[256,512]{0,1:T(8,128)}, u32[]{:S(2)}, u32[]{:S(2)}) collective-permute-start(f32[256,512]{0,1:T(8,128)S(1)} %pad_maximum_fusion.9), channel_id=1, source_target_pairs={{56,0},{60,4},{0,8},{4,12},{8,16},{12,20},{16,24},{20,28},{24,32},... | collective-permute-start | bytes 1572872 | tf_op jit(solution)/shard_map/while/body/eval_jaxpr/ppermute | solution.py:20
  112.2 1.4 fusion.112
  114.9 1.0 fusion.114
  115.9 1.7 %collective-permute-done = f32[256,512]{0,1:T(8,128)} collective-permute-done((f32[256,512]{0,1:T(8,128)S(1)}, f32[256,512]{0,1:T(8,128)}, u32[]{:S(2)}, u32[]{:S(2)}) %collective-permute-start) | collective-permute-done | bytes 524320 | tf_op jit(solution)/shard_map/while/body/eval_jaxpr/ppermute | solution.py:20
  117.7 1.6 %collective-permute-done.1 = f32[256,512]{0,1:T(8,128)} collective-permute-done((f32[256,512]{0,1:T(8,128)S(1)}, f32[256,512]{0,1:T(8,128)}, u32[]{:S(2)}, u32[]{:S(2)}) %collective-permute-start.1) | collective-permute-done | bytes 524320 | tf_op jit(solution)/shard_map/while/body/eval_jaxpr/ppermute | solution.py:20
  119.3 1.1 fusion.115
  120.6 1.0 slice.268
  121.7 1.0 slice.269
  123.5 2.1 %collective-permute-start.1 = (f32[256,512]{0,1:T(8,128)S(1)}, f32[256,512]{0,1:T(8,128)}, u32[]{:S(2)}, u32[]{:S(2)}) collective-permute-start(f32[256,512]{0,1:T(8,128)S(1)} %pad_maximum_fusion.9), channel_id=1, source_target_pairs={{56,0},{60,4},{0,8},{4,12},{8,16},{12,20},{16,24},{20,28},{24,32},... | collective-permute-start | bytes 1572872 | tf_op jit(solution)/shard_map/while/body/eval_jaxpr/ppermute | solution.py:20
  127.6 1.4 fusion.112
  130.3 1.0 fusion.114
  131.3 1.1 collective-permute-done
  132.5 1.6 %collective-permute-done.1 = f32[256,512]{0,1:T(8,128)} collective-permute-done((f32[256,512]{0,1:T(8,128)S(1)}, f32[256,512]{0,1:T(8,128)}, u32[]{:S(2)}, u32[]{:S(2)}) %collective-permute-start.1) | collective-permute-done | bytes 524320 | tf_op jit(solution)/shard_map/while/body/eval_jaxpr/ppermute | solution.py:20
  134.1 1.1 fusion.115
  139.6 1.4 fusion.24
  141.1 2.0 %collective-permute-start.6 = (f32[256,256]{1,0:T(8,128)S(1)}, f32[256,256]{1,0:T(8,128)S(1)}, u32[]{:S(2)}, u32[]{:S(2)}) collective-permute-start(f32[256,256]{1,0:T(8,128)S(1)} %get-tuple-element.458), channel_id=1, source_target_pairs={{56,0},{60,4},{0,8},{4,12},{8,16},{12,20},{16,24},{20,28},{24,32},... | collective-permute-start | bytes 786440 | tf_op jit(solution)/shard_map/ppermute | solution.py:20
  144.3 5.5 %collective-permute-done.5 = f32[256,256]{1,0:T(8,128)S(1)} collective-permute-done((f32[256,256]{1,0:T(8,128)S(1)}, f32[256,256]{1,0:T(8,128)S(1)}, u32[]{:S(2)}, u32[]{:S(2)}) %collective-permute-start.5) | collective-permute-done | bytes 262176 | tf_op jit(solution)/shard_map/ppermute | solution.py:20
  149.8 1.1 collective-permute-done.6
  151.7 1.0 copy.129
  152.7 4.8 %collective-permute-done.7 = f32[256,256]{1,0:T(8,128)S(1)} collective-permute-done((f32[256,256]{1,0:T(8,128)S(1)}, f32[256,256]{1,0:T(8,128)S(1)}, u32[]{:S(2)}, u32[]{:S(2)}) %collective-permute-start.7) | collective-permute-done | bytes 262176 | tf_op jit(solution)/shard_map/ppermute | solution.py:31
  157.5 2.8 %collective-permute-done.8 = f32[256,256]{1,0:T(8,128)S(1)} collective-permute-done((f32[256,256]{1,0:T(8,128)S(1)}, f32[256,256]{1,0:T(8,128)S(1)}, u32[]{:S(2)}, u32[]{:S(2)}) %collective-permute-start.8) | collective-permute-done | bytes 262176 | tf_op jit(solution)/shard_map/ppermute | solution.py:31
  (257 shorter events, 39.6 us)
Async XLA Ops:
  0.6 10.6 %copy-start = (s32[32,32]{1,0:T(8,128)S(1)}, s32[32,32]{1,0:T(8,128)}, u32[]{:S(2)}) copy-start(s32[32,32]{1,0:T(8,128)} %param.17) | copy-start | bytes 12292
  2.4 14.8 %collective-permute-start.2 = (bf16[256,256]{1,0:T(8,128)(2,1)S(1)}, bf16[256,256]{1,0:T(8,128)(2,1)S(1)}, u32[]{:S(2)}, u32[]{:S(2)}) collective-permute-start(bf16[256,256]{1,0:T(8,128)(2,1)S(1)} %constant_dynamic-update-slice_fusion.2), channel_id=1, source_target_pairs={{0,4},{4,0},{8,12},{12,8},{16,20},{20,16},{24,28},{28,24},{32,36},... | collective-permute-start | bytes 393224 | tf_op jit(solution)/shard_map/ppermute | solution.py:36
  7.5 18.3 %all-to-all-start = ((bf16[64,4,1024]{2,0,1:T(8,128)(2,1)}), bf16[64,4,1024]{2,0,1:T(8,128)(2,1)S(1)}, u32[]{:S(2)}, u32[]{:S(2)}) async-start(bf16[64,4,1024]{2,0,1:T(8,128)(2,1)} %bitcast.157), calls=%async_computation | async-start | bytes 1048576 | tf_op jit(solution)/shard_map/all_to_all | solution.py:82
  17.2 15.9 %collective-permute-start.3 = (bf16[256,256]{1,0:T(8,128)(2,1)S(1)}, bf16[256,256]{1,0:T(8,128)(2,1)S(1)}, u32[]{:S(2)}, u32[]{:S(2)}) collective-permute-start(bf16[256,256]{1,0:T(8,128)(2,1)S(1)} %get-tuple-element.651), channel_id=1, source_target_pairs={{8,0},{12,4},{16,8},{20,12},{24,16},{28,20},{32,24},{36,28},{40,32... | collective-permute-start | bytes 393224 | tf_op jit(solution)/shard_map/ppermute | solution.py:20
  23.1 10.0 %collective-permute-start.4 = (bf16[256,256]{1,0:T(8,128)(2,1)S(1)}, bf16[256,256]{1,0:T(8,128)(2,1)S(1)}, u32[]{:S(2)}, u32[]{:S(2)}) collective-permute-start(bf16[256,256]{1,0:T(8,128)(2,1)S(1)} %get-tuple-element.650), channel_id=1, source_target_pairs={{56,0},{60,4},{0,8},{4,12},{8,16},{12,20},{16,24},{20,28},{24,32},... | collective-permute-start | bytes 393224 | tf_op jit(solution)/shard_map/ppermute | solution.py:20
  23.1 3.5 %copy-start.8 = (f32[8,256]{1,0:T(8,128)S(1)}, f32[8,256]{1,0:T(8,128)}, u32[]{:S(2)}) copy-start(f32[8,256]{1,0:T(8,128)} %param.16) | copy-start | bytes 24580
  25.9 4.1 %copy-start.1 = (bf16[32,8,8,128]{3,2,1,0:T(8,128)(2,1)}, bf16[32,8,8,128]{3,2,1,0:T(8,128)(2,1)S(1)}, u32[]{:S(2)}) copy-start(bf16[32,8,8,128]{3,2,1,0:T(8,128)(2,1)S(1)} %copy.155) | copy-start | bytes 1572868
  26.2 3.8 %copy-start.4 = (bf16[256,8,128]{0,2,1:T(8,128)(2,1)}, bf16[256,8,128]{0,2,1:T(8,128)(2,1)S(1)}, u32[]{:S(2)}) copy-start(bf16[256,8,128]{0,2,1:T(8,128)(2,1)S(1)} %copy.114) | copy-start | bytes 1572868
  26.7 3.5 %copy-start.3 = (f32[512,256,8]{1,0,2:T(8,128)S(1)}, f32[512,256,8]{1,0,2:T(8,128)}, u32[]{:S(2)}) copy-start(f32[512,256,8]{1,0,2:T(8,128)} %fusion.60) | copy-start | bytes 12582916
  33.7 14.5 %collective-permute-start = (f32[256,512]{0,1:T(8,128)S(1)}, f32[256,512]{0,1:T(8,128)}, u32[]{:S(2)}, u32[]{:S(2)}) collective-permute-start(f32[256,512]{0,1:T(8,128)S(1)} %pad_maximum_fusion.8), channel_id=1, source_target_pairs={{8,0},{12,4},{16,8},{20,12},{24,16},{28,20},{32,24},{36,28},{40,32... | collective-permute-start | bytes 1572872 | tf_op jit(solution)/shard_map/while/body/eval_jaxpr/ppermute | solution.py:20
  37.3 14.8 %collective-permute-start.1 = (f32[256,512]{0,1:T(8,128)S(1)}, f32[256,512]{0,1:T(8,128)}, u32[]{:S(2)}, u32[]{:S(2)}) collective-permute-start(f32[256,512]{0,1:T(8,128)S(1)} %pad_maximum_fusion.9), channel_id=1, source_target_pairs={{56,0},{60,4},{0,8},{4,12},{8,16},{12,20},{16,24},{20,28},{24,32},... | collective-permute-start | bytes 1572872 | tf_op jit(solution)/shard_map/while/body/eval_jaxpr/ppermute | solution.py:20
  38.4 1.1 copy-start.5
  56.0 12.7 %collective-permute-start = (f32[256,512]{0,1:T(8,128)S(1)}, f32[256,512]{0,1:T(8,128)}, u32[]{:S(2)}, u32[]{:S(2)}) collective-permute-start(f32[256,512]{0,1:T(8,128)S(1)} %pad_maximum_fusion.8), channel_id=1, source_target_pairs={{8,0},{12,4},{16,8},{20,12},{24,16},{28,20},{32,24},{36,28},{40,32... | collective-permute-start | bytes 1572872 | tf_op jit(solution)/shard_map/while/body/eval_jaxpr/ppermute | solution.py:20
  56.4 13.9 %collective-permute-start.1 = (f32[256,512]{0,1:T(8,128)S(1)}, f32[256,512]{0,1:T(8,128)}, u32[]{:S(2)}, u32[]{:S(2)}) collective-permute-start(f32[256,512]{0,1:T(8,128)S(1)} %pad_maximum_fusion.9), channel_id=1, source_target_pairs={{56,0},{60,4},{0,8},{4,12},{8,16},{12,20},{16,24},{20,28},{24,32},... | collective-permute-start | bytes 1572872 | tf_op jit(solution)/shard_map/while/body/eval_jaxpr/ppermute | solution.py:20
  59.4 1.1 copy-start.5
  74.1 11.8 %collective-permute-start = (f32[256,512]{0,1:T(8,128)S(1)}, f32[256,512]{0,1:T(8,128)}, u32[]{:S(2)}, u32[]{:S(2)}) collective-permute-start(f32[256,512]{0,1:T(8,128)S(1)} %pad_maximum_fusion.8), channel_id=1, source_target_pairs={{8,0},{12,4},{16,8},{20,12},{24,16},{28,20},{32,24},{36,28},{40,32... | collective-permute-start | bytes 1572872 | tf_op jit(solution)/shard_map/while/body/eval_jaxpr/ppermute | solution.py:20
  74.5 13.0 %collective-permute-start.1 = (f32[256,512]{0,1:T(8,128)S(1)}, f32[256,512]{0,1:T(8,128)}, u32[]{:S(2)}, u32[]{:S(2)}) collective-permute-start(f32[256,512]{0,1:T(8,128)S(1)} %pad_maximum_fusion.9), channel_id=1, source_target_pairs={{56,0},{60,4},{0,8},{4,12},{8,16},{12,20},{16,24},{20,28},{24,32},... | collective-permute-start | bytes 1572872 | tf_op jit(solution)/shard_map/while/body/eval_jaxpr/ppermute | solution.py:20
  77.6 1.1 copy-start.5
  91.4 10.9 %collective-permute-start = (f32[256,512]{0,1:T(8,128)S(1)}, f32[256,512]{0,1:T(8,128)}, u32[]{:S(2)}, u32[]{:S(2)}) collective-permute-start(f32[256,512]{0,1:T(8,128)S(1)} %pad_maximum_fusion.8), channel_id=1, source_target_pairs={{8,0},{12,4},{16,8},{20,12},{24,16},{28,20},{32,24},{36,28},{40,32... | collective-permute-start | bytes 1572872 | tf_op jit(solution)/shard_map/while/body/eval_jaxpr/ppermute | solution.py:20
  91.8 12.1 %collective-permute-start.1 = (f32[256,512]{0,1:T(8,128)S(1)}, f32[256,512]{0,1:T(8,128)}, u32[]{:S(2)}, u32[]{:S(2)}) collective-permute-start(f32[256,512]{0,1:T(8,128)S(1)} %pad_maximum_fusion.9), channel_id=1, source_target_pairs={{56,0},{60,4},{0,8},{4,12},{8,16},{12,20},{16,24},{20,28},{24,32},... | collective-permute-start | bytes 1572872 | tf_op jit(solution)/shard_map/while/body/eval_jaxpr/ppermute | solution.py:20
  94.8 1.1 copy-start.5
  107.7 9.9 %collective-permute-start = (f32[256,512]{0,1:T(8,128)S(1)}, f32[256,512]{0,1:T(8,128)}, u32[]{:S(2)}, u32[]{:S(2)}) collective-permute-start(f32[256,512]{0,1:T(8,128)S(1)} %pad_maximum_fusion.8), channel_id=1, source_target_pairs={{8,0},{12,4},{16,8},{20,12},{24,16},{28,20},{32,24},{36,28},{40,32... | collective-permute-start | bytes 1572872 | tf_op jit(solution)/shard_map/while/body/eval_jaxpr/ppermute | solution.py:20
  108.1 11.1 %collective-permute-start.1 = (f32[256,512]{0,1:T(8,128)S(1)}, f32[256,512]{0,1:T(8,128)}, u32[]{:S(2)}, u32[]{:S(2)}) collective-permute-start(f32[256,512]{0,1:T(8,128)S(1)} %pad_maximum_fusion.9), channel_id=1, source_target_pairs={{56,0},{60,4},{0,8},{4,12},{8,16},{12,20},{16,24},{20,28},{24,32},... | collective-permute-start | bytes 1572872 | tf_op jit(solution)/shard_map/while/body/eval_jaxpr/ppermute | solution.py:20
  111.2 1.1 copy-start.5
  123.1 9.4 %collective-permute-start = (f32[256,512]{0,1:T(8,128)S(1)}, f32[256,512]{0,1:T(8,128)}, u32[]{:S(2)}, u32[]{:S(2)}) collective-permute-start(f32[256,512]{0,1:T(8,128)S(1)} %pad_maximum_fusion.8), channel_id=1, source_target_pairs={{8,0},{12,4},{16,8},{20,12},{24,16},{28,20},{32,24},{36,28},{40,32... | collective-permute-start | bytes 1572872 | tf_op jit(solution)/shard_map/while/body/eval_jaxpr/ppermute | solution.py:20
  123.5 10.6 %collective-permute-start.1 = (f32[256,512]{0,1:T(8,128)S(1)}, f32[256,512]{0,1:T(8,128)}, u32[]{:S(2)}, u32[]{:S(2)}) collective-permute-start(f32[256,512]{0,1:T(8,128)S(1)} %pad_maximum_fusion.9), channel_id=1, source_target_pairs={{56,0},{60,4},{0,8},{4,12},{8,16},{12,20},{16,24},{20,28},{24,32},... | collective-permute-start | bytes 1572872 | tf_op jit(solution)/shard_map/while/body/eval_jaxpr/ppermute | solution.py:20
  126.6 1.1 copy-start.5
  137.6 1.0 copy-start.6
  137.7 1.1 copy-start.7
  138.4 1.2 copy-start.2
  141.0 8.8 %collective-permute-start.5 = (f32[256,256]{1,0:T(8,128)S(1)}, f32[256,256]{1,0:T(8,128)S(1)}, u32[]{:S(2)}, u32[]{:S(2)}) collective-permute-start(f32[256,256]{1,0:T(8,128)S(1)} %get-tuple-element.457), channel_id=1, source_target_pairs={{8,0},{12,4},{16,8},{20,12},{24,16},{28,20},{32,24},{36,28},{40,32... | collective-permute-start | bytes 786440 | tf_op jit(solution)/shard_map/ppermute | solution.py:20
  141.1 9.9 %collective-permute-start.6 = (f32[256,256]{1,0:T(8,128)S(1)}, f32[256,256]{1,0:T(8,128)S(1)}, u32[]{:S(2)}, u32[]{:S(2)}) collective-permute-start(f32[256,256]{1,0:T(8,128)S(1)} %get-tuple-element.458), channel_id=1, source_target_pairs={{56,0},{60,4},{0,8},{4,12},{8,16},{12,20},{16,24},{20,28},{24,32},... | collective-permute-start | bytes 786440 | tf_op jit(solution)/shard_map/ppermute | solution.py:20
  151.0 6.5 %collective-permute-start.7 = (f32[256,256]{1,0:T(8,128)S(1)}, f32[256,256]{1,0:T(8,128)S(1)}, u32[]{:S(2)}, u32[]{:S(2)}) collective-permute-start(f32[256,256]{1,0:T(8,128)S(1)} %get-tuple-element.647), channel_id=1, source_target_pairs={{0,56},{4,12},{8,0},{12,20},{16,8},{20,28},{24,16},{28,36},{32,24}... | collective-permute-start | bytes 786440 | tf_op jit(solution)/shard_map/ppermute | solution.py:31
  151.5 8.8 %collective-permute-start.8 = (f32[256,256]{1,0:T(8,128)S(1)}, f32[256,256]{1,0:T(8,128)S(1)}, u32[]{:S(2)}, u32[]{:S(2)}) collective-permute-start(f32[256,256]{1,0:T(8,128)S(1)} %get-tuple-element.646), channel_id=1, source_target_pairs={{0,12},{4,56},{8,20},{12,0},{16,28},{20,8},{24,36},{28,16},{32,44}... | collective-permute-start | bytes 786440 | tf_op jit(solution)/shard_map/ppermute | solution.py:31

commit v10 on v8

--- a/solution.py
+++ b/solution.py
@@ -91,13 +91,19 @@
     super_rows = Y_HI * tok_rows
     offsets = jnp.arange(tok_rows, dtype=jnp.int32)
 
-    def terms(ahead_kv, behind_kv, turn):
+    def key_positions(turn):
         ahead_owner = (z_pos + turn) % z_count
         behind_owner = (z_pos - turn) % z_count
-        key_pos = jnp.concatenate(
+        return jnp.concatenate(
             [ahead_owner * super_rows + offsets, behind_owner * super_rows + tok_rows + offsets]
         )
-        live_mask = live_region(block_mask, query_start, tok_rows, key_pos)
+
+    all_masks = jax.vmap(
+        lambda turn: live_region(block_mask, query_start, tok_rows, key_positions(turn))
+    )(jnp.arange(z_count, dtype=jnp.int32))
+
+    def terms(ahead_kv, behind_kv, turn):
+        live_mask = lax.dynamic_index_in_dim(all_masks, turn, 0, keepdims=False)
         key_values = jnp.concatenate([ahead_kv, behind_kv], axis=0)
         query_term, key_term, value_term = contract(
             queries,

time: 139 us -> 140 us (level)
  other arithmetic: 11.2 us -> 9.52 us
    broadcast_in_dim x0 -> x9, local copies, waits for them, and re-layouts: none -> 6.03 us  [the longest x7 5.85 us: contract(): jnp.where(live_mask[None], jnp.exp(scores - log_sums[:, :, None]), 0.0)]
    gather x8 -> x2, local copies, waits for them, and re-layouts: 4.47 us -> 0.71 us  [live_region(): block_table = jnp.take(query_rows, key_pos[::BLK] // BLK, axis=1)]
    unnamed x21 -> x25, local copies, waits for them, and re-layouts: 5.02 us -> 4.97 us
  transfers between devices with their start and end apart: 32 -> 32, of which waited for: 4 -> 7; matrix products, arithmetic and copies ran while one was open for 46% -> 44% of each run, Pallas kernels for 0% -> 0%
where the time goes in v10:
time: 140 us; the launch traced here: 138 us
  starting transfers between devices  50.8 us (36%)
  matrix products  43.6 us (31%)
  local copies, waits for them, and re-layouts  18.6 us (13%)
  waiting for transfers between devices  13.8 us (10%)
  other arithmetic  9.52 us (7%)
    ppermute x28, starting transfers between devices, along_z(): return lax.ppermute(value, 'ctx', pairs)  42.2 us
    dot_general x8, matrix products, contract(): jnp.einsum('igd,jd->gij', out_grads, values_part, preferred_element_type=...  12.5 us
    dot_general x8, matrix products, contract(): jnp.einsum('gij,igd->jd', probabilities.astype(jnp.bfloat16), out_grads,...  10.3 us
    ppermute x28, waiting for transfers between devices, along_z(): return lax.ppermute(value, 'ctx', pairs)  8.03 us
    dot_general x8, matrix products, contract(): jnp.einsum('gij,igd->jd', dscore, queries, preferred_element_type=jnp.flo...  7.9 us
    dot_general x8, matrix products, contract(): jnp.einsum('igd,jd->gij', queries, keys_part, preferred_element_type=jnp....  7.49 us
    broadcast_in_dim x7, local copies, waits for them, and re-layouts, contract(): jnp.where(live_mask[None], jnp.exp(scores - log_sums[:, :, None]), 0.0)  5.85 us
    ppermute x2, waiting for transfers between devices, to_owner(): return lax.ppermute(value, 'ctx', pairs)  5.81 us
  transfers between devices with their start and end apart: 32, of which 7 were waited for; matrix products, arithmetic and copies ran while one was open for 44% of the time, Pallas kernels for 0%

profile of v10, /device:TPU:4, one launch (start us, length us, event | category | flops | bytes accessed | tf_op | source)
XLA Modules:
  0.0 138.3 jit_solution(5261916428198379179)
XLA Ops:
  0.6 0.9 constant_dynamic-update-slice_fusion.3
  1.5 0.9 constant_dynamic-update-slice_fusion.2
  2.4 3.3 %collective-permute-start.4 = (bf16[256,256]{1,0:T(8,128)(2,1)S(1)}, bf16[256,256]{1,0:T(8,128)(2,1)S(1)}, u32[]{:S(2)}, u32[]{:S(2)}) collective-permute-start(bf16[256,256]{1,0:T(8,128)(2,1)S(1)} %constant_dynamic-update-slice_fusion.2), channel_id=1, source_target_pairs={{0,4},{4,0},{8,12},{12,8},{16,20},{20,16},{24,28},{28,24},{32,36},... | collective-permute-start | bytes 393224 | tf_op jit(solution)/shard_map/ppermute | solution.py:36
  5.7 1.9 %copy.140 = bf16[8,4,8,1024]{3,2,0,1:T(8,128)(2,1)} copy(bf16[8,4,8,1024]{3,2,1,0:T(8,128)(2,1)} %bitcast.191) | data formatting | bytes 1048576 | tf_op jit(solution)/shard_map/reshape | solution.py:81
  7.5 3.5 %all-to-all-start = ((bf16[64,4,1024]{2,0,1:T(8,128)(2,1)}), bf16[64,4,1024]{2,0,1:T(8,128)(2,1)S(1)}, u32[]{:S(2)}, u32[]{:S(2)}) async-start(bf16[64,4,1024]{2,0,1:T(8,128)(2,1)} %bitcast.148), calls=%async_computation | async-start | bytes 1048576 | tf_op jit(solution)/shard_map/all_to_all | solution.py:82
  12.6 1.2 copy.82
  13.8 1.2 copy.86
  15.4 1.7 %fusion.26 = pred[8,256,512]{1,2,0:T(8,128)(4,1)S(1)} fusion(s32[256]{0:T(256)S(1)} %get-tuple-element.355, s32[8,512]{1,0:T(8,128)S(1)} %get-tuple-element.353, s32[256]{0:T(256)S(1)} %get-tuple-element.354, s32[8,512]{1,0:T(8,128)S(1)} %get-tuple-element.352, pred[8,256,4]{1,2,0:T(4,128)(4,1)S(1)} %copy.81), kind=kLoop, calls=%fused_computation.41 | loop fusion | flops 6291456 | bytes 1091584 | tf_op jit(solution)/shard_map/vmap()/or | solution.py:48
  17.2 2.0 %collective-permute-start.6 = (bf16[256,256]{1,0:T(8,128)(2,1)S(1)}, bf16[256,256]{1,0:T(8,128)(2,1)S(1)}, u32[]{:S(2)}, u32[]{:S(2)}) collective-permute-start(bf16[256,256]{1,0:T(8,128)(2,1)S(1)} %get-tuple-element.350), channel_id=1, source_target_pairs={{56,0},{60,4},{0,8},{4,12},{8,16},{12,20},{16,24},{20,28},{24,32},... | collective-permute-start | bytes 393224 | tf_op jit(solution)/shard_map/ppermute | solution.py:20
  19.2 4.8 %collective-permute-start.5 = (bf16[256,256]{1,0:T(8,128)(2,1)S(1)}, bf16[256,256]{1,0:T(8,128)(2,1)S(1)}, u32[]{:S(2)}, u32[]{:S(2)}) collective-permute-start(bf16[256,256]{1,0:T(8,128)(2,1)S(1)} %get-tuple-element.351), channel_id=1, source_target_pairs={{8,0},{12,4},{16,8},{20,12},{24,16},{28,20},{32,24},{36,28},{40,32... | collective-permute-start | bytes 393224 | tf_op jit(solution)/shard_map/ppermute | solution.py:20
  24.0 2.7 %fusion.54 = f32[512,256,8]{1,0,2:T(8,128)} fusion(bf16[256,8,128]{0,2,1:T(8,128)(2,1)S(1)} %bitcast.181, bf16[256,256]{1,0:T(8,128)(2,1)S(1)} %get-tuple-element.351, bf16[256,256]{1,0:T(8,128)(2,1)S(1)} %get-tuple-element.350), kind=kOutput, calls=%fused_computation.92 | convolution fusion | flops 268697600 | bytes 4980736 | tf_op jit(solution)/shard_map/igd,jd->gij/dot_general | solution.py:54
  27.6 3.4 %fusion.35 = f32[512,128]{0,1:T(8,128)S(1)} fusion(bf16[256,8,128]{0,2,1:T(8,128)(2,1)S(1)} %copy.93, f32[512,256,8]{1,0,2:T(8,128)} %fusion.54, f32[8,256]{1,0:T(8,128)} %param.14, pred[256,512]{0,1:T(8,128)(4,1)S(1)} %get-tuple-element.347), kind=kOutput, calls=%fused_computation.50 | convolution fusion | flops 272629760 | bytes 5120000 | tf_op jit(solution)/shard_map/gij,igd->jd/dot_general | solution.py:64
  31.0 1.4 %fusion.23 = bf16[8,256,512]{1,2,0:T(8,128)(2,1)S(1)} fusion(f32[512,256,8]{1,0,2:T(8,128)S(1)} %copy-done.1, f32[8,256]{1,0:T(8,128)S(1)} %copy.88, f32[8,256]{1,0:T(8,128)S(1)} %copy-done.9, pred[256,512]{0,1:T(8,128)(4,1)S(1)} %get-tuple-element.347, bf16[256,8,128]{2,1,0:T(8,128)(2,1)S(1)} %bitcast.186, bf16[256,256]{1,0:T(8,128)(2,1)S(1)} %get-tuple-element.350, ...), kind=kOutput, calls=%fused_computation.36 | convolution fusion | flops 274989056 | bytes 7225344 | tf_op jit(solution)/shard_map/igd,jd->gij/dot_general | solution.py:58
  34.6 75.6 %while.23 = (s32[]{:T(128)}, bf16[256,256]{1,0:T(8,128)(2,1)S(1)}, bf16[256,256]{1,0:T(8,128)(2,1)S(1)}, f32[256,8,128]{0,2,1:T(8,128)S(1)}, f32[256,256]{0,1:T(...) while((s32[]{:T(128)}, bf16[256,256]{1,0:T(8,128)(2,1)S(1)}, ...), condition=%wide.region_2.3_spmd, body=%wide.region_1.2_spmd.sunk | while | flops 1353187328 | bytes 32465312 | solution.py:143
  34.8 1.2 collective-permute-start
  36.0 0.9 collective-permute-start.1
  37.0 3.1 %collective-permute-start.3 = (f32[256,256]{0,1:T(8,128)}, f32[256,256]{0,1:T(8,128)S(1)}, u32[]{:S(2)}, u32[]{:S(2)}) collective-permute-start(f32[256,256]{0,1:T(8,128)} %get-tuple-element.447), channel_id=1, source_target_pairs={{8,0},{12,4},{16,8},{20,12},{24,16},{28,20},{32,24},{36,28},{40,32... | collective-permute-start | bytes 786440 | tf_op jit(solution)/shard_map/while/body/eval_jaxpr/ppermute | solution.py:20
  40.3 1.0 dynamic-slice_bitcast_fusion.2
  42.0 1.0 fusion.112
  43.0 1.4 fusion.110
  45.7 2.4 %collective-permute-done.2 = f32[256,256]{0,1:T(8,128)S(1)} collective-permute-done((f32[256,256]{0,1:T(8,128)}, f32[256,256]{0,1:T(8,128)S(1)}, u32[]{:S(2)}, u32[]{:S(2)}) %collective-permute-start.2) | collective-permute-done | bytes 262176 | tf_op jit(solution)/shard_map/while/body/eval_jaxpr/ppermute | solution.py:20
  48.1 0.9 fusion.113
  49.0 1.2 collective-permute-start
  50.2 1.0 collective-permute-start.1
  51.3 3.1 %collective-permute-start.3 = (f32[256,256]{0,1:T(8,128)}, f32[256,256]{0,1:T(8,128)S(1)}, u32[]{:S(2)}, u32[]{:S(2)}) collective-permute-start(f32[256,256]{0,1:T(8,128)} %get-tuple-element.447), channel_id=1, source_target_pairs={{8,0},{12,4},{16,8},{20,12},{24,16},{28,20},{32,24},{36,28},{40,32... | collective-permute-start | bytes 786440 | tf_op jit(solution)/shard_map/while/body/eval_jaxpr/ppermute | solution.py:20
  54.5 1.0 dynamic-slice_bitcast_fusion.2
  56.2 1.0 fusion.112
  57.2 1.4 fusion.110
  60.6 0.9 fusion.113
  61.5 1.7 %collective-permute-start = (bf16[256,256]{1,0:T(8,128)(2,1)S(1)}, bf16[256,256]{1,0:T(8,128)(2,1)S(1)}, u32[]{:S(2)}, u32[]{:S(2)}) collective-permute-start(bf16[256,256]{1,0:T(8,128)(2,1)S(1)} %copy.150), channel_id=1, source_target_pairs={{8,0},{12,4},{16,8},{20,12},{24,16},{28,20},{32,24},{36,28},{40,32... | collective-permute-start | bytes 393224 | tf_op jit(solution)/shard_map/while/body/eval_jaxpr/ppermute | solution.py:20
  63.9 3.1 %collective-permute-start.3 = (f32[256,256]{0,1:T(8,128)}, f32[256,256]{0,1:T(8,128)S(1)}, u32[]{:S(2)}, u32[]{:S(2)}) collective-permute-start(f32[256,256]{0,1:T(8,128)} %get-tuple-element.447), channel_id=1, source_target_pairs={{8,0},{12,4},{16,8},{20,12},{24,16},{28,20},{32,24},{36,28},{40,32... | collective-permute-start | bytes 786440 | tf_op jit(solution)/shard_map/while/body/eval_jaxpr/ppermute | solution.py:20
  67.0 1.0 dynamic-slice_bitcast_fusion.2
  68.7 1.0 fusion.112
  69.8 1.4 fusion.110
  72.5 0.9 fusion.113
  73.4 2.3 %collective-permute-start = (bf16[256,256]{1,0:T(8,128)(2,1)S(1)}, bf16[256,256]{1,0:T(8,128)(2,1)S(1)}, u32[]{:S(2)}, u32[]{:S(2)}) collective-permute-start(bf16[256,256]{1,0:T(8,128)(2,1)S(1)} %copy.150), channel_id=1, source_target_pairs={{8,0},{12,4},{16,8},{20,12},{24,16},{28,20},{32,24},{36,28},{40,32... | collective-permute-start | bytes 393224 | tf_op jit(solution)/shard_map/while/body/eval_jaxpr/ppermute | solution.py:20
  76.0 3.2 %collective-permute-start.3 = (f32[256,256]{0,1:T(8,128)}, f32[256,256]{0,1:T(8,128)S(1)}, u32[]{:S(2)}, u32[]{:S(2)}) collective-permute-start(f32[256,256]{0,1:T(8,128)} %get-tuple-element.447), channel_id=1, source_target_pairs={{8,0},{12,4},{16,8},{20,12},{24,16},{28,20},{32,24},{36,28},{40,32... | collective-permute-start | bytes 786440 | tf_op jit(solution)/shard_map/while/body/eval_jaxpr/ppermute | solution.py:20
  79.2 1.0 dynamic-slice_bitcast_fusion.2
  81.0 1.0 fusion.112
  82.0 1.4 fusion.110
  84.8 0.9 fusion.113
  85.8 2.2 %collective-permute-start = (bf16[256,256]{1,0:T(8,128)(2,1)S(1)}, bf16[256,256]{1,0:T(8,128)(2,1)S(1)}, u32[]{:S(2)}, u32[]{:S(2)}) collective-permute-start(bf16[256,256]{1,0:T(8,128)(2,1)S(1)} %copy.150), channel_id=1, source_target_pairs={{8,0},{12,4},{16,8},{20,12},{24,16},{28,20},{32,24},{36,28},{40,32... | collective-permute-start | bytes 393224 | tf_op jit(solution)/shard_map/while/body/eval_jaxpr/ppermute | solution.py:20
  88.5 2.9 %collective-permute-start.3 = (f32[256,256]{0,1:T(8,128)}, f32[256,256]{0,1:T(8,128)S(1)}, u32[]{:S(2)}, u32[]{:S(2)}) collective-permute-start(f32[256,256]{0,1:T(8,128)} %get-tuple-element.447), channel_id=1, source_target_pairs={{8,0},{12,4},{16,8},{20,12},{24,16},{28,20},{32,24},{36,28},{40,32... | collective-permute-start | bytes 786440 | tf_op jit(solution)/shard_map/while/body/eval_jaxpr/ppermute | solution.py:20
  91.5 1.0 dynamic-slice_bitcast_fusion.2
  93.2 1.0 fusion.112
  94.2 1.4 fusion.110
  97.1 0.9 fusion.113
  98.0 2.2 %collective-permute-start = (bf16[256,256]{1,0:T(8,128)(2,1)S(1)}, bf16[256,256]{1,0:T(8,128)(2,1)S(1)}, u32[]{:S(2)}, u32[]{:S(2)}) collective-permute-start(bf16[256,256]{1,0:T(8,128)(2,1)S(1)} %copy.150), channel_id=1, source_target_pairs={{8,0},{12,4},{16,8},{20,12},{24,16},{28,20},{32,24},{36,28},{40,32... | collective-permute-start | bytes 393224 | tf_op jit(solution)/shard_map/while/body/eval_jaxpr/ppermute | solution.py:20
  100.8 2.9 %collective-permute-start.3 = (f32[256,256]{0,1:T(8,128)}, f32[256,256]{0,1:T(8,128)S(1)}, u32[]{:S(2)}, u32[]{:S(2)}) collective-permute-start(f32[256,256]{0,1:T(8,128)} %get-tuple-element.447), channel_id=1, source_target_pairs={{8,0},{12,4},{16,8},{20,12},{24,16},{28,20},{32,24},{36,28},{40,32... | collective-permute-start | bytes 786440 | tf_op jit(solution)/shard_map/while/body/eval_jaxpr/ppermute | solution.py:20
  103.7 1.0 dynamic-slice_bitcast_fusion.2
  105.4 1.0 fusion.112
  106.4 1.4 fusion.110
  109.3 0.9 fusion.113
  111.2 0.9 fusion.38
  112.1 2.8 %fusion.19 = bf16[8,256,512]{1,2,0:T(8,128)(2,1)} fusion(f32[512,256,8]{1,0,2:T(8,128)S(1)} %fusion.53, f32[8,256]{1,0:T(8,128)S(1)} %copy-done.8, f32[8,256]{1,0:T(8,128)S(1)} %copy-done.11, pred[256,512]{0,1:T(8,128)(4,1)S(1)} %get-tuple-element.346, bf16[256,8,128]{2,1,0:T(8,128)(2,1)S(1)} %bitcast.187, ...), kind=kOutput, calls=%fused_computation.30 | convolution fusion | flops 274726912 | bytes 7094272 | tf_op jit(solution)/shard_map/igd,jd->gij/dot_general | solution.py:58
  114.9 1.1 copy.106
  116.0 1.1 copy.100
  117.0 2.2 %collective-permute-start.7 = (f32[256,256]{1,0:T(8,128)S(1)}, f32[256,256]{1,0:T(8,128)S(1)}, u32[]{:S(2)}, u32[]{:S(2)}) collective-permute-start(f32[256,256]{1,0:T(8,128)S(1)} %copy.100), channel_id=1, source_target_pairs={{8,0},{12,4},{16,8},{20,12},{24,16},{28,20},{32,24},{36,28},{40,32... | collective-permute-start | bytes 786440 | tf_op jit(solution)/shard_map/ppermute | solution.py:20
  119.3 2.1 %convolution_bitcast_fusion.2 = f32[256,8,128]{0,2,1:T(8,128)S(1)} fusion(bf16[8,256,512]{1,2,0:T(8,128)(2,1)} %fusion.19, bf16[512,256]{1,0:T(8,128)(2,1)S(1)} %constant_dynamic-update-slice_fusion.4), kind=kOutput, calls=%fused_computation.48 | convolution fusion | flops 268435456 | bytes 3276800 | tf_op jit(solution)/shard_map/gij,jd->igd/dot_general | solution.py:62
  121.3 2.3 %convolution_bitcast_fusion.4 = f32[512,128]{1,0:T(8,128)S(1)} fusion(bf16[8,256,512]{1,2,0:T(8,128)(2,1)} %fusion.19, bf16[256,8,128]{0,2,1:T(8,128)(2,1)S(1)} %get-tuple-element.471), kind=kOutput, calls=%fused_computation.52 | convolution fusion | flops 268435456 | bytes 2883584 | tf_op jit(solution)/shard_map/gij,igd->jd/dot_general | solution.py:63
  123.6 4.4 %collective-permute-done.8 = f32[256,256]{1,0:T(8,128)S(1)} collective-permute-done((f32[256,256]{1,0:T(8,128)S(1)}, f32[256,256]{1,0:T(8,128)S(1)}, u32[]{:S(2)}, u32[]{:S(2)}) %collective-permute-start.8) | collective-permute-done | bytes 262176 | tf_op jit(solution)/shard_map/ppermute | solution.py:20
  128.2 1.8 %collective-permute-start.9 = (f32[256,256]{1,0:T(8,128)S(1)}, f32[256,256]{1,0:T(8,128)S(1)}, u32[]{:S(2)}, u32[]{:S(2)}) collective-permute-start(f32[256,256]{1,0:T(8,128)S(1)} %get-tuple-element.345), channel_id=1, source_target_pairs={{0,56},{4,12},{8,0},{12,20},{16,8},{20,28},{24,16},{28,36},{32,24}... | collective-permute-start | bytes 786440 | tf_op jit(solution)/shard_map/ppermute | solution.py:31
  130.2 1.0 copy.107
  131.2 5.8 %collective-permute-done.10 = f32[256,256]{1,0:T(8,128)S(1)} collective-permute-done((f32[256,256]{1,0:T(8,128)S(1)}, f32[256,256]{1,0:T(8,128)S(1)}, u32[]{:S(2)}, u32[]{:S(2)}) %collective-permute-start.10) | collective-permute-done | bytes 262176 | tf_op jit(solution)/shard_map/ppermute | solution.py:31
  (173 shorter events, 23.0 us)
Async XLA Ops:
  0.6 10.6 %copy-start = (s32[32,32]{1,0:T(8,128)S(1)}, s32[32,32]{1,0:T(8,128)}, u32[]{:S(2)}) copy-start(s32[32,32]{1,0:T(8,128)} %param.15) | copy-start | bytes 12292
  2.4 14.8 %collective-permute-start.4 = (bf16[256,256]{1,0:T(8,128)(2,1)S(1)}, bf16[256,256]{1,0:T(8,128)(2,1)S(1)}, u32[]{:S(2)}, u32[]{:S(2)}) collective-permute-start(bf16[256,256]{1,0:T(8,128)(2,1)S(1)} %constant_dynamic-update-slice_fusion.2), channel_id=1, source_target_pairs={{0,4},{4,0},{8,12},{12,8},{16,20},{20,16},{24,28},{28,24},{32,36},... | collective-permute-start | bytes 393224 | tf_op jit(solution)/shard_map/ppermute | solution.py:36
  7.5 19.2 %all-to-all-start = ((bf16[64,4,1024]{2,0,1:T(8,128)(2,1)}), bf16[64,4,1024]{2,0,1:T(8,128)(2,1)S(1)}, u32[]{:S(2)}, u32[]{:S(2)}) async-start(bf16[64,4,1024]{2,0,1:T(8,128)(2,1)} %bitcast.148), calls=%async_computation | async-start | bytes 1048576 | tf_op jit(solution)/shard_map/all_to_all | solution.py:82
  17.2 2.1 %copy-start.2 = (pred[8,256,512]{1,2,0:T(8,128)(4,1)}, pred[8,256,512]{1,2,0:T(8,128)(4,1)S(1)}, u32[]{:S(2)}) copy-start(pred[8,256,512]{1,2,0:T(8,128)(4,1)S(1)} %fusion.26) | copy-start | bytes 3145732
  17.2 17.4 %collective-permute-start.6 = (bf16[256,256]{1,0:T(8,128)(2,1)S(1)}, bf16[256,256]{1,0:T(8,128)(2,1)S(1)}, u32[]{:S(2)}, u32[]{:S(2)}) collective-permute-start(bf16[256,256]{1,0:T(8,128)(2,1)S(1)} %get-tuple-element.350), channel_id=1, source_target_pairs={{56,0},{60,4},{0,8},{4,12},{8,16},{12,20},{16,24},{20,28},{24,32},... | collective-permute-start | bytes 393224 | tf_op jit(solution)/shard_map/ppermute | solution.py:20
  19.2 15.4 %collective-permute-start.5 = (bf16[256,256]{1,0:T(8,128)(2,1)S(1)}, bf16[256,256]{1,0:T(8,128)(2,1)S(1)}, u32[]{:S(2)}, u32[]{:S(2)}) collective-permute-start(bf16[256,256]{1,0:T(8,128)(2,1)S(1)} %get-tuple-element.351), channel_id=1, source_target_pairs={{8,0},{12,4},{16,8},{20,12},{24,16},{28,20},{32,24},{36,28},{40,32... | collective-permute-start | bytes 393224 | tf_op jit(solution)/shard_map/ppermute | solution.py:20
  27.1 5.3 %copy-start.3 = (bf16[256,8,128]{0,2,1:T(8,128)(2,1)}, bf16[256,8,128]{0,2,1:T(8,128)(2,1)S(1)}, u32[]{:S(2)}) copy-start(bf16[256,8,128]{0,2,1:T(8,128)(2,1)S(1)} %copy.93) | copy-start | bytes 1572868
  27.5 3.4 %copy-start.9 = (f32[8,256]{1,0:T(8,128)S(1)}, f32[8,256]{1,0:T(8,128)}, u32[]{:S(2)}) copy-start(f32[8,256]{1,0:T(8,128)} %param.14) | copy-start | bytes 24580
  27.6 3.4 %copy-start.6 = (f32[8,256]{1,0:T(8,128)}, f32[8,256]{1,0:T(8,128)S(1)}, u32[]{:S(2)}) copy-start(f32[8,256]{1,0:T(8,128)S(1)} %copy.88) | copy-start | bytes 24580
  27.6 3.5 %copy-start.1 = (f32[512,256,8]{1,0,2:T(8,128)S(1)}, f32[512,256,8]{1,0,2:T(8,128)}, u32[]{:S(2)}) copy-start(f32[512,256,8]{1,0,2:T(8,128)} %fusion.54) | copy-start | bytes 12582916
  34.8 14.2 %collective-permute-start = (bf16[256,256]{1,0:T(8,128)(2,1)S(1)}, bf16[256,256]{1,0:T(8,128)(2,1)S(1)}, u32[]{:S(2)}, u32[]{:S(2)}) collective-permute-start(bf16[256,256]{1,0:T(8,128)(2,1)S(1)} %copy.150), channel_id=1, source_target_pairs={{8,0},{12,4},{16,8},{20,12},{24,16},{28,20},{32,24},{36,28},{40,32... | collective-permute-start | bytes 393224 | tf_op jit(solution)/shard_map/while/body/eval_jaxpr/ppermute | solution.py:20
  36.0 12.9 %collective-permute-start.1 = (bf16[256,256]{1,0:T(8,128)(2,1)S(1)}, bf16[256,256]{1,0:T(8,128)(2,1)S(1)}, u32[]{:S(2)}, u32[]{:S(2)}) collective-permute-start(bf16[256,256]{1,0:T(8,128)(2,1)S(1)} %copy.151), channel_id=1, source_target_pairs={{56,0},{60,4},{0,8},{4,12},{8,16},{12,20},{16,24},{20,28},{24,32},... | collective-permute-start | bytes 393224 | tf_op jit(solution)/shard_map/while/body/eval_jaxpr/ppermute | solution.py:20
  37.0 11.1 %collective-permute-start.2 = (f32[256,256]{0,1:T(8,128)}, f32[256,256]{0,1:T(8,128)S(1)}, u32[]{:S(2)}, u32[]{:S(2)}) collective-permute-start(f32[256,256]{0,1:T(8,128)} %get-tuple-element.448), channel_id=1, source_target_pairs={{56,0},{60,4},{0,8},{4,12},{8,16},{12,20},{16,24},{20,28},{24,32},... | collective-permute-start | bytes 786440 | tf_op jit(solution)/shard_map/while/body/eval_jaxpr/ppermute | solution.py:20
  37.0 11.0 %collective-permute-start.3 = (f32[256,256]{0,1:T(8,128)}, f32[256,256]{0,1:T(8,128)S(1)}, u32[]{:S(2)}, u32[]{:S(2)}) collective-permute-start(f32[256,256]{0,1:T(8,128)} %get-tuple-element.447), channel_id=1, source_target_pairs={{8,0},{12,4},{16,8},{20,12},{24,16},{28,20},{32,24},{36,28},{40,32... | collective-permute-start | bytes 786440 | tf_op jit(solution)/shard_map/while/body/eval_jaxpr/ppermute | solution.py:20
  40.2 1.7 %copy-start.4 = (bf16[256,8,128]{0,2,1:T(8,128)(2,1)S(1)}, bf16[256,8,128]{0,2,1:T(8,128)(2,1)}, u32[]{:S(2)}) copy-start(bf16[256,8,128]{0,2,1:T(8,128)(2,1)} %get-tuple-element.466) | copy-start | bytes 1572868 | tf_op jit(solution)/shard_map/while
  40.3 1.7 %copy-start.10 = (f32[8,256]{1,0:T(8,128)S(1)}, f32[8,256]{1,0:T(8,128)}, u32[]{:S(2)}) copy-start(f32[8,256]{1,0:T(8,128)} %get-tuple-element.465) | copy-start | bytes 24580 | tf_op jit(solution)/shard_map/while
  41.9 1.1 copy-start.7
  49.0 12.5 %collective-permute-start = (bf16[256,256]{1,0:T(8,128)(2,1)S(1)}, bf16[256,256]{1,0:T(8,128)(2,1)S(1)}, u32[]{:S(2)}, u32[]{:S(2)}) collective-permute-start(bf16[256,256]{1,0:T(8,128)(2,1)S(1)} %copy.150), channel_id=1, source_target_pairs={{8,0},{12,4},{16,8},{20,12},{24,16},{28,20},{32,24},{36,28},{40,32... | collective-permute-start | bytes 393224 | tf_op jit(solution)/shard_map/while/body/eval_jaxpr/ppermute | solution.py:20
  50.2 11.3 %collective-permute-start.1 = (bf16[256,256]{1,0:T(8,128)(2,1)S(1)}, bf16[256,256]{1,0:T(8,128)(2,1)S(1)}, u32[]{:S(2)}, u32[]{:S(2)}) collective-permute-start(bf16[256,256]{1,0:T(8,128)(2,1)S(1)} %copy.151), channel_id=1, source_target_pairs={{56,0},{60,4},{0,8},{4,12},{8,16},{12,20},{16,24},{20,28},{24,32},... | collective-permute-start | bytes 393224 | tf_op jit(solution)/shard_map/while/body/eval_jaxpr/ppermute | solution.py:20
  51.2 9.4 %collective-permute-start.2 = (f32[256,256]{0,1:T(8,128)}, f32[256,256]{0,1:T(8,128)S(1)}, u32[]{:S(2)}, u32[]{:S(2)}) collective-permute-start(f32[256,256]{0,1:T(8,128)} %get-tuple-element.448), channel_id=1, source_target_pairs={{56,0},{60,4},{0,8},{4,12},{8,16},{12,20},{16,24},{20,28},{24,32},... | collective-permute-start | bytes 786440 | tf_op jit(solution)/shard_map/while/body/eval_jaxpr/ppermute | solution.py:20
  51.3 9.3 %collective-permute-start.3 = (f32[256,256]{0,1:T(8,128)}, f32[256,256]{0,1:T(8,128)S(1)}, u32[]{:S(2)}, u32[]{:S(2)}) collective-permute-start(f32[256,256]{0,1:T(8,128)} %get-tuple-element.447), channel_id=1, source_target_pairs={{8,0},{12,4},{16,8},{20,12},{24,16},{28,20},{32,24},{36,28},{40,32... | collective-permute-start | bytes 786440 | tf_op jit(solution)/shard_map/while/body/eval_jaxpr/ppermute | solution.py:20
  54.5 1.7 %copy-start.4 = (bf16[256,8,128]{0,2,1:T(8,128)(2,1)S(1)}, bf16[256,8,128]{0,2,1:T(8,128)(2,1)}, u32[]{:S(2)}) copy-start(bf16[256,8,128]{0,2,1:T(8,128)(2,1)} %get-tuple-element.466) | copy-start | bytes 1572868 | tf_op jit(solution)/shard_map/while
  54.5 1.7 %copy-start.10 = (f32[8,256]{1,0:T(8,128)S(1)}, f32[8,256]{1,0:T(8,128)}, u32[]{:S(2)}) copy-start(f32[8,256]{1,0:T(8,128)} %get-tuple-element.465) | copy-start | bytes 24580 | tf_op jit(solution)/shard_map/while
  56.2 1.1 copy-start.7
  61.5 11.9 %collective-permute-start = (bf16[256,256]{1,0:T(8,128)(2,1)S(1)}, bf16[256,256]{1,0:T(8,128)(2,1)S(1)}, u32[]{:S(2)}, u32[]{:S(2)}) collective-permute-start(bf16[256,256]{1,0:T(8,128)(2,1)S(1)} %copy.150), channel_id=1, source_target_pairs={{8,0},{12,4},{16,8},{20,12},{24,16},{28,20},{32,24},{36,28},{40,32... | collective-permute-start | bytes 393224 | tf_op jit(solution)/shard_map/while/body/eval_jaxpr/ppermute | solution.py:20
  63.2 10.2 %collective-permute-start.1 = (bf16[256,256]{1,0:T(8,128)(2,1)S(1)}, bf16[256,256]{1,0:T(8,128)(2,1)S(1)}, u32[]{:S(2)}, u32[]{:S(2)}) collective-permute-start(bf16[256,256]{1,0:T(8,128)(2,1)S(1)} %copy.151), channel_id=1, source_target_pairs={{56,0},{60,4},{0,8},{4,12},{8,16},{12,20},{16,24},{20,28},{24,32},... | collective-permute-start | bytes 393224 | tf_op jit(solution)/shard_map/while/body/eval_jaxpr/ppermute | solution.py:20
  63.7 8.7 %collective-permute-start.2 = (f32[256,256]{0,1:T(8,128)}, f32[256,256]{0,1:T(8,128)S(1)}, u32[]{:S(2)}, u32[]{:S(2)}) collective-permute-start(f32[256,256]{0,1:T(8,128)} %get-tuple-element.448), channel_id=1, source_target_pairs={{56,0},{60,4},{0,8},{4,12},{8,16},{12,20},{16,24},{20,28},{24,32},... | collective-permute-start | bytes 786440 | tf_op jit(solution)/shard_map/while/body/eval_jaxpr/ppermute | solution.py:20
  63.9 8.6 %collective-permute-start.3 = (f32[256,256]{0,1:T(8,128)}, f32[256,256]{0,1:T(8,128)S(1)}, u32[]{:S(2)}, u32[]{:S(2)}) collective-permute-start(f32[256,256]{0,1:T(8,128)} %get-tuple-element.447), channel_id=1, source_target_pairs={{8,0},{12,4},{16,8},{20,12},{24,16},{28,20},{32,24},{36,28},{40,32... | collective-permute-start | bytes 786440 | tf_op jit(solution)/shard_map/while/body/eval_jaxpr/ppermute | solution.py:20
  67.0 1.7 %copy-start.4 = (bf16[256,8,128]{0,2,1:T(8,128)(2,1)S(1)}, bf16[256,8,128]{0,2,1:T(8,128)(2,1)}, u32[]{:S(2)}) copy-start(bf16[256,8,128]{0,2,1:T(8,128)(2,1)} %get-tuple-element.466) | copy-start | bytes 1572868 | tf_op jit(solution)/shard_map/while
  67.0 1.7 %copy-start.10 = (f32[8,256]{1,0:T(8,128)S(1)}, f32[8,256]{1,0:T(8,128)}, u32[]{:S(2)}) copy-start(f32[8,256]{1,0:T(8,128)} %get-tuple-element.465) | copy-start | bytes 24580 | tf_op jit(solution)/shard_map/while
  68.7 1.1 copy-start.7
  73.4 12.3 %collective-permute-start = (bf16[256,256]{1,0:T(8,128)(2,1)S(1)}, bf16[256,256]{1,0:T(8,128)(2,1)S(1)}, u32[]{:S(2)}, u32[]{:S(2)}) collective-permute-start(bf16[256,256]{1,0:T(8,128)(2,1)S(1)} %copy.150), channel_id=1, source_target_pairs={{8,0},{12,4},{16,8},{20,12},{24,16},{28,20},{32,24},{36,28},{40,32... | collective-permute-start | bytes 393224 | tf_op jit(solution)/shard_map/while/body/eval_jaxpr/ppermute | solution.py:20
  75.8 10.0 %collective-permute-start.1 = (bf16[256,256]{1,0:T(8,128)(2,1)S(1)}, bf16[256,256]{1,0:T(8,128)(2,1)S(1)}, u32[]{:S(2)}, u32[]{:S(2)}) collective-permute-start(bf16[256,256]{1,0:T(8,128)(2,1)S(1)} %copy.151), channel_id=1, source_target_pairs={{56,0},{60,4},{0,8},{4,12},{8,16},{12,20},{16,24},{20,28},{24,32},... | collective-permute-start | bytes 393224 | tf_op jit(solution)/shard_map/while/body/eval_jaxpr/ppermute | solution.py:20
  75.9 9.0 %collective-permute-start.2 = (f32[256,256]{0,1:T(8,128)}, f32[256,256]{0,1:T(8,128)S(1)}, u32[]{:S(2)}, u32[]{:S(2)}) collective-permute-start(f32[256,256]{0,1:T(8,128)} %get-tuple-element.448), channel_id=1, source_target_pairs={{56,0},{60,4},{0,8},{4,12},{8,16},{12,20},{16,24},{20,28},{24,32},... | collective-permute-start | bytes 786440 | tf_op jit(solution)/shard_map/while/body/eval_jaxpr/ppermute | solution.py:20
  76.0 8.9 %collective-permute-start.3 = (f32[256,256]{0,1:T(8,128)}, f32[256,256]{0,1:T(8,128)S(1)}, u32[]{:S(2)}, u32[]{:S(2)}) collective-permute-start(f32[256,256]{0,1:T(8,128)} %get-tuple-element.447), channel_id=1, source_target_pairs={{8,0},{12,4},{16,8},{20,12},{24,16},{28,20},{32,24},{36,28},{40,32... | collective-permute-start | bytes 786440 | tf_op jit(solution)/shard_map/while/body/eval_jaxpr/ppermute | solution.py:20
  79.2 1.7 %copy-start.4 = (bf16[256,8,128]{0,2,1:T(8,128)(2,1)S(1)}, bf16[256,8,128]{0,2,1:T(8,128)(2,1)}, u32[]{:S(2)}) copy-start(bf16[256,8,128]{0,2,1:T(8,128)(2,1)} %get-tuple-element.466) | copy-start | bytes 1572868 | tf_op jit(solution)/shard_map/while
  79.2 1.7 %copy-start.10 = (f32[8,256]{1,0:T(8,128)S(1)}, f32[8,256]{1,0:T(8,128)}, u32[]{:S(2)}) copy-start(f32[8,256]{1,0:T(8,128)} %get-tuple-element.465) | copy-start | bytes 24580 | tf_op jit(solution)/shard_map/while
  80.9 1.1 copy-start.7
  85.8 12.2 %collective-permute-start = (bf16[256,256]{1,0:T(8,128)(2,1)S(1)}, bf16[256,256]{1,0:T(8,128)(2,1)S(1)}, u32[]{:S(2)}, u32[]{:S(2)}) collective-permute-start(bf16[256,256]{1,0:T(8,128)(2,1)S(1)} %copy.150), channel_id=1, source_target_pairs={{8,0},{12,4},{16,8},{20,12},{24,16},{28,20},{32,24},{36,28},{40,32... | collective-permute-start | bytes 393224 | tf_op jit(solution)/shard_map/while/body/eval_jaxpr/ppermute | solution.py:20
  88.0 10.0 %collective-permute-start.1 = (bf16[256,256]{1,0:T(8,128)(2,1)S(1)}, bf16[256,256]{1,0:T(8,128)(2,1)S(1)}, u32[]{:S(2)}, u32[]{:S(2)}) collective-permute-start(bf16[256,256]{1,0:T(8,128)(2,1)S(1)} %copy.151), channel_id=1, source_target_pairs={{56,0},{60,4},{0,8},{4,12},{8,16},{12,20},{16,24},{20,28},{24,32},... | collective-permute-start | bytes 393224 | tf_op jit(solution)/shard_map/while/body/eval_jaxpr/ppermute | solution.py:20
  88.1 9.0 %collective-permute-start.2 = (f32[256,256]{0,1:T(8,128)}, f32[256,256]{0,1:T(8,128)S(1)}, u32[]{:S(2)}, u32[]{:S(2)}) collective-permute-start(f32[256,256]{0,1:T(8,128)} %get-tuple-element.448), channel_id=1, source_target_pairs={{56,0},{60,4},{0,8},{4,12},{8,16},{12,20},{16,24},{20,28},{24,32},... | collective-permute-start | bytes 786440 | tf_op jit(solution)/shard_map/while/body/eval_jaxpr/ppermute | solution.py:20
  88.5 8.6 %collective-permute-start.3 = (f32[256,256]{0,1:T(8,128)}, f32[256,256]{0,1:T(8,128)S(1)}, u32[]{:S(2)}, u32[]{:S(2)}) collective-permute-start(f32[256,256]{0,1:T(8,128)} %get-tuple-element.447), channel_id=1, source_target_pairs={{8,0},{12,4},{16,8},{20,12},{24,16},{28,20},{32,24},{36,28},{40,32... | collective-permute-start | bytes 786440 | tf_op jit(solution)/shard_map/while/body/eval_jaxpr/ppermute | solution.py:20
  91.4 1.7 %copy-start.4 = (bf16[256,8,128]{0,2,1:T(8,128)(2,1)S(1)}, bf16[256,8,128]{0,2,1:T(8,128)(2,1)}, u32[]{:S(2)}) copy-start(bf16[256,8,128]{0,2,1:T(8,128)(2,1)} %get-tuple-element.466) | copy-start | bytes 1572868 | tf_op jit(solution)/shard_map/while
  91.5 1.7 %copy-start.10 = (f32[8,256]{1,0:T(8,128)S(1)}, f32[8,256]{1,0:T(8,128)}, u32[]{:S(2)}) copy-start(f32[8,256]{1,0:T(8,128)} %get-tuple-element.465) | copy-start | bytes 24580 | tf_op jit(solution)/shard_map/while
  93.1 1.1 copy-start.7
  98.0 12.2 %collective-permute-start = (bf16[256,256]{1,0:T(8,128)(2,1)S(1)}, bf16[256,256]{1,0:T(8,128)(2,1)S(1)}, u32[]{:S(2)}, u32[]{:S(2)}) collective-permute-start(bf16[256,256]{1,0:T(8,128)(2,1)S(1)} %copy.150), channel_id=1, source_target_pairs={{8,0},{12,4},{16,8},{20,12},{24,16},{28,20},{32,24},{36,28},{40,32... | collective-permute-start | bytes 393224 | tf_op jit(solution)/shard_map/while/body/eval_jaxpr/ppermute | solution.py:20
  100.2 10.0 %collective-permute-start.1 = (bf16[256,256]{1,0:T(8,128)(2,1)S(1)}, bf16[256,256]{1,0:T(8,128)(2,1)S(1)}, u32[]{:S(2)}, u32[]{:S(2)}) collective-permute-start(bf16[256,256]{1,0:T(8,128)(2,1)S(1)} %copy.151), channel_id=1, source_target_pairs={{56,0},{60,4},{0,8},{4,12},{8,16},{12,20},{16,24},{20,28},{24,32},... | collective-permute-start | bytes 393224 | tf_op jit(solution)/shard_map/while/body/eval_jaxpr/ppermute | solution.py:20
  100.3 9.0 %collective-permute-start.2 = (f32[256,256]{0,1:T(8,128)}, f32[256,256]{0,1:T(8,128)S(1)}, u32[]{:S(2)}, u32[]{:S(2)}) collective-permute-start(f32[256,256]{0,1:T(8,128)} %get-tuple-element.448), channel_id=1, source_target_pairs={{56,0},{60,4},{0,8},{4,12},{8,16},{12,20},{16,24},{20,28},{24,32},... | collective-permute-start | bytes 786440 | tf_op jit(solution)/shard_map/while/body/eval_jaxpr/ppermute | solution.py:20
  100.8 8.5 %collective-permute-start.3 = (f32[256,256]{0,1:T(8,128)}, f32[256,256]{0,1:T(8,128)S(1)}, u32[]{:S(2)}, u32[]{:S(2)}) collective-permute-start(f32[256,256]{0,1:T(8,128)} %get-tuple-element.447), channel_id=1, source_target_pairs={{8,0},{12,4},{16,8},{20,12},{24,16},{28,20},{32,24},{36,28},{40,32... | collective-permute-start | bytes 786440 | tf_op jit(solution)/shard_map/while/body/eval_jaxpr/ppermute | solution.py:20
  103.7 1.7 %copy-start.4 = (bf16[256,8,128]{0,2,1:T(8,128)(2,1)S(1)}, bf16[256,8,128]{0,2,1:T(8,128)(2,1)}, u32[]{:S(2)}) copy-start(bf16[256,8,128]{0,2,1:T(8,128)(2,1)} %get-tuple-element.466) | copy-start | bytes 1572868 | tf_op jit(solution)/shard_map/while
  103.7 1.7 %copy-start.10 = (f32[8,256]{1,0:T(8,128)S(1)}, f32[8,256]{1,0:T(8,128)}, u32[]{:S(2)}) copy-start(f32[8,256]{1,0:T(8,128)} %get-tuple-element.465) | copy-start | bytes 24580 | tf_op jit(solution)/shard_map/while
  105.4 1.1 copy-start.7
  110.2 1.0 copy-start.5
  110.2 1.0 copy-start.11
  110.9 1.2 copy-start.8
  117.0 6.6 %collective-permute-start.7 = (f32[256,256]{1,0:T(8,128)S(1)}, f32[256,256]{1,0:T(8,128)S(1)}, u32[]{:S(2)}, u32[]{:S(2)}) collective-permute-start(f32[256,256]{1,0:T(8,128)S(1)} %copy.100), channel_id=1, source_target_pairs={{8,0},{12,4},{16,8},{20,12},{24,16},{28,20},{32,24},{36,28},{40,32... | collective-permute-start | bytes 786440 | tf_op jit(solution)/shard_map/ppermute | solution.py:20
  119.3 8.8 %collective-permute-start.8 = (f32[256,256]{1,0:T(8,128)S(1)}, f32[256,256]{1,0:T(8,128)S(1)}, u32[]{:S(2)}, u32[]{:S(2)}) collective-permute-start(f32[256,256]{1,0:T(8,128)S(1)} %copy.106), channel_id=1, source_target_pairs={{56,0},{60,4},{0,8},{4,12},{8,16},{12,20},{16,24},{20,28},{24,32},... | collective-permute-start | bytes 786440 | tf_op jit(solution)/shard_map/ppermute | solution.py:20
  128.1 8.9 %collective-permute-start.10 = (f32[256,256]{1,0:T(8,128)S(1)}, f32[256,256]{1,0:T(8,128)S(1)}, u32[]{:S(2)}, u32[]{:S(2)}) collective-permute-start(f32[256,256]{1,0:T(8,128)S(1)} %get-tuple-element.344), channel_id=1, source_target_pairs={{0,12},{4,56},{8,20},{12,0},{16,28},{20,8},{24,36},{28,16},{32,44}... | collective-permute-start | bytes 786440 | tf_op jit(solution)/shard_map/ppermute | solution.py:31
  128.2 8.8 %collective-permute-start.9 = (f32[256,256]{1,0:T(8,128)S(1)}, f32[256,256]{1,0:T(8,128)S(1)}, u32[]{:S(2)}, u32[]{:S(2)}) collective-permute-start(f32[256,256]{1,0:T(8,128)S(1)} %get-tuple-element.345), channel_id=1, source_target_pairs={{0,56},{4,12},{8,0},{12,20},{16,8},{20,28},{24,16},{28,36},{32,24}... | collective-permute-start | bytes 786440 | tf_op jit(solution)/shard_map/ppermute | solution.py:31

commit v11 on v8

--- a/solution.py
+++ b/solution.py
@@ -134,10 +134,14 @@
             behind_received + behind_term,
         )
 
+    def visit_two(pair_index, carried):
+        carried = visit_turn(2 * pair_index + 1, carried)
+        return visit_turn(2 * pair_index + 2, carried)
+
     ahead_kv, behind_kv, query_acc, ahead_pending, behind_pending = lax.fori_loop(
-        1,
-        z_count - 1,
-        visit_turn,
+        0,
+        (z_count - 2) // 2,
+        visit_two,
         (next_ahead, next_behind, query_acc, ahead_pending, behind_pending),
     )
     ahead_received = along_z(ahead_pending, ctx_count, 1)

time: 139 us -> 181 us (1.30)
  matrix products: 43.7 us -> 61.2 us
  local copies, waits for them, and re-layouts: 18.2 us -> 34.6 us
  waiting for transfers between devices: 13 us -> 19.1 us
    dot_general x8, matrix products: 10.3 us -> 20.1 us  [contract(): jnp.einsum('gij,igd->jd', probabilities.astype(jnp.bfloat16), out_grads,...]
    dot_general x8, matrix products: 12.6 us -> 20.3 us  [contract(): jnp.einsum('igd,jd->gij', out_grads, values_part, preferred_element_type=...]
    ppermute x28, waiting for transfers between devices: 7.23 us -> 14.3 us  [along_z(): return lax.ppermute(value, 'ctx', pairs)]
    gather x8, local copies, waits for them, and re-layouts: 4.47 us -> 10.2 us  [live_region(): block_table = jnp.take(query_rows, key_pos[::BLK] // BLK, axis=1)]
    while x32 -> x20, local copies, waits for them, and re-layouts: 2.36 us -> 7.66 us  [the longest x2 2.15 us: local(): lax.fori_loop(1, z_count - 1, visit_turn, (next_ahead, next_behind, query...]
    concatenate x7, local copies, waits for them, and re-layouts: 0.07 us -> 2.78 us  [terms(): key_values = jnp.concatenate([ahead_kv, behind_kv], axis=0)]
    add x6, other arithmetic: 5.37 us -> 2.82 us  [visit_turn(): behind_received + behind_term]
    or x7 -> x4, other arithmetic: 2.68 us -> 4.7 us  [live_region(): return earlier | diagonal]
  transfers between devices with their start and end apart: 32 -> 32, of which waited for: 4 -> 10; matrix products, arithmetic and copies ran while one was open for 46% -> 53% of each run, Pallas kernels for 0% -> 0%
where the time goes in v11:
time: 181 us; the launch traced here: 178 us
  matrix products  61.2 us (34%)
  starting transfers between devices  51 us (28%)
  local copies, waits for them, and re-layouts  34.6 us (19%)
  waiting for transfers between devices  19.1 us (11%)
  other arithmetic  10.6 us (6%)
    ppermute x28, starting transfers between devices, along_z(): return lax.ppermute(value, 'ctx', pairs)  41.3 us
    dot_general x8, matrix products, contract(): jnp.einsum('igd,jd->gij', out_grads, values_part, preferred_element_type=...  20.3 us
    dot_general x8, matrix products, contract(): jnp.einsum('gij,igd->jd', probabilities.astype(jnp.bfloat16), out_grads,...  20.1 us
    ppermute x28, waiting for transfers between devices, along_z(): return lax.ppermute(value, 'ctx', pairs)  14.3 us
    gather x8, local copies, waits for them, and re-layouts, live_region(): block_table = jnp.take(query_rows, key_pos[::BLK] // BLK, axis=1)  10.2 us
    dot_general x8, matrix products, contract(): jnp.einsum('gij,igd->jd', dscore, queries, preferred_element_type=jnp.flo...  7.89 us
    dot_general x8, matrix products, contract(): jnp.einsum('igd,jd->gij', queries, keys_part, preferred_element_type=jnp....  7.51 us
    unnamed x17, local copies, waits for them, and re-layouts  6.25 us
  transfers between devices with their start and end apart: 32, of which 10 were waited for; matrix products, arithmetic and copies ran while one was open for 53% of the time, Pallas kernels for 0%

profile of v11, /device:TPU:4, one launch (start us, length us, event | category | flops | bytes accessed | tf_op | source)
XLA Modules:
  0.0 178.4 jit_solution(4062740720282743404)
XLA Ops:
  2.4 3.3 %collective-permute-start.8 = (bf16[256,256]{1,0:T(8,128)(2,1)S(1)}, bf16[256,256]{1,0:T(8,128)(2,1)S(1)}, u32[]{:S(2)}, u32[]{:S(2)}) collective-permute-start(bf16[256,256]{1,0:T(8,128)(2,1)S(1)} %constant_dynamic-update-slice_fusion.4), channel_id=1, source_target_pairs={{0,4},{4,0},{8,12},{12,8},{16,20},{20,16},{24,28},{28,24},{32,36},... | collective-permute-start | bytes 393224 | tf_op jit(solution)/shard_map/ppermute | solution.py:36
  5.7 1.9 %copy.164 = bf16[8,4,8,1024]{3,2,0,1:T(8,128)(2,1)} copy(bf16[8,4,8,1024]{3,2,1,0:T(8,128)(2,1)} %bitcast.287) | data formatting | bytes 1048576 | tf_op jit(solution)/shard_map/reshape | solution.py:81
  7.5 3.5 %all-to-all-start = ((bf16[64,4,1024]{2,0,1:T(8,128)(2,1)}), bf16[64,4,1024]{2,0,1:T(8,128)(2,1)S(1)}, u32[]{:S(2)}, u32[]{:S(2)}) async-start(bf16[64,4,1024]{2,0,1:T(8,128)(2,1)} %bitcast.206), calls=%async_computation | async-start | bytes 1048576 | tf_op jit(solution)/shard_map/all_to_all | solution.py:82
  12.1 1.3 gather_fusion.3
  13.4 1.3 gather_fusion.2
  15.2 1.2 copy.99
  16.5 1.2 copy.103
  18.0 1.2 fusion.66
  19.3 2.0 %collective-permute-start.10 = (bf16[256,256]{1,0:T(8,128)(2,1)S(1)}, bf16[256,256]{1,0:T(8,128)(2,1)S(1)}, u32[]{:S(2)}, u32[]{:S(2)}) collective-permute-start(bf16[256,256]{1,0:T(8,128)(2,1)S(1)} %get-tuple-element.631), channel_id=1, source_target_pairs={{56,0},{60,4},{0,8},{4,12},{8,16},{12,20},{16,24},{20,28},{24,32},... | collective-permute-start | bytes 393224 | tf_op jit(solution)/shard_map/ppermute | solution.py:20
  21.3 4.0 %collective-permute-start.9 = (bf16[256,256]{1,0:T(8,128)(2,1)S(1)}, bf16[256,256]{1,0:T(8,128)(2,1)}, u32[]{:S(2)}, u32[]{:S(2)}) collective-permute-start(bf16[256,256]{1,0:T(8,128)(2,1)S(1)} %get-tuple-element.632), channel_id=1, source_target_pairs={{8,0},{12,4},{16,8},{20,12},{24,16},{28,20},{32,24},{36,28},{40,32... | collective-permute-start | bytes 393224 | tf_op jit(solution)/shard_map/ppermute | solution.py:20
  25.3 2.7 %fusion.81 = f32[512,256,8]{1,0,2:T(8,128)} fusion(bf16[256,8,128]{0,2,1:T(8,128)(2,1)S(1)} %bitcast.277, bf16[256,256]{1,0:T(8,128)(2,1)S(1)} %get-tuple-element.632, bf16[256,256]{1,0:T(8,128)(2,1)S(1)} %get-tuple-element.631), kind=kOutput, calls=%fused_computation.164 | convolution fusion | flops 268697600 | bytes 4980736 | tf_op jit(solution)/shard_map/igd,jd->gij/dot_general | solution.py:54
  28.1 1.1 copy.110
  30.2 3.5 %fusion.60 = f32[512,128]{0,1:T(8,128)S(1)} fusion(bf16[256,8,128]{0,2,1:T(8,128)(2,1)} %copy.110, f32[512,256,8]{1,0,2:T(8,128)} %fusion.81, f32[8,256]{1,0:T(8,128)} %param.16, pred[256,512]{0,1:T(8,128)(4,1)S(1)} %get-tuple-element.634), kind=kOutput, calls=%fused_computation.124 | convolution fusion | flops 272629760 | bytes 5120000 | tf_op jit(solution)/shard_map/gij,igd->jd/dot_general | solution.py:64
  33.8 2.1 %fusion.49 = bf16[8,256,512]{1,2,0:T(8,128)(2,1)S(1)} fusion(f32[512,256,8]{1,0,2:T(8,128)S(1)} %copy-done.4, f32[8,256]{1,0:T(8,128)} %copy.105, f32[8,256]{1,0:T(8,128)} %param.16, pred[256,512]{0,1:T(8,128)(4,1)S(1)} %get-tuple-element.634, bf16[256,8,128]{2,1,0:T(8,128)(2,1)S(1)} %bitcast.282, bf16[256,256]{1,0:T(8,128)(2,1)S(1)} %get-tuple-element.631, ...), kind=kOutput, calls=%fused_computation.112 | convolution fusion | flops 274989056 | bytes 7225344 | tf_op jit(solution)/shard_map/igd,jd->gij/dot_general | solution.py:58
  38.1 110.4 %while.26 = (s32[]{:T(128)}, bf16[256,256]{1,0:T(8,128)(2,1)}, bf16[256,256]{1,0:T(8,128)(2,1)S(1)}, f32[256,8,128]{0,2,1:T(8,128)S(1)}, f32[256,256]{0,1:T(8,12...) while((s32[]{:T(128)}, bf16[256,256]{1,0:T(8,128)(2,1)}, ...), condition=%wide.region_2.4_spmd.clone.clone, body=%wide.region_1.3_spmd.clone.clone.sunk | while | flops 2707971328 | bytes 60909152 | solution.py:141
  38.2 2.0 %collective-permute-start = (bf16[256,256]{1,0:T(8,128)(2,1)}, bf16[256,256]{1,0:T(8,128)(2,1)}, u32[]{:S(2)}, u32[]{:S(2)}) collective-permute-start(bf16[256,256]{1,0:T(8,128)(2,1)} %get-tuple-element.785), channel_id=1, source_target_pairs={{8,0},{12,4},{16,8},{20,12},{24,16},{28,20},{32,24},{36,28},{40,32... | collective-permute-start | bytes 393224 | tf_op jit(solution)/shard_map/while/body/eval_jaxpr/ppermute | solution.py:20
  40.4 3.2 %collective-permute-start.5 = (f32[256,256]{0,1:T(8,128)}, f32[256,256]{0,1:T(8,128)S(1)}, u32[]{:S(2)}, u32[]{:S(2)}) collective-permute-start(f32[256,256]{0,1:T(8,128)} %get-tuple-element.788), channel_id=1, source_target_pairs={{8,0},{12,4},{16,8},{20,12},{24,16},{28,20},{32,24},{36,28},{40,32... | collective-permute-start | bytes 786440 | tf_op jit(solution)/shard_map/while/body/eval_jaxpr/ppermute | solution.py:20
  44.9 1.3 gather_fusion.1
  46.4 1.3 gather_fusion
  48.7 1.2 fusion.157
  49.8 2.8 %fusion.163 = f32[512,128]{0,1:T(8,128)} fusion(bf16[256,8,128]{0,2,1:T(8,128)(2,1)} %get-tuple-element.815, f32[512,256,8]{1,0,2:T(8,128)S(1)} %fusion.156, f32[8,256]{1,0:T(8,128)} %get-tuple-element.814, pred[256,512]{0,1:T(8,128)(4,1)S(1)} %get-tuple-element.758), kind=kOutput, calls=%fused_computation.27.clone.1 | convolution fusion | flops 272629760 | bytes 5120000 | tf_op jit(solution)/shard_map/while/body/eval_jaxpr/gij,igd->jd/dot_general | solution.py:64
  52.6 2.4 %fusion.158 = bf16[8,256,512]{1,2,0:T(8,128)(2,1)S(1)} fusion(f32[512,256,8]{1,0,2:T(8,128)S(1)} %fusion.156, bf16[256,8,128]{0,2,1:T(8,128)(2,1)} %get-tuple-element.815, f32[8,256]{1,0:T(8,128)} %get-tuple-element.816, f32[8,256]{1,0:T(8,128)} %get-tuple-element.814, pred[256,512]{0,1:T(8,128)(4,1)S(1)} %get-tuple-element.758, ...), kind=kOutput, calls=%fused_computation.13.clone.1 | convolution fusion | flops 274726912 | bytes 7094272 | tf_op jit(solution)/shard_map/while/body/eval_jaxpr/igd,jd->gij/dot_general | solution.py:58
  58.9 2.4 %fusion.161 = bf16[8,256,512]{1,2,0:T(8,128)(2,1)S(1)} fusion(f32[512,256,8]{1,0,2:T(8,128)S(1)} %fusion.160, bf16[256,8,128]{0,2,1:T(8,128)(2,1)} %get-tuple-element.815, f32[8,256]{1,0:T(8,128)} %get-tuple-element.816, f32[8,256]{1,0:T(8,128)} %get-tuple-element.814, pred[256,512]{0,1:T(8,128)(4,1)S(1)} %copy-done.5, ...), kind=kOutput, calls=%fused_computation.7.clone.1 | convolution fusion | flops 274726912 | bytes 7094272 | tf_op jit(solution)/shard_map/while/body/eval_jaxpr/igd,jd->gij/dot_general | solution.py:58
  61.4 2.1 %fusion.165 = f32[512,128]{0,1:T(8,128)S(1)} fusion(bf16[256,8,128]{0,2,1:T(8,128)(2,1)} %get-tuple-element.815, f32[512,256,8]{1,0,2:T(8,128)S(1)} %fusion.160, f32[8,256]{1,0:T(8,128)} %get-tuple-element.814, pred[256,512]{0,1:T(8,128)(4,1)S(1)} %copy-done.5), kind=kOutput, calls=%fused_computation.28.clone.1 | convolution fusion | flops 272629760 | bytes 5120000 | tf_op jit(solution)/shard_map/while/body/eval_jaxpr/gij,igd->jd/dot_general | solution.py:64
  63.7 3.2 %collective-permute-start.7 = (f32[256,256]{0,1:T(8,128)S(1)}, f32[256,256]{0,1:T(8,128)S(1)}, u32[]{:S(2)}, u32[]{:S(2)}) collective-permute-start(f32[256,256]{0,1:T(8,128)S(1)} %get-tuple-element.761), channel_id=1, source_target_pairs={{8,0},{12,4},{16,8},{20,12},{24,16},{28,20},{32,24},{36,28},{40,32... | collective-permute-start | bytes 786440 | tf_op jit(solution)/shard_map/while/body/eval_jaxpr/ppermute | solution.py:20
  68.2 1.3 collective-permute-start.3
  70.3 3.2 %collective-permute-done.6 = f32[256,256]{0,1:T(8,128)S(1)} collective-permute-done((f32[256,256]{0,1:T(8,128)S(1)}, f32[256,256]{0,1:T(8,128)S(1)}, u32[]{:S(2)}, u32[]{:S(2)}) %collective-permute-start.6) | collective-permute-done | bytes 262176 | tf_op jit(solution)/shard_map/while/body/eval_jaxpr/ppermute | solution.py:20
  74.9 3.1 %collective-permute-start = (bf16[256,256]{1,0:T(8,128)(2,1)}, bf16[256,256]{1,0:T(8,128)(2,1)}, u32[]{:S(2)}, u32[]{:S(2)}) collective-permute-start(bf16[256,256]{1,0:T(8,128)(2,1)} %get-tuple-element.785), channel_id=1, source_target_pairs={{8,0},{12,4},{16,8},{20,12},{24,16},{28,20},{32,24},{36,28},{40,32... | collective-permute-start | bytes 393224 | tf_op jit(solution)/shard_map/while/body/eval_jaxpr/ppermute | solution.py:20
  78.0 3.3 %collective-permute-start.5 = (f32[256,256]{0,1:T(8,128)}, f32[256,256]{0,1:T(8,128)S(1)}, u32[]{:S(2)}, u32[]{:S(2)}) collective-permute-start(f32[256,256]{0,1:T(8,128)} %get-tuple-element.788), channel_id=1, source_target_pairs={{8,0},{12,4},{16,8},{20,12},{24,16},{28,20},{32,24},{36,28},{40,32... | collective-permute-start | bytes 786440 | tf_op jit(solution)/shard_map/while/body/eval_jaxpr/ppermute | solution.py:20
  82.5 1.3 gather_fusion.1
  84.1 1.3 gather_fusion
  86.3 1.2 fusion.157
  87.5 2.8 %fusion.163 = f32[512,128]{0,1:T(8,128)} fusion(bf16[256,8,128]{0,2,1:T(8,128)(2,1)} %get-tuple-element.815, f32[512,256,8]{1,0,2:T(8,128)S(1)} %fusion.156, f32[8,256]{1,0:T(8,128)} %get-tuple-element.814, pred[256,512]{0,1:T(8,128)(4,1)S(1)} %get-tuple-element.758), kind=kOutput, calls=%fused_computation.27.clone.1 | convolution fusion | flops 272629760 | bytes 5120000 | tf_op jit(solution)/shard_map/while/body/eval_jaxpr/gij,igd->jd/dot_general | solution.py:64
  90.3 2.4 %fusion.158 = bf16[8,256,512]{1,2,0:T(8,128)(2,1)S(1)} fusion(f32[512,256,8]{1,0,2:T(8,128)S(1)} %fusion.156, bf16[256,8,128]{0,2,1:T(8,128)(2,1)} %get-tuple-element.815, f32[8,256]{1,0:T(8,128)} %get-tuple-element.816, f32[8,256]{1,0:T(8,128)} %get-tuple-element.814, pred[256,512]{0,1:T(8,128)(4,1)S(1)} %get-tuple-element.758, ...), kind=kOutput, calls=%fused_computation.13.clone.1 | convolution fusion | flops 274726912 | bytes 7094272 | tf_op jit(solution)/shard_map/while/body/eval_jaxpr/igd,jd->gij/dot_general | solution.py:58
  96.6 2.4 %fusion.161 = bf16[8,256,512]{1,2,0:T(8,128)(2,1)S(1)} fusion(f32[512,256,8]{1,0,2:T(8,128)S(1)} %fusion.160, bf16[256,8,128]{0,2,1:T(8,128)(2,1)} %get-tuple-element.815, f32[8,256]{1,0:T(8,128)} %get-tuple-element.816, f32[8,256]{1,0:T(8,128)} %get-tuple-element.814, pred[256,512]{0,1:T(8,128)(4,1)S(1)} %copy-done.5, ...), kind=kOutput, calls=%fused_computation.7.clone.1 | convolution fusion | flops 274726912 | bytes 7094272 | tf_op jit(solution)/shard_map/while/body/eval_jaxpr/igd,jd->gij/dot_general | solution.py:58
  99.1 2.1 %fusion.165 = f32[512,128]{0,1:T(8,128)S(1)} fusion(bf16[256,8,128]{0,2,1:T(8,128)(2,1)} %get-tuple-element.815, f32[512,256,8]{1,0,2:T(8,128)S(1)} %fusion.160, f32[8,256]{1,0:T(8,128)} %get-tuple-element.814, pred[256,512]{0,1:T(8,128)(4,1)S(1)} %copy-done.5), kind=kOutput, calls=%fused_computation.28.clone.1 | convolution fusion | flops 272629760 | bytes 5120000 | tf_op jit(solution)/shard_map/while/body/eval_jaxpr/gij,igd->jd/dot_general | solution.py:64
  101.4 3.2 %collective-permute-start.7 = (f32[256,256]{0,1:T(8,128)S(1)}, f32[256,256]{0,1:T(8,128)S(1)}, u32[]{:S(2)}, u32[]{:S(2)}) collective-permute-start(f32[256,256]{0,1:T(8,128)S(1)} %get-tuple-element.761), channel_id=1, source_target_pairs={{8,0},{12,4},{16,8},{20,12},{24,16},{28,20},{32,24},{36,28},{40,32... | collective-permute-start | bytes 786440 | tf_op jit(solution)/shard_map/while/body/eval_jaxpr/ppermute | solution.py:20
  106.0 1.2 collective-permute-start.3
  108.0 1.8 %collective-permute-done.6 = f32[256,256]{0,1:T(8,128)S(1)} collective-permute-done((f32[256,256]{0,1:T(8,128)S(1)}, f32[256,256]{0,1:T(8,128)S(1)}, u32[]{:S(2)}, u32[]{:S(2)}) %collective-permute-start.6) | collective-permute-done | bytes 262176 | tf_op jit(solution)/shard_map/while/body/eval_jaxpr/ppermute | solution.py:20
  110.7 1.6 collective-permute-done.3
  112.4 1.8 %collective-permute-start = (bf16[256,256]{1,0:T(8,128)(2,1)}, bf16[256,256]{1,0:T(8,128)(2,1)}, u32[]{:S(2)}, u32[]{:S(2)}) collective-permute-start(bf16[256,256]{1,0:T(8,128)(2,1)} %get-tuple-element.785), channel_id=1, source_target_pairs={{8,0},{12,4},{16,8},{20,12},{24,16},{28,20},{32,24},{36,28},{40,32... | collective-permute-start | bytes 393224 | tf_op jit(solution)/shard_map/while/body/eval_jaxpr/ppermute | solution.py:20
  115.1 2.5 %collective-permute-start.5 = (f32[256,256]{0,1:T(8,128)}, f32[256,256]{0,1:T(8,128)S(1)}, u32[]{:S(2)}, u32[]{:S(2)}) collective-permute-start(f32[256,256]{0,1:T(8,128)} %get-tuple-element.788), channel_id=1, source_target_pairs={{8,0},{12,4},{16,8},{20,12},{24,16},{28,20},{32,24},{36,28},{40,32... | collective-permute-start | bytes 786440 | tf_op jit(solution)/shard_map/while/body/eval_jaxpr/ppermute | solution.py:20
  118.9 1.3 gather_fusion.1
  120.5 1.3 gather_fusion
  122.7 1.2 fusion.157
  123.9 2.8 %fusion.163 = f32[512,128]{0,1:T(8,128)} fusion(bf16[256,8,128]{0,2,1:T(8,128)(2,1)} %get-tuple-element.815, f32[512,256,8]{1,0,2:T(8,128)S(1)} %fusion.156, f32[8,256]{1,0:T(8,128)} %get-tuple-element.814, pred[256,512]{0,1:T(8,128)(4,1)S(1)} %get-tuple-element.758), kind=kOutput, calls=%fused_computation.27.clone.1 | convolution fusion | flops 272629760 | bytes 5120000 | tf_op jit(solution)/shard_map/while/body/eval_jaxpr/gij,igd->jd/dot_general | solution.py:64
  126.7 2.4 %fusion.158 = bf16[8,256,512]{1,2,0:T(8,128)(2,1)S(1)} fusion(f32[512,256,8]{1,0,2:T(8,128)S(1)} %fusion.156, bf16[256,8,128]{0,2,1:T(8,128)(2,1)} %get-tuple-element.815, f32[8,256]{1,0:T(8,128)} %get-tuple-element.816, f32[8,256]{1,0:T(8,128)} %get-tuple-element.814, pred[256,512]{0,1:T(8,128)(4,1)S(1)} %get-tuple-element.758, ...), kind=kOutput, calls=%fused_computation.13.clone.1 | convolution fusion | flops 274726912 | bytes 7094272 | tf_op jit(solution)/shard_map/while/body/eval_jaxpr/igd,jd->gij/dot_general | solution.py:58
  133.0 2.4 %fusion.161 = bf16[8,256,512]{1,2,0:T(8,128)(2,1)S(1)} fusion(f32[512,256,8]{1,0,2:T(8,128)S(1)} %fusion.160, bf16[256,8,128]{0,2,1:T(8,128)(2,1)} %get-tuple-element.815, f32[8,256]{1,0:T(8,128)} %get-tuple-element.816, f32[8,256]{1,0:T(8,128)} %get-tuple-element.814, pred[256,512]{0,1:T(8,128)(4,1)S(1)} %copy-done.5, ...), kind=kOutput, calls=%fused_computation.7.clone.1 | convolution fusion | flops 274726912 | bytes 7094272 | tf_op jit(solution)/shard_map/while/body/eval_jaxpr/igd,jd->gij/dot_general | solution.py:58
  135.4 2.1 %fusion.165 = f32[512,128]{0,1:T(8,128)S(1)} fusion(bf16[256,8,128]{0,2,1:T(8,128)(2,1)} %get-tuple-element.815, f32[512,256,8]{1,0,2:T(8,128)S(1)} %fusion.160, f32[8,256]{1,0:T(8,128)} %get-tuple-element.814, pred[256,512]{0,1:T(8,128)(4,1)S(1)} %copy-done.5), kind=kOutput, calls=%fused_computation.28.clone.1 | convolution fusion | flops 272629760 | bytes 5120000 | tf_op jit(solution)/shard_map/while/body/eval_jaxpr/gij,igd->jd/dot_general | solution.py:64
  137.8 3.2 %collective-permute-start.7 = (f32[256,256]{0,1:T(8,128)S(1)}, f32[256,256]{0,1:T(8,128)S(1)}, u32[]{:S(2)}, u32[]{:S(2)}) collective-permute-start(f32[256,256]{0,1:T(8,128)S(1)} %get-tuple-element.761), channel_id=1, source_target_pairs={{8,0},{12,4},{16,8},{20,12},{24,16},{28,20},{32,24},{36,28},{40,32... | collective-permute-start | bytes 786440 | tf_op jit(solution)/shard_map/while/body/eval_jaxpr/ppermute | solution.py:20
  142.1 1.4 collective-permute-start.3
  146.8 1.7 collective-permute-done.3
  150.2 2.0 %fusion.63 = f32[512,128]{1,0:T(8,128)S(1)} fusion(bf16[256,8,128]{0,2,1:T(8,128)(2,1)} %copy.110, f32[512,256,8]{1,0,2:T(8,128)S(1)} %fusion.80, f32[8,256]{1,0:T(8,128)} %param.16, pred[256,512]{0,1:T(8,128)(4,1)S(1)} %copy-done.6), kind=kOutput, calls=%fused_computation.125 | convolution fusion | flops 272629760 | bytes 5120000 | tf_op jit(solution)/shard_map/gij,igd->jd/dot_general | solution.py:64
  152.2 3.5 %fusion.45 = bf16[8,256,512]{1,2,0:T(8,128)(2,1)} fusion(f32[512,256,8]{1,0,2:T(8,128)S(1)} %fusion.80, f32[8,256]{1,0:T(8,128)} %copy.105, f32[8,256]{1,0:T(8,128)} %param.16, pred[256,512]{0,1:T(8,128)(4,1)S(1)} %copy-done.6, bf16[256,8,128]{2,1,0:T(8,128)(2,1)S(1)} %bitcast.283, bf16[512,256]{1,0:T(8,128)(2,1)S(1)} %constant_dynamic-update-slice_fusion.6), kind=kOutput, calls=%fused_computation.106 | convolution fusion | flops 274726912 | bytes 7094272 | tf_op jit(solution)/shard_map/igd,jd->gij/dot_general | solution.py:58
  155.7 1.1 copy.124
  156.8 1.1 copy.118
  157.9 1.6 collective-permute-start.11
  160.0 2.1 %convolution_bitcast_fusion.4 = f32[256,8,128]{0,2,1:T(8,128)S(1)} fusion(bf16[8,256,512]{1,2,0:T(8,128)(2,1)} %fusion.45, bf16[512,256]{1,0:T(8,128)(2,1)S(1)} %constant_dynamic-update-slice_fusion.6), kind=kOutput, calls=%fused_computation.122 | convolution fusion | flops 268435456 | bytes 3276800 | tf_op jit(solution)/shard_map/gij,jd->igd/dot_general | solution.py:62
  162.0 2.3 %convolution_bitcast_fusion.6 = f32[512,128]{1,0:T(8,128)S(1)} fusion(bf16[8,256,512]{1,2,0:T(8,128)(2,1)} %fusion.45, bf16[256,8,128]{0,2,1:T(8,128)(2,1)S(1)} %get-tuple-element.824), kind=kOutput, calls=%fused_computation.126 | convolution fusion | flops 268435456 | bytes 2883584 | tf_op jit(solution)/shard_map/gij,igd->jd/dot_general | solution.py:63
  164.3 2.6 %collective-permute-done.11 = f32[256,256]{1,0:T(8,128)S(1)} collective-permute-done((f32[256,256]{1,0:T(8,128)S(1)}, f32[256,256]{1,0:T(8,128)S(1)}, u32[]{:S(2)}, u32[]{:S(2)}) %collective-permute-start.11) | collective-permute-done | bytes 262176 | tf_op jit(solution)/shard_map/ppermute | solution.py:20
  167.0 1.3 collective-permute-done.12
  168.4 2.8 %collective-permute-start.13 = (f32[256,256]{1,0:T(8,128)S(1)}, f32[256,256]{1,0:T(8,128)S(1)}, u32[]{:S(2)}, u32[]{:S(2)}) collective-permute-start(f32[256,256]{1,0:T(8,128)S(1)} %get-tuple-element.628), channel_id=1, source_target_pairs={{0,56},{4,12},{8,0},{12,20},{16,8},{20,28},{24,16},{28,36},{32,24}... | collective-permute-start | bytes 786440 | tf_op jit(solution)/shard_map/ppermute | solution.py:31
  171.3 1.0 copy.125
  172.4 4.8 %collective-permute-done.14 = f32[256,256]{1,0:T(8,128)S(1)} collective-permute-done((f32[256,256]{1,0:T(8,128)S(1)}, f32[256,256]{1,0:T(8,128)S(1)}, u32[]{:S(2)}, u32[]{:S(2)}) %collective-permute-start.14) | collective-permute-done | bytes 262176 | tf_op jit(solution)/shard_map/ppermute | solution.py:31
  (185 shorter events, 41.9 us)
Async XLA Ops:
  0.6 10.8 %copy-start = (s32[32,32]{1,0:T(8,128)S(1)}, s32[32,32]{1,0:T(8,128)}, u32[]{:S(2)}) copy-start(s32[32,32]{1,0:T(8,128)} %param.17) | copy-start | bytes 12292
  2.4 16.9 %collective-permute-start.8 = (bf16[256,256]{1,0:T(8,128)(2,1)S(1)}, bf16[256,256]{1,0:T(8,128)(2,1)S(1)}, u32[]{:S(2)}, u32[]{:S(2)}) collective-permute-start(bf16[256,256]{1,0:T(8,128)(2,1)S(1)} %constant_dynamic-update-slice_fusion.4), channel_id=1, source_target_pairs={{0,4},{4,0},{8,12},{12,8},{16,20},{20,16},{24,28},{28,24},{32,36},... | collective-permute-start | bytes 393224 | tf_op jit(solution)/shard_map/ppermute | solution.py:36
  7.5 20.4 %all-to-all-start = ((bf16[64,4,1024]{2,0,1:T(8,128)(2,1)}), bf16[64,4,1024]{2,0,1:T(8,128)(2,1)S(1)}, u32[]{:S(2)}, u32[]{:S(2)}) async-start(bf16[64,4,1024]{2,0,1:T(8,128)(2,1)} %bitcast.206), calls=%async_computation | async-start | bytes 1048576 | tf_op jit(solution)/shard_map/all_to_all | solution.py:82
  19.3 18.9 %collective-permute-start.10 = (bf16[256,256]{1,0:T(8,128)(2,1)S(1)}, bf16[256,256]{1,0:T(8,128)(2,1)S(1)}, u32[]{:S(2)}, u32[]{:S(2)}) collective-permute-start(bf16[256,256]{1,0:T(8,128)(2,1)S(1)} %get-tuple-element.631), channel_id=1, source_target_pairs={{56,0},{60,4},{0,8},{4,12},{8,16},{12,20},{16,24},{20,28},{24,32},... | collective-permute-start | bytes 393224 | tf_op jit(solution)/shard_map/ppermute | solution.py:20
  21.3 16.9 %collective-permute-start.9 = (bf16[256,256]{1,0:T(8,128)(2,1)S(1)}, bf16[256,256]{1,0:T(8,128)(2,1)}, u32[]{:S(2)}, u32[]{:S(2)}) collective-permute-start(bf16[256,256]{1,0:T(8,128)(2,1)S(1)} %get-tuple-element.632), channel_id=1, source_target_pairs={{8,0},{12,4},{16,8},{20,12},{24,16},{28,20},{32,24},{36,28},{40,32... | collective-permute-start | bytes 393224 | tf_op jit(solution)/shard_map/ppermute | solution.py:20
  28.1 5.6 %copy-start.2 = (bf16[32,8,8,128]{3,2,1,0:T(8,128)(2,1)}, bf16[32,8,8,128]{3,2,1,0:T(8,128)(2,1)S(1)}, u32[]{:S(2)}) copy-start(bf16[32,8,8,128]{3,2,1,0:T(8,128)(2,1)S(1)} %copy.158) | copy-start | bytes 1572868
  30.2 3.6 %copy-start.4 = (f32[512,256,8]{1,0,2:T(8,128)S(1)}, f32[512,256,8]{1,0,2:T(8,128)}, u32[]{:S(2)}) copy-start(f32[512,256,8]{1,0,2:T(8,128)} %fusion.81) | copy-start | bytes 12582916
  38.2 18.1 %collective-permute-start = (bf16[256,256]{1,0:T(8,128)(2,1)}, bf16[256,256]{1,0:T(8,128)(2,1)}, u32[]{:S(2)}, u32[]{:S(2)}) collective-permute-start(bf16[256,256]{1,0:T(8,128)(2,1)} %get-tuple-element.785), channel_id=1, source_target_pairs={{8,0},{12,4},{16,8},{20,12},{24,16},{28,20},{32,24},{36,28},{40,32... | collective-permute-start | bytes 393224 | tf_op jit(solution)/shard_map/while/body/eval_jaxpr/ppermute | solution.py:20
  40.3 17.0 %collective-permute-start.2 = (bf16[256,256]{1,0:T(8,128)(2,1)S(1)}, bf16[256,256]{1,0:T(8,128)(2,1)}, u32[]{:S(2)}, u32[]{:S(2)}) collective-permute-start(bf16[256,256]{1,0:T(8,128)(2,1)S(1)} %get-tuple-element.786), channel_id=1, source_target_pairs={{56,0},{60,4},{0,8},{4,12},{8,16},{12,20},{16,24},{20,28},{24,32},... | collective-permute-start | bytes 393224 | tf_op jit(solution)/shard_map/while/body/eval_jaxpr/ppermute | solution.py:20
  40.4 23.2 %collective-permute-start.4 = (f32[256,256]{0,1:T(8,128)}, f32[256,256]{0,1:T(8,128)S(1)}, u32[]{:S(2)}, u32[]{:S(2)}) collective-permute-start(f32[256,256]{0,1:T(8,128)} %get-tuple-element.789), channel_id=1, source_target_pairs={{56,0},{60,4},{0,8},{4,12},{8,16},{12,20},{16,24},{20,28},{24,32},... | collective-permute-start | bytes 786440 | tf_op jit(solution)/shard_map/while/body/eval_jaxpr/ppermute | solution.py:20
  40.4 23.2 %collective-permute-start.5 = (f32[256,256]{0,1:T(8,128)}, f32[256,256]{0,1:T(8,128)S(1)}, u32[]{:S(2)}, u32[]{:S(2)}) collective-permute-start(f32[256,256]{0,1:T(8,128)} %get-tuple-element.788), channel_id=1, source_target_pairs={{8,0},{12,4},{16,8},{20,12},{24,16},{28,20},{32,24},{36,28},{40,32... | collective-permute-start | bytes 786440 | tf_op jit(solution)/shard_map/while/body/eval_jaxpr/ppermute | solution.py:20
  55.6 3.4 %copy-start.5 = (pred[256,512]{0,1:T(8,128)(4,1)S(1)}, pred[256,512]{0,1:T(8,128)(4,1)}, u32[]{:S(2)}) copy-start(pred[256,512]{0,1:T(8,128)(4,1)} %get-tuple-element.759) | copy-start | bytes 393220 | tf_op jit(solution)/shard_map/while
  61.4 2.2 %copy-start.1 = (f32[512,128]{0,1:T(8,128)S(1)}, f32[512,128]{0,1:T(8,128)}, u32[]{:S(2)}) copy-start(f32[512,128]{0,1:T(8,128)} %fusion.163) | copy-start | bytes 786436 | tf_op jit(solution)/shard_map/while
  63.6 9.9 %collective-permute-start.6 = (f32[256,256]{0,1:T(8,128)S(1)}, f32[256,256]{0,1:T(8,128)S(1)}, u32[]{:S(2)}, u32[]{:S(2)}) collective-permute-start(f32[256,256]{0,1:T(8,128)S(1)} %get-tuple-element.760), channel_id=1, source_target_pairs={{56,0},{60,4},{0,8},{4,12},{8,16},{12,20},{16,24},{20,28},{24,32},... | collective-permute-start | bytes 786440 | tf_op jit(solution)/shard_map/while/body/eval_jaxpr/ppermute | solution.py:20
  63.7 9.8 %collective-permute-start.7 = (f32[256,256]{0,1:T(8,128)S(1)}, f32[256,256]{0,1:T(8,128)S(1)}, u32[]{:S(2)}, u32[]{:S(2)}) collective-permute-start(f32[256,256]{0,1:T(8,128)S(1)} %get-tuple-element.761), channel_id=1, source_target_pairs={{8,0},{12,4},{16,8},{20,12},{24,16},{28,20},{32,24},{36,28},{40,32... | collective-permute-start | bytes 786440 | tf_op jit(solution)/shard_map/while/body/eval_jaxpr/ppermute | solution.py:20
  67.4 6.9 %collective-permute-start.1 = (bf16[256,256]{1,0:T(8,128)(2,1)}, bf16[256,256]{1,0:T(8,128)(2,1)}, u32[]{:S(2)}, u32[]{:S(2)}) collective-permute-start(bf16[256,256]{1,0:T(8,128)(2,1)} %collective-permute-done), channel_id=1, source_target_pairs={{8,0},{12,4},{16,8},{20,12},{24,16},{28,20},{32,24},{36,28},{40,32... | collective-permute-start | bytes 393224 | tf_op jit(solution)/shard_map/while/body/eval_jaxpr/ppermute | solution.py:20
  68.2 6.7 %collective-permute-start.3 = (bf16[256,256]{1,0:T(8,128)(2,1)}, bf16[256,256]{1,0:T(8,128)(2,1)S(1)}, u32[]{:S(2)}, u32[]{:S(2)}) collective-permute-start(bf16[256,256]{1,0:T(8,128)(2,1)} %collective-permute-done.2), channel_id=1, source_target_pairs={{56,0},{60,4},{0,8},{4,12},{8,16},{12,20},{16,24},{20,28},{24,32},... | collective-permute-start | bytes 393224 | tf_op jit(solution)/shard_map/while/body/eval_jaxpr/ppermute | solution.py:20
  74.9 19.1 %collective-permute-start = (bf16[256,256]{1,0:T(8,128)(2,1)}, bf16[256,256]{1,0:T(8,128)(2,1)}, u32[]{:S(2)}, u32[]{:S(2)}) collective-permute-start(bf16[256,256]{1,0:T(8,128)(2,1)} %get-tuple-element.785), channel_id=1, source_target_pairs={{8,0},{12,4},{16,8},{20,12},{24,16},{28,20},{32,24},{36,28},{40,32... | collective-permute-start | bytes 393224 | tf_op jit(solution)/shard_map/while/body/eval_jaxpr/ppermute | solution.py:20
  78.0 17.0 %collective-permute-start.2 = (bf16[256,256]{1,0:T(8,128)(2,1)S(1)}, bf16[256,256]{1,0:T(8,128)(2,1)}, u32[]{:S(2)}, u32[]{:S(2)}) collective-permute-start(bf16[256,256]{1,0:T(8,128)(2,1)S(1)} %get-tuple-element.786), channel_id=1, source_target_pairs={{56,0},{60,4},{0,8},{4,12},{8,16},{12,20},{16,24},{20,28},{24,32},... | collective-permute-start | bytes 393224 | tf_op jit(solution)/shard_map/while/body/eval_jaxpr/ppermute | solution.py:20
  78.0 23.2 %collective-permute-start.4 = (f32[256,256]{0,1:T(8,128)}, f32[256,256]{0,1:T(8,128)S(1)}, u32[]{:S(2)}, u32[]{:S(2)}) collective-permute-start(f32[256,256]{0,1:T(8,128)} %get-tuple-element.789), channel_id=1, source_target_pairs={{56,0},{60,4},{0,8},{4,12},{8,16},{12,20},{16,24},{20,28},{24,32},... | collective-permute-start | bytes 786440 | tf_op jit(solution)/shard_map/while/body/eval_jaxpr/ppermute | solution.py:20
  78.0 23.2 %collective-permute-start.5 = (f32[256,256]{0,1:T(8,128)}, f32[256,256]{0,1:T(8,128)S(1)}, u32[]{:S(2)}, u32[]{:S(2)}) collective-permute-start(f32[256,256]{0,1:T(8,128)} %get-tuple-element.788), channel_id=1, source_target_pairs={{8,0},{12,4},{16,8},{20,12},{24,16},{28,20},{32,24},{36,28},{40,32... | collective-permute-start | bytes 786440 | tf_op jit(solution)/shard_map/while/body/eval_jaxpr/ppermute | solution.py:20
  93.2 3.4 %copy-start.5 = (pred[256,512]{0,1:T(8,128)(4,1)S(1)}, pred[256,512]{0,1:T(8,128)(4,1)}, u32[]{:S(2)}) copy-start(pred[256,512]{0,1:T(8,128)(4,1)} %get-tuple-element.759) | copy-start | bytes 393220 | tf_op jit(solution)/shard_map/while
  99.1 2.2 %copy-start.1 = (f32[512,128]{0,1:T(8,128)S(1)}, f32[512,128]{0,1:T(8,128)}, u32[]{:S(2)}) copy-start(f32[512,128]{0,1:T(8,128)} %fusion.163) | copy-start | bytes 786436 | tf_op jit(solution)/shard_map/while
  101.3 8.5 %collective-permute-start.6 = (f32[256,256]{0,1:T(8,128)S(1)}, f32[256,256]{0,1:T(8,128)S(1)}, u32[]{:S(2)}, u32[]{:S(2)}) collective-permute-start(f32[256,256]{0,1:T(8,128)S(1)} %get-tuple-element.760), channel_id=1, source_target_pairs={{56,0},{60,4},{0,8},{4,12},{8,16},{12,20},{16,24},{20,28},{24,32},... | collective-permute-start | bytes 786440 | tf_op jit(solution)/shard_map/while/body/eval_jaxpr/ppermute | solution.py:20
  101.4 8.5 %collective-permute-start.7 = (f32[256,256]{0,1:T(8,128)S(1)}, f32[256,256]{0,1:T(8,128)S(1)}, u32[]{:S(2)}, u32[]{:S(2)}) collective-permute-start(f32[256,256]{0,1:T(8,128)S(1)} %get-tuple-element.761), channel_id=1, source_target_pairs={{8,0},{12,4},{16,8},{20,12},{24,16},{28,20},{32,24},{36,28},{40,32... | collective-permute-start | bytes 786440 | tf_op jit(solution)/shard_map/while/body/eval_jaxpr/ppermute | solution.py:20
  105.1 5.6 %collective-permute-start.1 = (bf16[256,256]{1,0:T(8,128)(2,1)}, bf16[256,256]{1,0:T(8,128)(2,1)}, u32[]{:S(2)}, u32[]{:S(2)}) collective-permute-start(bf16[256,256]{1,0:T(8,128)(2,1)} %collective-permute-done), channel_id=1, source_target_pairs={{8,0},{12,4},{16,8},{20,12},{24,16},{28,20},{32,24},{36,28},{40,32... | collective-permute-start | bytes 393224 | tf_op jit(solution)/shard_map/while/body/eval_jaxpr/ppermute | solution.py:20
  106.0 6.4 %collective-permute-start.3 = (bf16[256,256]{1,0:T(8,128)(2,1)}, bf16[256,256]{1,0:T(8,128)(2,1)S(1)}, u32[]{:S(2)}, u32[]{:S(2)}) collective-permute-start(bf16[256,256]{1,0:T(8,128)(2,1)} %collective-permute-done.2), channel_id=1, source_target_pairs={{56,0},{60,4},{0,8},{4,12},{8,16},{12,20},{16,24},{20,28},{24,32},... | collective-permute-start | bytes 393224 | tf_op jit(solution)/shard_map/while/body/eval_jaxpr/ppermute | solution.py:20
  112.4 18.1 %collective-permute-start = (bf16[256,256]{1,0:T(8,128)(2,1)}, bf16[256,256]{1,0:T(8,128)(2,1)}, u32[]{:S(2)}, u32[]{:S(2)}) collective-permute-start(bf16[256,256]{1,0:T(8,128)(2,1)} %get-tuple-element.785), channel_id=1, source_target_pairs={{8,0},{12,4},{16,8},{20,12},{24,16},{28,20},{32,24},{36,28},{40,32... | collective-permute-start | bytes 393224 | tf_op jit(solution)/shard_map/while/body/eval_jaxpr/ppermute | solution.py:20
  114.2 17.2 %collective-permute-start.2 = (bf16[256,256]{1,0:T(8,128)(2,1)S(1)}, bf16[256,256]{1,0:T(8,128)(2,1)}, u32[]{:S(2)}, u32[]{:S(2)}) collective-permute-start(bf16[256,256]{1,0:T(8,128)(2,1)S(1)} %get-tuple-element.786), channel_id=1, source_target_pairs={{56,0},{60,4},{0,8},{4,12},{8,16},{12,20},{16,24},{20,28},{24,32},... | collective-permute-start | bytes 393224 | tf_op jit(solution)/shard_map/while/body/eval_jaxpr/ppermute | solution.py:20
  114.4 23.2 %collective-permute-start.4 = (f32[256,256]{0,1:T(8,128)}, f32[256,256]{0,1:T(8,128)S(1)}, u32[]{:S(2)}, u32[]{:S(2)}) collective-permute-start(f32[256,256]{0,1:T(8,128)} %get-tuple-element.789), channel_id=1, source_target_pairs={{56,0},{60,4},{0,8},{4,12},{8,16},{12,20},{16,24},{20,28},{24,32},... | collective-permute-start | bytes 786440 | tf_op jit(solution)/shard_map/while/body/eval_jaxpr/ppermute | solution.py:20
  115.1 22.4 %collective-permute-start.5 = (f32[256,256]{0,1:T(8,128)}, f32[256,256]{0,1:T(8,128)S(1)}, u32[]{:S(2)}, u32[]{:S(2)}) collective-permute-start(f32[256,256]{0,1:T(8,128)} %get-tuple-element.788), channel_id=1, source_target_pairs={{8,0},{12,4},{16,8},{20,12},{24,16},{28,20},{32,24},{36,28},{40,32... | collective-permute-start | bytes 786440 | tf_op jit(solution)/shard_map/while/body/eval_jaxpr/ppermute | solution.py:20
  129.6 3.4 %copy-start.5 = (pred[256,512]{0,1:T(8,128)(4,1)S(1)}, pred[256,512]{0,1:T(8,128)(4,1)}, u32[]{:S(2)}) copy-start(pred[256,512]{0,1:T(8,128)(4,1)} %get-tuple-element.759) | copy-start | bytes 393220 | tf_op jit(solution)/shard_map/while
  135.4 2.2 %copy-start.1 = (f32[512,128]{0,1:T(8,128)S(1)}, f32[512,128]{0,1:T(8,128)}, u32[]{:S(2)}) copy-start(f32[512,128]{0,1:T(8,128)} %fusion.163) | copy-start | bytes 786436 | tf_op jit(solution)/shard_map/while
  137.7 7.7 %collective-permute-start.6 = (f32[256,256]{0,1:T(8,128)S(1)}, f32[256,256]{0,1:T(8,128)S(1)}, u32[]{:S(2)}, u32[]{:S(2)}) collective-permute-start(f32[256,256]{0,1:T(8,128)S(1)} %get-tuple-element.760), channel_id=1, source_target_pairs={{56,0},{60,4},{0,8},{4,12},{8,16},{12,20},{16,24},{20,28},{24,32},... | collective-permute-start | bytes 786440 | tf_op jit(solution)/shard_map/while/body/eval_jaxpr/ppermute | solution.py:20
  137.8 7.6 %collective-permute-start.7 = (f32[256,256]{0,1:T(8,128)S(1)}, f32[256,256]{0,1:T(8,128)S(1)}, u32[]{:S(2)}, u32[]{:S(2)}) collective-permute-start(f32[256,256]{0,1:T(8,128)S(1)} %get-tuple-element.761), channel_id=1, source_target_pairs={{8,0},{12,4},{16,8},{20,12},{24,16},{28,20},{32,24},{36,28},{40,32... | collective-permute-start | bytes 786440 | tf_op jit(solution)/shard_map/while/body/eval_jaxpr/ppermute | solution.py:20
  141.5 5.4 %collective-permute-start.1 = (bf16[256,256]{1,0:T(8,128)(2,1)}, bf16[256,256]{1,0:T(8,128)(2,1)}, u32[]{:S(2)}, u32[]{:S(2)}) collective-permute-start(bf16[256,256]{1,0:T(8,128)(2,1)} %collective-permute-done), channel_id=1, source_target_pairs={{8,0},{12,4},{16,8},{20,12},{24,16},{28,20},{32,24},{36,28},{40,32... | collective-permute-start | bytes 393224 | tf_op jit(solution)/shard_map/while/body/eval_jaxpr/ppermute | solution.py:20
  142.1 6.4 %collective-permute-start.3 = (bf16[256,256]{1,0:T(8,128)(2,1)}, bf16[256,256]{1,0:T(8,128)(2,1)S(1)}, u32[]{:S(2)}, u32[]{:S(2)}) collective-permute-start(bf16[256,256]{1,0:T(8,128)(2,1)} %collective-permute-done.2), channel_id=1, source_target_pairs={{56,0},{60,4},{0,8},{4,12},{8,16},{12,20},{16,24},{20,28},{24,32},... | collective-permute-start | bytes 393224 | tf_op jit(solution)/shard_map/while/body/eval_jaxpr/ppermute | solution.py:20
  148.5 1.7 copy-start.6
  150.2 2.0 %copy-start.3 = (bf16[32,8,8,128]{3,2,1,0:T(8,128)(2,1)S(1)}, bf16[32,8,8,128]{3,2,1,0:T(8,128)(2,1)}, u32[]{:S(2)}) copy-start(bf16[32,8,8,128]{3,2,1,0:T(8,128)(2,1)} %copy-done.2) | copy-start | bytes 1572868
  157.9 9.1 %collective-permute-start.11 = (f32[256,256]{1,0:T(8,128)S(1)}, f32[256,256]{1,0:T(8,128)S(1)}, u32[]{:S(2)}, u32[]{:S(2)}) collective-permute-start(f32[256,256]{1,0:T(8,128)S(1)} %copy.118), channel_id=1, source_target_pairs={{8,0},{12,4},{16,8},{20,12},{24,16},{28,20},{32,24},{36,28},{40,32... | collective-permute-start | bytes 786440 | tf_op jit(solution)/shard_map/ppermute | solution.py:20
  159.5 8.7 %collective-permute-start.12 = (f32[256,256]{1,0:T(8,128)S(1)}, f32[256,256]{1,0:T(8,128)S(1)}, u32[]{:S(2)}, u32[]{:S(2)}) collective-permute-start(f32[256,256]{1,0:T(8,128)S(1)} %copy.124), channel_id=1, source_target_pairs={{56,0},{60,4},{0,8},{4,12},{8,16},{12,20},{16,24},{20,28},{24,32},... | collective-permute-start | bytes 786440 | tf_op jit(solution)/shard_map/ppermute | solution.py:20
  168.3 8.9 %collective-permute-start.14 = (f32[256,256]{1,0:T(8,128)S(1)}, f32[256,256]{1,0:T(8,128)S(1)}, u32[]{:S(2)}, u32[]{:S(2)}) collective-permute-start(f32[256,256]{1,0:T(8,128)S(1)} %get-tuple-element.627), channel_id=1, source_target_pairs={{0,12},{4,56},{8,20},{12,0},{16,28},{20,8},{24,36},{28,16},{32,44}... | collective-permute-start | bytes 786440 | tf_op jit(solution)/shard_map/ppermute | solution.py:31
  168.4 8.8 %collective-permute-start.13 = (f32[256,256]{1,0:T(8,128)S(1)}, f32[256,256]{1,0:T(8,128)S(1)}, u32[]{:S(2)}, u32[]{:S(2)}) collective-permute-start(f32[256,256]{1,0:T(8,128)S(1)} %get-tuple-element.628), channel_id=1, source_target_pairs={{0,56},{4,12},{8,0},{12,20},{16,8},{20,28},{24,16},{28,36},{32,24}... | collective-permute-start | bytes 786440 | tf_op jit(solution)/shard_map/ppermute | solution.py:31

commit v12 on v8

--- a/solution.py
+++ b/solution.py
@@ -36,9 +36,15 @@
     return lax.ppermute(value, "ctx", pairs)
 
 
-def live_region(block_mask, query_start, tok_rows, key_pos):
-    query_rows = lax.dynamic_slice_in_dim(block_mask, query_start // BLK, tok_rows // BLK, 0)
-    block_table = jnp.take(query_rows, key_pos[::BLK] // BLK, axis=1)
+def live_region(block_mask, query_start, tok_rows, key_pos, key_starts):
+    row_count = tok_rows // BLK
+    block_table = jnp.concatenate(
+        [
+            lax.dynamic_slice(block_mask, (query_start // BLK, start // BLK), (row_count, row_count))
+            for start in key_starts
+        ],
+        axis=1,
+    )
     block_table = jnp.repeat(jnp.repeat(block_table, BLK, axis=0), BLK, axis=1)
     query_pos = query_start + jnp.arange(tok_rows, dtype=jnp.int32)
     query_block = (query_pos // BLK)[:, None]
@@ -94,10 +100,9 @@
     def terms(ahead_kv, behind_kv, turn):
         ahead_owner = (z_pos + turn) % z_count
         behind_owner = (z_pos - turn) % z_count
-        key_pos = jnp.concatenate(
-            [ahead_owner * super_rows + offsets, behind_owner * super_rows + tok_rows + offsets]
-        )
-        live_mask = live_region(block_mask, query_start, tok_rows, key_pos)
+        key_starts = (ahead_owner * super_rows, behind_owner * super_rows + tok_rows)
+        key_pos = jnp.concatenate([key_starts[0] + offsets, key_starts[1] + offsets])
+        live_mask = live_region(block_mask, query_start, tok_rows, key_pos, key_starts)
         key_values = jnp.concatenate([ahead_kv, behind_kv], axis=0)
         query_term, key_term, value_term = contract(
             queries,

time: 139 us -> 150 us (1.079)
  matrix products: 43.7 us -> 57.4 us
  waiting for transfers between devices: 13 us -> 8.27 us
    dot_general x8, matrix products: 10.3 us -> 17.8 us  [contract(): jnp.einsum('gij,igd->jd', probabilities.astype(jnp.bfloat16), out_grads,...]
    dot_general x8, matrix products: 12.6 us -> 18.8 us  [contract(): jnp.einsum('igd,jd->gij', out_grads, values_part, preferred_element_type=...]
    dynamic_slice x1 -> x7, local copies, waits for them, and re-layouts: 0.01 us -> 6.09 us  [live_region(): lax.dynamic_slice(block_mask, (query_start // BLK, start // BLK), (row_co...]
    gather x8 -> x0, local copies, waits for them, and re-layouts: 4.47 us -> none  [live_region(): block_table = jnp.take(query_rows, key_pos[::BLK] // BLK, axis=1)]
    ppermute x28, waiting for transfers between devices: 7.23 us -> 4.01 us  [along_z(): return lax.ppermute(value, 'ctx', pairs)]
    ppermute x2, starting transfers between devices: 1.92 us -> 3.42 us  [to_owner(): return lax.ppermute(value, 'ctx', pairs)]
    ppermute x2, waiting for transfers between devices: 5.76 us -> 4.26 us  [to_owner(): return lax.ppermute(value, 'ctx', pairs)]
    unnamed x21 -> x10, local copies, waits for them, and re-layouts: 5.02 us -> 4.6 us
  transfers between devices with their start and end apart: 32 -> 32, of which waited for: 4 -> 4; matrix products, arithmetic and copies ran while one was open for 46% -> 51% of each run, Pallas kernels for 0% -> 0%
where the time goes in v12:
time: 150 us; the launch traced here: 147 us
  matrix products  57.4 us (38%)
  starting transfers between devices  50.8 us (34%)
  local copies, waits for them, and re-layouts  18.6 us (12%)
  other arithmetic  10.3 us (7%)
  waiting for transfers between devices  8.27 us (6%)
    ppermute x28, starting transfers between devices, along_z(): return lax.ppermute(value, 'ctx', pairs)  40.6 us
    dot_general x8, matrix products, contract(): jnp.einsum('igd,jd->gij', out_grads, values_part, preferred_element_type=...  18.8 us
    dot_general x8, matrix products, contract(): jnp.einsum('gij,igd->jd', probabilities.astype(jnp.bfloat16), out_grads,...  17.8 us
    dot_general x8, matrix products, contract(): jnp.einsum('gij,igd->jd', dscore, queries, preferred_element_type=jnp.flo...  7.9 us
    dot_general x8, matrix products, contract(): jnp.einsum('igd,jd->gij', queries, keys_part, preferred_element_type=jnp....  7.48 us
    dynamic_slice x7, local copies, waits for them, and re-layouts, live_region(): lax.dynamic_slice(block_mask, (query_start // BLK, start // BLK), (row_co...  6.09 us
    dot_general x8, matrix products, contract(): jnp.einsum('gij,jd->igd', dscore, keys_part, preferred_element_type=jnp.f...  5.43 us
    add x6, other arithmetic, visit_turn(): behind_received + behind_term  5.39 us
  transfers between devices with their start and end apart: 32, of which 4 were waited for; matrix products, arithmetic and copies ran while one was open for 51% of the time, Pallas kernels for 0%

profile of v12, /device:TPU:4, one launch (start us, length us, event | category | flops | bytes accessed | tf_op | source)
XLA Modules:
  0.0 147.4 jit_solution(3510234373961150081)
XLA Ops:
  0.6 0.9 constant_dynamic-update-slice_fusion.3
  1.5 0.9 constant_dynamic-update-slice_fusion.2
  2.3 3.3 %collective-permute-start.4 = (bf16[256,256]{1,0:T(8,128)(2,1)S(1)}, bf16[256,256]{1,0:T(8,128)(2,1)S(1)}, u32[]{:S(2)}, u32[]{:S(2)}) collective-permute-start(bf16[256,256]{1,0:T(8,128)(2,1)S(1)} %constant_dynamic-update-slice_fusion.2), channel_id=1, source_target_pairs={{0,4},{4,0},{8,12},{12,8},{16,20},{20,16},{24,28},{28,24},{32,36},... | collective-permute-start | bytes 393224 | tf_op jit(solution)/shard_map/ppermute | solution.py:36
  5.6 1.9 %copy.130 = bf16[8,4,8,1024]{3,2,0,1:T(8,128)(2,1)} copy(bf16[8,4,8,1024]{3,2,1,0:T(8,128)(2,1)} %bitcast.196) | data formatting | bytes 1048576 | tf_op jit(solution)/shard_map/reshape | solution.py:87
  7.5 3.5 %all-to-all-start = ((bf16[64,4,1024]{2,0,1:T(8,128)(2,1)}), bf16[64,4,1024]{2,0,1:T(8,128)(2,1)S(1)}, u32[]{:S(2)}, u32[]{:S(2)}) async-start(bf16[64,4,1024]{2,0,1:T(8,128)(2,1)} %bitcast.151), calls=%async_computation | async-start | bytes 1048576 | tf_op jit(solution)/shard_map/all_to_all | solution.py:88
  11.2 0.9 fusion.75
  12.4 1.2 copy.74
  13.7 1.2 copy.78
  15.9 2.0 %collective-permute-start.6 = (bf16[256,256]{1,0:T(8,128)(2,1)S(1)}, bf16[256,256]{1,0:T(8,128)(2,1)S(1)}, u32[]{:S(2)}, u32[]{:S(2)}) collective-permute-start(bf16[256,256]{1,0:T(8,128)(2,1)S(1)} %get-tuple-element.616), channel_id=1, source_target_pairs={{56,0},{60,4},{0,8},{4,12},{8,16},{12,20},{16,24},{20,28},{24,32},... | collective-permute-start | bytes 393224 | tf_op jit(solution)/shard_map/ppermute | solution.py:20
  17.9 4.0 %collective-permute-start.5 = (bf16[256,256]{1,0:T(8,128)(2,1)S(1)}, bf16[256,256]{1,0:T(8,128)(2,1)S(1)}, u32[]{:S(2)}, u32[]{:S(2)}) collective-permute-start(bf16[256,256]{1,0:T(8,128)(2,1)S(1)} %get-tuple-element.617), channel_id=1, source_target_pairs={{8,0},{12,4},{16,8},{20,12},{24,16},{28,20},{32,24},{36,28},{40,32... | collective-permute-start | bytes 393224 | tf_op jit(solution)/shard_map/ppermute | solution.py:20
  21.9 2.6 %fusion.60 = f32[512,256,8]{1,0,2:T(8,128)} fusion(bf16[256,8,128]{0,2,1:T(8,128)(2,1)S(1)} %bitcast.186, bf16[256,256]{1,0:T(8,128)(2,1)S(1)} %get-tuple-element.617, bf16[256,256]{1,0:T(8,128)(2,1)S(1)} %get-tuple-element.616), kind=kOutput, calls=%fused_computation.106 | convolution fusion | flops 268697600 | bytes 4980736 | tf_op jit(solution)/shard_map/igd,jd->gij/dot_general | solution.py:60
  24.6 1.1 copy.85
  26.2 3.5 %fusion.39 = f32[512,128]{0,1:T(8,128)S(1)} fusion(bf16[256,8,128]{0,2,1:T(8,128)(2,1)} %copy.85, f32[512,256,8]{1,0,2:T(8,128)} %fusion.60, f32[8,256]{1,0:T(8,128)S(1)} %copy-done.1, pred[256,512]{0,1:T(8,128)(4,1)S(1)} %get-tuple-element.623), kind=kOutput, calls=%fused_computation.66 | convolution fusion | flops 272629760 | bytes 5120000 | tf_op jit(solution)/shard_map/gij,igd->jd/dot_general | solution.py:70
  29.8 1.4 fusion.28
  32.5 0.8 pad_maximum_fusion.2
  33.4 86.2 %while.26 = (s32[]{:T(128)}, bf16[256,256]{1,0:T(8,128)(2,1)S(1)}, bf16[256,256]{1,0:T(8,128)(2,1)S(1)}, f32[256,8,128]{0,2,1:T(8,128)S(1)}, f32[256,256]{0,1:T(...) while((s32[]{:T(128)}, bf16[256,256]{1,0:T(8,128)(2,1)S(1)}, ...), condition=%wide.region_2.3_spmd.clone.clone, body=%wide.region_1.2_spmd.clone.clone.sunk | while | flops 1353986560 | bytes 30223520 | solution.py:142
  33.5 2.0 %collective-permute-start = (bf16[256,256]{1,0:T(8,128)(2,1)S(1)}, bf16[256,256]{1,0:T(8,128)(2,1)S(1)}, u32[]{:S(2)}, u32[]{:S(2)}) collective-permute-start(bf16[256,256]{1,0:T(8,128)(2,1)S(1)} %copy.140), channel_id=1, source_target_pairs={{8,0},{12,4},{16,8},{20,12},{24,16},{28,20},{32,24},{36,28},{40,32... | collective-permute-start | bytes 393224 | tf_op jit(solution)/shard_map/while/body/eval_jaxpr/ppermute | solution.py:20
  35.8 3.1 %collective-permute-start.3 = (f32[256,256]{0,1:T(8,128)}, f32[256,256]{0,1:T(8,128)S(1)}, u32[]{:S(2)}, u32[]{:S(2)}) collective-permute-start(f32[256,256]{0,1:T(8,128)} %get-tuple-element.768), channel_id=1, source_target_pairs={{8,0},{12,4},{16,8},{20,12},{24,16},{28,20},{32,24},{36,28},{40,32... | collective-permute-start | bytes 786440 | tf_op jit(solution)/shard_map/while/body/eval_jaxpr/ppermute | solution.py:20
  39.0 0.9 fusion.114
  41.0 2.1 %fusion.118 = f32[512,128]{0,1:T(8,128)S(1)} fusion(bf16[256,8,128]{0,2,1:T(8,128)(2,1)} %get-tuple-element.799, f32[512,256,8]{1,0,2:T(8,128)S(1)} %fusion.113, f32[8,256]{1,0:T(8,128)} %get-tuple-element.856, pred[256,512]{0,1:T(8,128)(4,1)S(1)} %fusion.115), kind=kOutput, calls=%fused_computation.12.clone.1 | convolution fusion | flops 272629760 | bytes 5120000 | tf_op jit(solution)/shard_map/while/body/eval_jaxpr/gij,igd->jd/dot_general | solution.py:70
  43.1 2.4 %fusion.116 = bf16[8,256,512]{1,2,0:T(8,128)(2,1)S(1)} fusion(f32[512,256,8]{1,0,2:T(8,128)S(1)} %fusion.113, bf16[256,8,128]{0,2,1:T(8,128)(2,1)} %get-tuple-element.799, f32[8,256]{1,0:T(8,128)S(1)} %get-tuple-element.800, f32[8,256]{1,0:T(8,128)} %get-tuple-element.856, pred[256,512]{0,1:T(8,128)(4,1)S(1)} %fusion.115, ...), kind=kOutput, calls=%fused_computation.3.clone.1 | convolution fusion | flops 274726912 | bytes 7094272 | tf_op jit(solution)/shard_map/while/body/eval_jaxpr/igd,jd->gij/dot_general | solution.py:64
  47.2 0.9 fusion.119
  48.2 1.6 %collective-permute-start = (bf16[256,256]{1,0:T(8,128)(2,1)S(1)}, bf16[256,256]{1,0:T(8,128)(2,1)S(1)}, u32[]{:S(2)}, u32[]{:S(2)}) collective-permute-start(bf16[256,256]{1,0:T(8,128)(2,1)S(1)} %copy.140), channel_id=1, source_target_pairs={{8,0},{12,4},{16,8},{20,12},{24,16},{28,20},{32,24},{36,28},{40,32... | collective-permute-start | bytes 393224 | tf_op jit(solution)/shard_map/while/body/eval_jaxpr/ppermute | solution.py:20
  50.5 3.1 %collective-permute-start.3 = (f32[256,256]{0,1:T(8,128)}, f32[256,256]{0,1:T(8,128)S(1)}, u32[]{:S(2)}, u32[]{:S(2)}) collective-permute-start(f32[256,256]{0,1:T(8,128)} %get-tuple-element.768), channel_id=1, source_target_pairs={{8,0},{12,4},{16,8},{20,12},{24,16},{28,20},{32,24},{36,28},{40,32... | collective-permute-start | bytes 786440 | tf_op jit(solution)/shard_map/while/body/eval_jaxpr/ppermute | solution.py:20
  53.6 0.9 fusion.114
  55.7 2.1 %fusion.118 = f32[512,128]{0,1:T(8,128)S(1)} fusion(bf16[256,8,128]{0,2,1:T(8,128)(2,1)} %get-tuple-element.799, f32[512,256,8]{1,0,2:T(8,128)S(1)} %fusion.113, f32[8,256]{1,0:T(8,128)} %get-tuple-element.856, pred[256,512]{0,1:T(8,128)(4,1)S(1)} %fusion.115), kind=kOutput, calls=%fused_computation.12.clone.1 | convolution fusion | flops 272629760 | bytes 5120000 | tf_op jit(solution)/shard_map/while/body/eval_jaxpr/gij,igd->jd/dot_general | solution.py:70
  57.7 2.4 %fusion.116 = bf16[8,256,512]{1,2,0:T(8,128)(2,1)S(1)} fusion(f32[512,256,8]{1,0,2:T(8,128)S(1)} %fusion.113, bf16[256,8,128]{0,2,1:T(8,128)(2,1)} %get-tuple-element.799, f32[8,256]{1,0:T(8,128)S(1)} %get-tuple-element.800, f32[8,256]{1,0:T(8,128)} %get-tuple-element.856, pred[256,512]{0,1:T(8,128)(4,1)S(1)} %fusion.115, ...), kind=kOutput, calls=%fused_computation.3.clone.1 | convolution fusion | flops 274726912 | bytes 7094272 | tf_op jit(solution)/shard_map/while/body/eval_jaxpr/igd,jd->gij/dot_general | solution.py:64
  61.5 0.9 fusion.119
  62.5 1.6 %collective-permute-start = (bf16[256,256]{1,0:T(8,128)(2,1)S(1)}, bf16[256,256]{1,0:T(8,128)(2,1)S(1)}, u32[]{:S(2)}, u32[]{:S(2)}) collective-permute-start(bf16[256,256]{1,0:T(8,128)(2,1)S(1)} %copy.140), channel_id=1, source_target_pairs={{8,0},{12,4},{16,8},{20,12},{24,16},{28,20},{32,24},{36,28},{40,32... | collective-permute-start | bytes 393224 | tf_op jit(solution)/shard_map/while/body/eval_jaxpr/ppermute | solution.py:20
  64.7 3.1 %collective-permute-start.3 = (f32[256,256]{0,1:T(8,128)}, f32[256,256]{0,1:T(8,128)S(1)}, u32[]{:S(2)}, u32[]{:S(2)}) collective-permute-start(f32[256,256]{0,1:T(8,128)} %get-tuple-element.768), channel_id=1, source_target_pairs={{8,0},{12,4},{16,8},{20,12},{24,16},{28,20},{32,24},{36,28},{40,32... | collective-permute-start | bytes 786440 | tf_op jit(solution)/shard_map/while/body/eval_jaxpr/ppermute | solution.py:20
  67.9 0.9 fusion.114
  69.9 2.1 %fusion.118 = f32[512,128]{0,1:T(8,128)S(1)} fusion(bf16[256,8,128]{0,2,1:T(8,128)(2,1)} %get-tuple-element.799, f32[512,256,8]{1,0,2:T(8,128)S(1)} %fusion.113, f32[8,256]{1,0:T(8,128)} %get-tuple-element.856, pred[256,512]{0,1:T(8,128)(4,1)S(1)} %fusion.115), kind=kOutput, calls=%fused_computation.12.clone.1 | convolution fusion | flops 272629760 | bytes 5120000 | tf_op jit(solution)/shard_map/while/body/eval_jaxpr/gij,igd->jd/dot_general | solution.py:70
  72.0 2.4 %fusion.116 = bf16[8,256,512]{1,2,0:T(8,128)(2,1)S(1)} fusion(f32[512,256,8]{1,0,2:T(8,128)S(1)} %fusion.113, bf16[256,8,128]{0,2,1:T(8,128)(2,1)} %get-tuple-element.799, f32[8,256]{1,0:T(8,128)S(1)} %get-tuple-element.800, f32[8,256]{1,0:T(8,128)} %get-tuple-element.856, pred[256,512]{0,1:T(8,128)(4,1)S(1)} %fusion.115, ...), kind=kOutput, calls=%fused_computation.3.clone.1 | convolution fusion | flops 274726912 | bytes 7094272 | tf_op jit(solution)/shard_map/while/body/eval_jaxpr/igd,jd->gij/dot_general | solution.py:64
  75.8 0.9 fusion.119
  76.7 1.6 %collective-permute-start = (bf16[256,256]{1,0:T(8,128)(2,1)S(1)}, bf16[256,256]{1,0:T(8,128)(2,1)S(1)}, u32[]{:S(2)}, u32[]{:S(2)}) collective-permute-start(bf16[256,256]{1,0:T(8,128)(2,1)S(1)} %copy.140), channel_id=1, source_target_pairs={{8,0},{12,4},{16,8},{20,12},{24,16},{28,20},{32,24},{36,28},{40,32... | collective-permute-start | bytes 393224 | tf_op jit(solution)/shard_map/while/body/eval_jaxpr/ppermute | solution.py:20
  79.0 3.1 %collective-permute-start.3 = (f32[256,256]{0,1:T(8,128)}, f32[256,256]{0,1:T(8,128)S(1)}, u32[]{:S(2)}, u32[]{:S(2)}) collective-permute-start(f32[256,256]{0,1:T(8,128)} %get-tuple-element.768), channel_id=1, source_target_pairs={{8,0},{12,4},{16,8},{20,12},{24,16},{28,20},{32,24},{36,28},{40,32... | collective-permute-start | bytes 786440 | tf_op jit(solution)/shard_map/while/body/eval_jaxpr/ppermute | solution.py:20
  82.2 0.9 fusion.114
  84.2 2.1 %fusion.118 = f32[512,128]{0,1:T(8,128)S(1)} fusion(bf16[256,8,128]{0,2,1:T(8,128)(2,1)} %get-tuple-element.799, f32[512,256,8]{1,0,2:T(8,128)S(1)} %fusion.113, f32[8,256]{1,0:T(8,128)} %get-tuple-element.856, pred[256,512]{0,1:T(8,128)(4,1)S(1)} %fusion.115), kind=kOutput, calls=%fused_computation.12.clone.1 | convolution fusion | flops 272629760 | bytes 5120000 | tf_op jit(solution)/shard_map/while/body/eval_jaxpr/gij,igd->jd/dot_general | solution.py:70
  86.3 2.4 %fusion.116 = bf16[8,256,512]{1,2,0:T(8,128)(2,1)S(1)} fusion(f32[512,256,8]{1,0,2:T(8,128)S(1)} %fusion.113, bf16[256,8,128]{0,2,1:T(8,128)(2,1)} %get-tuple-element.799, f32[8,256]{1,0:T(8,128)S(1)} %get-tuple-element.800, f32[8,256]{1,0:T(8,128)} %get-tuple-element.856, pred[256,512]{0,1:T(8,128)(4,1)S(1)} %fusion.115, ...), kind=kOutput, calls=%fused_computation.3.clone.1 | convolution fusion | flops 274726912 | bytes 7094272 | tf_op jit(solution)/shard_map/while/body/eval_jaxpr/igd,jd->gij/dot_general | solution.py:64
  90.1 0.9 fusion.119
  91.0 1.6 %collective-permute-start = (bf16[256,256]{1,0:T(8,128)(2,1)S(1)}, bf16[256,256]{1,0:T(8,128)(2,1)S(1)}, u32[]{:S(2)}, u32[]{:S(2)}) collective-permute-start(bf16[256,256]{1,0:T(8,128)(2,1)S(1)} %copy.140), channel_id=1, source_target_pairs={{8,0},{12,4},{16,8},{20,12},{24,16},{28,20},{32,24},{36,28},{40,32... | collective-permute-start | bytes 393224 | tf_op jit(solution)/shard_map/while/body/eval_jaxpr/ppermute | solution.py:20
  93.3 3.1 %collective-permute-start.3 = (f32[256,256]{0,1:T(8,128)}, f32[256,256]{0,1:T(8,128)S(1)}, u32[]{:S(2)}, u32[]{:S(2)}) collective-permute-start(f32[256,256]{0,1:T(8,128)} %get-tuple-element.768), channel_id=1, source_target_pairs={{8,0},{12,4},{16,8},{20,12},{24,16},{28,20},{32,24},{36,28},{40,32... | collective-permute-start | bytes 786440 | tf_op jit(solution)/shard_map/while/body/eval_jaxpr/ppermute | solution.py:20
  96.5 0.9 fusion.114
  98.5 2.1 %fusion.118 = f32[512,128]{0,1:T(8,128)S(1)} fusion(bf16[256,8,128]{0,2,1:T(8,128)(2,1)} %get-tuple-element.799, f32[512,256,8]{1,0,2:T(8,128)S(1)} %fusion.113, f32[8,256]{1,0:T(8,128)} %get-tuple-element.856, pred[256,512]{0,1:T(8,128)(4,1)S(1)} %fusion.115), kind=kOutput, calls=%fused_computation.12.clone.1 | convolution fusion | flops 272629760 | bytes 5120000 | tf_op jit(solution)/shard_map/while/body/eval_jaxpr/gij,igd->jd/dot_general | solution.py:70
  100.6 2.4 %fusion.116 = bf16[8,256,512]{1,2,0:T(8,128)(2,1)S(1)} fusion(f32[512,256,8]{1,0,2:T(8,128)S(1)} %fusion.113, bf16[256,8,128]{0,2,1:T(8,128)(2,1)} %get-tuple-element.799, f32[8,256]{1,0:T(8,128)S(1)} %get-tuple-element.800, f32[8,256]{1,0:T(8,128)} %get-tuple-element.856, pred[256,512]{0,1:T(8,128)(4,1)S(1)} %fusion.115, ...), kind=kOutput, calls=%fused_computation.3.clone.1 | convolution fusion | flops 274726912 | bytes 7094272 | tf_op jit(solution)/shard_map/while/body/eval_jaxpr/igd,jd->gij/dot_general | solution.py:64
  104.3 0.9 fusion.119
  105.3 1.6 %collective-permute-start = (bf16[256,256]{1,0:T(8,128)(2,1)S(1)}, bf16[256,256]{1,0:T(8,128)(2,1)S(1)}, u32[]{:S(2)}, u32[]{:S(2)}) collective-permute-start(bf16[256,256]{1,0:T(8,128)(2,1)S(1)} %copy.140), channel_id=1, source_target_pairs={{8,0},{12,4},{16,8},{20,12},{24,16},{28,20},{32,24},{36,28},{40,32... | collective-permute-start | bytes 393224 | tf_op jit(solution)/shard_map/while/body/eval_jaxpr/ppermute | solution.py:20
  107.6 3.1 %collective-permute-start.3 = (f32[256,256]{0,1:T(8,128)}, f32[256,256]{0,1:T(8,128)S(1)}, u32[]{:S(2)}, u32[]{:S(2)}) collective-permute-start(f32[256,256]{0,1:T(8,128)} %get-tuple-element.768), channel_id=1, source_target_pairs={{8,0},{12,4},{16,8},{20,12},{24,16},{28,20},{32,24},{36,28},{40,32... | collective-permute-start | bytes 786440 | tf_op jit(solution)/shard_map/while/body/eval_jaxpr/ppermute | solution.py:20
  110.7 0.9 fusion.114
  112.7 2.1 %fusion.118 = f32[512,128]{0,1:T(8,128)S(1)} fusion(bf16[256,8,128]{0,2,1:T(8,128)(2,1)} %get-tuple-element.799, f32[512,256,8]{1,0,2:T(8,128)S(1)} %fusion.113, f32[8,256]{1,0:T(8,128)} %get-tuple-element.856, pred[256,512]{0,1:T(8,128)(4,1)S(1)} %fusion.115), kind=kOutput, calls=%fused_computation.12.clone.1 | convolution fusion | flops 272629760 | bytes 5120000 | tf_op jit(solution)/shard_map/while/body/eval_jaxpr/gij,igd->jd/dot_general | solution.py:70
  114.8 2.4 %fusion.116 = bf16[8,256,512]{1,2,0:T(8,128)(2,1)S(1)} fusion(f32[512,256,8]{1,0,2:T(8,128)S(1)} %fusion.113, bf16[256,8,128]{0,2,1:T(8,128)(2,1)} %get-tuple-element.799, f32[8,256]{1,0:T(8,128)S(1)} %get-tuple-element.800, f32[8,256]{1,0:T(8,128)} %get-tuple-element.856, pred[256,512]{0,1:T(8,128)(4,1)S(1)} %fusion.115, ...), kind=kOutput, calls=%fused_computation.3.clone.1 | convolution fusion | flops 274726912 | bytes 7094272 | tf_op jit(solution)/shard_map/while/body/eval_jaxpr/igd,jd->gij/dot_general | solution.py:64
  118.6 0.9 fusion.119
  120.3 1.9 %fusion.42 = f32[512,128]{1,0:T(8,128)S(1)} fusion(bf16[256,8,128]{0,2,1:T(8,128)(2,1)} %copy.85, f32[512,256,8]{1,0,2:T(8,128)S(1)} %fusion.59, f32[8,256]{1,0:T(8,128)S(1)} %get-tuple-element.844, pred[256,512]{0,1:T(8,128)(4,1)S(1)} %get-tuple-element.622), kind=kOutput, calls=%fused_computation.67 | convolution fusion | flops 272629760 | bytes 5120000 | tf_op jit(solution)/shard_map/gij,igd->jd/dot_general | solution.py:70
  122.2 2.8 %fusion.24 = bf16[8,256,512]{1,2,0:T(8,128)(2,1)} fusion(f32[512,256,8]{1,0,2:T(8,128)S(1)} %fusion.59, f32[8,256]{1,0:T(8,128)S(1)} %get-tuple-element.846, f32[8,256]{1,0:T(8,128)S(1)} %get-tuple-element.844, pred[256,512]{0,1:T(8,128)(4,1)S(1)} %get-tuple-element.622, bf16[256,8,128]{2,1,0:T(8,128)(2,1)S(1)} %bitcast.192, ...), kind=kOutput, calls=%fused_computation.48 | convolution fusion | flops 274726912 | bytes 7094272 | tf_op jit(solution)/shard_map/igd,jd->gij/dot_general | solution.py:64
  124.9 1.1 copy.98
  126.0 1.1 copy.92
  127.1 1.6 %collective-permute-start.7 = (f32[256,256]{1,0:T(8,128)S(1)}, f32[256,256]{1,0:T(8,128)S(1)}, u32[]{:S(2)}, u32[]{:S(2)}) collective-permute-start(f32[256,256]{1,0:T(8,128)S(1)} %copy.92), channel_id=1, source_target_pairs={{8,0},{12,4},{16,8},{20,12},{24,16},{28,20},{32,24},{36,28},{40,32... | collective-permute-start | bytes 786440 | tf_op jit(solution)/shard_map/ppermute | solution.py:20
  129.2 2.1 %convolution_bitcast_fusion.2 = f32[256,8,128]{0,2,1:T(8,128)S(1)} fusion(bf16[8,256,512]{1,2,0:T(8,128)(2,1)} %fusion.24, bf16[512,256]{1,0:T(8,128)(2,1)S(1)} %constant_dynamic-update-slice_fusion.4), kind=kOutput, calls=%fused_computation.64 | convolution fusion | flops 268435456 | bytes 3276800 | tf_op jit(solution)/shard_map/gij,jd->igd/dot_general | solution.py:68
  131.3 2.3 %convolution_bitcast_fusion.4 = f32[512,128]{1,0:T(8,128)S(1)} fusion(bf16[8,256,512]{1,2,0:T(8,128)(2,1)} %fusion.24, bf16[256,8,128]{0,2,1:T(8,128)(2,1)S(1)} %get-tuple-element.843), kind=kOutput, calls=%fused_computation.68 | convolution fusion | flops 268435456 | bytes 2883584 | tf_op jit(solution)/shard_map/gij,igd->jd/dot_general | solution.py:69
  133.6 2.6 %collective-permute-done.7 = f32[256,256]{1,0:T(8,128)S(1)} collective-permute-done((f32[256,256]{1,0:T(8,128)S(1)}, f32[256,256]{1,0:T(8,128)S(1)}, u32[]{:S(2)}, u32[]{:S(2)}) %collective-permute-start.7) | collective-permute-done | bytes 262176 | tf_op jit(solution)/shard_map/ppermute | solution.py:20
  136.2 0.9 collective-permute-done.8
  137.3 3.3 %collective-permute-start.9 = (f32[256,256]{1,0:T(8,128)S(1)}, f32[256,256]{1,0:T(8,128)S(1)}, u32[]{:S(2)}, u32[]{:S(2)}) collective-permute-start(f32[256,256]{1,0:T(8,128)S(1)} %get-tuple-element.613), channel_id=1, source_target_pairs={{0,56},{4,12},{8,0},{12,20},{16,8},{20,28},{24,16},{28,36},{32,24}... | collective-permute-start | bytes 786440 | tf_op jit(solution)/shard_map/ppermute | solution.py:31
  140.8 1.0 copy.99
  141.8 4.3 %collective-permute-done.10 = f32[256,256]{1,0:T(8,128)S(1)} collective-permute-done((f32[256,256]{1,0:T(8,128)S(1)}, f32[256,256]{1,0:T(8,128)S(1)}, u32[]{:S(2)}, u32[]{:S(2)}) %collective-permute-start.10) | collective-permute-done | bytes 262176 | tf_op jit(solution)/shard_map/ppermute | solution.py:31
  (161 shorter events, 24.9 us)
Async XLA Ops:
  2.3 13.5 %collective-permute-start.4 = (bf16[256,256]{1,0:T(8,128)(2,1)S(1)}, bf16[256,256]{1,0:T(8,128)(2,1)S(1)}, u32[]{:S(2)}, u32[]{:S(2)}) collective-permute-start(bf16[256,256]{1,0:T(8,128)(2,1)S(1)} %constant_dynamic-update-slice_fusion.2), channel_id=1, source_target_pairs={{0,4},{4,0},{8,12},{12,8},{16,20},{20,16},{24,28},{28,24},{32,36},... | collective-permute-start | bytes 393224 | tf_op jit(solution)/shard_map/ppermute | solution.py:36
  7.5 17.0 %all-to-all-start = ((bf16[64,4,1024]{2,0,1:T(8,128)(2,1)}), bf16[64,4,1024]{2,0,1:T(8,128)(2,1)S(1)}, u32[]{:S(2)}, u32[]{:S(2)}) async-start(bf16[64,4,1024]{2,0,1:T(8,128)(2,1)} %bitcast.151), calls=%async_computation | async-start | bytes 1048576 | tf_op jit(solution)/shard_map/all_to_all | solution.py:88
  15.9 17.5 %collective-permute-start.6 = (bf16[256,256]{1,0:T(8,128)(2,1)S(1)}, bf16[256,256]{1,0:T(8,128)(2,1)S(1)}, u32[]{:S(2)}, u32[]{:S(2)}) collective-permute-start(bf16[256,256]{1,0:T(8,128)(2,1)S(1)} %get-tuple-element.616), channel_id=1, source_target_pairs={{56,0},{60,4},{0,8},{4,12},{8,16},{12,20},{16,24},{20,28},{24,32},... | collective-permute-start | bytes 393224 | tf_op jit(solution)/shard_map/ppermute | solution.py:20
  17.9 15.5 %collective-permute-start.5 = (bf16[256,256]{1,0:T(8,128)(2,1)S(1)}, bf16[256,256]{1,0:T(8,128)(2,1)S(1)}, u32[]{:S(2)}, u32[]{:S(2)}) collective-permute-start(bf16[256,256]{1,0:T(8,128)(2,1)S(1)} %get-tuple-element.617), channel_id=1, source_target_pairs={{8,0},{12,4},{16,8},{20,12},{24,16},{28,20},{32,24},{36,28},{40,32... | collective-permute-start | bytes 393224 | tf_op jit(solution)/shard_map/ppermute | solution.py:20
  21.9 4.3 %copy-start.1 = (f32[8,256]{1,0:T(8,128)S(1)}, f32[8,256]{1,0:T(8,128)}, u32[]{:S(2)}) copy-start(f32[8,256]{1,0:T(8,128)} %param.14) | copy-start | bytes 24580
  26.2 3.6 %copy-start = (f32[512,256,8]{1,0,2:T(8,128)S(1)}, f32[512,256,8]{1,0,2:T(8,128)}, u32[]{:S(2)}) copy-start(f32[512,256,8]{1,0,2:T(8,128)} %fusion.60) | copy-start | bytes 12582916
  33.5 14.6 %collective-permute-start = (bf16[256,256]{1,0:T(8,128)(2,1)S(1)}, bf16[256,256]{1,0:T(8,128)(2,1)S(1)}, u32[]{:S(2)}, u32[]{:S(2)}) collective-permute-start(bf16[256,256]{1,0:T(8,128)(2,1)S(1)} %copy.140), channel_id=1, source_target_pairs={{8,0},{12,4},{16,8},{20,12},{24,16},{28,20},{32,24},{36,28},{40,32... | collective-permute-start | bytes 393224 | tf_op jit(solution)/shard_map/while/body/eval_jaxpr/ppermute | solution.py:20
  35.5 12.6 %collective-permute-start.1 = (bf16[256,256]{1,0:T(8,128)(2,1)S(1)}, bf16[256,256]{1,0:T(8,128)(2,1)S(1)}, u32[]{:S(2)}, u32[]{:S(2)}) collective-permute-start(bf16[256,256]{1,0:T(8,128)(2,1)S(1)} %copy.141), channel_id=1, source_target_pairs={{56,0},{60,4},{0,8},{4,12},{8,16},{12,20},{16,24},{20,28},{24,32},... | collective-permute-start | bytes 393224 | tf_op jit(solution)/shard_map/while/body/eval_jaxpr/ppermute | solution.py:20
  35.7 11.5 %collective-permute-start.2 = (f32[256,256]{0,1:T(8,128)}, f32[256,256]{0,1:T(8,128)S(1)}, u32[]{:S(2)}, u32[]{:S(2)}) collective-permute-start(f32[256,256]{0,1:T(8,128)} %get-tuple-element.769), channel_id=1, source_target_pairs={{56,0},{60,4},{0,8},{4,12},{8,16},{12,20},{16,24},{20,28},{24,32},... | collective-permute-start | bytes 786440 | tf_op jit(solution)/shard_map/while/body/eval_jaxpr/ppermute | solution.py:20
  35.8 11.4 %collective-permute-start.3 = (f32[256,256]{0,1:T(8,128)}, f32[256,256]{0,1:T(8,128)S(1)}, u32[]{:S(2)}, u32[]{:S(2)}) collective-permute-start(f32[256,256]{0,1:T(8,128)} %get-tuple-element.768), channel_id=1, source_target_pairs={{8,0},{12,4},{16,8},{20,12},{24,16},{28,20},{32,24},{36,28},{40,32... | collective-permute-start | bytes 786440 | tf_op jit(solution)/shard_map/while/body/eval_jaxpr/ppermute | solution.py:20
  46.0 2.1 %copy-start.2 = (f32[8,256]{1,0:T(8,128)S(1)}, f32[8,256]{1,0:T(8,128)}, u32[]{:S(2)}) copy-start(f32[8,256]{1,0:T(8,128)} %get-tuple-element.856) | copy-start | bytes 24580 | tf_op jit(solution)/shard_map/while
  48.2 14.2 %collective-permute-start = (bf16[256,256]{1,0:T(8,128)(2,1)S(1)}, bf16[256,256]{1,0:T(8,128)(2,1)S(1)}, u32[]{:S(2)}, u32[]{:S(2)}) collective-permute-start(bf16[256,256]{1,0:T(8,128)(2,1)S(1)} %copy.140), channel_id=1, source_target_pairs={{8,0},{12,4},{16,8},{20,12},{24,16},{28,20},{32,24},{36,28},{40,32... | collective-permute-start | bytes 393224 | tf_op jit(solution)/shard_map/while/body/eval_jaxpr/ppermute | solution.py:20
  49.8 12.6 %collective-permute-start.1 = (bf16[256,256]{1,0:T(8,128)(2,1)S(1)}, bf16[256,256]{1,0:T(8,128)(2,1)S(1)}, u32[]{:S(2)}, u32[]{:S(2)}) collective-permute-start(bf16[256,256]{1,0:T(8,128)(2,1)S(1)} %copy.141), channel_id=1, source_target_pairs={{56,0},{60,4},{0,8},{4,12},{8,16},{12,20},{16,24},{20,28},{24,32},... | collective-permute-start | bytes 393224 | tf_op jit(solution)/shard_map/while/body/eval_jaxpr/ppermute | solution.py:20
  50.4 11.1 %collective-permute-start.2 = (f32[256,256]{0,1:T(8,128)}, f32[256,256]{0,1:T(8,128)S(1)}, u32[]{:S(2)}, u32[]{:S(2)}) collective-permute-start(f32[256,256]{0,1:T(8,128)} %get-tuple-element.769), channel_id=1, source_target_pairs={{56,0},{60,4},{0,8},{4,12},{8,16},{12,20},{16,24},{20,28},{24,32},... | collective-permute-start | bytes 786440 | tf_op jit(solution)/shard_map/while/body/eval_jaxpr/ppermute | solution.py:20
  50.5 11.0 %collective-permute-start.3 = (f32[256,256]{0,1:T(8,128)}, f32[256,256]{0,1:T(8,128)S(1)}, u32[]{:S(2)}, u32[]{:S(2)}) collective-permute-start(f32[256,256]{0,1:T(8,128)} %get-tuple-element.768), channel_id=1, source_target_pairs={{8,0},{12,4},{16,8},{20,12},{24,16},{28,20},{32,24},{36,28},{40,32... | collective-permute-start | bytes 786440 | tf_op jit(solution)/shard_map/while/body/eval_jaxpr/ppermute | solution.py:20
  60.7 1.7 %copy-start.2 = (f32[8,256]{1,0:T(8,128)S(1)}, f32[8,256]{1,0:T(8,128)}, u32[]{:S(2)}) copy-start(f32[8,256]{1,0:T(8,128)} %get-tuple-element.856) | copy-start | bytes 24580 | tf_op jit(solution)/shard_map/while
  62.5 14.2 %collective-permute-start = (bf16[256,256]{1,0:T(8,128)(2,1)S(1)}, bf16[256,256]{1,0:T(8,128)(2,1)S(1)}, u32[]{:S(2)}, u32[]{:S(2)}) collective-permute-start(bf16[256,256]{1,0:T(8,128)(2,1)S(1)} %copy.140), channel_id=1, source_target_pairs={{8,0},{12,4},{16,8},{20,12},{24,16},{28,20},{32,24},{36,28},{40,32... | collective-permute-start | bytes 393224 | tf_op jit(solution)/shard_map/while/body/eval_jaxpr/ppermute | solution.py:20
  64.1 12.6 %collective-permute-start.1 = (bf16[256,256]{1,0:T(8,128)(2,1)S(1)}, bf16[256,256]{1,0:T(8,128)(2,1)S(1)}, u32[]{:S(2)}, u32[]{:S(2)}) collective-permute-start(bf16[256,256]{1,0:T(8,128)(2,1)S(1)} %copy.141), channel_id=1, source_target_pairs={{56,0},{60,4},{0,8},{4,12},{8,16},{12,20},{16,24},{20,28},{24,32},... | collective-permute-start | bytes 393224 | tf_op jit(solution)/shard_map/while/body/eval_jaxpr/ppermute | solution.py:20
  64.6 11.1 %collective-permute-start.2 = (f32[256,256]{0,1:T(8,128)}, f32[256,256]{0,1:T(8,128)S(1)}, u32[]{:S(2)}, u32[]{:S(2)}) collective-permute-start(f32[256,256]{0,1:T(8,128)} %get-tuple-element.769), channel_id=1, source_target_pairs={{56,0},{60,4},{0,8},{4,12},{8,16},{12,20},{16,24},{20,28},{24,32},... | collective-permute-start | bytes 786440 | tf_op jit(solution)/shard_map/while/body/eval_jaxpr/ppermute | solution.py:20
  64.7 11.0 %collective-permute-start.3 = (f32[256,256]{0,1:T(8,128)}, f32[256,256]{0,1:T(8,128)S(1)}, u32[]{:S(2)}, u32[]{:S(2)}) collective-permute-start(f32[256,256]{0,1:T(8,128)} %get-tuple-element.768), channel_id=1, source_target_pairs={{8,0},{12,4},{16,8},{20,12},{24,16},{28,20},{32,24},{36,28},{40,32... | collective-permute-start | bytes 786440 | tf_op jit(solution)/shard_map/while/body/eval_jaxpr/ppermute | solution.py:20
  74.9 1.7 %copy-start.2 = (f32[8,256]{1,0:T(8,128)S(1)}, f32[8,256]{1,0:T(8,128)}, u32[]{:S(2)}) copy-start(f32[8,256]{1,0:T(8,128)} %get-tuple-element.856) | copy-start | bytes 24580 | tf_op jit(solution)/shard_map/while
  76.7 14.2 %collective-permute-start = (bf16[256,256]{1,0:T(8,128)(2,1)S(1)}, bf16[256,256]{1,0:T(8,128)(2,1)S(1)}, u32[]{:S(2)}, u32[]{:S(2)}) collective-permute-start(bf16[256,256]{1,0:T(8,128)(2,1)S(1)} %copy.140), channel_id=1, source_target_pairs={{8,0},{12,4},{16,8},{20,12},{24,16},{28,20},{32,24},{36,28},{40,32... | collective-permute-start | bytes 393224 | tf_op jit(solution)/shard_map/while/body/eval_jaxpr/ppermute | solution.py:20
  78.3 12.6 %collective-permute-start.1 = (bf16[256,256]{1,0:T(8,128)(2,1)S(1)}, bf16[256,256]{1,0:T(8,128)(2,1)S(1)}, u32[]{:S(2)}, u32[]{:S(2)}) collective-permute-start(bf16[256,256]{1,0:T(8,128)(2,1)S(1)} %copy.141), channel_id=1, source_target_pairs={{56,0},{60,4},{0,8},{4,12},{8,16},{12,20},{16,24},{20,28},{24,32},... | collective-permute-start | bytes 393224 | tf_op jit(solution)/shard_map/while/body/eval_jaxpr/ppermute | solution.py:20
  78.9 11.1 %collective-permute-start.2 = (f32[256,256]{0,1:T(8,128)}, f32[256,256]{0,1:T(8,128)S(1)}, u32[]{:S(2)}, u32[]{:S(2)}) collective-permute-start(f32[256,256]{0,1:T(8,128)} %get-tuple-element.769), channel_id=1, source_target_pairs={{56,0},{60,4},{0,8},{4,12},{8,16},{12,20},{16,24},{20,28},{24,32},... | collective-permute-start | bytes 786440 | tf_op jit(solution)/shard_map/while/body/eval_jaxpr/ppermute | solution.py:20
  79.0 11.0 %collective-permute-start.3 = (f32[256,256]{0,1:T(8,128)}, f32[256,256]{0,1:T(8,128)S(1)}, u32[]{:S(2)}, u32[]{:S(2)}) collective-permute-start(f32[256,256]{0,1:T(8,128)} %get-tuple-element.768), channel_id=1, source_target_pairs={{8,0},{12,4},{16,8},{20,12},{24,16},{28,20},{32,24},{36,28},{40,32... | collective-permute-start | bytes 786440 | tf_op jit(solution)/shard_map/while/body/eval_jaxpr/ppermute | solution.py:20
  89.2 1.7 %copy-start.2 = (f32[8,256]{1,0:T(8,128)S(1)}, f32[8,256]{1,0:T(8,128)}, u32[]{:S(2)}) copy-start(f32[8,256]{1,0:T(8,128)} %get-tuple-element.856) | copy-start | bytes 24580 | tf_op jit(solution)/shard_map/while
  91.0 14.2 %collective-permute-start = (bf16[256,256]{1,0:T(8,128)(2,1)S(1)}, bf16[256,256]{1,0:T(8,128)(2,1)S(1)}, u32[]{:S(2)}, u32[]{:S(2)}) collective-permute-start(bf16[256,256]{1,0:T(8,128)(2,1)S(1)} %copy.140), channel_id=1, source_target_pairs={{8,0},{12,4},{16,8},{20,12},{24,16},{28,20},{32,24},{36,28},{40,32... | collective-permute-start | bytes 393224 | tf_op jit(solution)/shard_map/while/body/eval_jaxpr/ppermute | solution.py:20
  92.6 12.7 %collective-permute-start.1 = (bf16[256,256]{1,0:T(8,128)(2,1)S(1)}, bf16[256,256]{1,0:T(8,128)(2,1)S(1)}, u32[]{:S(2)}, u32[]{:S(2)}) collective-permute-start(bf16[256,256]{1,0:T(8,128)(2,1)S(1)} %copy.141), channel_id=1, source_target_pairs={{56,0},{60,4},{0,8},{4,12},{8,16},{12,20},{16,24},{20,28},{24,32},... | collective-permute-start | bytes 393224 | tf_op jit(solution)/shard_map/while/body/eval_jaxpr/ppermute | solution.py:20
  93.2 11.1 %collective-permute-start.2 = (f32[256,256]{0,1:T(8,128)}, f32[256,256]{0,1:T(8,128)S(1)}, u32[]{:S(2)}, u32[]{:S(2)}) collective-permute-start(f32[256,256]{0,1:T(8,128)} %get-tuple-element.769), channel_id=1, source_target_pairs={{56,0},{60,4},{0,8},{4,12},{8,16},{12,20},{16,24},{20,28},{24,32},... | collective-permute-start | bytes 786440 | tf_op jit(solution)/shard_map/while/body/eval_jaxpr/ppermute | solution.py:20
  93.3 11.0 %collective-permute-start.3 = (f32[256,256]{0,1:T(8,128)}, f32[256,256]{0,1:T(8,128)S(1)}, u32[]{:S(2)}, u32[]{:S(2)}) collective-permute-start(f32[256,256]{0,1:T(8,128)} %get-tuple-element.768), channel_id=1, source_target_pairs={{8,0},{12,4},{16,8},{20,12},{24,16},{28,20},{32,24},{36,28},{40,32... | collective-permute-start | bytes 786440 | tf_op jit(solution)/shard_map/while/body/eval_jaxpr/ppermute | solution.py:20
  103.5 1.7 %copy-start.2 = (f32[8,256]{1,0:T(8,128)S(1)}, f32[8,256]{1,0:T(8,128)}, u32[]{:S(2)}) copy-start(f32[8,256]{1,0:T(8,128)} %get-tuple-element.856) | copy-start | bytes 24580 | tf_op jit(solution)/shard_map/while
  105.3 14.2 %collective-permute-start = (bf16[256,256]{1,0:T(8,128)(2,1)S(1)}, bf16[256,256]{1,0:T(8,128)(2,1)S(1)}, u32[]{:S(2)}, u32[]{:S(2)}) collective-permute-start(bf16[256,256]{1,0:T(8,128)(2,1)S(1)} %copy.140), channel_id=1, source_target_pairs={{8,0},{12,4},{16,8},{20,12},{24,16},{28,20},{32,24},{36,28},{40,32... | collective-permute-start | bytes 393224 | tf_op jit(solution)/shard_map/while/body/eval_jaxpr/ppermute | solution.py:20
  106.8 12.7 %collective-permute-start.1 = (bf16[256,256]{1,0:T(8,128)(2,1)S(1)}, bf16[256,256]{1,0:T(8,128)(2,1)S(1)}, u32[]{:S(2)}, u32[]{:S(2)}) collective-permute-start(bf16[256,256]{1,0:T(8,128)(2,1)S(1)} %copy.141), channel_id=1, source_target_pairs={{56,0},{60,4},{0,8},{4,12},{8,16},{12,20},{16,24},{20,28},{24,32},... | collective-permute-start | bytes 393224 | tf_op jit(solution)/shard_map/while/body/eval_jaxpr/ppermute | solution.py:20
  107.5 11.1 %collective-permute-start.2 = (f32[256,256]{0,1:T(8,128)}, f32[256,256]{0,1:T(8,128)S(1)}, u32[]{:S(2)}, u32[]{:S(2)}) collective-permute-start(f32[256,256]{0,1:T(8,128)} %get-tuple-element.769), channel_id=1, source_target_pairs={{56,0},{60,4},{0,8},{4,12},{8,16},{12,20},{16,24},{20,28},{24,32},... | collective-permute-start | bytes 786440 | tf_op jit(solution)/shard_map/while/body/eval_jaxpr/ppermute | solution.py:20
  107.6 11.0 %collective-permute-start.3 = (f32[256,256]{0,1:T(8,128)}, f32[256,256]{0,1:T(8,128)S(1)}, u32[]{:S(2)}, u32[]{:S(2)}) collective-permute-start(f32[256,256]{0,1:T(8,128)} %get-tuple-element.768), channel_id=1, source_target_pairs={{8,0},{12,4},{16,8},{20,12},{24,16},{28,20},{32,24},{36,28},{40,32... | collective-permute-start | bytes 786440 | tf_op jit(solution)/shard_map/while/body/eval_jaxpr/ppermute | solution.py:20
  117.8 1.7 %copy-start.2 = (f32[8,256]{1,0:T(8,128)S(1)}, f32[8,256]{1,0:T(8,128)}, u32[]{:S(2)}) copy-start(f32[8,256]{1,0:T(8,128)} %get-tuple-element.856) | copy-start | bytes 24580 | tf_op jit(solution)/shard_map/while
  127.1 9.1 %collective-permute-start.7 = (f32[256,256]{1,0:T(8,128)S(1)}, f32[256,256]{1,0:T(8,128)S(1)}, u32[]{:S(2)}, u32[]{:S(2)}) collective-permute-start(f32[256,256]{1,0:T(8,128)S(1)} %copy.92), channel_id=1, source_target_pairs={{8,0},{12,4},{16,8},{20,12},{24,16},{28,20},{32,24},{36,28},{40,32... | collective-permute-start | bytes 786440 | tf_op jit(solution)/shard_map/ppermute | solution.py:20
  128.7 8.4 %collective-permute-start.8 = (f32[256,256]{1,0:T(8,128)S(1)}, f32[256,256]{1,0:T(8,128)S(1)}, u32[]{:S(2)}, u32[]{:S(2)}) collective-permute-start(f32[256,256]{1,0:T(8,128)S(1)} %copy.98), channel_id=1, source_target_pairs={{56,0},{60,4},{0,8},{4,12},{8,16},{12,20},{16,24},{20,28},{24,32},... | collective-permute-start | bytes 786440 | tf_op jit(solution)/shard_map/ppermute | solution.py:20
  137.2 8.9 %collective-permute-start.10 = (f32[256,256]{1,0:T(8,128)S(1)}, f32[256,256]{1,0:T(8,128)S(1)}, u32[]{:S(2)}, u32[]{:S(2)}) collective-permute-start(f32[256,256]{1,0:T(8,128)S(1)} %get-tuple-element.612), channel_id=1, source_target_pairs={{0,12},{4,56},{8,20},{12,0},{16,28},{20,8},{24,36},{28,16},{32,44}... | collective-permute-start | bytes 786440 | tf_op jit(solution)/shard_map/ppermute | solution.py:31
  137.3 8.8 %collective-permute-start.9 = (f32[256,256]{1,0:T(8,128)S(1)}, f32[256,256]{1,0:T(8,128)S(1)}, u32[]{:S(2)}, u32[]{:S(2)}) collective-permute-start(f32[256,256]{1,0:T(8,128)S(1)} %get-tuple-element.613), channel_id=1, source_target_pairs={{0,56},{4,12},{8,0},{12,20},{16,8},{20,28},{24,16},{28,36},{32,24}... | collective-permute-start | bytes 786440 | tf_op jit(solution)/shard_map/ppermute | solution.py:31

commit v13 on v12

--- a/solution.py
+++ b/solution.py
@@ -102,7 +102,9 @@
         behind_owner = (z_pos - turn) % z_count
         key_starts = (ahead_owner * super_rows, behind_owner * super_rows + tok_rows)
         key_pos = jnp.concatenate([key_starts[0] + offsets, key_starts[1] + offsets])
-        live_mask = live_region(block_mask, query_start, tok_rows, key_pos, key_starts)
+        live_mask = lax.optimization_barrier(
+            live_region(block_mask, query_start, tok_rows, key_pos, key_starts)
+        )
         key_values = jnp.concatenate([ahead_kv, behind_kv], axis=0)
         query_term, key_term, value_term = contract(
             queries,

time: 150 us -> 137 us (0.913)
  matrix products: 57.4 us -> 43.6 us
  waiting for transfers between devices: 8.27 us -> 13.1 us
  local copies, waits for them, and re-layouts: 18.6 us -> 17.1 us
  starting transfers between devices: 50.8 us -> 49.3 us
    dot_general x8, matrix products: 17.8 us -> 10.3 us  [contract(): jnp.einsum('gij,igd->jd', probabilities.astype(jnp.bfloat16), out_grads,...]
    dot_general x8, matrix products: 18.8 us -> 12.5 us  [contract(): jnp.einsum('igd,jd->gij', out_grads, values_part, preferred_element_type=...]
    ppermute x28, waiting for transfers between devices: 4.01 us -> 7 us  [along_z(): return lax.ppermute(value, 'ctx', pairs)]
    ppermute x2, starting transfers between devices: 3.42 us -> 1.61 us  [to_owner(): return lax.ppermute(value, 'ctx', pairs)]
    ppermute x2, waiting for transfers between devices: 4.26 us -> 6.07 us  [to_owner(): return lax.ppermute(value, 'ctx', pairs)]
    unnamed x10 -> x16, local copies, waits for them, and re-layouts: 4.6 us -> 3.89 us
  transfers between devices with their start and end apart: 32 -> 32, of which waited for: 4 -> 3; matrix products, arithmetic and copies ran while one was open for 51% -> 45% of each run, Pallas kernels for 0% -> 0%
where the time goes in v13:
time: 137 us; the launch traced here: 135 us
  starting transfers between devices  49.3 us (36%)
  matrix products  43.6 us (32%)
  local copies, waits for them, and re-layouts  17.1 us (12%)
  waiting for transfers between devices  13.1 us (10%)
  other arithmetic  10.3 us (8%)
    ppermute x28, starting transfers between devices, along_z(): return lax.ppermute(value, 'ctx', pairs)  40.9 us
    dot_general x8, matrix products, contract(): jnp.einsum('igd,jd->gij', out_grads, values_part, preferred_element_type=...  12.5 us
    dot_general x8, matrix products, contract(): jnp.einsum('gij,igd->jd', probabilities.astype(jnp.bfloat16), out_grads,...  10.3 us
    dot_general x8, matrix products, contract(): jnp.einsum('gij,igd->jd', dscore, queries, preferred_element_type=jnp.flo...  7.9 us
    dot_general x8, matrix products, contract(): jnp.einsum('igd,jd->gij', queries, keys_part, preferred_element_type=jnp....  7.49 us
    ppermute x28, waiting for transfers between devices, along_z(): return lax.ppermute(value, 'ctx', pairs)  7 us
    dynamic_slice x7, local copies, waits for them, and re-layouts, live_region(): lax.dynamic_slice(block_mask, (query_start // BLK, start // BLK), (row_co...  6.09 us
    ppermute x2, waiting for transfers between devices, to_owner(): return lax.ppermute(value, 'ctx', pairs)  6.07 us
  transfers between devices with their start and end apart: 32, of which 3 were waited for; matrix products, arithmetic and copies ran while one was open for 45% of the time, Pallas kernels for 0%

profile of v13, /device:TPU:4, one launch (start us, length us, event | category | flops | bytes accessed | tf_op | source)
XLA Modules:
  0.0 135.5 jit_solution(16549763490031509383)
XLA Ops:
  0.6 0.9 constant_dynamic-update-slice_fusion.3
  1.6 0.9 constant_dynamic-update-slice_fusion.2
  2.4 3.3 %collective-permute-start.4 = (bf16[256,256]{1,0:T(8,128)(2,1)S(1)}, bf16[256,256]{1,0:T(8,128)(2,1)S(1)}, u32[]{:S(2)}, u32[]{:S(2)}) collective-permute-start(bf16[256,256]{1,0:T(8,128)(2,1)S(1)} %constant_dynamic-update-slice_fusion.2), channel_id=1, source_target_pairs={{0,4},{4,0},{8,12},{12,8},{16,20},{20,16},{24,28},{28,24},{32,36},... | collective-permute-start | bytes 393224 | tf_op jit(solution)/shard_map/ppermute | solution.py:36
  5.7 1.9 %copy.130 = bf16[8,4,8,1024]{3,2,0,1:T(8,128)(2,1)} copy(bf16[8,4,8,1024]{3,2,1,0:T(8,128)(2,1)} %bitcast.196) | data formatting | bytes 1048576 | tf_op jit(solution)/shard_map/reshape | solution.py:87
  7.6 3.5 %all-to-all-start = ((bf16[64,4,1024]{2,0,1:T(8,128)(2,1)}), bf16[64,4,1024]{2,0,1:T(8,128)(2,1)S(1)}, u32[]{:S(2)}, u32[]{:S(2)}) async-start(bf16[64,4,1024]{2,0,1:T(8,128)(2,1)} %bitcast.151), calls=%async_computation | async-start | bytes 1048576 | tf_op jit(solution)/shard_map/all_to_all | solution.py:88
  11.3 0.9 fusion.75
  13.1 1.2 copy.74
  14.9 2.0 %collective-permute-start.6 = (bf16[256,256]{1,0:T(8,128)(2,1)S(1)}, bf16[256,256]{1,0:T(8,128)(2,1)S(1)}, u32[]{:S(2)}, u32[]{:S(2)}) collective-permute-start(bf16[256,256]{1,0:T(8,128)(2,1)S(1)} %get-tuple-element.616), channel_id=1, source_target_pairs={{56,0},{60,4},{0,8},{4,12},{8,16},{12,20},{16,24},{20,28},{24,32},... | collective-permute-start | bytes 393224 | tf_op jit(solution)/shard_map/ppermute | solution.py:20
  16.9 4.0 %collective-permute-start.5 = (bf16[256,256]{1,0:T(8,128)(2,1)S(1)}, bf16[256,256]{1,0:T(8,128)(2,1)S(1)}, u32[]{:S(2)}, u32[]{:S(2)}) collective-permute-start(bf16[256,256]{1,0:T(8,128)(2,1)S(1)} %get-tuple-element.617), channel_id=1, source_target_pairs={{8,0},{12,4},{16,8},{20,12},{24,16},{28,20},{32,24},{36,28},{40,32... | collective-permute-start | bytes 393224 | tf_op jit(solution)/shard_map/ppermute | solution.py:20
  20.9 2.7 %fusion.60 = f32[512,256,8]{1,0,2:T(8,128)} fusion(bf16[256,8,128]{0,2,1:T(8,128)(2,1)S(1)} %bitcast.186, bf16[256,256]{1,0:T(8,128)(2,1)S(1)} %get-tuple-element.617, bf16[256,256]{1,0:T(8,128)(2,1)S(1)} %get-tuple-element.616), kind=kOutput, calls=%fused_computation.106 | convolution fusion | flops 268697600 | bytes 4980736 | tf_op jit(solution)/shard_map/igd,jd->gij/dot_general | solution.py:60
  24.5 3.4 %fusion.39 = f32[512,128]{0,1:T(8,128)S(1)} fusion(bf16[256,8,128]{0,2,1:T(8,128)(2,1)S(1)} %copy.85, f32[512,256,8]{1,0,2:T(8,128)} %fusion.60, f32[8,256]{1,0:T(8,128)S(1)} %copy-done.5, pred[256,512]{0,1:T(8,128)(4,1)S(1)} %get-tuple-element.623), kind=kOutput, calls=%fused_computation.66 | convolution fusion | flops 272629760 | bytes 5120000 | tf_op jit(solution)/shard_map/gij,igd->jd/dot_general | solution.py:70
  27.9 1.4 %fusion.28 = bf16[8,256,512]{1,2,0:T(8,128)(2,1)S(1)} fusion(f32[512,256,8]{1,0,2:T(8,128)S(1)} %copy-done, f32[8,256]{1,0:T(8,128)S(1)} %copy.80, f32[8,256]{1,0:T(8,128)S(1)} %copy-done.5, pred[256,512]{0,1:T(8,128)(4,1)S(1)} %get-tuple-element.623, bf16[256,8,128]{2,1,0:T(8,128)(2,1)S(1)} %bitcast.191, bf16[256,256]{1,0:T(8,128)(2,1)S(1)} %get-tuple-element.616, ...), kind=kOutput, calls=%fused_computation.54 | convolution fusion | flops 274989056 | bytes 7225344 | tf_op jit(solution)/shard_map/igd,jd->gij/dot_general | solution.py:64
  30.6 0.8 pad_maximum_fusion.2
  31.5 76.0 %while.26 = (s32[]{:T(128)}, bf16[256,256]{1,0:T(8,128)(2,1)S(1)}, bf16[256,256]{1,0:T(8,128)(2,1)S(1)}, f32[256,8,128]{0,2,1:T(8,128)S(1)}, f32[256,256]{0,1:T(...) while((s32[]{:T(128)}, bf16[256,256]{1,0:T(8,128)(2,1)S(1)}, ...), condition=%wide.region_2.3_spmd.clone.clone, body=%wide.region_1.2_spmd.clone.clone.sunk | while | flops 1353986560 | bytes 32320700 | solution.py:144
  31.6 2.2 %collective-permute-start = (bf16[256,256]{1,0:T(8,128)(2,1)S(1)}, bf16[256,256]{1,0:T(8,128)(2,1)S(1)}, u32[]{:S(2)}, u32[]{:S(2)}) collective-permute-start(bf16[256,256]{1,0:T(8,128)(2,1)S(1)} %copy.140), channel_id=1, source_target_pairs={{8,0},{12,4},{16,8},{20,12},{24,16},{28,20},{32,24},{36,28},{40,32... | collective-permute-start | bytes 393224 | tf_op jit(solution)/shard_map/while/body/eval_jaxpr/ppermute | solution.py:20
  34.0 3.2 %collective-permute-start.3 = (f32[256,256]{0,1:T(8,128)}, f32[256,256]{0,1:T(8,128)S(1)}, u32[]{:S(2)}, u32[]{:S(2)}) collective-permute-start(f32[256,256]{0,1:T(8,128)} %get-tuple-element.768), channel_id=1, source_target_pairs={{8,0},{12,4},{16,8},{20,12},{24,16},{28,20},{32,24},{36,28},{40,32... | collective-permute-start | bytes 786440 | tf_op jit(solution)/shard_map/while/body/eval_jaxpr/ppermute | solution.py:20
  37.3 0.9 fusion.114
  39.3 1.0 fusion.118
  40.4 1.4 %fusion.116 = bf16[8,256,512]{1,2,0:T(8,128)(2,1)S(1)} fusion(f32[512,256,8]{1,0,2:T(8,128)S(1)} %fusion.113, bf16[256,8,128]{0,2,1:T(8,128)(2,1)S(1)} %copy-done.3, f32[8,256]{1,0:T(8,128)S(1)} %get-tuple-element.800, f32[8,256]{1,0:T(8,128)S(1)} %copy-done.6, pred[256,512]{0,1:T(8,128)(4,1)S(1)} %fusion.115, ...), kind=kOutput, calls=%fused_computation.3.clone.1 | convolution fusion | flops 274726912 | bytes 7094272 | tf_op jit(solution)/shard_map/while/body/eval_jaxpr/igd,jd->gij/dot_general | solution.py:64
  43.1 2.5 %collective-permute-done.2 = f32[256,256]{0,1:T(8,128)S(1)} collective-permute-done((f32[256,256]{0,1:T(8,128)}, f32[256,256]{0,1:T(8,128)S(1)}, u32[]{:S(2)}, u32[]{:S(2)}) %collective-permute-start.2) | collective-permute-done | bytes 262176 | tf_op jit(solution)/shard_map/while/body/eval_jaxpr/ppermute | solution.py:20
  45.5 0.9 fusion.119
  47.0 1.7 %collective-permute-start.1 = (bf16[256,256]{1,0:T(8,128)(2,1)S(1)}, bf16[256,256]{1,0:T(8,128)(2,1)S(1)}, u32[]{:S(2)}, u32[]{:S(2)}) collective-permute-start(bf16[256,256]{1,0:T(8,128)(2,1)S(1)} %copy.141), channel_id=1, source_target_pairs={{56,0},{60,4},{0,8},{4,12},{8,16},{12,20},{16,24},{20,28},{24,32},... | collective-permute-start | bytes 393224 | tf_op jit(solution)/shard_map/while/body/eval_jaxpr/ppermute | solution.py:20
  48.7 3.1 %collective-permute-start.3 = (f32[256,256]{0,1:T(8,128)}, f32[256,256]{0,1:T(8,128)S(1)}, u32[]{:S(2)}, u32[]{:S(2)}) collective-permute-start(f32[256,256]{0,1:T(8,128)} %get-tuple-element.768), channel_id=1, source_target_pairs={{8,0},{12,4},{16,8},{20,12},{24,16},{28,20},{32,24},{36,28},{40,32... | collective-permute-start | bytes 786440 | tf_op jit(solution)/shard_map/while/body/eval_jaxpr/ppermute | solution.py:20
  51.9 0.9 fusion.114
  54.0 1.0 fusion.118
  55.0 1.4 %fusion.116 = bf16[8,256,512]{1,2,0:T(8,128)(2,1)S(1)} fusion(f32[512,256,8]{1,0,2:T(8,128)S(1)} %fusion.113, bf16[256,8,128]{0,2,1:T(8,128)(2,1)S(1)} %copy-done.3, f32[8,256]{1,0:T(8,128)S(1)} %get-tuple-element.800, f32[8,256]{1,0:T(8,128)S(1)} %copy-done.6, pred[256,512]{0,1:T(8,128)(4,1)S(1)} %fusion.115, ...), kind=kOutput, calls=%fused_computation.3.clone.1 | convolution fusion | flops 274726912 | bytes 7094272 | tf_op jit(solution)/shard_map/while/body/eval_jaxpr/igd,jd->gij/dot_general | solution.py:64
  57.7 0.9 fusion.119
  58.6 2.0 %collective-permute-start = (bf16[256,256]{1,0:T(8,128)(2,1)S(1)}, bf16[256,256]{1,0:T(8,128)(2,1)S(1)}, u32[]{:S(2)}, u32[]{:S(2)}) collective-permute-start(bf16[256,256]{1,0:T(8,128)(2,1)S(1)} %copy.140), channel_id=1, source_target_pairs={{8,0},{12,4},{16,8},{20,12},{24,16},{28,20},{32,24},{36,28},{40,32... | collective-permute-start | bytes 393224 | tf_op jit(solution)/shard_map/while/body/eval_jaxpr/ppermute | solution.py:20
  60.9 3.2 %collective-permute-start.3 = (f32[256,256]{0,1:T(8,128)}, f32[256,256]{0,1:T(8,128)S(1)}, u32[]{:S(2)}, u32[]{:S(2)}) collective-permute-start(f32[256,256]{0,1:T(8,128)} %get-tuple-element.768), channel_id=1, source_target_pairs={{8,0},{12,4},{16,8},{20,12},{24,16},{28,20},{32,24},{36,28},{40,32... | collective-permute-start | bytes 786440 | tf_op jit(solution)/shard_map/while/body/eval_jaxpr/ppermute | solution.py:20
  64.1 0.9 fusion.114
  66.2 1.0 fusion.118
  67.2 1.4 %fusion.116 = bf16[8,256,512]{1,2,0:T(8,128)(2,1)S(1)} fusion(f32[512,256,8]{1,0,2:T(8,128)S(1)} %fusion.113, bf16[256,8,128]{0,2,1:T(8,128)(2,1)S(1)} %copy-done.3, f32[8,256]{1,0:T(8,128)S(1)} %get-tuple-element.800, f32[8,256]{1,0:T(8,128)S(1)} %copy-done.6, pred[256,512]{0,1:T(8,128)(4,1)S(1)} %fusion.115, ...), kind=kOutput, calls=%fused_computation.3.clone.1 | convolution fusion | flops 274726912 | bytes 7094272 | tf_op jit(solution)/shard_map/while/body/eval_jaxpr/igd,jd->gij/dot_general | solution.py:64
  69.9 0.9 fusion.119
  70.8 2.1 %collective-permute-start = (bf16[256,256]{1,0:T(8,128)(2,1)S(1)}, bf16[256,256]{1,0:T(8,128)(2,1)S(1)}, u32[]{:S(2)}, u32[]{:S(2)}) collective-permute-start(bf16[256,256]{1,0:T(8,128)(2,1)S(1)} %copy.140), channel_id=1, source_target_pairs={{8,0},{12,4},{16,8},{20,12},{24,16},{28,20},{32,24},{36,28},{40,32... | collective-permute-start | bytes 393224 | tf_op jit(solution)/shard_map/while/body/eval_jaxpr/ppermute | solution.py:20
  73.3 3.0 %collective-permute-start.3 = (f32[256,256]{0,1:T(8,128)}, f32[256,256]{0,1:T(8,128)S(1)}, u32[]{:S(2)}, u32[]{:S(2)}) collective-permute-start(f32[256,256]{0,1:T(8,128)} %get-tuple-element.768), channel_id=1, source_target_pairs={{8,0},{12,4},{16,8},{20,12},{24,16},{28,20},{32,24},{36,28},{40,32... | collective-permute-start | bytes 786440 | tf_op jit(solution)/shard_map/while/body/eval_jaxpr/ppermute | solution.py:20
  76.3 0.9 fusion.114
  78.4 1.0 fusion.118
  79.4 1.4 %fusion.116 = bf16[8,256,512]{1,2,0:T(8,128)(2,1)S(1)} fusion(f32[512,256,8]{1,0,2:T(8,128)S(1)} %fusion.113, bf16[256,8,128]{0,2,1:T(8,128)(2,1)S(1)} %copy-done.3, f32[8,256]{1,0:T(8,128)S(1)} %get-tuple-element.800, f32[8,256]{1,0:T(8,128)S(1)} %copy-done.6, pred[256,512]{0,1:T(8,128)(4,1)S(1)} %fusion.115, ...), kind=kOutput, calls=%fused_computation.3.clone.1 | convolution fusion | flops 274726912 | bytes 7094272 | tf_op jit(solution)/shard_map/while/body/eval_jaxpr/igd,jd->gij/dot_general | solution.py:64
  81.3 0.8 convolution_bitcast_fusion.7
  82.1 0.9 fusion.119
  83.0 2.0 %collective-permute-start = (bf16[256,256]{1,0:T(8,128)(2,1)S(1)}, bf16[256,256]{1,0:T(8,128)(2,1)S(1)}, u32[]{:S(2)}, u32[]{:S(2)}) collective-permute-start(bf16[256,256]{1,0:T(8,128)(2,1)S(1)} %copy.140), channel_id=1, source_target_pairs={{8,0},{12,4},{16,8},{20,12},{24,16},{28,20},{32,24},{36,28},{40,32... | collective-permute-start | bytes 393224 | tf_op jit(solution)/shard_map/while/body/eval_jaxpr/ppermute | solution.py:20
  85.9 2.6 %collective-permute-start.3 = (f32[256,256]{0,1:T(8,128)}, f32[256,256]{0,1:T(8,128)S(1)}, u32[]{:S(2)}, u32[]{:S(2)}) collective-permute-start(f32[256,256]{0,1:T(8,128)} %get-tuple-element.768), channel_id=1, source_target_pairs={{8,0},{12,4},{16,8},{20,12},{24,16},{28,20},{32,24},{36,28},{40,32... | collective-permute-start | bytes 786440 | tf_op jit(solution)/shard_map/while/body/eval_jaxpr/ppermute | solution.py:20
  88.5 0.9 fusion.114
  90.6 1.0 fusion.118
  91.6 1.4 %fusion.116 = bf16[8,256,512]{1,2,0:T(8,128)(2,1)S(1)} fusion(f32[512,256,8]{1,0,2:T(8,128)S(1)} %fusion.113, bf16[256,8,128]{0,2,1:T(8,128)(2,1)S(1)} %copy-done.3, f32[8,256]{1,0:T(8,128)S(1)} %get-tuple-element.800, f32[8,256]{1,0:T(8,128)S(1)} %copy-done.6, pred[256,512]{0,1:T(8,128)(4,1)S(1)} %fusion.115, ...), kind=kOutput, calls=%fused_computation.3.clone.1 | convolution fusion | flops 274726912 | bytes 7094272 | tf_op jit(solution)/shard_map/while/body/eval_jaxpr/igd,jd->gij/dot_general | solution.py:64
  94.3 0.9 fusion.119
  95.2 2.0 %collective-permute-start = (bf16[256,256]{1,0:T(8,128)(2,1)S(1)}, bf16[256,256]{1,0:T(8,128)(2,1)S(1)}, u32[]{:S(2)}, u32[]{:S(2)}) collective-permute-start(bf16[256,256]{1,0:T(8,128)(2,1)S(1)} %copy.140), channel_id=1, source_target_pairs={{8,0},{12,4},{16,8},{20,12},{24,16},{28,20},{32,24},{36,28},{40,32... | collective-permute-start | bytes 393224 | tf_op jit(solution)/shard_map/while/body/eval_jaxpr/ppermute | solution.py:20
  97.4 0.8 collective-permute-start.2
  98.2 2.4 %collective-permute-start.3 = (f32[256,256]{0,1:T(8,128)}, f32[256,256]{0,1:T(8,128)S(1)}, u32[]{:S(2)}, u32[]{:S(2)}) collective-permute-start(f32[256,256]{0,1:T(8,128)} %get-tuple-element.768), channel_id=1, source_target_pairs={{8,0},{12,4},{16,8},{20,12},{24,16},{28,20},{32,24},{36,28},{40,32... | collective-permute-start | bytes 786440 | tf_op jit(solution)/shard_map/while/body/eval_jaxpr/ppermute | solution.py:20
  100.7 0.9 fusion.114
  102.8 1.0 fusion.118
  103.8 1.4 %fusion.116 = bf16[8,256,512]{1,2,0:T(8,128)(2,1)S(1)} fusion(f32[512,256,8]{1,0,2:T(8,128)S(1)} %fusion.113, bf16[256,8,128]{0,2,1:T(8,128)(2,1)S(1)} %copy-done.3, f32[8,256]{1,0:T(8,128)S(1)} %get-tuple-element.800, f32[8,256]{1,0:T(8,128)S(1)} %copy-done.6, pred[256,512]{0,1:T(8,128)(4,1)S(1)} %fusion.115, ...), kind=kOutput, calls=%fused_computation.3.clone.1 | convolution fusion | flops 274726912 | bytes 7094272 | tf_op jit(solution)/shard_map/while/body/eval_jaxpr/igd,jd->gij/dot_general | solution.py:64
  106.5 0.9 fusion.119
  108.5 0.9 fusion.42
  109.3 2.8 %fusion.24 = bf16[8,256,512]{1,2,0:T(8,128)(2,1)} fusion(f32[512,256,8]{1,0,2:T(8,128)S(1)} %fusion.59, f32[8,256]{1,0:T(8,128)S(1)} %get-tuple-element.847, f32[8,256]{1,0:T(8,128)S(1)} %get-tuple-element.845, pred[256,512]{0,1:T(8,128)(4,1)S(1)} %get-tuple-element.622, bf16[256,8,128]{2,1,0:T(8,128)(2,1)S(1)} %bitcast.192, ...), kind=kOutput, calls=%fused_computation.48 | convolution fusion | flops 274726912 | bytes 7094272 | tf_op jit(solution)/shard_map/igd,jd->gij/dot_general | solution.py:64
  112.1 1.1 copy.98
  113.2 1.1 copy.92
  114.3 2.0 %collective-permute-start.7 = (f32[256,256]{1,0:T(8,128)S(1)}, f32[256,256]{1,0:T(8,128)S(1)}, u32[]{:S(2)}, u32[]{:S(2)}) collective-permute-start(f32[256,256]{1,0:T(8,128)S(1)} %copy.92), channel_id=1, source_target_pairs={{8,0},{12,4},{16,8},{20,12},{24,16},{28,20},{32,24},{36,28},{40,32... | collective-permute-start | bytes 786440 | tf_op jit(solution)/shard_map/ppermute | solution.py:20
  116.4 2.1 %convolution_bitcast_fusion.2 = f32[256,8,128]{0,2,1:T(8,128)S(1)} fusion(bf16[8,256,512]{1,2,0:T(8,128)(2,1)} %fusion.24, bf16[512,256]{1,0:T(8,128)(2,1)S(1)} %constant_dynamic-update-slice_fusion.4), kind=kOutput, calls=%fused_computation.64 | convolution fusion | flops 268435456 | bytes 3276800 | tf_op jit(solution)/shard_map/gij,jd->igd/dot_general | solution.py:68
  118.5 2.3 %convolution_bitcast_fusion.4 = f32[512,128]{1,0:T(8,128)S(1)} fusion(bf16[8,256,512]{1,2,0:T(8,128)(2,1)} %fusion.24, bf16[256,8,128]{0,2,1:T(8,128)(2,1)S(1)} %get-tuple-element.844), kind=kOutput, calls=%fused_computation.68 | convolution fusion | flops 268435456 | bytes 2883584 | tf_op jit(solution)/shard_map/gij,igd->jd/dot_general | solution.py:69
  120.8 4.5 %collective-permute-done.8 = f32[256,256]{1,0:T(8,128)S(1)} collective-permute-done((f32[256,256]{1,0:T(8,128)S(1)}, f32[256,256]{1,0:T(8,128)S(1)}, u32[]{:S(2)}, u32[]{:S(2)}) %collective-permute-start.8) | collective-permute-done | bytes 262176 | tf_op jit(solution)/shard_map/ppermute | solution.py:20
  125.4 1.5 %collective-permute-start.9 = (f32[256,256]{1,0:T(8,128)S(1)}, f32[256,256]{1,0:T(8,128)S(1)}, u32[]{:S(2)}, u32[]{:S(2)}) collective-permute-start(f32[256,256]{1,0:T(8,128)S(1)} %get-tuple-element.613), channel_id=1, source_target_pairs={{0,56},{4,12},{8,0},{12,20},{16,8},{20,28},{24,16},{28,36},{32,24}... | collective-permute-start | bytes 786440 | tf_op jit(solution)/shard_map/ppermute | solution.py:31
  127.1 1.0 copy.99
  128.1 6.1 %collective-permute-done.10 = f32[256,256]{1,0:T(8,128)S(1)} collective-permute-done((f32[256,256]{1,0:T(8,128)S(1)}, f32[256,256]{1,0:T(8,128)S(1)}, u32[]{:S(2)}, u32[]{:S(2)}) %collective-permute-start.10) | collective-permute-done | bytes 262176 | tf_op jit(solution)/shard_map/ppermute | solution.py:31
  (179 shorter events, 22.6 us)
Async XLA Ops:
  0.6 13.7 %copy-start.1 = (bf16[256,1024]{1,0:T(8,128)(2,1)S(1)}, bf16[256,1024]{1,0:T(8,128)(2,1)}, u32[]{:S(2)}) copy-start(bf16[256,1024]{1,0:T(8,128)(2,1)} %param.12) | copy-start | bytes 1572868
  2.4 12.5 %collective-permute-start.4 = (bf16[256,256]{1,0:T(8,128)(2,1)S(1)}, bf16[256,256]{1,0:T(8,128)(2,1)S(1)}, u32[]{:S(2)}, u32[]{:S(2)}) collective-permute-start(bf16[256,256]{1,0:T(8,128)(2,1)S(1)} %constant_dynamic-update-slice_fusion.2), channel_id=1, source_target_pairs={{0,4},{4,0},{8,12},{12,8},{16,20},{20,16},{24,28},{28,24},{32,36},... | collective-permute-start | bytes 393224 | tf_op jit(solution)/shard_map/ppermute | solution.py:36
  7.6 16.0 %all-to-all-start = ((bf16[64,4,1024]{2,0,1:T(8,128)(2,1)}), bf16[64,4,1024]{2,0,1:T(8,128)(2,1)S(1)}, u32[]{:S(2)}, u32[]{:S(2)}) async-start(bf16[64,4,1024]{2,0,1:T(8,128)(2,1)} %bitcast.151), calls=%async_computation | async-start | bytes 1048576 | tf_op jit(solution)/shard_map/all_to_all | solution.py:88
  14.9 16.5 %collective-permute-start.6 = (bf16[256,256]{1,0:T(8,128)(2,1)S(1)}, bf16[256,256]{1,0:T(8,128)(2,1)S(1)}, u32[]{:S(2)}, u32[]{:S(2)}) collective-permute-start(bf16[256,256]{1,0:T(8,128)(2,1)S(1)} %get-tuple-element.616), channel_id=1, source_target_pairs={{56,0},{60,4},{0,8},{4,12},{8,16},{12,20},{16,24},{20,28},{24,32},... | collective-permute-start | bytes 393224 | tf_op jit(solution)/shard_map/ppermute | solution.py:20
  16.9 14.6 %collective-permute-start.5 = (bf16[256,256]{1,0:T(8,128)(2,1)S(1)}, bf16[256,256]{1,0:T(8,128)(2,1)S(1)}, u32[]{:S(2)}, u32[]{:S(2)}) collective-permute-start(bf16[256,256]{1,0:T(8,128)(2,1)S(1)} %get-tuple-element.617), channel_id=1, source_target_pairs={{8,0},{12,4},{16,8},{20,12},{24,16},{28,20},{32,24},{36,28},{40,32... | collective-permute-start | bytes 393224 | tf_op jit(solution)/shard_map/ppermute | solution.py:20
  20.9 3.5 %copy-start.5 = (f32[8,256]{1,0:T(8,128)S(1)}, f32[8,256]{1,0:T(8,128)}, u32[]{:S(2)}) copy-start(f32[8,256]{1,0:T(8,128)} %param.14) | copy-start | bytes 24580
  24.0 5.3 %copy-start.2 = (bf16[256,8,128]{0,2,1:T(8,128)(2,1)}, bf16[256,8,128]{0,2,1:T(8,128)(2,1)S(1)}, u32[]{:S(2)}) copy-start(bf16[256,8,128]{0,2,1:T(8,128)(2,1)S(1)} %copy.85) | copy-start | bytes 1572868
  24.5 3.5 %copy-start = (f32[512,256,8]{1,0,2:T(8,128)S(1)}, f32[512,256,8]{1,0,2:T(8,128)}, u32[]{:S(2)}) copy-start(f32[512,256,8]{1,0,2:T(8,128)} %fusion.60) | copy-start | bytes 12582916
  31.6 14.8 %collective-permute-start = (bf16[256,256]{1,0:T(8,128)(2,1)S(1)}, bf16[256,256]{1,0:T(8,128)(2,1)S(1)}, u32[]{:S(2)}, u32[]{:S(2)}) collective-permute-start(bf16[256,256]{1,0:T(8,128)(2,1)S(1)} %copy.140), channel_id=1, source_target_pairs={{8,0},{12,4},{16,8},{20,12},{24,16},{28,20},{32,24},{36,28},{40,32... | collective-permute-start | bytes 393224 | tf_op jit(solution)/shard_map/while/body/eval_jaxpr/ppermute | solution.py:20
  33.8 12.6 %collective-permute-start.1 = (bf16[256,256]{1,0:T(8,128)(2,1)S(1)}, bf16[256,256]{1,0:T(8,128)(2,1)S(1)}, u32[]{:S(2)}, u32[]{:S(2)}) collective-permute-start(bf16[256,256]{1,0:T(8,128)(2,1)S(1)} %copy.141), channel_id=1, source_target_pairs={{56,0},{60,4},{0,8},{4,12},{8,16},{12,20},{16,24},{20,28},{24,32},... | collective-permute-start | bytes 393224 | tf_op jit(solution)/shard_map/while/body/eval_jaxpr/ppermute | solution.py:20
  33.9 11.6 %collective-permute-start.2 = (f32[256,256]{0,1:T(8,128)}, f32[256,256]{0,1:T(8,128)S(1)}, u32[]{:S(2)}, u32[]{:S(2)}) collective-permute-start(f32[256,256]{0,1:T(8,128)} %get-tuple-element.769), channel_id=1, source_target_pairs={{56,0},{60,4},{0,8},{4,12},{8,16},{12,20},{16,24},{20,28},{24,32},... | collective-permute-start | bytes 786440 | tf_op jit(solution)/shard_map/while/body/eval_jaxpr/ppermute | solution.py:20
  34.0 11.5 %collective-permute-start.3 = (f32[256,256]{0,1:T(8,128)}, f32[256,256]{0,1:T(8,128)S(1)}, u32[]{:S(2)}, u32[]{:S(2)}) collective-permute-start(f32[256,256]{0,1:T(8,128)} %get-tuple-element.768), channel_id=1, source_target_pairs={{8,0},{12,4},{16,8},{20,12},{24,16},{28,20},{32,24},{36,28},{40,32... | collective-permute-start | bytes 786440 | tf_op jit(solution)/shard_map/while/body/eval_jaxpr/ppermute | solution.py:20
  37.3 2.0 %copy-start.3 = (bf16[256,8,128]{0,2,1:T(8,128)(2,1)S(1)}, bf16[256,8,128]{0,2,1:T(8,128)(2,1)}, u32[]{:S(2)}) copy-start(bf16[256,8,128]{0,2,1:T(8,128)(2,1)} %get-tuple-element.799) | copy-start | bytes 1572868 | tf_op jit(solution)/shard_map/while
  38.3 1.0 copy-start.6
  46.4 12.2 %collective-permute-start = (bf16[256,256]{1,0:T(8,128)(2,1)S(1)}, bf16[256,256]{1,0:T(8,128)(2,1)S(1)}, u32[]{:S(2)}, u32[]{:S(2)}) collective-permute-start(bf16[256,256]{1,0:T(8,128)(2,1)S(1)} %copy.140), channel_id=1, source_target_pairs={{8,0},{12,4},{16,8},{20,12},{24,16},{28,20},{32,24},{36,28},{40,32... | collective-permute-start | bytes 393224 | tf_op jit(solution)/shard_map/while/body/eval_jaxpr/ppermute | solution.py:20
  47.0 11.6 %collective-permute-start.1 = (bf16[256,256]{1,0:T(8,128)(2,1)S(1)}, bf16[256,256]{1,0:T(8,128)(2,1)S(1)}, u32[]{:S(2)}, u32[]{:S(2)}) collective-permute-start(bf16[256,256]{1,0:T(8,128)(2,1)S(1)} %copy.141), channel_id=1, source_target_pairs={{56,0},{60,4},{0,8},{4,12},{8,16},{12,20},{16,24},{20,28},{24,32},... | collective-permute-start | bytes 393224 | tf_op jit(solution)/shard_map/while/body/eval_jaxpr/ppermute | solution.py:20
  48.6 9.0 %collective-permute-start.2 = (f32[256,256]{0,1:T(8,128)}, f32[256,256]{0,1:T(8,128)S(1)}, u32[]{:S(2)}, u32[]{:S(2)}) collective-permute-start(f32[256,256]{0,1:T(8,128)} %get-tuple-element.769), channel_id=1, source_target_pairs={{56,0},{60,4},{0,8},{4,12},{8,16},{12,20},{16,24},{20,28},{24,32},... | collective-permute-start | bytes 786440 | tf_op jit(solution)/shard_map/while/body/eval_jaxpr/ppermute | solution.py:20
  48.7 9.0 %collective-permute-start.3 = (f32[256,256]{0,1:T(8,128)}, f32[256,256]{0,1:T(8,128)S(1)}, u32[]{:S(2)}, u32[]{:S(2)}) collective-permute-start(f32[256,256]{0,1:T(8,128)} %get-tuple-element.768), channel_id=1, source_target_pairs={{8,0},{12,4},{16,8},{20,12},{24,16},{28,20},{32,24},{36,28},{40,32... | collective-permute-start | bytes 786440 | tf_op jit(solution)/shard_map/while/body/eval_jaxpr/ppermute | solution.py:20
  51.9 2.0 %copy-start.3 = (bf16[256,8,128]{0,2,1:T(8,128)(2,1)S(1)}, bf16[256,8,128]{0,2,1:T(8,128)(2,1)}, u32[]{:S(2)}) copy-start(bf16[256,8,128]{0,2,1:T(8,128)(2,1)} %get-tuple-element.799) | copy-start | bytes 1572868 | tf_op jit(solution)/shard_map/while
  53.0 1.0 copy-start.6
  58.6 12.2 %collective-permute-start = (bf16[256,256]{1,0:T(8,128)(2,1)S(1)}, bf16[256,256]{1,0:T(8,128)(2,1)S(1)}, u32[]{:S(2)}, u32[]{:S(2)}) collective-permute-start(bf16[256,256]{1,0:T(8,128)(2,1)S(1)} %copy.140), channel_id=1, source_target_pairs={{8,0},{12,4},{16,8},{20,12},{24,16},{28,20},{32,24},{36,28},{40,32... | collective-permute-start | bytes 393224 | tf_op jit(solution)/shard_map/while/body/eval_jaxpr/ppermute | solution.py:20
  60.7 10.1 %collective-permute-start.1 = (bf16[256,256]{1,0:T(8,128)(2,1)S(1)}, bf16[256,256]{1,0:T(8,128)(2,1)S(1)}, u32[]{:S(2)}, u32[]{:S(2)}) collective-permute-start(bf16[256,256]{1,0:T(8,128)(2,1)S(1)} %copy.141), channel_id=1, source_target_pairs={{56,0},{60,4},{0,8},{4,12},{8,16},{12,20},{16,24},{20,28},{24,32},... | collective-permute-start | bytes 393224 | tf_op jit(solution)/shard_map/while/body/eval_jaxpr/ppermute | solution.py:20
  60.8 9.1 %collective-permute-start.2 = (f32[256,256]{0,1:T(8,128)}, f32[256,256]{0,1:T(8,128)S(1)}, u32[]{:S(2)}, u32[]{:S(2)}) collective-permute-start(f32[256,256]{0,1:T(8,128)} %get-tuple-element.769), channel_id=1, source_target_pairs={{56,0},{60,4},{0,8},{4,12},{8,16},{12,20},{16,24},{20,28},{24,32},... | collective-permute-start | bytes 786440 | tf_op jit(solution)/shard_map/while/body/eval_jaxpr/ppermute | solution.py:20
  60.9 9.0 %collective-permute-start.3 = (f32[256,256]{0,1:T(8,128)}, f32[256,256]{0,1:T(8,128)S(1)}, u32[]{:S(2)}, u32[]{:S(2)}) collective-permute-start(f32[256,256]{0,1:T(8,128)} %get-tuple-element.768), channel_id=1, source_target_pairs={{8,0},{12,4},{16,8},{20,12},{24,16},{28,20},{32,24},{36,28},{40,32... | collective-permute-start | bytes 786440 | tf_op jit(solution)/shard_map/while/body/eval_jaxpr/ppermute | solution.py:20
  64.1 2.0 %copy-start.3 = (bf16[256,8,128]{0,2,1:T(8,128)(2,1)S(1)}, bf16[256,8,128]{0,2,1:T(8,128)(2,1)}, u32[]{:S(2)}) copy-start(bf16[256,8,128]{0,2,1:T(8,128)(2,1)} %get-tuple-element.799) | copy-start | bytes 1572868 | tf_op jit(solution)/shard_map/while
  65.2 1.0 copy-start.6
  70.8 12.2 %collective-permute-start = (bf16[256,256]{1,0:T(8,128)(2,1)S(1)}, bf16[256,256]{1,0:T(8,128)(2,1)S(1)}, u32[]{:S(2)}, u32[]{:S(2)}) collective-permute-start(bf16[256,256]{1,0:T(8,128)(2,1)S(1)} %copy.140), channel_id=1, source_target_pairs={{8,0},{12,4},{16,8},{20,12},{24,16},{28,20},{32,24},{36,28},{40,32... | collective-permute-start | bytes 393224 | tf_op jit(solution)/shard_map/while/body/eval_jaxpr/ppermute | solution.py:20
  72.9 10.1 %collective-permute-start.1 = (bf16[256,256]{1,0:T(8,128)(2,1)S(1)}, bf16[256,256]{1,0:T(8,128)(2,1)S(1)}, u32[]{:S(2)}, u32[]{:S(2)}) collective-permute-start(bf16[256,256]{1,0:T(8,128)(2,1)S(1)} %copy.141), channel_id=1, source_target_pairs={{56,0},{60,4},{0,8},{4,12},{8,16},{12,20},{16,24},{20,28},{24,32},... | collective-permute-start | bytes 393224 | tf_op jit(solution)/shard_map/while/body/eval_jaxpr/ppermute | solution.py:20
  73.0 9.1 %collective-permute-start.2 = (f32[256,256]{0,1:T(8,128)}, f32[256,256]{0,1:T(8,128)S(1)}, u32[]{:S(2)}, u32[]{:S(2)}) collective-permute-start(f32[256,256]{0,1:T(8,128)} %get-tuple-element.769), channel_id=1, source_target_pairs={{56,0},{60,4},{0,8},{4,12},{8,16},{12,20},{16,24},{20,28},{24,32},... | collective-permute-start | bytes 786440 | tf_op jit(solution)/shard_map/while/body/eval_jaxpr/ppermute | solution.py:20
  73.3 8.8 %collective-permute-start.3 = (f32[256,256]{0,1:T(8,128)}, f32[256,256]{0,1:T(8,128)S(1)}, u32[]{:S(2)}, u32[]{:S(2)}) collective-permute-start(f32[256,256]{0,1:T(8,128)} %get-tuple-element.768), channel_id=1, source_target_pairs={{8,0},{12,4},{16,8},{20,12},{24,16},{28,20},{32,24},{36,28},{40,32... | collective-permute-start | bytes 786440 | tf_op jit(solution)/shard_map/while/body/eval_jaxpr/ppermute | solution.py:20
  76.3 2.0 %copy-start.3 = (bf16[256,8,128]{0,2,1:T(8,128)(2,1)S(1)}, bf16[256,8,128]{0,2,1:T(8,128)(2,1)}, u32[]{:S(2)}) copy-start(bf16[256,8,128]{0,2,1:T(8,128)(2,1)} %get-tuple-element.799) | copy-start | bytes 1572868 | tf_op jit(solution)/shard_map/while
  77.4 1.0 copy-start.6
  83.0 12.2 %collective-permute-start = (bf16[256,256]{1,0:T(8,128)(2,1)S(1)}, bf16[256,256]{1,0:T(8,128)(2,1)S(1)}, u32[]{:S(2)}, u32[]{:S(2)}) collective-permute-start(bf16[256,256]{1,0:T(8,128)(2,1)S(1)} %copy.140), channel_id=1, source_target_pairs={{8,0},{12,4},{16,8},{20,12},{24,16},{28,20},{32,24},{36,28},{40,32... | collective-permute-start | bytes 393224 | tf_op jit(solution)/shard_map/while/body/eval_jaxpr/ppermute | solution.py:20
  85.1 10.1 %collective-permute-start.1 = (bf16[256,256]{1,0:T(8,128)(2,1)S(1)}, bf16[256,256]{1,0:T(8,128)(2,1)S(1)}, u32[]{:S(2)}, u32[]{:S(2)}) collective-permute-start(bf16[256,256]{1,0:T(8,128)(2,1)S(1)} %copy.141), channel_id=1, source_target_pairs={{56,0},{60,4},{0,8},{4,12},{8,16},{12,20},{16,24},{20,28},{24,32},... | collective-permute-start | bytes 393224 | tf_op jit(solution)/shard_map/while/body/eval_jaxpr/ppermute | solution.py:20
  85.2 9.1 %collective-permute-start.2 = (f32[256,256]{0,1:T(8,128)}, f32[256,256]{0,1:T(8,128)S(1)}, u32[]{:S(2)}, u32[]{:S(2)}) collective-permute-start(f32[256,256]{0,1:T(8,128)} %get-tuple-element.769), channel_id=1, source_target_pairs={{56,0},{60,4},{0,8},{4,12},{8,16},{12,20},{16,24},{20,28},{24,32},... | collective-permute-start | bytes 786440 | tf_op jit(solution)/shard_map/while/body/eval_jaxpr/ppermute | solution.py:20
  85.9 8.4 %collective-permute-start.3 = (f32[256,256]{0,1:T(8,128)}, f32[256,256]{0,1:T(8,128)S(1)}, u32[]{:S(2)}, u32[]{:S(2)}) collective-permute-start(f32[256,256]{0,1:T(8,128)} %get-tuple-element.768), channel_id=1, source_target_pairs={{8,0},{12,4},{16,8},{20,12},{24,16},{28,20},{32,24},{36,28},{40,32... | collective-permute-start | bytes 786440 | tf_op jit(solution)/shard_map/while/body/eval_jaxpr/ppermute | solution.py:20
  88.5 2.0 %copy-start.3 = (bf16[256,8,128]{0,2,1:T(8,128)(2,1)S(1)}, bf16[256,8,128]{0,2,1:T(8,128)(2,1)}, u32[]{:S(2)}) copy-start(bf16[256,8,128]{0,2,1:T(8,128)(2,1)} %get-tuple-element.799) | copy-start | bytes 1572868 | tf_op jit(solution)/shard_map/while
  89.6 1.0 copy-start.6
  95.2 12.2 %collective-permute-start = (bf16[256,256]{1,0:T(8,128)(2,1)S(1)}, bf16[256,256]{1,0:T(8,128)(2,1)S(1)}, u32[]{:S(2)}, u32[]{:S(2)}) collective-permute-start(bf16[256,256]{1,0:T(8,128)(2,1)S(1)} %copy.140), channel_id=1, source_target_pairs={{8,0},{12,4},{16,8},{20,12},{24,16},{28,20},{32,24},{36,28},{40,32... | collective-permute-start | bytes 393224 | tf_op jit(solution)/shard_map/while/body/eval_jaxpr/ppermute | solution.py:20
  97.3 10.1 %collective-permute-start.1 = (bf16[256,256]{1,0:T(8,128)(2,1)S(1)}, bf16[256,256]{1,0:T(8,128)(2,1)S(1)}, u32[]{:S(2)}, u32[]{:S(2)}) collective-permute-start(bf16[256,256]{1,0:T(8,128)(2,1)S(1)} %copy.141), channel_id=1, source_target_pairs={{56,0},{60,4},{0,8},{4,12},{8,16},{12,20},{16,24},{20,28},{24,32},... | collective-permute-start | bytes 393224 | tf_op jit(solution)/shard_map/while/body/eval_jaxpr/ppermute | solution.py:20
  97.4 9.1 %collective-permute-start.2 = (f32[256,256]{0,1:T(8,128)}, f32[256,256]{0,1:T(8,128)S(1)}, u32[]{:S(2)}, u32[]{:S(2)}) collective-permute-start(f32[256,256]{0,1:T(8,128)} %get-tuple-element.769), channel_id=1, source_target_pairs={{56,0},{60,4},{0,8},{4,12},{8,16},{12,20},{16,24},{20,28},{24,32},... | collective-permute-start | bytes 786440 | tf_op jit(solution)/shard_map/while/body/eval_jaxpr/ppermute | solution.py:20
  98.2 8.3 %collective-permute-start.3 = (f32[256,256]{0,1:T(8,128)}, f32[256,256]{0,1:T(8,128)S(1)}, u32[]{:S(2)}, u32[]{:S(2)}) collective-permute-start(f32[256,256]{0,1:T(8,128)} %get-tuple-element.768), channel_id=1, source_target_pairs={{8,0},{12,4},{16,8},{20,12},{24,16},{28,20},{32,24},{36,28},{40,32... | collective-permute-start | bytes 786440 | tf_op jit(solution)/shard_map/while/body/eval_jaxpr/ppermute | solution.py:20
  100.7 2.0 %copy-start.3 = (bf16[256,8,128]{0,2,1:T(8,128)(2,1)S(1)}, bf16[256,8,128]{0,2,1:T(8,128)(2,1)}, u32[]{:S(2)}) copy-start(bf16[256,8,128]{0,2,1:T(8,128)(2,1)} %get-tuple-element.799) | copy-start | bytes 1572868 | tf_op jit(solution)/shard_map/while
  101.8 1.0 copy-start.6
  107.4 1.0 copy-start.4
  114.3 6.5 %collective-permute-start.7 = (f32[256,256]{1,0:T(8,128)S(1)}, f32[256,256]{1,0:T(8,128)S(1)}, u32[]{:S(2)}, u32[]{:S(2)}) collective-permute-start(f32[256,256]{1,0:T(8,128)S(1)} %copy.92), channel_id=1, source_target_pairs={{8,0},{12,4},{16,8},{20,12},{24,16},{28,20},{32,24},{36,28},{40,32... | collective-permute-start | bytes 786440 | tf_op jit(solution)/shard_map/ppermute | solution.py:20
  116.3 8.9 %collective-permute-start.8 = (f32[256,256]{1,0:T(8,128)S(1)}, f32[256,256]{1,0:T(8,128)S(1)}, u32[]{:S(2)}, u32[]{:S(2)}) collective-permute-start(f32[256,256]{1,0:T(8,128)S(1)} %copy.98), channel_id=1, source_target_pairs={{56,0},{60,4},{0,8},{4,12},{8,16},{12,20},{16,24},{20,28},{24,32},... | collective-permute-start | bytes 786440 | tf_op jit(solution)/shard_map/ppermute | solution.py:20
  125.3 8.9 %collective-permute-start.10 = (f32[256,256]{1,0:T(8,128)S(1)}, f32[256,256]{1,0:T(8,128)S(1)}, u32[]{:S(2)}, u32[]{:S(2)}) collective-permute-start(f32[256,256]{1,0:T(8,128)S(1)} %get-tuple-element.612), channel_id=1, source_target_pairs={{0,12},{4,56},{8,20},{12,0},{16,28},{20,8},{24,36},{28,16},{32,44}... | collective-permute-start | bytes 786440 | tf_op jit(solution)/shard_map/ppermute | solution.py:31
  125.4 8.8 %collective-permute-start.9 = (f32[256,256]{1,0:T(8,128)S(1)}, f32[256,256]{1,0:T(8,128)S(1)}, u32[]{:S(2)}, u32[]{:S(2)}) collective-permute-start(f32[256,256]{1,0:T(8,128)S(1)} %get-tuple-element.613), channel_id=1, source_target_pairs={{0,56},{4,12},{8,0},{12,20},{16,8},{20,28},{24,16},{28,36},{32,24}... | collective-permute-start | bytes 786440 | tf_op jit(solution)/shard_map/ppermute | solution.py:31

commit v14 on v13

--- a/solution.py
+++ b/solution.py
@@ -36,7 +36,7 @@
     return lax.ppermute(value, "ctx", pairs)
 
 
-def live_region(block_mask, query_start, tok_rows, key_pos, key_starts):
+def live_region(block_mask, query_start, tok_rows, key_pos, key_starts, with_diagonal):
     row_count = tok_rows // BLK
     block_table = jnp.concatenate(
         [
@@ -50,6 +50,8 @@
     query_block = (query_pos // BLK)[:, None]
     key_block = (key_pos // BLK)[None, :]
     earlier = (key_block < query_block) & (block_table == 1)
+    if not with_diagonal:
+        return earlier
     diagonal = (key_block == query_block) & (key_pos[None, :] <= query_pos[:, None])
     return earlier | diagonal
 
@@ -97,13 +99,13 @@
     super_rows = Y_HI * tok_rows
     offsets = jnp.arange(tok_rows, dtype=jnp.int32)
 
-    def terms(ahead_kv, behind_kv, turn):
+    def terms(ahead_kv, behind_kv, turn, with_diagonal=False):
         ahead_owner = (z_pos + turn) % z_count
         behind_owner = (z_pos - turn) % z_count
         key_starts = (ahead_owner * super_rows, behind_owner * super_rows + tok_rows)
         key_pos = jnp.concatenate([key_starts[0] + offsets, key_starts[1] + offsets])
         live_mask = lax.optimization_barrier(
-            live_region(block_mask, query_start, tok_rows, key_pos, key_starts)
+            live_region(block_mask, query_start, tok_rows, key_pos, key_starts, with_diagonal)
         )
         key_values = jnp.concatenate([ahead_kv, behind_kv], axis=0)
         query_term, key_term, value_term = contract(
@@ -124,7 +126,7 @@
     behind_kv = jnp.where(y_hi == 0, partner_kv, key_values)
     next_ahead = along_z(ahead_kv, ctx_count, 1)
     next_behind = along_z(behind_kv, ctx_count, -1)
-    query_acc, ahead_pending, behind_pending = terms(ahead_kv, behind_kv, 0)
+    query_acc, ahead_pending, behind_pending = terms(ahead_kv, behind_kv, 0, with_diagonal=True)
 
     def visit_turn(turn, carried):
         ahead_kv, behind_kv, query_acc, ahead_pending, behind_pending = carried

time: 137 us -> 136 us (level)
    or x7 -> x0, other arithmetic: 2.04 us -> none  [live_region(): return earlier | diagonal]
    unnamed x16 -> x20, local copies, waits for them, and re-layouts: 3.89 us -> 3.89 us
  transfers between devices with their start and end apart: 32 -> 32, of which waited for: 3 -> 3; matrix products, arithmetic and copies ran while one was open for 45% -> 44% of each run, Pallas kernels for 0% -> 0%
where the time goes in v14:
time: 136 us; the launch traced here: 135 us
  starting transfers between devices  49.9 us (37%)
  matrix products  43.6 us (32%)
  local copies, waits for them, and re-layouts  17.2 us (13%)
  waiting for transfers between devices  13 us (10%)
  other arithmetic  9.51 us (7%)
    ppermute x28, starting transfers between devices, along_z(): return lax.ppermute(value, 'ctx', pairs)  41.4 us
    dot_general x8, matrix products, contract(): jnp.einsum('igd,jd->gij', out_grads, values_part, preferred_element_type=...  12.4 us
    dot_general x8, matrix products, contract(): jnp.einsum('gij,igd->jd', probabilities.astype(jnp.bfloat16), out_grads,...  10.3 us
    dot_general x8, matrix products, contract(): jnp.einsum('gij,igd->jd', dscore, queries, preferred_element_type=jnp.flo...  7.89 us
    dot_general x8, matrix products, contract(): jnp.einsum('igd,jd->gij', queries, keys_part, preferred_element_type=jnp....  7.5 us
    ppermute x28, waiting for transfers between devices, along_z(): return lax.ppermute(value, 'ctx', pairs)  7.07 us
    dynamic_slice x7, local copies, waits for them, and re-layouts, live_region(): lax.dynamic_slice(block_mask, (query_start // BLK, start // BLK), (row_co...  6.09 us
    ppermute x2, waiting for transfers between devices, to_owner(): return lax.ppermute(value, 'ctx', pairs)  5.96 us
  transfers between devices with their start and end apart: 32, of which 3 were waited for; matrix products, arithmetic and copies ran while one was open for 44% of the time, Pallas kernels for 0%

profile of v14, /device:TPU:4, one launch (start us, length us, event | category | flops | bytes accessed | tf_op | source)
XLA Modules:
  0.0 135.4 jit_solution(11752406274828768844)
XLA Ops:
  0.6 0.9 constant_dynamic-update-slice_fusion.3
  1.6 0.9 constant_dynamic-update-slice_fusion.2
  2.4 3.3 %collective-permute-start.4 = (bf16[256,256]{1,0:T(8,128)(2,1)S(1)}, bf16[256,256]{1,0:T(8,128)(2,1)S(1)}, u32[]{:S(2)}, u32[]{:S(2)}) collective-permute-start(bf16[256,256]{1,0:T(8,128)(2,1)S(1)} %constant_dynamic-update-slice_fusion.2), channel_id=1, source_target_pairs={{0,4},{4,0},{8,12},{12,8},{16,20},{20,16},{24,28},{28,24},{32,36},... | collective-permute-start | bytes 393224 | tf_op jit(solution)/shard_map/ppermute | solution.py:36
  5.7 1.9 %copy.130 = bf16[8,4,8,1024]{3,2,0,1:T(8,128)(2,1)} copy(bf16[8,4,8,1024]{3,2,1,0:T(8,128)(2,1)} %bitcast.192) | data formatting | bytes 1048576 | tf_op jit(solution)/shard_map/reshape | solution.py:89
  7.6 3.5 %all-to-all-start = ((bf16[64,4,1024]{2,0,1:T(8,128)(2,1)}), bf16[64,4,1024]{2,0,1:T(8,128)(2,1)S(1)}, u32[]{:S(2)}, u32[]{:S(2)}) async-start(bf16[64,4,1024]{2,0,1:T(8,128)(2,1)} %bitcast.147), calls=%async_computation | async-start | bytes 1048576 | tf_op jit(solution)/shard_map/all_to_all | solution.py:90
  11.3 0.9 fusion.73
  12.8 1.2 copy.74
  14.7 2.0 %collective-permute-start.6 = (bf16[256,256]{1,0:T(8,128)(2,1)S(1)}, bf16[256,256]{1,0:T(8,128)(2,1)S(1)}, u32[]{:S(2)}, u32[]{:S(2)}) collective-permute-start(bf16[256,256]{1,0:T(8,128)(2,1)S(1)} %get-tuple-element.612), channel_id=1, source_target_pairs={{56,0},{60,4},{0,8},{4,12},{8,16},{12,20},{16,24},{20,28},{24,32},... | collective-permute-start | bytes 393224 | tf_op jit(solution)/shard_map/ppermute | solution.py:20
  16.7 4.0 %collective-permute-start.5 = (bf16[256,256]{1,0:T(8,128)(2,1)S(1)}, bf16[256,256]{1,0:T(8,128)(2,1)S(1)}, u32[]{:S(2)}, u32[]{:S(2)}) collective-permute-start(bf16[256,256]{1,0:T(8,128)(2,1)S(1)} %get-tuple-element.613), channel_id=1, source_target_pairs={{8,0},{12,4},{16,8},{20,12},{24,16},{28,20},{32,24},{36,28},{40,32... | collective-permute-start | bytes 393224 | tf_op jit(solution)/shard_map/ppermute | solution.py:20
  20.7 2.7 %fusion.58 = f32[512,256,8]{1,0,2:T(8,128)} fusion(bf16[256,8,128]{0,2,1:T(8,128)(2,1)S(1)} %bitcast.182, bf16[256,256]{1,0:T(8,128)(2,1)S(1)} %get-tuple-element.613, bf16[256,256]{1,0:T(8,128)(2,1)S(1)} %get-tuple-element.612), kind=kOutput, calls=%fused_computation.103 | convolution fusion | flops 268697600 | bytes 4980736 | tf_op jit(solution)/shard_map/igd,jd->gij/dot_general | solution.py:62
  24.2 3.3 %fusion.38 = f32[512,128]{0,1:T(8,128)S(1)} fusion(bf16[256,8,128]{0,2,1:T(8,128)(2,1)S(1)} %copy.85, f32[512,256,8]{1,0,2:T(8,128)} %fusion.58, f32[8,256]{1,0:T(8,128)S(1)} %copy-done.8, pred[256,512]{0,1:T(8,128)(4,1)S(1)} %get-tuple-element.621), kind=kOutput, calls=%fused_computation.64 | convolution fusion | flops 272629760 | bytes 5120000 | tf_op jit(solution)/shard_map/gij,igd->jd/dot_general | solution.py:72
  27.7 1.4 %fusion.27 = bf16[8,256,512]{1,2,0:T(8,128)(2,1)S(1)} fusion(f32[512,256,8]{1,0,2:T(8,128)S(1)} %copy-done, f32[8,256]{1,0:T(8,128)S(1)} %copy.80, f32[8,256]{1,0:T(8,128)S(1)} %copy-done.8, pred[256,512]{0,1:T(8,128)(4,1)S(1)} %get-tuple-element.621, bf16[256,8,128]{2,1,0:T(8,128)(2,1)S(1)} %bitcast.187, bf16[256,256]{1,0:T(8,128)(2,1)S(1)} %get-tuple-element.612, ...), kind=kOutput, calls=%fused_computation.52 | convolution fusion | flops 274989056 | bytes 7225344 | tf_op jit(solution)/shard_map/igd,jd->gij/dot_general | solution.py:66
  30.4 0.8 pad_maximum_fusion.2
  31.2 76.1 %while.26 = (s32[]{:T(128)}, bf16[256,256]{1,0:T(8,128)(2,1)S(1)}, bf16[256,256]{1,0:T(8,128)(2,1)S(1)}, f32[256,8,128]{0,2,1:T(8,128)S(1)}, f32[256,256]{0,1:T(...) while((s32[]{:T(128)}, bf16[256,256]{1,0:T(8,128)(2,1)S(1)}, ...), condition=%wide.region_2.3_spmd.clone.clone, body=%wide.region_1.2_spmd.clone.clone.sunk | while | flops 1353462272 | bytes 32347352 | solution.py:146
  31.4 2.4 %collective-permute-start = (bf16[256,256]{1,0:T(8,128)(2,1)S(1)}, bf16[256,256]{1,0:T(8,128)(2,1)S(1)}, u32[]{:S(2)}, u32[]{:S(2)}) collective-permute-start(bf16[256,256]{1,0:T(8,128)(2,1)S(1)} %copy.140), channel_id=1, source_target_pairs={{8,0},{12,4},{16,8},{20,12},{24,16},{28,20},{32,24},{36,28},{40,32... | collective-permute-start | bytes 393224 | tf_op jit(solution)/shard_map/while/body/eval_jaxpr/ppermute | solution.py:20
  34.0 3.2 %collective-permute-start.3 = (f32[256,256]{0,1:T(8,128)}, f32[256,256]{0,1:T(8,128)S(1)}, u32[]{:S(2)}, u32[]{:S(2)}) collective-permute-start(f32[256,256]{0,1:T(8,128)} %get-tuple-element.754), channel_id=1, source_target_pairs={{8,0},{12,4},{16,8},{20,12},{24,16},{28,20},{32,24},{36,28},{40,32... | collective-permute-start | bytes 786440 | tf_op jit(solution)/shard_map/while/body/eval_jaxpr/ppermute | solution.py:20
  37.3 0.9 fusion.111
  39.3 1.0 fusion.114
  40.3 1.4 %fusion.112 = bf16[8,256,512]{1,2,0:T(8,128)(2,1)S(1)} fusion(f32[512,256,8]{1,0,2:T(8,128)S(1)} %fusion.110, bf16[256,8,128]{0,2,1:T(8,128)(2,1)S(1)} %copy-done.3, f32[8,256]{1,0:T(8,128)S(1)} %copy-done.6, f32[8,256]{1,0:T(8,128)S(1)} %copy-done.9, pred[256,512]{0,1:T(8,128)(4,1)S(1)} %bitcast_and_fusion.4, ...), kind=kOutput, calls=%fused_computation.3.clone.1 | convolution fusion | flops 274726912 | bytes 7094272 | tf_op jit(solution)/shard_map/while/body/eval_jaxpr/igd,jd->gij/dot_general | solution.py:66
  42.2 0.8 convolution_bitcast_fusion.7
  43.0 2.5 %collective-permute-done.2 = f32[256,256]{0,1:T(8,128)S(1)} collective-permute-done((f32[256,256]{0,1:T(8,128)}, f32[256,256]{0,1:T(8,128)S(1)}, u32[]{:S(2)}, u32[]{:S(2)}) %collective-permute-start.2) | collective-permute-done | bytes 262176 | tf_op jit(solution)/shard_map/while/body/eval_jaxpr/ppermute | solution.py:20
  45.5 0.9 fusion.115
  47.0 1.7 %collective-permute-start.1 = (bf16[256,256]{1,0:T(8,128)(2,1)S(1)}, bf16[256,256]{1,0:T(8,128)(2,1)S(1)}, u32[]{:S(2)}, u32[]{:S(2)}) collective-permute-start(bf16[256,256]{1,0:T(8,128)(2,1)S(1)} %copy.141), channel_id=1, source_target_pairs={{56,0},{60,4},{0,8},{4,12},{8,16},{12,20},{16,24},{20,28},{24,32},... | collective-permute-start | bytes 393224 | tf_op jit(solution)/shard_map/while/body/eval_jaxpr/ppermute | solution.py:20
  48.7 3.1 %collective-permute-start.3 = (f32[256,256]{0,1:T(8,128)}, f32[256,256]{0,1:T(8,128)S(1)}, u32[]{:S(2)}, u32[]{:S(2)}) collective-permute-start(f32[256,256]{0,1:T(8,128)} %get-tuple-element.754), channel_id=1, source_target_pairs={{8,0},{12,4},{16,8},{20,12},{24,16},{28,20},{32,24},{36,28},{40,32... | collective-permute-start | bytes 786440 | tf_op jit(solution)/shard_map/while/body/eval_jaxpr/ppermute | solution.py:20
  51.9 0.9 fusion.111
  53.9 1.0 fusion.114
  54.9 1.4 %fusion.112 = bf16[8,256,512]{1,2,0:T(8,128)(2,1)S(1)} fusion(f32[512,256,8]{1,0,2:T(8,128)S(1)} %fusion.110, bf16[256,8,128]{0,2,1:T(8,128)(2,1)S(1)} %copy-done.3, f32[8,256]{1,0:T(8,128)S(1)} %copy-done.6, f32[8,256]{1,0:T(8,128)S(1)} %copy-done.9, pred[256,512]{0,1:T(8,128)(4,1)S(1)} %bitcast_and_fusion.4, ...), kind=kOutput, calls=%fused_computation.3.clone.1 | convolution fusion | flops 274726912 | bytes 7094272 | tf_op jit(solution)/shard_map/while/body/eval_jaxpr/igd,jd->gij/dot_general | solution.py:66
  56.8 0.8 convolution_bitcast_fusion.7
  57.6 0.9 fusion.115
  58.5 2.1 %collective-permute-start = (bf16[256,256]{1,0:T(8,128)(2,1)S(1)}, bf16[256,256]{1,0:T(8,128)(2,1)S(1)}, u32[]{:S(2)}, u32[]{:S(2)}) collective-permute-start(bf16[256,256]{1,0:T(8,128)(2,1)S(1)} %copy.140), channel_id=1, source_target_pairs={{8,0},{12,4},{16,8},{20,12},{24,16},{28,20},{32,24},{36,28},{40,32... | collective-permute-start | bytes 393224 | tf_op jit(solution)/shard_map/while/body/eval_jaxpr/ppermute | solution.py:20
  60.9 3.1 %collective-permute-start.3 = (f32[256,256]{0,1:T(8,128)}, f32[256,256]{0,1:T(8,128)S(1)}, u32[]{:S(2)}, u32[]{:S(2)}) collective-permute-start(f32[256,256]{0,1:T(8,128)} %get-tuple-element.754), channel_id=1, source_target_pairs={{8,0},{12,4},{16,8},{20,12},{24,16},{28,20},{32,24},{36,28},{40,32... | collective-permute-start | bytes 786440 | tf_op jit(solution)/shard_map/while/body/eval_jaxpr/ppermute | solution.py:20
  64.1 0.9 fusion.111
  66.1 1.0 fusion.114
  67.1 1.4 %fusion.112 = bf16[8,256,512]{1,2,0:T(8,128)(2,1)S(1)} fusion(f32[512,256,8]{1,0,2:T(8,128)S(1)} %fusion.110, bf16[256,8,128]{0,2,1:T(8,128)(2,1)S(1)} %copy-done.3, f32[8,256]{1,0:T(8,128)S(1)} %copy-done.6, f32[8,256]{1,0:T(8,128)S(1)} %copy-done.9, pred[256,512]{0,1:T(8,128)(4,1)S(1)} %bitcast_and_fusion.4, ...), kind=kOutput, calls=%fused_computation.3.clone.1 | convolution fusion | flops 274726912 | bytes 7094272 | tf_op jit(solution)/shard_map/while/body/eval_jaxpr/igd,jd->gij/dot_general | solution.py:66
  69.8 0.9 fusion.115
  70.8 2.1 %collective-permute-start = (bf16[256,256]{1,0:T(8,128)(2,1)S(1)}, bf16[256,256]{1,0:T(8,128)(2,1)S(1)}, u32[]{:S(2)}, u32[]{:S(2)}) collective-permute-start(bf16[256,256]{1,0:T(8,128)(2,1)S(1)} %copy.140), channel_id=1, source_target_pairs={{8,0},{12,4},{16,8},{20,12},{24,16},{28,20},{32,24},{36,28},{40,32... | collective-permute-start | bytes 393224 | tf_op jit(solution)/shard_map/while/body/eval_jaxpr/ppermute | solution.py:20
  73.1 3.2 %collective-permute-start.3 = (f32[256,256]{0,1:T(8,128)}, f32[256,256]{0,1:T(8,128)S(1)}, u32[]{:S(2)}, u32[]{:S(2)}) collective-permute-start(f32[256,256]{0,1:T(8,128)} %get-tuple-element.754), channel_id=1, source_target_pairs={{8,0},{12,4},{16,8},{20,12},{24,16},{28,20},{32,24},{36,28},{40,32... | collective-permute-start | bytes 786440 | tf_op jit(solution)/shard_map/while/body/eval_jaxpr/ppermute | solution.py:20
  76.3 0.9 fusion.111
  78.3 1.0 fusion.114
  79.3 1.4 %fusion.112 = bf16[8,256,512]{1,2,0:T(8,128)(2,1)S(1)} fusion(f32[512,256,8]{1,0,2:T(8,128)S(1)} %fusion.110, bf16[256,8,128]{0,2,1:T(8,128)(2,1)S(1)} %copy-done.3, f32[8,256]{1,0:T(8,128)S(1)} %copy-done.6, f32[8,256]{1,0:T(8,128)S(1)} %copy-done.9, pred[256,512]{0,1:T(8,128)(4,1)S(1)} %bitcast_and_fusion.4, ...), kind=kOutput, calls=%fused_computation.3.clone.1 | convolution fusion | flops 274726912 | bytes 7094272 | tf_op jit(solution)/shard_map/while/body/eval_jaxpr/igd,jd->gij/dot_general | solution.py:66
  82.0 0.9 fusion.115
  83.0 2.1 %collective-permute-start = (bf16[256,256]{1,0:T(8,128)(2,1)S(1)}, bf16[256,256]{1,0:T(8,128)(2,1)S(1)}, u32[]{:S(2)}, u32[]{:S(2)}) collective-permute-start(bf16[256,256]{1,0:T(8,128)(2,1)S(1)} %copy.140), channel_id=1, source_target_pairs={{8,0},{12,4},{16,8},{20,12},{24,16},{28,20},{32,24},{36,28},{40,32... | collective-permute-start | bytes 393224 | tf_op jit(solution)/shard_map/while/body/eval_jaxpr/ppermute | solution.py:20
  85.6 2.9 %collective-permute-start.3 = (f32[256,256]{0,1:T(8,128)}, f32[256,256]{0,1:T(8,128)S(1)}, u32[]{:S(2)}, u32[]{:S(2)}) collective-permute-start(f32[256,256]{0,1:T(8,128)} %get-tuple-element.754), channel_id=1, source_target_pairs={{8,0},{12,4},{16,8},{20,12},{24,16},{28,20},{32,24},{36,28},{40,32... | collective-permute-start | bytes 786440 | tf_op jit(solution)/shard_map/while/body/eval_jaxpr/ppermute | solution.py:20
  88.5 0.9 fusion.111
  90.5 1.0 fusion.114
  91.5 1.4 %fusion.112 = bf16[8,256,512]{1,2,0:T(8,128)(2,1)S(1)} fusion(f32[512,256,8]{1,0,2:T(8,128)S(1)} %fusion.110, bf16[256,8,128]{0,2,1:T(8,128)(2,1)S(1)} %copy-done.3, f32[8,256]{1,0:T(8,128)S(1)} %copy-done.6, f32[8,256]{1,0:T(8,128)S(1)} %copy-done.9, pred[256,512]{0,1:T(8,128)(4,1)S(1)} %bitcast_and_fusion.4, ...), kind=kOutput, calls=%fused_computation.3.clone.1 | convolution fusion | flops 274726912 | bytes 7094272 | tf_op jit(solution)/shard_map/while/body/eval_jaxpr/igd,jd->gij/dot_general | solution.py:66
  94.2 0.9 fusion.115
  95.2 2.1 %collective-permute-start = (bf16[256,256]{1,0:T(8,128)(2,1)S(1)}, bf16[256,256]{1,0:T(8,128)(2,1)S(1)}, u32[]{:S(2)}, u32[]{:S(2)}) collective-permute-start(bf16[256,256]{1,0:T(8,128)(2,1)S(1)} %copy.140), channel_id=1, source_target_pairs={{8,0},{12,4},{16,8},{20,12},{24,16},{28,20},{32,24},{36,28},{40,32... | collective-permute-start | bytes 393224 | tf_op jit(solution)/shard_map/while/body/eval_jaxpr/ppermute | solution.py:20
  98.0 2.7 %collective-permute-start.3 = (f32[256,256]{0,1:T(8,128)}, f32[256,256]{0,1:T(8,128)S(1)}, u32[]{:S(2)}, u32[]{:S(2)}) collective-permute-start(f32[256,256]{0,1:T(8,128)} %get-tuple-element.754), channel_id=1, source_target_pairs={{8,0},{12,4},{16,8},{20,12},{24,16},{28,20},{32,24},{36,28},{40,32... | collective-permute-start | bytes 786440 | tf_op jit(solution)/shard_map/while/body/eval_jaxpr/ppermute | solution.py:20
  100.8 0.9 fusion.111
  102.7 1.0 fusion.114
  103.7 1.4 %fusion.112 = bf16[8,256,512]{1,2,0:T(8,128)(2,1)S(1)} fusion(f32[512,256,8]{1,0,2:T(8,128)S(1)} %fusion.110, bf16[256,8,128]{0,2,1:T(8,128)(2,1)S(1)} %copy-done.3, f32[8,256]{1,0:T(8,128)S(1)} %copy-done.6, f32[8,256]{1,0:T(8,128)S(1)} %copy-done.9, pred[256,512]{0,1:T(8,128)(4,1)S(1)} %bitcast_and_fusion.4, ...), kind=kOutput, calls=%fused_computation.3.clone.1 | convolution fusion | flops 274726912 | bytes 7094272 | tf_op jit(solution)/shard_map/while/body/eval_jaxpr/igd,jd->gij/dot_general | solution.py:66
  106.5 0.9 fusion.115
  108.4 0.9 fusion.41
  109.3 2.8 %fusion.23 = bf16[8,256,512]{1,2,0:T(8,128)(2,1)} fusion(f32[512,256,8]{1,0,2:T(8,128)S(1)} %fusion.57, f32[8,256]{1,0:T(8,128)S(1)} %copy-done.7, f32[8,256]{1,0:T(8,128)S(1)} %get-tuple-element.831, pred[256,512]{0,1:T(8,128)(4,1)S(1)} %get-tuple-element.620, bf16[256,8,128]{2,1,0:T(8,128)(2,1)S(1)} %bitcast.188, ...), kind=kOutput, calls=%fused_computation.46 | convolution fusion | flops 274726912 | bytes 7094272 | tf_op jit(solution)/shard_map/igd,jd->gij/dot_general | solution.py:66
  112.0 1.1 copy.98
  113.1 1.1 copy.92
  114.2 2.1 %collective-permute-start.7 = (f32[256,256]{1,0:T(8,128)S(1)}, f32[256,256]{1,0:T(8,128)S(1)}, u32[]{:S(2)}, u32[]{:S(2)}) collective-permute-start(f32[256,256]{1,0:T(8,128)S(1)} %copy.92), channel_id=1, source_target_pairs={{8,0},{12,4},{16,8},{20,12},{24,16},{28,20},{32,24},{36,28},{40,32... | collective-permute-start | bytes 786440 | tf_op jit(solution)/shard_map/ppermute | solution.py:20
  116.3 2.1 %convolution_bitcast_fusion.2 = f32[256,8,128]{0,2,1:T(8,128)S(1)} fusion(bf16[8,256,512]{1,2,0:T(8,128)(2,1)} %fusion.23, bf16[512,256]{1,0:T(8,128)(2,1)S(1)} %constant_dynamic-update-slice_fusion.4), kind=kOutput, calls=%fused_computation.62 | convolution fusion | flops 268435456 | bytes 3276800 | tf_op jit(solution)/shard_map/gij,jd->igd/dot_general | solution.py:70
  118.4 2.3 %convolution_bitcast_fusion.4 = f32[512,128]{1,0:T(8,128)S(1)} fusion(bf16[8,256,512]{1,2,0:T(8,128)(2,1)} %fusion.23, bf16[256,8,128]{0,2,1:T(8,128)(2,1)S(1)} %get-tuple-element.830), kind=kOutput, calls=%fused_computation.66 | convolution fusion | flops 268435456 | bytes 2883584 | tf_op jit(solution)/shard_map/gij,igd->jd/dot_general | solution.py:71
  120.7 4.5 %collective-permute-done.8 = f32[256,256]{1,0:T(8,128)S(1)} collective-permute-done((f32[256,256]{1,0:T(8,128)S(1)}, f32[256,256]{1,0:T(8,128)S(1)}, u32[]{:S(2)}, u32[]{:S(2)}) %collective-permute-start.8) | collective-permute-done | bytes 262176 | tf_op jit(solution)/shard_map/ppermute | solution.py:20
  125.3 1.6 %collective-permute-start.9 = (f32[256,256]{1,0:T(8,128)S(1)}, f32[256,256]{1,0:T(8,128)S(1)}, u32[]{:S(2)}, u32[]{:S(2)}) collective-permute-start(f32[256,256]{1,0:T(8,128)S(1)} %get-tuple-element.609), channel_id=1, source_target_pairs={{0,56},{4,12},{8,0},{12,20},{16,8},{20,28},{24,16},{28,36},{32,24}... | collective-permute-start | bytes 786440 | tf_op jit(solution)/shard_map/ppermute | solution.py:31
  127.1 1.0 copy.99
  128.1 6.0 %collective-permute-done.10 = f32[256,256]{1,0:T(8,128)S(1)} collective-permute-done((f32[256,256]{1,0:T(8,128)S(1)}, f32[256,256]{1,0:T(8,128)S(1)}, u32[]{:S(2)}, u32[]{:S(2)}) %collective-permute-start.10) | collective-permute-done | bytes 262176 | tf_op jit(solution)/shard_map/ppermute | solution.py:31
  (195 shorter events, 21.1 us)
Async XLA Ops:
  0.6 13.5 %copy-start.1 = (bf16[256,1024]{1,0:T(8,128)(2,1)S(1)}, bf16[256,1024]{1,0:T(8,128)(2,1)}, u32[]{:S(2)}) copy-start(bf16[256,1024]{1,0:T(8,128)(2,1)} %param.12) | copy-start | bytes 1572868
  2.4 12.2 %collective-permute-start.4 = (bf16[256,256]{1,0:T(8,128)(2,1)S(1)}, bf16[256,256]{1,0:T(8,128)(2,1)S(1)}, u32[]{:S(2)}, u32[]{:S(2)}) collective-permute-start(bf16[256,256]{1,0:T(8,128)(2,1)S(1)} %constant_dynamic-update-slice_fusion.2), channel_id=1, source_target_pairs={{0,4},{4,0},{8,12},{12,8},{16,20},{20,16},{24,28},{28,24},{32,36},... | collective-permute-start | bytes 393224 | tf_op jit(solution)/shard_map/ppermute | solution.py:36
  7.6 15.8 %all-to-all-start = ((bf16[64,4,1024]{2,0,1:T(8,128)(2,1)}), bf16[64,4,1024]{2,0,1:T(8,128)(2,1)S(1)}, u32[]{:S(2)}, u32[]{:S(2)}) async-start(bf16[64,4,1024]{2,0,1:T(8,128)(2,1)} %bitcast.147), calls=%async_computation | async-start | bytes 1048576 | tf_op jit(solution)/shard_map/all_to_all | solution.py:90
  14.7 16.6 %collective-permute-start.6 = (bf16[256,256]{1,0:T(8,128)(2,1)S(1)}, bf16[256,256]{1,0:T(8,128)(2,1)S(1)}, u32[]{:S(2)}, u32[]{:S(2)}) collective-permute-start(bf16[256,256]{1,0:T(8,128)(2,1)S(1)} %get-tuple-element.612), channel_id=1, source_target_pairs={{56,0},{60,4},{0,8},{4,12},{8,16},{12,20},{16,24},{20,28},{24,32},... | collective-permute-start | bytes 393224 | tf_op jit(solution)/shard_map/ppermute | solution.py:20
  16.7 14.6 %collective-permute-start.5 = (bf16[256,256]{1,0:T(8,128)(2,1)S(1)}, bf16[256,256]{1,0:T(8,128)(2,1)S(1)}, u32[]{:S(2)}, u32[]{:S(2)}) collective-permute-start(bf16[256,256]{1,0:T(8,128)(2,1)S(1)} %get-tuple-element.613), channel_id=1, source_target_pairs={{8,0},{12,4},{16,8},{20,12},{24,16},{28,20},{32,24},{36,28},{40,32... | collective-permute-start | bytes 393224 | tf_op jit(solution)/shard_map/ppermute | solution.py:20
  20.7 3.5 %copy-start.8 = (f32[8,256]{1,0:T(8,128)S(1)}, f32[8,256]{1,0:T(8,128)}, u32[]{:S(2)}) copy-start(f32[8,256]{1,0:T(8,128)} %param.14) | copy-start | bytes 24580
  23.8 5.3 %copy-start.2 = (bf16[256,8,128]{0,2,1:T(8,128)(2,1)}, bf16[256,8,128]{0,2,1:T(8,128)(2,1)S(1)}, u32[]{:S(2)}) copy-start(bf16[256,8,128]{0,2,1:T(8,128)(2,1)S(1)} %copy.85) | copy-start | bytes 1572868
  24.2 3.4 %copy-start.5 = (f32[8,256]{1,0:T(8,128)}, f32[8,256]{1,0:T(8,128)S(1)}, u32[]{:S(2)}) copy-start(f32[8,256]{1,0:T(8,128)S(1)} %copy.80) | copy-start | bytes 24580
  24.2 3.5 %copy-start = (f32[512,256,8]{1,0,2:T(8,128)S(1)}, f32[512,256,8]{1,0,2:T(8,128)}, u32[]{:S(2)}) copy-start(f32[512,256,8]{1,0,2:T(8,128)} %fusion.58) | copy-start | bytes 12582916
  31.4 15.0 %collective-permute-start = (bf16[256,256]{1,0:T(8,128)(2,1)S(1)}, bf16[256,256]{1,0:T(8,128)(2,1)S(1)}, u32[]{:S(2)}, u32[]{:S(2)}) collective-permute-start(bf16[256,256]{1,0:T(8,128)(2,1)S(1)} %copy.140), channel_id=1, source_target_pairs={{8,0},{12,4},{16,8},{20,12},{24,16},{28,20},{32,24},{36,28},{40,32... | collective-permute-start | bytes 393224 | tf_op jit(solution)/shard_map/while/body/eval_jaxpr/ppermute | solution.py:20
  33.8 12.6 %collective-permute-start.1 = (bf16[256,256]{1,0:T(8,128)(2,1)S(1)}, bf16[256,256]{1,0:T(8,128)(2,1)S(1)}, u32[]{:S(2)}, u32[]{:S(2)}) collective-permute-start(bf16[256,256]{1,0:T(8,128)(2,1)S(1)} %copy.141), channel_id=1, source_target_pairs={{56,0},{60,4},{0,8},{4,12},{8,16},{12,20},{16,24},{20,28},{24,32},... | collective-permute-start | bytes 393224 | tf_op jit(solution)/shard_map/while/body/eval_jaxpr/ppermute | solution.py:20
  33.9 11.6 %collective-permute-start.2 = (f32[256,256]{0,1:T(8,128)}, f32[256,256]{0,1:T(8,128)S(1)}, u32[]{:S(2)}, u32[]{:S(2)}) collective-permute-start(f32[256,256]{0,1:T(8,128)} %get-tuple-element.755), channel_id=1, source_target_pairs={{56,0},{60,4},{0,8},{4,12},{8,16},{12,20},{16,24},{20,28},{24,32},... | collective-permute-start | bytes 786440 | tf_op jit(solution)/shard_map/while/body/eval_jaxpr/ppermute | solution.py:20
  34.0 11.5 %collective-permute-start.3 = (f32[256,256]{0,1:T(8,128)}, f32[256,256]{0,1:T(8,128)S(1)}, u32[]{:S(2)}, u32[]{:S(2)}) collective-permute-start(f32[256,256]{0,1:T(8,128)} %get-tuple-element.754), channel_id=1, source_target_pairs={{8,0},{12,4},{16,8},{20,12},{24,16},{28,20},{32,24},{36,28},{40,32... | collective-permute-start | bytes 786440 | tf_op jit(solution)/shard_map/while/body/eval_jaxpr/ppermute | solution.py:20
  37.3 1.9 %copy-start.3 = (bf16[256,8,128]{0,2,1:T(8,128)(2,1)S(1)}, bf16[256,8,128]{0,2,1:T(8,128)(2,1)}, u32[]{:S(2)}) copy-start(bf16[256,8,128]{0,2,1:T(8,128)(2,1)} %get-tuple-element.785) | copy-start | bytes 1572868 | tf_op jit(solution)/shard_map/while
  38.3 0.9 copy-start.9
  39.2 1.1 copy-start.6
  46.4 12.1 %collective-permute-start = (bf16[256,256]{1,0:T(8,128)(2,1)S(1)}, bf16[256,256]{1,0:T(8,128)(2,1)S(1)}, u32[]{:S(2)}, u32[]{:S(2)}) collective-permute-start(bf16[256,256]{1,0:T(8,128)(2,1)S(1)} %copy.140), channel_id=1, source_target_pairs={{8,0},{12,4},{16,8},{20,12},{24,16},{28,20},{32,24},{36,28},{40,32... | collective-permute-start | bytes 393224 | tf_op jit(solution)/shard_map/while/body/eval_jaxpr/ppermute | solution.py:20
  47.0 11.6 %collective-permute-start.1 = (bf16[256,256]{1,0:T(8,128)(2,1)S(1)}, bf16[256,256]{1,0:T(8,128)(2,1)S(1)}, u32[]{:S(2)}, u32[]{:S(2)}) collective-permute-start(bf16[256,256]{1,0:T(8,128)(2,1)S(1)} %copy.141), channel_id=1, source_target_pairs={{56,0},{60,4},{0,8},{4,12},{8,16},{12,20},{16,24},{20,28},{24,32},... | collective-permute-start | bytes 393224 | tf_op jit(solution)/shard_map/while/body/eval_jaxpr/ppermute | solution.py:20
  48.6 9.0 %collective-permute-start.2 = (f32[256,256]{0,1:T(8,128)}, f32[256,256]{0,1:T(8,128)S(1)}, u32[]{:S(2)}, u32[]{:S(2)}) collective-permute-start(f32[256,256]{0,1:T(8,128)} %get-tuple-element.755), channel_id=1, source_target_pairs={{56,0},{60,4},{0,8},{4,12},{8,16},{12,20},{16,24},{20,28},{24,32},... | collective-permute-start | bytes 786440 | tf_op jit(solution)/shard_map/while/body/eval_jaxpr/ppermute | solution.py:20
  48.7 8.9 %collective-permute-start.3 = (f32[256,256]{0,1:T(8,128)}, f32[256,256]{0,1:T(8,128)S(1)}, u32[]{:S(2)}, u32[]{:S(2)}) collective-permute-start(f32[256,256]{0,1:T(8,128)} %get-tuple-element.754), channel_id=1, source_target_pairs={{8,0},{12,4},{16,8},{20,12},{24,16},{28,20},{32,24},{36,28},{40,32... | collective-permute-start | bytes 786440 | tf_op jit(solution)/shard_map/while/body/eval_jaxpr/ppermute | solution.py:20
  51.9 1.9 %copy-start.3 = (bf16[256,8,128]{0,2,1:T(8,128)(2,1)S(1)}, bf16[256,8,128]{0,2,1:T(8,128)(2,1)}, u32[]{:S(2)}) copy-start(bf16[256,8,128]{0,2,1:T(8,128)(2,1)} %get-tuple-element.785) | copy-start | bytes 1572868 | tf_op jit(solution)/shard_map/while
  53.0 0.9 copy-start.9
  53.8 1.1 copy-start.6
  58.5 12.2 %collective-permute-start = (bf16[256,256]{1,0:T(8,128)(2,1)S(1)}, bf16[256,256]{1,0:T(8,128)(2,1)S(1)}, u32[]{:S(2)}, u32[]{:S(2)}) collective-permute-start(bf16[256,256]{1,0:T(8,128)(2,1)S(1)} %copy.140), channel_id=1, source_target_pairs={{8,0},{12,4},{16,8},{20,12},{24,16},{28,20},{32,24},{36,28},{40,32... | collective-permute-start | bytes 393224 | tf_op jit(solution)/shard_map/while/body/eval_jaxpr/ppermute | solution.py:20
  60.7 10.1 %collective-permute-start.1 = (bf16[256,256]{1,0:T(8,128)(2,1)S(1)}, bf16[256,256]{1,0:T(8,128)(2,1)S(1)}, u32[]{:S(2)}, u32[]{:S(2)}) collective-permute-start(bf16[256,256]{1,0:T(8,128)(2,1)S(1)} %copy.141), channel_id=1, source_target_pairs={{56,0},{60,4},{0,8},{4,12},{8,16},{12,20},{16,24},{20,28},{24,32},... | collective-permute-start | bytes 393224 | tf_op jit(solution)/shard_map/while/body/eval_jaxpr/ppermute | solution.py:20
  60.8 9.1 %collective-permute-start.2 = (f32[256,256]{0,1:T(8,128)}, f32[256,256]{0,1:T(8,128)S(1)}, u32[]{:S(2)}, u32[]{:S(2)}) collective-permute-start(f32[256,256]{0,1:T(8,128)} %get-tuple-element.755), channel_id=1, source_target_pairs={{56,0},{60,4},{0,8},{4,12},{8,16},{12,20},{16,24},{20,28},{24,32},... | collective-permute-start | bytes 786440 | tf_op jit(solution)/shard_map/while/body/eval_jaxpr/ppermute | solution.py:20
  60.9 8.9 %collective-permute-start.3 = (f32[256,256]{0,1:T(8,128)}, f32[256,256]{0,1:T(8,128)S(1)}, u32[]{:S(2)}, u32[]{:S(2)}) collective-permute-start(f32[256,256]{0,1:T(8,128)} %get-tuple-element.754), channel_id=1, source_target_pairs={{8,0},{12,4},{16,8},{20,12},{24,16},{28,20},{32,24},{36,28},{40,32... | collective-permute-start | bytes 786440 | tf_op jit(solution)/shard_map/while/body/eval_jaxpr/ppermute | solution.py:20
  64.1 1.9 %copy-start.3 = (bf16[256,8,128]{0,2,1:T(8,128)(2,1)S(1)}, bf16[256,8,128]{0,2,1:T(8,128)(2,1)}, u32[]{:S(2)}) copy-start(bf16[256,8,128]{0,2,1:T(8,128)(2,1)} %get-tuple-element.785) | copy-start | bytes 1572868 | tf_op jit(solution)/shard_map/while
  65.2 0.9 copy-start.9
  66.1 1.1 copy-start.6
  70.8 12.2 %collective-permute-start = (bf16[256,256]{1,0:T(8,128)(2,1)S(1)}, bf16[256,256]{1,0:T(8,128)(2,1)S(1)}, u32[]{:S(2)}, u32[]{:S(2)}) collective-permute-start(bf16[256,256]{1,0:T(8,128)(2,1)S(1)} %copy.140), channel_id=1, source_target_pairs={{8,0},{12,4},{16,8},{20,12},{24,16},{28,20},{32,24},{36,28},{40,32... | collective-permute-start | bytes 393224 | tf_op jit(solution)/shard_map/while/body/eval_jaxpr/ppermute | solution.py:20
  72.9 10.1 %collective-permute-start.1 = (bf16[256,256]{1,0:T(8,128)(2,1)S(1)}, bf16[256,256]{1,0:T(8,128)(2,1)S(1)}, u32[]{:S(2)}, u32[]{:S(2)}) collective-permute-start(bf16[256,256]{1,0:T(8,128)(2,1)S(1)} %copy.141), channel_id=1, source_target_pairs={{56,0},{60,4},{0,8},{4,12},{8,16},{12,20},{16,24},{20,28},{24,32},... | collective-permute-start | bytes 393224 | tf_op jit(solution)/shard_map/while/body/eval_jaxpr/ppermute | solution.py:20
  73.0 9.1 %collective-permute-start.2 = (f32[256,256]{0,1:T(8,128)}, f32[256,256]{0,1:T(8,128)S(1)}, u32[]{:S(2)}, u32[]{:S(2)}) collective-permute-start(f32[256,256]{0,1:T(8,128)} %get-tuple-element.755), channel_id=1, source_target_pairs={{56,0},{60,4},{0,8},{4,12},{8,16},{12,20},{16,24},{20,28},{24,32},... | collective-permute-start | bytes 786440 | tf_op jit(solution)/shard_map/while/body/eval_jaxpr/ppermute | solution.py:20
  73.1 9.0 %collective-permute-start.3 = (f32[256,256]{0,1:T(8,128)}, f32[256,256]{0,1:T(8,128)S(1)}, u32[]{:S(2)}, u32[]{:S(2)}) collective-permute-start(f32[256,256]{0,1:T(8,128)} %get-tuple-element.754), channel_id=1, source_target_pairs={{8,0},{12,4},{16,8},{20,12},{24,16},{28,20},{32,24},{36,28},{40,32... | collective-permute-start | bytes 786440 | tf_op jit(solution)/shard_map/while/body/eval_jaxpr/ppermute | solution.py:20
  76.3 2.0 %copy-start.3 = (bf16[256,8,128]{0,2,1:T(8,128)(2,1)S(1)}, bf16[256,8,128]{0,2,1:T(8,128)(2,1)}, u32[]{:S(2)}) copy-start(bf16[256,8,128]{0,2,1:T(8,128)(2,1)} %get-tuple-element.785) | copy-start | bytes 1572868 | tf_op jit(solution)/shard_map/while
  77.4 0.9 copy-start.9
  78.3 1.1 copy-start.6
  83.0 12.2 %collective-permute-start = (bf16[256,256]{1,0:T(8,128)(2,1)S(1)}, bf16[256,256]{1,0:T(8,128)(2,1)S(1)}, u32[]{:S(2)}, u32[]{:S(2)}) collective-permute-start(bf16[256,256]{1,0:T(8,128)(2,1)S(1)} %copy.140), channel_id=1, source_target_pairs={{8,0},{12,4},{16,8},{20,12},{24,16},{28,20},{32,24},{36,28},{40,32... | collective-permute-start | bytes 393224 | tf_op jit(solution)/shard_map/while/body/eval_jaxpr/ppermute | solution.py:20
  85.1 10.1 %collective-permute-start.1 = (bf16[256,256]{1,0:T(8,128)(2,1)S(1)}, bf16[256,256]{1,0:T(8,128)(2,1)S(1)}, u32[]{:S(2)}, u32[]{:S(2)}) collective-permute-start(bf16[256,256]{1,0:T(8,128)(2,1)S(1)} %copy.141), channel_id=1, source_target_pairs={{56,0},{60,4},{0,8},{4,12},{8,16},{12,20},{16,24},{20,28},{24,32},... | collective-permute-start | bytes 393224 | tf_op jit(solution)/shard_map/while/body/eval_jaxpr/ppermute | solution.py:20
  85.2 9.0 %collective-permute-start.2 = (f32[256,256]{0,1:T(8,128)}, f32[256,256]{0,1:T(8,128)S(1)}, u32[]{:S(2)}, u32[]{:S(2)}) collective-permute-start(f32[256,256]{0,1:T(8,128)} %get-tuple-element.755), channel_id=1, source_target_pairs={{56,0},{60,4},{0,8},{4,12},{8,16},{12,20},{16,24},{20,28},{24,32},... | collective-permute-start | bytes 786440 | tf_op jit(solution)/shard_map/while/body/eval_jaxpr/ppermute | solution.py:20
  85.6 8.6 %collective-permute-start.3 = (f32[256,256]{0,1:T(8,128)}, f32[256,256]{0,1:T(8,128)S(1)}, u32[]{:S(2)}, u32[]{:S(2)}) collective-permute-start(f32[256,256]{0,1:T(8,128)} %get-tuple-element.754), channel_id=1, source_target_pairs={{8,0},{12,4},{16,8},{20,12},{24,16},{28,20},{32,24},{36,28},{40,32... | collective-permute-start | bytes 786440 | tf_op jit(solution)/shard_map/while/body/eval_jaxpr/ppermute | solution.py:20
  88.5 1.9 %copy-start.3 = (bf16[256,8,128]{0,2,1:T(8,128)(2,1)S(1)}, bf16[256,8,128]{0,2,1:T(8,128)(2,1)}, u32[]{:S(2)}) copy-start(bf16[256,8,128]{0,2,1:T(8,128)(2,1)} %get-tuple-element.785) | copy-start | bytes 1572868 | tf_op jit(solution)/shard_map/while
  89.6 0.9 copy-start.9
  90.5 1.1 copy-start.6
  95.2 12.2 %collective-permute-start = (bf16[256,256]{1,0:T(8,128)(2,1)S(1)}, bf16[256,256]{1,0:T(8,128)(2,1)S(1)}, u32[]{:S(2)}, u32[]{:S(2)}) collective-permute-start(bf16[256,256]{1,0:T(8,128)(2,1)S(1)} %copy.140), channel_id=1, source_target_pairs={{8,0},{12,4},{16,8},{20,12},{24,16},{28,20},{32,24},{36,28},{40,32... | collective-permute-start | bytes 393224 | tf_op jit(solution)/shard_map/while/body/eval_jaxpr/ppermute | solution.py:20
  97.3 10.1 %collective-permute-start.1 = (bf16[256,256]{1,0:T(8,128)(2,1)S(1)}, bf16[256,256]{1,0:T(8,128)(2,1)S(1)}, u32[]{:S(2)}, u32[]{:S(2)}) collective-permute-start(bf16[256,256]{1,0:T(8,128)(2,1)S(1)} %copy.141), channel_id=1, source_target_pairs={{56,0},{60,4},{0,8},{4,12},{8,16},{12,20},{16,24},{20,28},{24,32},... | collective-permute-start | bytes 393224 | tf_op jit(solution)/shard_map/while/body/eval_jaxpr/ppermute | solution.py:20
  97.4 9.1 %collective-permute-start.2 = (f32[256,256]{0,1:T(8,128)}, f32[256,256]{0,1:T(8,128)S(1)}, u32[]{:S(2)}, u32[]{:S(2)}) collective-permute-start(f32[256,256]{0,1:T(8,128)} %get-tuple-element.755), channel_id=1, source_target_pairs={{56,0},{60,4},{0,8},{4,12},{8,16},{12,20},{16,24},{20,28},{24,32},... | collective-permute-start | bytes 786440 | tf_op jit(solution)/shard_map/while/body/eval_jaxpr/ppermute | solution.py:20
  98.0 8.4 %collective-permute-start.3 = (f32[256,256]{0,1:T(8,128)}, f32[256,256]{0,1:T(8,128)S(1)}, u32[]{:S(2)}, u32[]{:S(2)}) collective-permute-start(f32[256,256]{0,1:T(8,128)} %get-tuple-element.754), channel_id=1, source_target_pairs={{8,0},{12,4},{16,8},{20,12},{24,16},{28,20},{32,24},{36,28},{40,32... | collective-permute-start | bytes 786440 | tf_op jit(solution)/shard_map/while/body/eval_jaxpr/ppermute | solution.py:20
  100.7 1.9 %copy-start.3 = (bf16[256,8,128]{0,2,1:T(8,128)(2,1)S(1)}, bf16[256,8,128]{0,2,1:T(8,128)(2,1)}, u32[]{:S(2)}) copy-start(bf16[256,8,128]{0,2,1:T(8,128)(2,1)} %get-tuple-element.785) | copy-start | bytes 1572868 | tf_op jit(solution)/shard_map/while
  101.8 0.9 copy-start.9
  102.7 1.1 copy-start.6
  107.4 1.0 copy-start.4
  108.4 0.9 copy-start.7
  114.2 6.5 %collective-permute-start.7 = (f32[256,256]{1,0:T(8,128)S(1)}, f32[256,256]{1,0:T(8,128)S(1)}, u32[]{:S(2)}, u32[]{:S(2)}) collective-permute-start(f32[256,256]{1,0:T(8,128)S(1)} %copy.92), channel_id=1, source_target_pairs={{8,0},{12,4},{16,8},{20,12},{24,16},{28,20},{32,24},{36,28},{40,32... | collective-permute-start | bytes 786440 | tf_op jit(solution)/shard_map/ppermute | solution.py:20
  116.3 8.8 %collective-permute-start.8 = (f32[256,256]{1,0:T(8,128)S(1)}, f32[256,256]{1,0:T(8,128)S(1)}, u32[]{:S(2)}, u32[]{:S(2)}) collective-permute-start(f32[256,256]{1,0:T(8,128)S(1)} %copy.98), channel_id=1, source_target_pairs={{56,0},{60,4},{0,8},{4,12},{8,16},{12,20},{16,24},{20,28},{24,32},... | collective-permute-start | bytes 786440 | tf_op jit(solution)/shard_map/ppermute | solution.py:20
  125.2 8.9 %collective-permute-start.10 = (f32[256,256]{1,0:T(8,128)S(1)}, f32[256,256]{1,0:T(8,128)S(1)}, u32[]{:S(2)}, u32[]{:S(2)}) collective-permute-start(f32[256,256]{1,0:T(8,128)S(1)} %get-tuple-element.608), channel_id=1, source_target_pairs={{0,12},{4,56},{8,20},{12,0},{16,28},{20,8},{24,36},{28,16},{32,44}... | collective-permute-start | bytes 786440 | tf_op jit(solution)/shard_map/ppermute | solution.py:31
  125.3 8.8 %collective-permute-start.9 = (f32[256,256]{1,0:T(8,128)S(1)}, f32[256,256]{1,0:T(8,128)S(1)}, u32[]{:S(2)}, u32[]{:S(2)}) collective-permute-start(f32[256,256]{1,0:T(8,128)S(1)} %get-tuple-element.609), channel_id=1, source_target_pairs={{0,56},{4,12},{8,0},{12,20},{16,8},{20,28},{24,16},{28,36},{32,24}... | collective-permute-start | bytes 786440 | tf_op jit(solution)/shard_map/ppermute | solution.py:31

commit v15 on v14

--- a/solution.py
+++ b/solution.py
@@ -45,13 +45,17 @@
         ],
         axis=1,
     )
+    if not with_diagonal:
+        query_blocks = query_start // BLK + jnp.arange(row_count, dtype=jnp.int32)
+        key_blocks = key_pos[::BLK] // BLK
+        block_live = (key_blocks[None, :] < query_blocks[:, None]) & (block_table == 1)
+        block_live = lax.optimization_barrier(block_live)
+        return jnp.repeat(jnp.repeat(block_live, BLK, axis=0), BLK, axis=1)
     block_table = jnp.repeat(jnp.repeat(block_table, BLK, axis=0), BLK, axis=1)
     query_pos = query_start + jnp.arange(tok_rows, dtype=jnp.int32)
     query_block = (query_pos // BLK)[:, None]
     key_block = (key_pos // BLK)[None, :]
     earlier = (key_block < query_block) & (block_table == 1)
-    if not with_diagonal:
-        return earlier
     diagonal = (key_block == query_block) & (key_pos[None, :] <= query_pos[:, None])
     return earlier | diagonal
 
@@ -104,9 +108,9 @@
         behind_owner = (z_pos - turn) % z_count
         key_starts = (ahead_owner * super_rows, behind_owner * super_rows + tok_rows)
         key_pos = jnp.concatenate([key_starts[0] + offsets, key_starts[1] + offsets])
-        live_mask = lax.optimization_barrier(
-            live_region(block_mask, query_start, tok_rows, key_pos, key_starts, with_diagonal)
-        )
+        live_mask = live_region(block_mask, query_start, tok_rows, key_pos, key_starts, with_diagonal)
+        if with_diagonal:
+            live_mask = lax.optimization_barrier(live_mask)
         key_values = jnp.concatenate([ahead_kv, behind_kv], axis=0)
         query_term, key_term, value_term = contract(
             queries,

time: 136 us -> 134 us (0.985)
  waiting for transfers between devices: 13 us -> 9.49 us
  starting transfers between devices: 49.9 us -> 51.6 us
    ppermute x28, waiting for transfers between devices: 7.07 us -> 4.66 us  [along_z(): return lax.ppermute(value, 'ctx', pairs)]
    unnamed x20 -> x16, local copies, waits for them, and re-layouts: 3.89 us -> 3.84 us
  transfers between devices with their start and end apart: 32 -> 32, of which waited for: 3 -> 3; matrix products, arithmetic and copies ran while one was open for 44% -> 46% of each run, Pallas kernels for 0% -> 0%
where the time goes in v15:
time: 134 us; the launch traced here: 133 us
  starting transfers between devices  51.6 us (39%)
  matrix products  43.6 us (33%)
  local copies, waits for them, and re-layouts  18 us (13%)
  waiting for transfers between devices  9.49 us (7%)
  other arithmetic  8.57 us (6%)
    ppermute x28, starting transfers between devices, along_z(): return lax.ppermute(value, 'ctx', pairs)  42 us
    dot_general x8, matrix products, contract(): jnp.einsum('igd,jd->gij', out_grads, values_part, preferred_element_type=...  12.5 us
    dot_general x8, matrix products, contract(): jnp.einsum('gij,igd->jd', probabilities.astype(jnp.bfloat16), out_grads,...  10.3 us
    dot_general x8, matrix products, contract(): jnp.einsum('gij,igd->jd', dscore, queries, preferred_element_type=jnp.flo...  7.89 us
    dot_general x8, matrix products, contract(): jnp.einsum('igd,jd->gij', queries, keys_part, preferred_element_type=jnp....  7.48 us
    dynamic_slice x7, local copies, waits for them, and re-layouts, live_region(): lax.dynamic_slice(block_mask, (query_start // BLK, start // BLK), (row_co...  6.09 us
    add x6, other arithmetic, visit_turn(): behind_received + behind_term  5.44 us
    dot_general x8, matrix products, contract(): jnp.einsum('gij,jd->igd', dscore, keys_part, preferred_element_type=jnp.f...  5.42 us
  transfers between devices with their start and end apart: 32, of which 3 were waited for; matrix products, arithmetic and copies ran while one was open for 46% of the time, Pallas kernels for 0%

profile of v15, /device:TPU:4, one launch (start us, length us, event | category | flops | bytes accessed | tf_op | source)
XLA Modules:
  0.0 133.3 jit_solution(15659879043160222506)
XLA Ops:
  0.6 0.9 constant_dynamic-update-slice_fusion.3
  1.6 0.9 constant_dynamic-update-slice_fusion.2
  2.4 3.3 %collective-permute-start.4 = (bf16[256,256]{1,0:T(8,128)(2,1)S(1)}, bf16[256,256]{1,0:T(8,128)(2,1)S(1)}, u32[]{:S(2)}, u32[]{:S(2)}) collective-permute-start(bf16[256,256]{1,0:T(8,128)(2,1)S(1)} %constant_dynamic-update-slice_fusion.2), channel_id=1, source_target_pairs={{0,4},{4,0},{8,12},{12,8},{16,20},{20,16},{24,28},{28,24},{32,36},... | collective-permute-start | bytes 393224 | tf_op jit(solution)/shard_map/ppermute | solution.py:36
  5.7 1.9 %copy.130 = bf16[8,4,8,1024]{3,2,0,1:T(8,128)(2,1)} copy(bf16[8,4,8,1024]{3,2,1,0:T(8,128)(2,1)} %bitcast.192) | data formatting | bytes 1048576 | tf_op jit(solution)/shard_map/reshape | solution.py:93
  7.6 3.5 %all-to-all-start = ((bf16[64,4,1024]{2,0,1:T(8,128)(2,1)}), bf16[64,4,1024]{2,0,1:T(8,128)(2,1)S(1)}, u32[]{:S(2)}, u32[]{:S(2)}) async-start(bf16[64,4,1024]{2,0,1:T(8,128)(2,1)} %bitcast.145), calls=%async_computation | async-start | bytes 1048576 | tf_op jit(solution)/shard_map/all_to_all | solution.py:94
  11.4 0.9 fusion.69
  12.8 1.2 copy.74
  14.7 5.9 %collective-permute-start.5 = (bf16[256,256]{1,0:T(8,128)(2,1)S(1)}, bf16[256,256]{1,0:T(8,128)(2,1)S(1)}, u32[]{:S(2)}, u32[]{:S(2)}) collective-permute-start(bf16[256,256]{1,0:T(8,128)(2,1)S(1)} %get-tuple-element.612), channel_id=1, source_target_pairs={{8,0},{12,4},{16,8},{20,12},{24,16},{28,20},{32,24},{36,28},{40,32... | collective-permute-start | bytes 393224 | tf_op jit(solution)/shard_map/ppermute | solution.py:20
  20.6 2.6 %fusion.56 = f32[512,256,8]{1,0,2:T(8,128)} fusion(bf16[256,8,128]{0,2,1:T(8,128)(2,1)S(1)} %bitcast.180, bf16[256,256]{1,0:T(8,128)(2,1)S(1)} %get-tuple-element.612, bf16[256,256]{1,0:T(8,128)(2,1)S(1)} %get-tuple-element.611), kind=kOutput, calls=%fused_computation.95 | convolution fusion | flops 268697600 | bytes 4980736 | tf_op jit(solution)/shard_map/igd,jd->gij/dot_general | solution.py:66
  24.1 3.4 %fusion.36 = f32[512,128]{0,1:T(8,128)S(1)} fusion(bf16[256,8,128]{0,2,1:T(8,128)(2,1)S(1)} %copy.85, f32[512,256,8]{1,0,2:T(8,128)} %fusion.56, f32[8,256]{1,0:T(8,128)S(1)} %copy-done.5, pred[256,512]{0,1:T(8,128)(4,1)S(1)} %fusion.42), kind=kOutput, calls=%fused_computation.57 | convolution fusion | flops 272629760 | bytes 5120000 | tf_op jit(solution)/shard_map/gij,igd->jd/dot_general | solution.py:76
  27.6 1.4 %fusion.25 = bf16[8,256,512]{1,2,0:T(8,128)(2,1)S(1)} fusion(f32[512,256,8]{1,0,2:T(8,128)S(1)} %copy-done, f32[8,256]{1,0:T(8,128)S(1)} %copy.80, f32[8,256]{1,0:T(8,128)S(1)} %copy-done.5, pred[256,512]{0,1:T(8,128)(4,1)S(1)} %fusion.42, bf16[256,8,128]{2,1,0:T(8,128)(2,1)S(1)} %bitcast.185, bf16[256,256]{1,0:T(8,128)(2,1)S(1)} %get-tuple-element.611, ...), kind=kOutput, calls=%fused_computation.45 | convolution fusion | flops 274989056 | bytes 7225344 | tf_op jit(solution)/shard_map/igd,jd->gij/dot_general | solution.py:70
  29.5 0.8 convolution_bitcast_fusion.5
  30.3 0.8 pad_maximum_fusion.2
  31.2 73.0 %while.26 = (s32[]{:T(128)}, bf16[256,256]{1,0:T(8,128)(2,1)S(1)}, bf16[256,256]{1,0:T(8,128)(2,1)S(1)}, f32[256,8,128]{0,2,1:T(8,128)S(1)}, f32[256,256]{0,1:T(...) while((s32[]{:T(128)}, bf16[256,256]{1,0:T(8,128)(2,1)S(1)}, ...), condition=%wide.region_2.3_spmd.clone.clone, body=%wide.region_1.2_spmd.clone.clone.sunk | while | flops 1353188480 | bytes 32277752 | solution.py:150
  31.4 3.3 %collective-permute-start.3 = (f32[256,256]{0,1:T(8,128)}, f32[256,256]{0,1:T(8,128)S(1)}, u32[]{:S(2)}, u32[]{:S(2)}) collective-permute-start(f32[256,256]{0,1:T(8,128)} %get-tuple-element.749), channel_id=1, source_target_pairs={{8,0},{12,4},{16,8},{20,12},{24,16},{28,20},{32,24},{36,28},{40,32... | collective-permute-start | bytes 786440 | tf_op jit(solution)/shard_map/while/body/eval_jaxpr/ppermute | solution.py:20
  34.7 2.0 %collective-permute-start = (bf16[256,256]{1,0:T(8,128)(2,1)S(1)}, bf16[256,256]{1,0:T(8,128)(2,1)S(1)}, u32[]{:S(2)}, u32[]{:S(2)}) collective-permute-start(bf16[256,256]{1,0:T(8,128)(2,1)S(1)} %copy.140), channel_id=1, source_target_pairs={{8,0},{12,4},{16,8},{20,12},{24,16},{28,20},{32,24},{36,28},{40,32... | collective-permute-start | bytes 393224 | tf_op jit(solution)/shard_map/while/body/eval_jaxpr/ppermute | solution.py:20
  37.1 0.9 fusion.107
  38.9 1.0 fusion.110
  39.9 1.4 %fusion.108 = bf16[8,256,512]{1,2,0:T(8,128)(2,1)S(1)} fusion(f32[512,256,8]{1,0,2:T(8,128)S(1)} %fusion.106, bf16[256,8,128]{0,2,1:T(8,128)(2,1)S(1)} %copy-done.3, f32[8,256]{1,0:T(8,128)S(1)} %get-tuple-element.781, f32[8,256]{1,0:T(8,128)S(1)} %get-tuple-element.779, pred[256,512]{0,1:T(8,128)(4,1)S(1)} %bitcast.188, ...), kind=kOutput, calls=%fused_computation.3.clone.1 | convolution fusion | flops 274726912 | bytes 7094272 | tf_op jit(solution)/shard_map/while/body/eval_jaxpr/igd,jd->gij/dot_general | solution.py:70
  41.8 0.8 convolution_bitcast_fusion.7
  42.6 0.9 fusion.111
  43.8 3.2 %collective-permute-start.3 = (f32[256,256]{0,1:T(8,128)}, f32[256,256]{0,1:T(8,128)S(1)}, u32[]{:S(2)}, u32[]{:S(2)}) collective-permute-start(f32[256,256]{0,1:T(8,128)} %get-tuple-element.749), channel_id=1, source_target_pairs={{8,0},{12,4},{16,8},{20,12},{24,16},{28,20},{32,24},{36,28},{40,32... | collective-permute-start | bytes 786440 | tf_op jit(solution)/shard_map/while/body/eval_jaxpr/ppermute | solution.py:20
  47.0 1.9 %collective-permute-start = (bf16[256,256]{1,0:T(8,128)(2,1)S(1)}, bf16[256,256]{1,0:T(8,128)(2,1)S(1)}, u32[]{:S(2)}, u32[]{:S(2)}) collective-permute-start(bf16[256,256]{1,0:T(8,128)(2,1)S(1)} %copy.140), channel_id=1, source_target_pairs={{8,0},{12,4},{16,8},{20,12},{24,16},{28,20},{32,24},{36,28},{40,32... | collective-permute-start | bytes 393224 | tf_op jit(solution)/shard_map/while/body/eval_jaxpr/ppermute | solution.py:20
  49.4 0.9 fusion.107
  51.2 1.0 fusion.110
  52.2 1.4 %fusion.108 = bf16[8,256,512]{1,2,0:T(8,128)(2,1)S(1)} fusion(f32[512,256,8]{1,0,2:T(8,128)S(1)} %fusion.106, bf16[256,8,128]{0,2,1:T(8,128)(2,1)S(1)} %copy-done.3, f32[8,256]{1,0:T(8,128)S(1)} %get-tuple-element.781, f32[8,256]{1,0:T(8,128)S(1)} %get-tuple-element.779, pred[256,512]{0,1:T(8,128)(4,1)S(1)} %bitcast.188, ...), kind=kOutput, calls=%fused_computation.3.clone.1 | convolution fusion | flops 274726912 | bytes 7094272 | tf_op jit(solution)/shard_map/while/body/eval_jaxpr/igd,jd->gij/dot_general | solution.py:70
  54.9 0.9 fusion.111
  56.3 2.8 %collective-permute-start.3 = (f32[256,256]{0,1:T(8,128)}, f32[256,256]{0,1:T(8,128)S(1)}, u32[]{:S(2)}, u32[]{:S(2)}) collective-permute-start(f32[256,256]{0,1:T(8,128)} %get-tuple-element.749), channel_id=1, source_target_pairs={{8,0},{12,4},{16,8},{20,12},{24,16},{28,20},{32,24},{36,28},{40,32... | collective-permute-start | bytes 786440 | tf_op jit(solution)/shard_map/while/body/eval_jaxpr/ppermute | solution.py:20
  59.1 1.9 %collective-permute-start = (bf16[256,256]{1,0:T(8,128)(2,1)S(1)}, bf16[256,256]{1,0:T(8,128)(2,1)S(1)}, u32[]{:S(2)}, u32[]{:S(2)}) collective-permute-start(bf16[256,256]{1,0:T(8,128)(2,1)S(1)} %copy.140), channel_id=1, source_target_pairs={{8,0},{12,4},{16,8},{20,12},{24,16},{28,20},{32,24},{36,28},{40,32... | collective-permute-start | bytes 393224 | tf_op jit(solution)/shard_map/while/body/eval_jaxpr/ppermute | solution.py:20
  61.5 0.9 fusion.107
  63.3 1.0 fusion.110
  64.3 1.4 %fusion.108 = bf16[8,256,512]{1,2,0:T(8,128)(2,1)S(1)} fusion(f32[512,256,8]{1,0,2:T(8,128)S(1)} %fusion.106, bf16[256,8,128]{0,2,1:T(8,128)(2,1)S(1)} %copy-done.3, f32[8,256]{1,0:T(8,128)S(1)} %get-tuple-element.781, f32[8,256]{1,0:T(8,128)S(1)} %get-tuple-element.779, pred[256,512]{0,1:T(8,128)(4,1)S(1)} %bitcast.188, ...), kind=kOutput, calls=%fused_computation.3.clone.1 | convolution fusion | flops 274726912 | bytes 7094272 | tf_op jit(solution)/shard_map/while/body/eval_jaxpr/igd,jd->gij/dot_general | solution.py:70
  67.0 0.9 fusion.111
  68.0 3.1 %collective-permute-start.3 = (f32[256,256]{0,1:T(8,128)}, f32[256,256]{0,1:T(8,128)S(1)}, u32[]{:S(2)}, u32[]{:S(2)}) collective-permute-start(f32[256,256]{0,1:T(8,128)} %get-tuple-element.749), channel_id=1, source_target_pairs={{8,0},{12,4},{16,8},{20,12},{24,16},{28,20},{32,24},{36,28},{40,32... | collective-permute-start | bytes 786440 | tf_op jit(solution)/shard_map/while/body/eval_jaxpr/ppermute | solution.py:20
  71.2 1.9 %collective-permute-start = (bf16[256,256]{1,0:T(8,128)(2,1)S(1)}, bf16[256,256]{1,0:T(8,128)(2,1)S(1)}, u32[]{:S(2)}, u32[]{:S(2)}) collective-permute-start(bf16[256,256]{1,0:T(8,128)(2,1)S(1)} %copy.140), channel_id=1, source_target_pairs={{8,0},{12,4},{16,8},{20,12},{24,16},{28,20},{32,24},{36,28},{40,32... | collective-permute-start | bytes 393224 | tf_op jit(solution)/shard_map/while/body/eval_jaxpr/ppermute | solution.py:20
  73.5 0.9 fusion.107
  75.3 1.0 fusion.110
  76.4 1.4 %fusion.108 = bf16[8,256,512]{1,2,0:T(8,128)(2,1)S(1)} fusion(f32[512,256,8]{1,0,2:T(8,128)S(1)} %fusion.106, bf16[256,8,128]{0,2,1:T(8,128)(2,1)S(1)} %copy-done.3, f32[8,256]{1,0:T(8,128)S(1)} %get-tuple-element.781, f32[8,256]{1,0:T(8,128)S(1)} %get-tuple-element.779, pred[256,512]{0,1:T(8,128)(4,1)S(1)} %bitcast.188, ...), kind=kOutput, calls=%fused_computation.3.clone.1 | convolution fusion | flops 274726912 | bytes 7094272 | tf_op jit(solution)/shard_map/while/body/eval_jaxpr/igd,jd->gij/dot_general | solution.py:70
  78.2 0.8 convolution_bitcast_fusion.7
  79.1 0.9 fusion.111
  80.1 3.1 %collective-permute-start.3 = (f32[256,256]{0,1:T(8,128)}, f32[256,256]{0,1:T(8,128)S(1)}, u32[]{:S(2)}, u32[]{:S(2)}) collective-permute-start(f32[256,256]{0,1:T(8,128)} %get-tuple-element.749), channel_id=1, source_target_pairs={{8,0},{12,4},{16,8},{20,12},{24,16},{28,20},{32,24},{36,28},{40,32... | collective-permute-start | bytes 786440 | tf_op jit(solution)/shard_map/while/body/eval_jaxpr/ppermute | solution.py:20
  83.3 1.9 %collective-permute-start = (bf16[256,256]{1,0:T(8,128)(2,1)S(1)}, bf16[256,256]{1,0:T(8,128)(2,1)S(1)}, u32[]{:S(2)}, u32[]{:S(2)}) collective-permute-start(bf16[256,256]{1,0:T(8,128)(2,1)S(1)} %copy.140), channel_id=1, source_target_pairs={{8,0},{12,4},{16,8},{20,12},{24,16},{28,20},{32,24},{36,28},{40,32... | collective-permute-start | bytes 393224 | tf_op jit(solution)/shard_map/while/body/eval_jaxpr/ppermute | solution.py:20
  85.6 0.9 fusion.107
  87.4 1.0 fusion.110
  88.4 1.4 %fusion.108 = bf16[8,256,512]{1,2,0:T(8,128)(2,1)S(1)} fusion(f32[512,256,8]{1,0,2:T(8,128)S(1)} %fusion.106, bf16[256,8,128]{0,2,1:T(8,128)(2,1)S(1)} %copy-done.3, f32[8,256]{1,0:T(8,128)S(1)} %get-tuple-element.781, f32[8,256]{1,0:T(8,128)S(1)} %get-tuple-element.779, pred[256,512]{0,1:T(8,128)(4,1)S(1)} %bitcast.188, ...), kind=kOutput, calls=%fused_computation.3.clone.1 | convolution fusion | flops 274726912 | bytes 7094272 | tf_op jit(solution)/shard_map/while/body/eval_jaxpr/igd,jd->gij/dot_general | solution.py:70
  90.3 0.8 convolution_bitcast_fusion.7
  91.2 0.9 fusion.111
  92.2 3.1 %collective-permute-start.3 = (f32[256,256]{0,1:T(8,128)}, f32[256,256]{0,1:T(8,128)S(1)}, u32[]{:S(2)}, u32[]{:S(2)}) collective-permute-start(f32[256,256]{0,1:T(8,128)} %get-tuple-element.749), channel_id=1, source_target_pairs={{8,0},{12,4},{16,8},{20,12},{24,16},{28,20},{32,24},{36,28},{40,32... | collective-permute-start | bytes 786440 | tf_op jit(solution)/shard_map/while/body/eval_jaxpr/ppermute | solution.py:20
  95.3 1.8 %collective-permute-start = (bf16[256,256]{1,0:T(8,128)(2,1)S(1)}, bf16[256,256]{1,0:T(8,128)(2,1)S(1)}, u32[]{:S(2)}, u32[]{:S(2)}) collective-permute-start(bf16[256,256]{1,0:T(8,128)(2,1)S(1)} %copy.140), channel_id=1, source_target_pairs={{8,0},{12,4},{16,8},{20,12},{24,16},{28,20},{32,24},{36,28},{40,32... | collective-permute-start | bytes 393224 | tf_op jit(solution)/shard_map/while/body/eval_jaxpr/ppermute | solution.py:20
  97.7 0.9 fusion.107
  99.5 1.0 fusion.110
  100.5 1.4 %fusion.108 = bf16[8,256,512]{1,2,0:T(8,128)(2,1)S(1)} fusion(f32[512,256,8]{1,0,2:T(8,128)S(1)} %fusion.106, bf16[256,8,128]{0,2,1:T(8,128)(2,1)S(1)} %copy-done.3, f32[8,256]{1,0:T(8,128)S(1)} %get-tuple-element.781, f32[8,256]{1,0:T(8,128)S(1)} %get-tuple-element.779, pred[256,512]{0,1:T(8,128)(4,1)S(1)} %bitcast.188, ...), kind=kOutput, calls=%fused_computation.3.clone.1 | convolution fusion | flops 274726912 | bytes 7094272 | tf_op jit(solution)/shard_map/while/body/eval_jaxpr/igd,jd->gij/dot_general | solution.py:70
  103.2 0.9 fusion.111
  105.2 0.9 fusion.39
  106.0 2.8 %fusion.21 = bf16[8,256,512]{1,2,0:T(8,128)(2,1)} fusion(f32[512,256,8]{1,0,2:T(8,128)S(1)} %fusion.55, f32[8,256]{1,0:T(8,128)S(1)} %get-tuple-element.814, f32[8,256]{1,0:T(8,128)S(1)} %get-tuple-element.815, pred[256,512]{0,1:T(8,128)(4,1)S(1)} %bitcast.195, bf16[256,8,128]{2,1,0:T(8,128)(2,1)S(1)} %bitcast.186, ...), kind=kOutput, calls=%fused_computation.39 | convolution fusion | flops 274726912 | bytes 7094272 | tf_op jit(solution)/shard_map/igd,jd->gij/dot_general | solution.py:70
  108.8 1.1 copy.92
  109.9 3.0 %collective-permute-start.7 = (f32[256,256]{1,0:T(8,128)S(1)}, f32[256,256]{1,0:T(8,128)S(1)}, u32[]{:S(2)}, u32[]{:S(2)}) collective-permute-start(f32[256,256]{1,0:T(8,128)S(1)} %copy.92), channel_id=1, source_target_pairs={{8,0},{12,4},{16,8},{20,12},{24,16},{28,20},{32,24},{36,28},{40,32... | collective-permute-start | bytes 786440 | tf_op jit(solution)/shard_map/ppermute | solution.py:20
  112.9 1.1 copy.98
  114.3 2.1 %convolution_bitcast_fusion.2 = f32[256,8,128]{0,2,1:T(8,128)S(1)} fusion(bf16[8,256,512]{1,2,0:T(8,128)(2,1)} %fusion.21, bf16[512,256]{1,0:T(8,128)(2,1)S(1)} %constant_dynamic-update-slice_fusion.4), kind=kOutput, calls=%fused_computation.55 | convolution fusion | flops 268435456 | bytes 3276800 | tf_op jit(solution)/shard_map/gij,jd->igd/dot_general | solution.py:74
  116.4 2.3 %convolution_bitcast_fusion.4 = f32[512,128]{1,0:T(8,128)S(1)} fusion(bf16[8,256,512]{1,2,0:T(8,128)(2,1)} %fusion.21, bf16[256,8,128]{0,2,1:T(8,128)(2,1)S(1)} %get-tuple-element.791), kind=kOutput, calls=%fused_computation.59 | convolution fusion | flops 268435456 | bytes 2883584 | tf_op jit(solution)/shard_map/gij,igd->jd/dot_general | solution.py:75
  118.7 4.3 %collective-permute-done.8 = f32[256,256]{1,0:T(8,128)S(1)} collective-permute-done((f32[256,256]{1,0:T(8,128)S(1)}, f32[256,256]{1,0:T(8,128)S(1)}, u32[]{:S(2)}, u32[]{:S(2)}) %collective-permute-start.8) | collective-permute-done | bytes 262176 | tf_op jit(solution)/shard_map/ppermute | solution.py:20
  123.2 2.8 %collective-permute-start.9 = (f32[256,256]{1,0:T(8,128)S(1)}, f32[256,256]{1,0:T(8,128)S(1)}, u32[]{:S(2)}, u32[]{:S(2)}) collective-permute-start(f32[256,256]{1,0:T(8,128)S(1)} %get-tuple-element.608), channel_id=1, source_target_pairs={{0,56},{4,12},{8,0},{12,20},{16,8},{20,28},{24,16},{28,36},{32,24}... | collective-permute-start | bytes 786440 | tf_op jit(solution)/shard_map/ppermute | solution.py:31
  126.1 1.0 copy.99
  127.1 4.8 %collective-permute-done.10 = f32[256,256]{1,0:T(8,128)S(1)} collective-permute-done((f32[256,256]{1,0:T(8,128)S(1)}, f32[256,256]{1,0:T(8,128)S(1)}, u32[]{:S(2)}, u32[]{:S(2)}) %collective-permute-start.10) | collective-permute-done | bytes 262176 | tf_op jit(solution)/shard_map/ppermute | solution.py:31
  (184 shorter events, 20.0 us)
Async XLA Ops:
  0.6 13.4 %copy-start.1 = (bf16[256,1024]{1,0:T(8,128)(2,1)S(1)}, bf16[256,1024]{1,0:T(8,128)(2,1)}, u32[]{:S(2)}) copy-start(bf16[256,1024]{1,0:T(8,128)(2,1)} %param.12) | copy-start | bytes 1572868
  2.4 12.3 %collective-permute-start.4 = (bf16[256,256]{1,0:T(8,128)(2,1)S(1)}, bf16[256,256]{1,0:T(8,128)(2,1)S(1)}, u32[]{:S(2)}, u32[]{:S(2)}) collective-permute-start(bf16[256,256]{1,0:T(8,128)(2,1)S(1)} %constant_dynamic-update-slice_fusion.2), channel_id=1, source_target_pairs={{0,4},{4,0},{8,12},{12,8},{16,20},{20,16},{24,28},{28,24},{32,36},... | collective-permute-start | bytes 393224 | tf_op jit(solution)/shard_map/ppermute | solution.py:36
  7.6 15.7 %all-to-all-start = ((bf16[64,4,1024]{2,0,1:T(8,128)(2,1)}), bf16[64,4,1024]{2,0,1:T(8,128)(2,1)S(1)}, u32[]{:S(2)}, u32[]{:S(2)}) async-start(bf16[64,4,1024]{2,0,1:T(8,128)(2,1)} %bitcast.145), calls=%async_computation | async-start | bytes 1048576 | tf_op jit(solution)/shard_map/all_to_all | solution.py:94
  14.7 16.5 %collective-permute-start.5 = (bf16[256,256]{1,0:T(8,128)(2,1)S(1)}, bf16[256,256]{1,0:T(8,128)(2,1)S(1)}, u32[]{:S(2)}, u32[]{:S(2)}) collective-permute-start(bf16[256,256]{1,0:T(8,128)(2,1)S(1)} %get-tuple-element.612), channel_id=1, source_target_pairs={{8,0},{12,4},{16,8},{20,12},{24,16},{28,20},{32,24},{36,28},{40,32... | collective-permute-start | bytes 393224 | tf_op jit(solution)/shard_map/ppermute | solution.py:20
  20.6 10.5 %collective-permute-start.6 = (bf16[256,256]{1,0:T(8,128)(2,1)S(1)}, bf16[256,256]{1,0:T(8,128)(2,1)S(1)}, u32[]{:S(2)}, u32[]{:S(2)}) collective-permute-start(bf16[256,256]{1,0:T(8,128)(2,1)S(1)} %get-tuple-element.611), channel_id=1, source_target_pairs={{56,0},{60,4},{0,8},{4,12},{8,16},{12,20},{16,24},{20,28},{24,32},... | collective-permute-start | bytes 393224 | tf_op jit(solution)/shard_map/ppermute | solution.py:20
  20.6 3.5 %copy-start.5 = (f32[8,256]{1,0:T(8,128)S(1)}, f32[8,256]{1,0:T(8,128)}, u32[]{:S(2)}) copy-start(f32[8,256]{1,0:T(8,128)} %param.14) | copy-start | bytes 24580
  23.7 5.3 %copy-start.2 = (bf16[256,8,128]{0,2,1:T(8,128)(2,1)}, bf16[256,8,128]{0,2,1:T(8,128)(2,1)S(1)}, u32[]{:S(2)}) copy-start(bf16[256,8,128]{0,2,1:T(8,128)(2,1)S(1)} %copy.85) | copy-start | bytes 1572868
  24.1 3.5 %copy-start = (f32[512,256,8]{1,0,2:T(8,128)S(1)}, f32[512,256,8]{1,0,2:T(8,128)}, u32[]{:S(2)}) copy-start(f32[512,256,8]{1,0,2:T(8,128)} %fusion.56) | copy-start | bytes 12582916
  31.3 11.3 %collective-permute-start.2 = (f32[256,256]{0,1:T(8,128)}, f32[256,256]{0,1:T(8,128)S(1)}, u32[]{:S(2)}, u32[]{:S(2)}) collective-permute-start(f32[256,256]{0,1:T(8,128)} %get-tuple-element.750), channel_id=1, source_target_pairs={{56,0},{60,4},{0,8},{4,12},{8,16},{12,20},{16,24},{20,28},{24,32},... | collective-permute-start | bytes 786440 | tf_op jit(solution)/shard_map/while/body/eval_jaxpr/ppermute | solution.py:20
  31.4 11.2 %collective-permute-start.3 = (f32[256,256]{0,1:T(8,128)}, f32[256,256]{0,1:T(8,128)S(1)}, u32[]{:S(2)}, u32[]{:S(2)}) collective-permute-start(f32[256,256]{0,1:T(8,128)} %get-tuple-element.749), channel_id=1, source_target_pairs={{8,0},{12,4},{16,8},{20,12},{24,16},{28,20},{32,24},{36,28},{40,32... | collective-permute-start | bytes 786440 | tf_op jit(solution)/shard_map/while/body/eval_jaxpr/ppermute | solution.py:20
  34.7 8.8 %collective-permute-start = (bf16[256,256]{1,0:T(8,128)(2,1)S(1)}, bf16[256,256]{1,0:T(8,128)(2,1)S(1)}, u32[]{:S(2)}, u32[]{:S(2)}) collective-permute-start(bf16[256,256]{1,0:T(8,128)(2,1)S(1)} %copy.140), channel_id=1, source_target_pairs={{8,0},{12,4},{16,8},{20,12},{24,16},{28,20},{32,24},{36,28},{40,32... | collective-permute-start | bytes 393224 | tf_op jit(solution)/shard_map/while/body/eval_jaxpr/ppermute | solution.py:20
  36.7 7.1 %collective-permute-start.1 = (bf16[256,256]{1,0:T(8,128)(2,1)S(1)}, bf16[256,256]{1,0:T(8,128)(2,1)S(1)}, u32[]{:S(2)}, u32[]{:S(2)}) collective-permute-start(bf16[256,256]{1,0:T(8,128)(2,1)S(1)} %copy.141), channel_id=1, source_target_pairs={{56,0},{60,4},{0,8},{4,12},{8,16},{12,20},{16,24},{20,28},{24,32},... | collective-permute-start | bytes 393224 | tf_op jit(solution)/shard_map/while/body/eval_jaxpr/ppermute | solution.py:20
  37.1 1.8 %copy-start.3 = (bf16[256,8,128]{0,2,1:T(8,128)(2,1)S(1)}, bf16[256,8,128]{0,2,1:T(8,128)(2,1)}, u32[]{:S(2)}) copy-start(bf16[256,8,128]{0,2,1:T(8,128)(2,1)} %get-tuple-element.780) | copy-start | bytes 1572868 | tf_op jit(solution)/shard_map/while
  43.8 11.1 %collective-permute-start.2 = (f32[256,256]{0,1:T(8,128)}, f32[256,256]{0,1:T(8,128)S(1)}, u32[]{:S(2)}, u32[]{:S(2)}) collective-permute-start(f32[256,256]{0,1:T(8,128)} %get-tuple-element.750), channel_id=1, source_target_pairs={{56,0},{60,4},{0,8},{4,12},{8,16},{12,20},{16,24},{20,28},{24,32},... | collective-permute-start | bytes 786440 | tf_op jit(solution)/shard_map/while/body/eval_jaxpr/ppermute | solution.py:20
  43.8 11.1 %collective-permute-start.3 = (f32[256,256]{0,1:T(8,128)}, f32[256,256]{0,1:T(8,128)S(1)}, u32[]{:S(2)}, u32[]{:S(2)}) collective-permute-start(f32[256,256]{0,1:T(8,128)} %get-tuple-element.749), channel_id=1, source_target_pairs={{8,0},{12,4},{16,8},{20,12},{24,16},{28,20},{32,24},{36,28},{40,32... | collective-permute-start | bytes 786440 | tf_op jit(solution)/shard_map/while/body/eval_jaxpr/ppermute | solution.py:20
  47.0 8.8 %collective-permute-start = (bf16[256,256]{1,0:T(8,128)(2,1)S(1)}, bf16[256,256]{1,0:T(8,128)(2,1)S(1)}, u32[]{:S(2)}, u32[]{:S(2)}) collective-permute-start(bf16[256,256]{1,0:T(8,128)(2,1)S(1)} %copy.140), channel_id=1, source_target_pairs={{8,0},{12,4},{16,8},{20,12},{24,16},{28,20},{32,24},{36,28},{40,32... | collective-permute-start | bytes 393224 | tf_op jit(solution)/shard_map/while/body/eval_jaxpr/ppermute | solution.py:20
  49.0 6.9 %collective-permute-start.1 = (bf16[256,256]{1,0:T(8,128)(2,1)S(1)}, bf16[256,256]{1,0:T(8,128)(2,1)S(1)}, u32[]{:S(2)}, u32[]{:S(2)}) collective-permute-start(bf16[256,256]{1,0:T(8,128)(2,1)S(1)} %copy.141), channel_id=1, source_target_pairs={{56,0},{60,4},{0,8},{4,12},{8,16},{12,20},{16,24},{20,28},{24,32},... | collective-permute-start | bytes 393224 | tf_op jit(solution)/shard_map/while/body/eval_jaxpr/ppermute | solution.py:20
  49.4 1.8 %copy-start.3 = (bf16[256,8,128]{0,2,1:T(8,128)(2,1)S(1)}, bf16[256,8,128]{0,2,1:T(8,128)(2,1)}, u32[]{:S(2)}) copy-start(bf16[256,8,128]{0,2,1:T(8,128)(2,1)} %get-tuple-element.780) | copy-start | bytes 1572868 | tf_op jit(solution)/shard_map/while
  55.8 11.1 %collective-permute-start.2 = (f32[256,256]{0,1:T(8,128)}, f32[256,256]{0,1:T(8,128)S(1)}, u32[]{:S(2)}, u32[]{:S(2)}) collective-permute-start(f32[256,256]{0,1:T(8,128)} %get-tuple-element.750), channel_id=1, source_target_pairs={{56,0},{60,4},{0,8},{4,12},{8,16},{12,20},{16,24},{20,28},{24,32},... | collective-permute-start | bytes 786440 | tf_op jit(solution)/shard_map/while/body/eval_jaxpr/ppermute | solution.py:20
  56.3 10.7 %collective-permute-start.3 = (f32[256,256]{0,1:T(8,128)}, f32[256,256]{0,1:T(8,128)S(1)}, u32[]{:S(2)}, u32[]{:S(2)}) collective-permute-start(f32[256,256]{0,1:T(8,128)} %get-tuple-element.749), channel_id=1, source_target_pairs={{8,0},{12,4},{16,8},{20,12},{24,16},{28,20},{32,24},{36,28},{40,32... | collective-permute-start | bytes 786440 | tf_op jit(solution)/shard_map/while/body/eval_jaxpr/ppermute | solution.py:20
  59.1 8.8 %collective-permute-start = (bf16[256,256]{1,0:T(8,128)(2,1)S(1)}, bf16[256,256]{1,0:T(8,128)(2,1)S(1)}, u32[]{:S(2)}, u32[]{:S(2)}) collective-permute-start(bf16[256,256]{1,0:T(8,128)(2,1)S(1)} %copy.140), channel_id=1, source_target_pairs={{8,0},{12,4},{16,8},{20,12},{24,16},{28,20},{32,24},{36,28},{40,32... | collective-permute-start | bytes 393224 | tf_op jit(solution)/shard_map/while/body/eval_jaxpr/ppermute | solution.py:20
  61.0 6.9 %collective-permute-start.1 = (bf16[256,256]{1,0:T(8,128)(2,1)S(1)}, bf16[256,256]{1,0:T(8,128)(2,1)S(1)}, u32[]{:S(2)}, u32[]{:S(2)}) collective-permute-start(bf16[256,256]{1,0:T(8,128)(2,1)S(1)} %copy.141), channel_id=1, source_target_pairs={{56,0},{60,4},{0,8},{4,12},{8,16},{12,20},{16,24},{20,28},{24,32},... | collective-permute-start | bytes 393224 | tf_op jit(solution)/shard_map/while/body/eval_jaxpr/ppermute | solution.py:20
  61.5 1.8 %copy-start.3 = (bf16[256,8,128]{0,2,1:T(8,128)(2,1)S(1)}, bf16[256,8,128]{0,2,1:T(8,128)(2,1)}, u32[]{:S(2)}) copy-start(bf16[256,8,128]{0,2,1:T(8,128)(2,1)} %get-tuple-element.780) | copy-start | bytes 1572868 | tf_op jit(solution)/shard_map/while
  67.9 11.1 %collective-permute-start.2 = (f32[256,256]{0,1:T(8,128)}, f32[256,256]{0,1:T(8,128)S(1)}, u32[]{:S(2)}, u32[]{:S(2)}) collective-permute-start(f32[256,256]{0,1:T(8,128)} %get-tuple-element.750), channel_id=1, source_target_pairs={{56,0},{60,4},{0,8},{4,12},{8,16},{12,20},{16,24},{20,28},{24,32},... | collective-permute-start | bytes 786440 | tf_op jit(solution)/shard_map/while/body/eval_jaxpr/ppermute | solution.py:20
  68.0 11.0 %collective-permute-start.3 = (f32[256,256]{0,1:T(8,128)}, f32[256,256]{0,1:T(8,128)S(1)}, u32[]{:S(2)}, u32[]{:S(2)}) collective-permute-start(f32[256,256]{0,1:T(8,128)} %get-tuple-element.749), channel_id=1, source_target_pairs={{8,0},{12,4},{16,8},{20,12},{24,16},{28,20},{32,24},{36,28},{40,32... | collective-permute-start | bytes 786440 | tf_op jit(solution)/shard_map/while/body/eval_jaxpr/ppermute | solution.py:20
  71.2 8.8 %collective-permute-start = (bf16[256,256]{1,0:T(8,128)(2,1)S(1)}, bf16[256,256]{1,0:T(8,128)(2,1)S(1)}, u32[]{:S(2)}, u32[]{:S(2)}) collective-permute-start(bf16[256,256]{1,0:T(8,128)(2,1)S(1)} %copy.140), channel_id=1, source_target_pairs={{8,0},{12,4},{16,8},{20,12},{24,16},{28,20},{32,24},{36,28},{40,32... | collective-permute-start | bytes 393224 | tf_op jit(solution)/shard_map/while/body/eval_jaxpr/ppermute | solution.py:20
  73.1 6.9 %collective-permute-start.1 = (bf16[256,256]{1,0:T(8,128)(2,1)S(1)}, bf16[256,256]{1,0:T(8,128)(2,1)S(1)}, u32[]{:S(2)}, u32[]{:S(2)}) collective-permute-start(bf16[256,256]{1,0:T(8,128)(2,1)S(1)} %copy.141), channel_id=1, source_target_pairs={{56,0},{60,4},{0,8},{4,12},{8,16},{12,20},{16,24},{20,28},{24,32},... | collective-permute-start | bytes 393224 | tf_op jit(solution)/shard_map/while/body/eval_jaxpr/ppermute | solution.py:20
  73.5 1.8 %copy-start.3 = (bf16[256,8,128]{0,2,1:T(8,128)(2,1)S(1)}, bf16[256,8,128]{0,2,1:T(8,128)(2,1)}, u32[]{:S(2)}) copy-start(bf16[256,8,128]{0,2,1:T(8,128)(2,1)} %get-tuple-element.780) | copy-start | bytes 1572868 | tf_op jit(solution)/shard_map/while
  80.0 11.1 %collective-permute-start.2 = (f32[256,256]{0,1:T(8,128)}, f32[256,256]{0,1:T(8,128)S(1)}, u32[]{:S(2)}, u32[]{:S(2)}) collective-permute-start(f32[256,256]{0,1:T(8,128)} %get-tuple-element.750), channel_id=1, source_target_pairs={{56,0},{60,4},{0,8},{4,12},{8,16},{12,20},{16,24},{20,28},{24,32},... | collective-permute-start | bytes 786440 | tf_op jit(solution)/shard_map/while/body/eval_jaxpr/ppermute | solution.py:20
  80.1 11.0 %collective-permute-start.3 = (f32[256,256]{0,1:T(8,128)}, f32[256,256]{0,1:T(8,128)S(1)}, u32[]{:S(2)}, u32[]{:S(2)}) collective-permute-start(f32[256,256]{0,1:T(8,128)} %get-tuple-element.749), channel_id=1, source_target_pairs={{8,0},{12,4},{16,8},{20,12},{24,16},{28,20},{32,24},{36,28},{40,32... | collective-permute-start | bytes 786440 | tf_op jit(solution)/shard_map/while/body/eval_jaxpr/ppermute | solution.py:20
  83.3 8.8 %collective-permute-start = (bf16[256,256]{1,0:T(8,128)(2,1)S(1)}, bf16[256,256]{1,0:T(8,128)(2,1)S(1)}, u32[]{:S(2)}, u32[]{:S(2)}) collective-permute-start(bf16[256,256]{1,0:T(8,128)(2,1)S(1)} %copy.140), channel_id=1, source_target_pairs={{8,0},{12,4},{16,8},{20,12},{24,16},{28,20},{32,24},{36,28},{40,32... | collective-permute-start | bytes 393224 | tf_op jit(solution)/shard_map/while/body/eval_jaxpr/ppermute | solution.py:20
  85.1 6.9 %collective-permute-start.1 = (bf16[256,256]{1,0:T(8,128)(2,1)S(1)}, bf16[256,256]{1,0:T(8,128)(2,1)S(1)}, u32[]{:S(2)}, u32[]{:S(2)}) collective-permute-start(bf16[256,256]{1,0:T(8,128)(2,1)S(1)} %copy.141), channel_id=1, source_target_pairs={{56,0},{60,4},{0,8},{4,12},{8,16},{12,20},{16,24},{20,28},{24,32},... | collective-permute-start | bytes 393224 | tf_op jit(solution)/shard_map/while/body/eval_jaxpr/ppermute | solution.py:20
  85.6 1.8 %copy-start.3 = (bf16[256,8,128]{0,2,1:T(8,128)(2,1)S(1)}, bf16[256,8,128]{0,2,1:T(8,128)(2,1)}, u32[]{:S(2)}) copy-start(bf16[256,8,128]{0,2,1:T(8,128)(2,1)} %get-tuple-element.780) | copy-start | bytes 1572868 | tf_op jit(solution)/shard_map/while
  92.1 11.1 %collective-permute-start.2 = (f32[256,256]{0,1:T(8,128)}, f32[256,256]{0,1:T(8,128)S(1)}, u32[]{:S(2)}, u32[]{:S(2)}) collective-permute-start(f32[256,256]{0,1:T(8,128)} %get-tuple-element.750), channel_id=1, source_target_pairs={{56,0},{60,4},{0,8},{4,12},{8,16},{12,20},{16,24},{20,28},{24,32},... | collective-permute-start | bytes 786440 | tf_op jit(solution)/shard_map/while/body/eval_jaxpr/ppermute | solution.py:20
  92.2 11.0 %collective-permute-start.3 = (f32[256,256]{0,1:T(8,128)}, f32[256,256]{0,1:T(8,128)S(1)}, u32[]{:S(2)}, u32[]{:S(2)}) collective-permute-start(f32[256,256]{0,1:T(8,128)} %get-tuple-element.749), channel_id=1, source_target_pairs={{8,0},{12,4},{16,8},{20,12},{24,16},{28,20},{32,24},{36,28},{40,32... | collective-permute-start | bytes 786440 | tf_op jit(solution)/shard_map/while/body/eval_jaxpr/ppermute | solution.py:20
  95.3 8.8 %collective-permute-start = (bf16[256,256]{1,0:T(8,128)(2,1)S(1)}, bf16[256,256]{1,0:T(8,128)(2,1)S(1)}, u32[]{:S(2)}, u32[]{:S(2)}) collective-permute-start(bf16[256,256]{1,0:T(8,128)(2,1)S(1)} %copy.140), channel_id=1, source_target_pairs={{8,0},{12,4},{16,8},{20,12},{24,16},{28,20},{32,24},{36,28},{40,32... | collective-permute-start | bytes 393224 | tf_op jit(solution)/shard_map/while/body/eval_jaxpr/ppermute | solution.py:20
  97.2 7.0 %collective-permute-start.1 = (bf16[256,256]{1,0:T(8,128)(2,1)S(1)}, bf16[256,256]{1,0:T(8,128)(2,1)S(1)}, u32[]{:S(2)}, u32[]{:S(2)}) collective-permute-start(bf16[256,256]{1,0:T(8,128)(2,1)S(1)} %copy.141), channel_id=1, source_target_pairs={{56,0},{60,4},{0,8},{4,12},{8,16},{12,20},{16,24},{20,28},{24,32},... | collective-permute-start | bytes 393224 | tf_op jit(solution)/shard_map/while/body/eval_jaxpr/ppermute | solution.py:20
  97.7 1.8 %copy-start.3 = (bf16[256,8,128]{0,2,1:T(8,128)(2,1)S(1)}, bf16[256,8,128]{0,2,1:T(8,128)(2,1)}, u32[]{:S(2)}) copy-start(bf16[256,8,128]{0,2,1:T(8,128)(2,1)} %get-tuple-element.780) | copy-start | bytes 1572868 | tf_op jit(solution)/shard_map/while
  104.1 1.0 copy-start.4
  109.9 8.8 %collective-permute-start.7 = (f32[256,256]{1,0:T(8,128)S(1)}, f32[256,256]{1,0:T(8,128)S(1)}, u32[]{:S(2)}, u32[]{:S(2)}) collective-permute-start(f32[256,256]{1,0:T(8,128)S(1)} %copy.92), channel_id=1, source_target_pairs={{8,0},{12,4},{16,8},{20,12},{24,16},{28,20},{32,24},{36,28},{40,32... | collective-permute-start | bytes 786440 | tf_op jit(solution)/shard_map/ppermute | solution.py:20
  114.0 9.0 %collective-permute-start.8 = (f32[256,256]{1,0:T(8,128)S(1)}, f32[256,256]{1,0:T(8,128)S(1)}, u32[]{:S(2)}, u32[]{:S(2)}) collective-permute-start(f32[256,256]{1,0:T(8,128)S(1)} %copy.98), channel_id=1, source_target_pairs={{56,0},{60,4},{0,8},{4,12},{8,16},{12,20},{16,24},{20,28},{24,32},... | collective-permute-start | bytes 786440 | tf_op jit(solution)/shard_map/ppermute | solution.py:20
  123.1 8.9 %collective-permute-start.10 = (f32[256,256]{1,0:T(8,128)S(1)}, f32[256,256]{1,0:T(8,128)S(1)}, u32[]{:S(2)}, u32[]{:S(2)}) collective-permute-start(f32[256,256]{1,0:T(8,128)S(1)} %get-tuple-element.607), channel_id=1, source_target_pairs={{0,12},{4,56},{8,20},{12,0},{16,28},{20,8},{24,36},{28,16},{32,44}... | collective-permute-start | bytes 786440 | tf_op jit(solution)/shard_map/ppermute | solution.py:31
  123.2 8.8 %collective-permute-start.9 = (f32[256,256]{1,0:T(8,128)S(1)}, f32[256,256]{1,0:T(8,128)S(1)}, u32[]{:S(2)}, u32[]{:S(2)}) collective-permute-start(f32[256,256]{1,0:T(8,128)S(1)} %get-tuple-element.608), channel_id=1, source_target_pairs={{0,56},{4,12},{8,0},{12,20},{16,8},{20,28},{24,16},{28,36},{32,24}... | collective-permute-start | bytes 786440 | tf_op jit(solution)/shard_map/ppermute | solution.py:31

commit v16 on v15

--- a/solution.py
+++ b/solution.py
@@ -38,7 +38,10 @@
 
 def live_region(block_mask, query_start, tok_rows, key_pos, key_starts, with_diagonal):
     row_count = tok_rows // BLK
-    block_table = jnp.concatenate(
+    if not with_diagonal:
+        block_table = None
+    else:
+        block_table = jnp.concatenate(
         [
             lax.dynamic_slice(block_mask, (query_start // BLK, start // BLK), (row_count, row_count))
             for start in key_starts
@@ -48,7 +51,10 @@
     if not with_diagonal:
         query_blocks = query_start // BLK + jnp.arange(row_count, dtype=jnp.int32)
         key_blocks = key_pos[::BLK] // BLK
-        block_live = (key_blocks[None, :] < query_blocks[:, None]) & (block_table == 1)
+        own_rows = lax.dynamic_slice_in_dim(block_mask, query_start // BLK, row_count, 0)
+        picks = jnp.arange(block_mask.shape[1], dtype=jnp.int32)[None, :] == key_blocks[:, None]
+        chosen = jnp.any((own_rows[:, None, :] == 1) & picks[None, :, :], axis=2)
+        block_live = (key_blocks[None, :] < query_blocks[:, None]) & chosen
         block_live = lax.optimization_barrier(block_live)
         return jnp.repeat(jnp.repeat(block_live, BLK, axis=0), BLK, axis=1)
     block_table = jnp.repeat(jnp.repeat(block_table, BLK, axis=0), BLK, axis=1)

time: 134 us -> 137 us (1.022)
  waiting for transfers between devices: 9.49 us -> 16.6 us
  local copies, waits for them, and re-layouts: 18 us -> 12.7 us
  other arithmetic: 8.57 us -> 10.8 us
  starting transfers between devices: 51.6 us -> 50 us
    ppermute x28, waiting for transfers between devices: 4.66 us -> 10.8 us  [along_z(): return lax.ppermute(value, 'ctx', pairs)]
    dynamic_slice x7 -> x1, local copies, waits for them, and re-layouts: 6.09 us -> 0.85 us  [live_region(): lax.dynamic_slice(block_mask, (query_start // BLK, start // BLK), (row_co...]
  transfers between devices with their start and end apart: 32 -> 32, of which waited for: 3 -> 8; matrix products, arithmetic and copies ran while one was open for 46% -> 42% of each run, Pallas kernels for 0% -> 0%
where the time goes in v16:
time: 137 us; the launch traced here: 136 us
  starting transfers between devices  50 us (36%)
  matrix products  43.6 us (32%)
  waiting for transfers between devices  16.6 us (12%)
  local copies, waits for them, and re-layouts  12.7 us (9%)
  other arithmetic  10.8 us (8%)
    ppermute x28, starting transfers between devices, along_z(): return lax.ppermute(value, 'ctx', pairs)  41.3 us
    dot_general x8, matrix products, contract(): jnp.einsum('igd,jd->gij', out_grads, values_part, preferred_element_type=...  12.5 us
    ppermute x28, waiting for transfers between devices, along_z(): return lax.ppermute(value, 'ctx', pairs)  10.8 us
    dot_general x8, matrix products, contract(): jnp.einsum('gij,igd->jd', probabilities.astype(jnp.bfloat16), out_grads,...  10.3 us
    dot_general x8, matrix products, contract(): jnp.einsum('gij,igd->jd', dscore, queries, preferred_element_type=jnp.flo...  7.9 us
    dot_general x8, matrix products, contract(): jnp.einsum('igd,jd->gij', queries, keys_part, preferred_element_type=jnp....  7.47 us
    ppermute x2, waiting for transfers between devices, to_owner(): return lax.ppermute(value, 'ctx', pairs)  5.74 us
    dot_general x8, matrix products, contract(): jnp.einsum('gij,jd->igd', dscore, keys_part, preferred_element_type=jnp.f...  5.42 us
  transfers between devices with their start and end apart: 32, of which 8 were waited for; matrix products, arithmetic and copies ran while one was open for 42% of the time, Pallas kernels for 0%

profile of v16, /device:TPU:4, one launch (start us, length us, event | category | flops | bytes accessed | tf_op | source)
XLA Modules:
  0.0 135.8 jit_solution(10744682917295013409)
XLA Ops:
  0.6 0.9 constant_dynamic-update-slice_fusion.3
  1.6 0.9 constant_dynamic-update-slice_fusion.2
  2.4 3.3 %collective-permute-start.4 = (bf16[256,256]{1,0:T(8,128)(2,1)S(1)}, bf16[256,256]{1,0:T(8,128)(2,1)S(1)}, u32[]{:S(2)}, u32[]{:S(2)}) collective-permute-start(bf16[256,256]{1,0:T(8,128)(2,1)S(1)} %constant_dynamic-update-slice_fusion.2), channel_id=1, source_target_pairs={{0,4},{4,0},{8,12},{12,8},{16,20},{20,16},{24,28},{28,24},{32,36},... | collective-permute-start | bytes 393224 | tf_op jit(solution)/shard_map/ppermute | solution.py:36
  5.7 1.9 %copy.160 = bf16[8,4,8,1024]{3,2,0,1:T(8,128)(2,1)} copy(bf16[8,4,8,1024]{3,2,1,0:T(8,128)(2,1)} %bitcast.192) | data formatting | bytes 1048576 | tf_op jit(solution)/shard_map/reshape | solution.py:99
  7.6 3.5 %all-to-all-start = ((bf16[64,4,1024]{2,0,1:T(8,128)(2,1)}), bf16[64,4,1024]{2,0,1:T(8,128)(2,1)S(1)}, u32[]{:S(2)}, u32[]{:S(2)}) async-start(bf16[64,4,1024]{2,0,1:T(8,128)(2,1)} %bitcast.145), calls=%async_computation | async-start | bytes 1048576 | tf_op jit(solution)/shard_map/all_to_all | solution.py:100
  12.0 0.8 fusion.68
  13.7 1.2 copy.104
  15.6 2.0 %collective-permute-start.6 = (bf16[256,256]{1,0:T(8,128)(2,1)S(1)}, bf16[256,256]{1,0:T(8,128)(2,1)S(1)}, u32[]{:S(2)}, u32[]{:S(2)}) collective-permute-start(bf16[256,256]{1,0:T(8,128)(2,1)S(1)} %get-tuple-element.616), channel_id=1, source_target_pairs={{56,0},{60,4},{0,8},{4,12},{8,16},{12,20},{16,24},{20,28},{24,32},... | collective-permute-start | bytes 393224 | tf_op jit(solution)/shard_map/ppermute | solution.py:20
  17.6 4.0 %collective-permute-start.5 = (bf16[256,256]{1,0:T(8,128)(2,1)S(1)}, bf16[256,256]{1,0:T(8,128)(2,1)S(1)}, u32[]{:S(2)}, u32[]{:S(2)}) collective-permute-start(bf16[256,256]{1,0:T(8,128)(2,1)S(1)} %get-tuple-element.617), channel_id=1, source_target_pairs={{8,0},{12,4},{16,8},{20,12},{24,16},{28,20},{32,24},{36,28},{40,32... | collective-permute-start | bytes 393224 | tf_op jit(solution)/shard_map/ppermute | solution.py:20
  21.6 2.6 %fusion.56 = f32[512,256,8]{1,0,2:T(8,128)} fusion(bf16[256,8,128]{0,2,1:T(8,128)(2,1)S(1)} %bitcast.180, bf16[256,256]{1,0:T(8,128)(2,1)S(1)} %get-tuple-element.617, bf16[256,256]{1,0:T(8,128)(2,1)S(1)} %get-tuple-element.616), kind=kOutput, calls=%fused_computation.98 | convolution fusion | flops 268697600 | bytes 4980736 | tf_op jit(solution)/shard_map/igd,jd->gij/dot_general | solution.py:72
  25.1 3.4 %fusion.36 = f32[512,128]{0,1:T(8,128)S(1)} fusion(bf16[256,8,128]{0,2,1:T(8,128)(2,1)S(1)} %copy.115, f32[512,256,8]{1,0,2:T(8,128)} %fusion.56, f32[8,256]{1,0:T(8,128)S(1)} %copy-done.5, pred[256,512]{0,1:T(8,128)(4,1)S(1)} %fusion.42), kind=kOutput, calls=%fused_computation.60 | convolution fusion | flops 272629760 | bytes 5120000 | tf_op jit(solution)/shard_map/gij,igd->jd/dot_general | solution.py:82
  28.5 1.4 %fusion.25 = bf16[8,256,512]{1,2,0:T(8,128)(2,1)S(1)} fusion(f32[512,256,8]{1,0,2:T(8,128)S(1)} %copy-done, f32[8,256]{1,0:T(8,128)S(1)} %copy.110, f32[8,256]{1,0:T(8,128)S(1)} %copy-done.5, pred[256,512]{0,1:T(8,128)(4,1)S(1)} %fusion.42, bf16[256,8,128]{2,1,0:T(8,128)(2,1)S(1)} %bitcast.185, bf16[256,256]{1,0:T(8,128)(2,1)S(1)} %get-tuple-element.616, ...), kind=kOutput, calls=%fused_computation.48 | convolution fusion | flops 274989056 | bytes 7225344 | tf_op jit(solution)/shard_map/igd,jd->gij/dot_general | solution.py:76
  30.5 0.8 convolution_bitcast_fusion.5
  31.3 0.8 pad_maximum_fusion.2
  32.1 75.7 %while.26 = (s32[]{:T(128)}, bf16[256,256]{1,0:T(8,128)(2,1)S(1)}, bf16[256,256]{1,0:T(8,128)(2,1)S(1)}, f32[256,8,128]{0,2,1:T(8,128)S(1)}, f32[256,256]{0,1:T(...) while((s32[]{:T(128)}, bf16[256,256]{1,0:T(8,128)(2,1)S(1)}, ...), condition=%wide.region_3.4_spmd.clone.clone, body=%wide.region_1.3_spmd.clone.clone.sunk | while | flops 1353189120 | bytes 32277916 | solution.py:156
  32.3 2.0 %collective-permute-start = (bf16[256,256]{1,0:T(8,128)(2,1)S(1)}, bf16[256,256]{1,0:T(8,128)(2,1)S(1)}, u32[]{:S(2)}, u32[]{:S(2)}) collective-permute-start(bf16[256,256]{1,0:T(8,128)(2,1)S(1)} %copy.170), channel_id=1, source_target_pairs={{8,0},{12,4},{16,8},{20,12},{24,16},{28,20},{32,24},{36,28},{40,32... | collective-permute-start | bytes 393224 | tf_op jit(solution)/shard_map/while/body/eval_jaxpr/ppermute | solution.py:20
  34.5 3.1 %collective-permute-start.3 = (f32[256,256]{0,1:T(8,128)}, f32[256,256]{0,1:T(8,128)S(1)}, u32[]{:S(2)}, u32[]{:S(2)}) collective-permute-start(f32[256,256]{0,1:T(8,128)} %get-tuple-element.738), channel_id=1, source_target_pairs={{8,0},{12,4},{16,8},{20,12},{24,16},{28,20},{32,24},{36,28},{40,32... | collective-permute-start | bytes 786440 | tf_op jit(solution)/shard_map/while/body/eval_jaxpr/ppermute | solution.py:20
  39.0 1.0 fusion.107
  40.1 1.4 %fusion.105 = bf16[8,256,512]{1,2,0:T(8,128)(2,1)S(1)} fusion(f32[512,256,8]{1,0,2:T(8,128)S(1)} %fusion.104, bf16[256,8,128]{0,2,1:T(8,128)(2,1)S(1)} %copy-done.3, f32[8,256]{1,0:T(8,128)S(1)} %get-tuple-element.765, f32[8,256]{1,0:T(8,128)S(1)} %get-tuple-element.763, pred[256,512]{0,1:T(8,128)(4,1)S(1)} %bitcast.188, ...), kind=kOutput, calls=%fused_computation.3.clone.1 | convolution fusion | flops 274726912 | bytes 7094272 | tf_op jit(solution)/shard_map/while/body/eval_jaxpr/igd,jd->gij/dot_general | solution.py:76
  41.9 0.8 convolution_bitcast_fusion.7
  42.8 3.3 %collective-permute-done.2 = f32[256,256]{0,1:T(8,128)S(1)} collective-permute-done((f32[256,256]{0,1:T(8,128)}, f32[256,256]{0,1:T(8,128)S(1)}, u32[]{:S(2)}, u32[]{:S(2)}) %collective-permute-start.2) | collective-permute-done | bytes 262176 | tf_op jit(solution)/shard_map/while/body/eval_jaxpr/ppermute | solution.py:20
  46.1 0.9 fusion.108
  47.5 1.7 %collective-permute-start.1 = (bf16[256,256]{1,0:T(8,128)(2,1)S(1)}, bf16[256,256]{1,0:T(8,128)(2,1)S(1)}, u32[]{:S(2)}, u32[]{:S(2)}) collective-permute-start(bf16[256,256]{1,0:T(8,128)(2,1)S(1)} %copy.171), channel_id=1, source_target_pairs={{56,0},{60,4},{0,8},{4,12},{8,16},{12,20},{16,24},{20,28},{24,32},... | collective-permute-start | bytes 393224 | tf_op jit(solution)/shard_map/while/body/eval_jaxpr/ppermute | solution.py:20
  49.3 3.1 %collective-permute-start.3 = (f32[256,256]{0,1:T(8,128)}, f32[256,256]{0,1:T(8,128)S(1)}, u32[]{:S(2)}, u32[]{:S(2)}) collective-permute-start(f32[256,256]{0,1:T(8,128)} %get-tuple-element.738), channel_id=1, source_target_pairs={{8,0},{12,4},{16,8},{20,12},{24,16},{28,20},{32,24},{36,28},{40,32... | collective-permute-start | bytes 786440 | tf_op jit(solution)/shard_map/while/body/eval_jaxpr/ppermute | solution.py:20
  53.8 1.0 fusion.107
  54.8 1.4 %fusion.105 = bf16[8,256,512]{1,2,0:T(8,128)(2,1)S(1)} fusion(f32[512,256,8]{1,0,2:T(8,128)S(1)} %fusion.104, bf16[256,8,128]{0,2,1:T(8,128)(2,1)S(1)} %copy-done.3, f32[8,256]{1,0:T(8,128)S(1)} %get-tuple-element.765, f32[8,256]{1,0:T(8,128)S(1)} %get-tuple-element.763, pred[256,512]{0,1:T(8,128)(4,1)S(1)} %bitcast.188, ...), kind=kOutput, calls=%fused_computation.3.clone.1 | convolution fusion | flops 274726912 | bytes 7094272 | tf_op jit(solution)/shard_map/while/body/eval_jaxpr/igd,jd->gij/dot_general | solution.py:76
  56.7 0.8 convolution_bitcast_fusion.7
  58.2 0.9 fusion.108
  59.1 2.1 %collective-permute-start = (bf16[256,256]{1,0:T(8,128)(2,1)S(1)}, bf16[256,256]{1,0:T(8,128)(2,1)S(1)}, u32[]{:S(2)}, u32[]{:S(2)}) collective-permute-start(bf16[256,256]{1,0:T(8,128)(2,1)S(1)} %copy.170), channel_id=1, source_target_pairs={{8,0},{12,4},{16,8},{20,12},{24,16},{28,20},{32,24},{36,28},{40,32... | collective-permute-start | bytes 393224 | tf_op jit(solution)/shard_map/while/body/eval_jaxpr/ppermute | solution.py:20
  61.6 3.0 %collective-permute-start.3 = (f32[256,256]{0,1:T(8,128)}, f32[256,256]{0,1:T(8,128)S(1)}, u32[]{:S(2)}, u32[]{:S(2)}) collective-permute-start(f32[256,256]{0,1:T(8,128)} %get-tuple-element.738), channel_id=1, source_target_pairs={{8,0},{12,4},{16,8},{20,12},{24,16},{28,20},{32,24},{36,28},{40,32... | collective-permute-start | bytes 786440 | tf_op jit(solution)/shard_map/while/body/eval_jaxpr/ppermute | solution.py:20
  66.0 1.0 fusion.107
  67.0 1.4 %fusion.105 = bf16[8,256,512]{1,2,0:T(8,128)(2,1)S(1)} fusion(f32[512,256,8]{1,0,2:T(8,128)S(1)} %fusion.104, bf16[256,8,128]{0,2,1:T(8,128)(2,1)S(1)} %copy-done.3, f32[8,256]{1,0:T(8,128)S(1)} %get-tuple-element.765, f32[8,256]{1,0:T(8,128)S(1)} %get-tuple-element.763, pred[256,512]{0,1:T(8,128)(4,1)S(1)} %bitcast.188, ...), kind=kOutput, calls=%fused_computation.3.clone.1 | convolution fusion | flops 274726912 | bytes 7094272 | tf_op jit(solution)/shard_map/while/body/eval_jaxpr/igd,jd->gij/dot_general | solution.py:76
  68.9 0.8 convolution_bitcast_fusion.7
  70.3 0.9 fusion.108
  71.2 2.2 %collective-permute-start = (bf16[256,256]{1,0:T(8,128)(2,1)S(1)}, bf16[256,256]{1,0:T(8,128)(2,1)S(1)}, u32[]{:S(2)}, u32[]{:S(2)}) collective-permute-start(bf16[256,256]{1,0:T(8,128)(2,1)S(1)} %copy.170), channel_id=1, source_target_pairs={{8,0},{12,4},{16,8},{20,12},{24,16},{28,20},{32,24},{36,28},{40,32... | collective-permute-start | bytes 393224 | tf_op jit(solution)/shard_map/while/body/eval_jaxpr/ppermute | solution.py:20
  74.0 2.8 %collective-permute-start.3 = (f32[256,256]{0,1:T(8,128)}, f32[256,256]{0,1:T(8,128)S(1)}, u32[]{:S(2)}, u32[]{:S(2)}) collective-permute-start(f32[256,256]{0,1:T(8,128)} %get-tuple-element.738), channel_id=1, source_target_pairs={{8,0},{12,4},{16,8},{20,12},{24,16},{28,20},{32,24},{36,28},{40,32... | collective-permute-start | bytes 786440 | tf_op jit(solution)/shard_map/while/body/eval_jaxpr/ppermute | solution.py:20
  78.2 1.0 fusion.107
  79.2 1.4 %fusion.105 = bf16[8,256,512]{1,2,0:T(8,128)(2,1)S(1)} fusion(f32[512,256,8]{1,0,2:T(8,128)S(1)} %fusion.104, bf16[256,8,128]{0,2,1:T(8,128)(2,1)S(1)} %copy-done.3, f32[8,256]{1,0:T(8,128)S(1)} %get-tuple-element.765, f32[8,256]{1,0:T(8,128)S(1)} %get-tuple-element.763, pred[256,512]{0,1:T(8,128)(4,1)S(1)} %bitcast.188, ...), kind=kOutput, calls=%fused_computation.3.clone.1 | convolution fusion | flops 274726912 | bytes 7094272 | tf_op jit(solution)/shard_map/while/body/eval_jaxpr/igd,jd->gij/dot_general | solution.py:76
  81.1 0.8 convolution_bitcast_fusion.7
  82.5 0.9 fusion.108
  83.4 2.2 %collective-permute-start = (bf16[256,256]{1,0:T(8,128)(2,1)S(1)}, bf16[256,256]{1,0:T(8,128)(2,1)S(1)}, u32[]{:S(2)}, u32[]{:S(2)}) collective-permute-start(bf16[256,256]{1,0:T(8,128)(2,1)S(1)} %copy.170), channel_id=1, source_target_pairs={{8,0},{12,4},{16,8},{20,12},{24,16},{28,20},{32,24},{36,28},{40,32... | collective-permute-start | bytes 393224 | tf_op jit(solution)/shard_map/while/body/eval_jaxpr/ppermute | solution.py:20
  85.7 0.8 collective-permute-start.2
  86.5 2.5 %collective-permute-start.3 = (f32[256,256]{0,1:T(8,128)}, f32[256,256]{0,1:T(8,128)S(1)}, u32[]{:S(2)}, u32[]{:S(2)}) collective-permute-start(f32[256,256]{0,1:T(8,128)} %get-tuple-element.738), channel_id=1, source_target_pairs={{8,0},{12,4},{16,8},{20,12},{24,16},{28,20},{32,24},{36,28},{40,32... | collective-permute-start | bytes 786440 | tf_op jit(solution)/shard_map/while/body/eval_jaxpr/ppermute | solution.py:20
  90.4 1.0 fusion.107
  91.4 1.4 %fusion.105 = bf16[8,256,512]{1,2,0:T(8,128)(2,1)S(1)} fusion(f32[512,256,8]{1,0,2:T(8,128)S(1)} %fusion.104, bf16[256,8,128]{0,2,1:T(8,128)(2,1)S(1)} %copy-done.3, f32[8,256]{1,0:T(8,128)S(1)} %get-tuple-element.765, f32[8,256]{1,0:T(8,128)S(1)} %get-tuple-element.763, pred[256,512]{0,1:T(8,128)(4,1)S(1)} %bitcast.188, ...), kind=kOutput, calls=%fused_computation.3.clone.1 | convolution fusion | flops 274726912 | bytes 7094272 | tf_op jit(solution)/shard_map/while/body/eval_jaxpr/igd,jd->gij/dot_general | solution.py:76
  93.3 0.8 convolution_bitcast_fusion.7
  94.7 0.9 fusion.108
  95.6 2.2 %collective-permute-start = (bf16[256,256]{1,0:T(8,128)(2,1)S(1)}, bf16[256,256]{1,0:T(8,128)(2,1)S(1)}, u32[]{:S(2)}, u32[]{:S(2)}) collective-permute-start(bf16[256,256]{1,0:T(8,128)(2,1)S(1)} %copy.170), channel_id=1, source_target_pairs={{8,0},{12,4},{16,8},{20,12},{24,16},{28,20},{32,24},{36,28},{40,32... | collective-permute-start | bytes 393224 | tf_op jit(solution)/shard_map/while/body/eval_jaxpr/ppermute | solution.py:20
  97.9 1.0 collective-permute-start.2
  98.8 2.4 %collective-permute-start.3 = (f32[256,256]{0,1:T(8,128)}, f32[256,256]{0,1:T(8,128)S(1)}, u32[]{:S(2)}, u32[]{:S(2)}) collective-permute-start(f32[256,256]{0,1:T(8,128)} %get-tuple-element.738), channel_id=1, source_target_pairs={{8,0},{12,4},{16,8},{20,12},{24,16},{28,20},{32,24},{36,28},{40,32... | collective-permute-start | bytes 786440 | tf_op jit(solution)/shard_map/while/body/eval_jaxpr/ppermute | solution.py:20
  102.5 1.0 fusion.107
  103.6 1.4 %fusion.105 = bf16[8,256,512]{1,2,0:T(8,128)(2,1)S(1)} fusion(f32[512,256,8]{1,0,2:T(8,128)S(1)} %fusion.104, bf16[256,8,128]{0,2,1:T(8,128)(2,1)S(1)} %copy-done.3, f32[8,256]{1,0:T(8,128)S(1)} %get-tuple-element.765, f32[8,256]{1,0:T(8,128)S(1)} %get-tuple-element.763, pred[256,512]{0,1:T(8,128)(4,1)S(1)} %bitcast.188, ...), kind=kOutput, calls=%fused_computation.3.clone.1 | convolution fusion | flops 274726912 | bytes 7094272 | tf_op jit(solution)/shard_map/while/body/eval_jaxpr/igd,jd->gij/dot_general | solution.py:76
  106.9 0.9 fusion.108
  108.8 0.9 fusion.39
  109.7 2.7 %fusion.21 = bf16[8,256,512]{1,2,0:T(8,128)(2,1)} fusion(f32[512,256,8]{1,0,2:T(8,128)S(1)} %fusion.55, f32[8,256]{1,0:T(8,128)S(1)} %get-tuple-element.795, f32[8,256]{1,0:T(8,128)S(1)} %get-tuple-element.796, pred[256,512]{0,1:T(8,128)(4,1)S(1)} %bitcast.195, bf16[256,8,128]{2,1,0:T(8,128)(2,1)S(1)} %bitcast.186, ...), kind=kOutput, calls=%fused_computation.42 | convolution fusion | flops 274726912 | bytes 7094272 | tf_op jit(solution)/shard_map/igd,jd->gij/dot_general | solution.py:76
  112.4 1.1 copy.128
  113.5 1.1 copy.122
  114.6 2.2 %collective-permute-start.7 = (f32[256,256]{1,0:T(8,128)S(1)}, f32[256,256]{1,0:T(8,128)S(1)}, u32[]{:S(2)}, u32[]{:S(2)}) collective-permute-start(f32[256,256]{1,0:T(8,128)S(1)} %copy.122), channel_id=1, source_target_pairs={{8,0},{12,4},{16,8},{20,12},{24,16},{28,20},{32,24},{36,28},{40,32... | collective-permute-start | bytes 786440 | tf_op jit(solution)/shard_map/ppermute | solution.py:20
  116.8 2.1 %convolution_bitcast_fusion.2 = f32[256,8,128]{0,2,1:T(8,128)S(1)} fusion(bf16[8,256,512]{1,2,0:T(8,128)(2,1)} %fusion.21, bf16[512,256]{1,0:T(8,128)(2,1)S(1)} %constant_dynamic-update-slice_fusion.4), kind=kOutput, calls=%fused_computation.58 | convolution fusion | flops 268435456 | bytes 3276800 | tf_op jit(solution)/shard_map/gij,jd->igd/dot_general | solution.py:80
  118.9 2.3 %convolution_bitcast_fusion.4 = f32[512,128]{1,0:T(8,128)S(1)} fusion(bf16[8,256,512]{1,2,0:T(8,128)(2,1)} %fusion.21, bf16[256,8,128]{0,2,1:T(8,128)(2,1)S(1)} %get-tuple-element.772), kind=kOutput, calls=%fused_computation.62 | convolution fusion | flops 268435456 | bytes 2883584 | tf_op jit(solution)/shard_map/gij,igd->jd/dot_general | solution.py:81
  121.2 4.4 %collective-permute-done.8 = f32[256,256]{1,0:T(8,128)S(1)} collective-permute-done((f32[256,256]{1,0:T(8,128)S(1)}, f32[256,256]{1,0:T(8,128)S(1)}, u32[]{:S(2)}, u32[]{:S(2)}) %collective-permute-start.8) | collective-permute-done | bytes 262176 | tf_op jit(solution)/shard_map/ppermute | solution.py:20
  125.7 1.8 %collective-permute-start.9 = (f32[256,256]{1,0:T(8,128)S(1)}, f32[256,256]{1,0:T(8,128)S(1)}, u32[]{:S(2)}, u32[]{:S(2)}) collective-permute-start(f32[256,256]{1,0:T(8,128)S(1)} %get-tuple-element.613), channel_id=1, source_target_pairs={{0,56},{4,12},{8,0},{12,20},{16,8},{20,28},{24,16},{28,36},{32,24}... | collective-permute-start | bytes 786440 | tf_op jit(solution)/shard_map/ppermute | solution.py:31
  127.7 1.0 copy.129
  128.7 5.7 %collective-permute-done.10 = f32[256,256]{1,0:T(8,128)S(1)} collective-permute-done((f32[256,256]{1,0:T(8,128)S(1)}, f32[256,256]{1,0:T(8,128)S(1)}, u32[]{:S(2)}, u32[]{:S(2)}) %collective-permute-start.10) | collective-permute-done | bytes 262176 | tf_op jit(solution)/shard_map/ppermute | solution.py:31
  (199 shorter events, 22.7 us)
Async XLA Ops:
  0.6 14.3 %copy-start.1 = (bf16[256,1024]{1,0:T(8,128)(2,1)S(1)}, bf16[256,1024]{1,0:T(8,128)(2,1)}, u32[]{:S(2)}) copy-start(bf16[256,1024]{1,0:T(8,128)(2,1)} %param.12) | copy-start | bytes 1572868
  2.4 13.1 %collective-permute-start.4 = (bf16[256,256]{1,0:T(8,128)(2,1)S(1)}, bf16[256,256]{1,0:T(8,128)(2,1)S(1)}, u32[]{:S(2)}, u32[]{:S(2)}) collective-permute-start(bf16[256,256]{1,0:T(8,128)(2,1)S(1)} %constant_dynamic-update-slice_fusion.2), channel_id=1, source_target_pairs={{0,4},{4,0},{8,12},{12,8},{16,20},{20,16},{24,28},{28,24},{32,36},... | collective-permute-start | bytes 393224 | tf_op jit(solution)/shard_map/ppermute | solution.py:36
  7.6 16.6 %all-to-all-start = ((bf16[64,4,1024]{2,0,1:T(8,128)(2,1)}), bf16[64,4,1024]{2,0,1:T(8,128)(2,1)S(1)}, u32[]{:S(2)}, u32[]{:S(2)}) async-start(bf16[64,4,1024]{2,0,1:T(8,128)(2,1)} %bitcast.145), calls=%async_computation | async-start | bytes 1048576 | tf_op jit(solution)/shard_map/all_to_all | solution.py:100
  15.6 16.5 %collective-permute-start.6 = (bf16[256,256]{1,0:T(8,128)(2,1)S(1)}, bf16[256,256]{1,0:T(8,128)(2,1)S(1)}, u32[]{:S(2)}, u32[]{:S(2)}) collective-permute-start(bf16[256,256]{1,0:T(8,128)(2,1)S(1)} %get-tuple-element.616), channel_id=1, source_target_pairs={{56,0},{60,4},{0,8},{4,12},{8,16},{12,20},{16,24},{20,28},{24,32},... | collective-permute-start | bytes 393224 | tf_op jit(solution)/shard_map/ppermute | solution.py:20
  17.6 14.5 %collective-permute-start.5 = (bf16[256,256]{1,0:T(8,128)(2,1)S(1)}, bf16[256,256]{1,0:T(8,128)(2,1)S(1)}, u32[]{:S(2)}, u32[]{:S(2)}) collective-permute-start(bf16[256,256]{1,0:T(8,128)(2,1)S(1)} %get-tuple-element.617), channel_id=1, source_target_pairs={{8,0},{12,4},{16,8},{20,12},{24,16},{28,20},{32,24},{36,28},{40,32... | collective-permute-start | bytes 393224 | tf_op jit(solution)/shard_map/ppermute | solution.py:20
  21.6 3.5 %copy-start.5 = (f32[8,256]{1,0:T(8,128)S(1)}, f32[8,256]{1,0:T(8,128)}, u32[]{:S(2)}) copy-start(f32[8,256]{1,0:T(8,128)} %param.14) | copy-start | bytes 24580
  24.7 5.3 %copy-start.2 = (bf16[256,8,128]{0,2,1:T(8,128)(2,1)}, bf16[256,8,128]{0,2,1:T(8,128)(2,1)S(1)}, u32[]{:S(2)}) copy-start(bf16[256,8,128]{0,2,1:T(8,128)(2,1)S(1)} %copy.115) | copy-start | bytes 1572868
  25.1 3.5 %copy-start = (f32[512,256,8]{1,0,2:T(8,128)S(1)}, f32[512,256,8]{1,0,2:T(8,128)}, u32[]{:S(2)}) copy-start(f32[512,256,8]{1,0,2:T(8,128)} %fusion.56) | copy-start | bytes 12582916
  32.3 14.7 %collective-permute-start = (bf16[256,256]{1,0:T(8,128)(2,1)S(1)}, bf16[256,256]{1,0:T(8,128)(2,1)S(1)}, u32[]{:S(2)}, u32[]{:S(2)}) collective-permute-start(bf16[256,256]{1,0:T(8,128)(2,1)S(1)} %copy.170), channel_id=1, source_target_pairs={{8,0},{12,4},{16,8},{20,12},{24,16},{28,20},{32,24},{36,28},{40,32... | collective-permute-start | bytes 393224 | tf_op jit(solution)/shard_map/while/body/eval_jaxpr/ppermute | solution.py:20
  34.3 12.7 %collective-permute-start.1 = (bf16[256,256]{1,0:T(8,128)(2,1)S(1)}, bf16[256,256]{1,0:T(8,128)(2,1)S(1)}, u32[]{:S(2)}, u32[]{:S(2)}) collective-permute-start(bf16[256,256]{1,0:T(8,128)(2,1)S(1)} %copy.171), channel_id=1, source_target_pairs={{56,0},{60,4},{0,8},{4,12},{8,16},{12,20},{16,24},{20,28},{24,32},... | collective-permute-start | bytes 393224 | tf_op jit(solution)/shard_map/while/body/eval_jaxpr/ppermute | solution.py:20
  34.5 11.6 %collective-permute-start.2 = (f32[256,256]{0,1:T(8,128)}, f32[256,256]{0,1:T(8,128)S(1)}, u32[]{:S(2)}, u32[]{:S(2)}) collective-permute-start(f32[256,256]{0,1:T(8,128)} %get-tuple-element.739), channel_id=1, source_target_pairs={{56,0},{60,4},{0,8},{4,12},{8,16},{12,20},{16,24},{20,28},{24,32},... | collective-permute-start | bytes 786440 | tf_op jit(solution)/shard_map/while/body/eval_jaxpr/ppermute | solution.py:20
  34.5 11.5 %collective-permute-start.3 = (f32[256,256]{0,1:T(8,128)}, f32[256,256]{0,1:T(8,128)S(1)}, u32[]{:S(2)}, u32[]{:S(2)}) collective-permute-start(f32[256,256]{0,1:T(8,128)} %get-tuple-element.738), channel_id=1, source_target_pairs={{8,0},{12,4},{16,8},{20,12},{24,16},{28,20},{32,24},{36,28},{40,32... | collective-permute-start | bytes 786440 | tf_op jit(solution)/shard_map/while/body/eval_jaxpr/ppermute | solution.py:20
  37.9 1.2 copy-start.3
  47.0 12.1 %collective-permute-start = (bf16[256,256]{1,0:T(8,128)(2,1)S(1)}, bf16[256,256]{1,0:T(8,128)(2,1)S(1)}, u32[]{:S(2)}, u32[]{:S(2)}) collective-permute-start(bf16[256,256]{1,0:T(8,128)(2,1)S(1)} %copy.170), channel_id=1, source_target_pairs={{8,0},{12,4},{16,8},{20,12},{24,16},{28,20},{32,24},{36,28},{40,32... | collective-permute-start | bytes 393224 | tf_op jit(solution)/shard_map/while/body/eval_jaxpr/ppermute | solution.py:20
  47.5 11.6 %collective-permute-start.1 = (bf16[256,256]{1,0:T(8,128)(2,1)S(1)}, bf16[256,256]{1,0:T(8,128)(2,1)S(1)}, u32[]{:S(2)}, u32[]{:S(2)}) collective-permute-start(bf16[256,256]{1,0:T(8,128)(2,1)S(1)} %copy.171), channel_id=1, source_target_pairs={{56,0},{60,4},{0,8},{4,12},{8,16},{12,20},{16,24},{20,28},{24,32},... | collective-permute-start | bytes 393224 | tf_op jit(solution)/shard_map/while/body/eval_jaxpr/ppermute | solution.py:20
  49.2 9.0 %collective-permute-start.2 = (f32[256,256]{0,1:T(8,128)}, f32[256,256]{0,1:T(8,128)S(1)}, u32[]{:S(2)}, u32[]{:S(2)}) collective-permute-start(f32[256,256]{0,1:T(8,128)} %get-tuple-element.739), channel_id=1, source_target_pairs={{56,0},{60,4},{0,8},{4,12},{8,16},{12,20},{16,24},{20,28},{24,32},... | collective-permute-start | bytes 786440 | tf_op jit(solution)/shard_map/while/body/eval_jaxpr/ppermute | solution.py:20
  49.3 8.9 %collective-permute-start.3 = (f32[256,256]{0,1:T(8,128)}, f32[256,256]{0,1:T(8,128)S(1)}, u32[]{:S(2)}, u32[]{:S(2)}) collective-permute-start(f32[256,256]{0,1:T(8,128)} %get-tuple-element.738), channel_id=1, source_target_pairs={{8,0},{12,4},{16,8},{20,12},{24,16},{28,20},{32,24},{36,28},{40,32... | collective-permute-start | bytes 786440 | tf_op jit(solution)/shard_map/while/body/eval_jaxpr/ppermute | solution.py:20
  52.6 1.2 copy-start.3
  59.1 12.0 %collective-permute-start = (bf16[256,256]{1,0:T(8,128)(2,1)S(1)}, bf16[256,256]{1,0:T(8,128)(2,1)S(1)}, u32[]{:S(2)}, u32[]{:S(2)}) collective-permute-start(bf16[256,256]{1,0:T(8,128)(2,1)S(1)} %copy.170), channel_id=1, source_target_pairs={{8,0},{12,4},{16,8},{20,12},{24,16},{28,20},{32,24},{36,28},{40,32... | collective-permute-start | bytes 393224 | tf_op jit(solution)/shard_map/while/body/eval_jaxpr/ppermute | solution.py:20
  61.2 10.0 %collective-permute-start.1 = (bf16[256,256]{1,0:T(8,128)(2,1)S(1)}, bf16[256,256]{1,0:T(8,128)(2,1)S(1)}, u32[]{:S(2)}, u32[]{:S(2)}) collective-permute-start(bf16[256,256]{1,0:T(8,128)(2,1)S(1)} %copy.171), channel_id=1, source_target_pairs={{56,0},{60,4},{0,8},{4,12},{8,16},{12,20},{16,24},{20,28},{24,32},... | collective-permute-start | bytes 393224 | tf_op jit(solution)/shard_map/while/body/eval_jaxpr/ppermute | solution.py:20
  61.3 9.0 %collective-permute-start.2 = (f32[256,256]{0,1:T(8,128)}, f32[256,256]{0,1:T(8,128)S(1)}, u32[]{:S(2)}, u32[]{:S(2)}) collective-permute-start(f32[256,256]{0,1:T(8,128)} %get-tuple-element.739), channel_id=1, source_target_pairs={{56,0},{60,4},{0,8},{4,12},{8,16},{12,20},{16,24},{20,28},{24,32},... | collective-permute-start | bytes 786440 | tf_op jit(solution)/shard_map/while/body/eval_jaxpr/ppermute | solution.py:20
  61.6 8.7 %collective-permute-start.3 = (f32[256,256]{0,1:T(8,128)}, f32[256,256]{0,1:T(8,128)S(1)}, u32[]{:S(2)}, u32[]{:S(2)}) collective-permute-start(f32[256,256]{0,1:T(8,128)} %get-tuple-element.738), channel_id=1, source_target_pairs={{8,0},{12,4},{16,8},{20,12},{24,16},{28,20},{32,24},{36,28},{40,32... | collective-permute-start | bytes 786440 | tf_op jit(solution)/shard_map/while/body/eval_jaxpr/ppermute | solution.py:20
  64.8 1.2 copy-start.3
  71.2 12.2 %collective-permute-start = (bf16[256,256]{1,0:T(8,128)(2,1)S(1)}, bf16[256,256]{1,0:T(8,128)(2,1)S(1)}, u32[]{:S(2)}, u32[]{:S(2)}) collective-permute-start(bf16[256,256]{1,0:T(8,128)(2,1)S(1)} %copy.170), channel_id=1, source_target_pairs={{8,0},{12,4},{16,8},{20,12},{24,16},{28,20},{32,24},{36,28},{40,32... | collective-permute-start | bytes 393224 | tf_op jit(solution)/shard_map/while/body/eval_jaxpr/ppermute | solution.py:20
  73.4 10.0 %collective-permute-start.1 = (bf16[256,256]{1,0:T(8,128)(2,1)S(1)}, bf16[256,256]{1,0:T(8,128)(2,1)S(1)}, u32[]{:S(2)}, u32[]{:S(2)}) collective-permute-start(bf16[256,256]{1,0:T(8,128)(2,1)S(1)} %copy.171), channel_id=1, source_target_pairs={{56,0},{60,4},{0,8},{4,12},{8,16},{12,20},{16,24},{20,28},{24,32},... | collective-permute-start | bytes 393224 | tf_op jit(solution)/shard_map/while/body/eval_jaxpr/ppermute | solution.py:20
  73.5 9.0 %collective-permute-start.2 = (f32[256,256]{0,1:T(8,128)}, f32[256,256]{0,1:T(8,128)S(1)}, u32[]{:S(2)}, u32[]{:S(2)}) collective-permute-start(f32[256,256]{0,1:T(8,128)} %get-tuple-element.739), channel_id=1, source_target_pairs={{56,0},{60,4},{0,8},{4,12},{8,16},{12,20},{16,24},{20,28},{24,32},... | collective-permute-start | bytes 786440 | tf_op jit(solution)/shard_map/while/body/eval_jaxpr/ppermute | solution.py:20
  74.0 8.5 %collective-permute-start.3 = (f32[256,256]{0,1:T(8,128)}, f32[256,256]{0,1:T(8,128)S(1)}, u32[]{:S(2)}, u32[]{:S(2)}) collective-permute-start(f32[256,256]{0,1:T(8,128)} %get-tuple-element.738), channel_id=1, source_target_pairs={{8,0},{12,4},{16,8},{20,12},{24,16},{28,20},{32,24},{36,28},{40,32... | collective-permute-start | bytes 786440 | tf_op jit(solution)/shard_map/while/body/eval_jaxpr/ppermute | solution.py:20
  77.0 1.2 copy-start.3
  83.4 12.2 %collective-permute-start = (bf16[256,256]{1,0:T(8,128)(2,1)S(1)}, bf16[256,256]{1,0:T(8,128)(2,1)S(1)}, u32[]{:S(2)}, u32[]{:S(2)}) collective-permute-start(bf16[256,256]{1,0:T(8,128)(2,1)S(1)} %copy.170), channel_id=1, source_target_pairs={{8,0},{12,4},{16,8},{20,12},{24,16},{28,20},{32,24},{36,28},{40,32... | collective-permute-start | bytes 393224 | tf_op jit(solution)/shard_map/while/body/eval_jaxpr/ppermute | solution.py:20
  85.6 10.0 %collective-permute-start.1 = (bf16[256,256]{1,0:T(8,128)(2,1)S(1)}, bf16[256,256]{1,0:T(8,128)(2,1)S(1)}, u32[]{:S(2)}, u32[]{:S(2)}) collective-permute-start(bf16[256,256]{1,0:T(8,128)(2,1)S(1)} %copy.171), channel_id=1, source_target_pairs={{56,0},{60,4},{0,8},{4,12},{8,16},{12,20},{16,24},{20,28},{24,32},... | collective-permute-start | bytes 393224 | tf_op jit(solution)/shard_map/while/body/eval_jaxpr/ppermute | solution.py:20
  85.7 9.0 %collective-permute-start.2 = (f32[256,256]{0,1:T(8,128)}, f32[256,256]{0,1:T(8,128)S(1)}, u32[]{:S(2)}, u32[]{:S(2)}) collective-permute-start(f32[256,256]{0,1:T(8,128)} %get-tuple-element.739), channel_id=1, source_target_pairs={{56,0},{60,4},{0,8},{4,12},{8,16},{12,20},{16,24},{20,28},{24,32},... | collective-permute-start | bytes 786440 | tf_op jit(solution)/shard_map/while/body/eval_jaxpr/ppermute | solution.py:20
  86.5 8.1 %collective-permute-start.3 = (f32[256,256]{0,1:T(8,128)}, f32[256,256]{0,1:T(8,128)S(1)}, u32[]{:S(2)}, u32[]{:S(2)}) collective-permute-start(f32[256,256]{0,1:T(8,128)} %get-tuple-element.738), channel_id=1, source_target_pairs={{8,0},{12,4},{16,8},{20,12},{24,16},{28,20},{32,24},{36,28},{40,32... | collective-permute-start | bytes 786440 | tf_op jit(solution)/shard_map/while/body/eval_jaxpr/ppermute | solution.py:20
  89.2 1.2 copy-start.3
  95.6 12.2 %collective-permute-start = (bf16[256,256]{1,0:T(8,128)(2,1)S(1)}, bf16[256,256]{1,0:T(8,128)(2,1)S(1)}, u32[]{:S(2)}, u32[]{:S(2)}) collective-permute-start(bf16[256,256]{1,0:T(8,128)(2,1)S(1)} %copy.170), channel_id=1, source_target_pairs={{8,0},{12,4},{16,8},{20,12},{24,16},{28,20},{32,24},{36,28},{40,32... | collective-permute-start | bytes 393224 | tf_op jit(solution)/shard_map/while/body/eval_jaxpr/ppermute | solution.py:20
  97.8 10.0 %collective-permute-start.1 = (bf16[256,256]{1,0:T(8,128)(2,1)S(1)}, bf16[256,256]{1,0:T(8,128)(2,1)S(1)}, u32[]{:S(2)}, u32[]{:S(2)}) collective-permute-start(bf16[256,256]{1,0:T(8,128)(2,1)S(1)} %copy.171), channel_id=1, source_target_pairs={{56,0},{60,4},{0,8},{4,12},{8,16},{12,20},{16,24},{20,28},{24,32},... | collective-permute-start | bytes 393224 | tf_op jit(solution)/shard_map/while/body/eval_jaxpr/ppermute | solution.py:20
  97.9 9.0 %collective-permute-start.2 = (f32[256,256]{0,1:T(8,128)}, f32[256,256]{0,1:T(8,128)S(1)}, u32[]{:S(2)}, u32[]{:S(2)}) collective-permute-start(f32[256,256]{0,1:T(8,128)} %get-tuple-element.739), channel_id=1, source_target_pairs={{56,0},{60,4},{0,8},{4,12},{8,16},{12,20},{16,24},{20,28},{24,32},... | collective-permute-start | bytes 786440 | tf_op jit(solution)/shard_map/while/body/eval_jaxpr/ppermute | solution.py:20
  98.8 8.0 %collective-permute-start.3 = (f32[256,256]{0,1:T(8,128)}, f32[256,256]{0,1:T(8,128)S(1)}, u32[]{:S(2)}, u32[]{:S(2)}) collective-permute-start(f32[256,256]{0,1:T(8,128)} %get-tuple-element.738), channel_id=1, source_target_pairs={{8,0},{12,4},{16,8},{20,12},{24,16},{28,20},{32,24},{36,28},{40,32... | collective-permute-start | bytes 786440 | tf_op jit(solution)/shard_map/while/body/eval_jaxpr/ppermute | solution.py:20
  101.4 1.2 copy-start.3
  107.7 1.0 copy-start.4
  114.6 6.6 %collective-permute-start.7 = (f32[256,256]{1,0:T(8,128)S(1)}, f32[256,256]{1,0:T(8,128)S(1)}, u32[]{:S(2)}, u32[]{:S(2)}) collective-permute-start(f32[256,256]{1,0:T(8,128)S(1)} %copy.122), channel_id=1, source_target_pairs={{8,0},{12,4},{16,8},{20,12},{24,16},{28,20},{32,24},{36,28},{40,32... | collective-permute-start | bytes 786440 | tf_op jit(solution)/shard_map/ppermute | solution.py:20
  116.8 8.7 %collective-permute-start.8 = (f32[256,256]{1,0:T(8,128)S(1)}, f32[256,256]{1,0:T(8,128)S(1)}, u32[]{:S(2)}, u32[]{:S(2)}) collective-permute-start(f32[256,256]{1,0:T(8,128)S(1)} %copy.128), channel_id=1, source_target_pairs={{56,0},{60,4},{0,8},{4,12},{8,16},{12,20},{16,24},{20,28},{24,32},... | collective-permute-start | bytes 786440 | tf_op jit(solution)/shard_map/ppermute | solution.py:20
  125.6 8.9 %collective-permute-start.10 = (f32[256,256]{1,0:T(8,128)S(1)}, f32[256,256]{1,0:T(8,128)S(1)}, u32[]{:S(2)}, u32[]{:S(2)}) collective-permute-start(f32[256,256]{1,0:T(8,128)S(1)} %get-tuple-element.612), channel_id=1, source_target_pairs={{0,12},{4,56},{8,20},{12,0},{16,28},{20,8},{24,36},{28,16},{32,44}... | collective-permute-start | bytes 786440 | tf_op jit(solution)/shard_map/ppermute | solution.py:31
  125.7 8.8 %collective-permute-start.9 = (f32[256,256]{1,0:T(8,128)S(1)}, f32[256,256]{1,0:T(8,128)S(1)}, u32[]{:S(2)}, u32[]{:S(2)}) collective-permute-start(f32[256,256]{1,0:T(8,128)S(1)} %get-tuple-element.613), channel_id=1, source_target_pairs={{0,56},{4,12},{8,0},{12,20},{16,8},{20,28},{24,16},{28,36},{32,24}... | collective-permute-start | bytes 786440 | tf_op jit(solution)/shard_map/ppermute | solution.py:31

commit v17 on v15

--- a/solution.py
+++ b/solution.py
@@ -49,8 +49,7 @@
         query_blocks = query_start // BLK + jnp.arange(row_count, dtype=jnp.int32)
         key_blocks = key_pos[::BLK] // BLK
         block_live = (key_blocks[None, :] < query_blocks[:, None]) & (block_table == 1)
-        block_live = lax.optimization_barrier(block_live)
-        return jnp.repeat(jnp.repeat(block_live, BLK, axis=0), BLK, axis=1)
+        return block_live
     block_table = jnp.repeat(jnp.repeat(block_table, BLK, axis=0), BLK, axis=1)
     query_pos = query_start + jnp.arange(tok_rows, dtype=jnp.int32)
     query_block = (query_pos // BLK)[:, None]
@@ -103,14 +102,29 @@
     super_rows = Y_HI * tok_rows
     offsets = jnp.arange(tok_rows, dtype=jnp.int32)
 
+    def turn_table(turn):
+        ahead_owner = (z_pos + turn) % z_count
+        behind_owner = (z_pos - turn) % z_count
+        key_starts = (ahead_owner * super_rows, behind_owner * super_rows + tok_rows)
+        key_pos = jnp.concatenate([key_starts[0] + offsets, key_starts[1] + offsets])
+        return live_region(block_mask, query_start, tok_rows, key_pos, key_starts, False)
+
+    turn_ids = jnp.arange(z_count, dtype=jnp.int32)
+    all_tables = jax.vmap(turn_table)(turn_ids)
+
     def terms(ahead_kv, behind_kv, turn, with_diagonal=False):
         ahead_owner = (z_pos + turn) % z_count
         behind_owner = (z_pos - turn) % z_count
         key_starts = (ahead_owner * super_rows, behind_owner * super_rows + tok_rows)
         key_pos = jnp.concatenate([key_starts[0] + offsets, key_starts[1] + offsets])
-        live_mask = live_region(block_mask, query_start, tok_rows, key_pos, key_starts, with_diagonal)
         if with_diagonal:
-            live_mask = lax.optimization_barrier(live_mask)
+            live_mask = lax.optimization_barrier(
+                live_region(block_mask, query_start, tok_rows, key_pos, key_starts, True)
+            )
+        else:
+            chosen = (turn_ids == turn)[:, None, None] & all_tables
+            block_live = lax.optimization_barrier(jnp.any(chosen, axis=0))
+            live_mask = jnp.repeat(jnp.repeat(block_live, BLK, axis=0), BLK, axis=1)
         key_values = jnp.concatenate([ahead_kv, behind_kv], axis=0)
         query_term, key_term, value_term = contract(
             queries,

time: 134 us -> 181 us (1.35)
  local copies, waits for them, and re-layouts: 18 us -> 55.9 us
  waiting for transfers between devices: 9.49 us -> 18.6 us
    gather x0 -> x50, local copies, waits for them, and re-layouts: none -> 43 us
    ppermute x28, waiting for transfers between devices: 4.66 us -> 12.8 us  [along_z(): return lax.ppermute(value, 'ctx', pairs)]
    dynamic_slice x7 -> x1, local copies, waits for them, and re-layouts: 6.09 us -> 0.86 us  [live_region(): lax.dynamic_slice(block_mask, (query_start // BLK, start // BLK), (row_co...]
    unnamed x16 -> x19, local copies, waits for them, and re-layouts: 3.84 us -> 3.96 us
  transfers between devices with their start and end apart: 32 -> 32, of which waited for: 3 -> 8; matrix products, arithmetic and copies ran while one was open for 46% -> 55% of each run, Pallas kernels for 0% -> 0%
where the time goes in v17:
time: 181 us; the launch traced here: 179 us
  local copies, waits for them, and re-layouts  55.9 us (31%)
  starting transfers between devices  49.9 us (28%)
  matrix products  43.5 us (24%)
  waiting for transfers between devices  18.6 us (10%)
  other arithmetic  8.87 us (5%)
    gather x48, local copies, waits for them, and re-layouts  42.8 us
    ppermute x28, starting transfers between devices, along_z(): return lax.ppermute(value, 'ctx', pairs)  41.2 us
    ppermute x28, waiting for transfers between devices, along_z(): return lax.ppermute(value, 'ctx', pairs)  12.8 us
    dot_general x8, matrix products, contract(): jnp.einsum('igd,jd->gij', out_grads, values_part, preferred_element_type=...  12.4 us
    dot_general x8, matrix products, contract(): jnp.einsum('gij,igd->jd', probabilities.astype(jnp.bfloat16), out_grads,...  10.3 us
    dot_general x8, matrix products, contract(): jnp.einsum('gij,igd->jd', dscore, queries, preferred_element_type=jnp.flo...  7.89 us
    dot_general x8, matrix products, contract(): jnp.einsum('igd,jd->gij', queries, keys_part, preferred_element_type=jnp....  7.47 us
    ppermute x2, waiting for transfers between devices, to_owner(): return lax.ppermute(value, 'ctx', pairs)  5.79 us
  transfers between devices with their start and end apart: 32, of which 8 were waited for; matrix products, arithmetic and copies ran while one was open for 55% of the time, Pallas kernels for 0%

profile of v17, /device:TPU:4, one launch (start us, length us, event | category | flops | bytes accessed | tf_op | source)
XLA Modules:
  0.0 178.6 jit_solution(15960412131863319202)
XLA Ops:
  2.4 3.3 %collective-permute-start.4 = (bf16[256,256]{1,0:T(8,128)(2,1)S(1)}, bf16[256,256]{1,0:T(8,128)(2,1)S(1)}, u32[]{:S(2)}, u32[]{:S(2)}) collective-permute-start(bf16[256,256]{1,0:T(8,128)(2,1)S(1)} %constant_dynamic-update-slice_fusion.2), channel_id=1, source_target_pairs={{0,4},{4,0},{8,12},{12,8},{16,20},{20,16},{24,28},{28,24},{32,36},... | collective-permute-start | bytes 393224 | tf_op jit(solution)/shard_map/ppermute | solution.py:36
  5.7 1.9 %copy.203 = bf16[8,4,8,1024]{3,2,0,1:T(8,128)(2,1)} copy(bf16[8,4,8,1024]{3,2,1,0:T(8,128)(2,1)} %bitcast.212) | data formatting | bytes 1048576 | tf_op jit(solution)/shard_map/reshape | solution.py:92
  7.6 3.5 %all-to-all-start = ((bf16[64,4,1024]{2,0,1:T(8,128)(2,1)}), bf16[64,4,1024]{2,0,1:T(8,128)(2,1)S(1)}, u32[]{:S(2)}, u32[]{:S(2)}) async-start(bf16[64,4,1024]{2,0,1:T(8,128)(2,1)} %bitcast.153), calls=%async_computation | async-start | bytes 1048576 | tf_op jit(solution)/shard_map/all_to_all | solution.py:93
  12.7 21.4 %while.25 = (s32[]{:T(128)}, s32[32,32]{1,0:T(8,128)}, s32[8,2]{0,1:T(2,128)S(1)}, s32[8,2,2]{2,1,0:T(2,128)S(1)}, s32[]{:T(128)}) while((s32[]{:T(128)}, s32[32,32]{1,0:T(8,128)}, s32[8,2]{0,1:T(2,128)S(1)}, s32[8,2,2]{2,1,0:T(2,128)S(1)}, s32[]{:T(128)}) %tuple.86), condition=%wide.while_cond.1, body=%wide.while_body.1.sunk | while | flops 2 | bytes 1157 | solution.py:43
  13.3 2.0 %bitcast_dynamic-update-slice_fusion.5 = s32[8,2,2]{2,1,0:T(2,128)S(1)} fusion(s32[8,2,2]{2,1,0:T(2,128)S(1)} %get-tuple-element.522, s32[]{:T(128)S(6)} %copy.210, s32[32,32]{1,0:T(8,128)} %get-tuple-element.525, s32[]{:T(128)} %bitcast.181, s32[]{:T(128)} %bitcast.182), kind=kLoop, calls=%fused_computation.3.clone.1 | loop fusion | bytes 1052 | tf_op jit(solution)/shard_map/vmap()/gather
  16.0 2.0 %bitcast_dynamic-update-slice_fusion.5 = s32[8,2,2]{2,1,0:T(2,128)S(1)} fusion(s32[8,2,2]{2,1,0:T(2,128)S(1)} %get-tuple-element.522, s32[]{:T(128)S(6)} %copy.210, s32[32,32]{1,0:T(8,128)} %get-tuple-element.525, s32[]{:T(128)} %bitcast.181, s32[]{:T(128)} %bitcast.182), kind=kLoop, calls=%fused_computation.3.clone.1 | loop fusion | bytes 1052 | tf_op jit(solution)/shard_map/vmap()/gather
  18.7 2.0 %bitcast_dynamic-update-slice_fusion.5 = s32[8,2,2]{2,1,0:T(2,128)S(1)} fusion(s32[8,2,2]{2,1,0:T(2,128)S(1)} %get-tuple-element.522, s32[]{:T(128)S(6)} %copy.210, s32[32,32]{1,0:T(8,128)} %get-tuple-element.525, s32[]{:T(128)} %bitcast.181, s32[]{:T(128)} %bitcast.182), kind=kLoop, calls=%fused_computation.3.clone.1 | loop fusion | bytes 1052 | tf_op jit(solution)/shard_map/vmap()/gather
  21.3 2.0 %bitcast_dynamic-update-slice_fusion.5 = s32[8,2,2]{2,1,0:T(2,128)S(1)} fusion(s32[8,2,2]{2,1,0:T(2,128)S(1)} %get-tuple-element.522, s32[]{:T(128)S(6)} %copy.210, s32[32,32]{1,0:T(8,128)} %get-tuple-element.525, s32[]{:T(128)} %bitcast.181, s32[]{:T(128)} %bitcast.182), kind=kLoop, calls=%fused_computation.3.clone.1 | loop fusion | bytes 1052 | tf_op jit(solution)/shard_map/vmap()/gather
  24.0 2.0 %bitcast_dynamic-update-slice_fusion.5 = s32[8,2,2]{2,1,0:T(2,128)S(1)} fusion(s32[8,2,2]{2,1,0:T(2,128)S(1)} %get-tuple-element.522, s32[]{:T(128)S(6)} %copy.210, s32[32,32]{1,0:T(8,128)} %get-tuple-element.525, s32[]{:T(128)} %bitcast.181, s32[]{:T(128)} %bitcast.182), kind=kLoop, calls=%fused_computation.3.clone.1 | loop fusion | bytes 1052 | tf_op jit(solution)/shard_map/vmap()/gather
  26.7 2.0 %bitcast_dynamic-update-slice_fusion.5 = s32[8,2,2]{2,1,0:T(2,128)S(1)} fusion(s32[8,2,2]{2,1,0:T(2,128)S(1)} %get-tuple-element.522, s32[]{:T(128)S(6)} %copy.210, s32[32,32]{1,0:T(8,128)} %get-tuple-element.525, s32[]{:T(128)} %bitcast.181, s32[]{:T(128)} %bitcast.182), kind=kLoop, calls=%fused_computation.3.clone.1 | loop fusion | bytes 1052 | tf_op jit(solution)/shard_map/vmap()/gather
  29.4 2.0 %bitcast_dynamic-update-slice_fusion.5 = s32[8,2,2]{2,1,0:T(2,128)S(1)} fusion(s32[8,2,2]{2,1,0:T(2,128)S(1)} %get-tuple-element.522, s32[]{:T(128)S(6)} %copy.210, s32[32,32]{1,0:T(8,128)} %get-tuple-element.525, s32[]{:T(128)} %bitcast.181, s32[]{:T(128)} %bitcast.182), kind=kLoop, calls=%fused_computation.3.clone.1 | loop fusion | bytes 1052 | tf_op jit(solution)/shard_map/vmap()/gather
  32.1 2.0 %bitcast_dynamic-update-slice_fusion.5 = s32[8,2,2]{2,1,0:T(2,128)S(1)} fusion(s32[8,2,2]{2,1,0:T(2,128)S(1)} %get-tuple-element.522, s32[]{:T(128)S(6)} %copy.210, s32[32,32]{1,0:T(8,128)} %get-tuple-element.525, s32[]{:T(128)} %bitcast.181, s32[]{:T(128)} %bitcast.182), kind=kLoop, calls=%fused_computation.3.clone.1 | loop fusion | bytes 1052 | tf_op jit(solution)/shard_map/vmap()/gather
  34.2 21.4 %while.24 = (s32[]{:T(128)}, s32[32,32]{1,0:T(8,128)}, s32[8,2]{0,1:T(2,128)S(1)}, s32[8,2,2]{2,1,0:T(2,128)S(1)}, s32[]{:T(128)}) while((s32[]{:T(128)}, s32[32,32]{1,0:T(8,128)}, s32[8,2]{0,1:T(2,128)S(1)}, s32[8,2,2]{2,1,0:T(2,128)S(1)}, s32[]{:T(128)}) %tuple.97), condition=%wide.while_cond, body=%wide.while_body.sunk | while | flops 2 | bytes 1157 | solution.py:43
  34.8 2.0 %bitcast_dynamic-update-slice_fusion.4 = s32[8,2,2]{2,1,0:T(2,128)S(1)} fusion(s32[8,2,2]{2,1,0:T(2,128)S(1)} %get-tuple-element.537, s32[]{:T(128)S(6)} %copy.216, s32[32,32]{1,0:T(8,128)} %get-tuple-element.540, s32[]{:T(128)} %bitcast.178, s32[]{:T(128)} %bitcast.179), kind=kLoop, calls=%fused_computation.1.clone.1 | loop fusion | bytes 1052 | tf_op jit(solution)/shard_map/vmap()/gather
  37.5 2.0 %bitcast_dynamic-update-slice_fusion.4 = s32[8,2,2]{2,1,0:T(2,128)S(1)} fusion(s32[8,2,2]{2,1,0:T(2,128)S(1)} %get-tuple-element.537, s32[]{:T(128)S(6)} %copy.216, s32[32,32]{1,0:T(8,128)} %get-tuple-element.540, s32[]{:T(128)} %bitcast.178, s32[]{:T(128)} %bitcast.179), kind=kLoop, calls=%fused_computation.1.clone.1 | loop fusion | bytes 1052 | tf_op jit(solution)/shard_map/vmap()/gather
  40.2 2.0 %bitcast_dynamic-update-slice_fusion.4 = s32[8,2,2]{2,1,0:T(2,128)S(1)} fusion(s32[8,2,2]{2,1,0:T(2,128)S(1)} %get-tuple-element.537, s32[]{:T(128)S(6)} %copy.216, s32[32,32]{1,0:T(8,128)} %get-tuple-element.540, s32[]{:T(128)} %bitcast.178, s32[]{:T(128)} %bitcast.179), kind=kLoop, calls=%fused_computation.1.clone.1 | loop fusion | bytes 1052 | tf_op jit(solution)/shard_map/vmap()/gather
  42.9 2.0 %bitcast_dynamic-update-slice_fusion.4 = s32[8,2,2]{2,1,0:T(2,128)S(1)} fusion(s32[8,2,2]{2,1,0:T(2,128)S(1)} %get-tuple-element.537, s32[]{:T(128)S(6)} %copy.216, s32[32,32]{1,0:T(8,128)} %get-tuple-element.540, s32[]{:T(128)} %bitcast.178, s32[]{:T(128)} %bitcast.179), kind=kLoop, calls=%fused_computation.1.clone.1 | loop fusion | bytes 1052 | tf_op jit(solution)/shard_map/vmap()/gather
  45.5 2.0 %bitcast_dynamic-update-slice_fusion.4 = s32[8,2,2]{2,1,0:T(2,128)S(1)} fusion(s32[8,2,2]{2,1,0:T(2,128)S(1)} %get-tuple-element.537, s32[]{:T(128)S(6)} %copy.216, s32[32,32]{1,0:T(8,128)} %get-tuple-element.540, s32[]{:T(128)} %bitcast.178, s32[]{:T(128)} %bitcast.179), kind=kLoop, calls=%fused_computation.1.clone.1 | loop fusion | bytes 1052 | tf_op jit(solution)/shard_map/vmap()/gather
  48.2 2.0 %bitcast_dynamic-update-slice_fusion.4 = s32[8,2,2]{2,1,0:T(2,128)S(1)} fusion(s32[8,2,2]{2,1,0:T(2,128)S(1)} %get-tuple-element.537, s32[]{:T(128)S(6)} %copy.216, s32[32,32]{1,0:T(8,128)} %get-tuple-element.540, s32[]{:T(128)} %bitcast.178, s32[]{:T(128)} %bitcast.179), kind=kLoop, calls=%fused_computation.1.clone.1 | loop fusion | bytes 1052 | tf_op jit(solution)/shard_map/vmap()/gather
  50.9 2.0 %bitcast_dynamic-update-slice_fusion.4 = s32[8,2,2]{2,1,0:T(2,128)S(1)} fusion(s32[8,2,2]{2,1,0:T(2,128)S(1)} %get-tuple-element.537, s32[]{:T(128)S(6)} %copy.216, s32[32,32]{1,0:T(8,128)} %get-tuple-element.540, s32[]{:T(128)} %bitcast.178, s32[]{:T(128)} %bitcast.179), kind=kLoop, calls=%fused_computation.1.clone.1 | loop fusion | bytes 1052 | tf_op jit(solution)/shard_map/vmap()/gather
  53.6 2.0 %bitcast_dynamic-update-slice_fusion.4 = s32[8,2,2]{2,1,0:T(2,128)S(1)} fusion(s32[8,2,2]{2,1,0:T(2,128)S(1)} %get-tuple-element.537, s32[]{:T(128)S(6)} %copy.216, s32[32,32]{1,0:T(8,128)} %get-tuple-element.540, s32[]{:T(128)} %bitcast.178, s32[]{:T(128)} %bitcast.179), kind=kLoop, calls=%fused_computation.1.clone.1 | loop fusion | bytes 1052 | tf_op jit(solution)/shard_map/vmap()/gather
  56.3 1.2 copy.143
  58.2 2.0 %collective-permute-start.6 = (bf16[256,256]{1,0:T(8,128)(2,1)S(1)}, bf16[256,256]{1,0:T(8,128)(2,1)S(1)}, u32[]{:S(2)}, u32[]{:S(2)}) collective-permute-start(bf16[256,256]{1,0:T(8,128)(2,1)S(1)} %get-tuple-element.371), channel_id=1, source_target_pairs={{56,0},{60,4},{0,8},{4,12},{8,16},{12,20},{16,24},{20,28},{24,32},... | collective-permute-start | bytes 393224 | tf_op jit(solution)/shard_map/ppermute | solution.py:20
  60.2 3.9 %collective-permute-start.5 = (bf16[256,256]{1,0:T(8,128)(2,1)S(1)}, bf16[256,256]{1,0:T(8,128)(2,1)S(1)}, u32[]{:S(2)}, u32[]{:S(2)}) collective-permute-start(bf16[256,256]{1,0:T(8,128)(2,1)S(1)} %get-tuple-element.372), channel_id=1, source_target_pairs={{8,0},{12,4},{16,8},{20,12},{24,16},{28,20},{32,24},{36,28},{40,32... | collective-permute-start | bytes 393224 | tf_op jit(solution)/shard_map/ppermute | solution.py:20
  64.0 2.6 %fusion.56 = f32[512,256,8]{1,0,2:T(8,128)} fusion(bf16[256,8,128]{0,2,1:T(8,128)(2,1)S(1)} %bitcast.200, bf16[256,256]{1,0:T(8,128)(2,1)S(1)} %get-tuple-element.372, bf16[256,256]{1,0:T(8,128)(2,1)S(1)} %get-tuple-element.371), kind=kOutput, calls=%fused_computation.92 | convolution fusion | flops 268697600 | bytes 4980736 | tf_op jit(solution)/shard_map/igd,jd->gij/dot_general | solution.py:65
  67.5 3.3 %fusion.36 = f32[512,128]{0,1:T(8,128)S(1)} fusion(bf16[256,8,128]{0,2,1:T(8,128)(2,1)S(1)} %copy.154, f32[512,256,8]{1,0,2:T(8,128)} %fusion.56, f32[8,256]{1,0:T(8,128)S(1)} %copy-done.5, pred[256,512]{0,1:T(8,128)(4,1)S(1)} %fusion.42), kind=kOutput, calls=%fused_computation.54 | convolution fusion | flops 272629760 | bytes 5120000 | tf_op jit(solution)/shard_map/gij,igd->jd/dot_general | solution.py:75
  71.0 1.4 fusion.25
  74.5 76.0 %while.26 = (s32[]{:T(128)}, bf16[256,256]{1,0:T(8,128)(2,1)S(1)}, bf16[256,256]{1,0:T(8,128)(2,1)S(1)}, f32[256,8,128]{0,2,1:T(8,128)S(1)}, f32[256,256]{0,1:T(...) while((s32[]{:T(128)}, bf16[256,256]{1,0:T(8,128)(2,1)S(1)}, ...), condition=%wide.region_3.4_spmd.clone, body=%wide.region_1.3_spmd.clone.sunk | while | flops 1353187456 | bytes 32270740 | solution.py:164
  74.7 2.0 %collective-permute-start = (bf16[256,256]{1,0:T(8,128)(2,1)S(1)}, bf16[256,256]{1,0:T(8,128)(2,1)S(1)}, u32[]{:S(2)}, u32[]{:S(2)}) collective-permute-start(bf16[256,256]{1,0:T(8,128)(2,1)S(1)} %copy.227), channel_id=1, source_target_pairs={{8,0},{12,4},{16,8},{20,12},{24,16},{28,20},{32,24},{36,28},{40,32... | collective-permute-start | bytes 393224 | tf_op jit(solution)/shard_map/while/body/eval_jaxpr/ppermute | solution.py:20
  77.0 3.1 %collective-permute-start.3 = (f32[256,256]{0,1:T(8,128)}, f32[256,256]{0,1:T(8,128)S(1)}, u32[]{:S(2)}, u32[]{:S(2)}) collective-permute-start(f32[256,256]{0,1:T(8,128)} %get-tuple-element.560), channel_id=1, source_target_pairs={{8,0},{12,4},{16,8},{20,12},{24,16},{28,20},{32,24},{36,28},{40,32... | collective-permute-start | bytes 786440 | tf_op jit(solution)/shard_map/while/body/eval_jaxpr/ppermute | solution.py:20
  81.2 1.0 fusion.125
  82.2 1.4 fusion.123
  84.9 3.7 %collective-permute-done.2 = f32[256,256]{0,1:T(8,128)S(1)} collective-permute-done((f32[256,256]{0,1:T(8,128)}, f32[256,256]{0,1:T(8,128)S(1)}, u32[]{:S(2)}, u32[]{:S(2)}) %collective-permute-start.2) | collective-permute-done | bytes 262176 | tf_op jit(solution)/shard_map/while/body/eval_jaxpr/ppermute | solution.py:20
  90.1 1.7 collective-permute-start.1
  91.8 3.1 %collective-permute-start.3 = (f32[256,256]{0,1:T(8,128)}, f32[256,256]{0,1:T(8,128)S(1)}, u32[]{:S(2)}, u32[]{:S(2)}) collective-permute-start(f32[256,256]{0,1:T(8,128)} %get-tuple-element.560), channel_id=1, source_target_pairs={{8,0},{12,4},{16,8},{20,12},{24,16},{28,20},{32,24},{36,28},{40,32... | collective-permute-start | bytes 786440 | tf_op jit(solution)/shard_map/while/body/eval_jaxpr/ppermute | solution.py:20
  96.0 1.0 fusion.125
  97.1 1.4 fusion.123
  99.8 1.1 collective-permute-done.2
  101.8 1.9 %collective-permute-start = (bf16[256,256]{1,0:T(8,128)(2,1)S(1)}, bf16[256,256]{1,0:T(8,128)(2,1)S(1)}, u32[]{:S(2)}, u32[]{:S(2)}) collective-permute-start(bf16[256,256]{1,0:T(8,128)(2,1)S(1)} %copy.227), channel_id=1, source_target_pairs={{8,0},{12,4},{16,8},{20,12},{24,16},{28,20},{32,24},{36,28},{40,32... | collective-permute-start | bytes 393224 | tf_op jit(solution)/shard_map/while/body/eval_jaxpr/ppermute | solution.py:20
  104.3 3.0 %collective-permute-start.3 = (f32[256,256]{0,1:T(8,128)}, f32[256,256]{0,1:T(8,128)S(1)}, u32[]{:S(2)}, u32[]{:S(2)}) collective-permute-start(f32[256,256]{0,1:T(8,128)} %get-tuple-element.560), channel_id=1, source_target_pairs={{8,0},{12,4},{16,8},{20,12},{24,16},{28,20},{32,24},{36,28},{40,32... | collective-permute-start | bytes 786440 | tf_op jit(solution)/shard_map/while/body/eval_jaxpr/ppermute | solution.py:20
  108.3 1.0 fusion.125
  109.4 1.4 fusion.123
  113.8 2.3 %collective-permute-start = (bf16[256,256]{1,0:T(8,128)(2,1)S(1)}, bf16[256,256]{1,0:T(8,128)(2,1)S(1)}, u32[]{:S(2)}, u32[]{:S(2)}) collective-permute-start(bf16[256,256]{1,0:T(8,128)(2,1)S(1)} %copy.227), channel_id=1, source_target_pairs={{8,0},{12,4},{16,8},{20,12},{24,16},{28,20},{32,24},{36,28},{40,32... | collective-permute-start | bytes 393224 | tf_op jit(solution)/shard_map/while/body/eval_jaxpr/ppermute | solution.py:20
  116.7 2.8 %collective-permute-start.3 = (f32[256,256]{0,1:T(8,128)}, f32[256,256]{0,1:T(8,128)S(1)}, u32[]{:S(2)}, u32[]{:S(2)}) collective-permute-start(f32[256,256]{0,1:T(8,128)} %get-tuple-element.560), channel_id=1, source_target_pairs={{8,0},{12,4},{16,8},{20,12},{24,16},{28,20},{32,24},{36,28},{40,32... | collective-permute-start | bytes 786440 | tf_op jit(solution)/shard_map/while/body/eval_jaxpr/ppermute | solution.py:20
  120.6 1.0 fusion.125
  121.6 1.4 fusion.123
  126.1 2.2 %collective-permute-start = (bf16[256,256]{1,0:T(8,128)(2,1)S(1)}, bf16[256,256]{1,0:T(8,128)(2,1)S(1)}, u32[]{:S(2)}, u32[]{:S(2)}) collective-permute-start(bf16[256,256]{1,0:T(8,128)(2,1)S(1)} %copy.227), channel_id=1, source_target_pairs={{8,0},{12,4},{16,8},{20,12},{24,16},{28,20},{32,24},{36,28},{40,32... | collective-permute-start | bytes 393224 | tf_op jit(solution)/shard_map/while/body/eval_jaxpr/ppermute | solution.py:20
  129.3 2.4 %collective-permute-start.3 = (f32[256,256]{0,1:T(8,128)}, f32[256,256]{0,1:T(8,128)S(1)}, u32[]{:S(2)}, u32[]{:S(2)}) collective-permute-start(f32[256,256]{0,1:T(8,128)} %get-tuple-element.560), channel_id=1, source_target_pairs={{8,0},{12,4},{16,8},{20,12},{24,16},{28,20},{32,24},{36,28},{40,32... | collective-permute-start | bytes 786440 | tf_op jit(solution)/shard_map/while/body/eval_jaxpr/ppermute | solution.py:20
  132.8 1.0 fusion.125
  133.8 1.4 fusion.123
  138.3 2.2 %collective-permute-start = (bf16[256,256]{1,0:T(8,128)(2,1)S(1)}, bf16[256,256]{1,0:T(8,128)(2,1)S(1)}, u32[]{:S(2)}, u32[]{:S(2)}) collective-permute-start(bf16[256,256]{1,0:T(8,128)(2,1)S(1)} %copy.227), channel_id=1, source_target_pairs={{8,0},{12,4},{16,8},{20,12},{24,16},{28,20},{32,24},{36,28},{40,32... | collective-permute-start | bytes 393224 | tf_op jit(solution)/shard_map/while/body/eval_jaxpr/ppermute | solution.py:20
  141.6 2.4 %collective-permute-start.3 = (f32[256,256]{0,1:T(8,128)}, f32[256,256]{0,1:T(8,128)S(1)}, u32[]{:S(2)}, u32[]{:S(2)}) collective-permute-start(f32[256,256]{0,1:T(8,128)} %get-tuple-element.560), channel_id=1, source_target_pairs={{8,0},{12,4},{16,8},{20,12},{24,16},{28,20},{32,24},{36,28},{40,32... | collective-permute-start | bytes 786440 | tf_op jit(solution)/shard_map/while/body/eval_jaxpr/ppermute | solution.py:20
  145.0 1.0 fusion.125
  146.0 1.4 fusion.123
  152.4 2.7 %fusion.21 = bf16[8,256,512]{1,2,0:T(8,128)(2,1)} fusion(f32[512,256,8]{1,0,2:T(8,128)S(1)} %fusion.55, f32[8,256]{1,0:T(8,128)S(1)} %get-tuple-element.604, f32[8,256]{1,0:T(8,128)S(1)} %get-tuple-element.605, pred[256,512]{0,1:T(8,128)(4,1)S(1)} %bitcast.215, bf16[256,8,128]{2,1,0:T(8,128)(2,1)S(1)} %bitcast.206, ...), kind=kOutput, calls=%fused_computation.36 | convolution fusion | flops 274726912 | bytes 7094272 | tf_op jit(solution)/shard_map/igd,jd->gij/dot_general | solution.py:69
  155.2 1.1 copy.171
  156.3 1.1 copy.165
  157.4 2.2 %collective-permute-start.7 = (f32[256,256]{1,0:T(8,128)S(1)}, f32[256,256]{1,0:T(8,128)S(1)}, u32[]{:S(2)}, u32[]{:S(2)}) collective-permute-start(f32[256,256]{1,0:T(8,128)S(1)} %copy.165), channel_id=1, source_target_pairs={{8,0},{12,4},{16,8},{20,12},{24,16},{28,20},{32,24},{36,28},{40,32... | collective-permute-start | bytes 786440 | tf_op jit(solution)/shard_map/ppermute | solution.py:20
  159.6 2.1 %convolution_bitcast_fusion.2 = f32[256,8,128]{0,2,1:T(8,128)S(1)} fusion(bf16[8,256,512]{1,2,0:T(8,128)(2,1)} %fusion.21, bf16[512,256]{1,0:T(8,128)(2,1)S(1)} %constant_dynamic-update-slice_fusion.4), kind=kOutput, calls=%fused_computation.52 | convolution fusion | flops 268435456 | bytes 3276800 | tf_op jit(solution)/shard_map/gij,jd->igd/dot_general | solution.py:73
  161.6 2.3 %convolution_bitcast_fusion.4 = f32[512,128]{1,0:T(8,128)S(1)} fusion(bf16[8,256,512]{1,2,0:T(8,128)(2,1)} %fusion.21, bf16[256,8,128]{0,2,1:T(8,128)(2,1)S(1)} %get-tuple-element.580), kind=kOutput, calls=%fused_computation.56 | convolution fusion | flops 268435456 | bytes 2883584 | tf_op jit(solution)/shard_map/gij,igd->jd/dot_general | solution.py:74
  163.9 4.4 %collective-permute-done.8 = f32[256,256]{1,0:T(8,128)S(1)} collective-permute-done((f32[256,256]{1,0:T(8,128)S(1)}, f32[256,256]{1,0:T(8,128)S(1)}, u32[]{:S(2)}, u32[]{:S(2)}) %collective-permute-start.8) | collective-permute-done | bytes 262176 | tf_op jit(solution)/shard_map/ppermute | solution.py:20
  168.5 1.8 %collective-permute-start.9 = (f32[256,256]{1,0:T(8,128)S(1)}, f32[256,256]{1,0:T(8,128)S(1)}, u32[]{:S(2)}, u32[]{:S(2)}) collective-permute-start(f32[256,256]{1,0:T(8,128)S(1)} %get-tuple-element.368), channel_id=1, source_target_pairs={{0,56},{4,12},{8,0},{12,20},{16,8},{20,28},{24,16},{28,36},{32,24}... | collective-permute-start | bytes 786440 | tf_op jit(solution)/shard_map/ppermute | solution.py:31
  170.5 1.0 copy.172
  171.5 5.8 %collective-permute-done.10 = f32[256,256]{1,0:T(8,128)S(1)} collective-permute-done((f32[256,256]{1,0:T(8,128)S(1)}, f32[256,256]{1,0:T(8,128)S(1)}, u32[]{:S(2)}, u32[]{:S(2)}) %collective-permute-start.10) | collective-permute-done | bytes 262176 | tf_op jit(solution)/shard_map/ppermute | solution.py:31
  (216 shorter events, 48.4 us)
Async XLA Ops:
  0.6 56.9 %copy-start.1 = (bf16[256,1024]{1,0:T(8,128)(2,1)S(1)}, bf16[256,1024]{1,0:T(8,128)(2,1)}, u32[]{:S(2)}) copy-start(bf16[256,1024]{1,0:T(8,128)(2,1)} %param.12) | copy-start | bytes 1572868
  2.4 55.7 %collective-permute-start.4 = (bf16[256,256]{1,0:T(8,128)(2,1)S(1)}, bf16[256,256]{1,0:T(8,128)(2,1)S(1)}, u32[]{:S(2)}, u32[]{:S(2)}) collective-permute-start(bf16[256,256]{1,0:T(8,128)(2,1)S(1)} %constant_dynamic-update-slice_fusion.2), channel_id=1, source_target_pairs={{0,4},{4,0},{8,12},{12,8},{16,20},{20,16},{24,28},{28,24},{32,36},... | collective-permute-start | bytes 393224 | tf_op jit(solution)/shard_map/ppermute | solution.py:36
  7.6 59.1 %all-to-all-start = ((bf16[64,4,1024]{2,0,1:T(8,128)(2,1)}), bf16[64,4,1024]{2,0,1:T(8,128)(2,1)S(1)}, u32[]{:S(2)}, u32[]{:S(2)}) async-start(bf16[64,4,1024]{2,0,1:T(8,128)(2,1)} %bitcast.153), calls=%async_computation | async-start | bytes 1048576 | tf_op jit(solution)/shard_map/all_to_all | solution.py:93
  58.2 16.4 %collective-permute-start.6 = (bf16[256,256]{1,0:T(8,128)(2,1)S(1)}, bf16[256,256]{1,0:T(8,128)(2,1)S(1)}, u32[]{:S(2)}, u32[]{:S(2)}) collective-permute-start(bf16[256,256]{1,0:T(8,128)(2,1)S(1)} %get-tuple-element.371), channel_id=1, source_target_pairs={{56,0},{60,4},{0,8},{4,12},{8,16},{12,20},{16,24},{20,28},{24,32},... | collective-permute-start | bytes 393224 | tf_op jit(solution)/shard_map/ppermute | solution.py:20
  60.2 14.4 %collective-permute-start.5 = (bf16[256,256]{1,0:T(8,128)(2,1)S(1)}, bf16[256,256]{1,0:T(8,128)(2,1)S(1)}, u32[]{:S(2)}, u32[]{:S(2)}) collective-permute-start(bf16[256,256]{1,0:T(8,128)(2,1)S(1)} %get-tuple-element.372), channel_id=1, source_target_pairs={{8,0},{12,4},{16,8},{20,12},{24,16},{28,20},{32,24},{36,28},{40,32... | collective-permute-start | bytes 393224 | tf_op jit(solution)/shard_map/ppermute | solution.py:20
  64.0 3.5 %copy-start.5 = (f32[8,256]{1,0:T(8,128)S(1)}, f32[8,256]{1,0:T(8,128)}, u32[]{:S(2)}) copy-start(f32[8,256]{1,0:T(8,128)} %param.14) | copy-start | bytes 24580
  67.1 5.3 %copy-start.2 = (bf16[256,8,128]{0,2,1:T(8,128)(2,1)}, bf16[256,8,128]{0,2,1:T(8,128)(2,1)S(1)}, u32[]{:S(2)}) copy-start(bf16[256,8,128]{0,2,1:T(8,128)(2,1)S(1)} %copy.154) | copy-start | bytes 1572868
  67.5 3.5 %copy-start = (f32[512,256,8]{1,0,2:T(8,128)S(1)}, f32[512,256,8]{1,0,2:T(8,128)}, u32[]{:S(2)}) copy-start(f32[512,256,8]{1,0,2:T(8,128)} %fusion.56) | copy-start | bytes 12582916
  74.7 14.8 %collective-permute-start = (bf16[256,256]{1,0:T(8,128)(2,1)S(1)}, bf16[256,256]{1,0:T(8,128)(2,1)S(1)}, u32[]{:S(2)}, u32[]{:S(2)}) collective-permute-start(bf16[256,256]{1,0:T(8,128)(2,1)S(1)} %copy.227), channel_id=1, source_target_pairs={{8,0},{12,4},{16,8},{20,12},{24,16},{28,20},{32,24},{36,28},{40,32... | collective-permute-start | bytes 393224 | tf_op jit(solution)/shard_map/while/body/eval_jaxpr/ppermute | solution.py:20
  76.7 12.8 %collective-permute-start.1 = (bf16[256,256]{1,0:T(8,128)(2,1)S(1)}, bf16[256,256]{1,0:T(8,128)(2,1)S(1)}, u32[]{:S(2)}, u32[]{:S(2)}) collective-permute-start(bf16[256,256]{1,0:T(8,128)(2,1)S(1)} %copy.228), channel_id=1, source_target_pairs={{56,0},{60,4},{0,8},{4,12},{8,16},{12,20},{16,24},{20,28},{24,32},... | collective-permute-start | bytes 393224 | tf_op jit(solution)/shard_map/while/body/eval_jaxpr/ppermute | solution.py:20
  76.9 11.7 %collective-permute-start.2 = (f32[256,256]{0,1:T(8,128)}, f32[256,256]{0,1:T(8,128)S(1)}, u32[]{:S(2)}, u32[]{:S(2)}) collective-permute-start(f32[256,256]{0,1:T(8,128)} %get-tuple-element.561), channel_id=1, source_target_pairs={{56,0},{60,4},{0,8},{4,12},{8,16},{12,20},{16,24},{20,28},{24,32},... | collective-permute-start | bytes 786440 | tf_op jit(solution)/shard_map/while/body/eval_jaxpr/ppermute | solution.py:20
  77.0 11.6 %collective-permute-start.3 = (f32[256,256]{0,1:T(8,128)}, f32[256,256]{0,1:T(8,128)S(1)}, u32[]{:S(2)}, u32[]{:S(2)}) collective-permute-start(f32[256,256]{0,1:T(8,128)} %get-tuple-element.560), channel_id=1, source_target_pairs={{8,0},{12,4},{16,8},{20,12},{24,16},{28,20},{32,24},{36,28},{40,32... | collective-permute-start | bytes 786440 | tf_op jit(solution)/shard_map/while/body/eval_jaxpr/ppermute | solution.py:20
  80.2 1.0 copy-start.3
  89.6 12.3 %collective-permute-start = (bf16[256,256]{1,0:T(8,128)(2,1)S(1)}, bf16[256,256]{1,0:T(8,128)(2,1)S(1)}, u32[]{:S(2)}, u32[]{:S(2)}) collective-permute-start(bf16[256,256]{1,0:T(8,128)(2,1)S(1)} %copy.227), channel_id=1, source_target_pairs={{8,0},{12,4},{16,8},{20,12},{24,16},{28,20},{32,24},{36,28},{40,32... | collective-permute-start | bytes 393224 | tf_op jit(solution)/shard_map/while/body/eval_jaxpr/ppermute | solution.py:20
  90.1 11.7 %collective-permute-start.1 = (bf16[256,256]{1,0:T(8,128)(2,1)S(1)}, bf16[256,256]{1,0:T(8,128)(2,1)S(1)}, u32[]{:S(2)}, u32[]{:S(2)}) collective-permute-start(bf16[256,256]{1,0:T(8,128)(2,1)S(1)} %copy.228), channel_id=1, source_target_pairs={{56,0},{60,4},{0,8},{4,12},{8,16},{12,20},{16,24},{20,28},{24,32},... | collective-permute-start | bytes 393224 | tf_op jit(solution)/shard_map/while/body/eval_jaxpr/ppermute | solution.py:20
  91.7 9.2 %collective-permute-start.2 = (f32[256,256]{0,1:T(8,128)}, f32[256,256]{0,1:T(8,128)S(1)}, u32[]{:S(2)}, u32[]{:S(2)}) collective-permute-start(f32[256,256]{0,1:T(8,128)} %get-tuple-element.561), channel_id=1, source_target_pairs={{56,0},{60,4},{0,8},{4,12},{8,16},{12,20},{16,24},{20,28},{24,32},... | collective-permute-start | bytes 786440 | tf_op jit(solution)/shard_map/while/body/eval_jaxpr/ppermute | solution.py:20
  91.8 9.1 %collective-permute-start.3 = (f32[256,256]{0,1:T(8,128)}, f32[256,256]{0,1:T(8,128)S(1)}, u32[]{:S(2)}, u32[]{:S(2)}) collective-permute-start(f32[256,256]{0,1:T(8,128)} %get-tuple-element.560), channel_id=1, source_target_pairs={{8,0},{12,4},{16,8},{20,12},{24,16},{28,20},{32,24},{36,28},{40,32... | collective-permute-start | bytes 786440 | tf_op jit(solution)/shard_map/while/body/eval_jaxpr/ppermute | solution.py:20
  95.0 1.0 copy-start.3
  101.8 11.9 %collective-permute-start = (bf16[256,256]{1,0:T(8,128)(2,1)S(1)}, bf16[256,256]{1,0:T(8,128)(2,1)S(1)}, u32[]{:S(2)}, u32[]{:S(2)}) collective-permute-start(bf16[256,256]{1,0:T(8,128)(2,1)S(1)} %copy.227), channel_id=1, source_target_pairs={{8,0},{12,4},{16,8},{20,12},{24,16},{28,20},{32,24},{36,28},{40,32... | collective-permute-start | bytes 393224 | tf_op jit(solution)/shard_map/while/body/eval_jaxpr/ppermute | solution.py:20
  103.8 10.0 %collective-permute-start.1 = (bf16[256,256]{1,0:T(8,128)(2,1)S(1)}, bf16[256,256]{1,0:T(8,128)(2,1)S(1)}, u32[]{:S(2)}, u32[]{:S(2)}) collective-permute-start(bf16[256,256]{1,0:T(8,128)(2,1)S(1)} %copy.228), channel_id=1, source_target_pairs={{56,0},{60,4},{0,8},{4,12},{8,16},{12,20},{16,24},{20,28},{24,32},... | collective-permute-start | bytes 393224 | tf_op jit(solution)/shard_map/while/body/eval_jaxpr/ppermute | solution.py:20
  104.0 8.8 %collective-permute-start.2 = (f32[256,256]{0,1:T(8,128)}, f32[256,256]{0,1:T(8,128)S(1)}, u32[]{:S(2)}, u32[]{:S(2)}) collective-permute-start(f32[256,256]{0,1:T(8,128)} %get-tuple-element.561), channel_id=1, source_target_pairs={{56,0},{60,4},{0,8},{4,12},{8,16},{12,20},{16,24},{20,28},{24,32},... | collective-permute-start | bytes 786440 | tf_op jit(solution)/shard_map/while/body/eval_jaxpr/ppermute | solution.py:20
  104.3 8.6 %collective-permute-start.3 = (f32[256,256]{0,1:T(8,128)}, f32[256,256]{0,1:T(8,128)S(1)}, u32[]{:S(2)}, u32[]{:S(2)}) collective-permute-start(f32[256,256]{0,1:T(8,128)} %get-tuple-element.560), channel_id=1, source_target_pairs={{8,0},{12,4},{16,8},{20,12},{24,16},{28,20},{32,24},{36,28},{40,32... | collective-permute-start | bytes 786440 | tf_op jit(solution)/shard_map/while/body/eval_jaxpr/ppermute | solution.py:20
  107.3 1.0 copy-start.3
  113.8 12.3 %collective-permute-start = (bf16[256,256]{1,0:T(8,128)(2,1)S(1)}, bf16[256,256]{1,0:T(8,128)(2,1)S(1)}, u32[]{:S(2)}, u32[]{:S(2)}) collective-permute-start(bf16[256,256]{1,0:T(8,128)(2,1)S(1)} %copy.227), channel_id=1, source_target_pairs={{8,0},{12,4},{16,8},{20,12},{24,16},{28,20},{32,24},{36,28},{40,32... | collective-permute-start | bytes 393224 | tf_op jit(solution)/shard_map/while/body/eval_jaxpr/ppermute | solution.py:20
  116.1 10.0 %collective-permute-start.1 = (bf16[256,256]{1,0:T(8,128)(2,1)S(1)}, bf16[256,256]{1,0:T(8,128)(2,1)S(1)}, u32[]{:S(2)}, u32[]{:S(2)}) collective-permute-start(bf16[256,256]{1,0:T(8,128)(2,1)S(1)} %copy.228), channel_id=1, source_target_pairs={{56,0},{60,4},{0,8},{4,12},{8,16},{12,20},{16,24},{20,28},{24,32},... | collective-permute-start | bytes 393224 | tf_op jit(solution)/shard_map/while/body/eval_jaxpr/ppermute | solution.py:20
  116.2 9.0 %collective-permute-start.2 = (f32[256,256]{0,1:T(8,128)}, f32[256,256]{0,1:T(8,128)S(1)}, u32[]{:S(2)}, u32[]{:S(2)}) collective-permute-start(f32[256,256]{0,1:T(8,128)} %get-tuple-element.561), channel_id=1, source_target_pairs={{56,0},{60,4},{0,8},{4,12},{8,16},{12,20},{16,24},{20,28},{24,32},... | collective-permute-start | bytes 786440 | tf_op jit(solution)/shard_map/while/body/eval_jaxpr/ppermute | solution.py:20
  116.7 8.5 %collective-permute-start.3 = (f32[256,256]{0,1:T(8,128)}, f32[256,256]{0,1:T(8,128)S(1)}, u32[]{:S(2)}, u32[]{:S(2)}) collective-permute-start(f32[256,256]{0,1:T(8,128)} %get-tuple-element.560), channel_id=1, source_target_pairs={{8,0},{12,4},{16,8},{20,12},{24,16},{28,20},{32,24},{36,28},{40,32... | collective-permute-start | bytes 786440 | tf_op jit(solution)/shard_map/while/body/eval_jaxpr/ppermute | solution.py:20
  119.5 1.0 copy-start.3
  126.1 12.2 %collective-permute-start = (bf16[256,256]{1,0:T(8,128)(2,1)S(1)}, bf16[256,256]{1,0:T(8,128)(2,1)S(1)}, u32[]{:S(2)}, u32[]{:S(2)}) collective-permute-start(bf16[256,256]{1,0:T(8,128)(2,1)S(1)} %copy.227), channel_id=1, source_target_pairs={{8,0},{12,4},{16,8},{20,12},{24,16},{28,20},{32,24},{36,28},{40,32... | collective-permute-start | bytes 393224 | tf_op jit(solution)/shard_map/while/body/eval_jaxpr/ppermute | solution.py:20
  128.3 10.0 %collective-permute-start.1 = (bf16[256,256]{1,0:T(8,128)(2,1)S(1)}, bf16[256,256]{1,0:T(8,128)(2,1)S(1)}, u32[]{:S(2)}, u32[]{:S(2)}) collective-permute-start(bf16[256,256]{1,0:T(8,128)(2,1)S(1)} %copy.228), channel_id=1, source_target_pairs={{56,0},{60,4},{0,8},{4,12},{8,16},{12,20},{16,24},{20,28},{24,32},... | collective-permute-start | bytes 393224 | tf_op jit(solution)/shard_map/while/body/eval_jaxpr/ppermute | solution.py:20
  128.4 9.0 %collective-permute-start.2 = (f32[256,256]{0,1:T(8,128)}, f32[256,256]{0,1:T(8,128)S(1)}, u32[]{:S(2)}, u32[]{:S(2)}) collective-permute-start(f32[256,256]{0,1:T(8,128)} %get-tuple-element.561), channel_id=1, source_target_pairs={{56,0},{60,4},{0,8},{4,12},{8,16},{12,20},{16,24},{20,28},{24,32},... | collective-permute-start | bytes 786440 | tf_op jit(solution)/shard_map/while/body/eval_jaxpr/ppermute | solution.py:20
  129.3 8.1 %collective-permute-start.3 = (f32[256,256]{0,1:T(8,128)}, f32[256,256]{0,1:T(8,128)S(1)}, u32[]{:S(2)}, u32[]{:S(2)}) collective-permute-start(f32[256,256]{0,1:T(8,128)} %get-tuple-element.560), channel_id=1, source_target_pairs={{8,0},{12,4},{16,8},{20,12},{24,16},{28,20},{32,24},{36,28},{40,32... | collective-permute-start | bytes 786440 | tf_op jit(solution)/shard_map/while/body/eval_jaxpr/ppermute | solution.py:20
  131.8 1.0 copy-start.3
  138.3 12.2 %collective-permute-start = (bf16[256,256]{1,0:T(8,128)(2,1)S(1)}, bf16[256,256]{1,0:T(8,128)(2,1)S(1)}, u32[]{:S(2)}, u32[]{:S(2)}) collective-permute-start(bf16[256,256]{1,0:T(8,128)(2,1)S(1)} %copy.227), channel_id=1, source_target_pairs={{8,0},{12,4},{16,8},{20,12},{24,16},{28,20},{32,24},{36,28},{40,32... | collective-permute-start | bytes 393224 | tf_op jit(solution)/shard_map/while/body/eval_jaxpr/ppermute | solution.py:20
  140.6 10.0 %collective-permute-start.1 = (bf16[256,256]{1,0:T(8,128)(2,1)S(1)}, bf16[256,256]{1,0:T(8,128)(2,1)S(1)}, u32[]{:S(2)}, u32[]{:S(2)}) collective-permute-start(bf16[256,256]{1,0:T(8,128)(2,1)S(1)} %copy.228), channel_id=1, source_target_pairs={{56,0},{60,4},{0,8},{4,12},{8,16},{12,20},{16,24},{20,28},{24,32},... | collective-permute-start | bytes 393224 | tf_op jit(solution)/shard_map/while/body/eval_jaxpr/ppermute | solution.py:20
  140.6 9.0 %collective-permute-start.2 = (f32[256,256]{0,1:T(8,128)}, f32[256,256]{0,1:T(8,128)S(1)}, u32[]{:S(2)}, u32[]{:S(2)}) collective-permute-start(f32[256,256]{0,1:T(8,128)} %get-tuple-element.561), channel_id=1, source_target_pairs={{56,0},{60,4},{0,8},{4,12},{8,16},{12,20},{16,24},{20,28},{24,32},... | collective-permute-start | bytes 786440 | tf_op jit(solution)/shard_map/while/body/eval_jaxpr/ppermute | solution.py:20
  141.6 8.0 %collective-permute-start.3 = (f32[256,256]{0,1:T(8,128)}, f32[256,256]{0,1:T(8,128)S(1)}, u32[]{:S(2)}, u32[]{:S(2)}) collective-permute-start(f32[256,256]{0,1:T(8,128)} %get-tuple-element.560), channel_id=1, source_target_pairs={{8,0},{12,4},{16,8},{20,12},{24,16},{28,20},{32,24},{36,28},{40,32... | collective-permute-start | bytes 786440 | tf_op jit(solution)/shard_map/while/body/eval_jaxpr/ppermute | solution.py:20
  144.0 1.0 copy-start.3
  150.5 1.0 copy-start.4
  157.4 6.6 %collective-permute-start.7 = (f32[256,256]{1,0:T(8,128)S(1)}, f32[256,256]{1,0:T(8,128)S(1)}, u32[]{:S(2)}, u32[]{:S(2)}) collective-permute-start(f32[256,256]{1,0:T(8,128)S(1)} %copy.165), channel_id=1, source_target_pairs={{8,0},{12,4},{16,8},{20,12},{24,16},{28,20},{32,24},{36,28},{40,32... | collective-permute-start | bytes 786440 | tf_op jit(solution)/shard_map/ppermute | solution.py:20
  159.6 8.8 %collective-permute-start.8 = (f32[256,256]{1,0:T(8,128)S(1)}, f32[256,256]{1,0:T(8,128)S(1)}, u32[]{:S(2)}, u32[]{:S(2)}) collective-permute-start(f32[256,256]{1,0:T(8,128)S(1)} %copy.171), channel_id=1, source_target_pairs={{56,0},{60,4},{0,8},{4,12},{8,16},{12,20},{16,24},{20,28},{24,32},... | collective-permute-start | bytes 786440 | tf_op jit(solution)/shard_map/ppermute | solution.py:20
  168.4 8.9 %collective-permute-start.10 = (f32[256,256]{1,0:T(8,128)S(1)}, f32[256,256]{1,0:T(8,128)S(1)}, u32[]{:S(2)}, u32[]{:S(2)}) collective-permute-start(f32[256,256]{1,0:T(8,128)S(1)} %get-tuple-element.367), channel_id=1, source_target_pairs={{0,12},{4,56},{8,20},{12,0},{16,28},{20,8},{24,36},{28,16},{32,44}... | collective-permute-start | bytes 786440 | tf_op jit(solution)/shard_map/ppermute | solution.py:31
  168.5 8.8 %collective-permute-start.9 = (f32[256,256]{1,0:T(8,128)S(1)}, f32[256,256]{1,0:T(8,128)S(1)}, u32[]{:S(2)}, u32[]{:S(2)}) collective-permute-start(f32[256,256]{1,0:T(8,128)S(1)} %get-tuple-element.368), channel_id=1, source_target_pairs={{0,56},{4,12},{8,0},{12,20},{16,8},{20,28},{24,16},{28,36},{32,24}... | collective-permute-start | bytes 786440 | tf_op jit(solution)/shard_map/ppermute | solution.py:31
